TPU v7x, 32 devices: a whole 2x2x4 slice. The times are simulated.
32 devices in a mesh: grp: 2 (over x), blk: 2 (over core), head: 8 (over z, y).
Axes of the slice: x: 2, y: 2, z: 4, core: 2. Of those that a mesh axis runs over, the one named last changes fastest.
Arguments:
- stream: bfloat16 [1024, 3072], P(('grp', 'blk', 'head')), parts along dimension 0, may hold values from -6 to 6
- gains: float32 [3, 3072], replicated, may hold values from 0.25 to 1.75
- dilations: int32 [2], replicated, may hold values from 1 to 64, as said below
- w_conv: bfloat16 [2, 3, 3072, 2, 3072], P(None, None, None, None, 'head'), may hold values from -0.0625 to 0.0625
- w_mix: bfloat16 [2, 3072, 3072], P(None, 'head'), may hold values from -0.109375 to 0.109375
- w_qkv: bfloat16 [3072, 3, 8, 128], P(None, None, 'head')
- w_out: bfloat16 [8, 128, 3072], P('head'), may hold values from -0.1875 to 0.1875
Outputs:
- mixed: bfloat16 [1024, 3072], P(('grp', 'blk', 'head')), parts along dimension 0
There are 2 independent parts, one for each index of `grp`. A program takes and returns all parts, laid end to end along the dimension named above; an argument that names none is the same for every part. Nothing has to cross between parts.
Inputs may be any that keep to these rules, and one draw needn't show every extreme that they name: `dilations`: each dilation is a whole number; one is exactly 64.
All inputs are finite; a program needn't handle non-finite values.
Results may differ from a plain program's by a relative error of at most 0.03.
Values may be sent and summed in bfloat16 or wider, within the bound.
No kernel may reach another device: no remote copies, remote signals or barrier semaphores. Data moves between devices by JAX's collectives and lax.ppermute only.
A program may use at most 128 MiB of HBM per device.

v0:
```python
import jax
import jax.numpy as jnp
from jax import lax
from jax.sharding import PartitionSpec as P

LARGEST_DILATION = 64


def shifted(value, axis, by):
    length = lax.axis_size(axis)
    pairs = [(i, i + by) for i in range(length) if 0 <= i + by < length]
    return lax.ppermute(value, axis, pairs)


def normed(values, gain):
    wide = values.astype(jnp.float32)
    scale = lax.rsqrt(jnp.mean(wide * wide, axis=-1, keepdims=True) + 1e-06)
    return (wide * scale * gain).astype(jnp.bfloat16)


def rounded_term(left, right):
    term = jnp.dot(left, right, preferred_element_type=jnp.float32)
    return lax.optimization_barrier(term.astype(jnp.bfloat16)).astype(jnp.float32)


def convolution_gate(hidden, kernel, dilation_factor):
    all_rows = hidden.shape[0]
    width = hidden.shape[1]
    own_width = kernel.shape[-1]
    border_rows = 2 * LARGEST_DILATION
    before = shifted(hidden[all_rows - border_rows :], "blk", 1)
    padded = jnp.concatenate([before, hidden], axis=0)
    pre_act = jnp.zeros((all_rows, 2 * own_width), jnp.float32)
    for tap_idx in range(3):
        start = border_rows - tap_idx * dilation_factor
        slab = lax.dynamic_slice_in_dim(padded, start, all_rows, 0)
        pre_act = pre_act + jnp.dot(
            slab, kernel[tap_idx].reshape(width, 2 * own_width), preferred_element_type=jnp.float32
        )
    return (jnp.tanh(pre_act[:, :own_width]) * jax.nn.sigmoid(pre_act[:, own_width:])).astype(
        jnp.bfloat16
    )


def conv_share(gated, weight, tok_rows):

    def term(start, count):
        return rounded_term(gated, weight)

    return lax.psum_scatter(
        term(jnp.int32(0), tok_rows * lax.axis_size("head")).astype(jnp.bfloat16),
        "head",
        scatter_dimension=0,
        tiled=True,
    ).astype(jnp.float32)


def attention_portion_for(heads_out, out_block, tok_rows):

    def term(start, count):
        return rounded_term(heads_out, out_block)

    return lax.psum_scatter(
        term(jnp.int32(0), tok_rows * lax.axis_size("head")).astype(jnp.bfloat16),
        "head",
        scatter_dimension=0,
        tiled=True,
    ).astype(jnp.float32)


def attend(queries, keys_in, values_in, causal):
    scale = queries.shape[1] ** (-0.5)
    scores = jnp.einsum("qd,kd->qk", queries, keys_in, preferred_element_type=jnp.float32) * scale
    if causal:
        rows_q = lax.broadcasted_iota(jnp.int32, scores.shape, 0)
        rows_k = lax.broadcasted_iota(jnp.int32, scores.shape, 1)
        scores = jnp.where(rows_q >= rows_k, scores, -1e30)
    peak = jnp.max(scores, axis=1)
    probs = jnp.exp(scores - peak[:, None])
    denom = jnp.sum(probs, axis=1)
    weighted = jnp.dot(probs.astype(jnp.bfloat16), values_in, preferred_element_type=jnp.float32)
    return (peak, denom, weighted)


def neutral(count, head_size):
    return (
        jnp.full((count,), -1e30, jnp.float32),
        jnp.zeros((count,), jnp.float32),
        jnp.zeros((count, head_size), jnp.float32),
    )


def combine(first, second):
    peak = jnp.maximum(first[0], second[0])
    scale_one = jnp.exp(first[0] - peak)
    scale_two = jnp.exp(second[0] - peak)
    denom = first[1] * scale_one + second[1] * scale_two
    weighted = first[2] * scale_one[:, None] + second[2] * scale_two[:, None]
    return (peak, denom, weighted)


def per_device(stream, gains, dilations, w_conv, w_mix, w_qkv, w_out):
    blk_pos = lax.axis_index("blk")
    tok_rows = stream.shape[0]
    width = stream.shape[1]
    head_size = w_qkv.shape[3]
    layers = w_conv.shape[0]
    qkv_weight = w_qkv.reshape(width, 3 * head_size)
    share = stream
    state = lax.all_gather(stream, "head", axis=0, tiled=True)
    for layer_idx in range(layers):
        gated = convolution_gate(
            normed(state, gains[layer_idx]), w_conv[layer_idx], dilations[layer_idx]
        )
        summed = conv_share(gated, w_mix[layer_idx], tok_rows)
        share = (share.astype(jnp.float32) + summed).astype(jnp.bfloat16)
        state = lax.all_gather(share, "head", axis=0, tiled=True)
    all_rows = state.shape[0]
    attn_in = normed(state, gains[layers])
    projected = jnp.dot(attn_in, qkv_weight, preferred_element_type=jnp.float32).astype(
        jnp.bfloat16
    )
    queries = projected[:, :head_size]
    keys_own = projected[:, head_size : 2 * head_size]
    values_own = projected[:, 2 * head_size :]
    keys_prev, values_prev = shifted((keys_own, values_own), "blk", 1)
    own_part = attend(queries, keys_own, values_own, True)
    crossing_portion = lax.cond(
        blk_pos > 0,
        lambda: attend(queries, keys_prev, values_prev, False),
        lambda: neutral(all_rows, head_size),
    )
    peak, denom, weighted = combine(own_part, crossing_portion)
    heads_out = (weighted / denom[:, None]).astype(jnp.bfloat16)
    attn_share = attention_portion_for(heads_out, w_out[0], tok_rows)
    return (share.astype(jnp.float32) + attn_share).astype(jnp.bfloat16)


def solution(mesh):
    placed = (
        P(("grp", "blk", "head"), None),
        P(),
        P(),
        P(None, None, None, None, "head"),
        P(None, "head", None),
        P(None, None, "head", None),
        P("head", None, None),
    )
    return jax.shard_map(
        per_device,
        mesh=mesh,
        in_specs=placed,
        out_specs=P(("grp", "blk", "head"), None),
        check_vma=False,
    )
```

profile of v0, /device:TPU:0, one launch (start us, length us, event | category | flops | bytes accessed | tf_op | source)
XLA Modules:
  0.0 449.9 jit_solution(16338248343998651655)
XLA Ops:
  6.5 0.7 all-gather.4.cloned.1.call-update
  7.3 0.0 reduce-scatter.4.cloned.1.call-start
  7.3 0.9 fusion.97
  8.3 48.2 %all-gather.4.cloned.1.call-done = bf16[256,3072]{1,0:T(8,128)(2,1)} async-done(((bf16[32,3072]{1,0:T(8,128)(2,1)}), bf16[256,3072]{1,0:T(8,128)(2,1)}) %all-gather.4.cloned.1.call-update) | async-done | bytes 1572880 | tf_op jit(solution)/shard_map/all_gather | solution.py:110
  56.5 1.8 fusion.5
  58.3 1.9 fusion.7
  60.2 0.1 slice.102
  60.3 2.2 collective-permute-start
  62.4 22.4 %fusion.95 = (bf16[1,1,3072,2,384]{4,3,2,1,0:T(2,128)(2,1)}, bf16[1,1,3072,2,384]{4,3,2,1,0:T(2,128)(2,1)}, bf16[1,1,3072,2,384]{4,3,2,1,0:T(2,128)(2,1)S(1)}, b...) fusion(bf16[2,3,3072,2,384]{4,3,2,1,0:T(2,128)(2,1)} %param.12), kind=kLoop, calls=%fused_computation.106 | loop fusion | bytes 56623104 | tf_op jit(solution)/shard_map/slice | solution.py:38
  84.8 0.7 fusion.98
  87.4 3.0 copy.11
  90.4 3.0 copy.9
  93.4 3.1 copy.10
  96.5 3.9 fusion.100
  100.4 0.0 slice-start.6
  100.4 4.4 fusion.25
  104.8 0.0 slice-start.7
  104.8 2.8 fusion.37
  107.7 0.0 copy-start.5
  107.7 2.2 convolution_convert_fusion.2
  110.0 0.0 reduce-scatter.4.cloned.1.call-update
  110.0 0.0 all-gather.6.cloned.1.call-start
  110.0 64.2 %reduce-scatter.4.cloned.1.call-done = bf16[32,3072]{1,0:T(8,128)(2,1)} async-done(((bf16[256,3072]{1,0:T(8,128)(2,1)}), bf16[32,3072]{1,0:T(8,128)(2,1)}) %reduce-scatter.4.cloned.1.call-update) | async-done | bytes 196624 | tf_op jit(solution)/shard_map/reduce_scatter | solution.py:50
  174.3 1.6 add_convert_fusion.2
  175.9 0.0 all-gather.6.cloned.1.call-update
  175.9 0.0 reduce-scatter.6.cloned.1.call-start
  176.0 43.8 %all-gather.6.cloned.1.call-done = bf16[256,3072]{1,0:T(8,128)(2,1)} async-done(((bf16[32,3072]{1,0:T(8,128)(2,1)}), bf16[256,3072]{1,0:T(8,128)(2,1)}) %all-gather.6.cloned.1.call-update) | async-done | bytes 1572880 | tf_op jit(solution)/shard_map/all_gather | solution.py:117
  219.8 1.8 fusion.8
  221.6 1.9 fusion.10
  223.5 0.1 slice.105
  223.6 2.2 collective-permute-start.1
  227.7 5.3 %copy.14 = bf16[384,8,2,384]{3,1,2,0:T(8,128)(2,1)} copy(bf16[384,8,2,384]{3,2,1,0:T(2,128)(2,1)} %bitcast.55) | data formatting | bytes 9437184
  233.0 5.5 %copy.12 = bf16[384,8,2,384]{3,1,2,0:T(8,128)(2,1)} copy(bf16[384,8,2,384]{3,2,1,0:T(2,128)(2,1)} %bitcast.54) | data formatting | bytes 9437184
  238.5 3.0 copy.13
  241.5 3.9 fusion.101
  245.4 0.0 slice-start.8
  245.4 3.1 fusion.19
  248.6 0.0 slice-start.9
  248.6 2.9 fusion.43
  251.5 0.0 copy-start.4
  251.5 2.2 convolution_convert_fusion.1
  253.7 0.0 reduce-scatter.6.cloned.1.call-update
  253.7 0.0 all-gather.8.cloned.1.call-start
  253.8 64.2 %reduce-scatter.6.cloned.1.call-done = bf16[32,3072]{1,0:T(8,128)(2,1)} async-done(((bf16[256,3072]{1,0:T(8,128)(2,1)}), bf16[32,3072]{1,0:T(8,128)(2,1)}) %reduce-scatter.6.cloned.1.call-update) | async-done | bytes 196624 | tf_op jit(solution)/shard_map/reduce_scatter | solution.py:50
  318.0 1.6 add_convert_fusion.1
  319.7 0.0 all-gather.8.cloned.1.call-update
  319.7 0.0 reduce-scatter.8.cloned.1.call-start
  319.8 2.5 copy.8
  322.2 40.9 %all-gather.8.cloned.1.call-done = bf16[256,3072]{1,0:T(8,128)(2,1)} async-done(((bf16[32,3072]{1,0:T(8,128)(2,1)}), bf16[256,3072]{1,0:T(8,128)(2,1)}) %all-gather.8.cloned.1.call-update) | async-done | bytes 1572880 | tf_op jit(solution)/shard_map/all_gather | solution.py:117
  363.2 1.8 fusion.11
  365.0 3.2 fusion.46
  368.2 0.0 copy-start.3
  368.2 0.2 fusion.99
  368.5 1.3 collective-permute-start.2
  369.7 1.3 collective-permute-start.3
  371.1 0.1 fusion.61
  371.1 0.8 collective-permute-done.3
  371.9 0.6 conditional.1
  371.9 0.6 broadcast.54
  372.5 0.7 multiply_add_fusion
  373.2 1.9 convolution_convert_fusion
  375.2 0.0 reduce-scatter.8.cloned.1.call-update
  375.2 66.2 %reduce-scatter.8.cloned.1.call-done = bf16[32,3072]{1,0:T(8,128)(2,1)} async-done(((bf16[256,3072]{1,0:T(8,128)(2,1)}), bf16[32,3072]{1,0:T(8,128)(2,1)}) %reduce-scatter.8.cloned.1.call-update) | async-done | bytes 196624 | tf_op jit(solution)/shard_map/reduce_scatter | solution.py:63
  441.4 1.6 add_convert_fusion
  (42 shorter events, 0.1 us)
Async XLA Ops:
  6.5 366.7 %copy-start = (bf16[1,128,3072]{2,1,0:T(8,128)(2,1)S(1)}, bf16[1,128,3072]{2,1,0:T(8,128)(2,1)}, u32[]{:S(2)}) copy-start(bf16[1,128,3072]{2,1,0:T(8,128)(2,1)} %param.15) | copy-start | bytes 2359300
  6.5 49.9 %all-gather.4.cloned.1.call-start = ((), (), s32[]{:S(2)}) async-start(), calls=%async_computation.3 | async-start | bytes 1769472 | tf_op jit(solution)/shard_map/all_gather | solution.py:110
  7.3 167.0 %reduce-scatter.4.cloned.1.call-start = ((), (), s32[]{:S(2)}) async-start(), calls=%async_computation.4 | async-start | bytes 1769472 | tf_op jit(solution)/shard_map/reduce_scatter | solution.py:50
  60.2 24.6 %copy-start.6 = (s32[2]{0:T(128)S(1)}, s32[2]{0:T(128)}, u32[]{:S(2)}) copy-start(s32[2]{0:T(128)} %param.11) | copy-start | bytes 28
  60.3 40.1 %collective-permute-start = (bf16[128,3072]{1,0:T(8,128)(2,1)S(1)}, bf16[128,3072]{1,0:T(8,128)(2,1)}, u32[]{:S(2)}, u32[]{:S(2)}) collective-permute-start(bf16[128,3072]{1,0:T(8,128)(2,1)S(1)} %slice.102), channel_id=1, source_target_pairs={{0,8},{1,9},{2,10},{3,11},{4,12},{5,13},{6,14},{7,15},{16,24},{17,... | collective-permute-start | bytes 2359304 | tf_op jit(solution)/shard_map/ppermute | solution.py:12
  96.5 8.3 %slice-start.2 = ((s8[4718592]{0:T(1024)(128)(4,1)}), s8[4194304]{0:T(1024)(128)(4,1)S(1)}, s32[]{:S(2)}) async-start(s8[4718592]{0:T(1024)(128)(4,1)} %bitcast.59), calls=%async_computation.11 | async-start | bytes 8388608
  100.4 4.4 slice-start.3
  100.4 7.3 %slice-start.6 = ((s8[4718592]{0:T(1024)(128)(4,1)}), s8[4194304]{0:T(1024)(128)(4,1)S(1)}, s32[]{:S(2)}) async-start(s8[4718592]{0:T(1024)(128)(4,1)} %bitcast.73), calls=%async_computation.15 | async-start | bytes 8388608
  104.8 2.9 slice-start.7
  107.7 66.5 %copy-start.5 = (bf16[32,3072]{1,0:T(8,128)(2,1)S(1)}, bf16[32,3072]{1,0:T(8,128)(2,1)}, u32[]{:S(2)}) copy-start(bf16[32,3072]{1,0:T(8,128)(2,1)} %param.9) | copy-start | bytes 589828
  110.0 109.8 %all-gather.6.cloned.1.call-start = ((), (), s32[]{:S(2)}) async-start(), calls=%async_computation.5 | async-start | bytes 1769472 | tf_op jit(solution)/shard_map/all_gather | solution.py:117
  175.9 142.1 %reduce-scatter.6.cloned.1.call-start = ((), (), s32[]{:S(2)}) async-start(), calls=%async_computation.6 | async-start | bytes 1769472 | tf_op jit(solution)/shard_map/reduce_scatter | solution.py:50
  223.6 21.8 %collective-permute-start.1 = (bf16[128,3072]{1,0:T(8,128)(2,1)S(1)}, bf16[128,3072]{1,0:T(8,128)(2,1)}, u32[]{:S(2)}, u32[]{:S(2)}) collective-permute-start(bf16[128,3072]{1,0:T(8,128)(2,1)S(1)} %slice.105), channel_id=1, source_target_pairs={{0,8},{1,9},{2,10},{3,11},{4,12},{5,13},{6,14},{7,15},{16,24},{17,... | collective-permute-start | bytes 2359304 | tf_op jit(solution)/shard_map/ppermute | solution.py:12
  233.0 5.5 %slice-start = ((s8[4718592]{0:T(1024)(128)(4,1)}), s8[4194304]{0:T(1024)(128)(4,1)S(1)}, s32[]{:S(2)}) async-start(s8[4718592]{0:T(1024)(128)(4,1)} %bitcast.51), calls=%async_computation.9 | async-start | bytes 8388608
  233.0 5.5 %slice-start.1 = ((s8[4718592]{0:T(1024)(128)(4,1)}), s8[524288]{0:T(1024)(128)(4,1)S(1)}, s32[]{:S(2)}) async-start(s8[4718592]{0:T(1024)(128)(4,1)} %bitcast.51), calls=%async_computation.10 | async-start | bytes 1048576
  241.5 3.9 copy-start.1
  241.5 7.0 %slice-start.4 = ((s8[4718592]{0:T(1024)(128)(4,1)}), s8[4194304]{0:T(1024)(128)(4,1)S(1)}, s32[]{:S(2)}) async-start(s8[4718592]{0:T(1024)(128)(4,1)} %bitcast.64), calls=%async_computation.13 | async-start | bytes 8388608
  245.4 3.2 slice-start.5
  245.4 6.0 %slice-start.8 = ((s8[4718592]{0:T(1024)(128)(4,1)}), s8[4194304]{0:T(1024)(128)(4,1)S(1)}, s32[]{:S(2)}) async-start(s8[4718592]{0:T(1024)(128)(4,1)} %bitcast.75), calls=%async_computation.17 | async-start | bytes 8388608
  248.6 2.9 slice-start.9
  251.5 66.5 %copy-start.4 = (bf16[32,3072]{1,0:T(8,128)(2,1)S(1)}, bf16[32,3072]{1,0:T(8,128)(2,1)}, u32[]{:S(2)}) copy-start(bf16[32,3072]{1,0:T(8,128)(2,1)} %add_convert_fusion.2) | copy-start | bytes 589828
  251.5 68.3 %copy-start.2 = (bf16[3072,3,1,128]{3,0,2,1:T(8,128)(2,1)S(1)}, bf16[3072,3,1,128]{3,0,2,1:T(8,128)(2,1)}, u32[]{:S(2)}) copy-start(bf16[3072,3,1,128]{3,0,2,1:T(8,128)(2,1)} %param.14) | copy-start | bytes 7077892
  253.7 109.5 %all-gather.8.cloned.1.call-start = ((), (), s32[]{:S(2)}) async-start(), calls=%async_computation.7 | async-start | bytes 1769472 | tf_op jit(solution)/shard_map/all_gather | solution.py:117
  319.7 121.7 %reduce-scatter.8.cloned.1.call-start = ((), (), s32[]{:S(2)}) async-start(), calls=%async_computation.8 | async-start | bytes 1769472 | tf_op jit(solution)/shard_map/reduce_scatter | solution.py:63
  368.2 73.2 %copy-start.3 = (bf16[32,3072]{1,0:T(8,128)(2,1)S(1)}, bf16[32,3072]{1,0:T(8,128)(2,1)}, u32[]{:S(2)}) copy-start(bf16[32,3072]{1,0:T(8,128)(2,1)} %add_convert_fusion.1) | copy-start | bytes 589828
  368.5 2.7 collective-permute-start.2
  369.7 2.2 collective-permute-start.3
Sparse Core Ops, SparseCore 0:
  9.5 46.8 all-gather.3
  110.1 64.1 reduce-scatter.3
  176.7 43.0 all-gather.5
  253.9 64.1 reduce-scatter.5
  320.1 43.0 all-gather.7
  375.3 66.0 reduce-scatter.7
where the time goes:
time: 451 us; the launch traced here: 450 us
  waiting for transfers between devices  329 us (73%)
  local copies, waits for them, and re-layouts  50.2 us (11%)
  matrix products  30.7 us (7%)
  between operations  17.7 us (4%)
  other arithmetic  14.9 us (3%)
  starting transfers between devices  7.17 us (2%)
    reduce_scatter x2, waiting for transfers between devices, conv_share(): lax.psum_scatter(term(jnp.int32(0), tok_rows * lax.axis_size('head')).ast...  128 us
    all_gather x2, waiting for transfers between devices, per_device(): state = lax.all_gather(share, 'head', axis=0, tiled=True)  84.8 us
    reduce_scatter x1, waiting for transfers between devices, attention_portion_for(): lax.psum_scatter(term(jnp.int32(0), tok_rows * lax.axis_size('head')).ast...  66.2 us
    all_gather x1, waiting for transfers between devices, per_device(): state = lax.all_gather(stream, 'head', axis=0, tiled=True)  48.2 us
    unnamed x41, local copies, waits for them, and re-layouts  25.5 us
    slice x1, local copies, waits for them, and re-layouts, convolution_gate(): kernel[tap_idx].reshape(width, 2 * own_width)  22.4 us
    dot_general x6, matrix products, convolution_gate(): jnp.dot(slab, kernel[tap_idx].reshape(width, 2 * own_width), preferred_el...  20.9 us
  transfers between devices with their start and end apart: 10, of which 7 were waited for; matrix products, arithmetic and copies ran while one was open for 13% of the time, Pallas kernels for 0%

commit v1 on v0

--- a/solution.py
+++ b/solution.py
@@ -10,6 +10,72 @@
     length = lax.axis_size(axis)
     pairs = [(i, i + by) for i in range(length) if 0 <= i + by < length]
     return lax.ppermute(value, axis, pairs)
+
+
+def ring_order(length):
+    if length % 2:
+        return list(range(length))
+    return list(range(0, length, 2)) + list(range(length - 1, 0, -2))
+
+
+def ring_tables(axis):
+    length = lax.axis_size(axis)
+    order = ring_order(length)
+    place = [0] * length
+    for p, h in enumerate(order):
+        place[h] = p
+    me = jnp.array(place, jnp.int32)[lax.axis_index(axis)]
+    return length, order, jnp.array(order, jnp.int32), me
+
+
+def ring_gather(value, axis):
+    length, order, order_arr, me = ring_tables(axis)
+    forward = [(order[p], order[(p + 1) % length]) for p in range(length)]
+    backward = [(order[p], order[(p - 1) % length]) for p in range(length)]
+    ahead = length // 2
+    behind = length - 1 - ahead
+    rows = value.shape[0]
+    out = jnp.zeros((length * rows,) + value.shape[1:], value.dtype)
+    out = lax.dynamic_update_slice_in_dim(out, value, order_arr[me] * rows, 0)
+    fwd = value
+    bwd = value
+    for k in range(1, ahead + 1):
+        fwd = lax.ppermute(fwd, axis, forward)
+        out = lax.dynamic_update_slice_in_dim(out, fwd, order_arr[(me - k) % length] * rows, 0)
+        if k <= behind:
+            bwd = lax.ppermute(bwd, axis, backward)
+            out = lax.dynamic_update_slice_in_dim(out, bwd, order_arr[(me + k) % length] * rows, 0)
+    return out
+
+
+def ring_scatter_sum(value, axis):
+    length, order, order_arr, me = ring_tables(axis)
+    forward = [(order[p], order[(p + 1) % length]) for p in range(length)]
+    backward = [(order[p], order[(p - 1) % length]) for p in range(length)]
+    ahead = length // 2
+    behind = length - 1 - ahead
+    blocks = value.reshape((length, value.shape[0] // length) + value.shape[1:])
+
+    def own(offset):
+        return lax.dynamic_index_in_dim(blocks, order_arr[(me + offset) % length], 0, keepdims=False).astype(jnp.float32)
+
+    total = own(0)
+    fwd = None
+    bwd = None
+    for k in range(1, ahead + 1):
+        part = own(ahead + 1 - k)
+        if fwd is not None:
+            part = part + fwd.astype(jnp.float32)
+        fwd = lax.ppermute(part.astype(value.dtype), axis, forward)
+        if k <= behind:
+            part = own(k - behind - 1)
+            if bwd is not None:
+                part = part + bwd.astype(jnp.float32)
+            bwd = lax.ppermute(part.astype(value.dtype), axis, backward)
+    total = total + fwd.astype(jnp.float32)
+    if bwd is not None:
+        total = total + bwd.astype(jnp.float32)
+    return total
 
 
 def normed(values, gain):
@@ -47,12 +113,9 @@
     def term(start, count):
         return rounded_term(gated, weight)
 
-    return lax.psum_scatter(
-        term(jnp.int32(0), tok_rows * lax.axis_size("head")).astype(jnp.bfloat16),
-        "head",
-        scatter_dimension=0,
-        tiled=True,
-    ).astype(jnp.float32)
+    return ring_scatter_sum(
+        term(jnp.int32(0), tok_rows * lax.axis_size("head")).astype(jnp.bfloat16), "head"
+    )
 
 
 def attention_portion_for(heads_out, out_block, tok_rows):
@@ -60,12 +123,9 @@
     def term(start, count):
         return rounded_term(heads_out, out_block)
 
-    return lax.psum_scatter(
-        term(jnp.int32(0), tok_rows * lax.axis_size("head")).astype(jnp.bfloat16),
-        "head",
-        scatter_dimension=0,
-        tiled=True,
-    ).astype(jnp.float32)
+    return ring_scatter_sum(
+        term(jnp.int32(0), tok_rows * lax.axis_size("head")).astype(jnp.bfloat16), "head"
+    )
 
 
 def attend(queries, keys_in, values_in, causal):
@@ -107,14 +167,14 @@
     layers = w_conv.shape[0]
     qkv_weight = w_qkv.reshape(width, 3 * head_size)
     share = stream
-    state = lax.all_gather(stream, "head", axis=0, tiled=True)
+    state = ring_gather(stream, "head")
     for layer_idx in range(layers):
         gated = convolution_gate(
             normed(state, gains[layer_idx]), w_conv[layer_idx], dilations[layer_idx]
         )
         summed = conv_share(gated, w_mix[layer_idx], tok_rows)
         share = (share.astype(jnp.float32) + summed).astype(jnp.bfloat16)
-        state = lax.all_gather(share, "head", axis=0, tiled=True)
+        state = ring_gather(share, "head")
     all_rows = state.shape[0]
     attn_in = normed(state, gains[layers])
     projected = jnp.dot(attn_in, qkv_weight, preferred_element_type=jnp.float32).astype(

time: 451 us -> 291 us (0.65)
  waiting for transfers between devices: 329 us -> 105 us
  starting transfers between devices: 7.17 us -> 59.2 us
  between operations: 17.7 us -> 32.8 us
  local copies, waits for them, and re-layouts: 50.2 us -> 64.8 us
  other arithmetic: 14.9 us -> 4.71 us
  matrix products: 30.7 us -> 22.8 us
    reduce_scatter x3 -> x0, waiting for transfers between devices: 195 us -> none  [the longest x2 128 us: conv_share(): lax.psum_scatter(term(jnp.int32(0), tok_rows * lax.axis_size('head')).ast...]
    all_gather x3 -> x0, waiting for transfers between devices: 133 us -> none  [the longest x2 84.8 us: per_device(): state = lax.all_gather(share, 'head', axis=0, tiled=True)]
    ppermute x0 -> x42, waiting for transfers between devices: none -> 105 us  [the longest x12 45.4 us: ring_scatter_sum(): fwd = lax.ppermute(part.astype(value.dtype), axis, forward)]
    ppermute x0 -> x42, starting transfers between devices: none -> 52.2 us  [the longest x12 15.4 us: ring_gather(): fwd = lax.ppermute(fwd, axis, forward)]
    unnamed x41 -> x45, local copies, waits for them, and re-layouts: 25.5 us -> 31.8 us
  transfers between devices with their start and end apart: 10 -> 46, of which waited for: 7 -> 30; matrix products, arithmetic and copies ran while one was open for 13% -> 22% of each run, Pallas kernels for 0% -> 0%
where the time goes in v1:
time: 291 us; the launch traced here: 290 us
  waiting for transfers between devices  105 us (36%)
  local copies, waits for them, and re-layouts  64.8 us (22%)
  starting transfers between devices  59.2 us (20%)
  between operations  32.8 us (11%)
  matrix products  22.8 us (8%)
  other arithmetic  4.71 us (2%)
    ppermute x12, waiting for transfers between devices, ring_scatter_sum(): fwd = lax.ppermute(part.astype(value.dtype), axis, forward)  45.4 us
    unnamed x45, local copies, waits for them, and re-layouts  31.8 us
    ppermute x12, waiting for transfers between devices, ring_gather(): fwd = lax.ppermute(fwd, axis, forward)  29.1 us
    slice x1, local copies, waits for them, and re-layouts, convolution_gate(): kernel[tap_idx].reshape(width, 2 * own_width)  26.1 us
    ppermute x9, waiting for transfers between devices, ring_scatter_sum(): bwd = lax.ppermute(part.astype(value.dtype), axis, backward)  20.8 us
    dot_general x6, matrix products, convolution_gate(): jnp.dot(slab, kernel[tap_idx].reshape(width, 2 * own_width), preferred_el...  18.7 us
    ppermute x12, starting transfers between devices, ring_gather(): fwd = lax.ppermute(fwd, axis, forward)  15.4 us
    ppermute x9, starting transfers between devices, ring_scatter_sum(): bwd = lax.ppermute(part.astype(value.dtype), axis, backward)  14.1 us
  transfers between devices with their start and end apart: 46, of which 30 were waited for; matrix products, arithmetic and copies ran while one was open for 22% of the time, Pallas kernels for 0%

profile of v1, /device:TPU:0, one launch (start us, length us, event | category | flops | bytes accessed | tf_op | source)
XLA Modules:
  0.0 289.8 jit_solution(4075339070962055987)
XLA Ops:
  0.0 3.0 %collective-permute-start = (bf16[32,3072]{1,0:T(8,128)(2,1)}, bf16[32,3072]{1,0:T(8,128)(2,1)S(1)}, u32[]{:S(2)}, u32[]{:S(2)}) collective-permute-start(bf16[32,3072]{1,0:T(8,128)(2,1)} %param.21), channel_id=1, source_target_pairs={{0,2},{2,4},{4,6},{6,7},{7,5},{5,3},{3,1},{1,0},{8,10},{10,12},{12... | collective-permute-start | bytes 589832 | tf_op jit(solution)/shard_map/ppermute | solution.py:43
  12.8 1.7 fusion.112
  19.5 1.5 fusion.111
  21.3 2.1 collective-permute-start.2
  23.4 4.3 %collective-permute-done.2 = bf16[32,3072]{1,0:T(8,128)(2,1)S(1)} collective-permute-done((bf16[32,3072]{1,0:T(8,128)(2,1)S(1)}, bf16[32,3072]{1,0:T(8,128)(2,1)S(1)}, u32[]{:S(2)}, u32[]{:S(2)}) %collective-permute-start.2) | collective-permute-done | bytes 196640 | tf_op jit(solution)/shard_map/ppermute | solution.py:43
  27.7 1.7 collective-permute-start.4
  29.8 3.6 %collective-permute-done.4 = bf16[32,3072]{1,0:T(8,128)(2,1)S(1)} collective-permute-done((bf16[32,3072]{1,0:T(8,128)(2,1)S(1)}, bf16[32,3072]{1,0:T(8,128)(2,1)S(1)}, u32[]{:S(2)}, u32[]{:S(2)}) %collective-permute-start.4) | collective-permute-done | bytes 196640 | tf_op jit(solution)/shard_map/ppermute | solution.py:43
  33.4 1.9 collective-permute-start.6
  35.3 3.7 %collective-permute-done.6 = bf16[32,3072]{1,0:T(8,128)(2,1)S(1)} collective-permute-done((bf16[32,3072]{1,0:T(8,128)(2,1)S(1)}, bf16[32,3072]{1,0:T(8,128)(2,1)S(1)}, u32[]{:S(2)}, u32[]{:S(2)}) %collective-permute-start.6) | collective-permute-done | bytes 196640 | tf_op jit(solution)/shard_map/ppermute | solution.py:43
  40.0 2.2 collective-permute-start.7
  42.3 26.1 %fusion.109 = (bf16[1,1,3072,2,384]{4,3,2,1,0:T(2,128)(2,1)}, bf16[1,1,3072,2,384]{4,3,2,1,0:T(2,128)(2,1)}, bf16[1,1,3072,2,384]{4,3,2,1,0:T(2,128)(2,1)}, bf16...) fusion(bf16[2,3,3072,2,384]{4,3,2,1,0:T(2,128)(2,1)} %param.24), kind=kLoop, calls=%fused_computation.173 | loop fusion | bytes 56623104 | tf_op jit(solution)/shard_map/slice | solution.py:104
  73.5 5.3 %copy.22 = bf16[384,8,2,384]{3,1,2,0:T(8,128)(2,1)} copy(bf16[384,8,2,384]{3,2,1,0:T(2,128)(2,1)} %bitcast.148) | data formatting | bytes 9437184
  78.8 5.4 %copy.23 = bf16[384,8,2,384]{3,1,2,0:T(8,128)(2,1)} copy(bf16[384,8,2,384]{3,2,1,0:T(2,128)(2,1)} %bitcast.147) | data formatting | bytes 9437184
  84.2 3.0 %copy.21 = bf16[384,8,2,384]{3,1,2,0:T(8,128)(2,1)} copy(bf16[384,8,2,384]{3,2,1,0:T(2,128)(2,1)S(1)} %bitcast.146) | data formatting | bytes 9437184
  88.5 4.3 %fusion.28 = f32[256,768]{1,0:T(8,128)S(1)} fusion(bf16[3072,768]{1,0:T(8,128)(2,1)} %bitcast.159, s32[]{:T(128)S(6)} %select_n.520, bf16[256,3072]{1,0:T(8,128)(2,1)S(1)} %fusion.7, bf16[128,3072]{1,0:T(8,128)(2,1)} %collective-permute-done.7), kind=kOutput, calls=%fused_computation.43 | convolution fusion | flops 1211105280 | bytes 7864324 | tf_op jit(solution)/shard_map/dot_general | solution.py:103
  92.8 3.7 %fusion.25 = f32[256,768]{1,0:T(8,128)S(1)} fusion(bf16[3072,768]{1,0:T(8,128)(2,1)S(1)} %bitcast.158, s32[]{:T(128)S(6)} %select_n.521, bf16[256,3072]{1,0:T(8,128)(2,1)S(1)} %fusion.7, bf16[128,3072]{1,0:T(8,128)(2,1)} %collective-permute-done.7), kind=kOutput, calls=%fused_computation.41 | convolution fusion | flops 1211105280 | bytes 7864324 | tf_op jit(solution)/shard_map/dot_general | solution.py:103
  96.5 1.5 add_add_fusion.1
  99.2 1.9 collective-permute-start.8
  103.0 3.3 %collective-permute-done.8 = bf16[32,3072]{1,0:T(8,128)(2,1)S(1)} collective-permute-done((bf16[32,3072]{1,0:T(8,128)(2,1)S(1)}, bf16[32,3072]{1,0:T(8,128)(2,1)S(1)}, u32[]{:S(2)}, u32[]{:S(2)}) %collective-permute-start.8) | collective-permute-done | bytes 196640 | tf_op jit(solution)/shard_map/ppermute | solution.py:69
  106.3 1.7 collective-permute-start.9
  110.1 2.5 collective-permute-done.9
  112.7 1.4 collective-permute-start.10
  117.6 2.5 collective-permute-done.10
  124.3 1.6 collective-permute-done.13
  129.4 2.3 collective-permute-done.14
  132.0 1.8 collective-permute-start.15
  133.8 1.7 collective-permute-start.16
  135.5 3.6 %collective-permute-done.15 = bf16[32,3072]{1,0:T(8,128)(2,1)S(1)} collective-permute-done((bf16[32,3072]{1,0:T(8,128)(2,1)S(1)}, bf16[32,3072]{1,0:T(8,128)(2,1)S(1)}, u32[]{:S(2)}, u32[]{:S(2)}) %collective-permute-start.15) | collective-permute-done | bytes 196640 | tf_op jit(solution)/shard_map/ppermute | solution.py:43
  139.1 2.2 collective-permute-start.17
  141.3 1.9 collective-permute-start.18
  143.3 3.5 %collective-permute-done.17 = bf16[32,3072]{1,0:T(8,128)(2,1)S(1)} collective-permute-done((bf16[32,3072]{1,0:T(8,128)(2,1)S(1)}, bf16[32,3072]{1,0:T(8,128)(2,1)S(1)}, u32[]{:S(2)}, u32[]{:S(2)}) %collective-permute-start.17) | collective-permute-done | bytes 196640 | tf_op jit(solution)/shard_map/ppermute | solution.py:43
  149.2 3.3 %collective-permute-done.19 = bf16[32,3072]{1,0:T(8,128)(2,1)S(1)} collective-permute-done((bf16[32,3072]{1,0:T(8,128)(2,1)S(1)}, bf16[32,3072]{1,0:T(8,128)(2,1)S(1)}, u32[]{:S(2)}, u32[]{:S(2)}) %collective-permute-start.19) | collective-permute-done | bytes 196640 | tf_op jit(solution)/shard_map/ppermute | solution.py:43
  154.0 4.2 %collective-permute-done.21 = bf16[32,3072]{1,0:T(8,128)(2,1)S(1)} collective-permute-done((bf16[32,3072]{1,0:T(8,128)(2,1)S(1)}, bf16[32,3072]{1,0:T(8,128)(2,1)S(1)}, u32[]{:S(2)}, u32[]{:S(2)}) %collective-permute-start.21) | collective-permute-done | bytes 196640 | tf_op jit(solution)/shard_map/ppermute | solution.py:43
  159.2 2.2 collective-permute-start.22
  163.4 5.2 %copy.25 = bf16[384,8,2,384]{3,1,2,0:T(8,128)(2,1)} copy(bf16[384,8,2,384]{3,2,1,0:T(2,128)(2,1)} %bitcast.143) | data formatting | bytes 9437184
  168.6 5.5 %copy.26 = bf16[384,8,2,384]{3,1,2,0:T(8,128)(2,1)} copy(bf16[384,8,2,384]{3,2,1,0:T(2,128)(2,1)} %bitcast.142) | data formatting | bytes 9437184
  174.2 3.0 %copy.24 = bf16[384,8,2,384]{3,1,2,0:T(8,128)(2,1)} copy(bf16[384,8,2,384]{3,2,1,0:T(2,128)(2,1)S(1)} %bitcast.141) | data formatting | bytes 9437184
  177.2 4.3 %fusion.22 = f32[256,768]{1,0:T(8,128)S(1)} fusion(bf16[3072,768]{1,0:T(8,128)(2,1)} %bitcast.164, s32[]{:T(128)S(6)} %select_n.569, bf16[256,3072]{1,0:T(8,128)(2,1)S(1)} %fusion.10, bf16[128,3072]{1,0:T(8,128)(2,1)} %collective-permute-done.22), kind=kOutput, calls=%fused_computation.39 | convolution fusion | flops 1211105280 | bytes 7864324 | tf_op jit(solution)/shard_map/dot_general | solution.py:103
  181.5 3.5 %fusion.19 = f32[256,768]{1,0:T(8,128)S(1)} fusion(bf16[3072,768]{1,0:T(8,128)(2,1)S(1)} %bitcast.163, s32[]{:T(128)S(6)} %select_n.570, bf16[256,3072]{1,0:T(8,128)(2,1)S(1)} %fusion.10, bf16[128,3072]{1,0:T(8,128)(2,1)} %collective-permute-done.22), kind=kOutput, calls=%fused_computation.37 | convolution fusion | flops 1211105280 | bytes 7864324 | tf_op jit(solution)/shard_map/dot_general | solution.py:103
  185.1 1.5 add_add_fusion
  188.9 6.1 %collective-permute-done.23 = bf16[32,3072]{1,0:T(8,128)(2,1)S(1)} collective-permute-done((bf16[32,3072]{1,0:T(8,128)(2,1)S(1)}, bf16[32,3072]{1,0:T(8,128)(2,1)S(1)}, u32[]{:S(2)}, u32[]{:S(2)}) %collective-permute-start.23) | collective-permute-done | bytes 196640 | tf_op jit(solution)/shard_map/ppermute | solution.py:69
  195.0 1.5 collective-permute-start.24
  197.4 4.2 %collective-permute-done.24 = bf16[32,3072]{1,0:T(8,128)(2,1)S(1)} collective-permute-done((bf16[32,3072]{1,0:T(8,128)(2,1)S(1)}, bf16[32,3072]{1,0:T(8,128)(2,1)S(1)}, u32[]{:S(2)}, u32[]{:S(2)}) %collective-permute-start.24) | collective-permute-done | bytes 196640 | tf_op jit(solution)/shard_map/ppermute | solution.py:69
  202.4 7.6 %collective-permute-done.25 = bf16[32,3072]{1,0:T(8,128)(2,1)S(1)} collective-permute-done((bf16[32,3072]{1,0:T(8,128)(2,1)S(1)}, bf16[32,3072]{1,0:T(8,128)(2,1)S(1)}, u32[]{:S(2)}, u32[]{:S(2)}) %collective-permute-start.25) | collective-permute-done | bytes 196640 | tf_op jit(solution)/shard_map/ppermute | solution.py:69
  210.2 2.2 collective-permute-start.28
  212.3 5.1 %collective-permute-done.28 = bf16[32,3072]{1,0:T(8,128)(2,1)S(1)} collective-permute-done((bf16[32,3072]{1,0:T(8,128)(2,1)S(1)}, bf16[32,3072]{1,0:T(8,128)(2,1)S(1)}, u32[]{:S(2)}, u32[]{:S(2)}) %collective-permute-start.28) | collective-permute-done | bytes 196640 | tf_op jit(solution)/shard_map/ppermute | solution.py:74
  217.5 2.5 collective-permute-start.29
  220.0 3.2 %collective-permute-done.29 = bf16[32,3072]{1,0:T(8,128)(2,1)S(1)} collective-permute-done((bf16[32,3072]{1,0:T(8,128)(2,1)S(1)}, bf16[32,3072]{1,0:T(8,128)(2,1)S(1)}, u32[]{:S(2)}, u32[]{:S(2)}) %collective-permute-start.29) | collective-permute-done | bytes 196640 | tf_op jit(solution)/shard_map/ppermute | solution.py:74
  223.5 4.3 %copy.20 = bf16[3072,3,1,128]{0,3,1,2:T(8,128)(2,1)} copy(bf16[3072,3,1,128]{3,0,2,1:T(8,128)(2,1)} %param.26) | data formatting | bytes 4718592 | tf_op args[5]
  227.8 2.5 collective-permute-start.31
  230.3 3.2 %collective-permute-done.31 = bf16[32,3072]{1,0:T(8,128)(2,1)S(1)} collective-permute-done((bf16[32,3072]{1,0:T(8,128)(2,1)S(1)}, bf16[32,3072]{1,0:T(8,128)(2,1)S(1)}, u32[]{:S(2)}, u32[]{:S(2)}) %collective-permute-start.31) | collective-permute-done | bytes 196640 | tf_op jit(solution)/shard_map/ppermute | solution.py:46
  233.5 2.5 collective-permute-start.33
  236.1 3.0 %collective-permute-done.33 = bf16[32,3072]{1,0:T(8,128)(2,1)S(1)} collective-permute-done((bf16[32,3072]{1,0:T(8,128)(2,1)S(1)}, bf16[32,3072]{1,0:T(8,128)(2,1)S(1)}, u32[]{:S(2)}, u32[]{:S(2)}) %collective-permute-start.33) | collective-permute-done | bytes 196640 | tf_op jit(solution)/shard_map/ppermute | solution.py:46
  239.2 2.5 collective-permute-start.35
  242.0 2.8 collective-permute-done.35
  244.9 2.8 collective-permute-done.36
  255.0 6.2 %collective-permute-done.39 = bf16[32,3072]{1,0:T(8,128)(2,1)S(1)} collective-permute-done((bf16[32,3072]{1,0:T(8,128)(2,1)S(1)}, bf16[32,3072]{1,0:T(8,128)(2,1)S(1)}, u32[]{:S(2)}, u32[]{:S(2)}) %collective-permute-start.39) | collective-permute-done | bytes 196640 | tf_op jit(solution)/shard_map/ppermute | solution.py:69
  261.3 2.3 collective-permute-start.43
  263.6 5.3 %collective-permute-done.40 = bf16[32,3072]{1,0:T(8,128)(2,1)S(1)} collective-permute-done((bf16[32,3072]{1,0:T(8,128)(2,1)S(1)}, bf16[32,3072]{1,0:T(8,128)(2,1)S(1)}, u32[]{:S(2)}, u32[]{:S(2)}) %collective-permute-start.40) | collective-permute-done | bytes 196640 | tf_op jit(solution)/shard_map/ppermute | solution.py:69
  269.1 7.4 %collective-permute-done.41 = bf16[32,3072]{1,0:T(8,128)(2,1)S(1)} collective-permute-done((bf16[32,3072]{1,0:T(8,128)(2,1)S(1)}, bf16[32,3072]{1,0:T(8,128)(2,1)S(1)}, u32[]{:S(2)}, u32[]{:S(2)}) %collective-permute-start.41) | collective-permute-done | bytes 196640 | tf_op jit(solution)/shard_map/ppermute | solution.py:69
  276.7 1.8 collective-permute-start.44
  278.7 4.5 %collective-permute-done.44 = bf16[32,3072]{1,0:T(8,128)(2,1)S(1)} collective-permute-done((bf16[32,3072]{1,0:T(8,128)(2,1)S(1)}, bf16[32,3072]{1,0:T(8,128)(2,1)S(1)}, u32[]{:S(2)}, u32[]{:S(2)}) %collective-permute-start.44) | collective-permute-done | bytes 196640 | tf_op jit(solution)/shard_map/ppermute | solution.py:74
  283.2 1.5 collective-permute-start.45
  284.7 4.2 %collective-permute-done.45 = bf16[32,3072]{1,0:T(8,128)(2,1)S(1)} collective-permute-done((bf16[32,3072]{1,0:T(8,128)(2,1)S(1)}, bf16[32,3072]{1,0:T(8,128)(2,1)S(1)}, u32[]{:S(2)}, u32[]{:S(2)}) %collective-permute-start.45) | collective-permute-done | bytes 196640 | tf_op jit(solution)/shard_map/ppermute | solution.py:74
  (155 shorter events, 28.6 us)
Async XLA Ops:
  0.0 254.1 %copy-start = (bf16[1,128,3072]{2,1,0:T(8,128)(2,1)S(1)}, bf16[1,128,3072]{2,1,0:T(8,128)(2,1)}, u32[]{:S(2)}) copy-start(bf16[1,128,3072]{2,1,0:T(8,128)(2,1)} %param.27) | copy-start | bytes 2359300
  0.0 21.2 %copy-start.4 = (bf16[32,3072]{1,0:T(8,128)(2,1)S(1)}, bf16[32,3072]{1,0:T(8,128)(2,1)}, u32[]{:S(2)}) copy-start(bf16[32,3072]{1,0:T(8,128)(2,1)} %param.21) | copy-start | bytes 589828
  0.0 21.3 %collective-permute-start = (bf16[32,3072]{1,0:T(8,128)(2,1)}, bf16[32,3072]{1,0:T(8,128)(2,1)S(1)}, u32[]{:S(2)}, u32[]{:S(2)}) collective-permute-start(bf16[32,3072]{1,0:T(8,128)(2,1)} %param.21), channel_id=1, source_target_pairs={{0,2},{2,4},{4,6},{6,7},{7,5},{5,3},{3,1},{1,0},{8,10},{10,12},{12... | collective-permute-start | bytes 589832 | tf_op jit(solution)/shard_map/ppermute | solution.py:43
  3.0 20.3 %collective-permute-start.1 = (bf16[32,3072]{1,0:T(8,128)(2,1)}, bf16[32,3072]{1,0:T(8,128)(2,1)S(1)}, u32[]{:S(2)}, u32[]{:S(2)}) collective-permute-start(bf16[32,3072]{1,0:T(8,128)(2,1)} %param.21), channel_id=1, source_target_pairs={{0,1},{2,0},{4,2},{6,4},{7,6},{5,7},{3,5},{1,3},{8,9},{10,8},{12,1... | collective-permute-start | bytes 589832 | tf_op jit(solution)/shard_map/ppermute | solution.py:46
  21.3 6.4 %collective-permute-start.2 = (bf16[32,3072]{1,0:T(8,128)(2,1)S(1)}, bf16[32,3072]{1,0:T(8,128)(2,1)S(1)}, u32[]{:S(2)}, u32[]{:S(2)}) collective-permute-start(bf16[32,3072]{1,0:T(8,128)(2,1)S(1)} %collective-permute-done), channel_id=1, source_target_pairs={{0,2},{2,4},{4,6},{6,7},{7,5},{5,3},{3,1},{1,0},{8,10},{10,12},{12... | collective-permute-start | bytes 589832 | tf_op jit(solution)/shard_map/ppermute | solution.py:43
  23.4 6.1 %collective-permute-start.3 = (bf16[32,3072]{1,0:T(8,128)(2,1)S(1)}, bf16[32,3072]{1,0:T(8,128)(2,1)S(1)}, u32[]{:S(2)}, u32[]{:S(2)}) collective-permute-start(bf16[32,3072]{1,0:T(8,128)(2,1)S(1)} %collective-permute-done.1), channel_id=1, source_target_pairs={{0,1},{2,0},{4,2},{6,4},{7,6},{5,7},{3,5},{1,3},{8,9},{10,8},{12,1... | collective-permute-start | bytes 589832 | tf_op jit(solution)/shard_map/ppermute | solution.py:46
  27.7 5.7 %collective-permute-start.4 = (bf16[32,3072]{1,0:T(8,128)(2,1)S(1)}, bf16[32,3072]{1,0:T(8,128)(2,1)S(1)}, u32[]{:S(2)}, u32[]{:S(2)}) collective-permute-start(bf16[32,3072]{1,0:T(8,128)(2,1)S(1)} %collective-permute-done.2), channel_id=1, source_target_pairs={{0,2},{2,4},{4,6},{6,7},{7,5},{5,3},{3,1},{1,0},{8,10},{10,12},{12... | collective-permute-start | bytes 589832 | tf_op jit(solution)/shard_map/ppermute | solution.py:43
  29.4 5.8 %collective-permute-start.5 = (bf16[32,3072]{1,0:T(8,128)(2,1)S(1)}, bf16[32,3072]{1,0:T(8,128)(2,1)S(1)}, u32[]{:S(2)}, u32[]{:S(2)}) collective-permute-start(bf16[32,3072]{1,0:T(8,128)(2,1)S(1)} %collective-permute-done.3), channel_id=1, source_target_pairs={{0,1},{2,0},{4,2},{6,4},{7,6},{5,7},{3,5},{1,3},{8,9},{10,8},{12,1... | collective-permute-start | bytes 589832 | tf_op jit(solution)/shard_map/ppermute | solution.py:46
  33.4 5.7 %collective-permute-start.6 = (bf16[32,3072]{1,0:T(8,128)(2,1)S(1)}, bf16[32,3072]{1,0:T(8,128)(2,1)S(1)}, u32[]{:S(2)}, u32[]{:S(2)}) collective-permute-start(bf16[32,3072]{1,0:T(8,128)(2,1)S(1)} %collective-permute-done.4), channel_id=1, source_target_pairs={{0,2},{2,4},{4,6},{6,7},{7,5},{5,3},{3,1},{1,0},{8,10},{10,12},{12... | collective-permute-start | bytes 589832 | tf_op jit(solution)/shard_map/ppermute | solution.py:43
  40.0 28.4 %copy-start.6 = (s32[2]{0:T(128)S(1)}, s32[2]{0:T(128)}, u32[]{:S(2)}) copy-start(s32[2]{0:T(128)} %param.23) | copy-start | bytes 28
  40.0 48.4 %collective-permute-start.7 = (bf16[128,3072]{1,0:T(8,128)(2,1)S(1)}, bf16[128,3072]{1,0:T(8,128)(2,1)}, u32[]{:S(2)}, u32[]{:S(2)}) collective-permute-start(bf16[128,3072]{1,0:T(8,128)(2,1)S(1)} %slice.102), channel_id=1, source_target_pairs={{0,8},{1,9},{2,10},{3,11},{4,12},{5,13},{6,14},{7,15},{16,24},{17,... | collective-permute-start | bytes 2359304 | tf_op jit(solution)/shard_map/ppermute | solution.py:12
  78.8 5.4 %slice-start.2 = ((s8[4718592]{0:T(1024)(128)(4,1)}), s8[4194304]{0:T(1024)(128)(4,1)S(1)}, s32[]{:S(2)}) async-start(s8[4718592]{0:T(1024)(128)(4,1)} %bitcast.144), calls=%async_computation.2 | async-start | bytes 8388608
  78.8 5.4 %slice-start.3 = ((s8[4718592]{0:T(1024)(128)(4,1)}), s8[524288]{0:T(1024)(128)(4,1)S(1)}, s32[]{:S(2)}) async-start(s8[4718592]{0:T(1024)(128)(4,1)} %bitcast.144), calls=%async_computation.3 | async-start | bytes 1048576
  88.4 4.3 %copy-start.1 = (bf16[384,8,2,384]{3,1,2,0:T(8,128)(2,1)S(1)}, bf16[384,8,2,384]{3,1,2,0:T(8,128)(2,1)}, u32[]{:S(2)}) copy-start(bf16[384,8,2,384]{3,1,2,0:T(8,128)(2,1)} %copy.23) | copy-start | bytes 14155780
  88.5 8.1 %slice-start.4 = ((s8[4718592]{0:T(1024)(128)(4,1)}), s8[4194304]{0:T(1024)(128)(4,1)S(1)}, s32[]{:S(2)}) async-start(s8[4718592]{0:T(1024)(128)(4,1)} %bitcast.155), calls=%async_computation.4 | async-start | bytes 8388608
  88.5 9.6 %slice-start.8 = ((s8[4718592]{0:T(1024)(128)(4,1)}), s8[4194304]{0:T(1024)(128)(4,1)S(1)}, s32[]{:S(2)}) async-start(s8[4718592]{0:T(1024)(128)(4,1)} %bitcast.181), calls=%async_computation.8 | async-start | bytes 8388608
  92.8 3.7 %slice-start.5 = ((s8[4718592]{0:T(1024)(128)(4,1)}), s8[524288]{0:T(1024)(128)(4,1)S(1)}, s32[]{:S(2)}) async-start(s8[4718592]{0:T(1024)(128)(4,1)} %bitcast.155), calls=%async_computation.5 | async-start | bytes 1048576
  92.8 5.2 %slice-start.9 = ((s8[4718592]{0:T(1024)(128)(4,1)}), s8[524288]{0:T(1024)(128)(4,1)S(1)}, s32[]{:S(2)}) async-start(s8[4718592]{0:T(1024)(128)(4,1)} %bitcast.181), calls=%async_computation.9 | async-start | bytes 1048576
  99.2 7.1 %collective-permute-start.8 = (bf16[32,3072]{1,0:T(8,128)(2,1)S(1)}, bf16[32,3072]{1,0:T(8,128)(2,1)S(1)}, u32[]{:S(2)}, u32[]{:S(2)}) collective-permute-start(bf16[32,3072]{1,0:T(8,128)(2,1)S(1)} %get-tuple-element.45), channel_id=1, source_target_pairs={{0,2},{2,4},{4,6},{6,7},{7,5},{5,3},{3,1},{1,0},{8,10},{10,12},{12... | collective-permute-start | bytes 589832 | tf_op jit(solution)/shard_map/ppermute | solution.py:69
  106.3 6.3 %collective-permute-start.9 = (bf16[32,3072]{1,0:T(8,128)(2,1)S(1)}, bf16[32,3072]{1,0:T(8,128)(2,1)S(1)}, u32[]{:S(2)}, u32[]{:S(2)}) collective-permute-start(bf16[32,3072]{1,0:T(8,128)(2,1)S(1)} %fusion.65), channel_id=1, source_target_pairs={{0,2},{2,4},{4,6},{6,7},{7,5},{5,3},{3,1},{1,0},{8,10},{10,12},{12... | collective-permute-start | bytes 589832 | tf_op jit(solution)/shard_map/ppermute | solution.py:69
  109.7 7.9 %collective-permute-start.12 = (bf16[32,3072]{1,0:T(8,128)(2,1)S(1)}, bf16[32,3072]{1,0:T(8,128)(2,1)S(1)}, u32[]{:S(2)}, u32[]{:S(2)}) collective-permute-start(bf16[32,3072]{1,0:T(8,128)(2,1)S(1)} %get-tuple-element.46), channel_id=1, source_target_pairs={{0,1},{2,0},{4,2},{6,4},{7,6},{5,7},{3,5},{1,3},{8,9},{10,8},{12,1... | collective-permute-start | bytes 589832 | tf_op jit(solution)/shard_map/ppermute | solution.py:74
  112.7 7.4 %collective-permute-start.10 = (bf16[32,3072]{1,0:T(8,128)(2,1)S(1)}, bf16[32,3072]{1,0:T(8,128)(2,1)S(1)}, u32[]{:S(2)}, u32[]{:S(2)}) collective-permute-start(bf16[32,3072]{1,0:T(8,128)(2,1)S(1)} %fusion.66), channel_id=1, source_target_pairs={{0,2},{2,4},{4,6},{6,7},{7,5},{5,3},{3,1},{1,0},{8,10},{10,12},{12... | collective-permute-start | bytes 589832 | tf_op jit(solution)/shard_map/ppermute | solution.py:69
  120.2 5.7 %collective-permute-start.13 = (bf16[32,3072]{1,0:T(8,128)(2,1)S(1)}, bf16[32,3072]{1,0:T(8,128)(2,1)S(1)}, u32[]{:S(2)}, u32[]{:S(2)}) collective-permute-start(bf16[32,3072]{1,0:T(8,128)(2,1)S(1)} %get-tuple-element.44), channel_id=1, source_target_pairs={{0,1},{2,0},{4,2},{6,4},{7,6},{5,7},{3,5},{1,3},{8,9},{10,8},{12,1... | collective-permute-start | bytes 589832 | tf_op jit(solution)/shard_map/ppermute | solution.py:74
  123.4 6.1 %collective-permute-start.11 = (bf16[32,3072]{1,0:T(8,128)(2,1)S(1)}, bf16[32,3072]{1,0:T(8,128)(2,1)S(1)}, u32[]{:S(2)}, u32[]{:S(2)}) collective-permute-start(bf16[32,3072]{1,0:T(8,128)(2,1)S(1)} %get-tuple-element.43), channel_id=1, source_target_pairs={{0,2},{2,4},{4,6},{6,7},{7,5},{5,3},{3,1},{1,0},{8,10},{10,12},{12... | collective-permute-start | bytes 589832 | tf_op jit(solution)/shard_map/ppermute | solution.py:69
  126.0 5.7 %collective-permute-start.14 = (bf16[32,3072]{1,0:T(8,128)(2,1)S(1)}, bf16[32,3072]{1,0:T(8,128)(2,1)S(1)}, u32[]{:S(2)}, u32[]{:S(2)}) collective-permute-start(bf16[32,3072]{1,0:T(8,128)(2,1)S(1)} %fusion.64), channel_id=1, source_target_pairs={{0,1},{2,0},{4,2},{6,4},{7,6},{5,7},{3,5},{1,3},{8,9},{10,8},{12,1... | collective-permute-start | bytes 589832 | tf_op jit(solution)/shard_map/ppermute | solution.py:74
  132.0 7.2 %collective-permute-start.15 = (bf16[32,3072]{1,0:T(8,128)(2,1)S(1)}, bf16[32,3072]{1,0:T(8,128)(2,1)S(1)}, u32[]{:S(2)}, u32[]{:S(2)}) collective-permute-start(bf16[32,3072]{1,0:T(8,128)(2,1)S(1)} %get-tuple-element.26), channel_id=1, source_target_pairs={{0,2},{2,4},{4,6},{6,7},{7,5},{5,3},{3,1},{1,0},{8,10},{10,12},{12... | collective-permute-start | bytes 589832 | tf_op jit(solution)/shard_map/ppermute | solution.py:43
  133.8 7.5 %collective-permute-start.16 = (bf16[32,3072]{1,0:T(8,128)(2,1)S(1)}, bf16[32,3072]{1,0:T(8,128)(2,1)S(1)}, u32[]{:S(2)}, u32[]{:S(2)}) collective-permute-start(bf16[32,3072]{1,0:T(8,128)(2,1)S(1)} %get-tuple-element.26), channel_id=1, source_target_pairs={{0,1},{2,0},{4,2},{6,4},{7,6},{5,7},{3,5},{1,3},{8,9},{10,8},{12,1... | collective-permute-start | bytes 589832 | tf_op jit(solution)/shard_map/ppermute | solution.py:46
  139.1 7.7 %collective-permute-start.17 = (bf16[32,3072]{1,0:T(8,128)(2,1)S(1)}, bf16[32,3072]{1,0:T(8,128)(2,1)S(1)}, u32[]{:S(2)}, u32[]{:S(2)}) collective-permute-start(bf16[32,3072]{1,0:T(8,128)(2,1)S(1)} %collective-permute-done.15), channel_id=1, source_target_pairs={{0,2},{2,4},{4,6},{6,7},{7,5},{5,3},{3,1},{1,0},{8,10},{10,12},{12... | collective-permute-start | bytes 589832 | tf_op jit(solution)/shard_map/ppermute | solution.py:43
  141.3 6.7 %collective-permute-start.18 = (bf16[32,3072]{1,0:T(8,128)(2,1)S(1)}, bf16[32,3072]{1,0:T(8,128)(2,1)S(1)}, u32[]{:S(2)}, u32[]{:S(2)}) collective-permute-start(bf16[32,3072]{1,0:T(8,128)(2,1)S(1)} %collective-permute-done.16), channel_id=1, source_target_pairs={{0,1},{2,0},{4,2},{6,4},{7,6},{5,7},{3,5},{1,3},{8,9},{10,8},{12,1... | collective-permute-start | bytes 589832 | tf_op jit(solution)/shard_map/ppermute | solution.py:46
  146.8 5.7 %collective-permute-start.19 = (bf16[32,3072]{1,0:T(8,128)(2,1)S(1)}, bf16[32,3072]{1,0:T(8,128)(2,1)S(1)}, u32[]{:S(2)}, u32[]{:S(2)}) collective-permute-start(bf16[32,3072]{1,0:T(8,128)(2,1)S(1)} %collective-permute-done.17), channel_id=1, source_target_pairs={{0,2},{2,4},{4,6},{6,7},{7,5},{5,3},{3,1},{1,0},{8,10},{10,12},{12... | collective-permute-start | bytes 589832 | tf_op jit(solution)/shard_map/ppermute | solution.py:43
  148.0 5.9 %collective-permute-start.20 = (bf16[32,3072]{1,0:T(8,128)(2,1)S(1)}, bf16[32,3072]{1,0:T(8,128)(2,1)S(1)}, u32[]{:S(2)}, u32[]{:S(2)}) collective-permute-start(bf16[32,3072]{1,0:T(8,128)(2,1)S(1)} %collective-permute-done.18), channel_id=1, source_target_pairs={{0,1},{2,0},{4,2},{6,4},{7,6},{5,7},{3,5},{1,3},{8,9},{10,8},{12,1... | collective-permute-start | bytes 589832 | tf_op jit(solution)/shard_map/ppermute | solution.py:46
  152.5 5.7 %collective-permute-start.21 = (bf16[32,3072]{1,0:T(8,128)(2,1)S(1)}, bf16[32,3072]{1,0:T(8,128)(2,1)S(1)}, u32[]{:S(2)}, u32[]{:S(2)}) collective-permute-start(bf16[32,3072]{1,0:T(8,128)(2,1)S(1)} %collective-permute-done.19), channel_id=1, source_target_pairs={{0,2},{2,4},{4,6},{6,7},{7,5},{5,3},{3,1},{1,0},{8,10},{10,12},{12... | collective-permute-start | bytes 589832 | tf_op jit(solution)/shard_map/ppermute | solution.py:43
  159.2 18.0 %collective-permute-start.22 = (bf16[128,3072]{1,0:T(8,128)(2,1)S(1)}, bf16[128,3072]{1,0:T(8,128)(2,1)}, u32[]{:S(2)}, u32[]{:S(2)}) collective-permute-start(bf16[128,3072]{1,0:T(8,128)(2,1)S(1)} %slice.105), channel_id=1, source_target_pairs={{0,8},{1,9},{2,10},{3,11},{4,12},{5,13},{6,14},{7,15},{16,24},{17,... | collective-permute-start | bytes 2359304 | tf_op jit(solution)/shard_map/ppermute | solution.py:12
  168.6 5.5 %slice-start = ((s8[4718592]{0:T(1024)(128)(4,1)}), s8[4194304]{0:T(1024)(128)(4,1)S(1)}, s32[]{:S(2)}) async-start(s8[4718592]{0:T(1024)(128)(4,1)} %bitcast.139), calls=%async_computation | async-start | bytes 8388608
  168.6 5.5 %slice-start.1 = ((s8[4718592]{0:T(1024)(128)(4,1)}), s8[524288]{0:T(1024)(128)(4,1)S(1)}, s32[]{:S(2)}) async-start(s8[4718592]{0:T(1024)(128)(4,1)} %bitcast.139), calls=%async_computation.1 | async-start | bytes 1048576
  177.2 4.3 %copy-start.2 = (bf16[384,8,2,384]{3,1,2,0:T(8,128)(2,1)S(1)}, bf16[384,8,2,384]{3,1,2,0:T(8,128)(2,1)}, u32[]{:S(2)}) copy-start(bf16[384,8,2,384]{3,1,2,0:T(8,128)(2,1)} %copy.26) | copy-start | bytes 14155780
  177.2 7.8 %slice-start.6 = ((s8[4718592]{0:T(1024)(128)(4,1)}), s8[4194304]{0:T(1024)(128)(4,1)S(1)}, s32[]{:S(2)}) async-start(s8[4718592]{0:T(1024)(128)(4,1)} %bitcast.160), calls=%async_computation.6 | async-start | bytes 8388608
  177.2 9.3 %slice-start.10 = ((s8[4718592]{0:T(1024)(128)(4,1)}), s8[4194304]{0:T(1024)(128)(4,1)S(1)}, s32[]{:S(2)}) async-start(s8[4718592]{0:T(1024)(128)(4,1)} %bitcast.183), calls=%async_computation.10 | async-start | bytes 8388608
  181.5 5.1 %slice-start.11 = ((s8[4718592]{0:T(1024)(128)(4,1)}), s8[524288]{0:T(1024)(128)(4,1)S(1)}, s32[]{:S(2)}) async-start(s8[4718592]{0:T(1024)(128)(4,1)} %bitcast.183), calls=%async_computation.11 | async-start | bytes 1048576
  187.7 7.3 %collective-permute-start.23 = (bf16[32,3072]{1,0:T(8,128)(2,1)S(1)}, bf16[32,3072]{1,0:T(8,128)(2,1)S(1)}, u32[]{:S(2)}, u32[]{:S(2)}) collective-permute-start(bf16[32,3072]{1,0:T(8,128)(2,1)S(1)} %get-tuple-element.41), channel_id=1, source_target_pairs={{0,2},{2,4},{4,6},{6,7},{7,5},{5,3},{3,1},{1,0},{8,10},{10,12},{12... | collective-permute-start | bytes 589832 | tf_op jit(solution)/shard_map/ppermute | solution.py:69
  195.0 6.5 %collective-permute-start.24 = (bf16[32,3072]{1,0:T(8,128)(2,1)S(1)}, bf16[32,3072]{1,0:T(8,128)(2,1)S(1)}, u32[]{:S(2)}, u32[]{:S(2)}) collective-permute-start(bf16[32,3072]{1,0:T(8,128)(2,1)S(1)} %fusion.57), channel_id=1, source_target_pairs={{0,2},{2,4},{4,6},{6,7},{7,5},{5,3},{3,1},{1,0},{8,10},{10,12},{12... | collective-permute-start | bytes 589832 | tf_op jit(solution)/shard_map/ppermute | solution.py:69
  196.5 5.9 %collective-permute-start.27 = (bf16[32,3072]{1,0:T(8,128)(2,1)S(1)}, bf16[32,3072]{1,0:T(8,128)(2,1)S(1)}, u32[]{:S(2)}, u32[]{:S(2)}) collective-permute-start(bf16[32,3072]{1,0:T(8,128)(2,1)S(1)} %get-tuple-element.42), channel_id=1, source_target_pairs={{0,1},{2,0},{4,2},{6,4},{7,6},{5,7},{3,5},{1,3},{8,9},{10,8},{12,1... | collective-permute-start | bytes 589832 | tf_op jit(solution)/shard_map/ppermute | solution.py:74
  201.6 8.5 %collective-permute-start.25 = (bf16[32,3072]{1,0:T(8,128)(2,1)S(1)}, bf16[32,3072]{1,0:T(8,128)(2,1)S(1)}, u32[]{:S(2)}, u32[]{:S(2)}) collective-permute-start(bf16[32,3072]{1,0:T(8,128)(2,1)S(1)} %fusion.58), channel_id=1, source_target_pairs={{0,2},{2,4},{4,6},{6,7},{7,5},{5,3},{3,1},{1,0},{8,10},{10,12},{12... | collective-permute-start | bytes 589832 | tf_op jit(solution)/shard_map/ppermute | solution.py:69
  210.2 7.2 %collective-permute-start.28 = (bf16[32,3072]{1,0:T(8,128)(2,1)S(1)}, bf16[32,3072]{1,0:T(8,128)(2,1)S(1)}, u32[]{:S(2)}, u32[]{:S(2)}) collective-permute-start(bf16[32,3072]{1,0:T(8,128)(2,1)S(1)} %get-tuple-element.40), channel_id=1, source_target_pairs={{0,1},{2,0},{4,2},{6,4},{7,6},{5,7},{3,5},{1,3},{8,9},{10,8},{12,1... | collective-permute-start | bytes 589832 | tf_op jit(solution)/shard_map/ppermute | solution.py:74
  212.3 7.7 %collective-permute-start.26 = (bf16[32,3072]{1,0:T(8,128)(2,1)S(1)}, bf16[32,3072]{1,0:T(8,128)(2,1)S(1)}, u32[]{:S(2)}, u32[]{:S(2)}) collective-permute-start(bf16[32,3072]{1,0:T(8,128)(2,1)S(1)} %get-tuple-element.39), channel_id=1, source_target_pairs={{0,2},{2,4},{4,6},{6,7},{7,5},{5,3},{3,1},{1,0},{8,10},{10,12},{12... | collective-permute-start | bytes 589832 | tf_op jit(solution)/shard_map/ppermute | solution.py:69
  217.5 5.7 %collective-permute-start.29 = (bf16[32,3072]{1,0:T(8,128)(2,1)S(1)}, bf16[32,3072]{1,0:T(8,128)(2,1)S(1)}, u32[]{:S(2)}, u32[]{:S(2)}) collective-permute-start(bf16[32,3072]{1,0:T(8,128)(2,1)S(1)} %fusion.56), channel_id=1, source_target_pairs={{0,1},{2,0},{4,2},{6,4},{7,6},{5,7},{3,5},{1,3},{8,9},{10,8},{12,1... | collective-permute-start | bytes 589832 | tf_op jit(solution)/shard_map/ppermute | solution.py:74
  223.5 6.8 %collective-permute-start.30 = (bf16[32,3072]{1,0:T(8,128)(2,1)S(1)}, bf16[32,3072]{1,0:T(8,128)(2,1)S(1)}, u32[]{:S(2)}, u32[]{:S(2)}) collective-permute-start(bf16[32,3072]{1,0:T(8,128)(2,1)S(1)} %get-tuple-element.24), channel_id=1, source_target_pairs={{0,2},{2,4},{4,6},{6,7},{7,5},{5,3},{3,1},{1,0},{8,10},{10,12},{12... | collective-permute-start | bytes 589832 | tf_op jit(solution)/shard_map/ppermute | solution.py:43
  227.8 5.7 %collective-permute-start.31 = (bf16[32,3072]{1,0:T(8,128)(2,1)S(1)}, bf16[32,3072]{1,0:T(8,128)(2,1)S(1)}, u32[]{:S(2)}, u32[]{:S(2)}) collective-permute-start(bf16[32,3072]{1,0:T(8,128)(2,1)S(1)} %get-tuple-element.24), channel_id=1, source_target_pairs={{0,1},{2,0},{4,2},{6,4},{7,6},{5,7},{3,5},{1,3},{8,9},{10,8},{12,1... | collective-permute-start | bytes 589832 | tf_op jit(solution)/shard_map/ppermute | solution.py:46
  230.3 5.7 %collective-permute-start.32 = (bf16[32,3072]{1,0:T(8,128)(2,1)S(1)}, bf16[32,3072]{1,0:T(8,128)(2,1)S(1)}, u32[]{:S(2)}, u32[]{:S(2)}) collective-permute-start(bf16[32,3072]{1,0:T(8,128)(2,1)S(1)} %collective-permute-done.30), channel_id=1, source_target_pairs={{0,2},{2,4},{4,6},{6,7},{7,5},{5,3},{3,1},{1,0},{8,10},{10,12},{12... | collective-permute-start | bytes 589832 | tf_op jit(solution)/shard_map/ppermute | solution.py:43
  233.5 5.7 %collective-permute-start.33 = (bf16[32,3072]{1,0:T(8,128)(2,1)S(1)}, bf16[32,3072]{1,0:T(8,128)(2,1)S(1)}, u32[]{:S(2)}, u32[]{:S(2)}) collective-permute-start(bf16[32,3072]{1,0:T(8,128)(2,1)S(1)} %collective-permute-done.31), channel_id=1, source_target_pairs={{0,1},{2,0},{4,2},{6,4},{7,6},{5,7},{3,5},{1,3},{8,9},{10,8},{12,1... | collective-permute-start | bytes 589832 | tf_op jit(solution)/shard_map/ppermute | solution.py:46
  236.0 5.7 %collective-permute-start.34 = (bf16[32,3072]{1,0:T(8,128)(2,1)S(1)}, bf16[32,3072]{1,0:T(8,128)(2,1)S(1)}, u32[]{:S(2)}, u32[]{:S(2)}) collective-permute-start(bf16[32,3072]{1,0:T(8,128)(2,1)S(1)} %collective-permute-done.32), channel_id=1, source_target_pairs={{0,2},{2,4},{4,6},{6,7},{7,5},{5,3},{3,1},{1,0},{8,10},{10,12},{12... | collective-permute-start | bytes 589832 | tf_op jit(solution)/shard_map/ppermute | solution.py:43
  236.1 12.0 %copy-start.3 = (bf16[3072,3,1,128]{0,3,1,2:T(8,128)(2,1)S(1)}, bf16[3072,3,1,128]{0,3,1,2:T(8,128)(2,1)}, u32[]{:S(2)}) copy-start(bf16[3072,3,1,128]{0,3,1,2:T(8,128)(2,1)} %copy.20) | copy-start | bytes 7077892
  236.1 12.0 %copy-start.5 = (f32[1,3072]{1,0:T(1,128)S(1)}, f32[1,3072]{1,0:T(1,128)}, u32[]{:S(2)}) copy-start(f32[1,3072]{1,0:T(1,128)} %get-tuple-element.50) | copy-start | bytes 36868
  239.2 5.7 %collective-permute-start.35 = (bf16[32,3072]{1,0:T(8,128)(2,1)S(1)}, bf16[32,3072]{1,0:T(8,128)(2,1)S(1)}, u32[]{:S(2)}, u32[]{:S(2)}) collective-permute-start(bf16[32,3072]{1,0:T(8,128)(2,1)S(1)} %collective-permute-done.33), channel_id=1, source_target_pairs={{0,1},{2,0},{4,2},{6,4},{7,6},{5,7},{3,5},{1,3},{8,9},{10,8},{12,1... | collective-permute-start | bytes 589832 | tf_op jit(solution)/shard_map/ppermute | solution.py:46
  241.7 5.9 %collective-permute-start.36 = (bf16[32,3072]{1,0:T(8,128)(2,1)S(1)}, bf16[32,3072]{1,0:T(8,128)(2,1)S(1)}, u32[]{:S(2)}, u32[]{:S(2)}) collective-permute-start(bf16[32,3072]{1,0:T(8,128)(2,1)S(1)} %collective-permute-done.34), channel_id=1, source_target_pairs={{0,2},{2,4},{4,6},{6,7},{7,5},{5,3},{3,1},{1,0},{8,10},{10,12},{12... | collective-permute-start | bytes 589832 | tf_op jit(solution)/shard_map/ppermute | solution.py:43
  249.4 2.7 collective-permute-start.37
  250.7 2.2 collective-permute-start.38
  254.9 6.2 %collective-permute-start.39 = (bf16[32,3072]{1,0:T(8,128)(2,1)S(1)}, bf16[32,3072]{1,0:T(8,128)(2,1)S(1)}, u32[]{:S(2)}, u32[]{:S(2)}) collective-permute-start(bf16[32,3072]{1,0:T(8,128)(2,1)S(1)} %get-tuple-element.37), channel_id=1, source_target_pairs={{0,2},{2,4},{4,6},{6,7},{7,5},{5,3},{3,1},{1,0},{8,10},{10,12},{12... | collective-permute-start | bytes 589832 | tf_op jit(solution)/shard_map/ppermute | solution.py:69
  261.2 7.8 %collective-permute-start.40 = (bf16[32,3072]{1,0:T(8,128)(2,1)S(1)}, bf16[32,3072]{1,0:T(8,128)(2,1)S(1)}, u32[]{:S(2)}, u32[]{:S(2)}) collective-permute-start(bf16[32,3072]{1,0:T(8,128)(2,1)S(1)} %fusion.49), channel_id=1, source_target_pairs={{0,2},{2,4},{4,6},{6,7},{7,5},{5,3},{3,1},{1,0},{8,10},{10,12},{12... | collective-permute-start | bytes 589832 | tf_op jit(solution)/shard_map/ppermute | solution.py:69
  261.3 7.8 %collective-permute-start.43 = (bf16[32,3072]{1,0:T(8,128)(2,1)S(1)}, bf16[32,3072]{1,0:T(8,128)(2,1)S(1)}, u32[]{:S(2)}, u32[]{:S(2)}) collective-permute-start(bf16[32,3072]{1,0:T(8,128)(2,1)S(1)} %get-tuple-element.38), channel_id=1, source_target_pairs={{0,1},{2,0},{4,2},{6,4},{7,6},{5,7},{3,5},{1,3},{8,9},{10,8},{12,1... | collective-permute-start | bytes 589832 | tf_op jit(solution)/shard_map/ppermute | solution.py:74
  269.0 7.5 %collective-permute-start.41 = (bf16[32,3072]{1,0:T(8,128)(2,1)S(1)}, bf16[32,3072]{1,0:T(8,128)(2,1)S(1)}, u32[]{:S(2)}, u32[]{:S(2)}) collective-permute-start(bf16[32,3072]{1,0:T(8,128)(2,1)S(1)} %fusion.50), channel_id=1, source_target_pairs={{0,2},{2,4},{4,6},{6,7},{7,5},{5,3},{3,1},{1,0},{8,10},{10,12},{12... | collective-permute-start | bytes 589832 | tf_op jit(solution)/shard_map/ppermute | solution.py:69
  276.7 6.5 %collective-permute-start.44 = (bf16[32,3072]{1,0:T(8,128)(2,1)S(1)}, bf16[32,3072]{1,0:T(8,128)(2,1)S(1)}, u32[]{:S(2)}, u32[]{:S(2)}) collective-permute-start(bf16[32,3072]{1,0:T(8,128)(2,1)S(1)} %get-tuple-element.36), channel_id=1, source_target_pairs={{0,1},{2,0},{4,2},{6,4},{7,6},{5,7},{3,5},{1,3},{8,9},{10,8},{12,1... | collective-permute-start | bytes 589832 | tf_op jit(solution)/shard_map/ppermute | solution.py:74
  278.5 6.3 %collective-permute-start.42 = (bf16[32,3072]{1,0:T(8,128)(2,1)S(1)}, bf16[32,3072]{1,0:T(8,128)(2,1)S(1)}, u32[]{:S(2)}, u32[]{:S(2)}) collective-permute-start(bf16[32,3072]{1,0:T(8,128)(2,1)S(1)} %get-tuple-element.35), channel_id=1, source_target_pairs={{0,2},{2,4},{4,6},{6,7},{7,5},{5,3},{3,1},{1,0},{8,10},{10,12},{12... | collective-permute-start | bytes 589832 | tf_op jit(solution)/shard_map/ppermute | solution.py:69
  283.2 5.7 %collective-permute-start.45 = (bf16[32,3072]{1,0:T(8,128)(2,1)S(1)}, bf16[32,3072]{1,0:T(8,128)(2,1)S(1)}, u32[]{:S(2)}, u32[]{:S(2)}) collective-permute-start(bf16[32,3072]{1,0:T(8,128)(2,1)S(1)} %fusion.48), channel_id=1, source_target_pairs={{0,1},{2,0},{4,2},{6,4},{7,6},{5,7},{3,5},{1,3},{8,9},{10,8},{12,1... | collective-permute-start | bytes 589832 | tf_op jit(solution)/shard_map/ppermute | solution.py:74
  (1 other events, 3.6 us)

commit v2 on v1

--- a/solution.py
+++ b/solution.py
@@ -96,16 +96,15 @@
     border_rows = 2 * LARGEST_DILATION
     before = shifted(hidden[all_rows - border_rows :], "blk", 1)
     padded = jnp.concatenate([before, hidden], axis=0)
-    pre_act = jnp.zeros((all_rows, 2 * own_width), jnp.float32)
+    by_half = jnp.transpose(kernel, (0, 2, 1, 3))
+    filt = jnp.zeros((all_rows, own_width), jnp.float32)
+    gate = jnp.zeros((all_rows, own_width), jnp.float32)
     for tap_idx in range(3):
         start = border_rows - tap_idx * dilation_factor
         slab = lax.dynamic_slice_in_dim(padded, start, all_rows, 0)
-        pre_act = pre_act + jnp.dot(
-            slab, kernel[tap_idx].reshape(width, 2 * own_width), preferred_element_type=jnp.float32
-        )
-    return (jnp.tanh(pre_act[:, :own_width]) * jax.nn.sigmoid(pre_act[:, own_width:])).astype(
-        jnp.bfloat16
-    )
+        filt = filt + jnp.dot(slab, by_half[tap_idx, 0], preferred_element_type=jnp.float32)
+        gate = gate + jnp.dot(slab, by_half[tap_idx, 1], preferred_element_type=jnp.float32)
+    return (jnp.tanh(filt) * jax.nn.sigmoid(gate)).astype(jnp.bfloat16)
 
 
 def conv_share(gated, weight, tok_rows):
@@ -165,7 +164,6 @@
     width = stream.shape[1]
     head_size = w_qkv.shape[3]
     layers = w_conv.shape[0]
-    qkv_weight = w_qkv.reshape(width, 3 * head_size)
     share = stream
     state = ring_gather(stream, "head")
     for layer_idx in range(layers):
@@ -177,12 +175,11 @@
         state = ring_gather(share, "head")
     all_rows = state.shape[0]
     attn_in = normed(state, gains[layers])
-    projected = jnp.dot(attn_in, qkv_weight, preferred_element_type=jnp.float32).astype(
-        jnp.bfloat16
-    )
-    queries = projected[:, :head_size]
-    keys_own = projected[:, head_size : 2 * head_size]
-    values_own = projected[:, 2 * head_size :]
+    qkv_parts = jnp.transpose(w_qkv[:, :, 0, :], (1, 0, 2))
+    queries, keys_own, values_own = (
+        jnp.dot(attn_in, qkv_parts[i], preferred_element_type=jnp.float32).astype(jnp.bfloat16)
+        for i in range(3)
+    )
     keys_prev, values_prev = shifted((keys_own, values_own), "blk", 1)
     own_part = attend(queries, keys_own, values_own, True)
     crossing_portion = lax.cond(

time: 291 us -> 310 us (1.065)
  matrix products: 22.8 us -> 39.2 us
  local copies, waits for them, and re-layouts: 64.8 us -> 60.5 us
  other arithmetic: 4.71 us -> 8.4 us
    ppermute x12, waiting for transfers between devices: 29.1 us -> 43.7 us  [ring_gather(): fwd = lax.ppermute(fwd, axis, forward)]
    dot_general x3, matrix products: 2.81 us -> 12 us  [rounded_term(): term = jnp.dot(left, right, preferred_element_type=jnp.float32)]
    ppermute x9, waiting for transfers between devices: 9.3 us -> 0.26 us  [ring_gather(): bwd = lax.ppermute(bwd, axis, backward)]
    ppermute x9, starting transfers between devices: 12.5 us -> 4.98 us  [ring_gather(): bwd = lax.ppermute(bwd, axis, backward)]
    dot_general x7 -> x13, matrix products: 19.7 us -> 27 us  [the longest x6 15 us: convolution_gate(): jnp.dot(slab, by_half[tap_idx, 1], preferred_element_type=jnp.float32)]
    ppermute x12, waiting for transfers between devices: 45.4 us -> 39.9 us  [ring_scatter_sum(): fwd = lax.ppermute(part.astype(value.dtype), axis, forward)]
    ppermute x12, starting transfers between devices: 10.1 us -> 14.7 us  [ring_scatter_sum(): fwd = lax.ppermute(part.astype(value.dtype), axis, forward)]
    ppermute x12, starting transfers between devices: 15.4 us -> 19.2 us  [ring_gather(): fwd = lax.ppermute(fwd, axis, forward)]
  transfers between devices with their start and end apart: 46 -> 46, of which waited for: 30 -> 30; matrix products, arithmetic and copies ran while one was open for 22% -> 19% of each run, Pallas kernels for 0% -> 0%
where the time goes in v2:
time: 310 us; the launch traced here: 308 us
  waiting for transfers between devices  108 us (35%)
  local copies, waits for them, and re-layouts  60.5 us (20%)
  starting transfers between devices  60.1 us (19%)
  matrix products  39.2 us (13%)
  between operations  32.5 us (10%)
  other arithmetic  8.4 us (3%)
    ppermute x12, waiting for transfers between devices, ring_gather(): fwd = lax.ppermute(fwd, axis, forward)  43.7 us
    ppermute x12, waiting for transfers between devices, ring_scatter_sum(): fwd = lax.ppermute(part.astype(value.dtype), axis, forward)  39.9 us
    unnamed x20, local copies, waits for them, and re-layouts  28.8 us
    ppermute x9, waiting for transfers between devices, ring_scatter_sum(): bwd = lax.ppermute(part.astype(value.dtype), axis, backward)  22.9 us
    slice x1, local copies, waits for them, and re-layouts, per_device(): w_conv[layer_idx]  22.7 us
    ppermute x12, starting transfers between devices, ring_gather(): fwd = lax.ppermute(fwd, axis, forward)  19.2 us
    dot_general x6, matrix products, convolution_gate(): jnp.dot(slab, by_half[tap_idx, 1], preferred_element_type=jnp.float32)  15 us
    ppermute x12, starting transfers between devices, ring_scatter_sum(): fwd = lax.ppermute(part.astype(value.dtype), axis, forward)  14.7 us
  transfers between devices with their start and end apart: 46, of which 30 were waited for; matrix products, arithmetic and copies ran while one was open for 19% of the time, Pallas kernels for 0%

profile of v2, /device:TPU:0, one launch (start us, length us, event | category | flops | bytes accessed | tf_op | source)
XLA Modules:
  0.0 308.3 jit_solution(7859607963917421321)
XLA Ops:
  0.0 3.0 collective-permute-start
  12.8 1.7 fusion.113
  19.6 1.5 fusion.112
  21.4 2.1 collective-permute-start.2
  23.5 4.3 %collective-permute-done.2 = bf16[32,3072]{1,0:T(8,128)(2,1)S(1)} collective-permute-done((bf16[32,3072]{1,0:T(8,128)(2,1)S(1)}, bf16[32,3072]{1,0:T(8,128)(2,1)S(1)}, u32[]{:S(2)}, u32[]{:S(2)}) %collective-permute-start.2) | collective-permute-done | bytes 196640 | tf_op jit(solution)/shard_map/ppermute | solution.py:43
  27.8 1.7 collective-permute-start.4
  29.9 3.6 %collective-permute-done.4 = bf16[32,3072]{1,0:T(8,128)(2,1)S(1)} collective-permute-done((bf16[32,3072]{1,0:T(8,128)(2,1)S(1)}, bf16[32,3072]{1,0:T(8,128)(2,1)S(1)}, u32[]{:S(2)}, u32[]{:S(2)}) %collective-permute-start.4) | collective-permute-done | bytes 196640 | tf_op jit(solution)/shard_map/ppermute | solution.py:43
  33.5 1.9 collective-permute-start.6
  35.4 3.7 %collective-permute-done.6 = bf16[32,3072]{1,0:T(8,128)(2,1)S(1)} collective-permute-done((bf16[32,3072]{1,0:T(8,128)(2,1)S(1)}, bf16[32,3072]{1,0:T(8,128)(2,1)S(1)}, u32[]{:S(2)}, u32[]{:S(2)}) %collective-permute-start.6) | collective-permute-done | bytes 196640 | tf_op jit(solution)/shard_map/ppermute | solution.py:43
  40.2 2.2 collective-permute-start.7
  42.4 22.7 %fusion.111 = (bf16[1,3,3072,2,384]{4,3,2,1,0:T(2,128)(2,1)}, bf16[1,3,3072,2,384]{4,3,2,1,0:T(2,128)(2,1)}) fusion(bf16[2,3,3072,2,384]{4,3,2,1,0:T(2,128)(2,1)} %param.24), kind=kLoop, calls=%fused_computation.188 | loop fusion | bytes 56623104 | tf_op jit(solution)/shard_map/slice | solution.py:171
  70.0 14.1 %copy.27 = bf16[1,3,3072,2,384]{4,2,3,1,0:T(8,128)(2,1)} copy(bf16[1,3,3072,2,384]{4,3,2,1,0:T(2,128)(2,1)} %get-tuple-element.29) | data formatting | bytes 28311552
  85.3 2.9 fusion.21
  88.3 3.5 %fusion.20 = f32[256,384]{1,0:T(8,128)S(1)} fusion(bf16[3,2,3072,384]{3,2,1,0:T(8,128)(2,1)} %bitcast.225, s32[]{:T(128)S(6)} %select_n.521, bf16[256,3072]{1,0:T(8,128)(2,1)S(1)} %fusion.7, bf16[128,3072]{1,0:T(8,128)(2,1)} %collective-permute-done.7), kind=kOutput, calls=%fused_computation.47 | convolution fusion | flops 607125504 | bytes 5111812 | tf_op jit(solution)/shard_map/dot_general | solution.py:106
  93.0 2.0 fusion.24
  95.1 2.8 fusion.23
  97.9 5.7 %convolution_convert_fusion.2 = bf16[256,3072]{1,0:T(8,128)(2,1)} fusion(bf16[2,384,3072]{2,1,0:T(8,128)(2,1)} %param.25, f32[256,384]{1,0:T(8,128)S(1)} %fusion.56, f32[256,384]{1,0:T(8,128)} %fusion.23, f32[256,384]{1,0:T(8,128)S(1)} %fusion.24, bf16[256,3072]{1,0:T(8,128)(2,1)S(1)} %fusion.7, bf16[3,2,3072,384]{3,2,1,0:T(8,128)(2,1)} %bitcast.226), kind=kOutput, calls=%fused_computation.16 | convolution fusion | flops 1209139200 | bytes 9043968 | tf_op jit(solution)/shard_map/dot_general | solution.py:88
  104.7 1.9 collective-permute-start.8
  108.7 3.8 %collective-permute-done.8 = bf16[32,3072]{1,0:T(8,128)(2,1)S(1)} collective-permute-done((bf16[32,3072]{1,0:T(8,128)(2,1)S(1)}, bf16[32,3072]{1,0:T(8,128)(2,1)S(1)}, u32[]{:S(2)}, u32[]{:S(2)}) %collective-permute-start.8) | collective-permute-done | bytes 196640 | tf_op jit(solution)/shard_map/ppermute | solution.py:69
  113.5 1.7 collective-permute-start.9
  117.3 3.2 %collective-permute-done.9 = bf16[32,3072]{1,0:T(8,128)(2,1)S(1)} collective-permute-done((bf16[32,3072]{1,0:T(8,128)(2,1)S(1)}, bf16[32,3072]{1,0:T(8,128)(2,1)S(1)}, u32[]{:S(2)}, u32[]{:S(2)}) %collective-permute-start.9) | collective-permute-done | bytes 196640 | tf_op jit(solution)/shard_map/ppermute | solution.py:69
  121.5 1.5 collective-permute-start.10
  126.7 2.3 collective-permute-done.10
  133.2 2.9 collective-permute-done.13
  136.2 2.0 collective-permute-start.14
  140.1 3.7 %collective-permute-done.14 = bf16[32,3072]{1,0:T(8,128)(2,1)S(1)} collective-permute-done((bf16[32,3072]{1,0:T(8,128)(2,1)S(1)}, bf16[32,3072]{1,0:T(8,128)(2,1)S(1)}, u32[]{:S(2)}, u32[]{:S(2)}) %collective-permute-start.14) | collective-permute-done | bytes 196640 | tf_op jit(solution)/shard_map/ppermute | solution.py:74
  144.1 1.7 collective-permute-start.15
  146.2 5.5 %collective-permute-done.15 = bf16[32,3072]{1,0:T(8,128)(2,1)S(1)} collective-permute-done((bf16[32,3072]{1,0:T(8,128)(2,1)S(1)}, bf16[32,3072]{1,0:T(8,128)(2,1)S(1)}, u32[]{:S(2)}, u32[]{:S(2)}) %collective-permute-start.15) | collective-permute-done | bytes 196640 | tf_op jit(solution)/shard_map/ppermute | solution.py:43
  152.4 1.4 collective-permute-start.18
  153.8 3.5 %collective-permute-done.17 = bf16[32,3072]{1,0:T(8,128)(2,1)S(1)} collective-permute-done((bf16[32,3072]{1,0:T(8,128)(2,1)S(1)}, bf16[32,3072]{1,0:T(8,128)(2,1)S(1)}, u32[]{:S(2)}, u32[]{:S(2)}) %collective-permute-start.17) | collective-permute-done | bytes 196640 | tf_op jit(solution)/shard_map/ppermute | solution.py:43
  159.5 3.5 %collective-permute-done.19 = bf16[32,3072]{1,0:T(8,128)(2,1)S(1)} collective-permute-done((bf16[32,3072]{1,0:T(8,128)(2,1)S(1)}, bf16[32,3072]{1,0:T(8,128)(2,1)S(1)}, u32[]{:S(2)}, u32[]{:S(2)}) %collective-permute-start.19) | collective-permute-done | bytes 196640 | tf_op jit(solution)/shard_map/ppermute | solution.py:43
  163.8 4.9 %collective-permute-done.21 = bf16[32,3072]{1,0:T(8,128)(2,1)S(1)} collective-permute-done((bf16[32,3072]{1,0:T(8,128)(2,1)S(1)}, bf16[32,3072]{1,0:T(8,128)(2,1)S(1)}, u32[]{:S(2)}, u32[]{:S(2)}) %collective-permute-start.21) | collective-permute-done | bytes 196640 | tf_op jit(solution)/shard_map/ppermute | solution.py:43
  169.7 2.2 collective-permute-start.22
  173.6 14.1 %copy.26 = bf16[1,3,3072,2,384]{4,2,3,1,0:T(8,128)(2,1)} copy(bf16[1,3,3072,2,384]{4,3,2,1,0:T(2,128)(2,1)} %get-tuple-element.30) | data formatting | bytes 28311552
  187.7 2.9 fusion.15
  190.7 3.6 %fusion.14 = f32[256,384]{1,0:T(8,128)S(1)} fusion(bf16[3,2,3072,384]{3,2,1,0:T(8,128)(2,1)} %bitcast.231, s32[]{:T(128)S(6)} %select_n.570, bf16[256,3072]{1,0:T(8,128)(2,1)S(1)} %fusion.10, bf16[128,3072]{1,0:T(8,128)(2,1)} %collective-permute-done.22), kind=kOutput, calls=%fused_computation.35 | convolution fusion | flops 607125504 | bytes 5111812 | tf_op jit(solution)/shard_map/dot_general | solution.py:106
  195.6 2.1 fusion.18
  197.7 3.0 fusion.17
  200.6 5.6 %convolution_convert_fusion.1 = bf16[256,3072]{1,0:T(8,128)(2,1)} fusion(bf16[2,384,3072]{2,1,0:T(8,128)(2,1)} %param.25, f32[256,384]{1,0:T(8,128)S(1)} %fusion.55, f32[256,384]{1,0:T(8,128)} %fusion.17, f32[256,384]{1,0:T(8,128)S(1)} %fusion.18, bf16[256,3072]{1,0:T(8,128)(2,1)S(1)} %fusion.10, bf16[3,2,3072,384]{3,2,1,0:T(8,128)(2,1)} %bitcast.232), kind=kOutput, calls=%fused_computation.15 | convolution fusion | flops 1209139200 | bytes 9043968 | tf_op jit(solution)/shard_map/dot_general | solution.py:88
  208.1 5.4 %collective-permute-done.23 = bf16[32,3072]{1,0:T(8,128)(2,1)S(1)} collective-permute-done((bf16[32,3072]{1,0:T(8,128)(2,1)S(1)}, bf16[32,3072]{1,0:T(8,128)(2,1)S(1)}, u32[]{:S(2)}, u32[]{:S(2)}) %collective-permute-start.23) | collective-permute-done | bytes 196640 | tf_op jit(solution)/shard_map/ppermute | solution.py:69
  217.0 3.6 %collective-permute-done.24 = bf16[32,3072]{1,0:T(8,128)(2,1)S(1)} collective-permute-done((bf16[32,3072]{1,0:T(8,128)(2,1)S(1)}, bf16[32,3072]{1,0:T(8,128)(2,1)S(1)}, u32[]{:S(2)}, u32[]{:S(2)}) %collective-permute-start.24) | collective-permute-done | bytes 196640 | tf_op jit(solution)/shard_map/ppermute | solution.py:69
  222.6 5.9 %collective-permute-done.25 = bf16[32,3072]{1,0:T(8,128)(2,1)S(1)} collective-permute-done((bf16[32,3072]{1,0:T(8,128)(2,1)S(1)}, bf16[32,3072]{1,0:T(8,128)(2,1)S(1)}, u32[]{:S(2)}, u32[]{:S(2)}) %collective-permute-start.25) | collective-permute-done | bytes 196640 | tf_op jit(solution)/shard_map/ppermute | solution.py:69
  228.6 3.0 collective-permute-start.28
  231.6 4.4 %collective-permute-done.28 = bf16[32,3072]{1,0:T(8,128)(2,1)S(1)} collective-permute-done((bf16[32,3072]{1,0:T(8,128)(2,1)S(1)}, bf16[32,3072]{1,0:T(8,128)(2,1)S(1)}, u32[]{:S(2)}, u32[]{:S(2)}) %collective-permute-start.28) | collective-permute-done | bytes 196640 | tf_op jit(solution)/shard_map/ppermute | solution.py:74
  236.0 2.5 collective-permute-start.29
  238.5 3.2 %collective-permute-done.29 = bf16[32,3072]{1,0:T(8,128)(2,1)S(1)} collective-permute-done((bf16[32,3072]{1,0:T(8,128)(2,1)S(1)}, bf16[32,3072]{1,0:T(8,128)(2,1)S(1)}, u32[]{:S(2)}, u32[]{:S(2)}) %collective-permute-start.29) | collective-permute-done | bytes 196640 | tf_op jit(solution)/shard_map/ppermute | solution.py:74
  242.0 2.1 collective-permute-start.30
  244.6 3.6 %collective-permute-done.30 = bf16[32,3072]{1,0:T(8,128)(2,1)S(1)} collective-permute-done((bf16[32,3072]{1,0:T(8,128)(2,1)S(1)}, bf16[32,3072]{1,0:T(8,128)(2,1)S(1)}, u32[]{:S(2)}, u32[]{:S(2)}) %collective-permute-start.30) | collective-permute-done | bytes 196640 | tf_op jit(solution)/shard_map/ppermute | solution.py:43
  248.2 1.6 collective-permute-start.32
  250.3 3.5 %collective-permute-done.32 = bf16[32,3072]{1,0:T(8,128)(2,1)S(1)} collective-permute-done((bf16[32,3072]{1,0:T(8,128)(2,1)S(1)}, bf16[32,3072]{1,0:T(8,128)(2,1)S(1)}, u32[]{:S(2)}, u32[]{:S(2)}) %collective-permute-start.32) | collective-permute-done | bytes 196640 | tf_op jit(solution)/shard_map/ppermute | solution.py:43
  253.9 1.6 collective-permute-start.34
  256.0 3.5 %collective-permute-done.34 = bf16[32,3072]{1,0:T(8,128)(2,1)S(1)} collective-permute-done((bf16[32,3072]{1,0:T(8,128)(2,1)S(1)}, bf16[32,3072]{1,0:T(8,128)(2,1)S(1)}, u32[]{:S(2)}, u32[]{:S(2)}) %collective-permute-start.34) | collective-permute-done | bytes 196640 | tf_op jit(solution)/shard_map/ppermute | solution.py:43
  259.5 1.6 collective-permute-start.36
  261.2 4.0 %collective-permute-done.36 = bf16[32,3072]{1,0:T(8,128)(2,1)S(1)} collective-permute-done((bf16[32,3072]{1,0:T(8,128)(2,1)S(1)}, bf16[32,3072]{1,0:T(8,128)(2,1)S(1)}, u32[]{:S(2)}, u32[]{:S(2)}) %collective-permute-start.36) | collective-permute-done | bytes 196640 | tf_op jit(solution)/shard_map/ppermute | solution.py:43
  273.5 1.6 collective-permute-start.39
  275.1 4.6 %collective-permute-done.39 = bf16[32,3072]{1,0:T(8,128)(2,1)S(1)} collective-permute-done((bf16[32,3072]{1,0:T(8,128)(2,1)S(1)}, bf16[32,3072]{1,0:T(8,128)(2,1)S(1)}, u32[]{:S(2)}, u32[]{:S(2)}) %collective-permute-start.39) | collective-permute-done | bytes 196640 | tf_op jit(solution)/shard_map/ppermute | solution.py:69
  279.8 1.9 collective-permute-start.40
  282.2 5.3 %collective-permute-done.40 = bf16[32,3072]{1,0:T(8,128)(2,1)S(1)} collective-permute-done((bf16[32,3072]{1,0:T(8,128)(2,1)S(1)}, bf16[32,3072]{1,0:T(8,128)(2,1)S(1)}, u32[]{:S(2)}, u32[]{:S(2)}) %collective-permute-start.40) | collective-permute-done | bytes 196640 | tf_op jit(solution)/shard_map/ppermute | solution.py:69
  287.6 1.8 collective-permute-start.41
  289.4 5.7 %collective-permute-done.41 = bf16[32,3072]{1,0:T(8,128)(2,1)S(1)} collective-permute-done((bf16[32,3072]{1,0:T(8,128)(2,1)S(1)}, bf16[32,3072]{1,0:T(8,128)(2,1)S(1)}, u32[]{:S(2)}, u32[]{:S(2)}) %collective-permute-start.41) | collective-permute-done | bytes 196640 | tf_op jit(solution)/shard_map/ppermute | solution.py:69
  295.2 1.8 collective-permute-start.44
  297.3 4.5 %collective-permute-done.44 = bf16[32,3072]{1,0:T(8,128)(2,1)S(1)} collective-permute-done((bf16[32,3072]{1,0:T(8,128)(2,1)S(1)}, bf16[32,3072]{1,0:T(8,128)(2,1)S(1)}, u32[]{:S(2)}, u32[]{:S(2)}) %collective-permute-start.44) | collective-permute-done | bytes 196640 | tf_op jit(solution)/shard_map/ppermute | solution.py:74
  301.8 1.5 collective-permute-start.45
  303.3 4.2 %collective-permute-done.45 = bf16[32,3072]{1,0:T(8,128)(2,1)S(1)} collective-permute-done((bf16[32,3072]{1,0:T(8,128)(2,1)S(1)}, bf16[32,3072]{1,0:T(8,128)(2,1)S(1)}, u32[]{:S(2)}, u32[]{:S(2)}) %collective-permute-start.45) | collective-permute-done | bytes 196640 | tf_op jit(solution)/shard_map/ppermute | solution.py:74
  (129 shorter events, 37.4 us)
Async XLA Ops:
  0.0 272.7 %copy-start = (bf16[1,128,3072]{2,1,0:T(8,128)(2,1)S(1)}, bf16[1,128,3072]{2,1,0:T(8,128)(2,1)}, u32[]{:S(2)}) copy-start(bf16[1,128,3072]{2,1,0:T(8,128)(2,1)} %param.27) | copy-start | bytes 2359300
  0.0 21.3 %copy-start.5 = (bf16[32,3072]{1,0:T(8,128)(2,1)S(1)}, bf16[32,3072]{1,0:T(8,128)(2,1)}, u32[]{:S(2)}) copy-start(bf16[32,3072]{1,0:T(8,128)(2,1)} %param.21) | copy-start | bytes 589828
  0.0 21.4 %collective-permute-start = (bf16[32,3072]{1,0:T(8,128)(2,1)}, bf16[32,3072]{1,0:T(8,128)(2,1)S(1)}, u32[]{:S(2)}, u32[]{:S(2)}) collective-permute-start(bf16[32,3072]{1,0:T(8,128)(2,1)} %param.21), channel_id=1, source_target_pairs={{0,2},{2,4},{4,6},{6,7},{7,5},{5,3},{3,1},{1,0},{8,10},{10,12},{12... | collective-permute-start | bytes 589832 | tf_op jit(solution)/shard_map/ppermute | solution.py:43
  3.0 20.4 %collective-permute-start.1 = (bf16[32,3072]{1,0:T(8,128)(2,1)}, bf16[32,3072]{1,0:T(8,128)(2,1)S(1)}, u32[]{:S(2)}, u32[]{:S(2)}) collective-permute-start(bf16[32,3072]{1,0:T(8,128)(2,1)} %param.21), channel_id=1, source_target_pairs={{0,1},{2,0},{4,2},{6,4},{7,6},{5,7},{3,5},{1,3},{8,9},{10,8},{12,1... | collective-permute-start | bytes 589832 | tf_op jit(solution)/shard_map/ppermute | solution.py:46
  21.4 6.4 %collective-permute-start.2 = (bf16[32,3072]{1,0:T(8,128)(2,1)S(1)}, bf16[32,3072]{1,0:T(8,128)(2,1)S(1)}, u32[]{:S(2)}, u32[]{:S(2)}) collective-permute-start(bf16[32,3072]{1,0:T(8,128)(2,1)S(1)} %collective-permute-done), channel_id=1, source_target_pairs={{0,2},{2,4},{4,6},{6,7},{7,5},{5,3},{3,1},{1,0},{8,10},{10,12},{12... | collective-permute-start | bytes 589832 | tf_op jit(solution)/shard_map/ppermute | solution.py:43
  23.5 6.1 %collective-permute-start.3 = (bf16[32,3072]{1,0:T(8,128)(2,1)S(1)}, bf16[32,3072]{1,0:T(8,128)(2,1)S(1)}, u32[]{:S(2)}, u32[]{:S(2)}) collective-permute-start(bf16[32,3072]{1,0:T(8,128)(2,1)S(1)} %collective-permute-done.1), channel_id=1, source_target_pairs={{0,1},{2,0},{4,2},{6,4},{7,6},{5,7},{3,5},{1,3},{8,9},{10,8},{12,1... | collective-permute-start | bytes 589832 | tf_op jit(solution)/shard_map/ppermute | solution.py:46
  27.8 5.7 %collective-permute-start.4 = (bf16[32,3072]{1,0:T(8,128)(2,1)S(1)}, bf16[32,3072]{1,0:T(8,128)(2,1)S(1)}, u32[]{:S(2)}, u32[]{:S(2)}) collective-permute-start(bf16[32,3072]{1,0:T(8,128)(2,1)S(1)} %collective-permute-done.2), channel_id=1, source_target_pairs={{0,2},{2,4},{4,6},{6,7},{7,5},{5,3},{3,1},{1,0},{8,10},{10,12},{12... | collective-permute-start | bytes 589832 | tf_op jit(solution)/shard_map/ppermute | solution.py:43
  29.6 5.8 %collective-permute-start.5 = (bf16[32,3072]{1,0:T(8,128)(2,1)S(1)}, bf16[32,3072]{1,0:T(8,128)(2,1)S(1)}, u32[]{:S(2)}, u32[]{:S(2)}) collective-permute-start(bf16[32,3072]{1,0:T(8,128)(2,1)S(1)} %collective-permute-done.3), channel_id=1, source_target_pairs={{0,1},{2,0},{4,2},{6,4},{7,6},{5,7},{3,5},{1,3},{8,9},{10,8},{12,1... | collective-permute-start | bytes 589832 | tf_op jit(solution)/shard_map/ppermute | solution.py:46
  33.5 5.7 %collective-permute-start.6 = (bf16[32,3072]{1,0:T(8,128)(2,1)S(1)}, bf16[32,3072]{1,0:T(8,128)(2,1)S(1)}, u32[]{:S(2)}, u32[]{:S(2)}) collective-permute-start(bf16[32,3072]{1,0:T(8,128)(2,1)S(1)} %collective-permute-done.4), channel_id=1, source_target_pairs={{0,2},{2,4},{4,6},{6,7},{7,5},{5,3},{3,1},{1,0},{8,10},{10,12},{12... | collective-permute-start | bytes 589832 | tf_op jit(solution)/shard_map/ppermute | solution.py:43
  40.1 25.0 %copy-start.7 = (s32[2]{0:T(128)S(1)}, s32[2]{0:T(128)}, u32[]{:S(2)}) copy-start(s32[2]{0:T(128)} %param.23) | copy-start | bytes 28
  40.2 45.2 %collective-permute-start.7 = (bf16[128,3072]{1,0:T(8,128)(2,1)S(1)}, bf16[128,3072]{1,0:T(8,128)(2,1)}, u32[]{:S(2)}, u32[]{:S(2)}) collective-permute-start(bf16[128,3072]{1,0:T(8,128)(2,1)S(1)} %slice.105), channel_id=1, source_target_pairs={{0,8},{1,9},{2,10},{3,11},{4,12},{5,13},{6,14},{7,15},{16,24},{17,... | collective-permute-start | bytes 2359304 | tf_op jit(solution)/shard_map/ppermute | solution.py:12
  85.3 6.6 %copy-start.1 = (bf16[1,3,3072,2,384]{4,2,3,1,0:T(8,128)(2,1)S(1)}, bf16[1,3,3072,2,384]{4,2,3,1,0:T(8,128)(2,1)}, u32[]{:S(2)}) copy-start(bf16[1,3,3072,2,384]{4,2,3,1,0:T(8,128)(2,1)} %copy.27) | copy-start | bytes 42467332
  103.5 25.4 %copy-start.3 = (bf16[256,3072]{1,0:T(8,128)(2,1)S(1)}, bf16[256,3072]{1,0:T(8,128)(2,1)}, u32[]{:S(2)}) copy-start(bf16[256,3072]{1,0:T(8,128)(2,1)} %convolution_convert_fusion.2) | copy-start | bytes 4718596
  104.7 7.8 %collective-permute-start.8 = (bf16[32,3072]{1,0:T(8,128)(2,1)S(1)}, bf16[32,3072]{1,0:T(8,128)(2,1)S(1)}, u32[]{:S(2)}, u32[]{:S(2)}) collective-permute-start(bf16[32,3072]{1,0:T(8,128)(2,1)S(1)} %get-tuple-element.41), channel_id=1, source_target_pairs={{0,2},{2,4},{4,6},{6,7},{7,5},{5,3},{3,1},{1,0},{8,10},{10,12},{12... | collective-permute-start | bytes 589832 | tf_op jit(solution)/shard_map/ppermute | solution.py:69
  113.5 7.0 %collective-permute-start.9 = (bf16[32,3072]{1,0:T(8,128)(2,1)S(1)}, bf16[32,3072]{1,0:T(8,128)(2,1)S(1)}, u32[]{:S(2)}, u32[]{:S(2)}) collective-permute-start(bf16[32,3072]{1,0:T(8,128)(2,1)S(1)} %fusion.76), channel_id=1, source_target_pairs={{0,2},{2,4},{4,6},{6,7},{7,5},{5,3},{3,1},{1,0},{8,10},{10,12},{12... | collective-permute-start | bytes 589832 | tf_op jit(solution)/shard_map/ppermute | solution.py:69
  116.9 9.8 %collective-permute-start.12 = (bf16[32,3072]{1,0:T(8,128)(2,1)S(1)}, bf16[32,3072]{1,0:T(8,128)(2,1)S(1)}, u32[]{:S(2)}, u32[]{:S(2)}) collective-permute-start(bf16[32,3072]{1,0:T(8,128)(2,1)S(1)} %get-tuple-element.42), channel_id=1, source_target_pairs={{0,1},{2,0},{4,2},{6,4},{7,6},{5,7},{3,5},{1,3},{8,9},{10,8},{12,1... | collective-permute-start | bytes 589832 | tf_op jit(solution)/shard_map/ppermute | solution.py:74
  121.5 7.5 %collective-permute-start.10 = (bf16[32,3072]{1,0:T(8,128)(2,1)S(1)}, bf16[32,3072]{1,0:T(8,128)(2,1)S(1)}, u32[]{:S(2)}, u32[]{:S(2)}) collective-permute-start(bf16[32,3072]{1,0:T(8,128)(2,1)S(1)} %fusion.77), channel_id=1, source_target_pairs={{0,2},{2,4},{4,6},{6,7},{7,5},{5,3},{3,1},{1,0},{8,10},{10,12},{12... | collective-permute-start | bytes 589832 | tf_op jit(solution)/shard_map/ppermute | solution.py:69
  129.0 7.1 %collective-permute-start.13 = (bf16[32,3072]{1,0:T(8,128)(2,1)S(1)}, bf16[32,3072]{1,0:T(8,128)(2,1)S(1)}, u32[]{:S(2)}, u32[]{:S(2)}) collective-permute-start(bf16[32,3072]{1,0:T(8,128)(2,1)S(1)} %get-tuple-element.40), channel_id=1, source_target_pairs={{0,1},{2,0},{4,2},{6,4},{7,6},{5,7},{3,5},{1,3},{8,9},{10,8},{12,1... | collective-permute-start | bytes 589832 | tf_op jit(solution)/shard_map/ppermute | solution.py:74
  132.2 7.8 %collective-permute-start.11 = (bf16[32,3072]{1,0:T(8,128)(2,1)S(1)}, bf16[32,3072]{1,0:T(8,128)(2,1)S(1)}, u32[]{:S(2)}, u32[]{:S(2)}) collective-permute-start(bf16[32,3072]{1,0:T(8,128)(2,1)S(1)} %get-tuple-element.39), channel_id=1, source_target_pairs={{0,2},{2,4},{4,6},{6,7},{7,5},{5,3},{3,1},{1,0},{8,10},{10,12},{12... | collective-permute-start | bytes 589832 | tf_op jit(solution)/shard_map/ppermute | solution.py:69
  136.2 7.6 %collective-permute-start.14 = (bf16[32,3072]{1,0:T(8,128)(2,1)S(1)}, bf16[32,3072]{1,0:T(8,128)(2,1)S(1)}, u32[]{:S(2)}, u32[]{:S(2)}) collective-permute-start(bf16[32,3072]{1,0:T(8,128)(2,1)S(1)} %fusion.75), channel_id=1, source_target_pairs={{0,1},{2,0},{4,2},{6,4},{7,6},{5,7},{3,5},{1,3},{8,9},{10,8},{12,1... | collective-permute-start | bytes 589832 | tf_op jit(solution)/shard_map/ppermute | solution.py:74
  144.1 7.6 %collective-permute-start.15 = (bf16[32,3072]{1,0:T(8,128)(2,1)S(1)}, bf16[32,3072]{1,0:T(8,128)(2,1)S(1)}, u32[]{:S(2)}, u32[]{:S(2)}) collective-permute-start(bf16[32,3072]{1,0:T(8,128)(2,1)S(1)} %get-tuple-element.26), channel_id=1, source_target_pairs={{0,2},{2,4},{4,6},{6,7},{7,5},{5,3},{3,1},{1,0},{8,10},{10,12},{12... | collective-permute-start | bytes 589832 | tf_op jit(solution)/shard_map/ppermute | solution.py:43
  145.8 6.6 %collective-permute-start.16 = (bf16[32,3072]{1,0:T(8,128)(2,1)S(1)}, bf16[32,3072]{1,0:T(8,128)(2,1)S(1)}, u32[]{:S(2)}, u32[]{:S(2)}) collective-permute-start(bf16[32,3072]{1,0:T(8,128)(2,1)S(1)} %get-tuple-element.26), channel_id=1, source_target_pairs={{0,1},{2,0},{4,2},{6,4},{7,6},{5,7},{3,5},{1,3},{8,9},{10,8},{12,1... | collective-permute-start | bytes 589832 | tf_op jit(solution)/shard_map/ppermute | solution.py:46
  151.7 5.7 %collective-permute-start.17 = (bf16[32,3072]{1,0:T(8,128)(2,1)S(1)}, bf16[32,3072]{1,0:T(8,128)(2,1)S(1)}, u32[]{:S(2)}, u32[]{:S(2)}) collective-permute-start(bf16[32,3072]{1,0:T(8,128)(2,1)S(1)} %collective-permute-done.15), channel_id=1, source_target_pairs={{0,2},{2,4},{4,6},{6,7},{7,5},{5,3},{3,1},{1,0},{8,10},{10,12},{12... | collective-permute-start | bytes 589832 | tf_op jit(solution)/shard_map/ppermute | solution.py:43
  152.4 5.7 %collective-permute-start.18 = (bf16[32,3072]{1,0:T(8,128)(2,1)S(1)}, bf16[32,3072]{1,0:T(8,128)(2,1)S(1)}, u32[]{:S(2)}, u32[]{:S(2)}) collective-permute-start(bf16[32,3072]{1,0:T(8,128)(2,1)S(1)} %collective-permute-done.16), channel_id=1, source_target_pairs={{0,1},{2,0},{4,2},{6,4},{7,6},{5,7},{3,5},{1,3},{8,9},{10,8},{12,1... | collective-permute-start | bytes 589832 | tf_op jit(solution)/shard_map/ppermute | solution.py:46
  157.4 5.7 %collective-permute-start.19 = (bf16[32,3072]{1,0:T(8,128)(2,1)S(1)}, bf16[32,3072]{1,0:T(8,128)(2,1)S(1)}, u32[]{:S(2)}, u32[]{:S(2)}) collective-permute-start(bf16[32,3072]{1,0:T(8,128)(2,1)S(1)} %collective-permute-done.17), channel_id=1, source_target_pairs={{0,2},{2,4},{4,6},{6,7},{7,5},{5,3},{3,1},{1,0},{8,10},{10,12},{12... | collective-permute-start | bytes 589832 | tf_op jit(solution)/shard_map/ppermute | solution.py:43
  158.1 5.7 %collective-permute-start.20 = (bf16[32,3072]{1,0:T(8,128)(2,1)S(1)}, bf16[32,3072]{1,0:T(8,128)(2,1)S(1)}, u32[]{:S(2)}, u32[]{:S(2)}) collective-permute-start(bf16[32,3072]{1,0:T(8,128)(2,1)S(1)} %collective-permute-done.18), channel_id=1, source_target_pairs={{0,1},{2,0},{4,2},{6,4},{7,6},{5,7},{3,5},{1,3},{8,9},{10,8},{12,1... | collective-permute-start | bytes 589832 | tf_op jit(solution)/shard_map/ppermute | solution.py:46
  163.0 5.7 %collective-permute-start.21 = (bf16[32,3072]{1,0:T(8,128)(2,1)S(1)}, bf16[32,3072]{1,0:T(8,128)(2,1)S(1)}, u32[]{:S(2)}, u32[]{:S(2)}) collective-permute-start(bf16[32,3072]{1,0:T(8,128)(2,1)S(1)} %collective-permute-done.19), channel_id=1, source_target_pairs={{0,2},{2,4},{4,6},{6,7},{7,5},{5,3},{3,1},{1,0},{8,10},{10,12},{12... | collective-permute-start | bytes 589832 | tf_op jit(solution)/shard_map/ppermute | solution.py:43
  169.7 18.0 %collective-permute-start.22 = (bf16[128,3072]{1,0:T(8,128)(2,1)S(1)}, bf16[128,3072]{1,0:T(8,128)(2,1)}, u32[]{:S(2)}, u32[]{:S(2)}) collective-permute-start(bf16[128,3072]{1,0:T(8,128)(2,1)S(1)} %slice.112), channel_id=1, source_target_pairs={{0,8},{1,9},{2,10},{3,11},{4,12},{5,13},{6,14},{7,15},{16,24},{17,... | collective-permute-start | bytes 2359304 | tf_op jit(solution)/shard_map/ppermute | solution.py:12
  187.7 6.8 %copy-start.2 = (bf16[1,3,3072,2,384]{4,2,3,1,0:T(8,128)(2,1)S(1)}, bf16[1,3,3072,2,384]{4,2,3,1,0:T(8,128)(2,1)}, u32[]{:S(2)}) copy-start(bf16[1,3,3072,2,384]{4,2,3,1,0:T(8,128)(2,1)} %copy.26) | copy-start | bytes 42467332
  206.2 22.3 %copy-start.4 = (bf16[256,3072]{1,0:T(8,128)(2,1)S(1)}, bf16[256,3072]{1,0:T(8,128)(2,1)}, u32[]{:S(2)}) copy-start(bf16[256,3072]{1,0:T(8,128)(2,1)} %convolution_convert_fusion.1) | copy-start | bytes 4718596
  207.4 6.2 %collective-permute-start.23 = (bf16[32,3072]{1,0:T(8,128)(2,1)S(1)}, bf16[32,3072]{1,0:T(8,128)(2,1)S(1)}, u32[]{:S(2)}, u32[]{:S(2)}) collective-permute-start(bf16[32,3072]{1,0:T(8,128)(2,1)S(1)} %get-tuple-element.37), channel_id=1, source_target_pairs={{0,2},{2,4},{4,6},{6,7},{7,5},{5,3},{3,1},{1,0},{8,10},{10,12},{12... | collective-permute-start | bytes 589832 | tf_op jit(solution)/shard_map/ppermute | solution.py:69
  214.6 6.0 %collective-permute-start.24 = (bf16[32,3072]{1,0:T(8,128)(2,1)S(1)}, bf16[32,3072]{1,0:T(8,128)(2,1)S(1)}, u32[]{:S(2)}, u32[]{:S(2)}) collective-permute-start(bf16[32,3072]{1,0:T(8,128)(2,1)S(1)} %fusion.68), channel_id=1, source_target_pairs={{0,2},{2,4},{4,6},{6,7},{7,5},{5,3},{3,1},{1,0},{8,10},{10,12},{12... | collective-permute-start | bytes 589832 | tf_op jit(solution)/shard_map/ppermute | solution.py:69
  215.7 6.8 %collective-permute-start.27 = (bf16[32,3072]{1,0:T(8,128)(2,1)S(1)}, bf16[32,3072]{1,0:T(8,128)(2,1)S(1)}, u32[]{:S(2)}, u32[]{:S(2)}) collective-permute-start(bf16[32,3072]{1,0:T(8,128)(2,1)S(1)} %get-tuple-element.38), channel_id=1, source_target_pairs={{0,1},{2,0},{4,2},{6,4},{7,6},{5,7},{3,5},{1,3},{8,9},{10,8},{12,1... | collective-permute-start | bytes 589832 | tf_op jit(solution)/shard_map/ppermute | solution.py:74
  221.5 6.9 %collective-permute-start.25 = (bf16[32,3072]{1,0:T(8,128)(2,1)S(1)}, bf16[32,3072]{1,0:T(8,128)(2,1)S(1)}, u32[]{:S(2)}, u32[]{:S(2)}) collective-permute-start(bf16[32,3072]{1,0:T(8,128)(2,1)S(1)} %fusion.69), channel_id=1, source_target_pairs={{0,2},{2,4},{4,6},{6,7},{7,5},{5,3},{3,1},{1,0},{8,10},{10,12},{12... | collective-permute-start | bytes 589832 | tf_op jit(solution)/shard_map/ppermute | solution.py:69
  228.6 7.4 %collective-permute-start.28 = (bf16[32,3072]{1,0:T(8,128)(2,1)S(1)}, bf16[32,3072]{1,0:T(8,128)(2,1)S(1)}, u32[]{:S(2)}, u32[]{:S(2)}) collective-permute-start(bf16[32,3072]{1,0:T(8,128)(2,1)S(1)} %get-tuple-element.36), channel_id=1, source_target_pairs={{0,1},{2,0},{4,2},{6,4},{7,6},{5,7},{3,5},{1,3},{8,9},{10,8},{12,1... | collective-permute-start | bytes 589832 | tf_op jit(solution)/shard_map/ppermute | solution.py:74
  231.6 7.0 %collective-permute-start.26 = (bf16[32,3072]{1,0:T(8,128)(2,1)S(1)}, bf16[32,3072]{1,0:T(8,128)(2,1)S(1)}, u32[]{:S(2)}, u32[]{:S(2)}) collective-permute-start(bf16[32,3072]{1,0:T(8,128)(2,1)S(1)} %get-tuple-element.35), channel_id=1, source_target_pairs={{0,2},{2,4},{4,6},{6,7},{7,5},{5,3},{3,1},{1,0},{8,10},{10,12},{12... | collective-permute-start | bytes 589832 | tf_op jit(solution)/shard_map/ppermute | solution.py:69
  236.0 5.7 %collective-permute-start.29 = (bf16[32,3072]{1,0:T(8,128)(2,1)S(1)}, bf16[32,3072]{1,0:T(8,128)(2,1)S(1)}, u32[]{:S(2)}, u32[]{:S(2)}) collective-permute-start(bf16[32,3072]{1,0:T(8,128)(2,1)S(1)} %fusion.67), channel_id=1, source_target_pairs={{0,1},{2,0},{4,2},{6,4},{7,6},{5,7},{3,5},{1,3},{8,9},{10,8},{12,1... | collective-permute-start | bytes 589832 | tf_op jit(solution)/shard_map/ppermute | solution.py:74
  242.0 6.2 %collective-permute-start.30 = (bf16[32,3072]{1,0:T(8,128)(2,1)S(1)}, bf16[32,3072]{1,0:T(8,128)(2,1)S(1)}, u32[]{:S(2)}, u32[]{:S(2)}) collective-permute-start(bf16[32,3072]{1,0:T(8,128)(2,1)S(1)} %get-tuple-element.24), channel_id=1, source_target_pairs={{0,2},{2,4},{4,6},{6,7},{7,5},{5,3},{3,1},{1,0},{8,10},{10,12},{12... | collective-permute-start | bytes 589832 | tf_op jit(solution)/shard_map/ppermute | solution.py:43
  244.1 5.7 %collective-permute-start.31 = (bf16[32,3072]{1,0:T(8,128)(2,1)S(1)}, bf16[32,3072]{1,0:T(8,128)(2,1)S(1)}, u32[]{:S(2)}, u32[]{:S(2)}) collective-permute-start(bf16[32,3072]{1,0:T(8,128)(2,1)S(1)} %get-tuple-element.24), channel_id=1, source_target_pairs={{0,1},{2,0},{4,2},{6,4},{7,6},{5,7},{3,5},{1,3},{8,9},{10,8},{12,1... | collective-permute-start | bytes 589832 | tf_op jit(solution)/shard_map/ppermute | solution.py:46
  248.2 5.7 %collective-permute-start.32 = (bf16[32,3072]{1,0:T(8,128)(2,1)S(1)}, bf16[32,3072]{1,0:T(8,128)(2,1)S(1)}, u32[]{:S(2)}, u32[]{:S(2)}) collective-permute-start(bf16[32,3072]{1,0:T(8,128)(2,1)S(1)} %collective-permute-done.30), channel_id=1, source_target_pairs={{0,2},{2,4},{4,6},{6,7},{7,5},{5,3},{3,1},{1,0},{8,10},{10,12},{12... | collective-permute-start | bytes 589832 | tf_op jit(solution)/shard_map/ppermute | solution.py:43
  249.8 5.7 %collective-permute-start.33 = (bf16[32,3072]{1,0:T(8,128)(2,1)S(1)}, bf16[32,3072]{1,0:T(8,128)(2,1)S(1)}, u32[]{:S(2)}, u32[]{:S(2)}) collective-permute-start(bf16[32,3072]{1,0:T(8,128)(2,1)S(1)} %collective-permute-done.31), channel_id=1, source_target_pairs={{0,1},{2,0},{4,2},{6,4},{7,6},{5,7},{3,5},{1,3},{8,9},{10,8},{12,1... | collective-permute-start | bytes 589832 | tf_op jit(solution)/shard_map/ppermute | solution.py:46
  253.9 5.7 %collective-permute-start.34 = (bf16[32,3072]{1,0:T(8,128)(2,1)S(1)}, bf16[32,3072]{1,0:T(8,128)(2,1)S(1)}, u32[]{:S(2)}, u32[]{:S(2)}) collective-permute-start(bf16[32,3072]{1,0:T(8,128)(2,1)S(1)} %collective-permute-done.32), channel_id=1, source_target_pairs={{0,2},{2,4},{4,6},{6,7},{7,5},{5,3},{3,1},{1,0},{8,10},{10,12},{12... | collective-permute-start | bytes 589832 | tf_op jit(solution)/shard_map/ppermute | solution.py:43
  255.4 10.2 %copy-start.6 = (f32[1,3072]{1,0:T(1,128)S(1)}, f32[1,3072]{1,0:T(1,128)}, u32[]{:S(2)}) copy-start(f32[1,3072]{1,0:T(1,128)} %get-tuple-element.43) | copy-start | bytes 36868
  255.4 10.2 %copy-start.8 = (bf16[3072,3,1,128]{3,0,2,1:T(8,128)(2,1)S(1)}, bf16[3072,3,1,128]{3,0,2,1:T(8,128)(2,1)}, u32[]{:S(2)}) copy-start(bf16[3072,3,1,128]{3,0,2,1:T(8,128)(2,1)} %param.26) | copy-start | bytes 7077892
  255.5 5.7 %collective-permute-start.35 = (bf16[32,3072]{1,0:T(8,128)(2,1)S(1)}, bf16[32,3072]{1,0:T(8,128)(2,1)S(1)}, u32[]{:S(2)}, u32[]{:S(2)}) collective-permute-start(bf16[32,3072]{1,0:T(8,128)(2,1)S(1)} %collective-permute-done.33), channel_id=1, source_target_pairs={{0,1},{2,0},{4,2},{6,4},{7,6},{5,7},{3,5},{1,3},{8,9},{10,8},{12,1... | collective-permute-start | bytes 589832 | tf_op jit(solution)/shard_map/ppermute | solution.py:46
  259.5 5.7 %collective-permute-start.36 = (bf16[32,3072]{1,0:T(8,128)(2,1)S(1)}, bf16[32,3072]{1,0:T(8,128)(2,1)S(1)}, u32[]{:S(2)}, u32[]{:S(2)}) collective-permute-start(bf16[32,3072]{1,0:T(8,128)(2,1)S(1)} %collective-permute-done.34), channel_id=1, source_target_pairs={{0,2},{2,4},{4,6},{6,7},{7,5},{5,3},{3,1},{1,0},{8,10},{10,12},{12... | collective-permute-start | bytes 589832 | tf_op jit(solution)/shard_map/ppermute | solution.py:43
  267.7 3.7 %collective-permute-start.37 = (bf16[256,128]{1,0:T(8,128)(2,1)S(1)}, bf16[256,128]{1,0:T(8,128)(2,1)S(1)}, u32[]{:S(2)}, u32[]{:S(2)}) collective-permute-start(bf16[256,128]{1,0:T(8,128)(2,1)S(1)} %convolution_convert_fusion.4), channel_id=1, source_target_pairs={{0,8},{1,9},{2,10},{3,11},{4,12},{5,13},{6,14},{7,15},{16,24},{17,... | collective-permute-start | bytes 196616 | tf_op jit(solution)/shard_map/ppermute | solution.py:12
  269.2 2.2 collective-permute-start.38
  273.5 6.2 %collective-permute-start.39 = (bf16[32,3072]{1,0:T(8,128)(2,1)S(1)}, bf16[32,3072]{1,0:T(8,128)(2,1)S(1)}, u32[]{:S(2)}, u32[]{:S(2)}) collective-permute-start(bf16[32,3072]{1,0:T(8,128)(2,1)S(1)} %get-tuple-element.33), channel_id=1, source_target_pairs={{0,2},{2,4},{4,6},{6,7},{7,5},{5,3},{3,1},{1,0},{8,10},{10,12},{12... | collective-permute-start | bytes 589832 | tf_op jit(solution)/shard_map/ppermute | solution.py:69
  279.8 7.8 %collective-permute-start.40 = (bf16[32,3072]{1,0:T(8,128)(2,1)S(1)}, bf16[32,3072]{1,0:T(8,128)(2,1)S(1)}, u32[]{:S(2)}, u32[]{:S(2)}) collective-permute-start(bf16[32,3072]{1,0:T(8,128)(2,1)S(1)} %fusion.60), channel_id=1, source_target_pairs={{0,2},{2,4},{4,6},{6,7},{7,5},{5,3},{3,1},{1,0},{8,10},{10,12},{12... | collective-permute-start | bytes 589832 | tf_op jit(solution)/shard_map/ppermute | solution.py:69
  281.7 7.7 %collective-permute-start.43 = (bf16[32,3072]{1,0:T(8,128)(2,1)S(1)}, bf16[32,3072]{1,0:T(8,128)(2,1)S(1)}, u32[]{:S(2)}, u32[]{:S(2)}) collective-permute-start(bf16[32,3072]{1,0:T(8,128)(2,1)S(1)} %get-tuple-element.34), channel_id=1, source_target_pairs={{0,1},{2,0},{4,2},{6,4},{7,6},{5,7},{3,5},{1,3},{8,9},{10,8},{12,1... | collective-permute-start | bytes 589832 | tf_op jit(solution)/shard_map/ppermute | solution.py:74
  287.6 7.5 %collective-permute-start.41 = (bf16[32,3072]{1,0:T(8,128)(2,1)S(1)}, bf16[32,3072]{1,0:T(8,128)(2,1)S(1)}, u32[]{:S(2)}, u32[]{:S(2)}) collective-permute-start(bf16[32,3072]{1,0:T(8,128)(2,1)S(1)} %fusion.61), channel_id=1, source_target_pairs={{0,2},{2,4},{4,6},{6,7},{7,5},{5,3},{3,1},{1,0},{8,10},{10,12},{12... | collective-permute-start | bytes 589832 | tf_op jit(solution)/shard_map/ppermute | solution.py:69
  295.2 6.5 %collective-permute-start.44 = (bf16[32,3072]{1,0:T(8,128)(2,1)S(1)}, bf16[32,3072]{1,0:T(8,128)(2,1)S(1)}, u32[]{:S(2)}, u32[]{:S(2)}) collective-permute-start(bf16[32,3072]{1,0:T(8,128)(2,1)S(1)} %get-tuple-element.32), channel_id=1, source_target_pairs={{0,1},{2,0},{4,2},{6,4},{7,6},{5,7},{3,5},{1,3},{8,9},{10,8},{12,1... | collective-permute-start | bytes 589832 | tf_op jit(solution)/shard_map/ppermute | solution.py:74
  297.0 6.3 %collective-permute-start.42 = (bf16[32,3072]{1,0:T(8,128)(2,1)S(1)}, bf16[32,3072]{1,0:T(8,128)(2,1)S(1)}, u32[]{:S(2)}, u32[]{:S(2)}) collective-permute-start(bf16[32,3072]{1,0:T(8,128)(2,1)S(1)} %get-tuple-element.31), channel_id=1, source_target_pairs={{0,2},{2,4},{4,6},{6,7},{7,5},{5,3},{3,1},{1,0},{8,10},{10,12},{12... | collective-permute-start | bytes 589832 | tf_op jit(solution)/shard_map/ppermute | solution.py:69
  301.8 5.7 %collective-permute-start.45 = (bf16[32,3072]{1,0:T(8,128)(2,1)S(1)}, bf16[32,3072]{1,0:T(8,128)(2,1)S(1)}, u32[]{:S(2)}, u32[]{:S(2)}) collective-permute-start(bf16[32,3072]{1,0:T(8,128)(2,1)S(1)} %fusion.59), channel_id=1, source_target_pairs={{0,1},{2,0},{4,2},{6,4},{7,6},{5,7},{3,5},{1,3},{8,9},{10,8},{12,1... | collective-permute-start | bytes 589832 | tf_op jit(solution)/shard_map/ppermute | solution.py:74

commit v3 on v2

--- a/solution.py
+++ b/solution.py
@@ -2,6 +2,8 @@
 import jax.numpy as jnp
 from jax import lax
 from jax.sharding import PartitionSpec as P
+from jax.experimental import pallas as pl
+from jax.experimental.pallas import tpu as pltpu
 
 LARGEST_DILATION = 64
 
@@ -89,22 +91,56 @@
     return lax.optimization_barrier(term.astype(jnp.bfloat16)).astype(jnp.float32)
 
 
-def convolution_gate(hidden, kernel, dilation_factor):
+def conv_gate_kernel(slab_ref, weight_ref, out_ref, filt_acc, gate_acc):
+    tap = pl.program_id(0)
+    chunk = pl.program_id(1)
+
+    @pl.when((tap == 0) & (chunk == 0))
+    def _():
+        filt_acc[...] = jnp.zeros_like(filt_acc)
+        gate_acc[...] = jnp.zeros_like(gate_acc)
+
+    rows = slab_ref[...]
+    filt_acc[...] += jnp.dot(rows, weight_ref[0], preferred_element_type=jnp.float32)
+    gate_acc[...] += jnp.dot(rows, weight_ref[1], preferred_element_type=jnp.float32)
+
+    @pl.when((tap == pl.num_programs(0) - 1) & (chunk == pl.num_programs(1) - 1))
+    def _():
+        out_ref[...] = (jnp.tanh(filt_acc[...]) * jax.nn.sigmoid(gate_acc[...])).astype(out_ref.dtype)
+
+
+def convolution_gate(hidden, conv_by_half, layer_idx, dilation_factor):
     all_rows = hidden.shape[0]
     width = hidden.shape[1]
-    own_width = kernel.shape[-1]
+    taps = conv_by_half.shape[1]
+    own_width = conv_by_half.shape[-1]
     border_rows = 2 * LARGEST_DILATION
     before = shifted(hidden[all_rows - border_rows :], "blk", 1)
     padded = jnp.concatenate([before, hidden], axis=0)
-    by_half = jnp.transpose(kernel, (0, 2, 1, 3))
-    filt = jnp.zeros((all_rows, own_width), jnp.float32)
-    gate = jnp.zeros((all_rows, own_width), jnp.float32)
-    for tap_idx in range(3):
-        start = border_rows - tap_idx * dilation_factor
-        slab = lax.dynamic_slice_in_dim(padded, start, all_rows, 0)
-        filt = filt + jnp.dot(slab, by_half[tap_idx, 0], preferred_element_type=jnp.float32)
-        gate = gate + jnp.dot(slab, by_half[tap_idx, 1], preferred_element_type=jnp.float32)
-    return (jnp.tanh(filt) * jax.nn.sigmoid(gate)).astype(jnp.bfloat16)
+    slabs = jnp.stack(
+        [
+            lax.dynamic_slice_in_dim(padded, border_rows - tap_idx * dilation_factor, all_rows, 0)
+            for tap_idx in range(taps)
+        ]
+    )
+    chunk = 1024 if width % 1024 == 0 else width
+    return pl.pallas_call(
+        conv_gate_kernel,
+        out_shape=jax.ShapeDtypeStruct((all_rows, own_width), jnp.bfloat16),
+        grid=(taps, width // chunk),
+        in_specs=[
+            pl.BlockSpec((None, all_rows, chunk), lambda t, k: (t, 0, k)),
+            pl.BlockSpec((None, None, 2, chunk, own_width), lambda t, k: (layer_idx, t, 0, k, 0)),
+        ],
+        out_specs=pl.BlockSpec((all_rows, own_width), lambda t, k: (0, 0)),
+        scratch_shapes=[pltpu.VMEM((all_rows, own_width), jnp.float32)] * 2,
+        compiler_params=pltpu.CompilerParams(dimension_semantics=("arbitrary", "arbitrary")),
+        cost_estimate=pl.CostEstimate(
+            flops=4 * taps * all_rows * width * own_width,
+            transcendentals=2 * all_rows * own_width,
+            bytes_accessed=2 * taps * (all_rows * width + 2 * width * own_width + all_rows * own_width // taps),
+        ),
+    )(slabs, conv_by_half)
 
 
 def conv_share(gated, weight, tok_rows):
@@ -166,9 +202,10 @@
     layers = w_conv.shape[0]
     share = stream
     state = ring_gather(stream, "head")
+    conv_by_half = jnp.transpose(w_conv, (0, 1, 3, 2, 4))
     for layer_idx in range(layers):
         gated = convolution_gate(
-            normed(state, gains[layer_idx]), w_conv[layer_idx], dilations[layer_idx]
+            normed(state, gains[layer_idx]), conv_by_half, layer_idx, dilations[layer_idx]
         )
         summed = conv_share(gated, w_mix[layer_idx], tok_rows)
         share = (share.astype(jnp.float32) + summed).astype(jnp.bfloat16)

time: 310 us -> 283 us (0.913)
  matrix products: 39.2 us -> 8.53 us
  local copies, waits for them, and re-layouts: 60.5 us -> 30.7 us
  Pallas kernels: 0 us -> 25 us
  starting transfers between devices: 60.1 us -> 50.3 us
  other arithmetic: 8.4 us -> 17.5 us
  waiting for transfers between devices: 108 us -> 117 us
    pallas_call x0 -> x2, Pallas kernels: none -> 25 us  [convolution_gate(): pl.pallas_call(conv_gate_kernel, out_shape=jax.ShapeDtypeStruct((all_rows...]
    dot_general x10 -> x0, matrix products: 24.9 us -> none  [the longest x6 15 us: convolution_gate(): jnp.dot(slab, by_half[tap_idx, 1], preferred_element_type=jnp.float32)]
    slice x1 -> x0, local copies, waits for them, and re-layouts: 22.7 us -> none  [per_device(): w_conv[layer_idx]]
    another operation x0 -> x6, other arithmetic: none -> 11.8 us  [convolution_gate(): jnp.stack([lax.dynamic_slice_in_dim(padded, border_rows - tap_idx * dilat...]
    ppermute x9, starting transfers between devices: 14.3 us -> 7.75 us  [ring_scatter_sum(): bwd = lax.ppermute(part.astype(value.dtype), axis, backward)]
    ppermute x12, waiting for transfers between devices: 39.9 us -> 45.9 us  [ring_scatter_sum(): fwd = lax.ppermute(part.astype(value.dtype), axis, forward)]
    dot_general x3, matrix products: 12 us -> 6.26 us  [rounded_term(): term = jnp.dot(left, right, preferred_element_type=jnp.float32)]
    ppermute x12, starting transfers between devices: 19.2 us -> 13.5 us  [ring_gather(): fwd = lax.ppermute(fwd, axis, forward)]
  transfers between devices with their start and end apart: 46 -> 46, of which waited for: 30 -> 33; matrix products, arithmetic and copies ran while one was open for 19% -> 10% of each run, Pallas kernels for 0% -> 0%
where the time goes in v3:
time: 283 us; the launch traced here: 282 us
  waiting for transfers between devices  117 us (41%)
  starting transfers between devices  50.3 us (18%)
  between operations  33.2 us (12%)
  local copies, waits for them, and re-layouts  30.7 us (11%)
  Pallas kernels  25 us (9%)
  other arithmetic  17.5 us (6%)
  matrix products  8.53 us (3%)
    ppermute x12, waiting for transfers between devices, ring_gather(): fwd = lax.ppermute(fwd, axis, forward)  49 us
    ppermute x12, waiting for transfers between devices, ring_scatter_sum(): fwd = lax.ppermute(part.astype(value.dtype), axis, forward)  45.9 us
    pallas_call x2, Pallas kernels, convolution_gate(): pl.pallas_call(conv_gate_kernel, out_shape=jax.ShapeDtypeStruct((all_rows...  25 us
    unnamed x21, local copies, waits for them, and re-layouts  23.9 us
    ppermute x9, waiting for transfers between devices, ring_scatter_sum(): bwd = lax.ppermute(part.astype(value.dtype), axis, backward)  20.7 us
    ppermute x12, starting transfers between devices, ring_gather(): fwd = lax.ppermute(fwd, axis, forward)  13.5 us
    ppermute x12, starting transfers between devices, ring_scatter_sum(): fwd = lax.ppermute(part.astype(value.dtype), axis, forward)  13.2 us
    another operation x6, other arithmetic, convolution_gate(): jnp.stack([lax.dynamic_slice_in_dim(padded, border_rows - tap_idx * dilat...  11.8 us
  transfers between devices with their start and end apart: 46, of which 33 were waited for; matrix products, arithmetic and copies ran while one was open for 10% of the time, Pallas kernels for 0%

profile of v3, /device:TPU:0, one launch (start us, length us, event | category | flops | bytes accessed | tf_op | source)
XLA Modules:
  0.0 282.0 jit_solution(9074562989653191229)
XLA Ops:
  0.0 3.0 %collective-permute-start = (bf16[32,3072]{1,0:T(8,128)(2,1)}, bf16[32,3072]{1,0:T(8,128)(2,1)S(1)}, u32[]{:S(2)}, u32[]{:S(2)}) collective-permute-start(bf16[32,3072]{1,0:T(8,128)(2,1)} %param.21), channel_id=1, source_target_pairs={{0,2},{2,4},{4,6},{6,7},{7,5},{5,3},{3,1},{1,0},{8,10},{10,12},{12... | collective-permute-start | bytes 589832 | tf_op jit(solution)/shard_map/ppermute | solution.py:45
  3.0 1.2 dynamic_slice.247
  12.8 1.7 fusion.74
  19.7 1.5 fusion.73
  21.4 2.1 collective-permute-start.2
  23.6 4.3 %collective-permute-done.2 = bf16[32,3072]{1,0:T(8,128)(2,1)S(1)} collective-permute-done((bf16[32,3072]{1,0:T(8,128)(2,1)S(1)}, bf16[32,3072]{1,0:T(8,128)(2,1)S(1)}, u32[]{:S(2)}, u32[]{:S(2)}) %collective-permute-start.2) | collective-permute-done | bytes 196640 | tf_op jit(solution)/shard_map/ppermute | solution.py:45
  27.8 1.7 collective-permute-start.4
  29.9 3.6 %collective-permute-done.4 = bf16[32,3072]{1,0:T(8,128)(2,1)S(1)} collective-permute-done((bf16[32,3072]{1,0:T(8,128)(2,1)S(1)}, bf16[32,3072]{1,0:T(8,128)(2,1)S(1)}, u32[]{:S(2)}, u32[]{:S(2)}) %collective-permute-start.4) | collective-permute-done | bytes 196640 | tf_op jit(solution)/shard_map/ppermute | solution.py:45
  33.5 1.9 collective-permute-start.6
  35.5 3.7 %collective-permute-done.6 = bf16[32,3072]{1,0:T(8,128)(2,1)S(1)} collective-permute-done((bf16[32,3072]{1,0:T(8,128)(2,1)S(1)}, bf16[32,3072]{1,0:T(8,128)(2,1)S(1)}, u32[]{:S(2)}, u32[]{:S(2)}) %collective-permute-start.6) | collective-permute-done | bytes 196640 | tf_op jit(solution)/shard_map/ppermute | solution.py:45
  40.1 1.2 copy-done.1
  41.4 2.2 collective-permute-start.7
  48.9 19.6 %copy.22 = bf16[2,3,3072,2,384]{4,2,3,1,0:T(8,128)(2,1)} copy(bf16[2,3,3072,2,384]{4,3,2,1,0:T(2,128)(2,1)} %param.24) | data formatting | bytes 56623104 | tf_op args[3]
  71.2 3.0 %fusion.25 = (bf16[1,256,3072]{2,1,0:T(8,128)(2,1)S(1)}, bf16[1,256,3072]{2,1,0:T(8,128)(2,1)S(1)}) fusion(s32[]{:T(128)S(6)} %select_n.520, bf16[256,3072]{1,0:T(8,128)(2,1)S(1)} %copy-done.2, bf16[128,3072]{1,0:T(8,128)(2,1)} %collective-permute-done.7, s32[]{:T(128)S(6)} %select_n.521), kind=kLoop, calls=%fused_computation.46 | loop fusion | flops 6291456 | bytes 5505032 | tf_op jit(solution)/shard_map/stack | solution.py:120
  74.2 2.4 pad_maximum_fusion.slab_ref
  76.6 12.5 %shard_map.181 = bf16[256,384]{1,0:T(8,128)(2,1)} custom-call(bf16[3,256,3072]{2,1,0:T(8,128)(2,1)} %pad_maximum_fusion.slab_ref, bf16[2,3,2,3072,384]{4,3,2,1,0:T(8,128)(2,1)} %bitcast.143), custom_call_target="tpu_custom_call" | custom-call | flops 3623878656 | bytes 19070976 | tf_op jit(solution)/shard_map/pallas_call | solution.py:127
  89.1 2.8 convolution_convert_fusion.2
  91.9 1.9 collective-permute-start.8
  95.6 3.2 %collective-permute-done.8 = bf16[32,3072]{1,0:T(8,128)(2,1)S(1)} collective-permute-done((bf16[32,3072]{1,0:T(8,128)(2,1)S(1)}, bf16[32,3072]{1,0:T(8,128)(2,1)S(1)}, u32[]{:S(2)}, u32[]{:S(2)}) %collective-permute-start.8) | collective-permute-done | bytes 196640 | tf_op jit(solution)/shard_map/ppermute | solution.py:71
  98.9 1.7 collective-permute-start.9
  103.1 1.9 collective-permute-done.9
  105.1 1.5 collective-permute-start.10
  110.3 2.5 collective-permute-done.10
  112.8 1.2 collective-permute-start.13
  116.9 1.7 collective-permute-done.13
  118.6 1.2 collective-permute-start.14
  121.5 1.4 collective-permute-done.11
  122.9 1.4 collective-permute-done.14
  125.6 1.3 collective-permute-start.15
  127.6 5.6 %collective-permute-done.15 = bf16[32,3072]{1,0:T(8,128)(2,1)S(1)} collective-permute-done((bf16[32,3072]{1,0:T(8,128)(2,1)S(1)}, bf16[32,3072]{1,0:T(8,128)(2,1)S(1)}, u32[]{:S(2)}, u32[]{:S(2)}) %collective-permute-start.15) | collective-permute-done | bytes 196640 | tf_op jit(solution)/shard_map/ppermute | solution.py:45
  135.4 4.9 %collective-permute-done.17 = bf16[32,3072]{1,0:T(8,128)(2,1)S(1)} collective-permute-done((bf16[32,3072]{1,0:T(8,128)(2,1)S(1)}, bf16[32,3072]{1,0:T(8,128)(2,1)S(1)}, u32[]{:S(2)}, u32[]{:S(2)}) %collective-permute-start.17) | collective-permute-done | bytes 196640 | tf_op jit(solution)/shard_map/ppermute | solution.py:45
  140.9 1.5 collective-permute-start.20
  142.4 3.5 %collective-permute-done.19 = bf16[32,3072]{1,0:T(8,128)(2,1)S(1)} collective-permute-done((bf16[32,3072]{1,0:T(8,128)(2,1)S(1)}, bf16[32,3072]{1,0:T(8,128)(2,1)S(1)}, u32[]{:S(2)}, u32[]{:S(2)}) %collective-permute-start.19) | collective-permute-done | bytes 196640 | tf_op jit(solution)/shard_map/ppermute | solution.py:45
  146.7 5.0 %collective-permute-done.21 = bf16[32,3072]{1,0:T(8,128)(2,1)S(1)} collective-permute-done((bf16[32,3072]{1,0:T(8,128)(2,1)S(1)}, bf16[32,3072]{1,0:T(8,128)(2,1)S(1)}, u32[]{:S(2)}, u32[]{:S(2)}) %collective-permute-start.21) | collective-permute-done | bytes 196640 | tf_op jit(solution)/shard_map/ppermute | solution.py:45
  152.6 1.2 copy-done.3
  153.9 2.2 collective-permute-start.22
  159.6 3.1 %fusion.21 = (bf16[1,256,3072]{2,1,0:T(8,128)(2,1)S(1)}, bf16[1,256,3072]{2,1,0:T(8,128)(2,1)S(1)}) fusion(s32[]{:T(128)S(6)} %select_n.569, bf16[256,3072]{1,0:T(8,128)(2,1)S(1)} %copy-done.4, bf16[128,3072]{1,0:T(8,128)(2,1)} %collective-permute-done.22, s32[]{:T(128)S(6)} %select_n.570), kind=kLoop, calls=%fused_computation.42 | loop fusion | flops 6291456 | bytes 5505032 | tf_op jit(solution)/shard_map/stack | solution.py:120
  162.6 2.4 pad_maximum_fusion.1.slab_ref
  165.0 12.5 %shard_map.182 = bf16[256,384]{1,0:T(8,128)(2,1)} custom-call(bf16[3,256,3072]{2,1,0:T(8,128)(2,1)} %pad_maximum_fusion.1.slab_ref, bf16[2,3,2,3072,384]{4,3,2,1,0:T(8,128)(2,1)} %bitcast.144), custom_call_target="tpu_custom_call" | custom-call | flops 3623878656 | bytes 19070976 | tf_op jit(solution)/shard_map/pallas_call | solution.py:127
  177.5 2.8 convolution_convert_fusion.1
  181.0 5.5 %collective-permute-done.23 = bf16[32,3072]{1,0:T(8,128)(2,1)S(1)} collective-permute-done((bf16[32,3072]{1,0:T(8,128)(2,1)S(1)}, bf16[32,3072]{1,0:T(8,128)(2,1)S(1)}, u32[]{:S(2)}, u32[]{:S(2)}) %collective-permute-start.23) | collective-permute-done | bytes 196640 | tf_op jit(solution)/shard_map/ppermute | solution.py:71
  187.1 1.5 collective-permute-start.27
  188.6 5.2 %collective-permute-done.24 = bf16[32,3072]{1,0:T(8,128)(2,1)S(1)} collective-permute-done((bf16[32,3072]{1,0:T(8,128)(2,1)S(1)}, bf16[32,3072]{1,0:T(8,128)(2,1)S(1)}, u32[]{:S(2)}, u32[]{:S(2)}) %collective-permute-start.24) | collective-permute-done | bytes 196640 | tf_op jit(solution)/shard_map/ppermute | solution.py:71
  194.5 7.2 %collective-permute-done.25 = bf16[32,3072]{1,0:T(8,128)(2,1)S(1)} collective-permute-done((bf16[32,3072]{1,0:T(8,128)(2,1)S(1)}, bf16[32,3072]{1,0:T(8,128)(2,1)S(1)}, u32[]{:S(2)}, u32[]{:S(2)}) %collective-permute-start.25) | collective-permute-done | bytes 196640 | tf_op jit(solution)/shard_map/ppermute | solution.py:71
  201.8 2.0 collective-permute-start.26
  203.8 4.0 %collective-permute-done.28 = bf16[32,3072]{1,0:T(8,128)(2,1)S(1)} collective-permute-done((bf16[32,3072]{1,0:T(8,128)(2,1)S(1)}, bf16[32,3072]{1,0:T(8,128)(2,1)S(1)}, u32[]{:S(2)}, u32[]{:S(2)}) %collective-permute-start.28) | collective-permute-done | bytes 196640 | tf_op jit(solution)/shard_map/ppermute | solution.py:76
  207.9 1.1 collective-permute-done.26
  209.1 4.5 %collective-permute-done.29 = bf16[32,3072]{1,0:T(8,128)(2,1)S(1)} collective-permute-done((bf16[32,3072]{1,0:T(8,128)(2,1)S(1)}, bf16[32,3072]{1,0:T(8,128)(2,1)S(1)}, u32[]{:S(2)}, u32[]{:S(2)}) %collective-permute-start.29) | collective-permute-done | bytes 196640 | tf_op jit(solution)/shard_map/ppermute | solution.py:76
  214.0 2.0 collective-permute-start.31
  216.0 5.4 %collective-permute-done.30 = bf16[32,3072]{1,0:T(8,128)(2,1)S(1)} collective-permute-done((bf16[32,3072]{1,0:T(8,128)(2,1)S(1)}, bf16[32,3072]{1,0:T(8,128)(2,1)S(1)}, u32[]{:S(2)}, u32[]{:S(2)}) %collective-permute-start.30) | collective-permute-done | bytes 196640 | tf_op jit(solution)/shard_map/ppermute | solution.py:45
  221.4 2.1 collective-permute-start.33
  223.5 4.5 %collective-permute-done.32 = bf16[32,3072]{1,0:T(8,128)(2,1)S(1)} collective-permute-done((bf16[32,3072]{1,0:T(8,128)(2,1)S(1)}, bf16[32,3072]{1,0:T(8,128)(2,1)S(1)}, u32[]{:S(2)}, u32[]{:S(2)}) %collective-permute-start.32) | collective-permute-done | bytes 196640 | tf_op jit(solution)/shard_map/ppermute | solution.py:45
  228.7 1.4 collective-permute-start.35
  230.2 3.5 %collective-permute-done.34 = bf16[32,3072]{1,0:T(8,128)(2,1)S(1)} collective-permute-done((bf16[32,3072]{1,0:T(8,128)(2,1)S(1)}, bf16[32,3072]{1,0:T(8,128)(2,1)S(1)}, u32[]{:S(2)}, u32[]{:S(2)}) %collective-permute-start.34) | collective-permute-done | bytes 196640 | tf_op jit(solution)/shard_map/ppermute | solution.py:45
  234.4 4.9 %collective-permute-done.36 = bf16[32,3072]{1,0:T(8,128)(2,1)S(1)} collective-permute-done((bf16[32,3072]{1,0:T(8,128)(2,1)S(1)}, bf16[32,3072]{1,0:T(8,128)(2,1)S(1)}, u32[]{:S(2)}, u32[]{:S(2)}) %collective-permute-start.36) | collective-permute-done | bytes 196640 | tf_op jit(solution)/shard_map/ppermute | solution.py:45
  241.8 1.3 collective-permute-start.37
  243.4 1.3 collective-permute-start.38
  248.3 5.9 %collective-permute-done.39 = bf16[32,3072]{1,0:T(8,128)(2,1)S(1)} collective-permute-done((bf16[32,3072]{1,0:T(8,128)(2,1)S(1)}, bf16[32,3072]{1,0:T(8,128)(2,1)S(1)}, u32[]{:S(2)}, u32[]{:S(2)}) %collective-permute-start.39) | collective-permute-done | bytes 196640 | tf_op jit(solution)/shard_map/ppermute | solution.py:71
  254.9 1.4 collective-permute-start.43
  256.3 5.6 %collective-permute-done.40 = bf16[32,3072]{1,0:T(8,128)(2,1)S(1)} collective-permute-done((bf16[32,3072]{1,0:T(8,128)(2,1)S(1)}, bf16[32,3072]{1,0:T(8,128)(2,1)S(1)}, u32[]{:S(2)}, u32[]{:S(2)}) %collective-permute-start.40) | collective-permute-done | bytes 196640 | tf_op jit(solution)/shard_map/ppermute | solution.py:71
  262.7 6.4 %collective-permute-done.41 = bf16[32,3072]{1,0:T(8,128)(2,1)S(1)} collective-permute-done((bf16[32,3072]{1,0:T(8,128)(2,1)S(1)}, bf16[32,3072]{1,0:T(8,128)(2,1)S(1)}, u32[]{:S(2)}, u32[]{:S(2)}) %collective-permute-start.41) | collective-permute-done | bytes 196640 | tf_op jit(solution)/shard_map/ppermute | solution.py:71
  270.0 1.3 collective-permute-start.42
  271.3 4.2 %collective-permute-done.44 = bf16[32,3072]{1,0:T(8,128)(2,1)S(1)} collective-permute-done((bf16[32,3072]{1,0:T(8,128)(2,1)S(1)}, bf16[32,3072]{1,0:T(8,128)(2,1)S(1)}, u32[]{:S(2)}, u32[]{:S(2)}) %collective-permute-start.44) | collective-permute-done | bytes 196640 | tf_op jit(solution)/shard_map/ppermute | solution.py:76
  276.6 4.6 %collective-permute-done.45 = bf16[32,3072]{1,0:T(8,128)(2,1)S(1)} collective-permute-done((bf16[32,3072]{1,0:T(8,128)(2,1)S(1)}, bf16[32,3072]{1,0:T(8,128)(2,1)S(1)}, u32[]{:S(2)}, u32[]{:S(2)}) %collective-permute-start.45) | collective-permute-done | bytes 196640 | tf_op jit(solution)/shard_map/ppermute | solution.py:76
  (127 shorter events, 28.5 us)
Async XLA Ops:
  0.0 246.8 %copy-start = (bf16[1,128,3072]{2,1,0:T(8,128)(2,1)S(1)}, bf16[1,128,3072]{2,1,0:T(8,128)(2,1)}, u32[]{:S(2)}) copy-start(bf16[1,128,3072]{2,1,0:T(8,128)(2,1)} %param.27) | copy-start | bytes 2359300
  0.0 21.4 %copy-start.6 = (bf16[32,3072]{1,0:T(8,128)(2,1)S(1)}, bf16[32,3072]{1,0:T(8,128)(2,1)}, u32[]{:S(2)}) copy-start(bf16[32,3072]{1,0:T(8,128)(2,1)} %param.21) | copy-start | bytes 589828
  0.0 21.4 %collective-permute-start = (bf16[32,3072]{1,0:T(8,128)(2,1)}, bf16[32,3072]{1,0:T(8,128)(2,1)S(1)}, u32[]{:S(2)}, u32[]{:S(2)}) collective-permute-start(bf16[32,3072]{1,0:T(8,128)(2,1)} %param.21), channel_id=1, source_target_pairs={{0,2},{2,4},{4,6},{6,7},{7,5},{5,3},{3,1},{1,0},{8,10},{10,12},{12... | collective-permute-start | bytes 589832 | tf_op jit(solution)/shard_map/ppermute | solution.py:45
  3.0 20.5 %collective-permute-start.1 = (bf16[32,3072]{1,0:T(8,128)(2,1)}, bf16[32,3072]{1,0:T(8,128)(2,1)S(1)}, u32[]{:S(2)}, u32[]{:S(2)}) collective-permute-start(bf16[32,3072]{1,0:T(8,128)(2,1)} %param.21), channel_id=1, source_target_pairs={{0,1},{2,0},{4,2},{6,4},{7,6},{5,7},{3,5},{1,3},{8,9},{10,8},{12,1... | collective-permute-start | bytes 589832 | tf_op jit(solution)/shard_map/ppermute | solution.py:48
  21.4 6.4 %collective-permute-start.2 = (bf16[32,3072]{1,0:T(8,128)(2,1)S(1)}, bf16[32,3072]{1,0:T(8,128)(2,1)S(1)}, u32[]{:S(2)}, u32[]{:S(2)}) collective-permute-start(bf16[32,3072]{1,0:T(8,128)(2,1)S(1)} %collective-permute-done), channel_id=1, source_target_pairs={{0,2},{2,4},{4,6},{6,7},{7,5},{5,3},{3,1},{1,0},{8,10},{10,12},{12... | collective-permute-start | bytes 589832 | tf_op jit(solution)/shard_map/ppermute | solution.py:45
  23.5 6.1 %collective-permute-start.3 = (bf16[32,3072]{1,0:T(8,128)(2,1)S(1)}, bf16[32,3072]{1,0:T(8,128)(2,1)S(1)}, u32[]{:S(2)}, u32[]{:S(2)}) collective-permute-start(bf16[32,3072]{1,0:T(8,128)(2,1)S(1)} %collective-permute-done.1), channel_id=1, source_target_pairs={{0,1},{2,0},{4,2},{6,4},{7,6},{5,7},{3,5},{1,3},{8,9},{10,8},{12,1... | collective-permute-start | bytes 589832 | tf_op jit(solution)/shard_map/ppermute | solution.py:48
  27.8 5.7 %collective-permute-start.4 = (bf16[32,3072]{1,0:T(8,128)(2,1)S(1)}, bf16[32,3072]{1,0:T(8,128)(2,1)S(1)}, u32[]{:S(2)}, u32[]{:S(2)}) collective-permute-start(bf16[32,3072]{1,0:T(8,128)(2,1)S(1)} %collective-permute-done.2), channel_id=1, source_target_pairs={{0,2},{2,4},{4,6},{6,7},{7,5},{5,3},{3,1},{1,0},{8,10},{10,12},{12... | collective-permute-start | bytes 589832 | tf_op jit(solution)/shard_map/ppermute | solution.py:45
  29.6 5.8 %collective-permute-start.5 = (bf16[32,3072]{1,0:T(8,128)(2,1)S(1)}, bf16[32,3072]{1,0:T(8,128)(2,1)S(1)}, u32[]{:S(2)}, u32[]{:S(2)}) collective-permute-start(bf16[32,3072]{1,0:T(8,128)(2,1)S(1)} %collective-permute-done.3), channel_id=1, source_target_pairs={{0,1},{2,0},{4,2},{6,4},{7,6},{5,7},{3,5},{1,3},{8,9},{10,8},{12,1... | collective-permute-start | bytes 589832 | tf_op jit(solution)/shard_map/ppermute | solution.py:48
  33.5 5.7 %collective-permute-start.6 = (bf16[32,3072]{1,0:T(8,128)(2,1)S(1)}, bf16[32,3072]{1,0:T(8,128)(2,1)S(1)}, u32[]{:S(2)}, u32[]{:S(2)}) collective-permute-start(bf16[32,3072]{1,0:T(8,128)(2,1)S(1)} %collective-permute-done.4), channel_id=1, source_target_pairs={{0,2},{2,4},{4,6},{6,7},{7,5},{5,3},{3,1},{1,0},{8,10},{10,12},{12... | collective-permute-start | bytes 589832 | tf_op jit(solution)/shard_map/ppermute | solution.py:45
  40.1 1.2 copy-start.1
  41.4 2.3 copy-start.8
  41.4 28.9 %collective-permute-start.7 = (bf16[128,3072]{1,0:T(8,128)(2,1)S(1)}, bf16[128,3072]{1,0:T(8,128)(2,1)}, u32[]{:S(2)}, u32[]{:S(2)}) collective-permute-start(bf16[128,3072]{1,0:T(8,128)(2,1)S(1)} %slice.48), channel_id=1, source_target_pairs={{0,8},{1,9},{2,10},{3,11},{4,12},{5,13},{6,14},{7,15},{16,24},{17,... | collective-permute-start | bytes 2359304 | tf_op jit(solution)/shard_map/ppermute | solution.py:14
  69.8 1.4 copy-start.2
  91.8 26.7 %copy-start.5 = (bf16[256,3072]{1,0:T(8,128)(2,1)}, bf16[256,3072]{1,0:T(8,128)(2,1)S(1)}, u32[]{:S(2)}) copy-start(bf16[256,3072]{1,0:T(8,128)(2,1)S(1)} %convolution_convert_fusion.2) | copy-start | bytes 4718596
  91.9 6.9 %collective-permute-start.8 = (bf16[32,3072]{1,0:T(8,128)(2,1)S(1)}, bf16[32,3072]{1,0:T(8,128)(2,1)S(1)}, u32[]{:S(2)}, u32[]{:S(2)}) collective-permute-start(bf16[32,3072]{1,0:T(8,128)(2,1)S(1)} %get-tuple-element.43), channel_id=1, source_target_pairs={{0,2},{2,4},{4,6},{6,7},{7,5},{5,3},{3,1},{1,0},{8,10},{10,12},{12... | collective-permute-start | bytes 589832 | tf_op jit(solution)/shard_map/ppermute | solution.py:71
  98.9 6.1 %collective-permute-start.9 = (bf16[32,3072]{1,0:T(8,128)(2,1)S(1)}, bf16[32,3072]{1,0:T(8,128)(2,1)S(1)}, u32[]{:S(2)}, u32[]{:S(2)}) collective-permute-start(bf16[32,3072]{1,0:T(8,128)(2,1)S(1)} %fusion.46), channel_id=1, source_target_pairs={{0,2},{2,4},{4,6},{6,7},{7,5},{5,3},{3,1},{1,0},{8,10},{10,12},{12... | collective-permute-start | bytes 589832 | tf_op jit(solution)/shard_map/ppermute | solution.py:71
  102.6 7.6 %collective-permute-start.12 = (bf16[32,3072]{1,0:T(8,128)(2,1)S(1)}, bf16[32,3072]{1,0:T(8,128)(2,1)S(1)}, u32[]{:S(2)}, u32[]{:S(2)}) collective-permute-start(bf16[32,3072]{1,0:T(8,128)(2,1)S(1)} %get-tuple-element.44), channel_id=1, source_target_pairs={{0,1},{2,0},{4,2},{6,4},{7,6},{5,7},{3,5},{1,3},{8,9},{10,8},{12,1... | collective-permute-start | bytes 589832 | tf_op jit(solution)/shard_map/ppermute | solution.py:76
  105.1 7.7 %collective-permute-start.10 = (bf16[32,3072]{1,0:T(8,128)(2,1)S(1)}, bf16[32,3072]{1,0:T(8,128)(2,1)S(1)}, u32[]{:S(2)}, u32[]{:S(2)}) collective-permute-start(bf16[32,3072]{1,0:T(8,128)(2,1)S(1)} %fusion.47), channel_id=1, source_target_pairs={{0,2},{2,4},{4,6},{6,7},{7,5},{5,3},{3,1},{1,0},{8,10},{10,12},{12... | collective-permute-start | bytes 589832 | tf_op jit(solution)/shard_map/ppermute | solution.py:71
  112.8 5.7 %collective-permute-start.13 = (bf16[32,3072]{1,0:T(8,128)(2,1)S(1)}, bf16[32,3072]{1,0:T(8,128)(2,1)S(1)}, u32[]{:S(2)}, u32[]{:S(2)}) collective-permute-start(bf16[32,3072]{1,0:T(8,128)(2,1)S(1)} %get-tuple-element.42), channel_id=1, source_target_pairs={{0,1},{2,0},{4,2},{6,4},{7,6},{5,7},{3,5},{1,3},{8,9},{10,8},{12,1... | collective-permute-start | bytes 589832 | tf_op jit(solution)/shard_map/ppermute | solution.py:76
  116.0 7.0 %collective-permute-start.11 = (bf16[32,3072]{1,0:T(8,128)(2,1)S(1)}, bf16[32,3072]{1,0:T(8,128)(2,1)S(1)}, u32[]{:S(2)}, u32[]{:S(2)}) collective-permute-start(bf16[32,3072]{1,0:T(8,128)(2,1)S(1)} %get-tuple-element.41), channel_id=1, source_target_pairs={{0,2},{2,4},{4,6},{6,7},{7,5},{5,3},{3,1},{1,0},{8,10},{10,12},{12... | collective-permute-start | bytes 589832 | tf_op jit(solution)/shard_map/ppermute | solution.py:71
  118.6 5.7 %collective-permute-start.14 = (bf16[32,3072]{1,0:T(8,128)(2,1)S(1)}, bf16[32,3072]{1,0:T(8,128)(2,1)S(1)}, u32[]{:S(2)}, u32[]{:S(2)}) collective-permute-start(bf16[32,3072]{1,0:T(8,128)(2,1)S(1)} %fusion.45), channel_id=1, source_target_pairs={{0,1},{2,0},{4,2},{6,4},{7,6},{5,7},{3,5},{1,3},{8,9},{10,8},{12,1... | collective-permute-start | bytes 589832 | tf_op jit(solution)/shard_map/ppermute | solution.py:76
  125.6 7.7 %collective-permute-start.15 = (bf16[32,3072]{1,0:T(8,128)(2,1)S(1)}, bf16[32,3072]{1,0:T(8,128)(2,1)S(1)}, u32[]{:S(2)}, u32[]{:S(2)}) collective-permute-start(bf16[32,3072]{1,0:T(8,128)(2,1)S(1)} %get-tuple-element.26), channel_id=1, source_target_pairs={{0,2},{2,4},{4,6},{6,7},{7,5},{5,3},{3,1},{1,0},{8,10},{10,12},{12... | collective-permute-start | bytes 589832 | tf_op jit(solution)/shard_map/ppermute | solution.py:45
  126.8 7.8 %collective-permute-start.16 = (bf16[32,3072]{1,0:T(8,128)(2,1)S(1)}, bf16[32,3072]{1,0:T(8,128)(2,1)S(1)}, u32[]{:S(2)}, u32[]{:S(2)}) collective-permute-start(bf16[32,3072]{1,0:T(8,128)(2,1)S(1)} %get-tuple-element.26), channel_id=1, source_target_pairs={{0,1},{2,0},{4,2},{6,4},{7,6},{5,7},{3,5},{1,3},{8,9},{10,8},{12,1... | collective-permute-start | bytes 589832 | tf_op jit(solution)/shard_map/ppermute | solution.py:48
  133.3 7.0 %collective-permute-start.17 = (bf16[32,3072]{1,0:T(8,128)(2,1)S(1)}, bf16[32,3072]{1,0:T(8,128)(2,1)S(1)}, u32[]{:S(2)}, u32[]{:S(2)}) collective-permute-start(bf16[32,3072]{1,0:T(8,128)(2,1)S(1)} %collective-permute-done.15), channel_id=1, source_target_pairs={{0,2},{2,4},{4,6},{6,7},{7,5},{5,3},{3,1},{1,0},{8,10},{10,12},{12... | collective-permute-start | bytes 589832 | tf_op jit(solution)/shard_map/ppermute | solution.py:45
  134.6 6.3 %collective-permute-start.18 = (bf16[32,3072]{1,0:T(8,128)(2,1)S(1)}, bf16[32,3072]{1,0:T(8,128)(2,1)S(1)}, u32[]{:S(2)}, u32[]{:S(2)}) collective-permute-start(bf16[32,3072]{1,0:T(8,128)(2,1)S(1)} %collective-permute-done.16), channel_id=1, source_target_pairs={{0,1},{2,0},{4,2},{6,4},{7,6},{5,7},{3,5},{1,3},{8,9},{10,8},{12,1... | collective-permute-start | bytes 589832 | tf_op jit(solution)/shard_map/ppermute | solution.py:48
  140.3 5.7 %collective-permute-start.19 = (bf16[32,3072]{1,0:T(8,128)(2,1)S(1)}, bf16[32,3072]{1,0:T(8,128)(2,1)S(1)}, u32[]{:S(2)}, u32[]{:S(2)}) collective-permute-start(bf16[32,3072]{1,0:T(8,128)(2,1)S(1)} %collective-permute-done.17), channel_id=1, source_target_pairs={{0,2},{2,4},{4,6},{6,7},{7,5},{5,3},{3,1},{1,0},{8,10},{10,12},{12... | collective-permute-start | bytes 589832 | tf_op jit(solution)/shard_map/ppermute | solution.py:45
  140.9 5.7 %collective-permute-start.20 = (bf16[32,3072]{1,0:T(8,128)(2,1)S(1)}, bf16[32,3072]{1,0:T(8,128)(2,1)S(1)}, u32[]{:S(2)}, u32[]{:S(2)}) collective-permute-start(bf16[32,3072]{1,0:T(8,128)(2,1)S(1)} %collective-permute-done.18), channel_id=1, source_target_pairs={{0,1},{2,0},{4,2},{6,4},{7,6},{5,7},{3,5},{1,3},{8,9},{10,8},{12,1... | collective-permute-start | bytes 589832 | tf_op jit(solution)/shard_map/ppermute | solution.py:48
  146.0 5.7 %collective-permute-start.21 = (bf16[32,3072]{1,0:T(8,128)(2,1)S(1)}, bf16[32,3072]{1,0:T(8,128)(2,1)S(1)}, u32[]{:S(2)}, u32[]{:S(2)}) collective-permute-start(bf16[32,3072]{1,0:T(8,128)(2,1)S(1)} %collective-permute-done.19), channel_id=1, source_target_pairs={{0,2},{2,4},{4,6},{6,7},{7,5},{5,3},{3,1},{1,0},{8,10},{10,12},{12... | collective-permute-start | bytes 589832 | tf_op jit(solution)/shard_map/ppermute | solution.py:45
  152.6 1.2 copy-start.3
  153.9 4.8 %collective-permute-start.22 = (bf16[128,3072]{1,0:T(8,128)(2,1)S(1)}, bf16[128,3072]{1,0:T(8,128)(2,1)}, u32[]{:S(2)}, u32[]{:S(2)}) collective-permute-start(bf16[128,3072]{1,0:T(8,128)(2,1)S(1)} %slice.49), channel_id=1, source_target_pairs={{0,8},{1,9},{2,10},{3,11},{4,12},{5,13},{6,14},{7,15},{16,24},{17,... | collective-permute-start | bytes 2359304 | tf_op jit(solution)/shard_map/ppermute | solution.py:14
  158.2 1.4 copy-start.4
  180.3 6.1 %collective-permute-start.23 = (bf16[32,3072]{1,0:T(8,128)(2,1)S(1)}, bf16[32,3072]{1,0:T(8,128)(2,1)S(1)}, u32[]{:S(2)}, u32[]{:S(2)}) collective-permute-start(bf16[32,3072]{1,0:T(8,128)(2,1)S(1)} %get-tuple-element.39), channel_id=1, source_target_pairs={{0,2},{2,4},{4,6},{6,7},{7,5},{5,3},{3,1},{1,0},{8,10},{10,12},{12... | collective-permute-start | bytes 589832 | tf_op jit(solution)/shard_map/ppermute | solution.py:71
  186.5 7.3 %collective-permute-start.24 = (bf16[32,3072]{1,0:T(8,128)(2,1)S(1)}, bf16[32,3072]{1,0:T(8,128)(2,1)S(1)}, u32[]{:S(2)}, u32[]{:S(2)}) collective-permute-start(bf16[32,3072]{1,0:T(8,128)(2,1)S(1)} %fusion.38), channel_id=1, source_target_pairs={{0,2},{2,4},{4,6},{6,7},{7,5},{5,3},{3,1},{1,0},{8,10},{10,12},{12... | collective-permute-start | bytes 589832 | tf_op jit(solution)/shard_map/ppermute | solution.py:71
  187.1 7.3 %collective-permute-start.27 = (bf16[32,3072]{1,0:T(8,128)(2,1)S(1)}, bf16[32,3072]{1,0:T(8,128)(2,1)S(1)}, u32[]{:S(2)}, u32[]{:S(2)}) collective-permute-start(bf16[32,3072]{1,0:T(8,128)(2,1)S(1)} %get-tuple-element.40), channel_id=1, source_target_pairs={{0,1},{2,0},{4,2},{6,4},{7,6},{5,7},{3,5},{1,3},{8,9},{10,8},{12,1... | collective-permute-start | bytes 589832 | tf_op jit(solution)/shard_map/ppermute | solution.py:76
  193.8 7.8 %collective-permute-start.25 = (bf16[32,3072]{1,0:T(8,128)(2,1)S(1)}, bf16[32,3072]{1,0:T(8,128)(2,1)S(1)}, u32[]{:S(2)}, u32[]{:S(2)}) collective-permute-start(bf16[32,3072]{1,0:T(8,128)(2,1)S(1)} %fusion.39), channel_id=1, source_target_pairs={{0,2},{2,4},{4,6},{6,7},{7,5},{5,3},{3,1},{1,0},{8,10},{10,12},{12... | collective-permute-start | bytes 589832 | tf_op jit(solution)/shard_map/ppermute | solution.py:71
  201.7 6.1 %collective-permute-start.28 = (bf16[32,3072]{1,0:T(8,128)(2,1)S(1)}, bf16[32,3072]{1,0:T(8,128)(2,1)S(1)}, u32[]{:S(2)}, u32[]{:S(2)}) collective-permute-start(bf16[32,3072]{1,0:T(8,128)(2,1)S(1)} %get-tuple-element.38), channel_id=1, source_target_pairs={{0,1},{2,0},{4,2},{6,4},{7,6},{5,7},{3,5},{1,3},{8,9},{10,8},{12,1... | collective-permute-start | bytes 589832 | tf_op jit(solution)/shard_map/ppermute | solution.py:76
  201.8 7.3 %collective-permute-start.26 = (bf16[32,3072]{1,0:T(8,128)(2,1)S(1)}, bf16[32,3072]{1,0:T(8,128)(2,1)S(1)}, u32[]{:S(2)}, u32[]{:S(2)}) collective-permute-start(bf16[32,3072]{1,0:T(8,128)(2,1)S(1)} %get-tuple-element.37), channel_id=1, source_target_pairs={{0,2},{2,4},{4,6},{6,7},{7,5},{5,3},{3,1},{1,0},{8,10},{10,12},{12... | collective-permute-start | bytes 589832 | tf_op jit(solution)/shard_map/ppermute | solution.py:71
  207.9 5.7 %collective-permute-start.29 = (bf16[32,3072]{1,0:T(8,128)(2,1)S(1)}, bf16[32,3072]{1,0:T(8,128)(2,1)S(1)}, u32[]{:S(2)}, u32[]{:S(2)}) collective-permute-start(bf16[32,3072]{1,0:T(8,128)(2,1)S(1)} %fusion.37), channel_id=1, source_target_pairs={{0,1},{2,0},{4,2},{6,4},{7,6},{5,7},{3,5},{1,3},{8,9},{10,8},{12,1... | collective-permute-start | bytes 589832 | tf_op jit(solution)/shard_map/ppermute | solution.py:76
  213.9 7.5 %collective-permute-start.30 = (bf16[32,3072]{1,0:T(8,128)(2,1)S(1)}, bf16[32,3072]{1,0:T(8,128)(2,1)S(1)}, u32[]{:S(2)}, u32[]{:S(2)}) collective-permute-start(bf16[32,3072]{1,0:T(8,128)(2,1)S(1)} %get-tuple-element.24), channel_id=1, source_target_pairs={{0,2},{2,4},{4,6},{6,7},{7,5},{5,3},{3,1},{1,0},{8,10},{10,12},{12... | collective-permute-start | bytes 589832 | tf_op jit(solution)/shard_map/ppermute | solution.py:45
  214.0 7.4 %collective-permute-start.31 = (bf16[32,3072]{1,0:T(8,128)(2,1)S(1)}, bf16[32,3072]{1,0:T(8,128)(2,1)S(1)}, u32[]{:S(2)}, u32[]{:S(2)}) collective-permute-start(bf16[32,3072]{1,0:T(8,128)(2,1)S(1)} %get-tuple-element.24), channel_id=1, source_target_pairs={{0,1},{2,0},{4,2},{6,4},{7,6},{5,7},{3,5},{1,3},{8,9},{10,8},{12,1... | collective-permute-start | bytes 589832 | tf_op jit(solution)/shard_map/ppermute | solution.py:48
  221.4 6.6 %collective-permute-start.32 = (bf16[32,3072]{1,0:T(8,128)(2,1)S(1)}, bf16[32,3072]{1,0:T(8,128)(2,1)S(1)}, u32[]{:S(2)}, u32[]{:S(2)}) collective-permute-start(bf16[32,3072]{1,0:T(8,128)(2,1)S(1)} %collective-permute-done.30), channel_id=1, source_target_pairs={{0,2},{2,4},{4,6},{6,7},{7,5},{5,3},{3,1},{1,0},{8,10},{10,12},{12... | collective-permute-start | bytes 589832 | tf_op jit(solution)/shard_map/ppermute | solution.py:45
  221.4 7.3 %collective-permute-start.33 = (bf16[32,3072]{1,0:T(8,128)(2,1)S(1)}, bf16[32,3072]{1,0:T(8,128)(2,1)S(1)}, u32[]{:S(2)}, u32[]{:S(2)}) collective-permute-start(bf16[32,3072]{1,0:T(8,128)(2,1)S(1)} %collective-permute-done.31), channel_id=1, source_target_pairs={{0,1},{2,0},{4,2},{6,4},{7,6},{5,7},{3,5},{1,3},{8,9},{10,8},{12,1... | collective-permute-start | bytes 589832 | tf_op jit(solution)/shard_map/ppermute | solution.py:48
  228.0 5.7 %collective-permute-start.34 = (bf16[32,3072]{1,0:T(8,128)(2,1)S(1)}, bf16[32,3072]{1,0:T(8,128)(2,1)S(1)}, u32[]{:S(2)}, u32[]{:S(2)}) collective-permute-start(bf16[32,3072]{1,0:T(8,128)(2,1)S(1)} %collective-permute-done.32), channel_id=1, source_target_pairs={{0,2},{2,4},{4,6},{6,7},{7,5},{5,3},{3,1},{1,0},{8,10},{10,12},{12... | collective-permute-start | bytes 589832 | tf_op jit(solution)/shard_map/ppermute | solution.py:45
  228.7 11.1 %copy-start.7 = (f32[1,3072]{1,0:T(1,128)S(1)}, f32[1,3072]{1,0:T(1,128)}, u32[]{:S(2)}) copy-start(f32[1,3072]{1,0:T(1,128)} %get-tuple-element.45) | copy-start | bytes 36868
  228.7 11.1 %copy-start.9 = (bf16[3072,3,1,128]{3,0,2,1:T(8,128)(2,1)S(1)}, bf16[3072,3,1,128]{3,0,2,1:T(8,128)(2,1)}, u32[]{:S(2)}) copy-start(bf16[3072,3,1,128]{3,0,2,1:T(8,128)(2,1)} %param.26) | copy-start | bytes 7077892
  228.7 5.7 %collective-permute-start.35 = (bf16[32,3072]{1,0:T(8,128)(2,1)S(1)}, bf16[32,3072]{1,0:T(8,128)(2,1)S(1)}, u32[]{:S(2)}, u32[]{:S(2)}) collective-permute-start(bf16[32,3072]{1,0:T(8,128)(2,1)S(1)} %collective-permute-done.33), channel_id=1, source_target_pairs={{0,1},{2,0},{4,2},{6,4},{7,6},{5,7},{3,5},{1,3},{8,9},{10,8},{12,1... | collective-permute-start | bytes 589832 | tf_op jit(solution)/shard_map/ppermute | solution.py:48
  233.7 5.7 %collective-permute-start.36 = (bf16[32,3072]{1,0:T(8,128)(2,1)S(1)}, bf16[32,3072]{1,0:T(8,128)(2,1)S(1)}, u32[]{:S(2)}, u32[]{:S(2)}) collective-permute-start(bf16[32,3072]{1,0:T(8,128)(2,1)S(1)} %collective-permute-done.34), channel_id=1, source_target_pairs={{0,2},{2,4},{4,6},{6,7},{7,5},{5,3},{3,1},{1,0},{8,10},{10,12},{12... | collective-permute-start | bytes 589832 | tf_op jit(solution)/shard_map/ppermute | solution.py:45
  241.8 3.7 %collective-permute-start.37 = (bf16[256,128]{1,0:T(8,128)(2,1)S(1)}, bf16[256,128]{1,0:T(8,128)(2,1)S(1)}, u32[]{:S(2)}, u32[]{:S(2)}) collective-permute-start(bf16[256,128]{1,0:T(8,128)(2,1)S(1)} %convolution_convert_fusion.4), channel_id=1, source_target_pairs={{0,8},{1,9},{2,10},{3,11},{4,12},{5,13},{6,14},{7,15},{16,24},{17,... | collective-permute-start | bytes 196616 | tf_op jit(solution)/shard_map/ppermute | solution.py:14
  243.4 2.2 collective-permute-start.38
  247.6 6.6 %collective-permute-start.39 = (bf16[32,3072]{1,0:T(8,128)(2,1)S(1)}, bf16[32,3072]{1,0:T(8,128)(2,1)S(1)}, u32[]{:S(2)}, u32[]{:S(2)}) collective-permute-start(bf16[32,3072]{1,0:T(8,128)(2,1)S(1)} %get-tuple-element.35), channel_id=1, source_target_pairs={{0,2},{2,4},{4,6},{6,7},{7,5},{5,3},{3,1},{1,0},{8,10},{10,12},{12... | collective-permute-start | bytes 589832 | tf_op jit(solution)/shard_map/ppermute | solution.py:71
  254.2 7.7 %collective-permute-start.40 = (bf16[32,3072]{1,0:T(8,128)(2,1)S(1)}, bf16[32,3072]{1,0:T(8,128)(2,1)S(1)}, u32[]{:S(2)}, u32[]{:S(2)}) collective-permute-start(bf16[32,3072]{1,0:T(8,128)(2,1)S(1)} %fusion.30), channel_id=1, source_target_pairs={{0,2},{2,4},{4,6},{6,7},{7,5},{5,3},{3,1},{1,0},{8,10},{10,12},{12... | collective-permute-start | bytes 589832 | tf_op jit(solution)/shard_map/ppermute | solution.py:71
  254.9 7.8 %collective-permute-start.43 = (bf16[32,3072]{1,0:T(8,128)(2,1)S(1)}, bf16[32,3072]{1,0:T(8,128)(2,1)S(1)}, u32[]{:S(2)}, u32[]{:S(2)}) collective-permute-start(bf16[32,3072]{1,0:T(8,128)(2,1)S(1)} %get-tuple-element.36), channel_id=1, source_target_pairs={{0,1},{2,0},{4,2},{6,4},{7,6},{5,7},{3,5},{1,3},{8,9},{10,8},{12,1... | collective-permute-start | bytes 589832 | tf_op jit(solution)/shard_map/ppermute | solution.py:76
  262.0 7.1 %collective-permute-start.41 = (bf16[32,3072]{1,0:T(8,128)(2,1)S(1)}, bf16[32,3072]{1,0:T(8,128)(2,1)S(1)}, u32[]{:S(2)}, u32[]{:S(2)}) collective-permute-start(bf16[32,3072]{1,0:T(8,128)(2,1)S(1)} %fusion.31), channel_id=1, source_target_pairs={{0,2},{2,4},{4,6},{6,7},{7,5},{5,3},{3,1},{1,0},{8,10},{10,12},{12... | collective-permute-start | bytes 589832 | tf_op jit(solution)/shard_map/ppermute | solution.py:71
  269.2 6.3 %collective-permute-start.44 = (bf16[32,3072]{1,0:T(8,128)(2,1)S(1)}, bf16[32,3072]{1,0:T(8,128)(2,1)S(1)}, u32[]{:S(2)}, u32[]{:S(2)}) collective-permute-start(bf16[32,3072]{1,0:T(8,128)(2,1)S(1)} %get-tuple-element.34), channel_id=1, source_target_pairs={{0,1},{2,0},{4,2},{6,4},{7,6},{5,7},{3,5},{1,3},{8,9},{10,8},{12,1... | collective-permute-start | bytes 589832 | tf_op jit(solution)/shard_map/ppermute | solution.py:76
  270.0 6.6 %collective-permute-start.42 = (bf16[32,3072]{1,0:T(8,128)(2,1)S(1)}, bf16[32,3072]{1,0:T(8,128)(2,1)S(1)}, u32[]{:S(2)}, u32[]{:S(2)}) collective-permute-start(bf16[32,3072]{1,0:T(8,128)(2,1)S(1)} %get-tuple-element.33), channel_id=1, source_target_pairs={{0,2},{2,4},{4,6},{6,7},{7,5},{5,3},{3,1},{1,0},{8,10},{10,12},{12... | collective-permute-start | bytes 589832 | tf_op jit(solution)/shard_map/ppermute | solution.py:71
  275.5 5.7 %collective-permute-start.45 = (bf16[32,3072]{1,0:T(8,128)(2,1)S(1)}, bf16[32,3072]{1,0:T(8,128)(2,1)S(1)}, u32[]{:S(2)}, u32[]{:S(2)}) collective-permute-start(bf16[32,3072]{1,0:T(8,128)(2,1)S(1)} %fusion.29), channel_id=1, source_target_pairs={{0,1},{2,0},{4,2},{6,4},{7,6},{5,7},{3,5},{1,3},{8,9},{10,8},{12,1... | collective-permute-start | bytes 589832 | tf_op jit(solution)/shard_map/ppermute | solution.py:76

commit v4 on v3

--- a/solution.py
+++ b/solution.py
@@ -37,11 +37,20 @@
     ahead = length // 2
     behind = length - 1 - ahead
     rows = value.shape[0]
+    split = behind < ahead and rows % 2 == 0
+    half = rows // 2
     out = jnp.zeros((length * rows,) + value.shape[1:], value.dtype)
     out = lax.dynamic_update_slice_in_dim(out, value, order_arr[me] * rows, 0)
     fwd = value
     bwd = value
     for k in range(1, ahead + 1):
+        if k == ahead and split:
+            fwd = lax.ppermute(fwd[:half], axis, forward)
+            bwd = lax.ppermute(bwd[half:], axis, backward)
+            far = order_arr[(me - k) % length] * rows
+            out = lax.dynamic_update_slice_in_dim(out, fwd, far, 0)
+            out = lax.dynamic_update_slice_in_dim(out, bwd, far + half, 0)
+            break
         fwd = lax.ppermute(fwd, axis, forward)
         out = lax.dynamic_update_slice_in_dim(out, fwd, order_arr[(me - k) % length] * rows, 0)
         if k <= behind:
@@ -56,27 +65,39 @@
     backward = [(order[p], order[(p - 1) % length]) for p in range(length)]
     ahead = length // 2
     behind = length - 1 - ahead
-    blocks = value.reshape((length, value.shape[0] // length) + value.shape[1:])
+    rows = value.shape[0] // length
+    split = behind < ahead and rows % 2 == 0
+    half = rows // 2
+    blocks = value.reshape((length, rows) + value.shape[1:])
 
     def own(offset):
         return lax.dynamic_index_in_dim(blocks, order_arr[(me + offset) % length], 0, keepdims=False).astype(jnp.float32)
 
+    def chain(offsets, pairs, first_rows):
+        passed = None
+        for step, offset in enumerate(offsets):
+            part = own(offset)
+            if step == 0:
+                part = part[first_rows]
+            elif step == 1 and passed.shape[0] != rows:
+                part = part.at[first_rows].add(passed.astype(jnp.float32))
+            else:
+                part = part + passed.astype(jnp.float32)
+            passed = lax.ppermute(part.astype(value.dtype), axis, pairs)
+        return passed
+
+    fwd_offsets = list(range(ahead, 0, -1))
+    bwd_offsets = list(range(-behind, 0))
+    fwd_rows = slice(0, rows)
+    bwd_rows = slice(0, rows)
+    if split:
+        bwd_offsets = [-ahead] + bwd_offsets
+        fwd_rows = slice(0, half)
+        bwd_rows = slice(half, rows)
     total = own(0)
-    fwd = None
-    bwd = None
-    for k in range(1, ahead + 1):
-        part = own(ahead + 1 - k)
-        if fwd is not None:
-            part = part + fwd.astype(jnp.float32)
-        fwd = lax.ppermute(part.astype(value.dtype), axis, forward)
-        if k <= behind:
-            part = own(k - behind - 1)
-            if bwd is not None:
-                part = part + bwd.astype(jnp.float32)
-            bwd = lax.ppermute(part.astype(value.dtype), axis, backward)
-    total = total + fwd.astype(jnp.float32)
-    if bwd is not None:
-        total = total + bwd.astype(jnp.float32)
+    total = total + chain(fwd_offsets, forward, fwd_rows).astype(jnp.float32)
+    if bwd_offsets:
+        total = total + chain(bwd_offsets, backward, bwd_rows).astype(jnp.float32)
     return total
 
 

time: 283 us -> 284 us (level)
  waiting for transfers between devices: 117 us -> 106 us
  starting transfers between devices: 50.3 us -> 59.8 us
    ppermute x12 -> x9, waiting for transfers between devices: 49 us -> 32.6 us  [ring_gather(): fwd = lax.ppermute(fwd, axis, forward)]
    ppermute x21 -> x30, starting transfers between devices: 20.9 us -> 34.1 us  [the longest x24 28.7 us: chain(): passed = lax.ppermute(part.astype(value.dtype), axis, pairs)]
    ppermute x21 -> x30, waiting for transfers between devices: 66.6 us -> 69.8 us  [the longest x24 58.1 us: chain(): passed = lax.ppermute(part.astype(value.dtype), axis, pairs)]
    ppermute x12 -> x9, starting transfers between devices: 13.5 us -> 11.2 us  [ring_gather(): fwd = lax.ppermute(fwd, axis, forward)]
  transfers between devices with their start and end apart: 46 -> 52, of which waited for: 33 -> 37; matrix products, arithmetic and copies ran while one was open for 10% -> 10% of each run, Pallas kernels for 0% -> 0%
where the time goes in v4:
time: 284 us; the launch traced here: 283 us
  waiting for transfers between devices  106 us (37%)
  starting transfers between devices  59.8 us (21%)
  between operations  35.6 us (13%)
  local copies, waits for them, and re-layouts  30.7 us (11%)
  Pallas kernels  25 us (9%)
  other arithmetic  17.7 us (6%)
  matrix products  8.54 us (3%)
    ppermute x24, waiting for transfers between devices, chain(): passed = lax.ppermute(part.astype(value.dtype), axis, pairs)  58.1 us
    ppermute x9, waiting for transfers between devices, ring_gather(): fwd = lax.ppermute(fwd, axis, forward)  32.6 us
    ppermute x24, starting transfers between devices, chain(): passed = lax.ppermute(part.astype(value.dtype), axis, pairs)  28.7 us
    pallas_call x2, Pallas kernels, convolution_gate(): pl.pallas_call(conv_gate_kernel, out_shape=jax.ShapeDtypeStruct((all_rows...  25 us
    unnamed x21, local copies, waits for them, and re-layouts  23.9 us
    another operation x6, other arithmetic, convolution_gate(): jnp.stack([lax.dynamic_slice_in_dim(padded, border_rows - tap_idx * dilat...  11.8 us
    ppermute x9, starting transfers between devices, ring_gather(): fwd = lax.ppermute(fwd, axis, forward)  11.2 us
    ppermute x9, starting transfers between devices, ring_gather(): bwd = lax.ppermute(bwd, axis, backward)  7.6 us
  transfers between devices with their start and end apart: 52, of which 37 were waited for; matrix products, arithmetic and copies ran while one was open for 10% of the time, Pallas kernels for 0%

profile of v4, /device:TPU:0, one launch (start us, length us, event | category | flops | bytes accessed | tf_op | source)
XLA Modules:
  0.0 283.0 jit_solution(8019621080123477098)
XLA Ops:
  0.0 3.0 %collective-permute-start = (bf16[32,3072]{1,0:T(8,128)(2,1)}, bf16[32,3072]{1,0:T(8,128)(2,1)S(1)}, u32[]{:S(2)}, u32[]{:S(2)}) collective-permute-start(bf16[32,3072]{1,0:T(8,128)(2,1)} %param.33), channel_id=1, source_target_pairs={{0,2},{2,4},{4,6},{6,7},{7,5},{5,3},{3,1},{1,0},{8,10},{10,12},{12... | collective-permute-start | bytes 589832 | tf_op jit(solution)/shard_map/ppermute | solution.py:54
  12.8 1.7 fusion.89
  19.7 1.6 fusion.88
  21.4 2.1 collective-permute-start.2
  23.6 4.3 %collective-permute-done.2 = bf16[32,3072]{1,0:T(8,128)(2,1)S(1)} collective-permute-done((bf16[32,3072]{1,0:T(8,128)(2,1)S(1)}, bf16[32,3072]{1,0:T(8,128)(2,1)S(1)}, u32[]{:S(2)}, u32[]{:S(2)}) %collective-permute-start.2) | collective-permute-done | bytes 196640 | tf_op jit(solution)/shard_map/ppermute | solution.py:54
  27.9 1.7 collective-permute-start.4
  29.9 3.6 %collective-permute-done.4 = bf16[32,3072]{1,0:T(8,128)(2,1)S(1)} collective-permute-done((bf16[32,3072]{1,0:T(8,128)(2,1)S(1)}, bf16[32,3072]{1,0:T(8,128)(2,1)S(1)}, u32[]{:S(2)}, u32[]{:S(2)}) %collective-permute-start.4) | collective-permute-done | bytes 196640 | tf_op jit(solution)/shard_map/ppermute | solution.py:54
  33.5 1.9 collective-permute-start.6
  35.7 2.5 collective-permute-done.6
  38.2 1.9 collective-permute-done.7
  42.3 2.2 collective-permute-start.8
  53.6 19.7 %copy.22 = bf16[2,3,3072,2,384]{4,2,3,1,0:T(8,128)(2,1)} copy(bf16[2,3,3072,2,384]{4,3,2,1,0:T(2,128)(2,1)} %param.36) | data formatting | bytes 56623104 | tf_op args[3]
  77.9 2.9 %fusion.25 = (bf16[1,256,3072]{2,1,0:T(8,128)(2,1)S(1)}, bf16[1,256,3072]{2,1,0:T(8,128)(2,1)S(1)}) fusion(s32[]{:T(128)S(6)} %select_n.560, bf16[256,3072]{1,0:T(8,128)(2,1)S(1)} %copy-done.2, bf16[128,3072]{1,0:T(8,128)(2,1)} %collective-permute-done.8, s32[]{:T(128)S(6)} %select_n.561), kind=kLoop, calls=%fused_computation.46 | loop fusion | flops 6291456 | bytes 5505032 | tf_op jit(solution)/shard_map/stack | solution.py:141
  80.7 2.4 pad_maximum_fusion.slab_ref
  83.2 12.5 %shard_map.181 = bf16[256,384]{1,0:T(8,128)(2,1)} custom-call(bf16[3,256,3072]{2,1,0:T(8,128)(2,1)} %pad_maximum_fusion.slab_ref, bf16[2,3,2,3072,384]{4,3,2,1,0:T(8,128)(2,1)} %bitcast.183), custom_call_target="tpu_custom_call" | custom-call | flops 3623878656 | bytes 19070976 | tf_op jit(solution)/shard_map/pallas_call | solution.py:148
  95.7 2.8 convolution_convert_fusion.2
  98.7 1.8 collective-permute-start.9
  100.6 2.7 collective-permute-done.9
  103.4 1.9 collective-permute-start.10
  105.5 3.6 %collective-permute-done.10 = bf16[32,3072]{1,0:T(8,128)(2,1)S(1)} collective-permute-done((bf16[32,3072]{1,0:T(8,128)(2,1)S(1)}, bf16[32,3072]{1,0:T(8,128)(2,1)S(1)}, u32[]{:S(2)}, u32[]{:S(2)}) %collective-permute-start.10) | collective-permute-done | bytes 196640 | tf_op jit(solution)/shard_map/ppermute | solution.py:86
  109.1 1.9 collective-permute-start.11
  114.9 2.0 collective-permute-done.11
  117.0 1.6 collective-permute-start.15
  121.0 1.8 collective-permute-done.15
  122.8 2.6 collective-permute-start.16
  127.5 3.1 %collective-permute-done.16 = bf16[32,3072]{1,0:T(8,128)(2,1)S(1)} collective-permute-done((bf16[32,3072]{1,0:T(8,128)(2,1)S(1)}, bf16[32,3072]{1,0:T(8,128)(2,1)S(1)}, u32[]{:S(2)}, u32[]{:S(2)}) %collective-permute-start.16) | collective-permute-done | bytes 196640 | tf_op jit(solution)/shard_map/ppermute | solution.py:86
  131.9 2.5 collective-permute-start.18
  134.4 4.6 %collective-permute-done.17 = bf16[32,3072]{1,0:T(8,128)(2,1)S(1)} collective-permute-done((bf16[32,3072]{1,0:T(8,128)(2,1)S(1)}, bf16[32,3072]{1,0:T(8,128)(2,1)S(1)}, u32[]{:S(2)}, u32[]{:S(2)}) %collective-permute-start.17) | collective-permute-done | bytes 196640 | tf_op jit(solution)/shard_map/ppermute | solution.py:54
  139.0 2.1 collective-permute-start.20
  141.1 3.5 %collective-permute-done.19 = bf16[32,3072]{1,0:T(8,128)(2,1)S(1)} collective-permute-done((bf16[32,3072]{1,0:T(8,128)(2,1)S(1)}, bf16[32,3072]{1,0:T(8,128)(2,1)S(1)}, u32[]{:S(2)}, u32[]{:S(2)}) %collective-permute-start.19) | collective-permute-done | bytes 196640 | tf_op jit(solution)/shard_map/ppermute | solution.py:54
  144.7 2.0 collective-permute-start.22
  146.8 3.5 %collective-permute-done.21 = bf16[32,3072]{1,0:T(8,128)(2,1)S(1)} collective-permute-done((bf16[32,3072]{1,0:T(8,128)(2,1)S(1)}, bf16[32,3072]{1,0:T(8,128)(2,1)S(1)}, u32[]{:S(2)}, u32[]{:S(2)}) %collective-permute-start.21) | collective-permute-done | bytes 196640 | tf_op jit(solution)/shard_map/ppermute | solution.py:54
  150.6 1.9 collective-permute-start.24
  152.5 2.5 collective-permute-done.23
  157.8 2.2 collective-permute-start.25
  163.3 3.1 %fusion.21 = (bf16[1,256,3072]{2,1,0:T(8,128)(2,1)S(1)}, bf16[1,256,3072]{2,1,0:T(8,128)(2,1)S(1)}) fusion(s32[]{:T(128)S(6)} %select_n.613, bf16[256,3072]{1,0:T(8,128)(2,1)S(1)} %copy-done.4, bf16[128,3072]{1,0:T(8,128)(2,1)} %collective-permute-done.25, s32[]{:T(128)S(6)} %select_n.614), kind=kLoop, calls=%fused_computation.42 | loop fusion | flops 6291456 | bytes 5505032 | tf_op jit(solution)/shard_map/stack | solution.py:141
  166.3 2.4 pad_maximum_fusion.1.slab_ref
  168.8 12.5 %shard_map.182 = bf16[256,384]{1,0:T(8,128)(2,1)} custom-call(bf16[3,256,3072]{2,1,0:T(8,128)(2,1)} %pad_maximum_fusion.1.slab_ref, bf16[2,3,2,3072,384]{4,3,2,1,0:T(8,128)(2,1)} %bitcast.184), custom_call_target="tpu_custom_call" | custom-call | flops 3623878656 | bytes 19070976 | tf_op jit(solution)/shard_map/pallas_call | solution.py:148
  181.3 2.8 convolution_convert_fusion.1
  184.1 2.1 collective-permute-start.26
  186.3 2.7 collective-permute-done.26
  189.0 2.1 collective-permute-start.27
  191.2 4.6 %collective-permute-done.27 = bf16[32,3072]{1,0:T(8,128)(2,1)S(1)} collective-permute-done((bf16[32,3072]{1,0:T(8,128)(2,1)S(1)}, bf16[32,3072]{1,0:T(8,128)(2,1)S(1)}, u32[]{:S(2)}, u32[]{:S(2)}) %collective-permute-start.27) | collective-permute-done | bytes 196640 | tf_op jit(solution)/shard_map/ppermute | solution.py:86
  195.9 2.1 collective-permute-start.28
  198.0 5.0 %collective-permute-done.28 = bf16[32,3072]{1,0:T(8,128)(2,1)S(1)} collective-permute-done((bf16[32,3072]{1,0:T(8,128)(2,1)S(1)}, bf16[32,3072]{1,0:T(8,128)(2,1)S(1)}, u32[]{:S(2)}, u32[]{:S(2)}) %collective-permute-start.28) | collective-permute-done | bytes 196640 | tf_op jit(solution)/shard_map/ppermute | solution.py:86
  203.6 2.1 collective-permute-start.29
  205.7 3.7 %collective-permute-done.32 = bf16[32,3072]{1,0:T(8,128)(2,1)S(1)} collective-permute-done((bf16[32,3072]{1,0:T(8,128)(2,1)S(1)}, bf16[32,3072]{1,0:T(8,128)(2,1)S(1)}, u32[]{:S(2)}, u32[]{:S(2)}) %collective-permute-start.32) | collective-permute-done | bytes 196640 | tf_op jit(solution)/shard_map/ppermute | solution.py:86
  209.9 5.8 %collective-permute-done.33 = bf16[32,3072]{1,0:T(8,128)(2,1)S(1)} collective-permute-done((bf16[32,3072]{1,0:T(8,128)(2,1)S(1)}, bf16[32,3072]{1,0:T(8,128)(2,1)S(1)}, u32[]{:S(2)}, u32[]{:S(2)}) %collective-permute-start.33) | collective-permute-done | bytes 196640 | tf_op jit(solution)/shard_map/ppermute | solution.py:86
  216.0 1.8 collective-permute-start.34
  218.1 5.4 %collective-permute-done.34 = bf16[32,3072]{1,0:T(8,128)(2,1)S(1)} collective-permute-done((bf16[32,3072]{1,0:T(8,128)(2,1)S(1)}, bf16[32,3072]{1,0:T(8,128)(2,1)S(1)}, u32[]{:S(2)}, u32[]{:S(2)}) %collective-permute-start.34) | collective-permute-done | bytes 196640 | tf_op jit(solution)/shard_map/ppermute | solution.py:54
  223.5 1.5 collective-permute-start.36
  225.7 4.1 %collective-permute-done.36 = bf16[32,3072]{1,0:T(8,128)(2,1)S(1)} collective-permute-done((bf16[32,3072]{1,0:T(8,128)(2,1)S(1)}, bf16[32,3072]{1,0:T(8,128)(2,1)S(1)}, u32[]{:S(2)}, u32[]{:S(2)}) %collective-permute-start.36) | collective-permute-done | bytes 196640 | tf_op jit(solution)/shard_map/ppermute | solution.py:54
  231.9 3.5 %collective-permute-done.38 = bf16[32,3072]{1,0:T(8,128)(2,1)S(1)} collective-permute-done((bf16[32,3072]{1,0:T(8,128)(2,1)S(1)}, bf16[32,3072]{1,0:T(8,128)(2,1)S(1)}, u32[]{:S(2)}, u32[]{:S(2)}) %collective-permute-start.38) | collective-permute-done | bytes 196640 | tf_op jit(solution)/shard_map/ppermute | solution.py:54
  237.7 2.5 collective-permute-done.40
  240.1 1.8 collective-permute-done.41
  250.2 1.8 collective-permute-start.44
  252.5 2.4 collective-permute-done.44
  254.9 1.8 collective-permute-start.45
  257.2 5.2 %collective-permute-done.45 = bf16[32,3072]{1,0:T(8,128)(2,1)S(1)} collective-permute-done((bf16[32,3072]{1,0:T(8,128)(2,1)S(1)}, bf16[32,3072]{1,0:T(8,128)(2,1)S(1)}, u32[]{:S(2)}, u32[]{:S(2)}) %collective-permute-start.45) | collective-permute-done | bytes 196640 | tf_op jit(solution)/shard_map/ppermute | solution.py:86
  262.5 1.8 collective-permute-start.46
  264.7 5.1 %collective-permute-done.46 = bf16[32,3072]{1,0:T(8,128)(2,1)S(1)} collective-permute-done((bf16[32,3072]{1,0:T(8,128)(2,1)S(1)}, bf16[32,3072]{1,0:T(8,128)(2,1)S(1)}, u32[]{:S(2)}, u32[]{:S(2)}) %collective-permute-start.46) | collective-permute-done | bytes 196640 | tf_op jit(solution)/shard_map/ppermute | solution.py:86
  270.2 1.8 collective-permute-start.47
  272.0 4.4 %collective-permute-done.50 = bf16[32,3072]{1,0:T(8,128)(2,1)S(1)} collective-permute-done((bf16[32,3072]{1,0:T(8,128)(2,1)S(1)}, bf16[32,3072]{1,0:T(8,128)(2,1)S(1)}, u32[]{:S(2)}, u32[]{:S(2)}) %collective-permute-start.50) | collective-permute-done | bytes 196640 | tf_op jit(solution)/shard_map/ppermute | solution.py:86
  276.8 5.4 %collective-permute-done.51 = bf16[32,3072]{1,0:T(8,128)(2,1)S(1)} collective-permute-done((bf16[32,3072]{1,0:T(8,128)(2,1)S(1)}, bf16[32,3072]{1,0:T(8,128)(2,1)S(1)}, u32[]{:S(2)}, u32[]{:S(2)}) %collective-permute-start.51) | collective-permute-done | bytes 196640 | tf_op jit(solution)/shard_map/ppermute | solution.py:86
  (154 shorter events, 32.4 us)
Async XLA Ops:
  0.0 249.5 %copy-start = (bf16[1,128,3072]{2,1,0:T(8,128)(2,1)S(1)}, bf16[1,128,3072]{2,1,0:T(8,128)(2,1)}, u32[]{:S(2)}) copy-start(bf16[1,128,3072]{2,1,0:T(8,128)(2,1)} %param.39) | copy-start | bytes 2359300
  0.0 21.4 %copy-start.6 = (bf16[32,3072]{1,0:T(8,128)(2,1)S(1)}, bf16[32,3072]{1,0:T(8,128)(2,1)}, u32[]{:S(2)}) copy-start(bf16[32,3072]{1,0:T(8,128)(2,1)} %param.33) | copy-start | bytes 589828
  0.0 21.4 %collective-permute-start = (bf16[32,3072]{1,0:T(8,128)(2,1)}, bf16[32,3072]{1,0:T(8,128)(2,1)S(1)}, u32[]{:S(2)}, u32[]{:S(2)}) collective-permute-start(bf16[32,3072]{1,0:T(8,128)(2,1)} %param.33), channel_id=1, source_target_pairs={{0,2},{2,4},{4,6},{6,7},{7,5},{5,3},{3,1},{1,0},{8,10},{10,12},{12... | collective-permute-start | bytes 589832 | tf_op jit(solution)/shard_map/ppermute | solution.py:54
  3.0 20.5 %collective-permute-start.1 = (bf16[32,3072]{1,0:T(8,128)(2,1)}, bf16[32,3072]{1,0:T(8,128)(2,1)S(1)}, u32[]{:S(2)}, u32[]{:S(2)}) collective-permute-start(bf16[32,3072]{1,0:T(8,128)(2,1)} %param.33), channel_id=1, source_target_pairs={{0,1},{2,0},{4,2},{6,4},{7,6},{5,7},{3,5},{1,3},{8,9},{10,8},{12,1... | collective-permute-start | bytes 589832 | tf_op jit(solution)/shard_map/ppermute | solution.py:57
  21.4 6.4 %collective-permute-start.2 = (bf16[32,3072]{1,0:T(8,128)(2,1)S(1)}, bf16[32,3072]{1,0:T(8,128)(2,1)S(1)}, u32[]{:S(2)}, u32[]{:S(2)}) collective-permute-start(bf16[32,3072]{1,0:T(8,128)(2,1)S(1)} %collective-permute-done), channel_id=1, source_target_pairs={{0,2},{2,4},{4,6},{6,7},{7,5},{5,3},{3,1},{1,0},{8,10},{10,12},{12... | collective-permute-start | bytes 589832 | tf_op jit(solution)/shard_map/ppermute | solution.py:54
  23.5 6.1 %collective-permute-start.3 = (bf16[32,3072]{1,0:T(8,128)(2,1)S(1)}, bf16[32,3072]{1,0:T(8,128)(2,1)S(1)}, u32[]{:S(2)}, u32[]{:S(2)}) collective-permute-start(bf16[32,3072]{1,0:T(8,128)(2,1)S(1)} %collective-permute-done.1), channel_id=1, source_target_pairs={{0,1},{2,0},{4,2},{6,4},{7,6},{5,7},{3,5},{1,3},{8,9},{10,8},{12,1... | collective-permute-start | bytes 589832 | tf_op jit(solution)/shard_map/ppermute | solution.py:57
  27.9 5.7 %collective-permute-start.4 = (bf16[32,3072]{1,0:T(8,128)(2,1)S(1)}, bf16[32,3072]{1,0:T(8,128)(2,1)S(1)}, u32[]{:S(2)}, u32[]{:S(2)}) collective-permute-start(bf16[32,3072]{1,0:T(8,128)(2,1)S(1)} %collective-permute-done.2), channel_id=1, source_target_pairs={{0,2},{2,4},{4,6},{6,7},{7,5},{5,3},{3,1},{1,0},{8,10},{10,12},{12... | collective-permute-start | bytes 589832 | tf_op jit(solution)/shard_map/ppermute | solution.py:54
  29.6 5.8 %collective-permute-start.5 = (bf16[32,3072]{1,0:T(8,128)(2,1)S(1)}, bf16[32,3072]{1,0:T(8,128)(2,1)S(1)}, u32[]{:S(2)}, u32[]{:S(2)}) collective-permute-start(bf16[32,3072]{1,0:T(8,128)(2,1)S(1)} %collective-permute-done.3), channel_id=1, source_target_pairs={{0,1},{2,0},{4,2},{6,4},{7,6},{5,7},{3,5},{1,3},{8,9},{10,8},{12,1... | collective-permute-start | bytes 589832 | tf_op jit(solution)/shard_map/ppermute | solution.py:57
  33.5 4.7 %collective-permute-start.6 = (bf16[16,3072]{1,0:T(8,128)(2,1)S(1)}, bf16[16,3072]{1,0:T(8,128)(2,1)S(1)}, u32[]{:S(2)}, u32[]{:S(2)}) collective-permute-start(bf16[16,3072]{1,0:T(8,128)(2,1)S(1)} %slice.234), channel_id=1, source_target_pairs={{0,2},{2,4},{4,6},{6,7},{7,5},{5,3},{3,1},{1,0},{8,10},{10,12},{12... | collective-permute-start | bytes 294920 | tf_op jit(solution)/shard_map/ppermute | solution.py:48
  35.4 4.7 %collective-permute-start.7 = (bf16[16,3072]{1,0:T(8,128)(2,1)S(1)}, bf16[16,3072]{1,0:T(8,128)(2,1)S(1)}, u32[]{:S(2)}, u32[]{:S(2)}) collective-permute-start(bf16[16,3072]{1,0:T(8,128)(2,1)S(1)} %slice.235), channel_id=1, source_target_pairs={{0,1},{2,0},{4,2},{6,4},{7,6},{5,7},{3,5},{1,3},{8,9},{10,8},{12,1... | collective-permute-start | bytes 294920 | tf_op jit(solution)/shard_map/ppermute | solution.py:49
  41.0 1.2 copy-start.1
  42.2 2.2 copy-start.8
  42.3 34.7 %collective-permute-start.8 = (bf16[128,3072]{1,0:T(8,128)(2,1)S(1)}, bf16[128,3072]{1,0:T(8,128)(2,1)}, u32[]{:S(2)}, u32[]{:S(2)}) collective-permute-start(bf16[128,3072]{1,0:T(8,128)(2,1)S(1)} %slice.236), channel_id=1, source_target_pairs={{0,8},{1,9},{2,10},{3,11},{4,12},{5,13},{6,14},{7,15},{16,24},{17,... | collective-permute-start | bytes 2359304 | tf_op jit(solution)/shard_map/ppermute | solution.py:14
  76.5 1.4 copy-start.2
  98.4 24.3 %copy-start.5 = (bf16[256,3072]{1,0:T(8,128)(2,1)}, bf16[256,3072]{1,0:T(8,128)(2,1)S(1)}, u32[]{:S(2)}) copy-start(bf16[256,3072]{1,0:T(8,128)(2,1)S(1)} %convolution_convert_fusion.2) | copy-start | bytes 4718596
  98.5 6.8 %collective-permute-start.13 = (bf16[16,3072]{1,0:T(8,128)(2,1)S(1)}, bf16[16,3072]{1,0:T(8,128)(2,1)S(1)}, u32[]{:S(2)}, u32[]{:S(2)}) collective-permute-start(bf16[16,3072]{1,0:T(8,128)(2,1)S(1)} %get-tuple-element.124), channel_id=1, source_target_pairs={{0,1},{2,0},{4,2},{6,4},{7,6},{5,7},{3,5},{1,3},{8,9},{10,8},{12,1... | collective-permute-start | bytes 294920 | tf_op jit(solution)/shard_map/ppermute | solution.py:86
  98.7 4.6 %collective-permute-start.9 = (bf16[16,3072]{1,0:T(8,128)(2,1)S(1)}, bf16[16,3072]{1,0:T(8,128)(2,1)S(1)}, u32[]{:S(2)}, u32[]{:S(2)}) collective-permute-start(bf16[16,3072]{1,0:T(8,128)(2,1)S(1)} %get-tuple-element.123), channel_id=1, source_target_pairs={{0,2},{2,4},{4,6},{6,7},{7,5},{5,3},{3,1},{1,0},{8,10},{10,12},{12... | collective-permute-start | bytes 294920 | tf_op jit(solution)/shard_map/ppermute | solution.py:86
  103.4 5.7 %collective-permute-start.10 = (bf16[32,3072]{1,0:T(8,128)(2,1)S(1)}, bf16[32,3072]{1,0:T(8,128)(2,1)S(1)}, u32[]{:S(2)}, u32[]{:S(2)}) collective-permute-start(bf16[32,3072]{1,0:T(8,128)(2,1)S(1)} %fusion.62), channel_id=1, source_target_pairs={{0,2},{2,4},{4,6},{6,7},{7,5},{5,3},{3,1},{1,0},{8,10},{10,12},{12... | collective-permute-start | bytes 589832 | tf_op jit(solution)/shard_map/ppermute | solution.py:86
  105.3 9.6 %collective-permute-start.14 = (bf16[32,3072]{1,0:T(8,128)(2,1)S(1)}, bf16[32,3072]{1,0:T(8,128)(2,1)S(1)}, u32[]{:S(2)}, u32[]{:S(2)}) collective-permute-start(bf16[32,3072]{1,0:T(8,128)(2,1)S(1)} %fusion.60), channel_id=1, source_target_pairs={{0,1},{2,0},{4,2},{6,4},{7,6},{5,7},{3,5},{1,3},{8,9},{10,8},{12,1... | collective-permute-start | bytes 589832 | tf_op jit(solution)/shard_map/ppermute | solution.py:86
  109.1 7.8 %collective-permute-start.11 = (bf16[32,3072]{1,0:T(8,128)(2,1)S(1)}, bf16[32,3072]{1,0:T(8,128)(2,1)S(1)}, u32[]{:S(2)}, u32[]{:S(2)}) collective-permute-start(bf16[32,3072]{1,0:T(8,128)(2,1)S(1)} %fusion.44), channel_id=1, source_target_pairs={{0,2},{2,4},{4,6},{6,7},{7,5},{5,3},{3,1},{1,0},{8,10},{10,12},{12... | collective-permute-start | bytes 589832 | tf_op jit(solution)/shard_map/ppermute | solution.py:86
  117.0 5.7 %collective-permute-start.15 = (bf16[32,3072]{1,0:T(8,128)(2,1)S(1)}, bf16[32,3072]{1,0:T(8,128)(2,1)S(1)}, u32[]{:S(2)}, u32[]{:S(2)}) collective-permute-start(bf16[32,3072]{1,0:T(8,128)(2,1)S(1)} %get-tuple-element.122), channel_id=1, source_target_pairs={{0,1},{2,0},{4,2},{6,4},{7,6},{5,7},{3,5},{1,3},{8,9},{10,8},{12,1... | collective-permute-start | bytes 589832 | tf_op jit(solution)/shard_map/ppermute | solution.py:86
  120.5 7.0 %collective-permute-start.12 = (bf16[32,3072]{1,0:T(8,128)(2,1)S(1)}, bf16[32,3072]{1,0:T(8,128)(2,1)S(1)}, u32[]{:S(2)}, u32[]{:S(2)}) collective-permute-start(bf16[32,3072]{1,0:T(8,128)(2,1)S(1)} %get-tuple-element.121), channel_id=1, source_target_pairs={{0,2},{2,4},{4,6},{6,7},{7,5},{5,3},{3,1},{1,0},{8,10},{10,12},{12... | collective-permute-start | bytes 589832 | tf_op jit(solution)/shard_map/ppermute | solution.py:86
  122.8 7.8 %collective-permute-start.16 = (bf16[32,3072]{1,0:T(8,128)(2,1)S(1)}, bf16[32,3072]{1,0:T(8,128)(2,1)S(1)}, u32[]{:S(2)}, u32[]{:S(2)}) collective-permute-start(bf16[32,3072]{1,0:T(8,128)(2,1)S(1)} %fusion.43), channel_id=1, source_target_pairs={{0,1},{2,0},{4,2},{6,4},{7,6},{5,7},{3,5},{1,3},{8,9},{10,8},{12,1... | collective-permute-start | bytes 589832 | tf_op jit(solution)/shard_map/ppermute | solution.py:86
  131.8 7.2 %collective-permute-start.17 = (bf16[32,3072]{1,0:T(8,128)(2,1)S(1)}, bf16[32,3072]{1,0:T(8,128)(2,1)S(1)}, u32[]{:S(2)}, u32[]{:S(2)}) collective-permute-start(bf16[32,3072]{1,0:T(8,128)(2,1)S(1)} %get-tuple-element.98), channel_id=1, source_target_pairs={{0,2},{2,4},{4,6},{6,7},{7,5},{5,3},{3,1},{1,0},{8,10},{10,12},{12... | collective-permute-start | bytes 589832 | tf_op jit(solution)/shard_map/ppermute | solution.py:54
  131.9 7.1 %collective-permute-start.18 = (bf16[32,3072]{1,0:T(8,128)(2,1)S(1)}, bf16[32,3072]{1,0:T(8,128)(2,1)S(1)}, u32[]{:S(2)}, u32[]{:S(2)}) collective-permute-start(bf16[32,3072]{1,0:T(8,128)(2,1)S(1)} %get-tuple-element.98), channel_id=1, source_target_pairs={{0,1},{2,0},{4,2},{6,4},{7,6},{5,7},{3,5},{1,3},{8,9},{10,8},{12,1... | collective-permute-start | bytes 589832 | tf_op jit(solution)/shard_map/ppermute | solution.py:57
  139.0 5.7 %collective-permute-start.19 = (bf16[32,3072]{1,0:T(8,128)(2,1)S(1)}, bf16[32,3072]{1,0:T(8,128)(2,1)S(1)}, u32[]{:S(2)}, u32[]{:S(2)}) collective-permute-start(bf16[32,3072]{1,0:T(8,128)(2,1)S(1)} %collective-permute-done.17), channel_id=1, source_target_pairs={{0,2},{2,4},{4,6},{6,7},{7,5},{5,3},{3,1},{1,0},{8,10},{10,12},{12... | collective-permute-start | bytes 589832 | tf_op jit(solution)/shard_map/ppermute | solution.py:54
  139.0 5.7 %collective-permute-start.20 = (bf16[32,3072]{1,0:T(8,128)(2,1)S(1)}, bf16[32,3072]{1,0:T(8,128)(2,1)S(1)}, u32[]{:S(2)}, u32[]{:S(2)}) collective-permute-start(bf16[32,3072]{1,0:T(8,128)(2,1)S(1)} %collective-permute-done.18), channel_id=1, source_target_pairs={{0,1},{2,0},{4,2},{6,4},{7,6},{5,7},{3,5},{1,3},{8,9},{10,8},{12,1... | collective-permute-start | bytes 589832 | tf_op jit(solution)/shard_map/ppermute | solution.py:57
  144.6 5.7 %collective-permute-start.21 = (bf16[32,3072]{1,0:T(8,128)(2,1)S(1)}, bf16[32,3072]{1,0:T(8,128)(2,1)S(1)}, u32[]{:S(2)}, u32[]{:S(2)}) collective-permute-start(bf16[32,3072]{1,0:T(8,128)(2,1)S(1)} %collective-permute-done.19), channel_id=1, source_target_pairs={{0,2},{2,4},{4,6},{6,7},{7,5},{5,3},{3,1},{1,0},{8,10},{10,12},{12... | collective-permute-start | bytes 589832 | tf_op jit(solution)/shard_map/ppermute | solution.py:54
  144.7 5.9 %collective-permute-start.22 = (bf16[32,3072]{1,0:T(8,128)(2,1)S(1)}, bf16[32,3072]{1,0:T(8,128)(2,1)S(1)}, u32[]{:S(2)}, u32[]{:S(2)}) collective-permute-start(bf16[32,3072]{1,0:T(8,128)(2,1)S(1)} %collective-permute-done.20), channel_id=1, source_target_pairs={{0,1},{2,0},{4,2},{6,4},{7,6},{5,7},{3,5},{1,3},{8,9},{10,8},{12,1... | collective-permute-start | bytes 589832 | tf_op jit(solution)/shard_map/ppermute | solution.py:57
  150.3 4.7 %collective-permute-start.23 = (bf16[16,3072]{1,0:T(8,128)(2,1)S(1)}, bf16[16,3072]{1,0:T(8,128)(2,1)S(1)}, u32[]{:S(2)}, u32[]{:S(2)}) collective-permute-start(bf16[16,3072]{1,0:T(8,128)(2,1)S(1)} %slice.239), channel_id=1, source_target_pairs={{0,2},{2,4},{4,6},{6,7},{7,5},{5,3},{3,1},{1,0},{8,10},{10,12},{12... | collective-permute-start | bytes 294920 | tf_op jit(solution)/shard_map/ppermute | solution.py:48
  150.6 5.0 %collective-permute-start.24 = (bf16[16,3072]{1,0:T(8,128)(2,1)S(1)}, bf16[16,3072]{1,0:T(8,128)(2,1)S(1)}, u32[]{:S(2)}, u32[]{:S(2)}) collective-permute-start(bf16[16,3072]{1,0:T(8,128)(2,1)S(1)} %slice.240), channel_id=1, source_target_pairs={{0,1},{2,0},{4,2},{6,4},{7,6},{5,7},{3,5},{1,3},{8,9},{10,8},{12,1... | collective-permute-start | bytes 294920 | tf_op jit(solution)/shard_map/ppermute | solution.py:49
  156.6 1.2 copy-start.3
  157.8 4.6 %collective-permute-start.25 = (bf16[128,3072]{1,0:T(8,128)(2,1)S(1)}, bf16[128,3072]{1,0:T(8,128)(2,1)}, u32[]{:S(2)}, u32[]{:S(2)}) collective-permute-start(bf16[128,3072]{1,0:T(8,128)(2,1)S(1)} %slice.241), channel_id=1, source_target_pairs={{0,8},{1,9},{2,10},{3,11},{4,12},{5,13},{6,14},{7,15},{16,24},{17,... | collective-permute-start | bytes 2359304 | tf_op jit(solution)/shard_map/ppermute | solution.py:14
  161.9 1.4 copy-start.4
  184.1 4.9 %collective-permute-start.26 = (bf16[16,3072]{1,0:T(8,128)(2,1)S(1)}, bf16[16,3072]{1,0:T(8,128)(2,1)S(1)}, u32[]{:S(2)}, u32[]{:S(2)}) collective-permute-start(bf16[16,3072]{1,0:T(8,128)(2,1)S(1)} %get-tuple-element.115), channel_id=1, source_target_pairs={{0,2},{2,4},{4,6},{6,7},{7,5},{5,3},{3,1},{1,0},{8,10},{10,12},{12... | collective-permute-start | bytes 294920 | tf_op jit(solution)/shard_map/ppermute | solution.py:86
  186.2 4.9 %collective-permute-start.30 = (bf16[16,3072]{1,0:T(8,128)(2,1)S(1)}, bf16[16,3072]{1,0:T(8,128)(2,1)S(1)}, u32[]{:S(2)}, u32[]{:S(2)}) collective-permute-start(bf16[16,3072]{1,0:T(8,128)(2,1)S(1)} %get-tuple-element.116), channel_id=1, source_target_pairs={{0,1},{2,0},{4,2},{6,4},{7,6},{5,7},{3,5},{1,3},{8,9},{10,8},{12,1... | collective-permute-start | bytes 294920 | tf_op jit(solution)/shard_map/ppermute | solution.py:86
  189.0 6.8 %collective-permute-start.27 = (bf16[32,3072]{1,0:T(8,128)(2,1)S(1)}, bf16[32,3072]{1,0:T(8,128)(2,1)S(1)}, u32[]{:S(2)}, u32[]{:S(2)}) collective-permute-start(bf16[32,3072]{1,0:T(8,128)(2,1)S(1)} %fusion.58), channel_id=1, source_target_pairs={{0,2},{2,4},{4,6},{6,7},{7,5},{5,3},{3,1},{1,0},{8,10},{10,12},{12... | collective-permute-start | bytes 589832 | tf_op jit(solution)/shard_map/ppermute | solution.py:86
  191.1 6.8 %collective-permute-start.31 = (bf16[32,3072]{1,0:T(8,128)(2,1)S(1)}, bf16[32,3072]{1,0:T(8,128)(2,1)S(1)}, u32[]{:S(2)}, u32[]{:S(2)}) collective-permute-start(bf16[32,3072]{1,0:T(8,128)(2,1)S(1)} %fusion.56), channel_id=1, source_target_pairs={{0,1},{2,0},{4,2},{6,4},{7,6},{5,7},{3,5},{1,3},{8,9},{10,8},{12,1... | collective-permute-start | bytes 589832 | tf_op jit(solution)/shard_map/ppermute | solution.py:86
  195.9 7.1 %collective-permute-start.28 = (bf16[32,3072]{1,0:T(8,128)(2,1)S(1)}, bf16[32,3072]{1,0:T(8,128)(2,1)S(1)}, u32[]{:S(2)}, u32[]{:S(2)}) collective-permute-start(bf16[32,3072]{1,0:T(8,128)(2,1)S(1)} %fusion.37), channel_id=1, source_target_pairs={{0,2},{2,4},{4,6},{6,7},{7,5},{5,3},{3,1},{1,0},{8,10},{10,12},{12... | collective-permute-start | bytes 589832 | tf_op jit(solution)/shard_map/ppermute | solution.py:86
  203.1 6.3 %collective-permute-start.32 = (bf16[32,3072]{1,0:T(8,128)(2,1)S(1)}, bf16[32,3072]{1,0:T(8,128)(2,1)S(1)}, u32[]{:S(2)}, u32[]{:S(2)}) collective-permute-start(bf16[32,3072]{1,0:T(8,128)(2,1)S(1)} %get-tuple-element.114), channel_id=1, source_target_pairs={{0,1},{2,0},{4,2},{6,4},{7,6},{5,7},{3,5},{1,3},{8,9},{10,8},{12,1... | collective-permute-start | bytes 589832 | tf_op jit(solution)/shard_map/ppermute | solution.py:86
  203.6 6.3 %collective-permute-start.29 = (bf16[32,3072]{1,0:T(8,128)(2,1)S(1)}, bf16[32,3072]{1,0:T(8,128)(2,1)S(1)}, u32[]{:S(2)}, u32[]{:S(2)}) collective-permute-start(bf16[32,3072]{1,0:T(8,128)(2,1)S(1)} %get-tuple-element.113), channel_id=1, source_target_pairs={{0,2},{2,4},{4,6},{6,7},{7,5},{5,3},{3,1},{1,0},{8,10},{10,12},{12... | collective-permute-start | bytes 589832 | tf_op jit(solution)/shard_map/ppermute | solution.py:86
  209.5 6.3 %collective-permute-start.33 = (bf16[32,3072]{1,0:T(8,128)(2,1)S(1)}, bf16[32,3072]{1,0:T(8,128)(2,1)S(1)}, u32[]{:S(2)}, u32[]{:S(2)}) collective-permute-start(bf16[32,3072]{1,0:T(8,128)(2,1)S(1)} %fusion.36), channel_id=1, source_target_pairs={{0,1},{2,0},{4,2},{6,4},{7,6},{5,7},{3,5},{1,3},{8,9},{10,8},{12,1... | collective-permute-start | bytes 589832 | tf_op jit(solution)/shard_map/ppermute | solution.py:86
  216.0 7.5 %collective-permute-start.34 = (bf16[32,3072]{1,0:T(8,128)(2,1)S(1)}, bf16[32,3072]{1,0:T(8,128)(2,1)S(1)}, u32[]{:S(2)}, u32[]{:S(2)}) collective-permute-start(bf16[32,3072]{1,0:T(8,128)(2,1)S(1)} %get-tuple-element.96), channel_id=1, source_target_pairs={{0,2},{2,4},{4,6},{6,7},{7,5},{5,3},{3,1},{1,0},{8,10},{10,12},{12... | collective-permute-start | bytes 589832 | tf_op jit(solution)/shard_map/ppermute | solution.py:54
  217.8 7.7 %collective-permute-start.35 = (bf16[32,3072]{1,0:T(8,128)(2,1)S(1)}, bf16[32,3072]{1,0:T(8,128)(2,1)S(1)}, u32[]{:S(2)}, u32[]{:S(2)}) collective-permute-start(bf16[32,3072]{1,0:T(8,128)(2,1)S(1)} %get-tuple-element.96), channel_id=1, source_target_pairs={{0,1},{2,0},{4,2},{6,4},{7,6},{5,7},{3,5},{1,3},{8,9},{10,8},{12,1... | collective-permute-start | bytes 589832 | tf_op jit(solution)/shard_map/ppermute | solution.py:57
  223.5 6.2 %collective-permute-start.36 = (bf16[32,3072]{1,0:T(8,128)(2,1)S(1)}, bf16[32,3072]{1,0:T(8,128)(2,1)S(1)}, u32[]{:S(2)}, u32[]{:S(2)}) collective-permute-start(bf16[32,3072]{1,0:T(8,128)(2,1)S(1)} %collective-permute-done.34), channel_id=1, source_target_pairs={{0,2},{2,4},{4,6},{6,7},{7,5},{5,3},{3,1},{1,0},{8,10},{10,12},{12... | collective-permute-start | bytes 589832 | tf_op jit(solution)/shard_map/ppermute | solution.py:54
  225.5 6.1 %collective-permute-start.37 = (bf16[32,3072]{1,0:T(8,128)(2,1)S(1)}, bf16[32,3072]{1,0:T(8,128)(2,1)S(1)}, u32[]{:S(2)}, u32[]{:S(2)}) collective-permute-start(bf16[32,3072]{1,0:T(8,128)(2,1)S(1)} %collective-permute-done.35), channel_id=1, source_target_pairs={{0,1},{2,0},{4,2},{6,4},{7,6},{5,7},{3,5},{1,3},{8,9},{10,8},{12,1... | collective-permute-start | bytes 589832 | tf_op jit(solution)/shard_map/ppermute | solution.py:57
  229.8 5.7 %collective-permute-start.38 = (bf16[32,3072]{1,0:T(8,128)(2,1)S(1)}, bf16[32,3072]{1,0:T(8,128)(2,1)S(1)}, u32[]{:S(2)}, u32[]{:S(2)}) collective-permute-start(bf16[32,3072]{1,0:T(8,128)(2,1)S(1)} %collective-permute-done.36), channel_id=1, source_target_pairs={{0,2},{2,4},{4,6},{6,7},{7,5},{5,3},{3,1},{1,0},{8,10},{10,12},{12... | collective-permute-start | bytes 589832 | tf_op jit(solution)/shard_map/ppermute | solution.py:54
  231.6 5.7 %collective-permute-start.39 = (bf16[32,3072]{1,0:T(8,128)(2,1)S(1)}, bf16[32,3072]{1,0:T(8,128)(2,1)S(1)}, u32[]{:S(2)}, u32[]{:S(2)}) collective-permute-start(bf16[32,3072]{1,0:T(8,128)(2,1)S(1)} %collective-permute-done.37), channel_id=1, source_target_pairs={{0,1},{2,0},{4,2},{6,4},{7,6},{5,7},{3,5},{1,3},{8,9},{10,8},{12,1... | collective-permute-start | bytes 589832 | tf_op jit(solution)/shard_map/ppermute | solution.py:57
  231.9 10.5 %copy-start.7 = (f32[1,3072]{1,0:T(1,128)S(1)}, f32[1,3072]{1,0:T(1,128)}, u32[]{:S(2)}) copy-start(f32[1,3072]{1,0:T(1,128)} %get-tuple-element.129) | copy-start | bytes 36868
  231.9 10.5 %copy-start.9 = (bf16[3072,3,1,128]{3,0,2,1:T(8,128)(2,1)S(1)}, bf16[3072,3,1,128]{3,0,2,1:T(8,128)(2,1)}, u32[]{:S(2)}) copy-start(bf16[3072,3,1,128]{3,0,2,1:T(8,128)(2,1)} %param.38) | copy-start | bytes 7077892
  235.5 4.7 %collective-permute-start.40 = (bf16[16,3072]{1,0:T(8,128)(2,1)S(1)}, bf16[16,3072]{1,0:T(8,128)(2,1)S(1)}, u32[]{:S(2)}, u32[]{:S(2)}) collective-permute-start(bf16[16,3072]{1,0:T(8,128)(2,1)S(1)} %slice.244), channel_id=1, source_target_pairs={{0,2},{2,4},{4,6},{6,7},{7,5},{5,3},{3,1},{1,0},{8,10},{10,12},{12... | collective-permute-start | bytes 294920 | tf_op jit(solution)/shard_map/ppermute | solution.py:48
  237.3 4.7 %collective-permute-start.41 = (bf16[16,3072]{1,0:T(8,128)(2,1)S(1)}, bf16[16,3072]{1,0:T(8,128)(2,1)S(1)}, u32[]{:S(2)}, u32[]{:S(2)}) collective-permute-start(bf16[16,3072]{1,0:T(8,128)(2,1)S(1)} %slice.245), channel_id=1, source_target_pairs={{0,1},{2,0},{4,2},{6,4},{7,6},{5,7},{3,5},{1,3},{8,9},{10,8},{12,1... | collective-permute-start | bytes 294920 | tf_op jit(solution)/shard_map/ppermute | solution.py:49
  244.5 3.7 %collective-permute-start.42 = (bf16[256,128]{1,0:T(8,128)(2,1)S(1)}, bf16[256,128]{1,0:T(8,128)(2,1)S(1)}, u32[]{:S(2)}, u32[]{:S(2)}) collective-permute-start(bf16[256,128]{1,0:T(8,128)(2,1)S(1)} %convolution_convert_fusion.4), channel_id=1, source_target_pairs={{0,8},{1,9},{2,10},{3,11},{4,12},{5,13},{6,14},{7,15},{16,24},{17,... | collective-permute-start | bytes 196616 | tf_op jit(solution)/shard_map/ppermute | solution.py:14
  246.0 2.2 collective-permute-start.43
  250.2 4.7 %collective-permute-start.44 = (bf16[16,3072]{1,0:T(8,128)(2,1)S(1)}, bf16[16,3072]{1,0:T(8,128)(2,1)S(1)}, u32[]{:S(2)}, u32[]{:S(2)}) collective-permute-start(bf16[16,3072]{1,0:T(8,128)(2,1)S(1)} %get-tuple-element.107), channel_id=1, source_target_pairs={{0,2},{2,4},{4,6},{6,7},{7,5},{5,3},{3,1},{1,0},{8,10},{10,12},{12... | collective-permute-start | bytes 294920 | tf_op jit(solution)/shard_map/ppermute | solution.py:86
  252.1 4.8 %collective-permute-start.48 = (bf16[16,3072]{1,0:T(8,128)(2,1)S(1)}, bf16[16,3072]{1,0:T(8,128)(2,1)S(1)}, u32[]{:S(2)}, u32[]{:S(2)}) collective-permute-start(bf16[16,3072]{1,0:T(8,128)(2,1)S(1)} %get-tuple-element.108), channel_id=1, source_target_pairs={{0,1},{2,0},{4,2},{6,4},{7,6},{5,7},{3,5},{1,3},{8,9},{10,8},{12,1... | collective-permute-start | bytes 294920 | tf_op jit(solution)/shard_map/ppermute | solution.py:86
  254.9 7.5 %collective-permute-start.45 = (bf16[32,3072]{1,0:T(8,128)(2,1)S(1)}, bf16[32,3072]{1,0:T(8,128)(2,1)S(1)}, u32[]{:S(2)}, u32[]{:S(2)}) collective-permute-start(bf16[32,3072]{1,0:T(8,128)(2,1)S(1)} %fusion.54), channel_id=1, source_target_pairs={{0,2},{2,4},{4,6},{6,7},{7,5},{5,3},{3,1},{1,0},{8,10},{10,12},{12... | collective-permute-start | bytes 589832 | tf_op jit(solution)/shard_map/ppermute | solution.py:86
  256.9 7.8 %collective-permute-start.49 = (bf16[32,3072]{1,0:T(8,128)(2,1)S(1)}, bf16[32,3072]{1,0:T(8,128)(2,1)S(1)}, u32[]{:S(2)}, u32[]{:S(2)}) collective-permute-start(bf16[32,3072]{1,0:T(8,128)(2,1)S(1)} %fusion.52), channel_id=1, source_target_pairs={{0,1},{2,0},{4,2},{6,4},{7,6},{5,7},{3,5},{1,3},{8,9},{10,8},{12,1... | collective-permute-start | bytes 589832 | tf_op jit(solution)/shard_map/ppermute | solution.py:86
  262.5 7.3 %collective-permute-start.46 = (bf16[32,3072]{1,0:T(8,128)(2,1)S(1)}, bf16[32,3072]{1,0:T(8,128)(2,1)S(1)}, u32[]{:S(2)}, u32[]{:S(2)}) collective-permute-start(bf16[32,3072]{1,0:T(8,128)(2,1)S(1)} %fusion.30), channel_id=1, source_target_pairs={{0,2},{2,4},{4,6},{6,7},{7,5},{5,3},{3,1},{1,0},{8,10},{10,12},{12... | collective-permute-start | bytes 589832 | tf_op jit(solution)/shard_map/ppermute | solution.py:86
  269.9 6.5 %collective-permute-start.50 = (bf16[32,3072]{1,0:T(8,128)(2,1)S(1)}, bf16[32,3072]{1,0:T(8,128)(2,1)S(1)}, u32[]{:S(2)}, u32[]{:S(2)}) collective-permute-start(bf16[32,3072]{1,0:T(8,128)(2,1)S(1)} %get-tuple-element.106), channel_id=1, source_target_pairs={{0,1},{2,0},{4,2},{6,4},{7,6},{5,7},{3,5},{1,3},{8,9},{10,8},{12,1... | collective-permute-start | bytes 589832 | tf_op jit(solution)/shard_map/ppermute | solution.py:86
  270.2 6.6 %collective-permute-start.47 = (bf16[32,3072]{1,0:T(8,128)(2,1)S(1)}, bf16[32,3072]{1,0:T(8,128)(2,1)S(1)}, u32[]{:S(2)}, u32[]{:S(2)}) collective-permute-start(bf16[32,3072]{1,0:T(8,128)(2,1)S(1)} %get-tuple-element.105), channel_id=1, source_target_pairs={{0,2},{2,4},{4,6},{6,7},{7,5},{5,3},{3,1},{1,0},{8,10},{10,12},{12... | collective-permute-start | bytes 589832 | tf_op jit(solution)/shard_map/ppermute | solution.py:86
  276.5 5.7 %collective-permute-start.51 = (bf16[32,3072]{1,0:T(8,128)(2,1)S(1)}, bf16[32,3072]{1,0:T(8,128)(2,1)S(1)}, u32[]{:S(2)}, u32[]{:S(2)}) collective-permute-start(bf16[32,3072]{1,0:T(8,128)(2,1)S(1)} %fusion.29), channel_id=1, source_target_pairs={{0,1},{2,0},{4,2},{6,4},{7,6},{5,7},{3,5},{1,3},{8,9},{10,8},{12,1... | collective-permute-start | bytes 589832 | tf_op jit(solution)/shard_map/ppermute | solution.py:86

commit v5 on v4

--- a/solution.py
+++ b/solution.py
@@ -26,52 +26,60 @@
     place = [0] * length
     for p, h in enumerate(order):
         place[h] = p
-    me = jnp.array(place, jnp.int32)[lax.axis_index(axis)]
-    return length, order, jnp.array(order, jnp.int32), me
-
-
-def ring_gather(value, axis):
-    length, order, order_arr, me = ring_tables(axis)
+    head_at = [[order[(place[h] + m) % length] for m in range(length)] for h in range(length)]
+    offset_of = [[(place[j] - place[h]) % length for j in range(length)] for h in range(length)]
+    table = jnp.array([head_at, offset_of], jnp.int32)
+    mine = lax.dynamic_index_in_dim(table, lax.axis_index(axis), 1, keepdims=False)
+    return mine[0], mine[1]
+
+
+def ring_pairs(length):
+    order = ring_order(length)
     forward = [(order[p], order[(p + 1) % length]) for p in range(length)]
     backward = [(order[p], order[(p - 1) % length]) for p in range(length)]
+    return forward, backward
+
+
+def ring_gather(value, axis, tables):
+    length = lax.axis_size(axis)
+    forward, backward = ring_pairs(length)
     ahead = length // 2
     behind = length - 1 - ahead
     rows = value.shape[0]
     split = behind < ahead and rows % 2 == 0
     half = rows // 2
-    out = jnp.zeros((length * rows,) + value.shape[1:], value.dtype)
-    out = lax.dynamic_update_slice_in_dim(out, value, order_arr[me] * rows, 0)
+    pieces = [None] * length
+    pieces[0] = value
     fwd = value
     bwd = value
     for k in range(1, ahead + 1):
         if k == ahead and split:
             fwd = lax.ppermute(fwd[:half], axis, forward)
             bwd = lax.ppermute(bwd[half:], axis, backward)
-            far = order_arr[(me - k) % length] * rows
-            out = lax.dynamic_update_slice_in_dim(out, fwd, far, 0)
-            out = lax.dynamic_update_slice_in_dim(out, bwd, far + half, 0)
+            pieces[k] = jnp.concatenate([fwd, bwd], axis=0)
             break
         fwd = lax.ppermute(fwd, axis, forward)
-        out = lax.dynamic_update_slice_in_dim(out, fwd, order_arr[(me - k) % length] * rows, 0)
+        pieces[length - k] = fwd
         if k <= behind:
             bwd = lax.ppermute(bwd, axis, backward)
-            out = lax.dynamic_update_slice_in_dim(out, bwd, order_arr[(me + k) % length] * rows, 0)
-    return out
-
-
-def ring_scatter_sum(value, axis):
-    length, order, order_arr, me = ring_tables(axis)
-    forward = [(order[p], order[(p + 1) % length]) for p in range(length)]
-    backward = [(order[p], order[(p - 1) % length]) for p in range(length)]
+            pieces[k] = bwd
+    stacked = jnp.stack(pieces)
+    return jnp.take(stacked, tables[1], axis=0, mode="clip").reshape((length * rows,) + value.shape[1:])
+
+
+def ring_scatter_sum(value, axis, tables):
+    length = lax.axis_size(axis)
+    forward, backward = ring_pairs(length)
     ahead = length // 2
     behind = length - 1 - ahead
     rows = value.shape[0] // length
     split = behind < ahead and rows % 2 == 0
     half = rows // 2
     blocks = value.reshape((length, rows) + value.shape[1:])
+    by_offset = jnp.take(blocks, tables[0], axis=0, mode="clip")
 
     def own(offset):
-        return lax.dynamic_index_in_dim(blocks, order_arr[(me + offset) % length], 0, keepdims=False).astype(jnp.float32)
+        return by_offset[offset % length].astype(jnp.float32)
 
     def chain(offsets, pairs, first_rows):
         passed = None
@@ -164,23 +172,23 @@
     )(slabs, conv_by_half)
 
 
-def conv_share(gated, weight, tok_rows):
+def conv_share(gated, weight, tok_rows, tables):
 
     def term(start, count):
         return rounded_term(gated, weight)
 
     return ring_scatter_sum(
-        term(jnp.int32(0), tok_rows * lax.axis_size("head")).astype(jnp.bfloat16), "head"
-    )
-
-
-def attention_portion_for(heads_out, out_block, tok_rows):
+        term(jnp.int32(0), tok_rows * lax.axis_size("head")).astype(jnp.bfloat16), "head", tables
+    )
+
+
+def attention_portion_for(heads_out, out_block, tok_rows, tables):
 
     def term(start, count):
         return rounded_term(heads_out, out_block)
 
     return ring_scatter_sum(
-        term(jnp.int32(0), tok_rows * lax.axis_size("head")).astype(jnp.bfloat16), "head"
+        term(jnp.int32(0), tok_rows * lax.axis_size("head")).astype(jnp.bfloat16), "head", tables
     )
 
 
@@ -222,15 +230,16 @@
     head_size = w_qkv.shape[3]
     layers = w_conv.shape[0]
     share = stream
-    state = ring_gather(stream, "head")
+    tables = ring_tables("head")
+    state = ring_gather(stream, "head", tables)
     conv_by_half = jnp.transpose(w_conv, (0, 1, 3, 2, 4))
     for layer_idx in range(layers):
         gated = convolution_gate(
             normed(state, gains[layer_idx]), conv_by_half, layer_idx, dilations[layer_idx]
         )
-        summed = conv_share(gated, w_mix[layer_idx], tok_rows)
+        summed = conv_share(gated, w_mix[layer_idx], tok_rows, tables)
         share = (share.astype(jnp.float32) + summed).astype(jnp.bfloat16)
-        state = ring_gather(share, "head")
+        state = ring_gather(share, "head", tables)
     all_rows = state.shape[0]
     attn_in = normed(state, gains[layers])
     qkv_parts = jnp.transpose(w_qkv[:, :, 0, :], (1, 0, 2))
@@ -247,7 +256,7 @@
     )
     peak, denom, weighted = combine(own_part, crossing_portion)
     heads_out = (weighted / denom[:, None]).astype(jnp.bfloat16)
-    attn_share = attention_portion_for(heads_out, w_out[0], tok_rows)
+    attn_share = attention_portion_for(heads_out, w_out[0], tok_rows, tables)
     return (share.astype(jnp.float32) + attn_share).astype(jnp.bfloat16)
 
 

time: 284 us -> 279 us (0.982)
  between operations: 35.6 us -> 4.26 us
  local copies, waits for them, and re-layouts: 30.7 us -> 51.1 us
  other arithmetic: 17.7 us -> 23 us
  matrix products: 8.54 us -> 11.7 us
    ppermute x9, waiting for transfers between devices: 32.6 us -> 6.59 us  [ring_gather(): fwd = lax.ppermute(fwd, axis, forward)]
    ppermute x9, waiting for transfers between devices: 2.44 us -> 18.8 us  [ring_gather(): bwd = lax.ppermute(bwd, axis, backward)]
    gather x0 -> x6, local copies, waits for them, and re-layouts: none -> 12.3 us  [the longest x3 6.16 us: ring_gather(): jnp.take(stacked, tables[1], axis=0, mode='clip')]
    ppermute x24, waiting for transfers between devices: 58.1 us -> 67.2 us  [chain(): passed = lax.ppermute(part.astype(value.dtype), axis, pairs)]
    unnamed x21 -> x27, local copies, waits for them, and re-layouts: 23.9 us -> 32.8 us
    convert_element_type x3 -> x5, other arithmetic: 0.27 us -> 4.33 us  [the longest x2 4.06 us: normed(): wide = values.astype(jnp.float32)]
    unnamed x0 -> x5, other arithmetic: none -> 3.64 us
    dot_general x3, matrix products: 6.26 us -> 9.85 us  [rounded_term(): term = jnp.dot(left, right, preferred_element_type=jnp.float32)]
  transfers between devices with their start and end apart: 52 -> 52, of which waited for: 37 -> 34; matrix products, arithmetic and copies ran while one was open for 10% -> 12% of each run, Pallas kernels for 0% -> 0%
where the time goes in v5:
time: 279 us; the launch traced here: 278 us
  waiting for transfers between devices  105 us (38%)
  starting transfers between devices  57.5 us (21%)
  local copies, waits for them, and re-layouts  51.1 us (18%)
  Pallas kernels  25 us (9%)
  other arithmetic  23 us (8%)
  matrix products  11.7 us (4%)
  between operations  4.26 us (2%)
    ppermute x24, waiting for transfers between devices, chain(): passed = lax.ppermute(part.astype(value.dtype), axis, pairs)  67.2 us
    unnamed x27, local copies, waits for them, and re-layouts  32.8 us
    ppermute x24, starting transfers between devices, chain(): passed = lax.ppermute(part.astype(value.dtype), axis, pairs)  26.1 us
    pallas_call x2, Pallas kernels, convolution_gate(): pl.pallas_call(conv_gate_kernel, out_shape=jax.ShapeDtypeStruct((all_rows...  25 us
    ppermute x9, waiting for transfers between devices, ring_gather(): bwd = lax.ppermute(bwd, axis, backward)  18.8 us
    ppermute x9, starting transfers between devices, ring_gather(): fwd = lax.ppermute(fwd, axis, forward)  13.4 us
    dot_general x3, matrix products, rounded_term(): term = jnp.dot(left, right, preferred_element_type=jnp.float32)  9.85 us
    another operation x4, other arithmetic, convolution_gate(): jnp.stack([lax.dynamic_slice_in_dim(padded, border_rows - tap_idx * dilat...  9.18 us
  transfers between devices with their start and end apart: 52, of which 34 were waited for; matrix products, arithmetic and copies ran while one was open for 12% of the time, Pallas kernels for 0%

profile of v5, /device:TPU:0, one launch (start us, length us, event | category | flops | bytes accessed | tf_op | source)
XLA Modules:
  0.0 277.9 jit_solution(12698915556114629799)
XLA Ops:
  0.0 3.0 %collective-permute-start.3 = (bf16[32,3072]{1,0:T(8,128)(2,1)}, bf16[32,3072]{1,0:T(8,128)(2,1)S(1)}, u32[]{:S(2)}, u32[]{:S(2)}) collective-permute-start(bf16[32,3072]{1,0:T(8,128)(2,1)} %param.22), channel_id=1, source_target_pairs={{0,2},{2,4},{4,6},{6,7},{7,5},{5,3},{3,1},{1,0},{8,10},{10,12},{12... | collective-permute-start | bytes 589832 | tf_op jit(solution)/shard_map/ppermute | solution.py:61
  6.3 1.6 bitcast_dynamic-update-slice_fusion.20
  8.9 19.6 %copy.11 = bf16[2,3,3072,2,384]{4,2,3,1,0:T(8,128)(2,1)} copy(bf16[2,3,3072,2,384]{4,3,2,1,0:T(2,128)(2,1)} %param.25) | data formatting | bytes 56623104 | tf_op args[3]
  29.2 2.1 collective-permute-start.4
  32.0 3.6 %collective-permute-done.4 = bf16[32,3072]{1,0:T(8,128)(2,1)S(1)} collective-permute-done((bf16[32,3072]{1,0:T(8,128)(2,1)S(1)}, bf16[32,3072]{1,0:T(8,128)(2,1)S(1)}, u32[]{:S(2)}, u32[]{:S(2)}) %collective-permute-start.4) | collective-permute-done | bytes 196640 | tf_op jit(solution)/shard_map/ppermute | solution.py:61
  35.6 1.7 collective-permute-start.5
  38.4 2.9 %collective-permute-done.5 = bf16[32,3072]{1,0:T(8,128)(2,1)S(1)} collective-permute-done((bf16[32,3072]{1,0:T(8,128)(2,1)S(1)}, bf16[32,3072]{1,0:T(8,128)(2,1)S(1)}, u32[]{:S(2)}, u32[]{:S(2)}) %collective-permute-start.5) | collective-permute-done | bytes 196640 | tf_op jit(solution)/shard_map/ppermute | solution.py:61
  41.3 1.9 collective-permute-start.6
  44.2 1.8 collective-permute-done.6
  46.0 1.9 collective-permute-done.7
  50.6 2.1 gather_fusion
  53.1 2.0 convert_element_type.566
  59.1 2.2 fusion.27
  61.3 2.4 pad_maximum_fusion.slab_ref
  63.7 12.5 %shard_map.82 = bf16[256,384]{1,0:T(8,128)(2,1)} custom-call(bf16[3,256,3072]{2,1,0:T(8,128)(2,1)} %pad_maximum_fusion.slab_ref, bf16[2,3,2,3072,384]{4,3,2,1,0:T(8,128)(2,1)} %bitcast.279), custom_call_target="tpu_custom_call" | custom-call | flops 3623878656 | bytes 19070976 | tf_op jit(solution)/shard_map/pallas_call | solution.py:156
  76.2 4.0 %convolution_convert_fusion.2 = bf16[256,3072]{1,0:T(8,128)(2,1)} fusion(bf16[256,384]{1,0:T(8,128)(2,1)} %shard_map.82, bf16[2,384,3072]{2,1,0:T(8,128)(2,1)} %param.26), kind=kOutput, calls=%fused_computation.19 | convolution fusion | flops 604766208 | bytes 4128768 | tf_op jit(solution)/shard_map/dot_general | solution.py:119
  80.2 2.1 gather_fusion.1
  82.2 1.6 collective-permute-start.9
  84.5 2.9 %collective-permute-done.9 = bf16[16,3072]{1,0:T(8,128)(2,1)S(1)} collective-permute-done((bf16[16,3072]{1,0:T(8,128)(2,1)S(1)}, bf16[16,3072]{1,0:T(8,128)(2,1)S(1)}, u32[]{:S(2)}, u32[]{:S(2)}) %collective-permute-start.9) | collective-permute-done | bytes 98336 | tf_op jit(solution)/shard_map/ppermute | solution.py:94
  87.4 1.6 collective-permute-start.10
  89.5 4.3 %collective-permute-done.10 = bf16[32,3072]{1,0:T(8,128)(2,1)S(1)} collective-permute-done((bf16[32,3072]{1,0:T(8,128)(2,1)S(1)}, bf16[32,3072]{1,0:T(8,128)(2,1)S(1)}, u32[]{:S(2)}, u32[]{:S(2)}) %collective-permute-start.10) | collective-permute-done | bytes 196640 | tf_op jit(solution)/shard_map/ppermute | solution.py:94
  93.9 1.6 collective-permute-start.11
  95.5 4.1 %collective-permute-done.11 = bf16[32,3072]{1,0:T(8,128)(2,1)S(1)} collective-permute-done((bf16[32,3072]{1,0:T(8,128)(2,1)S(1)}, bf16[32,3072]{1,0:T(8,128)(2,1)S(1)}, u32[]{:S(2)}, u32[]{:S(2)}) %collective-permute-start.11) | collective-permute-done | bytes 196640 | tf_op jit(solution)/shard_map/ppermute | solution.py:94
  101.8 4.6 %collective-permute-done.15 = bf16[32,3072]{1,0:T(8,128)(2,1)S(1)} collective-permute-done((bf16[32,3072]{1,0:T(8,128)(2,1)S(1)}, bf16[32,3072]{1,0:T(8,128)(2,1)S(1)}, u32[]{:S(2)}, u32[]{:S(2)}) %collective-permute-start.15) | collective-permute-done | bytes 196640 | tf_op jit(solution)/shard_map/ppermute | solution.py:94
  106.8 6.8 %collective-permute-done.16 = bf16[32,3072]{1,0:T(8,128)(2,1)S(1)} collective-permute-done((bf16[32,3072]{1,0:T(8,128)(2,1)S(1)}, bf16[32,3072]{1,0:T(8,128)(2,1)S(1)}, u32[]{:S(2)}, u32[]{:S(2)}) %collective-permute-start.16) | collective-permute-done | bytes 196640 | tf_op jit(solution)/shard_map/ppermute | solution.py:94
  114.4 2.0 collective-permute-start.20
  118.3 2.6 collective-permute-done.17
  121.2 1.7 collective-permute-start.21
  123.6 2.9 %collective-permute-done.18 = bf16[32,3072]{1,0:T(8,128)(2,1)S(1)} collective-permute-done((bf16[32,3072]{1,0:T(8,128)(2,1)S(1)}, bf16[32,3072]{1,0:T(8,128)(2,1)S(1)}, u32[]{:S(2)}, u32[]{:S(2)}) %collective-permute-start.18) | collective-permute-done | bytes 196640 | tf_op jit(solution)/shard_map/ppermute | solution.py:64
  129.2 2.9 %collective-permute-done.19 = bf16[32,3072]{1,0:T(8,128)(2,1)S(1)} collective-permute-done((bf16[32,3072]{1,0:T(8,128)(2,1)S(1)}, bf16[32,3072]{1,0:T(8,128)(2,1)S(1)}, u32[]{:S(2)}, u32[]{:S(2)}) %collective-permute-start.19) | collective-permute-done | bytes 196640 | tf_op jit(solution)/shard_map/ppermute | solution.py:64
  135.1 1.8 collective-permute-done.24
  140.3 2.1 gather_fusion.2
  142.8 2.0 convert_element_type.573
  145.4 1.7 collective-permute-start.25
  148.8 2.2 fusion.23
  151.0 2.4 pad_maximum_fusion.1.slab_ref
  153.4 12.5 %shard_map.83 = bf16[256,384]{1,0:T(8,128)(2,1)} custom-call(bf16[3,256,3072]{2,1,0:T(8,128)(2,1)} %pad_maximum_fusion.1.slab_ref, bf16[2,3,2,3072,384]{4,3,2,1,0:T(8,128)(2,1)} %bitcast.280), custom_call_target="tpu_custom_call" | custom-call | flops 3623878656 | bytes 19070976 | tf_op jit(solution)/shard_map/pallas_call | solution.py:156
  165.8 3.9 %convolution_convert_fusion.1 = bf16[256,3072]{1,0:T(8,128)(2,1)} fusion(bf16[256,384]{1,0:T(8,128)(2,1)} %shard_map.83, bf16[2,384,3072]{2,1,0:T(8,128)(2,1)} %param.26), kind=kOutput, calls=%fused_computation.18 | convolution fusion | flops 604766208 | bytes 4128768 | tf_op jit(solution)/shard_map/dot_general | solution.py:119
  169.8 2.1 gather_fusion.3
  174.1 2.9 %collective-permute-done.26 = bf16[16,3072]{1,0:T(8,128)(2,1)S(1)} collective-permute-done((bf16[16,3072]{1,0:T(8,128)(2,1)S(1)}, bf16[16,3072]{1,0:T(8,128)(2,1)S(1)}, u32[]{:S(2)}, u32[]{:S(2)}) %collective-permute-start.26) | collective-permute-done | bytes 98336 | tf_op jit(solution)/shard_map/ppermute | solution.py:94
  179.2 4.3 %collective-permute-done.27 = bf16[32,3072]{1,0:T(8,128)(2,1)S(1)} collective-permute-done((bf16[32,3072]{1,0:T(8,128)(2,1)S(1)}, bf16[32,3072]{1,0:T(8,128)(2,1)S(1)}, u32[]{:S(2)}, u32[]{:S(2)}) %collective-permute-start.27) | collective-permute-done | bytes 196640 | tf_op jit(solution)/shard_map/ppermute | solution.py:94
  185.0 4.3 %collective-permute-done.28 = bf16[32,3072]{1,0:T(8,128)(2,1)S(1)} collective-permute-done((bf16[32,3072]{1,0:T(8,128)(2,1)S(1)}, bf16[32,3072]{1,0:T(8,128)(2,1)S(1)}, u32[]{:S(2)}, u32[]{:S(2)}) %collective-permute-start.28) | collective-permute-done | bytes 196640 | tf_op jit(solution)/shard_map/ppermute | solution.py:94
  189.3 1.6 collective-permute-start.32
  191.4 4.6 %collective-permute-done.32 = bf16[32,3072]{1,0:T(8,128)(2,1)S(1)} collective-permute-done((bf16[32,3072]{1,0:T(8,128)(2,1)S(1)}, bf16[32,3072]{1,0:T(8,128)(2,1)S(1)}, u32[]{:S(2)}, u32[]{:S(2)}) %collective-permute-start.32) | collective-permute-done | bytes 196640 | tf_op jit(solution)/shard_map/ppermute | solution.py:94
  196.0 1.6 collective-permute-start.33
  197.6 5.6 %collective-permute-done.33 = bf16[32,3072]{1,0:T(8,128)(2,1)S(1)} collective-permute-done((bf16[32,3072]{1,0:T(8,128)(2,1)S(1)}, bf16[32,3072]{1,0:T(8,128)(2,1)S(1)}, u32[]{:S(2)}, u32[]{:S(2)}) %collective-permute-start.33) | collective-permute-done | bytes 196640 | tf_op jit(solution)/shard_map/ppermute | solution.py:94
  206.0 4.5 %collective-permute-done.34 = bf16[32,3072]{1,0:T(8,128)(2,1)S(1)} collective-permute-done((bf16[32,3072]{1,0:T(8,128)(2,1)S(1)}, bf16[32,3072]{1,0:T(8,128)(2,1)S(1)}, u32[]{:S(2)}, u32[]{:S(2)}) %collective-permute-start.34) | collective-permute-done | bytes 196640 | tf_op jit(solution)/shard_map/ppermute | solution.py:64
  213.2 2.9 %collective-permute-done.35 = bf16[32,3072]{1,0:T(8,128)(2,1)S(1)} collective-permute-done((bf16[32,3072]{1,0:T(8,128)(2,1)S(1)}, bf16[32,3072]{1,0:T(8,128)(2,1)S(1)}, u32[]{:S(2)}, u32[]{:S(2)}) %collective-permute-start.35) | collective-permute-done | bytes 196640 | tf_op jit(solution)/shard_map/ppermute | solution.py:64
  218.9 2.9 %collective-permute-done.36 = bf16[32,3072]{1,0:T(8,128)(2,1)S(1)} collective-permute-done((bf16[32,3072]{1,0:T(8,128)(2,1)S(1)}, bf16[32,3072]{1,0:T(8,128)(2,1)S(1)}, u32[]{:S(2)}, u32[]{:S(2)}) %collective-permute-start.36) | collective-permute-done | bytes 196640 | tf_op jit(solution)/shard_map/ppermute | solution.py:64
  221.8 1.6 collective-permute-start.41
  224.7 1.8 collective-permute-done.41
  226.5 1.6 collective-permute-done.40
  230.9 2.1 gather_fusion.4
  241.4 1.9 convolution_convert_fusion
  243.4 2.1 gather_fusion.5
  246.1 1.6 collective-permute-start.48
  247.7 2.4 collective-permute-done.44
  250.9 1.6 collective-permute-start.49
  252.4 5.4 %collective-permute-done.45 = bf16[32,3072]{1,0:T(8,128)(2,1)S(1)} collective-permute-done((bf16[32,3072]{1,0:T(8,128)(2,1)S(1)}, bf16[32,3072]{1,0:T(8,128)(2,1)S(1)}, u32[]{:S(2)}, u32[]{:S(2)}) %collective-permute-start.45) | collective-permute-done | bytes 196640 | tf_op jit(solution)/shard_map/ppermute | solution.py:94
  258.7 6.3 %collective-permute-done.46 = bf16[32,3072]{1,0:T(8,128)(2,1)S(1)} collective-permute-done((bf16[32,3072]{1,0:T(8,128)(2,1)S(1)}, bf16[32,3072]{1,0:T(8,128)(2,1)S(1)}, u32[]{:S(2)}, u32[]{:S(2)}) %collective-permute-start.46) | collective-permute-done | bytes 196640 | tf_op jit(solution)/shard_map/ppermute | solution.py:94
  265.1 1.6 collective-permute-start.50
  267.2 4.2 %collective-permute-done.50 = bf16[32,3072]{1,0:T(8,128)(2,1)S(1)} collective-permute-done((bf16[32,3072]{1,0:T(8,128)(2,1)S(1)}, bf16[32,3072]{1,0:T(8,128)(2,1)S(1)}, u32[]{:S(2)}, u32[]{:S(2)}) %collective-permute-start.50) | collective-permute-done | bytes 196640 | tf_op jit(solution)/shard_map/ppermute | solution.py:94
  271.4 1.6 collective-permute-start.51
  273.0 4.1 %collective-permute-done.51 = bf16[32,3072]{1,0:T(8,128)(2,1)S(1)} collective-permute-done((bf16[32,3072]{1,0:T(8,128)(2,1)S(1)}, bf16[32,3072]{1,0:T(8,128)(2,1)S(1)}, u32[]{:S(2)}, u32[]{:S(2)}) %collective-permute-start.51) | collective-permute-done | bytes 196640 | tf_op jit(solution)/shard_map/ppermute | solution.py:94
  (150 shorter events, 61.7 us)
Async XLA Ops:
  0.0 241.4 %copy-start = (bf16[1,128,3072]{2,1,0:T(8,128)(2,1)S(1)}, bf16[1,128,3072]{2,1,0:T(8,128)(2,1)}, u32[]{:S(2)}) copy-start(bf16[1,128,3072]{2,1,0:T(8,128)(2,1)} %param.28) | copy-start | bytes 2359300
  0.0 29.2 %collective-permute-start.3 = (bf16[32,3072]{1,0:T(8,128)(2,1)}, bf16[32,3072]{1,0:T(8,128)(2,1)S(1)}, u32[]{:S(2)}, u32[]{:S(2)}) collective-permute-start(bf16[32,3072]{1,0:T(8,128)(2,1)} %param.22), channel_id=1, source_target_pairs={{0,2},{2,4},{4,6},{6,7},{7,5},{5,3},{3,1},{1,0},{8,10},{10,12},{12... | collective-permute-start | bytes 589832 | tf_op jit(solution)/shard_map/ppermute | solution.py:61
  3.0 28.3 %collective-permute-start = (bf16[32,3072]{1,0:T(8,128)(2,1)}, bf16[32,3072]{1,0:T(8,128)(2,1)S(1)}, u32[]{:S(2)}, u32[]{:S(2)}) collective-permute-start(bf16[32,3072]{1,0:T(8,128)(2,1)} %param.22), channel_id=1, source_target_pairs={{0,1},{2,0},{4,2},{6,4},{7,6},{5,7},{3,5},{1,3},{8,9},{10,8},{12,1... | collective-permute-start | bytes 589832 | tf_op jit(solution)/shard_map/ppermute | solution.py:64
  29.2 6.4 %collective-permute-start.4 = (bf16[32,3072]{1,0:T(8,128)(2,1)S(1)}, bf16[32,3072]{1,0:T(8,128)(2,1)S(1)}, u32[]{:S(2)}, u32[]{:S(2)}) collective-permute-start(bf16[32,3072]{1,0:T(8,128)(2,1)S(1)} %collective-permute-done.3), channel_id=1, source_target_pairs={{0,2},{2,4},{4,6},{6,7},{7,5},{5,3},{3,1},{1,0},{8,10},{10,12},{12... | collective-permute-start | bytes 589832 | tf_op jit(solution)/shard_map/ppermute | solution.py:61
  31.3 6.1 %collective-permute-start.1 = (bf16[32,3072]{1,0:T(8,128)(2,1)S(1)}, bf16[32,3072]{1,0:T(8,128)(2,1)S(1)}, u32[]{:S(2)}, u32[]{:S(2)}) collective-permute-start(bf16[32,3072]{1,0:T(8,128)(2,1)S(1)} %collective-permute-done), channel_id=1, source_target_pairs={{0,1},{2,0},{4,2},{6,4},{7,6},{5,7},{3,5},{1,3},{8,9},{10,8},{12,1... | collective-permute-start | bytes 589832 | tf_op jit(solution)/shard_map/ppermute | solution.py:64
  35.6 5.7 %collective-permute-start.5 = (bf16[32,3072]{1,0:T(8,128)(2,1)S(1)}, bf16[32,3072]{1,0:T(8,128)(2,1)S(1)}, u32[]{:S(2)}, u32[]{:S(2)}) collective-permute-start(bf16[32,3072]{1,0:T(8,128)(2,1)S(1)} %collective-permute-done.4), channel_id=1, source_target_pairs={{0,2},{2,4},{4,6},{6,7},{7,5},{5,3},{3,1},{1,0},{8,10},{10,12},{12... | collective-permute-start | bytes 589832 | tf_op jit(solution)/shard_map/ppermute | solution.py:61
  37.4 5.8 %collective-permute-start.2 = (bf16[32,3072]{1,0:T(8,128)(2,1)S(1)}, bf16[32,3072]{1,0:T(8,128)(2,1)S(1)}, u32[]{:S(2)}, u32[]{:S(2)}) collective-permute-start(bf16[32,3072]{1,0:T(8,128)(2,1)S(1)} %collective-permute-done.1), channel_id=1, source_target_pairs={{0,1},{2,0},{4,2},{6,4},{7,6},{5,7},{3,5},{1,3},{8,9},{10,8},{12,1... | collective-permute-start | bytes 589832 | tf_op jit(solution)/shard_map/ppermute | solution.py:64
  41.3 4.7 %collective-permute-start.6 = (bf16[16,3072]{1,0:T(8,128)(2,1)S(1)}, bf16[16,3072]{1,0:T(8,128)(2,1)S(1)}, u32[]{:S(2)}, u32[]{:S(2)}) collective-permute-start(bf16[16,3072]{1,0:T(8,128)(2,1)S(1)} %slice.352), channel_id=1, source_target_pairs={{0,2},{2,4},{4,6},{6,7},{7,5},{5,3},{3,1},{1,0},{8,10},{10,12},{12... | collective-permute-start | bytes 294920 | tf_op jit(solution)/shard_map/ppermute | solution.py:57
  43.2 4.7 %collective-permute-start.7 = (bf16[16,3072]{1,0:T(8,128)(2,1)S(1)}, bf16[16,3072]{1,0:T(8,128)(2,1)S(1)}, u32[]{:S(2)}, u32[]{:S(2)}) collective-permute-start(bf16[16,3072]{1,0:T(8,128)(2,1)S(1)} %slice.353), channel_id=1, source_target_pairs={{0,1},{2,0},{4,2},{6,4},{7,6},{5,7},{3,5},{1,3},{8,9},{10,8},{12,1... | collective-permute-start | bytes 294920 | tf_op jit(solution)/shard_map/ppermute | solution.py:58
  55.2 2.0 copy-start.1
  55.8 3.3 %collective-permute-start.8 = (bf16[128,3072]{1,0:T(8,128)(2,1)S(1)}, bf16[128,3072]{1,0:T(8,128)(2,1)S(1)}, u32[]{:S(2)}, u32[]{:S(2)}) collective-permute-start(bf16[128,3072]{1,0:T(8,128)(2,1)S(1)} %slice.354), channel_id=1, source_target_pairs={{0,8},{1,9},{2,10},{3,11},{4,12},{5,13},{6,14},{7,15},{16,24},{17,... | collective-permute-start | bytes 2359304 | tf_op jit(solution)/shard_map/ppermute | solution.py:14
  82.2 5.1 %collective-permute-start.9 = (bf16[16,3072]{1,0:T(8,128)(2,1)S(1)}, bf16[16,3072]{1,0:T(8,128)(2,1)S(1)}, u32[]{:S(2)}, u32[]{:S(2)}) collective-permute-start(bf16[16,3072]{1,0:T(8,128)(2,1)S(1)} %get-tuple-element.123), channel_id=1, source_target_pairs={{0,2},{2,4},{4,6},{6,7},{7,5},{5,3},{3,1},{1,0},{8,10},{10,12},{12... | collective-permute-start | bytes 294920 | tf_op jit(solution)/shard_map/ppermute | solution.py:94
  84.0 5.0 %collective-permute-start.13 = (bf16[16,3072]{1,0:T(8,128)(2,1)S(1)}, bf16[16,3072]{1,0:T(8,128)(2,1)S(1)}, u32[]{:S(2)}, u32[]{:S(2)}) collective-permute-start(bf16[16,3072]{1,0:T(8,128)(2,1)S(1)} %get-tuple-element.124), channel_id=1, source_target_pairs={{0,1},{2,0},{4,2},{6,4},{7,6},{5,7},{3,5},{1,3},{8,9},{10,8},{12,1... | collective-permute-start | bytes 294920 | tf_op jit(solution)/shard_map/ppermute | solution.py:94
  87.4 26.2 %copy-start.3 = (bf16[32,3072]{1,0:T(8,128)(2,1)S(1)}, bf16[32,3072]{1,0:T(8,128)(2,1)}, u32[]{:S(2)}) copy-start(bf16[32,3072]{1,0:T(8,128)(2,1)} %param.22) | copy-start | bytes 589828
  87.4 6.4 %collective-permute-start.10 = (bf16[32,3072]{1,0:T(8,128)(2,1)S(1)}, bf16[32,3072]{1,0:T(8,128)(2,1)S(1)}, u32[]{:S(2)}, u32[]{:S(2)}) collective-permute-start(bf16[32,3072]{1,0:T(8,128)(2,1)S(1)} %fusion.64), channel_id=1, source_target_pairs={{0,2},{2,4},{4,6},{6,7},{7,5},{5,3},{3,1},{1,0},{8,10},{10,12},{12... | collective-permute-start | bytes 589832 | tf_op jit(solution)/shard_map/ppermute | solution.py:94
  89.0 6.4 %collective-permute-start.14 = (bf16[32,3072]{1,0:T(8,128)(2,1)S(1)}, bf16[32,3072]{1,0:T(8,128)(2,1)S(1)}, u32[]{:S(2)}, u32[]{:S(2)}) collective-permute-start(bf16[32,3072]{1,0:T(8,128)(2,1)S(1)} %fusion.62), channel_id=1, source_target_pairs={{0,1},{2,0},{4,2},{6,4},{7,6},{5,7},{3,5},{1,3},{8,9},{10,8},{12,1... | collective-permute-start | bytes 589832 | tf_op jit(solution)/shard_map/ppermute | solution.py:94
  93.9 5.7 %collective-permute-start.11 = (bf16[32,3072]{1,0:T(8,128)(2,1)S(1)}, bf16[32,3072]{1,0:T(8,128)(2,1)S(1)}, u32[]{:S(2)}, u32[]{:S(2)}) collective-permute-start(bf16[32,3072]{1,0:T(8,128)(2,1)S(1)} %fusion.46), channel_id=1, source_target_pairs={{0,2},{2,4},{4,6},{6,7},{7,5},{5,3},{3,1},{1,0},{8,10},{10,12},{12... | collective-permute-start | bytes 589832 | tf_op jit(solution)/shard_map/ppermute | solution.py:94
  99.7 6.6 %collective-permute-start.15 = (bf16[32,3072]{1,0:T(8,128)(2,1)S(1)}, bf16[32,3072]{1,0:T(8,128)(2,1)S(1)}, u32[]{:S(2)}, u32[]{:S(2)}) collective-permute-start(bf16[32,3072]{1,0:T(8,128)(2,1)S(1)} %get-tuple-element.122), channel_id=1, source_target_pairs={{0,1},{2,0},{4,2},{6,4},{7,6},{5,7},{3,5},{1,3},{8,9},{10,8},{12,1... | collective-permute-start | bytes 589832 | tf_op jit(solution)/shard_map/ppermute | solution.py:94
  100.3 6.5 %collective-permute-start.12 = (bf16[32,3072]{1,0:T(8,128)(2,1)S(1)}, bf16[32,3072]{1,0:T(8,128)(2,1)S(1)}, u32[]{:S(2)}, u32[]{:S(2)}) collective-permute-start(bf16[32,3072]{1,0:T(8,128)(2,1)S(1)} %get-tuple-element.121), channel_id=1, source_target_pairs={{0,2},{2,4},{4,6},{6,7},{7,5},{5,3},{3,1},{1,0},{8,10},{10,12},{12... | collective-permute-start | bytes 589832 | tf_op jit(solution)/shard_map/ppermute | solution.py:94
  106.4 7.2 %collective-permute-start.16 = (bf16[32,3072]{1,0:T(8,128)(2,1)S(1)}, bf16[32,3072]{1,0:T(8,128)(2,1)S(1)}, u32[]{:S(2)}, u32[]{:S(2)}) collective-permute-start(bf16[32,3072]{1,0:T(8,128)(2,1)S(1)} %fusion.45), channel_id=1, source_target_pairs={{0,1},{2,0},{4,2},{6,4},{7,6},{5,7},{3,5},{1,3},{8,9},{10,8},{12,1... | collective-permute-start | bytes 589832 | tf_op jit(solution)/shard_map/ppermute | solution.py:94
  114.3 6.5 %collective-permute-start.17 = (bf16[32,3072]{1,0:T(8,128)(2,1)S(1)}, bf16[32,3072]{1,0:T(8,128)(2,1)S(1)}, u32[]{:S(2)}, u32[]{:S(2)}) collective-permute-start(bf16[32,3072]{1,0:T(8,128)(2,1)S(1)} %get-tuple-element.98), channel_id=1, source_target_pairs={{0,1},{2,0},{4,2},{6,4},{7,6},{5,7},{3,5},{1,3},{8,9},{10,8},{12,1... | collective-permute-start | bytes 589832 | tf_op jit(solution)/shard_map/ppermute | solution.py:64
  114.4 6.8 %collective-permute-start.20 = (bf16[32,3072]{1,0:T(8,128)(2,1)S(1)}, bf16[32,3072]{1,0:T(8,128)(2,1)S(1)}, u32[]{:S(2)}, u32[]{:S(2)}) collective-permute-start(bf16[32,3072]{1,0:T(8,128)(2,1)S(1)} %get-tuple-element.98), channel_id=1, source_target_pairs={{0,2},{2,4},{4,6},{6,7},{7,5},{5,3},{3,1},{1,0},{8,10},{10,12},{12... | collective-permute-start | bytes 589832 | tf_op jit(solution)/shard_map/ppermute | solution.py:61
  120.9 5.7 %collective-permute-start.18 = (bf16[32,3072]{1,0:T(8,128)(2,1)S(1)}, bf16[32,3072]{1,0:T(8,128)(2,1)S(1)}, u32[]{:S(2)}, u32[]{:S(2)}) collective-permute-start(bf16[32,3072]{1,0:T(8,128)(2,1)S(1)} %collective-permute-done.17), channel_id=1, source_target_pairs={{0,1},{2,0},{4,2},{6,4},{7,6},{5,7},{3,5},{1,3},{8,9},{10,8},{12,1... | collective-permute-start | bytes 589832 | tf_op jit(solution)/shard_map/ppermute | solution.py:64
  121.2 5.9 %collective-permute-start.21 = (bf16[32,3072]{1,0:T(8,128)(2,1)S(1)}, bf16[32,3072]{1,0:T(8,128)(2,1)S(1)}, u32[]{:S(2)}, u32[]{:S(2)}) collective-permute-start(bf16[32,3072]{1,0:T(8,128)(2,1)S(1)} %collective-permute-done.20), channel_id=1, source_target_pairs={{0,2},{2,4},{4,6},{6,7},{7,5},{5,3},{3,1},{1,0},{8,10},{10,12},{12... | collective-permute-start | bytes 589832 | tf_op jit(solution)/shard_map/ppermute | solution.py:61
  126.5 5.7 %collective-permute-start.19 = (bf16[32,3072]{1,0:T(8,128)(2,1)S(1)}, bf16[32,3072]{1,0:T(8,128)(2,1)S(1)}, u32[]{:S(2)}, u32[]{:S(2)}) collective-permute-start(bf16[32,3072]{1,0:T(8,128)(2,1)S(1)} %collective-permute-done.18), channel_id=1, source_target_pairs={{0,1},{2,0},{4,2},{6,4},{7,6},{5,7},{3,5},{1,3},{8,9},{10,8},{12,1... | collective-permute-start | bytes 589832 | tf_op jit(solution)/shard_map/ppermute | solution.py:64
  127.1 5.7 %collective-permute-start.22 = (bf16[32,3072]{1,0:T(8,128)(2,1)S(1)}, bf16[32,3072]{1,0:T(8,128)(2,1)S(1)}, u32[]{:S(2)}, u32[]{:S(2)}) collective-permute-start(bf16[32,3072]{1,0:T(8,128)(2,1)S(1)} %collective-permute-done.21), channel_id=1, source_target_pairs={{0,2},{2,4},{4,6},{6,7},{7,5},{5,3},{3,1},{1,0},{8,10},{10,12},{12... | collective-permute-start | bytes 589832 | tf_op jit(solution)/shard_map/ppermute | solution.py:61
  132.2 4.7 %collective-permute-start.24 = (bf16[16,3072]{1,0:T(8,128)(2,1)S(1)}, bf16[16,3072]{1,0:T(8,128)(2,1)S(1)}, u32[]{:S(2)}, u32[]{:S(2)}) collective-permute-start(bf16[16,3072]{1,0:T(8,128)(2,1)S(1)} %slice.367), channel_id=1, source_target_pairs={{0,1},{2,0},{4,2},{6,4},{7,6},{5,7},{3,5},{1,3},{8,9},{10,8},{12,1... | collective-permute-start | bytes 294920 | tf_op jit(solution)/shard_map/ppermute | solution.py:58
  132.9 4.7 %collective-permute-start.23 = (bf16[16,3072]{1,0:T(8,128)(2,1)S(1)}, bf16[16,3072]{1,0:T(8,128)(2,1)S(1)}, u32[]{:S(2)}, u32[]{:S(2)}) collective-permute-start(bf16[16,3072]{1,0:T(8,128)(2,1)S(1)} %slice.366), channel_id=1, source_target_pairs={{0,2},{2,4},{4,6},{6,7},{7,5},{5,3},{3,1},{1,0},{8,10},{10,12},{12... | collective-permute-start | bytes 294920 | tf_op jit(solution)/shard_map/ppermute | solution.py:57
  144.9 2.2 copy-start.2
  145.4 3.3 %collective-permute-start.25 = (bf16[128,3072]{1,0:T(8,128)(2,1)S(1)}, bf16[128,3072]{1,0:T(8,128)(2,1)S(1)}, u32[]{:S(2)}, u32[]{:S(2)}) collective-permute-start(bf16[128,3072]{1,0:T(8,128)(2,1)S(1)} %slice.368), channel_id=1, source_target_pairs={{0,8},{1,9},{2,10},{3,11},{4,12},{5,13},{6,14},{7,15},{16,24},{17,... | collective-permute-start | bytes 2359304 | tf_op jit(solution)/shard_map/ppermute | solution.py:14
  171.9 5.1 %collective-permute-start.26 = (bf16[16,3072]{1,0:T(8,128)(2,1)S(1)}, bf16[16,3072]{1,0:T(8,128)(2,1)S(1)}, u32[]{:S(2)}, u32[]{:S(2)}) collective-permute-start(bf16[16,3072]{1,0:T(8,128)(2,1)S(1)} %get-tuple-element.115), channel_id=1, source_target_pairs={{0,2},{2,4},{4,6},{6,7},{7,5},{5,3},{3,1},{1,0},{8,10},{10,12},{12... | collective-permute-start | bytes 294920 | tf_op jit(solution)/shard_map/ppermute | solution.py:94
  173.4 5.0 %collective-permute-start.30 = (bf16[16,3072]{1,0:T(8,128)(2,1)S(1)}, bf16[16,3072]{1,0:T(8,128)(2,1)S(1)}, u32[]{:S(2)}, u32[]{:S(2)}) collective-permute-start(bf16[16,3072]{1,0:T(8,128)(2,1)S(1)} %get-tuple-element.116), channel_id=1, source_target_pairs={{0,1},{2,0},{4,2},{6,4},{7,6},{5,7},{3,5},{1,3},{8,9},{10,8},{12,1... | collective-permute-start | bytes 294920 | tf_op jit(solution)/shard_map/ppermute | solution.py:94
  177.0 6.4 %collective-permute-start.27 = (bf16[32,3072]{1,0:T(8,128)(2,1)S(1)}, bf16[32,3072]{1,0:T(8,128)(2,1)S(1)}, u32[]{:S(2)}, u32[]{:S(2)}) collective-permute-start(bf16[32,3072]{1,0:T(8,128)(2,1)S(1)} %fusion.60), channel_id=1, source_target_pairs={{0,2},{2,4},{4,6},{6,7},{7,5},{5,3},{3,1},{1,0},{8,10},{10,12},{12... | collective-permute-start | bytes 589832 | tf_op jit(solution)/shard_map/ppermute | solution.py:94
  178.5 6.4 %collective-permute-start.31 = (bf16[32,3072]{1,0:T(8,128)(2,1)S(1)}, bf16[32,3072]{1,0:T(8,128)(2,1)S(1)}, u32[]{:S(2)}, u32[]{:S(2)}) collective-permute-start(bf16[32,3072]{1,0:T(8,128)(2,1)S(1)} %fusion.58), channel_id=1, source_target_pairs={{0,1},{2,0},{4,2},{6,4},{7,6},{5,7},{3,5},{1,3},{8,9},{10,8},{12,1... | collective-permute-start | bytes 589832 | tf_op jit(solution)/shard_map/ppermute | solution.py:94
  183.5 5.7 %collective-permute-start.28 = (bf16[32,3072]{1,0:T(8,128)(2,1)S(1)}, bf16[32,3072]{1,0:T(8,128)(2,1)S(1)}, u32[]{:S(2)}, u32[]{:S(2)}) collective-permute-start(bf16[32,3072]{1,0:T(8,128)(2,1)S(1)} %fusion.39), channel_id=1, source_target_pairs={{0,2},{2,4},{4,6},{6,7},{7,5},{5,3},{3,1},{1,0},{8,10},{10,12},{12... | collective-permute-start | bytes 589832 | tf_op jit(solution)/shard_map/ppermute | solution.py:94
  189.3 6.6 %collective-permute-start.32 = (bf16[32,3072]{1,0:T(8,128)(2,1)S(1)}, bf16[32,3072]{1,0:T(8,128)(2,1)S(1)}, u32[]{:S(2)}, u32[]{:S(2)}) collective-permute-start(bf16[32,3072]{1,0:T(8,128)(2,1)S(1)} %get-tuple-element.114), channel_id=1, source_target_pairs={{0,1},{2,0},{4,2},{6,4},{7,6},{5,7},{3,5},{1,3},{8,9},{10,8},{12,1... | collective-permute-start | bytes 589832 | tf_op jit(solution)/shard_map/ppermute | solution.py:94
  190.9 6.7 %collective-permute-start.29 = (bf16[32,3072]{1,0:T(8,128)(2,1)S(1)}, bf16[32,3072]{1,0:T(8,128)(2,1)S(1)}, u32[]{:S(2)}, u32[]{:S(2)}) collective-permute-start(bf16[32,3072]{1,0:T(8,128)(2,1)S(1)} %get-tuple-element.113), channel_id=1, source_target_pairs={{0,2},{2,4},{4,6},{6,7},{7,5},{5,3},{3,1},{1,0},{8,10},{10,12},{12... | collective-permute-start | bytes 589832 | tf_op jit(solution)/shard_map/ppermute | solution.py:94
  196.0 7.2 %collective-permute-start.33 = (bf16[32,3072]{1,0:T(8,128)(2,1)S(1)}, bf16[32,3072]{1,0:T(8,128)(2,1)S(1)}, u32[]{:S(2)}, u32[]{:S(2)}) collective-permute-start(bf16[32,3072]{1,0:T(8,128)(2,1)S(1)} %fusion.38), channel_id=1, source_target_pairs={{0,1},{2,0},{4,2},{6,4},{7,6},{5,7},{3,5},{1,3},{8,9},{10,8},{12,1... | collective-permute-start | bytes 589832 | tf_op jit(solution)/shard_map/ppermute | solution.py:94
  204.0 6.5 %collective-permute-start.34 = (bf16[32,3072]{1,0:T(8,128)(2,1)S(1)}, bf16[32,3072]{1,0:T(8,128)(2,1)S(1)}, u32[]{:S(2)}, u32[]{:S(2)}) collective-permute-start(bf16[32,3072]{1,0:T(8,128)(2,1)S(1)} %get-tuple-element.96), channel_id=1, source_target_pairs={{0,1},{2,0},{4,2},{6,4},{7,6},{5,7},{3,5},{1,3},{8,9},{10,8},{12,1... | collective-permute-start | bytes 589832 | tf_op jit(solution)/shard_map/ppermute | solution.py:64
  205.5 6.5 %collective-permute-start.37 = (bf16[32,3072]{1,0:T(8,128)(2,1)S(1)}, bf16[32,3072]{1,0:T(8,128)(2,1)S(1)}, u32[]{:S(2)}, u32[]{:S(2)}) collective-permute-start(bf16[32,3072]{1,0:T(8,128)(2,1)S(1)} %get-tuple-element.96), channel_id=1, source_target_pairs={{0,2},{2,4},{4,6},{6,7},{7,5},{5,3},{3,1},{1,0},{8,10},{10,12},{12... | collective-permute-start | bytes 589832 | tf_op jit(solution)/shard_map/ppermute | solution.py:61
  210.5 5.7 %collective-permute-start.35 = (bf16[32,3072]{1,0:T(8,128)(2,1)S(1)}, bf16[32,3072]{1,0:T(8,128)(2,1)S(1)}, u32[]{:S(2)}, u32[]{:S(2)}) collective-permute-start(bf16[32,3072]{1,0:T(8,128)(2,1)S(1)} %collective-permute-done.34), channel_id=1, source_target_pairs={{0,1},{2,0},{4,2},{6,4},{7,6},{5,7},{3,5},{1,3},{8,9},{10,8},{12,1... | collective-permute-start | bytes 589832 | tf_op jit(solution)/shard_map/ppermute | solution.py:64
  212.0 5.7 %collective-permute-start.38 = (bf16[32,3072]{1,0:T(8,128)(2,1)S(1)}, bf16[32,3072]{1,0:T(8,128)(2,1)S(1)}, u32[]{:S(2)}, u32[]{:S(2)}) collective-permute-start(bf16[32,3072]{1,0:T(8,128)(2,1)S(1)} %collective-permute-done.37), channel_id=1, source_target_pairs={{0,2},{2,4},{4,6},{6,7},{7,5},{5,3},{3,1},{1,0},{8,10},{10,12},{12... | collective-permute-start | bytes 589832 | tf_op jit(solution)/shard_map/ppermute | solution.py:61
  216.2 5.7 %collective-permute-start.36 = (bf16[32,3072]{1,0:T(8,128)(2,1)S(1)}, bf16[32,3072]{1,0:T(8,128)(2,1)S(1)}, u32[]{:S(2)}, u32[]{:S(2)}) collective-permute-start(bf16[32,3072]{1,0:T(8,128)(2,1)S(1)} %collective-permute-done.35), channel_id=1, source_target_pairs={{0,1},{2,0},{4,2},{6,4},{7,6},{5,7},{3,5},{1,3},{8,9},{10,8},{12,1... | collective-permute-start | bytes 589832 | tf_op jit(solution)/shard_map/ppermute | solution.py:64
  217.7 5.7 %collective-permute-start.39 = (bf16[32,3072]{1,0:T(8,128)(2,1)S(1)}, bf16[32,3072]{1,0:T(8,128)(2,1)S(1)}, u32[]{:S(2)}, u32[]{:S(2)}) collective-permute-start(bf16[32,3072]{1,0:T(8,128)(2,1)S(1)} %collective-permute-done.38), channel_id=1, source_target_pairs={{0,2},{2,4},{4,6},{6,7},{7,5},{5,3},{3,1},{1,0},{8,10},{10,12},{12... | collective-permute-start | bytes 589832 | tf_op jit(solution)/shard_map/ppermute | solution.py:61
  221.8 4.7 %collective-permute-start.41 = (bf16[16,3072]{1,0:T(8,128)(2,1)S(1)}, bf16[16,3072]{1,0:T(8,128)(2,1)S(1)}, u32[]{:S(2)}, u32[]{:S(2)}) collective-permute-start(bf16[16,3072]{1,0:T(8,128)(2,1)S(1)} %slice.381), channel_id=1, source_target_pairs={{0,1},{2,0},{4,2},{6,4},{7,6},{5,7},{3,5},{1,3},{8,9},{10,8},{12,1... | collective-permute-start | bytes 294920 | tf_op jit(solution)/shard_map/ppermute | solution.py:58
  223.4 4.7 %collective-permute-start.40 = (bf16[16,3072]{1,0:T(8,128)(2,1)S(1)}, bf16[16,3072]{1,0:T(8,128)(2,1)S(1)}, u32[]{:S(2)}, u32[]{:S(2)}) collective-permute-start(bf16[16,3072]{1,0:T(8,128)(2,1)S(1)} %slice.380), channel_id=1, source_target_pairs={{0,2},{2,4},{4,6},{6,7},{7,5},{5,3},{3,1},{1,0},{8,10},{10,12},{12... | collective-permute-start | bytes 294920 | tf_op jit(solution)/shard_map/ppermute | solution.py:57
  233.3 1.7 copy-start.4
  236.7 2.9 %collective-permute-start.42 = (bf16[256,128]{1,0:T(8,128)(2,1)S(1)}, bf16[256,128]{1,0:T(8,128)(2,1)S(1)}, u32[]{:S(2)}, u32[]{:S(2)}) collective-permute-start(bf16[256,128]{1,0:T(8,128)(2,1)S(1)} %convolution_convert_fusion.4), channel_id=1, source_target_pairs={{0,8},{1,9},{2,10},{3,11},{4,12},{5,13},{6,14},{7,15},{16,24},{17,... | collective-permute-start | bytes 196616 | tf_op jit(solution)/shard_map/ppermute | solution.py:14
  238.0 2.2 collective-permute-start.43
  245.4 4.7 %collective-permute-start.44 = (bf16[16,3072]{1,0:T(8,128)(2,1)S(1)}, bf16[16,3072]{1,0:T(8,128)(2,1)S(1)}, u32[]{:S(2)}, u32[]{:S(2)}) collective-permute-start(bf16[16,3072]{1,0:T(8,128)(2,1)S(1)} %get-tuple-element.107), channel_id=1, source_target_pairs={{0,2},{2,4},{4,6},{6,7},{7,5},{5,3},{3,1},{1,0},{8,10},{10,12},{12... | collective-permute-start | bytes 294920 | tf_op jit(solution)/shard_map/ppermute | solution.py:94
  246.1 4.8 %collective-permute-start.48 = (bf16[16,3072]{1,0:T(8,128)(2,1)S(1)}, bf16[16,3072]{1,0:T(8,128)(2,1)S(1)}, u32[]{:S(2)}, u32[]{:S(2)}) collective-permute-start(bf16[16,3072]{1,0:T(8,128)(2,1)S(1)} %get-tuple-element.108), channel_id=1, source_target_pairs={{0,1},{2,0},{4,2},{6,4},{7,6},{5,7},{3,5},{1,3},{8,9},{10,8},{12,1... | collective-permute-start | bytes 294920 | tf_op jit(solution)/shard_map/ppermute | solution.py:94
  250.1 7.7 %collective-permute-start.45 = (bf16[32,3072]{1,0:T(8,128)(2,1)S(1)}, bf16[32,3072]{1,0:T(8,128)(2,1)S(1)}, u32[]{:S(2)}, u32[]{:S(2)}) collective-permute-start(bf16[32,3072]{1,0:T(8,128)(2,1)S(1)} %fusion.56), channel_id=1, source_target_pairs={{0,2},{2,4},{4,6},{6,7},{7,5},{5,3},{3,1},{1,0},{8,10},{10,12},{12... | collective-permute-start | bytes 589832 | tf_op jit(solution)/shard_map/ppermute | solution.py:94
  250.9 7.8 %collective-permute-start.49 = (bf16[32,3072]{1,0:T(8,128)(2,1)S(1)}, bf16[32,3072]{1,0:T(8,128)(2,1)S(1)}, u32[]{:S(2)}, u32[]{:S(2)}) collective-permute-start(bf16[32,3072]{1,0:T(8,128)(2,1)S(1)} %fusion.54), channel_id=1, source_target_pairs={{0,1},{2,0},{4,2},{6,4},{7,6},{5,7},{3,5},{1,3},{8,9},{10,8},{12,1... | collective-permute-start | bytes 589832 | tf_op jit(solution)/shard_map/ppermute | solution.py:94
  257.9 7.1 %collective-permute-start.46 = (bf16[32,3072]{1,0:T(8,128)(2,1)S(1)}, bf16[32,3072]{1,0:T(8,128)(2,1)S(1)}, u32[]{:S(2)}, u32[]{:S(2)}) collective-permute-start(bf16[32,3072]{1,0:T(8,128)(2,1)S(1)} %fusion.32), channel_id=1, source_target_pairs={{0,2},{2,4},{4,6},{6,7},{7,5},{5,3},{3,1},{1,0},{8,10},{10,12},{12... | collective-permute-start | bytes 589832 | tf_op jit(solution)/shard_map/ppermute | solution.py:94
  265.1 6.3 %collective-permute-start.50 = (bf16[32,3072]{1,0:T(8,128)(2,1)S(1)}, bf16[32,3072]{1,0:T(8,128)(2,1)S(1)}, u32[]{:S(2)}, u32[]{:S(2)}) collective-permute-start(bf16[32,3072]{1,0:T(8,128)(2,1)S(1)} %get-tuple-element.106), channel_id=1, source_target_pairs={{0,1},{2,0},{4,2},{6,4},{7,6},{5,7},{3,5},{1,3},{8,9},{10,8},{12,1... | collective-permute-start | bytes 589832 | tf_op jit(solution)/shard_map/ppermute | solution.py:94
  266.7 6.3 %collective-permute-start.47 = (bf16[32,3072]{1,0:T(8,128)(2,1)S(1)}, bf16[32,3072]{1,0:T(8,128)(2,1)S(1)}, u32[]{:S(2)}, u32[]{:S(2)}) collective-permute-start(bf16[32,3072]{1,0:T(8,128)(2,1)S(1)} %get-tuple-element.105), channel_id=1, source_target_pairs={{0,2},{2,4},{4,6},{6,7},{7,5},{5,3},{3,1},{1,0},{8,10},{10,12},{12... | collective-permute-start | bytes 589832 | tf_op jit(solution)/shard_map/ppermute | solution.py:94
  271.4 5.7 %collective-permute-start.51 = (bf16[32,3072]{1,0:T(8,128)(2,1)S(1)}, bf16[32,3072]{1,0:T(8,128)(2,1)S(1)}, u32[]{:S(2)}, u32[]{:S(2)}) collective-permute-start(bf16[32,3072]{1,0:T(8,128)(2,1)S(1)} %fusion.31), channel_id=1, source_target_pairs={{0,1},{2,0},{4,2},{6,4},{7,6},{5,7},{3,5},{1,3},{8,9},{10,8},{12,1... | collective-permute-start | bytes 589832 | tf_op jit(solution)/shard_map/ppermute | solution.py:94

commit v6 on v5

--- a/solution.py
+++ b/solution.py
@@ -130,19 +130,20 @@
         gate_acc[...] = jnp.zeros_like(gate_acc)
 
     rows = slab_ref[...]
-    filt_acc[...] += jnp.dot(rows, weight_ref[0], preferred_element_type=jnp.float32)
-    gate_acc[...] += jnp.dot(rows, weight_ref[1], preferred_element_type=jnp.float32)
+    weight = weight_ref[...]
+    filt_acc[...] += jnp.dot(rows, weight[:, 0, :], preferred_element_type=jnp.float32)
+    gate_acc[...] += jnp.dot(rows, weight[:, 1, :], preferred_element_type=jnp.float32)
 
     @pl.when((tap == pl.num_programs(0) - 1) & (chunk == pl.num_programs(1) - 1))
     def _():
         out_ref[...] = (jnp.tanh(filt_acc[...]) * jax.nn.sigmoid(gate_acc[...])).astype(out_ref.dtype)
 
 
-def convolution_gate(hidden, conv_by_half, layer_idx, dilation_factor):
+def convolution_gate(hidden, kernel, layer_idx, dilation_factor):
     all_rows = hidden.shape[0]
     width = hidden.shape[1]
-    taps = conv_by_half.shape[1]
-    own_width = conv_by_half.shape[-1]
+    taps = kernel.shape[1]
+    own_width = kernel.shape[-1]
     border_rows = 2 * LARGEST_DILATION
     before = shifted(hidden[all_rows - border_rows :], "blk", 1)
     padded = jnp.concatenate([before, hidden], axis=0)
@@ -152,14 +153,14 @@
             for tap_idx in range(taps)
         ]
     )
-    chunk = 1024 if width % 1024 == 0 else width
+    chunk = 512 if width % 512 == 0 else width
     return pl.pallas_call(
         conv_gate_kernel,
         out_shape=jax.ShapeDtypeStruct((all_rows, own_width), jnp.bfloat16),
         grid=(taps, width // chunk),
         in_specs=[
             pl.BlockSpec((None, all_rows, chunk), lambda t, k: (t, 0, k)),
-            pl.BlockSpec((None, None, 2, chunk, own_width), lambda t, k: (layer_idx, t, 0, k, 0)),
+            pl.BlockSpec((None, None, chunk, 2, own_width), lambda t, k: (layer_idx, t, k, 0, 0)),
         ],
         out_specs=pl.BlockSpec((all_rows, own_width), lambda t, k: (0, 0)),
         scratch_shapes=[pltpu.VMEM((all_rows, own_width), jnp.float32)] * 2,
@@ -169,7 +170,7 @@
             transcendentals=2 * all_rows * own_width,
             bytes_accessed=2 * taps * (all_rows * width + 2 * width * own_width + all_rows * own_width // taps),
         ),
-    )(slabs, conv_by_half)
+    )(slabs, kernel)
 
 
 def conv_share(gated, weight, tok_rows, tables):
@@ -232,10 +233,9 @@
     share = stream
     tables = ring_tables("head")
     state = ring_gather(stream, "head", tables)
-    conv_by_half = jnp.transpose(w_conv, (0, 1, 3, 2, 4))
     for layer_idx in range(layers):
         gated = convolution_gate(
-            normed(state, gains[layer_idx]), conv_by_half, layer_idx, dilations[layer_idx]
+            normed(state, gains[layer_idx]), w_conv, layer_idx, dilations[layer_idx]
         )
         summed = conv_share(gated, w_mix[layer_idx], tok_rows, tables)
         share = (share.astype(jnp.float32) + summed).astype(jnp.bfloat16)

time: 279 us -> 309 us (1.11)
  Pallas kernels: 25 us -> 74.2 us
  local copies, waits for them, and re-layouts: 51.1 us -> 31.6 us
    pallas_call x2, Pallas kernels: 25 us -> 74.2 us  [convolution_gate(): pl.pallas_call(conv_gate_kernel, out_shape=jax.ShapeDtypeStruct((all_rows...]
    unnamed x27 -> x26, local copies, waits for them, and re-layouts: 32.8 us -> 13.2 us
  transfers between devices with their start and end apart: 52 -> 52, of which waited for: 34 -> 34; matrix products, arithmetic and copies ran while one was open for 12% -> 4% of each run, Pallas kernels for 0% -> 0%
where the time goes in v6:
time: 309 us; the launch traced here: 308 us
  waiting for transfers between devices  105 us (34%)
  Pallas kernels  74.2 us (24%)
  starting transfers between devices  57.8 us (19%)
  local copies, waits for them, and re-layouts  31.6 us (10%)
  other arithmetic  23.1 us (7%)
  matrix products  11.7 us (4%)
  between operations  4.44 us (1%)
    pallas_call x2, Pallas kernels, convolution_gate(): pl.pallas_call(conv_gate_kernel, out_shape=jax.ShapeDtypeStruct((all_rows...  74.2 us
    ppermute x24, waiting for transfers between devices, chain(): passed = lax.ppermute(part.astype(value.dtype), axis, pairs)  66.9 us
    ppermute x24, starting transfers between devices, chain(): passed = lax.ppermute(part.astype(value.dtype), axis, pairs)  26.2 us
    ppermute x9, waiting for transfers between devices, ring_gather(): bwd = lax.ppermute(bwd, axis, backward)  19 us
    unnamed x26, local copies, waits for them, and re-layouts  13.2 us
    ppermute x9, starting transfers between devices, ring_gather(): fwd = lax.ppermute(fwd, axis, forward)  13 us
    dot_general x3, matrix products, rounded_term(): term = jnp.dot(left, right, preferred_element_type=jnp.float32)  9.8 us
    another operation x4, other arithmetic, convolution_gate(): jnp.stack([lax.dynamic_slice_in_dim(padded, border_rows - tap_idx * dilat...  9.36 us
  transfers between devices with their start and end apart: 52, of which 34 were waited for; matrix products, arithmetic and copies ran while one was open for 4% of the time, Pallas kernels for 0%

profile of v6, /device:TPU:0, one launch (start us, length us, event | category | flops | bytes accessed | tf_op | source)
XLA Modules:
  0.0 308.1 jit_solution(17112740639116841731)
XLA Ops:
  0.0 3.0 collective-permute-start.3
  9.7 2.1 collective-permute-start.4
  12.5 3.6 %collective-permute-done.4 = bf16[32,3072]{1,0:T(8,128)(2,1)S(1)} collective-permute-done((bf16[32,3072]{1,0:T(8,128)(2,1)S(1)}, bf16[32,3072]{1,0:T(8,128)(2,1)S(1)}, u32[]{:S(2)}, u32[]{:S(2)}) %collective-permute-start.4) | collective-permute-done | bytes 196640 | tf_op jit(solution)/shard_map/ppermute | solution.py:61
  16.1 1.7 collective-permute-start.5
  18.8 2.9 collective-permute-done.5
  21.8 1.9 collective-permute-start.6
  24.6 1.8 collective-permute-done.6
  26.5 1.9 collective-permute-done.7
  31.1 2.1 gather_fusion
  33.6 2.0 convert_element_type.566
  39.5 2.2 fusion.27
  41.7 2.5 pad_maximum_fusion.slab_ref
  44.2 37.1 %shard_map.82 = bf16[256,384]{1,0:T(8,128)(2,1)} custom-call(bf16[3,256,3072]{2,1,0:T(8,128)(2,1)} %pad_maximum_fusion.slab_ref, bf16[2,3,3072,2,384]{4,3,2,1,0:T(2,128)(2,1)} %weight_ref.3), custom_call_target="tpu_custom_call" | custom-call | flops 3623878656 | bytes 19070976 | tf_op jit(solution)/shard_map/pallas_call | solution.py:157
  81.3 3.9 %convolution_convert_fusion.2 = bf16[256,3072]{1,0:T(8,128)(2,1)} fusion(bf16[256,384]{1,0:T(8,128)(2,1)} %shard_map.82, bf16[2,384,3072]{2,1,0:T(8,128)(2,1)} %param.26), kind=kOutput, calls=%fused_computation.18 | convolution fusion | flops 604766208 | bytes 4128768 | tf_op jit(solution)/shard_map/dot_general | solution.py:119
  85.3 2.1 gather_fusion.1
  87.3 1.6 collective-permute-start.9
  89.6 3.0 collective-permute-done.9
  94.7 4.4 %collective-permute-done.10 = bf16[32,3072]{1,0:T(8,128)(2,1)S(1)} collective-permute-done((bf16[32,3072]{1,0:T(8,128)(2,1)S(1)}, bf16[32,3072]{1,0:T(8,128)(2,1)S(1)}, u32[]{:S(2)}, u32[]{:S(2)}) %collective-permute-start.10) | collective-permute-done | bytes 196640 | tf_op jit(solution)/shard_map/ppermute | solution.py:94
  100.8 4.1 %collective-permute-done.11 = bf16[32,3072]{1,0:T(8,128)(2,1)S(1)} collective-permute-done((bf16[32,3072]{1,0:T(8,128)(2,1)S(1)}, bf16[32,3072]{1,0:T(8,128)(2,1)S(1)}, u32[]{:S(2)}, u32[]{:S(2)}) %collective-permute-start.11) | collective-permute-done | bytes 196640 | tf_op jit(solution)/shard_map/ppermute | solution.py:94
  105.4 1.7 collective-permute-start.12
  107.1 4.4 %collective-permute-done.15 = bf16[32,3072]{1,0:T(8,128)(2,1)S(1)} collective-permute-done((bf16[32,3072]{1,0:T(8,128)(2,1)S(1)}, bf16[32,3072]{1,0:T(8,128)(2,1)S(1)}, u32[]{:S(2)}, u32[]{:S(2)}) %collective-permute-start.15) | collective-permute-done | bytes 196640 | tf_op jit(solution)/shard_map/ppermute | solution.py:94
  111.9 6.6 %collective-permute-done.16 = bf16[32,3072]{1,0:T(8,128)(2,1)S(1)} collective-permute-done((bf16[32,3072]{1,0:T(8,128)(2,1)S(1)}, bf16[32,3072]{1,0:T(8,128)(2,1)S(1)}, u32[]{:S(2)}, u32[]{:S(2)}) %collective-permute-start.16) | collective-permute-done | bytes 196640 | tf_op jit(solution)/shard_map/ppermute | solution.py:94
  119.6 1.7 collective-permute-start.20
  123.4 2.6 collective-permute-done.17
  126.3 1.7 collective-permute-start.21
  128.7 3.1 %collective-permute-done.18 = bf16[32,3072]{1,0:T(8,128)(2,1)S(1)} collective-permute-done((bf16[32,3072]{1,0:T(8,128)(2,1)S(1)}, bf16[32,3072]{1,0:T(8,128)(2,1)S(1)}, u32[]{:S(2)}, u32[]{:S(2)}) %collective-permute-start.18) | collective-permute-done | bytes 196640 | tf_op jit(solution)/shard_map/ppermute | solution.py:64
  132.1 1.7 collective-permute-start.22
  134.5 2.9 collective-permute-done.19
  137.9 1.9 collective-permute-start.23
  140.5 1.7 collective-permute-done.24
  145.5 2.1 gather_fusion.2
  147.9 2.0 convert_element_type.573
  153.9 2.2 fusion.23
  156.1 2.5 pad_maximum_fusion.1.slab_ref
  158.6 37.1 %shard_map.83 = bf16[256,384]{1,0:T(8,128)(2,1)} custom-call(bf16[3,256,3072]{2,1,0:T(8,128)(2,1)} %pad_maximum_fusion.1.slab_ref, bf16[2,3,3072,2,384]{4,3,2,1,0:T(2,128)(2,1)} %weight_ref.3), custom_call_target="tpu_custom_call" | custom-call | flops 3623878656 | bytes 19070976 | tf_op jit(solution)/shard_map/pallas_call | solution.py:157
  195.7 3.9 %convolution_convert_fusion.1 = bf16[256,3072]{1,0:T(8,128)(2,1)} fusion(bf16[256,384]{1,0:T(8,128)(2,1)} %shard_map.83, bf16[2,384,3072]{2,1,0:T(8,128)(2,1)} %param.26), kind=kOutput, calls=%fused_computation.17 | convolution fusion | flops 604766208 | bytes 4128768 | tf_op jit(solution)/shard_map/dot_general | solution.py:119
  199.6 2.1 gather_fusion.3
  201.7 1.8 collective-permute-start.26
  204.0 2.9 collective-permute-done.26
  206.9 1.8 collective-permute-start.27
  209.0 4.3 %collective-permute-done.27 = bf16[32,3072]{1,0:T(8,128)(2,1)S(1)} collective-permute-done((bf16[32,3072]{1,0:T(8,128)(2,1)S(1)}, bf16[32,3072]{1,0:T(8,128)(2,1)S(1)}, u32[]{:S(2)}, u32[]{:S(2)}) %collective-permute-start.27) | collective-permute-done | bytes 196640 | tf_op jit(solution)/shard_map/ppermute | solution.py:94
  213.3 1.7 collective-permute-start.28
  215.0 4.0 %collective-permute-done.28 = bf16[32,3072]{1,0:T(8,128)(2,1)S(1)} collective-permute-done((bf16[32,3072]{1,0:T(8,128)(2,1)S(1)}, bf16[32,3072]{1,0:T(8,128)(2,1)S(1)}, u32[]{:S(2)}, u32[]{:S(2)}) %collective-permute-start.28) | collective-permute-done | bytes 196640 | tf_op jit(solution)/shard_map/ppermute | solution.py:94
  221.3 4.6 %collective-permute-done.32 = bf16[32,3072]{1,0:T(8,128)(2,1)S(1)} collective-permute-done((bf16[32,3072]{1,0:T(8,128)(2,1)S(1)}, bf16[32,3072]{1,0:T(8,128)(2,1)S(1)}, u32[]{:S(2)}, u32[]{:S(2)}) %collective-permute-start.32) | collective-permute-done | bytes 196640 | tf_op jit(solution)/shard_map/ppermute | solution.py:94
  225.9 1.7 collective-permute-start.33
  227.6 5.4 %collective-permute-done.33 = bf16[32,3072]{1,0:T(8,128)(2,1)S(1)} collective-permute-done((bf16[32,3072]{1,0:T(8,128)(2,1)S(1)}, bf16[32,3072]{1,0:T(8,128)(2,1)S(1)}, u32[]{:S(2)}, u32[]{:S(2)}) %collective-permute-start.33) | collective-permute-done | bytes 196640 | tf_op jit(solution)/shard_map/ppermute | solution.py:94
  233.8 1.8 collective-permute-start.34
  235.8 4.5 %collective-permute-done.34 = bf16[32,3072]{1,0:T(8,128)(2,1)S(1)} collective-permute-done((bf16[32,3072]{1,0:T(8,128)(2,1)S(1)}, bf16[32,3072]{1,0:T(8,128)(2,1)S(1)}, u32[]{:S(2)}, u32[]{:S(2)}) %collective-permute-start.34) | collective-permute-done | bytes 196640 | tf_op jit(solution)/shard_map/ppermute | solution.py:64
  240.3 1.7 collective-permute-start.35
  243.1 2.9 collective-permute-done.35
  246.0 1.7 collective-permute-start.36
  248.7 2.9 collective-permute-done.36
  251.7 1.7 collective-permute-start.41
  256.4 2.0 collective-permute-done.40
  261.1 2.1 gather_fusion.4
  271.7 1.9 convolution_convert_fusion
  273.6 2.1 gather_fusion.5
  276.2 1.7 collective-permute-start.48
  277.9 2.4 collective-permute-done.44
  281.0 1.7 collective-permute-start.49
  282.7 5.4 %collective-permute-done.45 = bf16[32,3072]{1,0:T(8,128)(2,1)S(1)} collective-permute-done((bf16[32,3072]{1,0:T(8,128)(2,1)S(1)}, bf16[32,3072]{1,0:T(8,128)(2,1)S(1)}, u32[]{:S(2)}, u32[]{:S(2)}) %collective-permute-start.45) | collective-permute-done | bytes 196640 | tf_op jit(solution)/shard_map/ppermute | solution.py:94
  288.7 6.5 %collective-permute-done.46 = bf16[32,3072]{1,0:T(8,128)(2,1)S(1)} collective-permute-done((bf16[32,3072]{1,0:T(8,128)(2,1)S(1)}, bf16[32,3072]{1,0:T(8,128)(2,1)S(1)}, u32[]{:S(2)}, u32[]{:S(2)}) %collective-permute-start.46) | collective-permute-done | bytes 196640 | tf_op jit(solution)/shard_map/ppermute | solution.py:94
  297.4 4.2 %collective-permute-done.50 = bf16[32,3072]{1,0:T(8,128)(2,1)S(1)} collective-permute-done((bf16[32,3072]{1,0:T(8,128)(2,1)S(1)}, bf16[32,3072]{1,0:T(8,128)(2,1)S(1)}, u32[]{:S(2)}, u32[]{:S(2)}) %collective-permute-start.50) | collective-permute-done | bytes 196640 | tf_op jit(solution)/shard_map/ppermute | solution.py:94
  303.2 4.1 %collective-permute-done.51 = bf16[32,3072]{1,0:T(8,128)(2,1)S(1)} collective-permute-done((bf16[32,3072]{1,0:T(8,128)(2,1)S(1)}, bf16[32,3072]{1,0:T(8,128)(2,1)S(1)}, u32[]{:S(2)}, u32[]{:S(2)}) %collective-permute-start.51) | collective-permute-done | bytes 196640 | tf_op jit(solution)/shard_map/ppermute | solution.py:94
  (149 shorter events, 59.0 us)
Async XLA Ops:
  0.0 271.7 %copy-start = (bf16[1,128,3072]{2,1,0:T(8,128)(2,1)S(1)}, bf16[1,128,3072]{2,1,0:T(8,128)(2,1)}, u32[]{:S(2)}) copy-start(bf16[1,128,3072]{2,1,0:T(8,128)(2,1)} %param.28) | copy-start | bytes 2359300
  0.0 9.7 %collective-permute-start.3 = (bf16[32,3072]{1,0:T(8,128)(2,1)}, bf16[32,3072]{1,0:T(8,128)(2,1)S(1)}, u32[]{:S(2)}, u32[]{:S(2)}) collective-permute-start(bf16[32,3072]{1,0:T(8,128)(2,1)} %param.22), channel_id=1, source_target_pairs={{0,2},{2,4},{4,6},{6,7},{7,5},{5,3},{3,1},{1,0},{8,10},{10,12},{12... | collective-permute-start | bytes 589832 | tf_op jit(solution)/shard_map/ppermute | solution.py:61
  3.0 8.7 %collective-permute-start = (bf16[32,3072]{1,0:T(8,128)(2,1)}, bf16[32,3072]{1,0:T(8,128)(2,1)S(1)}, u32[]{:S(2)}, u32[]{:S(2)}) collective-permute-start(bf16[32,3072]{1,0:T(8,128)(2,1)} %param.22), channel_id=1, source_target_pairs={{0,1},{2,0},{4,2},{6,4},{7,6},{5,7},{3,5},{1,3},{8,9},{10,8},{12,1... | collective-permute-start | bytes 589832 | tf_op jit(solution)/shard_map/ppermute | solution.py:64
  9.7 6.4 %collective-permute-start.4 = (bf16[32,3072]{1,0:T(8,128)(2,1)S(1)}, bf16[32,3072]{1,0:T(8,128)(2,1)S(1)}, u32[]{:S(2)}, u32[]{:S(2)}) collective-permute-start(bf16[32,3072]{1,0:T(8,128)(2,1)S(1)} %collective-permute-done.3), channel_id=1, source_target_pairs={{0,2},{2,4},{4,6},{6,7},{7,5},{5,3},{3,1},{1,0},{8,10},{10,12},{12... | collective-permute-start | bytes 589832 | tf_op jit(solution)/shard_map/ppermute | solution.py:61
  11.8 6.1 %collective-permute-start.1 = (bf16[32,3072]{1,0:T(8,128)(2,1)S(1)}, bf16[32,3072]{1,0:T(8,128)(2,1)S(1)}, u32[]{:S(2)}, u32[]{:S(2)}) collective-permute-start(bf16[32,3072]{1,0:T(8,128)(2,1)S(1)} %collective-permute-done), channel_id=1, source_target_pairs={{0,1},{2,0},{4,2},{6,4},{7,6},{5,7},{3,5},{1,3},{8,9},{10,8},{12,1... | collective-permute-start | bytes 589832 | tf_op jit(solution)/shard_map/ppermute | solution.py:64
  16.1 5.7 %collective-permute-start.5 = (bf16[32,3072]{1,0:T(8,128)(2,1)S(1)}, bf16[32,3072]{1,0:T(8,128)(2,1)S(1)}, u32[]{:S(2)}, u32[]{:S(2)}) collective-permute-start(bf16[32,3072]{1,0:T(8,128)(2,1)S(1)} %collective-permute-done.4), channel_id=1, source_target_pairs={{0,2},{2,4},{4,6},{6,7},{7,5},{5,3},{3,1},{1,0},{8,10},{10,12},{12... | collective-permute-start | bytes 589832 | tf_op jit(solution)/shard_map/ppermute | solution.py:61
  17.9 5.8 %collective-permute-start.2 = (bf16[32,3072]{1,0:T(8,128)(2,1)S(1)}, bf16[32,3072]{1,0:T(8,128)(2,1)S(1)}, u32[]{:S(2)}, u32[]{:S(2)}) collective-permute-start(bf16[32,3072]{1,0:T(8,128)(2,1)S(1)} %collective-permute-done.1), channel_id=1, source_target_pairs={{0,1},{2,0},{4,2},{6,4},{7,6},{5,7},{3,5},{1,3},{8,9},{10,8},{12,1... | collective-permute-start | bytes 589832 | tf_op jit(solution)/shard_map/ppermute | solution.py:64
  21.8 4.7 %collective-permute-start.6 = (bf16[16,3072]{1,0:T(8,128)(2,1)S(1)}, bf16[16,3072]{1,0:T(8,128)(2,1)S(1)}, u32[]{:S(2)}, u32[]{:S(2)}) collective-permute-start(bf16[16,3072]{1,0:T(8,128)(2,1)S(1)} %slice.352), channel_id=1, source_target_pairs={{0,2},{2,4},{4,6},{6,7},{7,5},{5,3},{3,1},{1,0},{8,10},{10,12},{12... | collective-permute-start | bytes 294920 | tf_op jit(solution)/shard_map/ppermute | solution.py:57
  23.7 4.7 %collective-permute-start.7 = (bf16[16,3072]{1,0:T(8,128)(2,1)S(1)}, bf16[16,3072]{1,0:T(8,128)(2,1)S(1)}, u32[]{:S(2)}, u32[]{:S(2)}) collective-permute-start(bf16[16,3072]{1,0:T(8,128)(2,1)S(1)} %slice.353), channel_id=1, source_target_pairs={{0,1},{2,0},{4,2},{6,4},{7,6},{5,7},{3,5},{1,3},{8,9},{10,8},{12,1... | collective-permute-start | bytes 294920 | tf_op jit(solution)/shard_map/ppermute | solution.py:58
  35.6 2.0 copy-start.1
  36.2 3.3 %collective-permute-start.8 = (bf16[128,3072]{1,0:T(8,128)(2,1)S(1)}, bf16[128,3072]{1,0:T(8,128)(2,1)S(1)}, u32[]{:S(2)}, u32[]{:S(2)}) collective-permute-start(bf16[128,3072]{1,0:T(8,128)(2,1)S(1)} %slice.354), channel_id=1, source_target_pairs={{0,8},{1,9},{2,10},{3,11},{4,12},{5,13},{6,14},{7,15},{16,24},{17,... | collective-permute-start | bytes 2359304 | tf_op jit(solution)/shard_map/ppermute | solution.py:14
  87.3 5.2 %collective-permute-start.9 = (bf16[16,3072]{1,0:T(8,128)(2,1)S(1)}, bf16[16,3072]{1,0:T(8,128)(2,1)S(1)}, u32[]{:S(2)}, u32[]{:S(2)}) collective-permute-start(bf16[16,3072]{1,0:T(8,128)(2,1)S(1)} %get-tuple-element.123), channel_id=1, source_target_pairs={{0,2},{2,4},{4,6},{6,7},{7,5},{5,3},{3,1},{1,0},{8,10},{10,12},{12... | collective-permute-start | bytes 294920 | tf_op jit(solution)/shard_map/ppermute | solution.py:94
  89.1 5.1 %collective-permute-start.13 = (bf16[16,3072]{1,0:T(8,128)(2,1)S(1)}, bf16[16,3072]{1,0:T(8,128)(2,1)S(1)}, u32[]{:S(2)}, u32[]{:S(2)}) collective-permute-start(bf16[16,3072]{1,0:T(8,128)(2,1)S(1)} %get-tuple-element.124), channel_id=1, source_target_pairs={{0,1},{2,0},{4,2},{6,4},{7,6},{5,7},{3,5},{1,3},{8,9},{10,8},{12,1... | collective-permute-start | bytes 294920 | tf_op jit(solution)/shard_map/ppermute | solution.py:94
  92.5 26.0 %copy-start.3 = (bf16[32,3072]{1,0:T(8,128)(2,1)S(1)}, bf16[32,3072]{1,0:T(8,128)(2,1)}, u32[]{:S(2)}) copy-start(bf16[32,3072]{1,0:T(8,128)(2,1)} %param.22) | copy-start | bytes 589828
  92.6 6.5 %collective-permute-start.10 = (bf16[32,3072]{1,0:T(8,128)(2,1)S(1)}, bf16[32,3072]{1,0:T(8,128)(2,1)S(1)}, u32[]{:S(2)}, u32[]{:S(2)}) collective-permute-start(bf16[32,3072]{1,0:T(8,128)(2,1)S(1)} %fusion.64), channel_id=1, source_target_pairs={{0,2},{2,4},{4,6},{6,7},{7,5},{5,3},{3,1},{1,0},{8,10},{10,12},{12... | collective-permute-start | bytes 589832 | tf_op jit(solution)/shard_map/ppermute | solution.py:94
  94.2 6.6 %collective-permute-start.14 = (bf16[32,3072]{1,0:T(8,128)(2,1)S(1)}, bf16[32,3072]{1,0:T(8,128)(2,1)S(1)}, u32[]{:S(2)}, u32[]{:S(2)}) collective-permute-start(bf16[32,3072]{1,0:T(8,128)(2,1)S(1)} %fusion.62), channel_id=1, source_target_pairs={{0,1},{2,0},{4,2},{6,4},{7,6},{5,7},{3,5},{1,3},{8,9},{10,8},{12,1... | collective-permute-start | bytes 589832 | tf_op jit(solution)/shard_map/ppermute | solution.py:94
  99.1 5.7 %collective-permute-start.11 = (bf16[32,3072]{1,0:T(8,128)(2,1)S(1)}, bf16[32,3072]{1,0:T(8,128)(2,1)S(1)}, u32[]{:S(2)}, u32[]{:S(2)}) collective-permute-start(bf16[32,3072]{1,0:T(8,128)(2,1)S(1)} %fusion.46), channel_id=1, source_target_pairs={{0,2},{2,4},{4,6},{6,7},{7,5},{5,3},{3,1},{1,0},{8,10},{10,12},{12... | collective-permute-start | bytes 589832 | tf_op jit(solution)/shard_map/ppermute | solution.py:94
  105.0 6.5 %collective-permute-start.15 = (bf16[32,3072]{1,0:T(8,128)(2,1)S(1)}, bf16[32,3072]{1,0:T(8,128)(2,1)S(1)}, u32[]{:S(2)}, u32[]{:S(2)}) collective-permute-start(bf16[32,3072]{1,0:T(8,128)(2,1)S(1)} %get-tuple-element.122), channel_id=1, source_target_pairs={{0,1},{2,0},{4,2},{6,4},{7,6},{5,7},{3,5},{1,3},{8,9},{10,8},{12,1... | collective-permute-start | bytes 589832 | tf_op jit(solution)/shard_map/ppermute | solution.py:94
  105.4 6.5 %collective-permute-start.12 = (bf16[32,3072]{1,0:T(8,128)(2,1)S(1)}, bf16[32,3072]{1,0:T(8,128)(2,1)S(1)}, u32[]{:S(2)}, u32[]{:S(2)}) collective-permute-start(bf16[32,3072]{1,0:T(8,128)(2,1)S(1)} %get-tuple-element.121), channel_id=1, source_target_pairs={{0,2},{2,4},{4,6},{6,7},{7,5},{5,3},{3,1},{1,0},{8,10},{10,12},{12... | collective-permute-start | bytes 589832 | tf_op jit(solution)/shard_map/ppermute | solution.py:94
  111.5 7.0 %collective-permute-start.16 = (bf16[32,3072]{1,0:T(8,128)(2,1)S(1)}, bf16[32,3072]{1,0:T(8,128)(2,1)S(1)}, u32[]{:S(2)}, u32[]{:S(2)}) collective-permute-start(bf16[32,3072]{1,0:T(8,128)(2,1)S(1)} %fusion.45), channel_id=1, source_target_pairs={{0,1},{2,0},{4,2},{6,4},{7,6},{5,7},{3,5},{1,3},{8,9},{10,8},{12,1... | collective-permute-start | bytes 589832 | tf_op jit(solution)/shard_map/ppermute | solution.py:94
  119.3 6.7 %collective-permute-start.17 = (bf16[32,3072]{1,0:T(8,128)(2,1)S(1)}, bf16[32,3072]{1,0:T(8,128)(2,1)S(1)}, u32[]{:S(2)}, u32[]{:S(2)}) collective-permute-start(bf16[32,3072]{1,0:T(8,128)(2,1)S(1)} %get-tuple-element.98), channel_id=1, source_target_pairs={{0,1},{2,0},{4,2},{6,4},{7,6},{5,7},{3,5},{1,3},{8,9},{10,8},{12,1... | collective-permute-start | bytes 589832 | tf_op jit(solution)/shard_map/ppermute | solution.py:64
  119.6 6.7 %collective-permute-start.20 = (bf16[32,3072]{1,0:T(8,128)(2,1)S(1)}, bf16[32,3072]{1,0:T(8,128)(2,1)S(1)}, u32[]{:S(2)}, u32[]{:S(2)}) collective-permute-start(bf16[32,3072]{1,0:T(8,128)(2,1)S(1)} %get-tuple-element.98), channel_id=1, source_target_pairs={{0,2},{2,4},{4,6},{6,7},{7,5},{5,3},{3,1},{1,0},{8,10},{10,12},{12... | collective-permute-start | bytes 589832 | tf_op jit(solution)/shard_map/ppermute | solution.py:61
  126.0 5.8 %collective-permute-start.18 = (bf16[32,3072]{1,0:T(8,128)(2,1)S(1)}, bf16[32,3072]{1,0:T(8,128)(2,1)S(1)}, u32[]{:S(2)}, u32[]{:S(2)}) collective-permute-start(bf16[32,3072]{1,0:T(8,128)(2,1)S(1)} %collective-permute-done.17), channel_id=1, source_target_pairs={{0,1},{2,0},{4,2},{6,4},{7,6},{5,7},{3,5},{1,3},{8,9},{10,8},{12,1... | collective-permute-start | bytes 589832 | tf_op jit(solution)/shard_map/ppermute | solution.py:64
  126.3 5.8 %collective-permute-start.21 = (bf16[32,3072]{1,0:T(8,128)(2,1)S(1)}, bf16[32,3072]{1,0:T(8,128)(2,1)S(1)}, u32[]{:S(2)}, u32[]{:S(2)}) collective-permute-start(bf16[32,3072]{1,0:T(8,128)(2,1)S(1)} %collective-permute-done.20), channel_id=1, source_target_pairs={{0,2},{2,4},{4,6},{6,7},{7,5},{5,3},{3,1},{1,0},{8,10},{10,12},{12... | collective-permute-start | bytes 589832 | tf_op jit(solution)/shard_map/ppermute | solution.py:61
  131.8 5.7 %collective-permute-start.19 = (bf16[32,3072]{1,0:T(8,128)(2,1)S(1)}, bf16[32,3072]{1,0:T(8,128)(2,1)S(1)}, u32[]{:S(2)}, u32[]{:S(2)}) collective-permute-start(bf16[32,3072]{1,0:T(8,128)(2,1)S(1)} %collective-permute-done.18), channel_id=1, source_target_pairs={{0,1},{2,0},{4,2},{6,4},{7,6},{5,7},{3,5},{1,3},{8,9},{10,8},{12,1... | collective-permute-start | bytes 589832 | tf_op jit(solution)/shard_map/ppermute | solution.py:64
  132.1 5.7 %collective-permute-start.22 = (bf16[32,3072]{1,0:T(8,128)(2,1)S(1)}, bf16[32,3072]{1,0:T(8,128)(2,1)S(1)}, u32[]{:S(2)}, u32[]{:S(2)}) collective-permute-start(bf16[32,3072]{1,0:T(8,128)(2,1)S(1)} %collective-permute-done.21), channel_id=1, source_target_pairs={{0,2},{2,4},{4,6},{6,7},{7,5},{5,3},{3,1},{1,0},{8,10},{10,12},{12... | collective-permute-start | bytes 589832 | tf_op jit(solution)/shard_map/ppermute | solution.py:61
  137.5 4.7 %collective-permute-start.24 = (bf16[16,3072]{1,0:T(8,128)(2,1)S(1)}, bf16[16,3072]{1,0:T(8,128)(2,1)S(1)}, u32[]{:S(2)}, u32[]{:S(2)}) collective-permute-start(bf16[16,3072]{1,0:T(8,128)(2,1)S(1)} %slice.367), channel_id=1, source_target_pairs={{0,1},{2,0},{4,2},{6,4},{7,6},{5,7},{3,5},{1,3},{8,9},{10,8},{12,1... | collective-permute-start | bytes 294920 | tf_op jit(solution)/shard_map/ppermute | solution.py:58
  137.9 4.8 %collective-permute-start.23 = (bf16[16,3072]{1,0:T(8,128)(2,1)S(1)}, bf16[16,3072]{1,0:T(8,128)(2,1)S(1)}, u32[]{:S(2)}, u32[]{:S(2)}) collective-permute-start(bf16[16,3072]{1,0:T(8,128)(2,1)S(1)} %slice.366), channel_id=1, source_target_pairs={{0,2},{2,4},{4,6},{6,7},{7,5},{5,3},{3,1},{1,0},{8,10},{10,12},{12... | collective-permute-start | bytes 294920 | tf_op jit(solution)/shard_map/ppermute | solution.py:57
  150.0 2.0 copy-start.2
  150.6 3.3 %collective-permute-start.25 = (bf16[128,3072]{1,0:T(8,128)(2,1)S(1)}, bf16[128,3072]{1,0:T(8,128)(2,1)S(1)}, u32[]{:S(2)}, u32[]{:S(2)}) collective-permute-start(bf16[128,3072]{1,0:T(8,128)(2,1)S(1)} %slice.368), channel_id=1, source_target_pairs={{0,8},{1,9},{2,10},{3,11},{4,12},{5,13},{6,14},{7,15},{16,24},{17,... | collective-permute-start | bytes 2359304 | tf_op jit(solution)/shard_map/ppermute | solution.py:14
  201.7 5.1 %collective-permute-start.26 = (bf16[16,3072]{1,0:T(8,128)(2,1)S(1)}, bf16[16,3072]{1,0:T(8,128)(2,1)S(1)}, u32[]{:S(2)}, u32[]{:S(2)}) collective-permute-start(bf16[16,3072]{1,0:T(8,128)(2,1)S(1)} %get-tuple-element.115), channel_id=1, source_target_pairs={{0,2},{2,4},{4,6},{6,7},{7,5},{5,3},{3,1},{1,0},{8,10},{10,12},{12... | collective-permute-start | bytes 294920 | tf_op jit(solution)/shard_map/ppermute | solution.py:94
  203.7 5.0 %collective-permute-start.30 = (bf16[16,3072]{1,0:T(8,128)(2,1)S(1)}, bf16[16,3072]{1,0:T(8,128)(2,1)S(1)}, u32[]{:S(2)}, u32[]{:S(2)}) collective-permute-start(bf16[16,3072]{1,0:T(8,128)(2,1)S(1)} %get-tuple-element.116), channel_id=1, source_target_pairs={{0,1},{2,0},{4,2},{6,4},{7,6},{5,7},{3,5},{1,3},{8,9},{10,8},{12,1... | collective-permute-start | bytes 294920 | tf_op jit(solution)/shard_map/ppermute | solution.py:94
  206.9 6.4 %collective-permute-start.27 = (bf16[32,3072]{1,0:T(8,128)(2,1)S(1)}, bf16[32,3072]{1,0:T(8,128)(2,1)S(1)}, u32[]{:S(2)}, u32[]{:S(2)}) collective-permute-start(bf16[32,3072]{1,0:T(8,128)(2,1)S(1)} %fusion.60), channel_id=1, source_target_pairs={{0,2},{2,4},{4,6},{6,7},{7,5},{5,3},{3,1},{1,0},{8,10},{10,12},{12... | collective-permute-start | bytes 589832 | tf_op jit(solution)/shard_map/ppermute | solution.py:94
  208.7 6.4 %collective-permute-start.31 = (bf16[32,3072]{1,0:T(8,128)(2,1)S(1)}, bf16[32,3072]{1,0:T(8,128)(2,1)S(1)}, u32[]{:S(2)}, u32[]{:S(2)}) collective-permute-start(bf16[32,3072]{1,0:T(8,128)(2,1)S(1)} %fusion.58), channel_id=1, source_target_pairs={{0,1},{2,0},{4,2},{6,4},{7,6},{5,7},{3,5},{1,3},{8,9},{10,8},{12,1... | collective-permute-start | bytes 589832 | tf_op jit(solution)/shard_map/ppermute | solution.py:94
  213.3 5.7 %collective-permute-start.28 = (bf16[32,3072]{1,0:T(8,128)(2,1)S(1)}, bf16[32,3072]{1,0:T(8,128)(2,1)S(1)}, u32[]{:S(2)}, u32[]{:S(2)}) collective-permute-start(bf16[32,3072]{1,0:T(8,128)(2,1)S(1)} %fusion.39), channel_id=1, source_target_pairs={{0,2},{2,4},{4,6},{6,7},{7,5},{5,3},{3,1},{1,0},{8,10},{10,12},{12... | collective-permute-start | bytes 589832 | tf_op jit(solution)/shard_map/ppermute | solution.py:94
  219.2 6.6 %collective-permute-start.32 = (bf16[32,3072]{1,0:T(8,128)(2,1)S(1)}, bf16[32,3072]{1,0:T(8,128)(2,1)S(1)}, u32[]{:S(2)}, u32[]{:S(2)}) collective-permute-start(bf16[32,3072]{1,0:T(8,128)(2,1)S(1)} %get-tuple-element.114), channel_id=1, source_target_pairs={{0,1},{2,0},{4,2},{6,4},{7,6},{5,7},{3,5},{1,3},{8,9},{10,8},{12,1... | collective-permute-start | bytes 589832 | tf_op jit(solution)/shard_map/ppermute | solution.py:94
  220.8 6.8 %collective-permute-start.29 = (bf16[32,3072]{1,0:T(8,128)(2,1)S(1)}, bf16[32,3072]{1,0:T(8,128)(2,1)S(1)}, u32[]{:S(2)}, u32[]{:S(2)}) collective-permute-start(bf16[32,3072]{1,0:T(8,128)(2,1)S(1)} %get-tuple-element.113), channel_id=1, source_target_pairs={{0,2},{2,4},{4,6},{6,7},{7,5},{5,3},{3,1},{1,0},{8,10},{10,12},{12... | collective-permute-start | bytes 589832 | tf_op jit(solution)/shard_map/ppermute | solution.py:94
  225.9 7.2 %collective-permute-start.33 = (bf16[32,3072]{1,0:T(8,128)(2,1)S(1)}, bf16[32,3072]{1,0:T(8,128)(2,1)S(1)}, u32[]{:S(2)}, u32[]{:S(2)}) collective-permute-start(bf16[32,3072]{1,0:T(8,128)(2,1)S(1)} %fusion.38), channel_id=1, source_target_pairs={{0,1},{2,0},{4,2},{6,4},{7,6},{5,7},{3,5},{1,3},{8,9},{10,8},{12,1... | collective-permute-start | bytes 589832 | tf_op jit(solution)/shard_map/ppermute | solution.py:94
  233.8 6.5 %collective-permute-start.34 = (bf16[32,3072]{1,0:T(8,128)(2,1)S(1)}, bf16[32,3072]{1,0:T(8,128)(2,1)S(1)}, u32[]{:S(2)}, u32[]{:S(2)}) collective-permute-start(bf16[32,3072]{1,0:T(8,128)(2,1)S(1)} %get-tuple-element.96), channel_id=1, source_target_pairs={{0,1},{2,0},{4,2},{6,4},{7,6},{5,7},{3,5},{1,3},{8,9},{10,8},{12,1... | collective-permute-start | bytes 589832 | tf_op jit(solution)/shard_map/ppermute | solution.py:64
  235.6 6.4 %collective-permute-start.37 = (bf16[32,3072]{1,0:T(8,128)(2,1)S(1)}, bf16[32,3072]{1,0:T(8,128)(2,1)S(1)}, u32[]{:S(2)}, u32[]{:S(2)}) collective-permute-start(bf16[32,3072]{1,0:T(8,128)(2,1)S(1)} %get-tuple-element.96), channel_id=1, source_target_pairs={{0,2},{2,4},{4,6},{6,7},{7,5},{5,3},{3,1},{1,0},{8,10},{10,12},{12... | collective-permute-start | bytes 589832 | tf_op jit(solution)/shard_map/ppermute | solution.py:61
  240.3 5.7 %collective-permute-start.35 = (bf16[32,3072]{1,0:T(8,128)(2,1)S(1)}, bf16[32,3072]{1,0:T(8,128)(2,1)S(1)}, u32[]{:S(2)}, u32[]{:S(2)}) collective-permute-start(bf16[32,3072]{1,0:T(8,128)(2,1)S(1)} %collective-permute-done.34), channel_id=1, source_target_pairs={{0,1},{2,0},{4,2},{6,4},{7,6},{5,7},{3,5},{1,3},{8,9},{10,8},{12,1... | collective-permute-start | bytes 589832 | tf_op jit(solution)/shard_map/ppermute | solution.py:64
  242.0 5.7 %collective-permute-start.38 = (bf16[32,3072]{1,0:T(8,128)(2,1)S(1)}, bf16[32,3072]{1,0:T(8,128)(2,1)S(1)}, u32[]{:S(2)}, u32[]{:S(2)}) collective-permute-start(bf16[32,3072]{1,0:T(8,128)(2,1)S(1)} %collective-permute-done.37), channel_id=1, source_target_pairs={{0,2},{2,4},{4,6},{6,7},{7,5},{5,3},{3,1},{1,0},{8,10},{10,12},{12... | collective-permute-start | bytes 589832 | tf_op jit(solution)/shard_map/ppermute | solution.py:61
  246.0 5.7 %collective-permute-start.36 = (bf16[32,3072]{1,0:T(8,128)(2,1)S(1)}, bf16[32,3072]{1,0:T(8,128)(2,1)S(1)}, u32[]{:S(2)}, u32[]{:S(2)}) collective-permute-start(bf16[32,3072]{1,0:T(8,128)(2,1)S(1)} %collective-permute-done.35), channel_id=1, source_target_pairs={{0,1},{2,0},{4,2},{6,4},{7,6},{5,7},{3,5},{1,3},{8,9},{10,8},{12,1... | collective-permute-start | bytes 589832 | tf_op jit(solution)/shard_map/ppermute | solution.py:64
  247.7 5.7 %collective-permute-start.39 = (bf16[32,3072]{1,0:T(8,128)(2,1)S(1)}, bf16[32,3072]{1,0:T(8,128)(2,1)S(1)}, u32[]{:S(2)}, u32[]{:S(2)}) collective-permute-start(bf16[32,3072]{1,0:T(8,128)(2,1)S(1)} %collective-permute-done.38), channel_id=1, source_target_pairs={{0,2},{2,4},{4,6},{6,7},{7,5},{5,3},{3,1},{1,0},{8,10},{10,12},{12... | collective-permute-start | bytes 589832 | tf_op jit(solution)/shard_map/ppermute | solution.py:61
  251.7 4.7 %collective-permute-start.41 = (bf16[16,3072]{1,0:T(8,128)(2,1)S(1)}, bf16[16,3072]{1,0:T(8,128)(2,1)S(1)}, u32[]{:S(2)}, u32[]{:S(2)}) collective-permute-start(bf16[16,3072]{1,0:T(8,128)(2,1)S(1)} %slice.381), channel_id=1, source_target_pairs={{0,1},{2,0},{4,2},{6,4},{7,6},{5,7},{3,5},{1,3},{8,9},{10,8},{12,1... | collective-permute-start | bytes 294920 | tf_op jit(solution)/shard_map/ppermute | solution.py:58
  253.4 4.9 %collective-permute-start.40 = (bf16[16,3072]{1,0:T(8,128)(2,1)S(1)}, bf16[16,3072]{1,0:T(8,128)(2,1)S(1)}, u32[]{:S(2)}, u32[]{:S(2)}) collective-permute-start(bf16[16,3072]{1,0:T(8,128)(2,1)S(1)} %slice.380), channel_id=1, source_target_pairs={{0,2},{2,4},{4,6},{6,7},{7,5},{5,3},{3,1},{1,0},{8,10},{10,12},{12... | collective-permute-start | bytes 294920 | tf_op jit(solution)/shard_map/ppermute | solution.py:57
  263.5 1.7 copy-start.4
  266.9 2.9 collective-permute-start.42
  268.2 2.2 collective-permute-start.43
  275.7 4.7 %collective-permute-start.44 = (bf16[16,3072]{1,0:T(8,128)(2,1)S(1)}, bf16[16,3072]{1,0:T(8,128)(2,1)S(1)}, u32[]{:S(2)}, u32[]{:S(2)}) collective-permute-start(bf16[16,3072]{1,0:T(8,128)(2,1)S(1)} %get-tuple-element.107), channel_id=1, source_target_pairs={{0,2},{2,4},{4,6},{6,7},{7,5},{5,3},{3,1},{1,0},{8,10},{10,12},{12... | collective-permute-start | bytes 294920 | tf_op jit(solution)/shard_map/ppermute | solution.py:94
  276.2 4.8 %collective-permute-start.48 = (bf16[16,3072]{1,0:T(8,128)(2,1)S(1)}, bf16[16,3072]{1,0:T(8,128)(2,1)S(1)}, u32[]{:S(2)}, u32[]{:S(2)}) collective-permute-start(bf16[16,3072]{1,0:T(8,128)(2,1)S(1)} %get-tuple-element.108), channel_id=1, source_target_pairs={{0,1},{2,0},{4,2},{6,4},{7,6},{5,7},{3,5},{1,3},{8,9},{10,8},{12,1... | collective-permute-start | bytes 294920 | tf_op jit(solution)/shard_map/ppermute | solution.py:94
  280.4 7.7 %collective-permute-start.45 = (bf16[32,3072]{1,0:T(8,128)(2,1)S(1)}, bf16[32,3072]{1,0:T(8,128)(2,1)S(1)}, u32[]{:S(2)}, u32[]{:S(2)}) collective-permute-start(bf16[32,3072]{1,0:T(8,128)(2,1)S(1)} %fusion.56), channel_id=1, source_target_pairs={{0,2},{2,4},{4,6},{6,7},{7,5},{5,3},{3,1},{1,0},{8,10},{10,12},{12... | collective-permute-start | bytes 589832 | tf_op jit(solution)/shard_map/ppermute | solution.py:94
  281.0 7.8 %collective-permute-start.49 = (bf16[32,3072]{1,0:T(8,128)(2,1)S(1)}, bf16[32,3072]{1,0:T(8,128)(2,1)S(1)}, u32[]{:S(2)}, u32[]{:S(2)}) collective-permute-start(bf16[32,3072]{1,0:T(8,128)(2,1)S(1)} %fusion.54), channel_id=1, source_target_pairs={{0,1},{2,0},{4,2},{6,4},{7,6},{5,7},{3,5},{1,3},{8,9},{10,8},{12,1... | collective-permute-start | bytes 589832 | tf_op jit(solution)/shard_map/ppermute | solution.py:94
  288.1 7.1 %collective-permute-start.46 = (bf16[32,3072]{1,0:T(8,128)(2,1)S(1)}, bf16[32,3072]{1,0:T(8,128)(2,1)S(1)}, u32[]{:S(2)}, u32[]{:S(2)}) collective-permute-start(bf16[32,3072]{1,0:T(8,128)(2,1)S(1)} %fusion.32), channel_id=1, source_target_pairs={{0,2},{2,4},{4,6},{6,7},{7,5},{5,3},{3,1},{1,0},{8,10},{10,12},{12... | collective-permute-start | bytes 589832 | tf_op jit(solution)/shard_map/ppermute | solution.py:94
  295.3 6.3 %collective-permute-start.50 = (bf16[32,3072]{1,0:T(8,128)(2,1)S(1)}, bf16[32,3072]{1,0:T(8,128)(2,1)S(1)}, u32[]{:S(2)}, u32[]{:S(2)}) collective-permute-start(bf16[32,3072]{1,0:T(8,128)(2,1)S(1)} %get-tuple-element.106), channel_id=1, source_target_pairs={{0,1},{2,0},{4,2},{6,4},{7,6},{5,7},{3,5},{1,3},{8,9},{10,8},{12,1... | collective-permute-start | bytes 589832 | tf_op jit(solution)/shard_map/ppermute | solution.py:94
  296.9 6.3 %collective-permute-start.47 = (bf16[32,3072]{1,0:T(8,128)(2,1)S(1)}, bf16[32,3072]{1,0:T(8,128)(2,1)S(1)}, u32[]{:S(2)}, u32[]{:S(2)}) collective-permute-start(bf16[32,3072]{1,0:T(8,128)(2,1)S(1)} %get-tuple-element.105), channel_id=1, source_target_pairs={{0,2},{2,4},{4,6},{6,7},{7,5},{5,3},{3,1},{1,0},{8,10},{10,12},{12... | collective-permute-start | bytes 589832 | tf_op jit(solution)/shard_map/ppermute | solution.py:94
  301.6 5.7 %collective-permute-start.51 = (bf16[32,3072]{1,0:T(8,128)(2,1)S(1)}, bf16[32,3072]{1,0:T(8,128)(2,1)S(1)}, u32[]{:S(2)}, u32[]{:S(2)}) collective-permute-start(bf16[32,3072]{1,0:T(8,128)(2,1)S(1)} %fusion.31), channel_id=1, source_target_pairs={{0,1},{2,0},{4,2},{6,4},{7,6},{5,7},{3,5},{1,3},{8,9},{10,8},{12,1... | collective-permute-start | bytes 589832 | tf_op jit(solution)/shard_map/ppermute | solution.py:94

commit v7 on v5

--- a/solution.py
+++ b/solution.py
@@ -67,6 +67,12 @@
     return jnp.take(stacked, tables[1], axis=0, mode="clip").reshape((length * rows,) + value.shape[1:])
 
 
+def ring_ordered(rows_in, axis, tables):
+    length = lax.axis_size(axis)
+    blocks = rows_in.reshape((length, rows_in.shape[0] // length) + rows_in.shape[1:])
+    return jnp.take(blocks, tables[0], axis=0, mode="clip").reshape(rows_in.shape)
+
+
 def ring_scatter_sum(value, axis, tables):
     length = lax.axis_size(axis)
     forward, backward = ring_pairs(length)
@@ -75,8 +81,7 @@
     rows = value.shape[0] // length
     split = behind < ahead and rows % 2 == 0
     half = rows // 2
-    blocks = value.reshape((length, rows) + value.shape[1:])
-    by_offset = jnp.take(blocks, tables[0], axis=0, mode="clip")
+    by_offset = value.reshape((length, rows) + value.shape[1:])
 
     def own(offset):
         return by_offset[offset % length].astype(jnp.float32)
@@ -152,7 +157,7 @@
             for tap_idx in range(taps)
         ]
     )
-    chunk = 1024 if width % 1024 == 0 else width
+    chunk = width
     return pl.pallas_call(
         conv_gate_kernel,
         out_shape=jax.ShapeDtypeStruct((all_rows, own_width), jnp.bfloat16),
@@ -173,6 +178,7 @@
 
 
 def conv_share(gated, weight, tok_rows, tables):
+    gated = ring_ordered(gated, "head", tables)
 
     def term(start, count):
         return rounded_term(gated, weight)
@@ -183,6 +189,7 @@
 
 
 def attention_portion_for(heads_out, out_block, tok_rows, tables):
+    heads_out = ring_ordered(heads_out, "head", tables)
 
     def term(start, count):
         return rounded_term(heads_out, out_block)

time: 279 us -> 268 us (0.961)
  Pallas kernels: 25 us -> 20.2 us
  matrix products: 11.7 us -> 8.01 us
    pallas_call x2, Pallas kernels: 25 us -> 20.2 us  [convolution_gate(): pl.pallas_call(conv_gate_kernel, out_shape=jax.ShapeDtypeStruct((all_rows...]
    dot_general x3, matrix products: 9.85 us -> 5.88 us  [rounded_term(): term = jnp.dot(left, right, preferred_element_type=jnp.float32)]
where the time goes in v7:
time: 268 us; the launch traced here: 267 us
  waiting for transfers between devices  105 us (39%)
  starting transfers between devices  57.7 us (22%)
  local copies, waits for them, and re-layouts  48.5 us (18%)
  other arithmetic  23.2 us (9%)
  Pallas kernels  20.2 us (8%)
  matrix products  8.01 us (3%)
  between operations  4.35 us (2%)
    ppermute x24, waiting for transfers between devices, chain(): passed = lax.ppermute(part.astype(value.dtype), axis, pairs)  67.1 us
    unnamed x27, local copies, waits for them, and re-layouts  32.8 us
    ppermute x24, starting transfers between devices, chain(): passed = lax.ppermute(part.astype(value.dtype), axis, pairs)  26.1 us
    pallas_call x2, Pallas kernels, convolution_gate(): pl.pallas_call(conv_gate_kernel, out_shape=jax.ShapeDtypeStruct((all_rows...  20.2 us
    ppermute x9, waiting for transfers between devices, ring_gather(): bwd = lax.ppermute(bwd, axis, backward)  18.8 us
    ppermute x9, starting transfers between devices, ring_gather(): fwd = lax.ppermute(fwd, axis, forward)  13.5 us
    another operation x4, other arithmetic, convolution_gate(): jnp.stack([lax.dynamic_slice_in_dim(padded, border_rows - tap_idx * dilat...  9.07 us
    ppermute x9, waiting for transfers between devices, ring_gather(): fwd = lax.ppermute(fwd, axis, forward)  6.59 us
  transfers between devices with their start and end apart: 52, of which 34 were waited for; matrix products, arithmetic and copies ran while one was open for 12% of the time, Pallas kernels for 0%

profile of v7, /device:TPU:0, one launch (start us, length us, event | category | flops | bytes accessed | tf_op | source)
XLA Modules:
  0.0 267.5 jit_solution(6639512333378844624)
XLA Ops:
  0.0 3.0 %collective-permute-start.3 = (bf16[32,3072]{1,0:T(8,128)(2,1)}, bf16[32,3072]{1,0:T(8,128)(2,1)S(1)}, u32[]{:S(2)}, u32[]{:S(2)}) collective-permute-start(bf16[32,3072]{1,0:T(8,128)(2,1)} %param.22), channel_id=1, source_target_pairs={{0,2},{2,4},{4,6},{6,7},{7,5},{5,3},{3,1},{1,0},{8,10},{10,12},{12... | collective-permute-start | bytes 589832 | tf_op jit(solution)/shard_map/ppermute | solution.py:61
  6.3 1.6 bitcast_dynamic-update-slice_fusion.20
  8.9 19.6 %copy.11 = bf16[2,3,3072,2,384]{4,2,3,1,0:T(8,128)(2,1)} copy(bf16[2,3,3072,2,384]{4,3,2,1,0:T(2,128)(2,1)} %param.25) | data formatting | bytes 56623104 | tf_op args[3]
  29.2 2.1 collective-permute-start.4
  32.0 3.6 %collective-permute-done.4 = bf16[32,3072]{1,0:T(8,128)(2,1)S(1)} collective-permute-done((bf16[32,3072]{1,0:T(8,128)(2,1)S(1)}, bf16[32,3072]{1,0:T(8,128)(2,1)S(1)}, u32[]{:S(2)}, u32[]{:S(2)}) %collective-permute-start.4) | collective-permute-done | bytes 196640 | tf_op jit(solution)/shard_map/ppermute | solution.py:61
  35.6 1.7 collective-permute-start.5
  38.4 2.9 %collective-permute-done.5 = bf16[32,3072]{1,0:T(8,128)(2,1)S(1)} collective-permute-done((bf16[32,3072]{1,0:T(8,128)(2,1)S(1)}, bf16[32,3072]{1,0:T(8,128)(2,1)S(1)}, u32[]{:S(2)}, u32[]{:S(2)}) %collective-permute-start.5) | collective-permute-done | bytes 196640 | tf_op jit(solution)/shard_map/ppermute | solution.py:61
  41.3 1.9 collective-permute-start.6
  44.2 1.8 collective-permute-done.6
  46.0 1.9 collective-permute-done.7
  50.6 2.1 gather_fusion
  53.1 2.0 convert_element_type.455
  59.1 2.1 fusion.27
  61.2 2.4 pad_maximum_fusion.slab_ref
  63.6 10.1 %shard_map.82 = bf16[256,384]{1,0:T(8,128)(2,1)} custom-call(bf16[3,256,3072]{2,1,0:T(8,128)(2,1)} %pad_maximum_fusion.slab_ref, bf16[2,3,2,3072,384]{4,3,2,1,0:T(8,128)(2,1)} %bitcast.146), custom_call_target="tpu_custom_call" | custom-call | flops 3623878656 | bytes 19070976 | tf_op jit(solution)/shard_map/pallas_call | solution.py:161
  73.7 1.5 gather_fusion.1
  75.2 2.6 convolution_convert_fusion.2
  77.9 1.6 collective-permute-start.9
  80.1 2.9 %collective-permute-done.9 = bf16[16,3072]{1,0:T(8,128)(2,1)S(1)} collective-permute-done((bf16[16,3072]{1,0:T(8,128)(2,1)S(1)}, bf16[16,3072]{1,0:T(8,128)(2,1)S(1)}, u32[]{:S(2)}, u32[]{:S(2)}) %collective-permute-start.9) | collective-permute-done | bytes 98336 | tf_op jit(solution)/shard_map/ppermute | solution.py:99
  83.1 1.6 collective-permute-start.10
  85.3 4.2 %collective-permute-done.10 = bf16[32,3072]{1,0:T(8,128)(2,1)S(1)} collective-permute-done((bf16[32,3072]{1,0:T(8,128)(2,1)S(1)}, bf16[32,3072]{1,0:T(8,128)(2,1)S(1)}, u32[]{:S(2)}, u32[]{:S(2)}) %collective-permute-start.10) | collective-permute-done | bytes 196640 | tf_op jit(solution)/shard_map/ppermute | solution.py:99
  89.6 1.6 collective-permute-start.11
  91.2 4.1 %collective-permute-done.11 = bf16[32,3072]{1,0:T(8,128)(2,1)S(1)} collective-permute-done((bf16[32,3072]{1,0:T(8,128)(2,1)S(1)}, bf16[32,3072]{1,0:T(8,128)(2,1)S(1)}, u32[]{:S(2)}, u32[]{:S(2)}) %collective-permute-start.11) | collective-permute-done | bytes 196640 | tf_op jit(solution)/shard_map/ppermute | solution.py:99
  97.5 4.6 %collective-permute-done.15 = bf16[32,3072]{1,0:T(8,128)(2,1)S(1)} collective-permute-done((bf16[32,3072]{1,0:T(8,128)(2,1)S(1)}, bf16[32,3072]{1,0:T(8,128)(2,1)S(1)}, u32[]{:S(2)}, u32[]{:S(2)}) %collective-permute-start.15) | collective-permute-done | bytes 196640 | tf_op jit(solution)/shard_map/ppermute | solution.py:99
  102.5 6.8 %collective-permute-done.16 = bf16[32,3072]{1,0:T(8,128)(2,1)S(1)} collective-permute-done((bf16[32,3072]{1,0:T(8,128)(2,1)S(1)}, bf16[32,3072]{1,0:T(8,128)(2,1)S(1)}, u32[]{:S(2)}, u32[]{:S(2)}) %collective-permute-start.16) | collective-permute-done | bytes 196640 | tf_op jit(solution)/shard_map/ppermute | solution.py:99
  110.1 2.0 collective-permute-start.20
  114.0 2.6 collective-permute-done.17
  116.9 1.7 collective-permute-start.21
  119.3 2.9 %collective-permute-done.18 = bf16[32,3072]{1,0:T(8,128)(2,1)S(1)} collective-permute-done((bf16[32,3072]{1,0:T(8,128)(2,1)S(1)}, bf16[32,3072]{1,0:T(8,128)(2,1)S(1)}, u32[]{:S(2)}, u32[]{:S(2)}) %collective-permute-start.18) | collective-permute-done | bytes 196640 | tf_op jit(solution)/shard_map/ppermute | solution.py:64
  125.0 2.9 %collective-permute-done.19 = bf16[32,3072]{1,0:T(8,128)(2,1)S(1)} collective-permute-done((bf16[32,3072]{1,0:T(8,128)(2,1)S(1)}, bf16[32,3072]{1,0:T(8,128)(2,1)S(1)}, u32[]{:S(2)}, u32[]{:S(2)}) %collective-permute-start.19) | collective-permute-done | bytes 196640 | tf_op jit(solution)/shard_map/ppermute | solution.py:64
  128.6 1.7 collective-permute-start.23
  131.0 1.6 collective-permute-done.24
  136.2 2.1 gather_fusion.2
  138.7 2.0 convert_element_type.457
  144.7 2.1 fusion.23
  146.8 2.4 pad_maximum_fusion.1.slab_ref
  149.2 10.1 %shard_map.83 = bf16[256,384]{1,0:T(8,128)(2,1)} custom-call(bf16[3,256,3072]{2,1,0:T(8,128)(2,1)} %pad_maximum_fusion.1.slab_ref, bf16[2,3,2,3072,384]{4,3,2,1,0:T(8,128)(2,1)} %bitcast.147), custom_call_target="tpu_custom_call" | custom-call | flops 3623878656 | bytes 19070976 | tf_op jit(solution)/shard_map/pallas_call | solution.py:161
  159.3 1.5 gather_fusion.3
  160.8 2.7 convolution_convert_fusion.1
  165.7 2.9 %collective-permute-done.26 = bf16[16,3072]{1,0:T(8,128)(2,1)S(1)} collective-permute-done((bf16[16,3072]{1,0:T(8,128)(2,1)S(1)}, bf16[16,3072]{1,0:T(8,128)(2,1)S(1)}, u32[]{:S(2)}, u32[]{:S(2)}) %collective-permute-start.26) | collective-permute-done | bytes 98336 | tf_op jit(solution)/shard_map/ppermute | solution.py:99
  170.9 4.2 %collective-permute-done.27 = bf16[32,3072]{1,0:T(8,128)(2,1)S(1)} collective-permute-done((bf16[32,3072]{1,0:T(8,128)(2,1)S(1)}, bf16[32,3072]{1,0:T(8,128)(2,1)S(1)}, u32[]{:S(2)}, u32[]{:S(2)}) %collective-permute-start.27) | collective-permute-done | bytes 196640 | tf_op jit(solution)/shard_map/ppermute | solution.py:99
  176.7 4.2 %collective-permute-done.28 = bf16[32,3072]{1,0:T(8,128)(2,1)S(1)} collective-permute-done((bf16[32,3072]{1,0:T(8,128)(2,1)S(1)}, bf16[32,3072]{1,0:T(8,128)(2,1)S(1)}, u32[]{:S(2)}, u32[]{:S(2)}) %collective-permute-start.28) | collective-permute-done | bytes 196640 | tf_op jit(solution)/shard_map/ppermute | solution.py:99
  181.0 1.6 collective-permute-start.32
  183.1 4.6 %collective-permute-done.32 = bf16[32,3072]{1,0:T(8,128)(2,1)S(1)} collective-permute-done((bf16[32,3072]{1,0:T(8,128)(2,1)S(1)}, bf16[32,3072]{1,0:T(8,128)(2,1)S(1)}, u32[]{:S(2)}, u32[]{:S(2)}) %collective-permute-start.32) | collective-permute-done | bytes 196640 | tf_op jit(solution)/shard_map/ppermute | solution.py:99
  187.7 1.6 collective-permute-start.33
  189.3 5.6 %collective-permute-done.33 = bf16[32,3072]{1,0:T(8,128)(2,1)S(1)} collective-permute-done((bf16[32,3072]{1,0:T(8,128)(2,1)S(1)}, bf16[32,3072]{1,0:T(8,128)(2,1)S(1)}, u32[]{:S(2)}, u32[]{:S(2)}) %collective-permute-start.33) | collective-permute-done | bytes 196640 | tf_op jit(solution)/shard_map/ppermute | solution.py:99
  195.7 1.5 collective-permute-start.34
  197.7 4.5 %collective-permute-done.34 = bf16[32,3072]{1,0:T(8,128)(2,1)S(1)} collective-permute-done((bf16[32,3072]{1,0:T(8,128)(2,1)S(1)}, bf16[32,3072]{1,0:T(8,128)(2,1)S(1)}, u32[]{:S(2)}, u32[]{:S(2)}) %collective-permute-start.34) | collective-permute-done | bytes 196640 | tf_op jit(solution)/shard_map/ppermute | solution.py:64
  202.2 1.5 collective-permute-start.35
  204.9 2.9 %collective-permute-done.35 = bf16[32,3072]{1,0:T(8,128)(2,1)S(1)} collective-permute-done((bf16[32,3072]{1,0:T(8,128)(2,1)S(1)}, bf16[32,3072]{1,0:T(8,128)(2,1)S(1)}, u32[]{:S(2)}, u32[]{:S(2)}) %collective-permute-start.35) | collective-permute-done | bytes 196640 | tf_op jit(solution)/shard_map/ppermute | solution.py:64
  210.6 2.9 %collective-permute-done.36 = bf16[32,3072]{1,0:T(8,128)(2,1)S(1)} collective-permute-done((bf16[32,3072]{1,0:T(8,128)(2,1)S(1)}, bf16[32,3072]{1,0:T(8,128)(2,1)S(1)}, u32[]{:S(2)}, u32[]{:S(2)}) %collective-permute-start.36) | collective-permute-done | bytes 196640 | tf_op jit(solution)/shard_map/ppermute | solution.py:64
  213.5 1.6 collective-permute-start.41
  216.6 1.6 collective-permute-done.41
  218.2 1.8 collective-permute-done.40
  222.8 2.1 gather_fusion.4
  235.6 1.6 collective-permute-start.48
  237.1 2.5 collective-permute-done.44
  240.4 1.6 collective-permute-start.49
  241.9 5.5 %collective-permute-done.45 = bf16[32,3072]{1,0:T(8,128)(2,1)S(1)} collective-permute-done((bf16[32,3072]{1,0:T(8,128)(2,1)S(1)}, bf16[32,3072]{1,0:T(8,128)(2,1)S(1)}, u32[]{:S(2)}, u32[]{:S(2)}) %collective-permute-start.45) | collective-permute-done | bytes 196640 | tf_op jit(solution)/shard_map/ppermute | solution.py:99
  248.2 6.4 %collective-permute-done.46 = bf16[32,3072]{1,0:T(8,128)(2,1)S(1)} collective-permute-done((bf16[32,3072]{1,0:T(8,128)(2,1)S(1)}, bf16[32,3072]{1,0:T(8,128)(2,1)S(1)}, u32[]{:S(2)}, u32[]{:S(2)}) %collective-permute-start.46) | collective-permute-done | bytes 196640 | tf_op jit(solution)/shard_map/ppermute | solution.py:99
  254.6 1.6 collective-permute-start.50
  256.7 4.2 %collective-permute-done.50 = bf16[32,3072]{1,0:T(8,128)(2,1)S(1)} collective-permute-done((bf16[32,3072]{1,0:T(8,128)(2,1)S(1)}, bf16[32,3072]{1,0:T(8,128)(2,1)S(1)}, u32[]{:S(2)}, u32[]{:S(2)}) %collective-permute-start.50) | collective-permute-done | bytes 196640 | tf_op jit(solution)/shard_map/ppermute | solution.py:99
  260.9 1.6 collective-permute-start.51
  262.6 4.1 %collective-permute-done.51 = bf16[32,3072]{1,0:T(8,128)(2,1)S(1)} collective-permute-done((bf16[32,3072]{1,0:T(8,128)(2,1)S(1)}, bf16[32,3072]{1,0:T(8,128)(2,1)S(1)}, u32[]{:S(2)}, u32[]{:S(2)}) %collective-permute-start.51) | collective-permute-done | bytes 196640 | tf_op jit(solution)/shard_map/ppermute | solution.py:99
  (158 shorter events, 60.8 us)
Async XLA Ops:
  0.0 234.3 %copy-start = (bf16[1,128,3072]{2,1,0:T(8,128)(2,1)S(1)}, bf16[1,128,3072]{2,1,0:T(8,128)(2,1)}, u32[]{:S(2)}) copy-start(bf16[1,128,3072]{2,1,0:T(8,128)(2,1)} %param.28) | copy-start | bytes 2359300
  0.0 29.2 %collective-permute-start.3 = (bf16[32,3072]{1,0:T(8,128)(2,1)}, bf16[32,3072]{1,0:T(8,128)(2,1)S(1)}, u32[]{:S(2)}, u32[]{:S(2)}) collective-permute-start(bf16[32,3072]{1,0:T(8,128)(2,1)} %param.22), channel_id=1, source_target_pairs={{0,2},{2,4},{4,6},{6,7},{7,5},{5,3},{3,1},{1,0},{8,10},{10,12},{12... | collective-permute-start | bytes 589832 | tf_op jit(solution)/shard_map/ppermute | solution.py:61
  3.0 28.3 %collective-permute-start = (bf16[32,3072]{1,0:T(8,128)(2,1)}, bf16[32,3072]{1,0:T(8,128)(2,1)S(1)}, u32[]{:S(2)}, u32[]{:S(2)}) collective-permute-start(bf16[32,3072]{1,0:T(8,128)(2,1)} %param.22), channel_id=1, source_target_pairs={{0,1},{2,0},{4,2},{6,4},{7,6},{5,7},{3,5},{1,3},{8,9},{10,8},{12,1... | collective-permute-start | bytes 589832 | tf_op jit(solution)/shard_map/ppermute | solution.py:64
  29.2 6.4 %collective-permute-start.4 = (bf16[32,3072]{1,0:T(8,128)(2,1)S(1)}, bf16[32,3072]{1,0:T(8,128)(2,1)S(1)}, u32[]{:S(2)}, u32[]{:S(2)}) collective-permute-start(bf16[32,3072]{1,0:T(8,128)(2,1)S(1)} %collective-permute-done.3), channel_id=1, source_target_pairs={{0,2},{2,4},{4,6},{6,7},{7,5},{5,3},{3,1},{1,0},{8,10},{10,12},{12... | collective-permute-start | bytes 589832 | tf_op jit(solution)/shard_map/ppermute | solution.py:61
  31.3 6.1 %collective-permute-start.1 = (bf16[32,3072]{1,0:T(8,128)(2,1)S(1)}, bf16[32,3072]{1,0:T(8,128)(2,1)S(1)}, u32[]{:S(2)}, u32[]{:S(2)}) collective-permute-start(bf16[32,3072]{1,0:T(8,128)(2,1)S(1)} %collective-permute-done), channel_id=1, source_target_pairs={{0,1},{2,0},{4,2},{6,4},{7,6},{5,7},{3,5},{1,3},{8,9},{10,8},{12,1... | collective-permute-start | bytes 589832 | tf_op jit(solution)/shard_map/ppermute | solution.py:64
  35.6 5.7 %collective-permute-start.5 = (bf16[32,3072]{1,0:T(8,128)(2,1)S(1)}, bf16[32,3072]{1,0:T(8,128)(2,1)S(1)}, u32[]{:S(2)}, u32[]{:S(2)}) collective-permute-start(bf16[32,3072]{1,0:T(8,128)(2,1)S(1)} %collective-permute-done.4), channel_id=1, source_target_pairs={{0,2},{2,4},{4,6},{6,7},{7,5},{5,3},{3,1},{1,0},{8,10},{10,12},{12... | collective-permute-start | bytes 589832 | tf_op jit(solution)/shard_map/ppermute | solution.py:61
  37.4 5.8 %collective-permute-start.2 = (bf16[32,3072]{1,0:T(8,128)(2,1)S(1)}, bf16[32,3072]{1,0:T(8,128)(2,1)S(1)}, u32[]{:S(2)}, u32[]{:S(2)}) collective-permute-start(bf16[32,3072]{1,0:T(8,128)(2,1)S(1)} %collective-permute-done.1), channel_id=1, source_target_pairs={{0,1},{2,0},{4,2},{6,4},{7,6},{5,7},{3,5},{1,3},{8,9},{10,8},{12,1... | collective-permute-start | bytes 589832 | tf_op jit(solution)/shard_map/ppermute | solution.py:64
  41.3 4.7 %collective-permute-start.6 = (bf16[16,3072]{1,0:T(8,128)(2,1)S(1)}, bf16[16,3072]{1,0:T(8,128)(2,1)S(1)}, u32[]{:S(2)}, u32[]{:S(2)}) collective-permute-start(bf16[16,3072]{1,0:T(8,128)(2,1)S(1)} %slice.364), channel_id=1, source_target_pairs={{0,2},{2,4},{4,6},{6,7},{7,5},{5,3},{3,1},{1,0},{8,10},{10,12},{12... | collective-permute-start | bytes 294920 | tf_op jit(solution)/shard_map/ppermute | solution.py:57
  43.2 4.7 %collective-permute-start.7 = (bf16[16,3072]{1,0:T(8,128)(2,1)S(1)}, bf16[16,3072]{1,0:T(8,128)(2,1)S(1)}, u32[]{:S(2)}, u32[]{:S(2)}) collective-permute-start(bf16[16,3072]{1,0:T(8,128)(2,1)S(1)} %slice.365), channel_id=1, source_target_pairs={{0,1},{2,0},{4,2},{6,4},{7,6},{5,7},{3,5},{1,3},{8,9},{10,8},{12,1... | collective-permute-start | bytes 294920 | tf_op jit(solution)/shard_map/ppermute | solution.py:58
  55.2 2.1 copy-start.1
  55.8 3.3 %collective-permute-start.8 = (bf16[128,3072]{1,0:T(8,128)(2,1)S(1)}, bf16[128,3072]{1,0:T(8,128)(2,1)S(1)}, u32[]{:S(2)}, u32[]{:S(2)}) collective-permute-start(bf16[128,3072]{1,0:T(8,128)(2,1)S(1)} %slice.366), channel_id=1, source_target_pairs={{0,8},{1,9},{2,10},{3,11},{4,12},{5,13},{6,14},{7,15},{16,24},{17,... | collective-permute-start | bytes 2359304 | tf_op jit(solution)/shard_map/ppermute | solution.py:14
  77.9 5.1 %collective-permute-start.9 = (bf16[16,3072]{1,0:T(8,128)(2,1)S(1)}, bf16[16,3072]{1,0:T(8,128)(2,1)S(1)}, u32[]{:S(2)}, u32[]{:S(2)}) collective-permute-start(bf16[16,3072]{1,0:T(8,128)(2,1)S(1)} %get-tuple-element.119), channel_id=1, source_target_pairs={{0,2},{2,4},{4,6},{6,7},{7,5},{5,3},{3,1},{1,0},{8,10},{10,12},{12... | collective-permute-start | bytes 294920 | tf_op jit(solution)/shard_map/ppermute | solution.py:99
  79.6 5.1 %collective-permute-start.13 = (bf16[16,3072]{1,0:T(8,128)(2,1)S(1)}, bf16[16,3072]{1,0:T(8,128)(2,1)S(1)}, u32[]{:S(2)}, u32[]{:S(2)}) collective-permute-start(bf16[16,3072]{1,0:T(8,128)(2,1)S(1)} %get-tuple-element.120), channel_id=1, source_target_pairs={{0,1},{2,0},{4,2},{6,4},{7,6},{5,7},{3,5},{1,3},{8,9},{10,8},{12,1... | collective-permute-start | bytes 294920 | tf_op jit(solution)/shard_map/ppermute | solution.py:99
  83.1 6.4 %collective-permute-start.10 = (bf16[32,3072]{1,0:T(8,128)(2,1)S(1)}, bf16[32,3072]{1,0:T(8,128)(2,1)S(1)}, u32[]{:S(2)}, u32[]{:S(2)}) collective-permute-start(bf16[32,3072]{1,0:T(8,128)(2,1)S(1)} %convert_element_type.374), channel_id=1, source_target_pairs={{0,2},{2,4},{4,6},{6,7},{7,5},{5,3},{3,1},{1,0},{8,10},{10,12},{12... | collective-permute-start | bytes 589832 | tf_op jit(solution)/shard_map/ppermute | solution.py:99
  84.8 24.5 %copy-start.3 = (bf16[32,3072]{1,0:T(8,128)(2,1)S(1)}, bf16[32,3072]{1,0:T(8,128)(2,1)}, u32[]{:S(2)}) copy-start(bf16[32,3072]{1,0:T(8,128)(2,1)} %param.22) | copy-start | bytes 589828
  84.8 6.4 %collective-permute-start.14 = (bf16[32,3072]{1,0:T(8,128)(2,1)S(1)}, bf16[32,3072]{1,0:T(8,128)(2,1)S(1)}, u32[]{:S(2)}, u32[]{:S(2)}) collective-permute-start(bf16[32,3072]{1,0:T(8,128)(2,1)S(1)} %convert_element_type.384), channel_id=1, source_target_pairs={{0,1},{2,0},{4,2},{6,4},{7,6},{5,7},{3,5},{1,3},{8,9},{10,8},{12,1... | collective-permute-start | bytes 589832 | tf_op jit(solution)/shard_map/ppermute | solution.py:99
  89.6 5.7 %collective-permute-start.11 = (bf16[32,3072]{1,0:T(8,128)(2,1)S(1)}, bf16[32,3072]{1,0:T(8,128)(2,1)S(1)}, u32[]{:S(2)}, u32[]{:S(2)}) collective-permute-start(bf16[32,3072]{1,0:T(8,128)(2,1)S(1)} %add_convert_fusion.14), channel_id=1, source_target_pairs={{0,2},{2,4},{4,6},{6,7},{7,5},{5,3},{3,1},{1,0},{8,10},{10,12},{12... | collective-permute-start | bytes 589832 | tf_op jit(solution)/shard_map/ppermute | solution.py:99
  95.4 6.6 %collective-permute-start.15 = (bf16[32,3072]{1,0:T(8,128)(2,1)S(1)}, bf16[32,3072]{1,0:T(8,128)(2,1)S(1)}, u32[]{:S(2)}, u32[]{:S(2)}) collective-permute-start(bf16[32,3072]{1,0:T(8,128)(2,1)S(1)} %get-tuple-element.118), channel_id=1, source_target_pairs={{0,1},{2,0},{4,2},{6,4},{7,6},{5,7},{3,5},{1,3},{8,9},{10,8},{12,1... | collective-permute-start | bytes 589832 | tf_op jit(solution)/shard_map/ppermute | solution.py:99
  96.1 6.5 %collective-permute-start.12 = (bf16[32,3072]{1,0:T(8,128)(2,1)S(1)}, bf16[32,3072]{1,0:T(8,128)(2,1)S(1)}, u32[]{:S(2)}, u32[]{:S(2)}) collective-permute-start(bf16[32,3072]{1,0:T(8,128)(2,1)S(1)} %get-tuple-element.117), channel_id=1, source_target_pairs={{0,2},{2,4},{4,6},{6,7},{7,5},{5,3},{3,1},{1,0},{8,10},{10,12},{12... | collective-permute-start | bytes 589832 | tf_op jit(solution)/shard_map/ppermute | solution.py:99
  102.1 7.2 %collective-permute-start.16 = (bf16[32,3072]{1,0:T(8,128)(2,1)S(1)}, bf16[32,3072]{1,0:T(8,128)(2,1)S(1)}, u32[]{:S(2)}, u32[]{:S(2)}) collective-permute-start(bf16[32,3072]{1,0:T(8,128)(2,1)S(1)} %add_convert_fusion.11), channel_id=1, source_target_pairs={{0,1},{2,0},{4,2},{6,4},{7,6},{5,7},{3,5},{1,3},{8,9},{10,8},{12,1... | collective-permute-start | bytes 589832 | tf_op jit(solution)/shard_map/ppermute | solution.py:99
  110.1 6.5 %collective-permute-start.17 = (bf16[32,3072]{1,0:T(8,128)(2,1)S(1)}, bf16[32,3072]{1,0:T(8,128)(2,1)S(1)}, u32[]{:S(2)}, u32[]{:S(2)}) collective-permute-start(bf16[32,3072]{1,0:T(8,128)(2,1)S(1)} %get-tuple-element.98), channel_id=1, source_target_pairs={{0,1},{2,0},{4,2},{6,4},{7,6},{5,7},{3,5},{1,3},{8,9},{10,8},{12,1... | collective-permute-start | bytes 589832 | tf_op jit(solution)/shard_map/ppermute | solution.py:64
  110.1 6.8 %collective-permute-start.20 = (bf16[32,3072]{1,0:T(8,128)(2,1)S(1)}, bf16[32,3072]{1,0:T(8,128)(2,1)S(1)}, u32[]{:S(2)}, u32[]{:S(2)}) collective-permute-start(bf16[32,3072]{1,0:T(8,128)(2,1)S(1)} %get-tuple-element.98), channel_id=1, source_target_pairs={{0,2},{2,4},{4,6},{6,7},{7,5},{5,3},{3,1},{1,0},{8,10},{10,12},{12... | collective-permute-start | bytes 589832 | tf_op jit(solution)/shard_map/ppermute | solution.py:61
  116.6 5.7 %collective-permute-start.18 = (bf16[32,3072]{1,0:T(8,128)(2,1)S(1)}, bf16[32,3072]{1,0:T(8,128)(2,1)S(1)}, u32[]{:S(2)}, u32[]{:S(2)}) collective-permute-start(bf16[32,3072]{1,0:T(8,128)(2,1)S(1)} %collective-permute-done.17), channel_id=1, source_target_pairs={{0,1},{2,0},{4,2},{6,4},{7,6},{5,7},{3,5},{1,3},{8,9},{10,8},{12,1... | collective-permute-start | bytes 589832 | tf_op jit(solution)/shard_map/ppermute | solution.py:64
  116.9 5.9 %collective-permute-start.21 = (bf16[32,3072]{1,0:T(8,128)(2,1)S(1)}, bf16[32,3072]{1,0:T(8,128)(2,1)S(1)}, u32[]{:S(2)}, u32[]{:S(2)}) collective-permute-start(bf16[32,3072]{1,0:T(8,128)(2,1)S(1)} %collective-permute-done.20), channel_id=1, source_target_pairs={{0,2},{2,4},{4,6},{6,7},{7,5},{5,3},{3,1},{1,0},{8,10},{10,12},{12... | collective-permute-start | bytes 589832 | tf_op jit(solution)/shard_map/ppermute | solution.py:61
  122.3 5.7 %collective-permute-start.19 = (bf16[32,3072]{1,0:T(8,128)(2,1)S(1)}, bf16[32,3072]{1,0:T(8,128)(2,1)S(1)}, u32[]{:S(2)}, u32[]{:S(2)}) collective-permute-start(bf16[32,3072]{1,0:T(8,128)(2,1)S(1)} %collective-permute-done.18), channel_id=1, source_target_pairs={{0,1},{2,0},{4,2},{6,4},{7,6},{5,7},{3,5},{1,3},{8,9},{10,8},{12,1... | collective-permute-start | bytes 589832 | tf_op jit(solution)/shard_map/ppermute | solution.py:64
  122.9 5.7 %collective-permute-start.22 = (bf16[32,3072]{1,0:T(8,128)(2,1)S(1)}, bf16[32,3072]{1,0:T(8,128)(2,1)S(1)}, u32[]{:S(2)}, u32[]{:S(2)}) collective-permute-start(bf16[32,3072]{1,0:T(8,128)(2,1)S(1)} %collective-permute-done.21), channel_id=1, source_target_pairs={{0,2},{2,4},{4,6},{6,7},{7,5},{5,3},{3,1},{1,0},{8,10},{10,12},{12... | collective-permute-start | bytes 589832 | tf_op jit(solution)/shard_map/ppermute | solution.py:61
  127.9 4.7 %collective-permute-start.24 = (bf16[16,3072]{1,0:T(8,128)(2,1)S(1)}, bf16[16,3072]{1,0:T(8,128)(2,1)S(1)}, u32[]{:S(2)}, u32[]{:S(2)}) collective-permute-start(bf16[16,3072]{1,0:T(8,128)(2,1)S(1)} %slice.379), channel_id=1, source_target_pairs={{0,1},{2,0},{4,2},{6,4},{7,6},{5,7},{3,5},{1,3},{8,9},{10,8},{12,1... | collective-permute-start | bytes 294920 | tf_op jit(solution)/shard_map/ppermute | solution.py:58
  128.6 4.8 %collective-permute-start.23 = (bf16[16,3072]{1,0:T(8,128)(2,1)S(1)}, bf16[16,3072]{1,0:T(8,128)(2,1)S(1)}, u32[]{:S(2)}, u32[]{:S(2)}) collective-permute-start(bf16[16,3072]{1,0:T(8,128)(2,1)S(1)} %slice.378), channel_id=1, source_target_pairs={{0,2},{2,4},{4,6},{6,7},{7,5},{5,3},{3,1},{1,0},{8,10},{10,12},{12... | collective-permute-start | bytes 294920 | tf_op jit(solution)/shard_map/ppermute | solution.py:57
  140.8 2.0 copy-start.2
  141.4 3.3 %collective-permute-start.25 = (bf16[128,3072]{1,0:T(8,128)(2,1)S(1)}, bf16[128,3072]{1,0:T(8,128)(2,1)S(1)}, u32[]{:S(2)}, u32[]{:S(2)}) collective-permute-start(bf16[128,3072]{1,0:T(8,128)(2,1)S(1)} %slice.380), channel_id=1, source_target_pairs={{0,8},{1,9},{2,10},{3,11},{4,12},{5,13},{6,14},{7,15},{16,24},{17,... | collective-permute-start | bytes 2359304 | tf_op jit(solution)/shard_map/ppermute | solution.py:14
  163.5 5.1 %collective-permute-start.26 = (bf16[16,3072]{1,0:T(8,128)(2,1)S(1)}, bf16[16,3072]{1,0:T(8,128)(2,1)S(1)}, u32[]{:S(2)}, u32[]{:S(2)}) collective-permute-start(bf16[16,3072]{1,0:T(8,128)(2,1)S(1)} %get-tuple-element.113), channel_id=1, source_target_pairs={{0,2},{2,4},{4,6},{6,7},{7,5},{5,3},{3,1},{1,0},{8,10},{10,12},{12... | collective-permute-start | bytes 294920 | tf_op jit(solution)/shard_map/ppermute | solution.py:99
  165.1 5.1 %collective-permute-start.30 = (bf16[16,3072]{1,0:T(8,128)(2,1)S(1)}, bf16[16,3072]{1,0:T(8,128)(2,1)S(1)}, u32[]{:S(2)}, u32[]{:S(2)}) collective-permute-start(bf16[16,3072]{1,0:T(8,128)(2,1)S(1)} %get-tuple-element.114), channel_id=1, source_target_pairs={{0,1},{2,0},{4,2},{6,4},{7,6},{5,7},{3,5},{1,3},{8,9},{10,8},{12,1... | collective-permute-start | bytes 294920 | tf_op jit(solution)/shard_map/ppermute | solution.py:99
  168.7 6.4 %collective-permute-start.27 = (bf16[32,3072]{1,0:T(8,128)(2,1)S(1)}, bf16[32,3072]{1,0:T(8,128)(2,1)S(1)}, u32[]{:S(2)}, u32[]{:S(2)}) collective-permute-start(bf16[32,3072]{1,0:T(8,128)(2,1)S(1)} %convert_element_type.405), channel_id=1, source_target_pairs={{0,2},{2,4},{4,6},{6,7},{7,5},{5,3},{3,1},{1,0},{8,10},{10,12},{12... | collective-permute-start | bytes 589832 | tf_op jit(solution)/shard_map/ppermute | solution.py:99
  170.3 6.4 %collective-permute-start.31 = (bf16[32,3072]{1,0:T(8,128)(2,1)S(1)}, bf16[32,3072]{1,0:T(8,128)(2,1)S(1)}, u32[]{:S(2)}, u32[]{:S(2)}) collective-permute-start(bf16[32,3072]{1,0:T(8,128)(2,1)S(1)} %convert_element_type.415), channel_id=1, source_target_pairs={{0,1},{2,0},{4,2},{6,4},{7,6},{5,7},{3,5},{1,3},{8,9},{10,8},{12,1... | collective-permute-start | bytes 589832 | tf_op jit(solution)/shard_map/ppermute | solution.py:99
  175.2 5.7 %collective-permute-start.28 = (bf16[32,3072]{1,0:T(8,128)(2,1)S(1)}, bf16[32,3072]{1,0:T(8,128)(2,1)S(1)}, u32[]{:S(2)}, u32[]{:S(2)}) collective-permute-start(bf16[32,3072]{1,0:T(8,128)(2,1)S(1)} %add_convert_fusion.9), channel_id=1, source_target_pairs={{0,2},{2,4},{4,6},{6,7},{7,5},{5,3},{3,1},{1,0},{8,10},{10,12},{12... | collective-permute-start | bytes 589832 | tf_op jit(solution)/shard_map/ppermute | solution.py:99
  181.0 6.6 %collective-permute-start.32 = (bf16[32,3072]{1,0:T(8,128)(2,1)S(1)}, bf16[32,3072]{1,0:T(8,128)(2,1)S(1)}, u32[]{:S(2)}, u32[]{:S(2)}) collective-permute-start(bf16[32,3072]{1,0:T(8,128)(2,1)S(1)} %get-tuple-element.112), channel_id=1, source_target_pairs={{0,1},{2,0},{4,2},{6,4},{7,6},{5,7},{3,5},{1,3},{8,9},{10,8},{12,1... | collective-permute-start | bytes 589832 | tf_op jit(solution)/shard_map/ppermute | solution.py:99
  182.6 6.7 %collective-permute-start.29 = (bf16[32,3072]{1,0:T(8,128)(2,1)S(1)}, bf16[32,3072]{1,0:T(8,128)(2,1)S(1)}, u32[]{:S(2)}, u32[]{:S(2)}) collective-permute-start(bf16[32,3072]{1,0:T(8,128)(2,1)S(1)} %get-tuple-element.111), channel_id=1, source_target_pairs={{0,2},{2,4},{4,6},{6,7},{7,5},{5,3},{3,1},{1,0},{8,10},{10,12},{12... | collective-permute-start | bytes 589832 | tf_op jit(solution)/shard_map/ppermute | solution.py:99
  187.7 7.2 %collective-permute-start.33 = (bf16[32,3072]{1,0:T(8,128)(2,1)S(1)}, bf16[32,3072]{1,0:T(8,128)(2,1)S(1)}, u32[]{:S(2)}, u32[]{:S(2)}) collective-permute-start(bf16[32,3072]{1,0:T(8,128)(2,1)S(1)} %add_convert_fusion.6), channel_id=1, source_target_pairs={{0,1},{2,0},{4,2},{6,4},{7,6},{5,7},{3,5},{1,3},{8,9},{10,8},{12,1... | collective-permute-start | bytes 589832 | tf_op jit(solution)/shard_map/ppermute | solution.py:99
  195.7 6.5 %collective-permute-start.34 = (bf16[32,3072]{1,0:T(8,128)(2,1)S(1)}, bf16[32,3072]{1,0:T(8,128)(2,1)S(1)}, u32[]{:S(2)}, u32[]{:S(2)}) collective-permute-start(bf16[32,3072]{1,0:T(8,128)(2,1)S(1)} %get-tuple-element.96), channel_id=1, source_target_pairs={{0,1},{2,0},{4,2},{6,4},{7,6},{5,7},{3,5},{1,3},{8,9},{10,8},{12,1... | collective-permute-start | bytes 589832 | tf_op jit(solution)/shard_map/ppermute | solution.py:64
  197.2 6.5 %collective-permute-start.37 = (bf16[32,3072]{1,0:T(8,128)(2,1)S(1)}, bf16[32,3072]{1,0:T(8,128)(2,1)S(1)}, u32[]{:S(2)}, u32[]{:S(2)}) collective-permute-start(bf16[32,3072]{1,0:T(8,128)(2,1)S(1)} %get-tuple-element.96), channel_id=1, source_target_pairs={{0,2},{2,4},{4,6},{6,7},{7,5},{5,3},{3,1},{1,0},{8,10},{10,12},{12... | collective-permute-start | bytes 589832 | tf_op jit(solution)/shard_map/ppermute | solution.py:61
  202.2 5.7 %collective-permute-start.35 = (bf16[32,3072]{1,0:T(8,128)(2,1)S(1)}, bf16[32,3072]{1,0:T(8,128)(2,1)S(1)}, u32[]{:S(2)}, u32[]{:S(2)}) collective-permute-start(bf16[32,3072]{1,0:T(8,128)(2,1)S(1)} %collective-permute-done.34), channel_id=1, source_target_pairs={{0,1},{2,0},{4,2},{6,4},{7,6},{5,7},{3,5},{1,3},{8,9},{10,8},{12,1... | collective-permute-start | bytes 589832 | tf_op jit(solution)/shard_map/ppermute | solution.py:64
  203.7 5.7 %collective-permute-start.38 = (bf16[32,3072]{1,0:T(8,128)(2,1)S(1)}, bf16[32,3072]{1,0:T(8,128)(2,1)S(1)}, u32[]{:S(2)}, u32[]{:S(2)}) collective-permute-start(bf16[32,3072]{1,0:T(8,128)(2,1)S(1)} %collective-permute-done.37), channel_id=1, source_target_pairs={{0,2},{2,4},{4,6},{6,7},{7,5},{5,3},{3,1},{1,0},{8,10},{10,12},{12... | collective-permute-start | bytes 589832 | tf_op jit(solution)/shard_map/ppermute | solution.py:61
  207.9 5.7 %collective-permute-start.36 = (bf16[32,3072]{1,0:T(8,128)(2,1)S(1)}, bf16[32,3072]{1,0:T(8,128)(2,1)S(1)}, u32[]{:S(2)}, u32[]{:S(2)}) collective-permute-start(bf16[32,3072]{1,0:T(8,128)(2,1)S(1)} %collective-permute-done.35), channel_id=1, source_target_pairs={{0,1},{2,0},{4,2},{6,4},{7,6},{5,7},{3,5},{1,3},{8,9},{10,8},{12,1... | collective-permute-start | bytes 589832 | tf_op jit(solution)/shard_map/ppermute | solution.py:64
  209.4 5.7 %collective-permute-start.39 = (bf16[32,3072]{1,0:T(8,128)(2,1)S(1)}, bf16[32,3072]{1,0:T(8,128)(2,1)S(1)}, u32[]{:S(2)}, u32[]{:S(2)}) collective-permute-start(bf16[32,3072]{1,0:T(8,128)(2,1)S(1)} %collective-permute-done.38), channel_id=1, source_target_pairs={{0,2},{2,4},{4,6},{6,7},{7,5},{5,3},{3,1},{1,0},{8,10},{10,12},{12... | collective-permute-start | bytes 589832 | tf_op jit(solution)/shard_map/ppermute | solution.py:61
  213.5 4.7 %collective-permute-start.41 = (bf16[16,3072]{1,0:T(8,128)(2,1)S(1)}, bf16[16,3072]{1,0:T(8,128)(2,1)S(1)}, u32[]{:S(2)}, u32[]{:S(2)}) collective-permute-start(bf16[16,3072]{1,0:T(8,128)(2,1)S(1)} %slice.393), channel_id=1, source_target_pairs={{0,1},{2,0},{4,2},{6,4},{7,6},{5,7},{3,5},{1,3},{8,9},{10,8},{12,1... | collective-permute-start | bytes 294920 | tf_op jit(solution)/shard_map/ppermute | solution.py:58
  215.1 4.9 %collective-permute-start.40 = (bf16[16,3072]{1,0:T(8,128)(2,1)S(1)}, bf16[16,3072]{1,0:T(8,128)(2,1)S(1)}, u32[]{:S(2)}, u32[]{:S(2)}) collective-permute-start(bf16[16,3072]{1,0:T(8,128)(2,1)S(1)} %slice.392), channel_id=1, source_target_pairs={{0,2},{2,4},{4,6},{6,7},{7,5},{5,3},{3,1},{1,0},{8,10},{10,12},{12... | collective-permute-start | bytes 294920 | tf_op jit(solution)/shard_map/ppermute | solution.py:57
  225.2 1.7 copy-start.4
  228.6 2.9 %collective-permute-start.42 = (bf16[256,128]{1,0:T(8,128)(2,1)S(1)}, bf16[256,128]{1,0:T(8,128)(2,1)S(1)}, u32[]{:S(2)}, u32[]{:S(2)}) collective-permute-start(bf16[256,128]{1,0:T(8,128)(2,1)S(1)} %convolution_convert_fusion.4), channel_id=1, source_target_pairs={{0,8},{1,9},{2,10},{3,11},{4,12},{5,13},{6,14},{7,15},{16,24},{17,... | collective-permute-start | bytes 196616 | tf_op jit(solution)/shard_map/ppermute | solution.py:14
  229.9 2.2 collective-permute-start.43
  234.9 4.7 %collective-permute-start.44 = (bf16[16,3072]{1,0:T(8,128)(2,1)S(1)}, bf16[16,3072]{1,0:T(8,128)(2,1)S(1)}, u32[]{:S(2)}, u32[]{:S(2)}) collective-permute-start(bf16[16,3072]{1,0:T(8,128)(2,1)S(1)} %get-tuple-element.107), channel_id=1, source_target_pairs={{0,2},{2,4},{4,6},{6,7},{7,5},{5,3},{3,1},{1,0},{8,10},{10,12},{12... | collective-permute-start | bytes 294920 | tf_op jit(solution)/shard_map/ppermute | solution.py:99
  235.6 4.8 %collective-permute-start.48 = (bf16[16,3072]{1,0:T(8,128)(2,1)S(1)}, bf16[16,3072]{1,0:T(8,128)(2,1)S(1)}, u32[]{:S(2)}, u32[]{:S(2)}) collective-permute-start(bf16[16,3072]{1,0:T(8,128)(2,1)S(1)} %get-tuple-element.108), channel_id=1, source_target_pairs={{0,1},{2,0},{4,2},{6,4},{7,6},{5,7},{3,5},{1,3},{8,9},{10,8},{12,1... | collective-permute-start | bytes 294920 | tf_op jit(solution)/shard_map/ppermute | solution.py:99
  239.7 7.7 %collective-permute-start.45 = (bf16[32,3072]{1,0:T(8,128)(2,1)S(1)}, bf16[32,3072]{1,0:T(8,128)(2,1)S(1)}, u32[]{:S(2)}, u32[]{:S(2)}) collective-permute-start(bf16[32,3072]{1,0:T(8,128)(2,1)S(1)} %convert_element_type.438), channel_id=1, source_target_pairs={{0,2},{2,4},{4,6},{6,7},{7,5},{5,3},{3,1},{1,0},{8,10},{10,12},{12... | collective-permute-start | bytes 589832 | tf_op jit(solution)/shard_map/ppermute | solution.py:99
  240.4 7.8 %collective-permute-start.49 = (bf16[32,3072]{1,0:T(8,128)(2,1)S(1)}, bf16[32,3072]{1,0:T(8,128)(2,1)S(1)}, u32[]{:S(2)}, u32[]{:S(2)}) collective-permute-start(bf16[32,3072]{1,0:T(8,128)(2,1)S(1)} %convert_element_type.448), channel_id=1, source_target_pairs={{0,1},{2,0},{4,2},{6,4},{7,6},{5,7},{3,5},{1,3},{8,9},{10,8},{12,1... | collective-permute-start | bytes 589832 | tf_op jit(solution)/shard_map/ppermute | solution.py:99
  247.4 7.1 %collective-permute-start.46 = (bf16[32,3072]{1,0:T(8,128)(2,1)S(1)}, bf16[32,3072]{1,0:T(8,128)(2,1)S(1)}, u32[]{:S(2)}, u32[]{:S(2)}) collective-permute-start(bf16[32,3072]{1,0:T(8,128)(2,1)S(1)} %add_convert_fusion.4), channel_id=1, source_target_pairs={{0,2},{2,4},{4,6},{6,7},{7,5},{5,3},{3,1},{1,0},{8,10},{10,12},{12... | collective-permute-start | bytes 589832 | tf_op jit(solution)/shard_map/ppermute | solution.py:99
  254.6 6.3 %collective-permute-start.50 = (bf16[32,3072]{1,0:T(8,128)(2,1)S(1)}, bf16[32,3072]{1,0:T(8,128)(2,1)S(1)}, u32[]{:S(2)}, u32[]{:S(2)}) collective-permute-start(bf16[32,3072]{1,0:T(8,128)(2,1)S(1)} %get-tuple-element.106), channel_id=1, source_target_pairs={{0,1},{2,0},{4,2},{6,4},{7,6},{5,7},{3,5},{1,3},{8,9},{10,8},{12,1... | collective-permute-start | bytes 589832 | tf_op jit(solution)/shard_map/ppermute | solution.py:99
  256.3 6.3 %collective-permute-start.47 = (bf16[32,3072]{1,0:T(8,128)(2,1)S(1)}, bf16[32,3072]{1,0:T(8,128)(2,1)S(1)}, u32[]{:S(2)}, u32[]{:S(2)}) collective-permute-start(bf16[32,3072]{1,0:T(8,128)(2,1)S(1)} %get-tuple-element.105), channel_id=1, source_target_pairs={{0,2},{2,4},{4,6},{6,7},{7,5},{5,3},{3,1},{1,0},{8,10},{10,12},{12... | collective-permute-start | bytes 589832 | tf_op jit(solution)/shard_map/ppermute | solution.py:99
  260.9 5.7 %collective-permute-start.51 = (bf16[32,3072]{1,0:T(8,128)(2,1)S(1)}, bf16[32,3072]{1,0:T(8,128)(2,1)S(1)}, u32[]{:S(2)}, u32[]{:S(2)}) collective-permute-start(bf16[32,3072]{1,0:T(8,128)(2,1)S(1)} %add_convert_fusion.1), channel_id=1, source_target_pairs={{0,1},{2,0},{4,2},{6,4},{7,6},{5,7},{3,5},{1,3},{8,9},{10,8},{12,1... | collective-permute-start | bytes 589832 | tf_op jit(solution)/shard_map/ppermute | solution.py:99

commit v8 on v7

--- a/solution.py
+++ b/solution.py
@@ -125,7 +125,7 @@
     return lax.optimization_barrier(term.astype(jnp.bfloat16)).astype(jnp.float32)
 
 
-def conv_gate_kernel(slab_ref, weight_ref, out_ref, filt_acc, gate_acc):
+def conv_gate_kernel(slab_ref, gain_ref, weight_ref, out_ref, filt_acc, gate_acc):
     tap = pl.program_id(0)
     chunk = pl.program_id(1)
 
@@ -134,7 +134,9 @@
         filt_acc[...] = jnp.zeros_like(filt_acc)
         gate_acc[...] = jnp.zeros_like(gate_acc)
 
-    rows = slab_ref[...]
+    wide = slab_ref[...].astype(jnp.float32)
+    scale = lax.rsqrt(jnp.mean(wide * wide, axis=-1, keepdims=True) + 1e-06)
+    rows = (wide * scale * gain_ref[...]).astype(jnp.bfloat16)
     filt_acc[...] += jnp.dot(rows, weight_ref[0], preferred_element_type=jnp.float32)
     gate_acc[...] += jnp.dot(rows, weight_ref[1], preferred_element_type=jnp.float32)
 
@@ -143,7 +145,8 @@
         out_ref[...] = (jnp.tanh(filt_acc[...]) * jax.nn.sigmoid(gate_acc[...])).astype(out_ref.dtype)
 
 
-def convolution_gate(hidden, conv_by_half, layer_idx, dilation_factor):
+def convolution_gate(state, gain, conv_by_half, layer_idx, dilation_factor):
+    hidden = state
     all_rows = hidden.shape[0]
     width = hidden.shape[1]
     taps = conv_by_half.shape[1]
@@ -164,6 +167,7 @@
         grid=(taps, width // chunk),
         in_specs=[
             pl.BlockSpec((None, all_rows, chunk), lambda t, k: (t, 0, k)),
+            pl.BlockSpec((1, width), lambda t, k: (0, 0)),
             pl.BlockSpec((None, None, 2, chunk, own_width), lambda t, k: (layer_idx, t, 0, k, 0)),
         ],
         out_specs=pl.BlockSpec((all_rows, own_width), lambda t, k: (0, 0)),
@@ -174,7 +178,7 @@
             transcendentals=2 * all_rows * own_width,
             bytes_accessed=2 * taps * (all_rows * width + 2 * width * own_width + all_rows * own_width // taps),
         ),
-    )(slabs, conv_by_half)
+    )(slabs, gain.reshape(1, width), conv_by_half)
 
 
 def conv_share(gated, weight, tok_rows, tables):
@@ -242,7 +246,7 @@
     conv_by_half = jnp.transpose(w_conv, (0, 1, 3, 2, 4))
     for layer_idx in range(layers):
         gated = convolution_gate(
-            normed(state, gains[layer_idx]), conv_by_half, layer_idx, dilations[layer_idx]
+            state, gains[layer_idx], conv_by_half, layer_idx, dilations[layer_idx]
         )
         summed = conv_share(gated, w_mix[layer_idx], tok_rows, tables)
         share = (share.astype(jnp.float32) + summed).astype(jnp.bfloat16)

time: 268 us -> 264 us (0.985)
  other arithmetic: 23.2 us -> 17.4 us
    convert_element_type x2 -> x0, other arithmetic: 4.06 us -> none  [normed(): wide = values.astype(jnp.float32)]
    unnamed x27 -> x25, local copies, waits for them, and re-layouts: 32.8 us -> 32.8 us
  transfers between devices with their start and end apart: 52 -> 52, of which waited for: 34 -> 33; matrix products, arithmetic and copies ran while one was open for 12% -> 12% of each run, Pallas kernels for 0% -> 0%
where the time goes in v8:
time: 264 us; the launch traced here: 263 us
  waiting for transfers between devices  105 us (40%)
  starting transfers between devices  58.2 us (22%)
  local copies, waits for them, and re-layouts  48.1 us (18%)
  Pallas kernels  21.7 us (8%)
  other arithmetic  17.4 us (7%)
  matrix products  7.99 us (3%)
  between operations  4.26 us (2%)
    ppermute x24, waiting for transfers between devices, chain(): passed = lax.ppermute(part.astype(value.dtype), axis, pairs)  66.8 us
    unnamed x25, local copies, waits for them, and re-layouts  32.8 us
    ppermute x24, starting transfers between devices, chain(): passed = lax.ppermute(part.astype(value.dtype), axis, pairs)  26.4 us
    pallas_call x2, Pallas kernels, convolution_gate(): pl.pallas_call(conv_gate_kernel, out_shape=jax.ShapeDtypeStruct((all_rows...  21.7 us
    ppermute x9, waiting for transfers between devices, ring_gather(): bwd = lax.ppermute(bwd, axis, backward)  20.7 us
    ppermute x9, starting transfers between devices, ring_gather(): fwd = lax.ppermute(fwd, axis, forward)  13.2 us
    another operation x4, other arithmetic, convolution_gate(): jnp.stack([lax.dynamic_slice_in_dim(padded, border_rows - tap_idx * dilat...  9.98 us
    ppermute x9, waiting for transfers between devices, ring_gather(): fwd = lax.ppermute(fwd, axis, forward)  6.59 us
  transfers between devices with their start and end apart: 52, of which 33 were waited for; matrix products, arithmetic and copies ran while one was open for 12% of the time, Pallas kernels for 0%

profile of v8, /device:TPU:0, one launch (start us, length us, event | category | flops | bytes accessed | tf_op | source)
XLA Modules:
  0.0 262.9 jit_solution(16762521980324832332)
XLA Ops:
  0.0 3.0 %collective-permute-start.3 = (bf16[32,3072]{1,0:T(8,128)(2,1)}, bf16[32,3072]{1,0:T(8,128)(2,1)S(1)}, u32[]{:S(2)}, u32[]{:S(2)}) collective-permute-start(bf16[32,3072]{1,0:T(8,128)(2,1)} %param.22), channel_id=1, source_target_pairs={{0,2},{2,4},{4,6},{6,7},{7,5},{5,3},{3,1},{1,0},{8,10},{10,12},{12... | collective-permute-start | bytes 589832 | tf_op jit(solution)/shard_map/ppermute | solution.py:61
  6.3 1.6 bitcast_dynamic-update-slice_fusion.20
  7.9 19.6 %copy.11 = bf16[2,3,3072,2,384]{4,2,3,1,0:T(8,128)(2,1)} copy(bf16[2,3,3072,2,384]{4,3,2,1,0:T(2,128)(2,1)} %param.25) | data formatting | bytes 56623104 | tf_op args[3]
  28.2 2.1 collective-permute-start.4
  31.0 3.6 %collective-permute-done.4 = bf16[32,3072]{1,0:T(8,128)(2,1)S(1)} collective-permute-done((bf16[32,3072]{1,0:T(8,128)(2,1)S(1)}, bf16[32,3072]{1,0:T(8,128)(2,1)S(1)}, u32[]{:S(2)}, u32[]{:S(2)}) %collective-permute-start.4) | collective-permute-done | bytes 196640 | tf_op jit(solution)/shard_map/ppermute | solution.py:61
  34.6 1.7 collective-permute-start.5
  37.4 2.9 %collective-permute-done.5 = bf16[32,3072]{1,0:T(8,128)(2,1)S(1)} collective-permute-done((bf16[32,3072]{1,0:T(8,128)(2,1)S(1)}, bf16[32,3072]{1,0:T(8,128)(2,1)S(1)}, u32[]{:S(2)}, u32[]{:S(2)}) %collective-permute-start.5) | collective-permute-done | bytes 196640 | tf_op jit(solution)/shard_map/ppermute | solution.py:61
  40.3 1.9 collective-permute-start.6
  43.2 1.8 collective-permute-done.6
  45.0 1.9 collective-permute-done.7
  49.7 2.1 gather_fusion
  55.0 2.2 fusion.19
  57.2 2.4 pad_maximum_fusion.slab_ref
  59.6 10.8 %shard_map.82 = bf16[256,384]{1,0:T(8,128)(2,1)} custom-call(bf16[3,256,3072]{2,1,0:T(8,128)(2,1)} %pad_maximum_fusion.slab_ref, f32[1,3072]{1,0:T(1,128)} %get-tuple-element.124.gain_ref, bf16[2,3,2,3072,384]{4,3,2,1,0:T(8,128)(2,1)} %bitcast.124), custom_call_target="tpu_custom_call" | custom-call | flops 3623878656 | bytes 19070976 | tf_op jit(solution)/shard_map/pallas_call | solution.py:164
  70.4 1.5 gather_fusion.1
  71.9 2.6 %convolution_convert_fusion.2 = bf16[256,3072]{1,0:T(8,128)(2,1)S(1)} fusion(bf16[256,384]{1,0:T(8,128)(2,1)S(1)} %bitcast.139, bf16[2,384,3072]{2,1,0:T(8,128)(2,1)} %param.26), kind=kOutput, calls=%fused_computation.19 | convolution fusion | flops 604766208 | bytes 4128768 | tf_op jit(solution)/shard_map/dot_general | solution.py:124
  74.6 1.6 collective-permute-start.9
  76.8 2.9 %collective-permute-done.9 = bf16[16,3072]{1,0:T(8,128)(2,1)S(1)} collective-permute-done((bf16[16,3072]{1,0:T(8,128)(2,1)S(1)}, bf16[16,3072]{1,0:T(8,128)(2,1)S(1)}, u32[]{:S(2)}, u32[]{:S(2)}) %collective-permute-start.9) | collective-permute-done | bytes 98336 | tf_op jit(solution)/shard_map/ppermute | solution.py:99
  79.8 1.6 collective-permute-start.10
  82.0 4.2 %collective-permute-done.10 = bf16[32,3072]{1,0:T(8,128)(2,1)S(1)} collective-permute-done((bf16[32,3072]{1,0:T(8,128)(2,1)S(1)}, bf16[32,3072]{1,0:T(8,128)(2,1)S(1)}, u32[]{:S(2)}, u32[]{:S(2)}) %collective-permute-start.10) | collective-permute-done | bytes 196640 | tf_op jit(solution)/shard_map/ppermute | solution.py:99
  86.3 1.6 collective-permute-start.11
  87.9 4.1 %collective-permute-done.11 = bf16[32,3072]{1,0:T(8,128)(2,1)S(1)} collective-permute-done((bf16[32,3072]{1,0:T(8,128)(2,1)S(1)}, bf16[32,3072]{1,0:T(8,128)(2,1)S(1)}, u32[]{:S(2)}, u32[]{:S(2)}) %collective-permute-start.11) | collective-permute-done | bytes 196640 | tf_op jit(solution)/shard_map/ppermute | solution.py:99
  92.7 1.4 collective-permute-start.12
  94.2 4.6 %collective-permute-done.15 = bf16[32,3072]{1,0:T(8,128)(2,1)S(1)} collective-permute-done((bf16[32,3072]{1,0:T(8,128)(2,1)S(1)}, bf16[32,3072]{1,0:T(8,128)(2,1)S(1)}, u32[]{:S(2)}, u32[]{:S(2)}) %collective-permute-start.15) | collective-permute-done | bytes 196640 | tf_op jit(solution)/shard_map/ppermute | solution.py:99
  99.2 6.8 %collective-permute-done.16 = bf16[32,3072]{1,0:T(8,128)(2,1)S(1)} collective-permute-done((bf16[32,3072]{1,0:T(8,128)(2,1)S(1)}, bf16[32,3072]{1,0:T(8,128)(2,1)S(1)}, u32[]{:S(2)}, u32[]{:S(2)}) %collective-permute-start.16) | collective-permute-done | bytes 196640 | tf_op jit(solution)/shard_map/ppermute | solution.py:99
  106.8 2.0 collective-permute-start.20
  108.8 4.5 %collective-permute-done.17 = bf16[32,3072]{1,0:T(8,128)(2,1)S(1)} collective-permute-done((bf16[32,3072]{1,0:T(8,128)(2,1)S(1)}, bf16[32,3072]{1,0:T(8,128)(2,1)S(1)}, u32[]{:S(2)}, u32[]{:S(2)}) %collective-permute-start.17) | collective-permute-done | bytes 196640 | tf_op jit(solution)/shard_map/ppermute | solution.py:64
  113.6 1.7 collective-permute-start.21
  116.0 2.9 %collective-permute-done.18 = bf16[32,3072]{1,0:T(8,128)(2,1)S(1)} collective-permute-done((bf16[32,3072]{1,0:T(8,128)(2,1)S(1)}, bf16[32,3072]{1,0:T(8,128)(2,1)S(1)}, u32[]{:S(2)}, u32[]{:S(2)}) %collective-permute-start.18) | collective-permute-done | bytes 196640 | tf_op jit(solution)/shard_map/ppermute | solution.py:64
  121.7 2.9 %collective-permute-done.19 = bf16[32,3072]{1,0:T(8,128)(2,1)S(1)} collective-permute-done((bf16[32,3072]{1,0:T(8,128)(2,1)S(1)}, bf16[32,3072]{1,0:T(8,128)(2,1)S(1)}, u32[]{:S(2)}, u32[]{:S(2)}) %collective-permute-start.19) | collective-permute-done | bytes 196640 | tf_op jit(solution)/shard_map/ppermute | solution.py:64
  125.3 1.5 collective-permute-start.23
  127.5 1.8 collective-permute-done.24
  132.8 2.1 gather_fusion.2
  134.9 2.2 collective-permute-start.25
  139.0 3.0 %fusion.15 = (bf16[1,256,3072]{2,1,0:T(8,128)(2,1)S(1)}, bf16[1,256,3072]{2,1,0:T(8,128)(2,1)S(1)}) fusion(s32[]{:T(128)S(6)} %select_n.23, bf16[256,3072]{1,0:T(8,128)(2,1)S(1)} %bitcast.126, bf16[128,3072]{1,0:T(8,128)(2,1)} %collective-permute-done.25, s32[]{:T(128)S(6)} %select_n.24), kind=kLoop, calls=%fused_computation.38 | loop fusion | flops 6291456 | bytes 5505032 | tf_op jit(solution)/shard_map/stack | solution.py:157
  142.0 2.4 pad_maximum_fusion.1.slab_ref
  144.4 10.8 %shard_map.83 = bf16[256,384]{1,0:T(8,128)(2,1)} custom-call(bf16[3,256,3072]{2,1,0:T(8,128)(2,1)} %pad_maximum_fusion.1.slab_ref, f32[1,3072]{1,0:T(1,128)} %get-tuple-element.125.gain_ref, bf16[2,3,2,3072,384]{4,3,2,1,0:T(8,128)(2,1)} %bitcast.125), custom_call_target="tpu_custom_call" | custom-call | flops 3623878656 | bytes 19070976 | tf_op jit(solution)/shard_map/pallas_call | solution.py:164
  155.2 1.5 gather_fusion.3
  156.7 2.6 %convolution_convert_fusion.1 = bf16[256,3072]{1,0:T(8,128)(2,1)S(1)} fusion(bf16[256,384]{1,0:T(8,128)(2,1)S(1)} %bitcast.140, bf16[2,384,3072]{2,1,0:T(8,128)(2,1)} %param.26), kind=kOutput, calls=%fused_computation.18 | convolution fusion | flops 604766208 | bytes 4128768 | tf_op jit(solution)/shard_map/dot_general | solution.py:124
  159.4 1.5 collective-permute-start.26
  161.6 2.5 collective-permute-done.26
  164.2 1.5 collective-permute-start.27
  166.4 3.5 %collective-permute-done.27 = bf16[32,3072]{1,0:T(8,128)(2,1)S(1)} collective-permute-done((bf16[32,3072]{1,0:T(8,128)(2,1)S(1)}, bf16[32,3072]{1,0:T(8,128)(2,1)S(1)}, u32[]{:S(2)}, u32[]{:S(2)}) %collective-permute-start.27) | collective-permute-done | bytes 196640 | tf_op jit(solution)/shard_map/ppermute | solution.py:99
  169.9 1.5 collective-permute-start.28
  171.4 4.2 %collective-permute-done.28 = bf16[32,3072]{1,0:T(8,128)(2,1)S(1)} collective-permute-done((bf16[32,3072]{1,0:T(8,128)(2,1)S(1)}, bf16[32,3072]{1,0:T(8,128)(2,1)S(1)}, u32[]{:S(2)}, u32[]{:S(2)}) %collective-permute-start.28) | collective-permute-done | bytes 196640 | tf_op jit(solution)/shard_map/ppermute | solution.py:99
  175.8 1.6 collective-permute-start.32
  178.0 5.4 %collective-permute-done.32 = bf16[32,3072]{1,0:T(8,128)(2,1)S(1)} collective-permute-done((bf16[32,3072]{1,0:T(8,128)(2,1)S(1)}, bf16[32,3072]{1,0:T(8,128)(2,1)S(1)}, u32[]{:S(2)}, u32[]{:S(2)}) %collective-permute-start.32) | collective-permute-done | bytes 196640 | tf_op jit(solution)/shard_map/ppermute | solution.py:99
  183.5 1.6 collective-permute-start.33
  185.0 5.8 %collective-permute-done.33 = bf16[32,3072]{1,0:T(8,128)(2,1)S(1)} collective-permute-done((bf16[32,3072]{1,0:T(8,128)(2,1)S(1)}, bf16[32,3072]{1,0:T(8,128)(2,1)S(1)}, u32[]{:S(2)}, u32[]{:S(2)}) %collective-permute-start.33) | collective-permute-done | bytes 196640 | tf_op jit(solution)/shard_map/ppermute | solution.py:99
  191.6 1.6 collective-permute-start.34
  193.6 3.7 %collective-permute-done.34 = bf16[32,3072]{1,0:T(8,128)(2,1)S(1)} collective-permute-done((bf16[32,3072]{1,0:T(8,128)(2,1)S(1)}, bf16[32,3072]{1,0:T(8,128)(2,1)S(1)}, u32[]{:S(2)}, u32[]{:S(2)}) %collective-permute-start.34) | collective-permute-done | bytes 196640 | tf_op jit(solution)/shard_map/ppermute | solution.py:64
  197.3 1.8 collective-permute-start.35
  200.0 3.7 %collective-permute-done.35 = bf16[32,3072]{1,0:T(8,128)(2,1)S(1)} collective-permute-done((bf16[32,3072]{1,0:T(8,128)(2,1)S(1)}, bf16[32,3072]{1,0:T(8,128)(2,1)S(1)}, u32[]{:S(2)}, u32[]{:S(2)}) %collective-permute-start.35) | collective-permute-done | bytes 196640 | tf_op jit(solution)/shard_map/ppermute | solution.py:64
  206.4 2.9 %collective-permute-done.36 = bf16[32,3072]{1,0:T(8,128)(2,1)S(1)} collective-permute-done((bf16[32,3072]{1,0:T(8,128)(2,1)S(1)}, bf16[32,3072]{1,0:T(8,128)(2,1)S(1)}, u32[]{:S(2)}, u32[]{:S(2)}) %collective-permute-start.36) | collective-permute-done | bytes 196640 | tf_op jit(solution)/shard_map/ppermute | solution.py:64
  212.2 1.8 collective-permute-done.41
  214.0 1.4 collective-permute-done.40
  218.2 2.1 gather_fusion.4
  232.5 2.5 collective-permute-done.44
  237.4 5.5 %collective-permute-done.45 = bf16[32,3072]{1,0:T(8,128)(2,1)S(1)} collective-permute-done((bf16[32,3072]{1,0:T(8,128)(2,1)S(1)}, bf16[32,3072]{1,0:T(8,128)(2,1)S(1)}, u32[]{:S(2)}, u32[]{:S(2)}) %collective-permute-start.45) | collective-permute-done | bytes 196640 | tf_op jit(solution)/shard_map/ppermute | solution.py:99
  243.7 6.2 %collective-permute-done.46 = bf16[32,3072]{1,0:T(8,128)(2,1)S(1)} collective-permute-done((bf16[32,3072]{1,0:T(8,128)(2,1)S(1)}, bf16[32,3072]{1,0:T(8,128)(2,1)S(1)}, u32[]{:S(2)}, u32[]{:S(2)}) %collective-permute-start.46) | collective-permute-done | bytes 196640 | tf_op jit(solution)/shard_map/ppermute | solution.py:99
  250.1 1.6 collective-permute-start.50
  252.1 4.2 %collective-permute-done.50 = bf16[32,3072]{1,0:T(8,128)(2,1)S(1)} collective-permute-done((bf16[32,3072]{1,0:T(8,128)(2,1)S(1)}, bf16[32,3072]{1,0:T(8,128)(2,1)S(1)}, u32[]{:S(2)}, u32[]{:S(2)}) %collective-permute-start.50) | collective-permute-done | bytes 196640 | tf_op jit(solution)/shard_map/ppermute | solution.py:99
  256.4 1.6 collective-permute-start.51
  258.0 4.1 %collective-permute-done.51 = bf16[32,3072]{1,0:T(8,128)(2,1)S(1)} collective-permute-done((bf16[32,3072]{1,0:T(8,128)(2,1)S(1)}, bf16[32,3072]{1,0:T(8,128)(2,1)S(1)}, u32[]{:S(2)}, u32[]{:S(2)}) %collective-permute-start.51) | collective-permute-done | bytes 196640 | tf_op jit(solution)/shard_map/ppermute | solution.py:99
  (144 shorter events, 52.9 us)
Async XLA Ops:
  0.0 229.8 %copy-start = (bf16[1,128,3072]{2,1,0:T(8,128)(2,1)S(1)}, bf16[1,128,3072]{2,1,0:T(8,128)(2,1)}, u32[]{:S(2)}) copy-start(bf16[1,128,3072]{2,1,0:T(8,128)(2,1)} %param.28) | copy-start | bytes 2359300
  0.0 28.2 %collective-permute-start.3 = (bf16[32,3072]{1,0:T(8,128)(2,1)}, bf16[32,3072]{1,0:T(8,128)(2,1)S(1)}, u32[]{:S(2)}, u32[]{:S(2)}) collective-permute-start(bf16[32,3072]{1,0:T(8,128)(2,1)} %param.22), channel_id=1, source_target_pairs={{0,2},{2,4},{4,6},{6,7},{7,5},{5,3},{3,1},{1,0},{8,10},{10,12},{12... | collective-permute-start | bytes 589832 | tf_op jit(solution)/shard_map/ppermute | solution.py:61
  3.0 27.3 %collective-permute-start = (bf16[32,3072]{1,0:T(8,128)(2,1)}, bf16[32,3072]{1,0:T(8,128)(2,1)S(1)}, u32[]{:S(2)}, u32[]{:S(2)}) collective-permute-start(bf16[32,3072]{1,0:T(8,128)(2,1)} %param.22), channel_id=1, source_target_pairs={{0,1},{2,0},{4,2},{6,4},{7,6},{5,7},{3,5},{1,3},{8,9},{10,8},{12,1... | collective-permute-start | bytes 589832 | tf_op jit(solution)/shard_map/ppermute | solution.py:64
  28.2 6.4 %collective-permute-start.4 = (bf16[32,3072]{1,0:T(8,128)(2,1)S(1)}, bf16[32,3072]{1,0:T(8,128)(2,1)S(1)}, u32[]{:S(2)}, u32[]{:S(2)}) collective-permute-start(bf16[32,3072]{1,0:T(8,128)(2,1)S(1)} %collective-permute-done.3), channel_id=1, source_target_pairs={{0,2},{2,4},{4,6},{6,7},{7,5},{5,3},{3,1},{1,0},{8,10},{10,12},{12... | collective-permute-start | bytes 589832 | tf_op jit(solution)/shard_map/ppermute | solution.py:61
  30.3 6.1 %collective-permute-start.1 = (bf16[32,3072]{1,0:T(8,128)(2,1)S(1)}, bf16[32,3072]{1,0:T(8,128)(2,1)S(1)}, u32[]{:S(2)}, u32[]{:S(2)}) collective-permute-start(bf16[32,3072]{1,0:T(8,128)(2,1)S(1)} %collective-permute-done), channel_id=1, source_target_pairs={{0,1},{2,0},{4,2},{6,4},{7,6},{5,7},{3,5},{1,3},{8,9},{10,8},{12,1... | collective-permute-start | bytes 589832 | tf_op jit(solution)/shard_map/ppermute | solution.py:64
  34.6 5.7 %collective-permute-start.5 = (bf16[32,3072]{1,0:T(8,128)(2,1)S(1)}, bf16[32,3072]{1,0:T(8,128)(2,1)S(1)}, u32[]{:S(2)}, u32[]{:S(2)}) collective-permute-start(bf16[32,3072]{1,0:T(8,128)(2,1)S(1)} %collective-permute-done.4), channel_id=1, source_target_pairs={{0,2},{2,4},{4,6},{6,7},{7,5},{5,3},{3,1},{1,0},{8,10},{10,12},{12... | collective-permute-start | bytes 589832 | tf_op jit(solution)/shard_map/ppermute | solution.py:61
  36.4 5.8 %collective-permute-start.2 = (bf16[32,3072]{1,0:T(8,128)(2,1)S(1)}, bf16[32,3072]{1,0:T(8,128)(2,1)S(1)}, u32[]{:S(2)}, u32[]{:S(2)}) collective-permute-start(bf16[32,3072]{1,0:T(8,128)(2,1)S(1)} %collective-permute-done.1), channel_id=1, source_target_pairs={{0,1},{2,0},{4,2},{6,4},{7,6},{5,7},{3,5},{1,3},{8,9},{10,8},{12,1... | collective-permute-start | bytes 589832 | tf_op jit(solution)/shard_map/ppermute | solution.py:64
  40.3 4.7 %collective-permute-start.6 = (bf16[16,3072]{1,0:T(8,128)(2,1)S(1)}, bf16[16,3072]{1,0:T(8,128)(2,1)S(1)}, u32[]{:S(2)}, u32[]{:S(2)}) collective-permute-start(bf16[16,3072]{1,0:T(8,128)(2,1)S(1)} %slice.372), channel_id=1, source_target_pairs={{0,2},{2,4},{4,6},{6,7},{7,5},{5,3},{3,1},{1,0},{8,10},{10,12},{12... | collective-permute-start | bytes 294920 | tf_op jit(solution)/shard_map/ppermute | solution.py:57
  42.2 4.7 %collective-permute-start.7 = (bf16[16,3072]{1,0:T(8,128)(2,1)S(1)}, bf16[16,3072]{1,0:T(8,128)(2,1)S(1)}, u32[]{:S(2)}, u32[]{:S(2)}) collective-permute-start(bf16[16,3072]{1,0:T(8,128)(2,1)S(1)} %slice.373), channel_id=1, source_target_pairs={{0,1},{2,0},{4,2},{6,4},{7,6},{5,7},{3,5},{1,3},{8,9},{10,8},{12,1... | collective-permute-start | bytes 294920 | tf_op jit(solution)/shard_map/ppermute | solution.py:58
  51.7 1.4 copy-start.2
  51.8 3.2 %collective-permute-start.8 = (bf16[128,3072]{1,0:T(8,128)(2,1)S(1)}, bf16[128,3072]{1,0:T(8,128)(2,1)S(1)}, u32[]{:S(2)}, u32[]{:S(2)}) collective-permute-start(bf16[128,3072]{1,0:T(8,128)(2,1)S(1)} %bitcast.136), channel_id=1, source_target_pairs={{0,8},{1,9},{2,10},{3,11},{4,12},{5,13},{6,14},{7,15},{16,24},{17,... | collective-permute-start | bytes 2359304 | tf_op jit(solution)/shard_map/ppermute | solution.py:14
  74.6 5.1 %collective-permute-start.9 = (bf16[16,3072]{1,0:T(8,128)(2,1)S(1)}, bf16[16,3072]{1,0:T(8,128)(2,1)S(1)}, u32[]{:S(2)}, u32[]{:S(2)}) collective-permute-start(bf16[16,3072]{1,0:T(8,128)(2,1)S(1)} %get-tuple-element.119), channel_id=1, source_target_pairs={{0,2},{2,4},{4,6},{6,7},{7,5},{5,3},{3,1},{1,0},{8,10},{10,12},{12... | collective-permute-start | bytes 294920 | tf_op jit(solution)/shard_map/ppermute | solution.py:99
  76.3 5.1 %collective-permute-start.13 = (bf16[16,3072]{1,0:T(8,128)(2,1)S(1)}, bf16[16,3072]{1,0:T(8,128)(2,1)S(1)}, u32[]{:S(2)}, u32[]{:S(2)}) collective-permute-start(bf16[16,3072]{1,0:T(8,128)(2,1)S(1)} %get-tuple-element.120), channel_id=1, source_target_pairs={{0,1},{2,0},{4,2},{6,4},{7,6},{5,7},{3,5},{1,3},{8,9},{10,8},{12,1... | collective-permute-start | bytes 294920 | tf_op jit(solution)/shard_map/ppermute | solution.py:99
  79.8 6.4 %collective-permute-start.10 = (bf16[32,3072]{1,0:T(8,128)(2,1)S(1)}, bf16[32,3072]{1,0:T(8,128)(2,1)S(1)}, u32[]{:S(2)}, u32[]{:S(2)}) collective-permute-start(bf16[32,3072]{1,0:T(8,128)(2,1)S(1)} %convert_element_type.301), channel_id=1, source_target_pairs={{0,2},{2,4},{4,6},{6,7},{7,5},{5,3},{3,1},{1,0},{8,10},{10,12},{12... | collective-permute-start | bytes 589832 | tf_op jit(solution)/shard_map/ppermute | solution.py:99
  81.5 24.5 %copy-start.1 = (bf16[32,3072]{1,0:T(8,128)(2,1)S(1)}, bf16[32,3072]{1,0:T(8,128)(2,1)}, u32[]{:S(2)}) copy-start(bf16[32,3072]{1,0:T(8,128)(2,1)} %param.22) | copy-start | bytes 589828
  81.5 6.4 %collective-permute-start.14 = (bf16[32,3072]{1,0:T(8,128)(2,1)S(1)}, bf16[32,3072]{1,0:T(8,128)(2,1)S(1)}, u32[]{:S(2)}, u32[]{:S(2)}) collective-permute-start(bf16[32,3072]{1,0:T(8,128)(2,1)S(1)} %convert_element_type.311), channel_id=1, source_target_pairs={{0,1},{2,0},{4,2},{6,4},{7,6},{5,7},{3,5},{1,3},{8,9},{10,8},{12,1... | collective-permute-start | bytes 589832 | tf_op jit(solution)/shard_map/ppermute | solution.py:99
  86.3 5.7 %collective-permute-start.11 = (bf16[32,3072]{1,0:T(8,128)(2,1)S(1)}, bf16[32,3072]{1,0:T(8,128)(2,1)S(1)}, u32[]{:S(2)}, u32[]{:S(2)}) collective-permute-start(bf16[32,3072]{1,0:T(8,128)(2,1)S(1)} %add_convert_fusion.14), channel_id=1, source_target_pairs={{0,2},{2,4},{4,6},{6,7},{7,5},{5,3},{3,1},{1,0},{8,10},{10,12},{12... | collective-permute-start | bytes 589832 | tf_op jit(solution)/shard_map/ppermute | solution.py:99
  92.1 6.6 %collective-permute-start.15 = (bf16[32,3072]{1,0:T(8,128)(2,1)S(1)}, bf16[32,3072]{1,0:T(8,128)(2,1)S(1)}, u32[]{:S(2)}, u32[]{:S(2)}) collective-permute-start(bf16[32,3072]{1,0:T(8,128)(2,1)S(1)} %get-tuple-element.118), channel_id=1, source_target_pairs={{0,1},{2,0},{4,2},{6,4},{7,6},{5,7},{3,5},{1,3},{8,9},{10,8},{12,1... | collective-permute-start | bytes 589832 | tf_op jit(solution)/shard_map/ppermute | solution.py:99
  92.7 6.5 %collective-permute-start.12 = (bf16[32,3072]{1,0:T(8,128)(2,1)S(1)}, bf16[32,3072]{1,0:T(8,128)(2,1)S(1)}, u32[]{:S(2)}, u32[]{:S(2)}) collective-permute-start(bf16[32,3072]{1,0:T(8,128)(2,1)S(1)} %get-tuple-element.117), channel_id=1, source_target_pairs={{0,2},{2,4},{4,6},{6,7},{7,5},{5,3},{3,1},{1,0},{8,10},{10,12},{12... | collective-permute-start | bytes 589832 | tf_op jit(solution)/shard_map/ppermute | solution.py:99
  98.8 7.1 %collective-permute-start.16 = (bf16[32,3072]{1,0:T(8,128)(2,1)S(1)}, bf16[32,3072]{1,0:T(8,128)(2,1)S(1)}, u32[]{:S(2)}, u32[]{:S(2)}) collective-permute-start(bf16[32,3072]{1,0:T(8,128)(2,1)S(1)} %add_convert_fusion.11), channel_id=1, source_target_pairs={{0,1},{2,0},{4,2},{6,4},{7,6},{5,7},{3,5},{1,3},{8,9},{10,8},{12,1... | collective-permute-start | bytes 589832 | tf_op jit(solution)/shard_map/ppermute | solution.py:99
  106.8 6.5 %collective-permute-start.17 = (bf16[32,3072]{1,0:T(8,128)(2,1)S(1)}, bf16[32,3072]{1,0:T(8,128)(2,1)S(1)}, u32[]{:S(2)}, u32[]{:S(2)}) collective-permute-start(bf16[32,3072]{1,0:T(8,128)(2,1)S(1)} %get-tuple-element.98), channel_id=1, source_target_pairs={{0,1},{2,0},{4,2},{6,4},{7,6},{5,7},{3,5},{1,3},{8,9},{10,8},{12,1... | collective-permute-start | bytes 589832 | tf_op jit(solution)/shard_map/ppermute | solution.py:64
  106.8 6.8 %collective-permute-start.20 = (bf16[32,3072]{1,0:T(8,128)(2,1)S(1)}, bf16[32,3072]{1,0:T(8,128)(2,1)S(1)}, u32[]{:S(2)}, u32[]{:S(2)}) collective-permute-start(bf16[32,3072]{1,0:T(8,128)(2,1)S(1)} %get-tuple-element.98), channel_id=1, source_target_pairs={{0,2},{2,4},{4,6},{6,7},{7,5},{5,3},{3,1},{1,0},{8,10},{10,12},{12... | collective-permute-start | bytes 589832 | tf_op jit(solution)/shard_map/ppermute | solution.py:61
  113.3 5.7 %collective-permute-start.18 = (bf16[32,3072]{1,0:T(8,128)(2,1)S(1)}, bf16[32,3072]{1,0:T(8,128)(2,1)S(1)}, u32[]{:S(2)}, u32[]{:S(2)}) collective-permute-start(bf16[32,3072]{1,0:T(8,128)(2,1)S(1)} %collective-permute-done.17), channel_id=1, source_target_pairs={{0,1},{2,0},{4,2},{6,4},{7,6},{5,7},{3,5},{1,3},{8,9},{10,8},{12,1... | collective-permute-start | bytes 589832 | tf_op jit(solution)/shard_map/ppermute | solution.py:64
  113.6 5.9 %collective-permute-start.21 = (bf16[32,3072]{1,0:T(8,128)(2,1)S(1)}, bf16[32,3072]{1,0:T(8,128)(2,1)S(1)}, u32[]{:S(2)}, u32[]{:S(2)}) collective-permute-start(bf16[32,3072]{1,0:T(8,128)(2,1)S(1)} %collective-permute-done.20), channel_id=1, source_target_pairs={{0,2},{2,4},{4,6},{6,7},{7,5},{5,3},{3,1},{1,0},{8,10},{10,12},{12... | collective-permute-start | bytes 589832 | tf_op jit(solution)/shard_map/ppermute | solution.py:61
  118.9 5.7 %collective-permute-start.19 = (bf16[32,3072]{1,0:T(8,128)(2,1)S(1)}, bf16[32,3072]{1,0:T(8,128)(2,1)S(1)}, u32[]{:S(2)}, u32[]{:S(2)}) collective-permute-start(bf16[32,3072]{1,0:T(8,128)(2,1)S(1)} %collective-permute-done.18), channel_id=1, source_target_pairs={{0,1},{2,0},{4,2},{6,4},{7,6},{5,7},{3,5},{1,3},{8,9},{10,8},{12,1... | collective-permute-start | bytes 589832 | tf_op jit(solution)/shard_map/ppermute | solution.py:64
  119.6 5.7 %collective-permute-start.22 = (bf16[32,3072]{1,0:T(8,128)(2,1)S(1)}, bf16[32,3072]{1,0:T(8,128)(2,1)S(1)}, u32[]{:S(2)}, u32[]{:S(2)}) collective-permute-start(bf16[32,3072]{1,0:T(8,128)(2,1)S(1)} %collective-permute-done.21), channel_id=1, source_target_pairs={{0,2},{2,4},{4,6},{6,7},{7,5},{5,3},{3,1},{1,0},{8,10},{10,12},{12... | collective-permute-start | bytes 589832 | tf_op jit(solution)/shard_map/ppermute | solution.py:61
  124.6 4.7 %collective-permute-start.24 = (bf16[16,3072]{1,0:T(8,128)(2,1)S(1)}, bf16[16,3072]{1,0:T(8,128)(2,1)S(1)}, u32[]{:S(2)}, u32[]{:S(2)}) collective-permute-start(bf16[16,3072]{1,0:T(8,128)(2,1)S(1)} %slice.387), channel_id=1, source_target_pairs={{0,1},{2,0},{4,2},{6,4},{7,6},{5,7},{3,5},{1,3},{8,9},{10,8},{12,1... | collective-permute-start | bytes 294920 | tf_op jit(solution)/shard_map/ppermute | solution.py:58
  125.3 4.7 %collective-permute-start.23 = (bf16[16,3072]{1,0:T(8,128)(2,1)S(1)}, bf16[16,3072]{1,0:T(8,128)(2,1)S(1)}, u32[]{:S(2)}, u32[]{:S(2)}) collective-permute-start(bf16[16,3072]{1,0:T(8,128)(2,1)S(1)} %slice.386), channel_id=1, source_target_pairs={{0,2},{2,4},{4,6},{6,7},{7,5},{5,3},{3,1},{1,0},{8,10},{10,12},{12... | collective-permute-start | bytes 294920 | tf_op jit(solution)/shard_map/ppermute | solution.py:57
  134.9 4.1 %collective-permute-start.25 = (bf16[128,3072]{1,0:T(8,128)(2,1)S(1)}, bf16[128,3072]{1,0:T(8,128)(2,1)}, u32[]{:S(2)}, u32[]{:S(2)}) collective-permute-start(bf16[128,3072]{1,0:T(8,128)(2,1)S(1)} %bitcast.135), channel_id=1, source_target_pairs={{0,8},{1,9},{2,10},{3,11},{4,12},{5,13},{6,14},{7,15},{16,24},{17,... | collective-permute-start | bytes 2359304 | tf_op jit(solution)/shard_map/ppermute | solution.py:14
  159.4 4.7 %collective-permute-start.26 = (bf16[16,3072]{1,0:T(8,128)(2,1)S(1)}, bf16[16,3072]{1,0:T(8,128)(2,1)S(1)}, u32[]{:S(2)}, u32[]{:S(2)}) collective-permute-start(bf16[16,3072]{1,0:T(8,128)(2,1)S(1)} %get-tuple-element.113), channel_id=1, source_target_pairs={{0,2},{2,4},{4,6},{6,7},{7,5},{5,3},{3,1},{1,0},{8,10},{10,12},{12... | collective-permute-start | bytes 294920 | tf_op jit(solution)/shard_map/ppermute | solution.py:99
  160.9 4.7 %collective-permute-start.30 = (bf16[16,3072]{1,0:T(8,128)(2,1)S(1)}, bf16[16,3072]{1,0:T(8,128)(2,1)S(1)}, u32[]{:S(2)}, u32[]{:S(2)}) collective-permute-start(bf16[16,3072]{1,0:T(8,128)(2,1)S(1)} %get-tuple-element.114), channel_id=1, source_target_pairs={{0,1},{2,0},{4,2},{6,4},{7,6},{5,7},{3,5},{1,3},{8,9},{10,8},{12,1... | collective-permute-start | bytes 294920 | tf_op jit(solution)/shard_map/ppermute | solution.py:99
  164.2 5.7 %collective-permute-start.27 = (bf16[32,3072]{1,0:T(8,128)(2,1)S(1)}, bf16[32,3072]{1,0:T(8,128)(2,1)S(1)}, u32[]{:S(2)}, u32[]{:S(2)}) collective-permute-start(bf16[32,3072]{1,0:T(8,128)(2,1)S(1)} %convert_element_type.325), channel_id=1, source_target_pairs={{0,2},{2,4},{4,6},{6,7},{7,5},{5,3},{3,1},{1,0},{8,10},{10,12},{12... | collective-permute-start | bytes 589832 | tf_op jit(solution)/shard_map/ppermute | solution.py:99
  165.7 5.7 %collective-permute-start.31 = (bf16[32,3072]{1,0:T(8,128)(2,1)S(1)}, bf16[32,3072]{1,0:T(8,128)(2,1)S(1)}, u32[]{:S(2)}, u32[]{:S(2)}) collective-permute-start(bf16[32,3072]{1,0:T(8,128)(2,1)S(1)} %convert_element_type.335), channel_id=1, source_target_pairs={{0,1},{2,0},{4,2},{6,4},{7,6},{5,7},{3,5},{1,3},{8,9},{10,8},{12,1... | collective-permute-start | bytes 589832 | tf_op jit(solution)/shard_map/ppermute | solution.py:99
  169.9 5.7 %collective-permute-start.28 = (bf16[32,3072]{1,0:T(8,128)(2,1)S(1)}, bf16[32,3072]{1,0:T(8,128)(2,1)S(1)}, u32[]{:S(2)}, u32[]{:S(2)}) collective-permute-start(bf16[32,3072]{1,0:T(8,128)(2,1)S(1)} %add_convert_fusion.9), channel_id=1, source_target_pairs={{0,2},{2,4},{4,6},{6,7},{7,5},{5,3},{3,1},{1,0},{8,10},{10,12},{12... | collective-permute-start | bytes 589832 | tf_op jit(solution)/shard_map/ppermute | solution.py:99
  175.8 7.6 %collective-permute-start.32 = (bf16[32,3072]{1,0:T(8,128)(2,1)S(1)}, bf16[32,3072]{1,0:T(8,128)(2,1)S(1)}, u32[]{:S(2)}, u32[]{:S(2)}) collective-permute-start(bf16[32,3072]{1,0:T(8,128)(2,1)S(1)} %get-tuple-element.112), channel_id=1, source_target_pairs={{0,1},{2,0},{4,2},{6,4},{7,6},{5,7},{3,5},{1,3},{8,9},{10,8},{12,1... | collective-permute-start | bytes 589832 | tf_op jit(solution)/shard_map/ppermute | solution.py:99
  177.3 7.7 %collective-permute-start.29 = (bf16[32,3072]{1,0:T(8,128)(2,1)S(1)}, bf16[32,3072]{1,0:T(8,128)(2,1)S(1)}, u32[]{:S(2)}, u32[]{:S(2)}) collective-permute-start(bf16[32,3072]{1,0:T(8,128)(2,1)S(1)} %get-tuple-element.111), channel_id=1, source_target_pairs={{0,2},{2,4},{4,6},{6,7},{7,5},{5,3},{3,1},{1,0},{8,10},{10,12},{12... | collective-permute-start | bytes 589832 | tf_op jit(solution)/shard_map/ppermute | solution.py:99
  183.5 7.3 %collective-permute-start.33 = (bf16[32,3072]{1,0:T(8,128)(2,1)S(1)}, bf16[32,3072]{1,0:T(8,128)(2,1)S(1)}, u32[]{:S(2)}, u32[]{:S(2)}) collective-permute-start(bf16[32,3072]{1,0:T(8,128)(2,1)S(1)} %add_convert_fusion.6), channel_id=1, source_target_pairs={{0,1},{2,0},{4,2},{6,4},{7,6},{5,7},{3,5},{1,3},{8,9},{10,8},{12,1... | collective-permute-start | bytes 589832 | tf_op jit(solution)/shard_map/ppermute | solution.py:99
  191.6 5.7 %collective-permute-start.34 = (bf16[32,3072]{1,0:T(8,128)(2,1)S(1)}, bf16[32,3072]{1,0:T(8,128)(2,1)S(1)}, u32[]{:S(2)}, u32[]{:S(2)}) collective-permute-start(bf16[32,3072]{1,0:T(8,128)(2,1)S(1)} %get-tuple-element.96), channel_id=1, source_target_pairs={{0,1},{2,0},{4,2},{6,4},{7,6},{5,7},{3,5},{1,3},{8,9},{10,8},{12,1... | collective-permute-start | bytes 589832 | tf_op jit(solution)/shard_map/ppermute | solution.py:64
  193.2 5.8 %collective-permute-start.37 = (bf16[32,3072]{1,0:T(8,128)(2,1)S(1)}, bf16[32,3072]{1,0:T(8,128)(2,1)S(1)}, u32[]{:S(2)}, u32[]{:S(2)}) collective-permute-start(bf16[32,3072]{1,0:T(8,128)(2,1)S(1)} %get-tuple-element.96), channel_id=1, source_target_pairs={{0,2},{2,4},{4,6},{6,7},{7,5},{5,3},{3,1},{1,0},{8,10},{10,12},{12... | collective-permute-start | bytes 589832 | tf_op jit(solution)/shard_map/ppermute | solution.py:61
  197.3 6.4 %collective-permute-start.35 = (bf16[32,3072]{1,0:T(8,128)(2,1)S(1)}, bf16[32,3072]{1,0:T(8,128)(2,1)S(1)}, u32[]{:S(2)}, u32[]{:S(2)}) collective-permute-start(bf16[32,3072]{1,0:T(8,128)(2,1)S(1)} %collective-permute-done.34), channel_id=1, source_target_pairs={{0,1},{2,0},{4,2},{6,4},{7,6},{5,7},{3,5},{1,3},{8,9},{10,8},{12,1... | collective-permute-start | bytes 589832 | tf_op jit(solution)/shard_map/ppermute | solution.py:64
  199.1 6.0 %collective-permute-start.38 = (bf16[32,3072]{1,0:T(8,128)(2,1)S(1)}, bf16[32,3072]{1,0:T(8,128)(2,1)S(1)}, u32[]{:S(2)}, u32[]{:S(2)}) collective-permute-start(bf16[32,3072]{1,0:T(8,128)(2,1)S(1)} %collective-permute-done.37), channel_id=1, source_target_pairs={{0,2},{2,4},{4,6},{6,7},{7,5},{5,3},{3,1},{1,0},{8,10},{10,12},{12... | collective-permute-start | bytes 589832 | tf_op jit(solution)/shard_map/ppermute | solution.py:61
  203.7 5.7 %collective-permute-start.36 = (bf16[32,3072]{1,0:T(8,128)(2,1)S(1)}, bf16[32,3072]{1,0:T(8,128)(2,1)S(1)}, u32[]{:S(2)}, u32[]{:S(2)}) collective-permute-start(bf16[32,3072]{1,0:T(8,128)(2,1)S(1)} %collective-permute-done.35), channel_id=1, source_target_pairs={{0,1},{2,0},{4,2},{6,4},{7,6},{5,7},{3,5},{1,3},{8,9},{10,8},{12,1... | collective-permute-start | bytes 589832 | tf_op jit(solution)/shard_map/ppermute | solution.py:64
  205.0 5.7 %collective-permute-start.39 = (bf16[32,3072]{1,0:T(8,128)(2,1)S(1)}, bf16[32,3072]{1,0:T(8,128)(2,1)S(1)}, u32[]{:S(2)}, u32[]{:S(2)}) collective-permute-start(bf16[32,3072]{1,0:T(8,128)(2,1)S(1)} %collective-permute-done.38), channel_id=1, source_target_pairs={{0,2},{2,4},{4,6},{6,7},{7,5},{5,3},{3,1},{1,0},{8,10},{10,12},{12... | collective-permute-start | bytes 589832 | tf_op jit(solution)/shard_map/ppermute | solution.py:61
  209.4 4.7 %collective-permute-start.41 = (bf16[16,3072]{1,0:T(8,128)(2,1)S(1)}, bf16[16,3072]{1,0:T(8,128)(2,1)S(1)}, u32[]{:S(2)}, u32[]{:S(2)}) collective-permute-start(bf16[16,3072]{1,0:T(8,128)(2,1)S(1)} %slice.401), channel_id=1, source_target_pairs={{0,1},{2,0},{4,2},{6,4},{7,6},{5,7},{3,5},{1,3},{8,9},{10,8},{12,1... | collective-permute-start | bytes 294920 | tf_op jit(solution)/shard_map/ppermute | solution.py:58
  210.8 4.7 %collective-permute-start.40 = (bf16[16,3072]{1,0:T(8,128)(2,1)S(1)}, bf16[16,3072]{1,0:T(8,128)(2,1)S(1)}, u32[]{:S(2)}, u32[]{:S(2)}) collective-permute-start(bf16[16,3072]{1,0:T(8,128)(2,1)S(1)} %slice.400), channel_id=1, source_target_pairs={{0,2},{2,4},{4,6},{6,7},{7,5},{5,3},{3,1},{1,0},{8,10},{10,12},{12... | collective-permute-start | bytes 294920 | tf_op jit(solution)/shard_map/ppermute | solution.py:57
  220.7 1.7 copy-start.3
  224.0 2.9 %collective-permute-start.42 = (bf16[256,128]{1,0:T(8,128)(2,1)S(1)}, bf16[256,128]{1,0:T(8,128)(2,1)S(1)}, u32[]{:S(2)}, u32[]{:S(2)}) collective-permute-start(bf16[256,128]{1,0:T(8,128)(2,1)S(1)} %convolution_convert_fusion.4), channel_id=1, source_target_pairs={{0,8},{1,9},{2,10},{3,11},{4,12},{5,13},{6,14},{7,15},{16,24},{17,... | collective-permute-start | bytes 196616 | tf_op jit(solution)/shard_map/ppermute | solution.py:14
  225.3 2.2 collective-permute-start.43
  230.4 4.7 %collective-permute-start.44 = (bf16[16,3072]{1,0:T(8,128)(2,1)S(1)}, bf16[16,3072]{1,0:T(8,128)(2,1)S(1)}, u32[]{:S(2)}, u32[]{:S(2)}) collective-permute-start(bf16[16,3072]{1,0:T(8,128)(2,1)S(1)} %get-tuple-element.107), channel_id=1, source_target_pairs={{0,2},{2,4},{4,6},{6,7},{7,5},{5,3},{3,1},{1,0},{8,10},{10,12},{12... | collective-permute-start | bytes 294920 | tf_op jit(solution)/shard_map/ppermute | solution.py:99
  231.1 4.8 %collective-permute-start.48 = (bf16[16,3072]{1,0:T(8,128)(2,1)S(1)}, bf16[16,3072]{1,0:T(8,128)(2,1)S(1)}, u32[]{:S(2)}, u32[]{:S(2)}) collective-permute-start(bf16[16,3072]{1,0:T(8,128)(2,1)S(1)} %get-tuple-element.108), channel_id=1, source_target_pairs={{0,1},{2,0},{4,2},{6,4},{7,6},{5,7},{3,5},{1,3},{8,9},{10,8},{12,1... | collective-permute-start | bytes 294920 | tf_op jit(solution)/shard_map/ppermute | solution.py:99
  235.1 7.7 %collective-permute-start.45 = (bf16[32,3072]{1,0:T(8,128)(2,1)S(1)}, bf16[32,3072]{1,0:T(8,128)(2,1)S(1)}, u32[]{:S(2)}, u32[]{:S(2)}) collective-permute-start(bf16[32,3072]{1,0:T(8,128)(2,1)S(1)} %convert_element_type.358), channel_id=1, source_target_pairs={{0,2},{2,4},{4,6},{6,7},{7,5},{5,3},{3,1},{1,0},{8,10},{10,12},{12... | collective-permute-start | bytes 589832 | tf_op jit(solution)/shard_map/ppermute | solution.py:99
  236.0 7.8 %collective-permute-start.49 = (bf16[32,3072]{1,0:T(8,128)(2,1)S(1)}, bf16[32,3072]{1,0:T(8,128)(2,1)S(1)}, u32[]{:S(2)}, u32[]{:S(2)}) collective-permute-start(bf16[32,3072]{1,0:T(8,128)(2,1)S(1)} %convert_element_type.368), channel_id=1, source_target_pairs={{0,1},{2,0},{4,2},{6,4},{7,6},{5,7},{3,5},{1,3},{8,9},{10,8},{12,1... | collective-permute-start | bytes 589832 | tf_op jit(solution)/shard_map/ppermute | solution.py:99
  242.9 7.1 %collective-permute-start.46 = (bf16[32,3072]{1,0:T(8,128)(2,1)S(1)}, bf16[32,3072]{1,0:T(8,128)(2,1)S(1)}, u32[]{:S(2)}, u32[]{:S(2)}) collective-permute-start(bf16[32,3072]{1,0:T(8,128)(2,1)S(1)} %add_convert_fusion.4), channel_id=1, source_target_pairs={{0,2},{2,4},{4,6},{6,7},{7,5},{5,3},{3,1},{1,0},{8,10},{10,12},{12... | collective-permute-start | bytes 589832 | tf_op jit(solution)/shard_map/ppermute | solution.py:99
  250.1 6.3 %collective-permute-start.50 = (bf16[32,3072]{1,0:T(8,128)(2,1)S(1)}, bf16[32,3072]{1,0:T(8,128)(2,1)S(1)}, u32[]{:S(2)}, u32[]{:S(2)}) collective-permute-start(bf16[32,3072]{1,0:T(8,128)(2,1)S(1)} %get-tuple-element.106), channel_id=1, source_target_pairs={{0,1},{2,0},{4,2},{6,4},{7,6},{5,7},{3,5},{1,3},{8,9},{10,8},{12,1... | collective-permute-start | bytes 589832 | tf_op jit(solution)/shard_map/ppermute | solution.py:99
  251.7 6.3 %collective-permute-start.47 = (bf16[32,3072]{1,0:T(8,128)(2,1)S(1)}, bf16[32,3072]{1,0:T(8,128)(2,1)S(1)}, u32[]{:S(2)}, u32[]{:S(2)}) collective-permute-start(bf16[32,3072]{1,0:T(8,128)(2,1)S(1)} %get-tuple-element.105), channel_id=1, source_target_pairs={{0,2},{2,4},{4,6},{6,7},{7,5},{5,3},{3,1},{1,0},{8,10},{10,12},{12... | collective-permute-start | bytes 589832 | tf_op jit(solution)/shard_map/ppermute | solution.py:99
  256.4 5.7 %collective-permute-start.51 = (bf16[32,3072]{1,0:T(8,128)(2,1)S(1)}, bf16[32,3072]{1,0:T(8,128)(2,1)S(1)}, u32[]{:S(2)}, u32[]{:S(2)}) collective-permute-start(bf16[32,3072]{1,0:T(8,128)(2,1)S(1)} %add_convert_fusion.1), channel_id=1, source_target_pairs={{0,1},{2,0},{4,2},{6,4},{7,6},{5,7},{3,5},{1,3},{8,9},{10,8},{12,1... | collective-permute-start | bytes 589832 | tf_op jit(solution)/shard_map/ppermute | solution.py:99

commit v9 on v8

--- a/solution.py
+++ b/solution.py
@@ -40,11 +40,13 @@
     return forward, backward
 
 
-def ring_gather(value, axis, tables):
+def ring_gather(value, axis, tables, direct=1):
     length = lax.axis_size(axis)
     forward, backward = ring_pairs(length)
+    order = ring_order(length)
     ahead = length // 2
     behind = length - 1 - ahead
+    direct = max(1, min(direct, behind))
     rows = value.shape[0]
     split = behind < ahead and rows % 2 == 0
     half = rows // 2
@@ -52,7 +54,12 @@
     pieces[0] = value
     fwd = value
     bwd = value
-    for k in range(1, ahead + 1):
+    for k in range(1, direct + 1):
+        fwd = lax.ppermute(value, axis, [(order[p], order[(p + k) % length]) for p in range(length)])
+        bwd = lax.ppermute(value, axis, [(order[p], order[(p - k) % length]) for p in range(length)])
+        pieces[length - k] = fwd
+        pieces[k] = bwd
+    for k in range(direct + 1, ahead + 1):
         if k == ahead and split:
             fwd = lax.ppermute(fwd[:half], axis, forward)
             bwd = lax.ppermute(bwd[half:], axis, backward)
@@ -242,7 +249,7 @@
     layers = w_conv.shape[0]
     share = stream
     tables = ring_tables("head")
-    state = ring_gather(stream, "head", tables)
+    state = ring_gather(stream, "head", tables, direct=2)
     conv_by_half = jnp.transpose(w_conv, (0, 1, 3, 2, 4))
     for layer_idx in range(layers):
         gated = convolution_gate(

time: 264 us -> 261 us (0.989)
    ppermute x9 -> x5, starting transfers between devices: 13.2 us -> 2.03 us  [ring_gather(): fwd = lax.ppermute(fwd, axis, forward)]
    ppermute x0 -> x8, starting transfers between devices: none -> 10.2 us  [the longest x4 8.71 us: ring_gather(): lax.ppermute(value, axis, [(order[p], order[(p - k) % length]) for p in r...]
    ppermute x0 -> x8, waiting for transfers between devices: none -> 8.32 us  [the longest x4 8.31 us: ring_gather(): lax.ppermute(value, axis, [(order[p], order[(p - k) % length]) for p in r...]
    ppermute x9 -> x5, waiting for transfers between devices: 6.59 us -> 0.01 us  [ring_gather(): fwd = lax.ppermute(fwd, axis, forward)]
    ppermute x9 -> x5, waiting for transfers between devices: 20.7 us -> 14.5 us  [ring_gather(): bwd = lax.ppermute(bwd, axis, backward)]
    ppermute x3, starting transfers between devices: 2.33 us -> 4.98 us  [ring_gather(): bwd = lax.ppermute(bwd[half:], axis, backward)]
    ppermute x3, starting transfers between devices: 4.06 us -> 1.41 us  [ring_gather(): fwd = lax.ppermute(fwd[:half], axis, forward)]
    ppermute x9 -> x5, starting transfers between devices: 6.07 us -> 8.16 us  [ring_gather(): bwd = lax.ppermute(bwd, axis, backward)]
  transfers between devices with their start and end apart: 52 -> 52, of which waited for: 33 -> 31; matrix products, arithmetic and copies ran while one was open for 12% -> 13% of each run, Pallas kernels for 0% -> 0%
where the time goes in v9:
time: 261 us; the launch traced here: 260 us
  waiting for transfers between devices  103 us (39%)
  starting transfers between devices  58.3 us (22%)
  local copies, waits for them, and re-layouts  48.1 us (18%)
  Pallas kernels  21.7 us (8%)
  other arithmetic  17.2 us (7%)
  matrix products  7.99 us (3%)
  between operations  4.25 us (2%)
    ppermute x24, waiting for transfers between devices, chain(): passed = lax.ppermute(part.astype(value.dtype), axis, pairs)  67.9 us
    unnamed x25, local copies, waits for them, and re-layouts  32.8 us
    ppermute x24, starting transfers between devices, chain(): passed = lax.ppermute(part.astype(value.dtype), axis, pairs)  25.4 us
    pallas_call x2, Pallas kernels, convolution_gate(): pl.pallas_call(conv_gate_kernel, out_shape=jax.ShapeDtypeStruct((all_rows...  21.7 us
    ppermute x5, waiting for transfers between devices, ring_gather(): bwd = lax.ppermute(bwd, axis, backward)  14.5 us
    another operation x4, other arithmetic, convolution_gate(): jnp.stack([lax.dynamic_slice_in_dim(padded, border_rows - tap_idx * dilat...  9.79 us
    ppermute x4, starting transfers between devices, ring_gather(): lax.ppermute(value, axis, [(order[p], order[(p - k) % length]) for p in r...  8.71 us
    ppermute x4, waiting for transfers between devices, ring_gather(): lax.ppermute(value, axis, [(order[p], order[(p - k) % length]) for p in r...  8.31 us
  transfers between devices with their start and end apart: 52, of which 31 were waited for; matrix products, arithmetic and copies ran while one was open for 13% of the time, Pallas kernels for 0%

profile of v9, /device:TPU:0, one launch (start us, length us, event | category | flops | bytes accessed | tf_op | source)
XLA Modules:
  0.0 260.4 jit_solution(833525906643993840)
XLA Ops:
  0.0 4.0 %collective-permute-start.1 = (bf16[32,3072]{1,0:T(8,128)(2,1)}, bf16[32,3072]{1,0:T(8,128)(2,1)S(1)}, u32[]{:S(2)}, u32[]{:S(2)}) collective-permute-start(bf16[32,3072]{1,0:T(8,128)(2,1)} %param.22), channel_id=1, source_target_pairs={{0,3},{2,1},{4,0},{6,2},{7,4},{5,6},{3,7},{1,5},{8,11},{10,9},{12,... | collective-permute-start | bytes 589832 | tf_op jit(solution)/shard_map/ppermute | solution.py:59
  4.0 1.6 collective-permute-start
  9.4 1.6 bitcast_dynamic-update-slice_fusion.20
  11.0 19.6 %copy.11 = bf16[2,3,3072,2,384]{4,2,3,1,0:T(8,128)(2,1)} copy(bf16[2,3,3072,2,384]{4,3,2,1,0:T(2,128)(2,1)} %param.25) | data formatting | bytes 56623104 | tf_op args[3]
  31.3 1.8 collective-permute-start.2
  34.8 2.4 collective-permute-done.2
  37.2 1.7 collective-permute-start.6
  40.0 1.8 collective-permute-done.6
  41.9 1.7 collective-permute-done.5
  46.4 2.1 gather_fusion
  51.7 2.2 fusion.19
  53.9 2.4 pad_maximum_fusion.slab_ref
  56.3 10.8 %shard_map.82 = bf16[256,384]{1,0:T(8,128)(2,1)} custom-call(bf16[3,256,3072]{2,1,0:T(8,128)(2,1)} %pad_maximum_fusion.slab_ref, f32[1,3072]{1,0:T(1,128)} %get-tuple-element.124.gain_ref, bf16[2,3,2,3072,384]{4,3,2,1,0:T(8,128)(2,1)} %bitcast.124), custom_call_target="tpu_custom_call" | custom-call | flops 3623878656 | bytes 19070976 | tf_op jit(solution)/shard_map/pallas_call | solution.py:171
  68.7 2.6 %convolution_convert_fusion.2 = bf16[256,3072]{1,0:T(8,128)(2,1)S(1)} fusion(bf16[256,384]{1,0:T(8,128)(2,1)S(1)} %bitcast.139, bf16[2,384,3072]{2,1,0:T(8,128)(2,1)} %param.26), kind=kOutput, calls=%fused_computation.19 | convolution fusion | flops 604766208 | bytes 4128768 | tf_op jit(solution)/shard_map/dot_general | solution.py:131
  71.8 1.7 collective-permute-start.13
  73.5 2.9 %collective-permute-done.9 = bf16[16,3072]{1,0:T(8,128)(2,1)S(1)} collective-permute-done((bf16[16,3072]{1,0:T(8,128)(2,1)S(1)}, bf16[16,3072]{1,0:T(8,128)(2,1)S(1)}, u32[]{:S(2)}, u32[]{:S(2)}) %collective-permute-start.9) | collective-permute-done | bytes 98336 | tf_op jit(solution)/shard_map/ppermute | solution.py:106
  77.0 1.7 collective-permute-start.14
  78.7 4.2 %collective-permute-done.10 = bf16[32,3072]{1,0:T(8,128)(2,1)S(1)} collective-permute-done((bf16[32,3072]{1,0:T(8,128)(2,1)S(1)}, bf16[32,3072]{1,0:T(8,128)(2,1)S(1)}, u32[]{:S(2)}, u32[]{:S(2)}) %collective-permute-start.10) | collective-permute-done | bytes 196640 | tf_op jit(solution)/shard_map/ppermute | solution.py:106
  83.4 5.3 %collective-permute-done.11 = bf16[32,3072]{1,0:T(8,128)(2,1)S(1)} collective-permute-done((bf16[32,3072]{1,0:T(8,128)(2,1)S(1)}, bf16[32,3072]{1,0:T(8,128)(2,1)S(1)}, u32[]{:S(2)}, u32[]{:S(2)}) %collective-permute-start.11) | collective-permute-done | bytes 196640 | tf_op jit(solution)/shard_map/ppermute | solution.py:106
  88.8 1.6 collective-permute-start.15
  90.9 4.6 %collective-permute-done.15 = bf16[32,3072]{1,0:T(8,128)(2,1)S(1)} collective-permute-done((bf16[32,3072]{1,0:T(8,128)(2,1)S(1)}, bf16[32,3072]{1,0:T(8,128)(2,1)S(1)}, u32[]{:S(2)}, u32[]{:S(2)}) %collective-permute-start.15) | collective-permute-done | bytes 196640 | tf_op jit(solution)/shard_map/ppermute | solution.py:106
  95.5 1.6 collective-permute-start.16
  97.2 5.5 %collective-permute-done.16 = bf16[32,3072]{1,0:T(8,128)(2,1)S(1)} collective-permute-done((bf16[32,3072]{1,0:T(8,128)(2,1)S(1)}, bf16[32,3072]{1,0:T(8,128)(2,1)S(1)}, u32[]{:S(2)}, u32[]{:S(2)}) %collective-permute-start.16) | collective-permute-done | bytes 196640 | tf_op jit(solution)/shard_map/ppermute | solution.py:106
  103.5 1.6 collective-permute-start.17
  105.5 4.5 %collective-permute-done.17 = bf16[32,3072]{1,0:T(8,128)(2,1)S(1)} collective-permute-done((bf16[32,3072]{1,0:T(8,128)(2,1)S(1)}, bf16[32,3072]{1,0:T(8,128)(2,1)S(1)}, u32[]{:S(2)}, u32[]{:S(2)}) %collective-permute-start.17) | collective-permute-done | bytes 196640 | tf_op jit(solution)/shard_map/ppermute | solution.py:59
  112.7 2.9 %collective-permute-done.18 = bf16[32,3072]{1,0:T(8,128)(2,1)S(1)} collective-permute-done((bf16[32,3072]{1,0:T(8,128)(2,1)S(1)}, bf16[32,3072]{1,0:T(8,128)(2,1)S(1)}, u32[]{:S(2)}, u32[]{:S(2)}) %collective-permute-start.18) | collective-permute-done | bytes 196640 | tf_op jit(solution)/shard_map/ppermute | solution.py:71
  118.4 2.9 %collective-permute-done.19 = bf16[32,3072]{1,0:T(8,128)(2,1)S(1)} collective-permute-done((bf16[32,3072]{1,0:T(8,128)(2,1)S(1)}, bf16[32,3072]{1,0:T(8,128)(2,1)S(1)}, u32[]{:S(2)}, u32[]{:S(2)}) %collective-permute-start.19) | collective-permute-done | bytes 196640 | tf_op jit(solution)/shard_map/ppermute | solution.py:71
  121.3 1.6 collective-permute-start.24
  124.2 1.8 collective-permute-done.24
  126.0 1.6 collective-permute-done.23
  130.4 2.1 gather_fusion.2
  132.6 2.2 collective-permute-start.25
  136.7 2.8 %fusion.15 = (bf16[1,256,3072]{2,1,0:T(8,128)(2,1)S(1)}, bf16[1,256,3072]{2,1,0:T(8,128)(2,1)S(1)}) fusion(s32[]{:T(128)S(6)} %select_n.23, bf16[256,3072]{1,0:T(8,128)(2,1)S(1)} %bitcast.126, bf16[128,3072]{1,0:T(8,128)(2,1)} %collective-permute-done.25, s32[]{:T(128)S(6)} %select_n.24), kind=kLoop, calls=%fused_computation.38 | loop fusion | flops 6291456 | bytes 5505032 | tf_op jit(solution)/shard_map/stack | solution.py:164
  139.4 2.4 pad_maximum_fusion.1.slab_ref
  141.9 10.8 %shard_map.83 = bf16[256,384]{1,0:T(8,128)(2,1)} custom-call(bf16[3,256,3072]{2,1,0:T(8,128)(2,1)} %pad_maximum_fusion.1.slab_ref, f32[1,3072]{1,0:T(1,128)} %get-tuple-element.125.gain_ref, bf16[2,3,2,3072,384]{4,3,2,1,0:T(8,128)(2,1)} %bitcast.125), custom_call_target="tpu_custom_call" | custom-call | flops 3623878656 | bytes 19070976 | tf_op jit(solution)/shard_map/pallas_call | solution.py:171
  154.2 2.6 %convolution_convert_fusion.1 = bf16[256,3072]{1,0:T(8,128)(2,1)S(1)} fusion(bf16[256,384]{1,0:T(8,128)(2,1)S(1)} %bitcast.140, bf16[2,384,3072]{2,1,0:T(8,128)(2,1)} %param.26), kind=kOutput, calls=%fused_computation.18 | convolution fusion | flops 604766208 | bytes 4128768 | tf_op jit(solution)/shard_map/dot_general | solution.py:131
  157.5 1.6 collective-permute-start.30
  159.1 2.5 collective-permute-done.26
  162.2 1.6 collective-permute-start.31
  163.9 3.5 %collective-permute-done.27 = bf16[32,3072]{1,0:T(8,128)(2,1)S(1)} collective-permute-done((bf16[32,3072]{1,0:T(8,128)(2,1)S(1)}, bf16[32,3072]{1,0:T(8,128)(2,1)S(1)}, u32[]{:S(2)}, u32[]{:S(2)}) %collective-permute-start.27) | collective-permute-done | bytes 196640 | tf_op jit(solution)/shard_map/ppermute | solution.py:106
  168.0 5.2 %collective-permute-done.28 = bf16[32,3072]{1,0:T(8,128)(2,1)S(1)} collective-permute-done((bf16[32,3072]{1,0:T(8,128)(2,1)S(1)}, bf16[32,3072]{1,0:T(8,128)(2,1)S(1)}, u32[]{:S(2)}, u32[]{:S(2)}) %collective-permute-start.28) | collective-permute-done | bytes 196640 | tf_op jit(solution)/shard_map/ppermute | solution.py:106
  173.3 1.6 collective-permute-start.32
  175.3 5.6 %collective-permute-done.32 = bf16[32,3072]{1,0:T(8,128)(2,1)S(1)} collective-permute-done((bf16[32,3072]{1,0:T(8,128)(2,1)S(1)}, bf16[32,3072]{1,0:T(8,128)(2,1)S(1)}, u32[]{:S(2)}, u32[]{:S(2)}) %collective-permute-start.32) | collective-permute-done | bytes 196640 | tf_op jit(solution)/shard_map/ppermute | solution.py:106
  180.9 1.6 collective-permute-start.33
  182.6 5.8 %collective-permute-done.33 = bf16[32,3072]{1,0:T(8,128)(2,1)S(1)} collective-permute-done((bf16[32,3072]{1,0:T(8,128)(2,1)S(1)}, bf16[32,3072]{1,0:T(8,128)(2,1)S(1)}, u32[]{:S(2)}, u32[]{:S(2)}) %collective-permute-start.33) | collective-permute-done | bytes 196640 | tf_op jit(solution)/shard_map/ppermute | solution.py:106
  189.2 1.6 collective-permute-start.34
  191.2 3.8 %collective-permute-done.34 = bf16[32,3072]{1,0:T(8,128)(2,1)S(1)} collective-permute-done((bf16[32,3072]{1,0:T(8,128)(2,1)S(1)}, bf16[32,3072]{1,0:T(8,128)(2,1)S(1)}, u32[]{:S(2)}, u32[]{:S(2)}) %collective-permute-start.34) | collective-permute-done | bytes 196640 | tf_op jit(solution)/shard_map/ppermute | solution.py:59
  195.0 1.6 collective-permute-start.35
  197.8 3.3 %collective-permute-done.35 = bf16[32,3072]{1,0:T(8,128)(2,1)S(1)} collective-permute-done((bf16[32,3072]{1,0:T(8,128)(2,1)S(1)}, bf16[32,3072]{1,0:T(8,128)(2,1)S(1)}, u32[]{:S(2)}, u32[]{:S(2)}) %collective-permute-start.35) | collective-permute-done | bytes 196640 | tf_op jit(solution)/shard_map/ppermute | solution.py:71
  201.0 1.6 collective-permute-start.36
  203.7 2.9 %collective-permute-done.36 = bf16[32,3072]{1,0:T(8,128)(2,1)S(1)} collective-permute-done((bf16[32,3072]{1,0:T(8,128)(2,1)S(1)}, bf16[32,3072]{1,0:T(8,128)(2,1)S(1)}, u32[]{:S(2)}, u32[]{:S(2)}) %collective-permute-start.36) | collective-permute-done | bytes 196640 | tf_op jit(solution)/shard_map/ppermute | solution.py:71
  206.7 1.6 collective-permute-start.41
  209.5 1.8 collective-permute-done.41
  211.4 1.6 collective-permute-done.40
  215.8 2.1 gather_fusion.4
  228.5 1.6 collective-permute-start.48
  230.1 2.5 collective-permute-done.44
  233.3 1.6 collective-permute-start.49
  234.9 5.5 %collective-permute-done.45 = bf16[32,3072]{1,0:T(8,128)(2,1)S(1)} collective-permute-done((bf16[32,3072]{1,0:T(8,128)(2,1)S(1)}, bf16[32,3072]{1,0:T(8,128)(2,1)S(1)}, u32[]{:S(2)}, u32[]{:S(2)}) %collective-permute-start.45) | collective-permute-done | bytes 196640 | tf_op jit(solution)/shard_map/ppermute | solution.py:106
  240.9 6.6 %collective-permute-done.46 = bf16[32,3072]{1,0:T(8,128)(2,1)S(1)} collective-permute-done((bf16[32,3072]{1,0:T(8,128)(2,1)S(1)}, bf16[32,3072]{1,0:T(8,128)(2,1)S(1)}, u32[]{:S(2)}, u32[]{:S(2)}) %collective-permute-start.46) | collective-permute-done | bytes 196640 | tf_op jit(solution)/shard_map/ppermute | solution.py:106
  247.6 1.7 collective-permute-start.50
  249.7 4.2 %collective-permute-done.50 = bf16[32,3072]{1,0:T(8,128)(2,1)S(1)} collective-permute-done((bf16[32,3072]{1,0:T(8,128)(2,1)S(1)}, bf16[32,3072]{1,0:T(8,128)(2,1)S(1)}, u32[]{:S(2)}, u32[]{:S(2)}) %collective-permute-start.50) | collective-permute-done | bytes 196640 | tf_op jit(solution)/shard_map/ppermute | solution.py:106
  253.9 1.7 collective-permute-start.51
  255.6 4.0 %collective-permute-done.51 = bf16[32,3072]{1,0:T(8,128)(2,1)S(1)} collective-permute-done((bf16[32,3072]{1,0:T(8,128)(2,1)S(1)}, bf16[32,3072]{1,0:T(8,128)(2,1)S(1)}, u32[]{:S(2)}, u32[]{:S(2)}) %collective-permute-start.51) | collective-permute-done | bytes 196640 | tf_op jit(solution)/shard_map/ppermute | solution.py:106
  (144 shorter events, 50.8 us)
Async XLA Ops:
  0.0 227.3 %copy-start = (bf16[1,128,3072]{2,1,0:T(8,128)(2,1)S(1)}, bf16[1,128,3072]{2,1,0:T(8,128)(2,1)}, u32[]{:S(2)}) copy-start(bf16[1,128,3072]{2,1,0:T(8,128)(2,1)} %param.28) | copy-start | bytes 2359300
  0.0 31.3 %collective-permute-start.1 = (bf16[32,3072]{1,0:T(8,128)(2,1)}, bf16[32,3072]{1,0:T(8,128)(2,1)S(1)}, u32[]{:S(2)}, u32[]{:S(2)}) collective-permute-start(bf16[32,3072]{1,0:T(8,128)(2,1)} %param.22), channel_id=1, source_target_pairs={{0,3},{2,1},{4,0},{6,2},{7,4},{5,6},{3,7},{1,5},{8,11},{10,9},{12,... | collective-permute-start | bytes 589832 | tf_op jit(solution)/shard_map/ppermute | solution.py:59
  4.0 29.4 %collective-permute-start = (bf16[32,3072]{1,0:T(8,128)(2,1)}, bf16[32,3072]{1,0:T(8,128)(2,1)S(1)}, u32[]{:S(2)}, u32[]{:S(2)}) collective-permute-start(bf16[32,3072]{1,0:T(8,128)(2,1)} %param.22), channel_id=1, source_target_pairs={{0,1},{2,0},{4,2},{6,4},{7,6},{5,7},{3,5},{1,3},{8,9},{10,8},{12,1... | collective-permute-start | bytes 589832 | tf_op jit(solution)/shard_map/ppermute | solution.py:59
  5.6 40.1 %collective-permute-start.7 = (bf16[32,3072]{1,0:T(8,128)(2,1)}, bf16[32,3072]{1,0:T(8,128)(2,1)S(1)}, u32[]{:S(2)}, u32[]{:S(2)}) collective-permute-start(bf16[32,3072]{1,0:T(8,128)(2,1)} %param.22), channel_id=1, source_target_pairs={{0,2},{2,4},{4,6},{6,7},{7,5},{5,3},{3,1},{1,0},{8,10},{10,12},{12... | collective-permute-start | bytes 589832 | tf_op jit(solution)/shard_map/ppermute | solution.py:58
  6.0 27.2 %collective-permute-start.3 = (bf16[32,3072]{1,0:T(8,128)(2,1)}, bf16[32,3072]{1,0:T(8,128)(2,1)S(1)}, u32[]{:S(2)}, u32[]{:S(2)}) collective-permute-start(bf16[32,3072]{1,0:T(8,128)(2,1)} %param.22), channel_id=1, source_target_pairs={{0,4},{2,6},{4,7},{6,5},{7,3},{5,1},{3,0},{1,2},{8,12},{10,14},{12... | collective-permute-start | bytes 589832 | tf_op jit(solution)/shard_map/ppermute | solution.py:58
  31.3 5.9 %collective-permute-start.2 = (bf16[32,3072]{1,0:T(8,128)(2,1)S(1)}, bf16[32,3072]{1,0:T(8,128)(2,1)S(1)}, u32[]{:S(2)}, u32[]{:S(2)}) collective-permute-start(bf16[32,3072]{1,0:T(8,128)(2,1)S(1)} %collective-permute-done.1), channel_id=1, source_target_pairs={{0,1},{2,0},{4,2},{6,4},{7,6},{5,7},{3,5},{1,3},{8,9},{10,8},{12,1... | collective-permute-start | bytes 589832 | tf_op jit(solution)/shard_map/ppermute | solution.py:71
  33.2 5.7 %collective-permute-start.4 = (bf16[32,3072]{1,0:T(8,128)(2,1)S(1)}, bf16[32,3072]{1,0:T(8,128)(2,1)S(1)}, u32[]{:S(2)}, u32[]{:S(2)}) collective-permute-start(bf16[32,3072]{1,0:T(8,128)(2,1)S(1)} %collective-permute-done.3), channel_id=1, source_target_pairs={{0,2},{2,4},{4,6},{6,7},{7,5},{5,3},{3,1},{1,0},{8,10},{10,12},{12... | collective-permute-start | bytes 589832 | tf_op jit(solution)/shard_map/ppermute | solution.py:68
  37.2 4.7 %collective-permute-start.6 = (bf16[16,3072]{1,0:T(8,128)(2,1)S(1)}, bf16[16,3072]{1,0:T(8,128)(2,1)S(1)}, u32[]{:S(2)}, u32[]{:S(2)}) collective-permute-start(bf16[16,3072]{1,0:T(8,128)(2,1)S(1)} %slice.373), channel_id=1, source_target_pairs={{0,1},{2,0},{4,2},{6,4},{7,6},{5,7},{3,5},{1,3},{8,9},{10,8},{12,1... | collective-permute-start | bytes 294920 | tf_op jit(solution)/shard_map/ppermute | solution.py:65
  38.9 4.7 %collective-permute-start.5 = (bf16[16,3072]{1,0:T(8,128)(2,1)S(1)}, bf16[16,3072]{1,0:T(8,128)(2,1)S(1)}, u32[]{:S(2)}, u32[]{:S(2)}) collective-permute-start(bf16[16,3072]{1,0:T(8,128)(2,1)S(1)} %slice.372), channel_id=1, source_target_pairs={{0,2},{2,4},{4,6},{6,7},{7,5},{5,3},{3,1},{1,0},{8,10},{10,12},{12... | collective-permute-start | bytes 294920 | tf_op jit(solution)/shard_map/ppermute | solution.py:64
  48.4 1.4 copy-start.2
  48.5 3.2 %collective-permute-start.8 = (bf16[128,3072]{1,0:T(8,128)(2,1)S(1)}, bf16[128,3072]{1,0:T(8,128)(2,1)S(1)}, u32[]{:S(2)}, u32[]{:S(2)}) collective-permute-start(bf16[128,3072]{1,0:T(8,128)(2,1)S(1)} %bitcast.136), channel_id=1, source_target_pairs={{0,8},{1,9},{2,10},{3,11},{4,12},{5,13},{6,14},{7,15},{16,24},{17,... | collective-permute-start | bytes 2359304 | tf_op jit(solution)/shard_map/ppermute | solution.py:14
  71.3 5.1 %collective-permute-start.9 = (bf16[16,3072]{1,0:T(8,128)(2,1)S(1)}, bf16[16,3072]{1,0:T(8,128)(2,1)S(1)}, u32[]{:S(2)}, u32[]{:S(2)}) collective-permute-start(bf16[16,3072]{1,0:T(8,128)(2,1)S(1)} %get-tuple-element.119), channel_id=1, source_target_pairs={{0,2},{2,4},{4,6},{6,7},{7,5},{5,3},{3,1},{1,0},{8,10},{10,12},{12... | collective-permute-start | bytes 294920 | tf_op jit(solution)/shard_map/ppermute | solution.py:106
  71.8 5.1 %collective-permute-start.13 = (bf16[16,3072]{1,0:T(8,128)(2,1)S(1)}, bf16[16,3072]{1,0:T(8,128)(2,1)S(1)}, u32[]{:S(2)}, u32[]{:S(2)}) collective-permute-start(bf16[16,3072]{1,0:T(8,128)(2,1)S(1)} %get-tuple-element.120), channel_id=1, source_target_pairs={{0,1},{2,0},{4,2},{6,4},{7,6},{5,7},{3,5},{1,3},{8,9},{10,8},{12,1... | collective-permute-start | bytes 294920 | tf_op jit(solution)/shard_map/ppermute | solution.py:106
  76.5 6.4 %collective-permute-start.10 = (bf16[32,3072]{1,0:T(8,128)(2,1)S(1)}, bf16[32,3072]{1,0:T(8,128)(2,1)S(1)}, u32[]{:S(2)}, u32[]{:S(2)}) collective-permute-start(bf16[32,3072]{1,0:T(8,128)(2,1)S(1)} %convert_element_type.301), channel_id=1, source_target_pairs={{0,2},{2,4},{4,6},{6,7},{7,5},{5,3},{3,1},{1,0},{8,10},{10,12},{12... | collective-permute-start | bytes 589832 | tf_op jit(solution)/shard_map/ppermute | solution.py:106
  77.0 25.7 %copy-start.1 = (bf16[32,3072]{1,0:T(8,128)(2,1)S(1)}, bf16[32,3072]{1,0:T(8,128)(2,1)}, u32[]{:S(2)}) copy-start(bf16[32,3072]{1,0:T(8,128)(2,1)} %param.22) | copy-start | bytes 589828
  77.0 6.4 %collective-permute-start.14 = (bf16[32,3072]{1,0:T(8,128)(2,1)S(1)}, bf16[32,3072]{1,0:T(8,128)(2,1)S(1)}, u32[]{:S(2)}, u32[]{:S(2)}) collective-permute-start(bf16[32,3072]{1,0:T(8,128)(2,1)S(1)} %convert_element_type.311), channel_id=1, source_target_pairs={{0,1},{2,0},{4,2},{6,4},{7,6},{5,7},{3,5},{1,3},{8,9},{10,8},{12,1... | collective-permute-start | bytes 589832 | tf_op jit(solution)/shard_map/ppermute | solution.py:106
  83.0 5.7 %collective-permute-start.11 = (bf16[32,3072]{1,0:T(8,128)(2,1)S(1)}, bf16[32,3072]{1,0:T(8,128)(2,1)S(1)}, u32[]{:S(2)}, u32[]{:S(2)}) collective-permute-start(bf16[32,3072]{1,0:T(8,128)(2,1)S(1)} %add_convert_fusion.14), channel_id=1, source_target_pairs={{0,2},{2,4},{4,6},{6,7},{7,5},{5,3},{3,1},{1,0},{8,10},{10,12},{12... | collective-permute-start | bytes 589832 | tf_op jit(solution)/shard_map/ppermute | solution.py:106
  88.8 6.6 %collective-permute-start.15 = (bf16[32,3072]{1,0:T(8,128)(2,1)S(1)}, bf16[32,3072]{1,0:T(8,128)(2,1)S(1)}, u32[]{:S(2)}, u32[]{:S(2)}) collective-permute-start(bf16[32,3072]{1,0:T(8,128)(2,1)S(1)} %get-tuple-element.118), channel_id=1, source_target_pairs={{0,1},{2,0},{4,2},{6,4},{7,6},{5,7},{3,5},{1,3},{8,9},{10,8},{12,1... | collective-permute-start | bytes 589832 | tf_op jit(solution)/shard_map/ppermute | solution.py:106
  90.5 6.7 %collective-permute-start.12 = (bf16[32,3072]{1,0:T(8,128)(2,1)S(1)}, bf16[32,3072]{1,0:T(8,128)(2,1)S(1)}, u32[]{:S(2)}, u32[]{:S(2)}) collective-permute-start(bf16[32,3072]{1,0:T(8,128)(2,1)S(1)} %get-tuple-element.117), channel_id=1, source_target_pairs={{0,2},{2,4},{4,6},{6,7},{7,5},{5,3},{3,1},{1,0},{8,10},{10,12},{12... | collective-permute-start | bytes 589832 | tf_op jit(solution)/shard_map/ppermute | solution.py:106
  95.5 7.1 %collective-permute-start.16 = (bf16[32,3072]{1,0:T(8,128)(2,1)S(1)}, bf16[32,3072]{1,0:T(8,128)(2,1)S(1)}, u32[]{:S(2)}, u32[]{:S(2)}) collective-permute-start(bf16[32,3072]{1,0:T(8,128)(2,1)S(1)} %add_convert_fusion.11), channel_id=1, source_target_pairs={{0,1},{2,0},{4,2},{6,4},{7,6},{5,7},{3,5},{1,3},{8,9},{10,8},{12,1... | collective-permute-start | bytes 589832 | tf_op jit(solution)/shard_map/ppermute | solution.py:106
  103.5 6.5 %collective-permute-start.17 = (bf16[32,3072]{1,0:T(8,128)(2,1)S(1)}, bf16[32,3072]{1,0:T(8,128)(2,1)S(1)}, u32[]{:S(2)}, u32[]{:S(2)}) collective-permute-start(bf16[32,3072]{1,0:T(8,128)(2,1)S(1)} %get-tuple-element.98), channel_id=1, source_target_pairs={{0,1},{2,0},{4,2},{6,4},{7,6},{5,7},{3,5},{1,3},{8,9},{10,8},{12,1... | collective-permute-start | bytes 589832 | tf_op jit(solution)/shard_map/ppermute | solution.py:59
  105.1 6.5 %collective-permute-start.20 = (bf16[32,3072]{1,0:T(8,128)(2,1)S(1)}, bf16[32,3072]{1,0:T(8,128)(2,1)S(1)}, u32[]{:S(2)}, u32[]{:S(2)}) collective-permute-start(bf16[32,3072]{1,0:T(8,128)(2,1)S(1)} %get-tuple-element.98), channel_id=1, source_target_pairs={{0,2},{2,4},{4,6},{6,7},{7,5},{5,3},{3,1},{1,0},{8,10},{10,12},{12... | collective-permute-start | bytes 589832 | tf_op jit(solution)/shard_map/ppermute | solution.py:58
  110.0 5.7 %collective-permute-start.18 = (bf16[32,3072]{1,0:T(8,128)(2,1)S(1)}, bf16[32,3072]{1,0:T(8,128)(2,1)S(1)}, u32[]{:S(2)}, u32[]{:S(2)}) collective-permute-start(bf16[32,3072]{1,0:T(8,128)(2,1)S(1)} %collective-permute-done.17), channel_id=1, source_target_pairs={{0,1},{2,0},{4,2},{6,4},{7,6},{5,7},{3,5},{1,3},{8,9},{10,8},{12,1... | collective-permute-start | bytes 589832 | tf_op jit(solution)/shard_map/ppermute | solution.py:71
  111.6 5.7 %collective-permute-start.21 = (bf16[32,3072]{1,0:T(8,128)(2,1)S(1)}, bf16[32,3072]{1,0:T(8,128)(2,1)S(1)}, u32[]{:S(2)}, u32[]{:S(2)}) collective-permute-start(bf16[32,3072]{1,0:T(8,128)(2,1)S(1)} %collective-permute-done.20), channel_id=1, source_target_pairs={{0,2},{2,4},{4,6},{6,7},{7,5},{5,3},{3,1},{1,0},{8,10},{10,12},{12... | collective-permute-start | bytes 589832 | tf_op jit(solution)/shard_map/ppermute | solution.py:68
  115.7 5.7 %collective-permute-start.19 = (bf16[32,3072]{1,0:T(8,128)(2,1)S(1)}, bf16[32,3072]{1,0:T(8,128)(2,1)S(1)}, u32[]{:S(2)}, u32[]{:S(2)}) collective-permute-start(bf16[32,3072]{1,0:T(8,128)(2,1)S(1)} %collective-permute-done.18), channel_id=1, source_target_pairs={{0,1},{2,0},{4,2},{6,4},{7,6},{5,7},{3,5},{1,3},{8,9},{10,8},{12,1... | collective-permute-start | bytes 589832 | tf_op jit(solution)/shard_map/ppermute | solution.py:71
  117.2 5.7 %collective-permute-start.22 = (bf16[32,3072]{1,0:T(8,128)(2,1)S(1)}, bf16[32,3072]{1,0:T(8,128)(2,1)S(1)}, u32[]{:S(2)}, u32[]{:S(2)}) collective-permute-start(bf16[32,3072]{1,0:T(8,128)(2,1)S(1)} %collective-permute-done.21), channel_id=1, source_target_pairs={{0,2},{2,4},{4,6},{6,7},{7,5},{5,3},{3,1},{1,0},{8,10},{10,12},{12... | collective-permute-start | bytes 589832 | tf_op jit(solution)/shard_map/ppermute | solution.py:68
  121.3 4.7 %collective-permute-start.24 = (bf16[16,3072]{1,0:T(8,128)(2,1)S(1)}, bf16[16,3072]{1,0:T(8,128)(2,1)S(1)}, u32[]{:S(2)}, u32[]{:S(2)}) collective-permute-start(bf16[16,3072]{1,0:T(8,128)(2,1)S(1)} %slice.387), channel_id=1, source_target_pairs={{0,1},{2,0},{4,2},{6,4},{7,6},{5,7},{3,5},{1,3},{8,9},{10,8},{12,1... | collective-permute-start | bytes 294920 | tf_op jit(solution)/shard_map/ppermute | solution.py:65
  123.0 4.7 %collective-permute-start.23 = (bf16[16,3072]{1,0:T(8,128)(2,1)S(1)}, bf16[16,3072]{1,0:T(8,128)(2,1)S(1)}, u32[]{:S(2)}, u32[]{:S(2)}) collective-permute-start(bf16[16,3072]{1,0:T(8,128)(2,1)S(1)} %slice.386), channel_id=1, source_target_pairs={{0,2},{2,4},{4,6},{6,7},{7,5},{5,3},{3,1},{1,0},{8,10},{10,12},{12... | collective-permute-start | bytes 294920 | tf_op jit(solution)/shard_map/ppermute | solution.py:64
  132.6 4.1 %collective-permute-start.25 = (bf16[128,3072]{1,0:T(8,128)(2,1)S(1)}, bf16[128,3072]{1,0:T(8,128)(2,1)}, u32[]{:S(2)}, u32[]{:S(2)}) collective-permute-start(bf16[128,3072]{1,0:T(8,128)(2,1)S(1)} %bitcast.135), channel_id=1, source_target_pairs={{0,8},{1,9},{2,10},{3,11},{4,12},{5,13},{6,14},{7,15},{16,24},{17,... | collective-permute-start | bytes 2359304 | tf_op jit(solution)/shard_map/ppermute | solution.py:14
  156.9 4.7 %collective-permute-start.26 = (bf16[16,3072]{1,0:T(8,128)(2,1)S(1)}, bf16[16,3072]{1,0:T(8,128)(2,1)S(1)}, u32[]{:S(2)}, u32[]{:S(2)}) collective-permute-start(bf16[16,3072]{1,0:T(8,128)(2,1)S(1)} %get-tuple-element.113), channel_id=1, source_target_pairs={{0,2},{2,4},{4,6},{6,7},{7,5},{5,3},{3,1},{1,0},{8,10},{10,12},{12... | collective-permute-start | bytes 294920 | tf_op jit(solution)/shard_map/ppermute | solution.py:106
  157.5 4.7 %collective-permute-start.30 = (bf16[16,3072]{1,0:T(8,128)(2,1)S(1)}, bf16[16,3072]{1,0:T(8,128)(2,1)S(1)}, u32[]{:S(2)}, u32[]{:S(2)}) collective-permute-start(bf16[16,3072]{1,0:T(8,128)(2,1)S(1)} %get-tuple-element.114), channel_id=1, source_target_pairs={{0,1},{2,0},{4,2},{6,4},{7,6},{5,7},{3,5},{1,3},{8,9},{10,8},{12,1... | collective-permute-start | bytes 294920 | tf_op jit(solution)/shard_map/ppermute | solution.py:106
  161.7 5.7 %collective-permute-start.27 = (bf16[32,3072]{1,0:T(8,128)(2,1)S(1)}, bf16[32,3072]{1,0:T(8,128)(2,1)S(1)}, u32[]{:S(2)}, u32[]{:S(2)}) collective-permute-start(bf16[32,3072]{1,0:T(8,128)(2,1)S(1)} %convert_element_type.325), channel_id=1, source_target_pairs={{0,2},{2,4},{4,6},{6,7},{7,5},{5,3},{3,1},{1,0},{8,10},{10,12},{12... | collective-permute-start | bytes 589832 | tf_op jit(solution)/shard_map/ppermute | solution.py:106
  162.2 5.7 %collective-permute-start.31 = (bf16[32,3072]{1,0:T(8,128)(2,1)S(1)}, bf16[32,3072]{1,0:T(8,128)(2,1)S(1)}, u32[]{:S(2)}, u32[]{:S(2)}) collective-permute-start(bf16[32,3072]{1,0:T(8,128)(2,1)S(1)} %convert_element_type.335), channel_id=1, source_target_pairs={{0,1},{2,0},{4,2},{6,4},{7,6},{5,7},{3,5},{1,3},{8,9},{10,8},{12,1... | collective-permute-start | bytes 589832 | tf_op jit(solution)/shard_map/ppermute | solution.py:106
  167.4 5.7 %collective-permute-start.28 = (bf16[32,3072]{1,0:T(8,128)(2,1)S(1)}, bf16[32,3072]{1,0:T(8,128)(2,1)S(1)}, u32[]{:S(2)}, u32[]{:S(2)}) collective-permute-start(bf16[32,3072]{1,0:T(8,128)(2,1)S(1)} %add_convert_fusion.9), channel_id=1, source_target_pairs={{0,2},{2,4},{4,6},{6,7},{7,5},{5,3},{3,1},{1,0},{8,10},{10,12},{12... | collective-permute-start | bytes 589832 | tf_op jit(solution)/shard_map/ppermute | solution.py:106
  173.3 7.6 %collective-permute-start.32 = (bf16[32,3072]{1,0:T(8,128)(2,1)S(1)}, bf16[32,3072]{1,0:T(8,128)(2,1)S(1)}, u32[]{:S(2)}, u32[]{:S(2)}) collective-permute-start(bf16[32,3072]{1,0:T(8,128)(2,1)S(1)} %get-tuple-element.112), channel_id=1, source_target_pairs={{0,1},{2,0},{4,2},{6,4},{7,6},{5,7},{3,5},{1,3},{8,9},{10,8},{12,1... | collective-permute-start | bytes 589832 | tf_op jit(solution)/shard_map/ppermute | solution.py:106
  174.9 7.7 %collective-permute-start.29 = (bf16[32,3072]{1,0:T(8,128)(2,1)S(1)}, bf16[32,3072]{1,0:T(8,128)(2,1)S(1)}, u32[]{:S(2)}, u32[]{:S(2)}) collective-permute-start(bf16[32,3072]{1,0:T(8,128)(2,1)S(1)} %get-tuple-element.111), channel_id=1, source_target_pairs={{0,2},{2,4},{4,6},{6,7},{7,5},{5,3},{3,1},{1,0},{8,10},{10,12},{12... | collective-permute-start | bytes 589832 | tf_op jit(solution)/shard_map/ppermute | solution.py:106
  180.9 7.4 %collective-permute-start.33 = (bf16[32,3072]{1,0:T(8,128)(2,1)S(1)}, bf16[32,3072]{1,0:T(8,128)(2,1)S(1)}, u32[]{:S(2)}, u32[]{:S(2)}) collective-permute-start(bf16[32,3072]{1,0:T(8,128)(2,1)S(1)} %add_convert_fusion.6), channel_id=1, source_target_pairs={{0,1},{2,0},{4,2},{6,4},{7,6},{5,7},{3,5},{1,3},{8,9},{10,8},{12,1... | collective-permute-start | bytes 589832 | tf_op jit(solution)/shard_map/ppermute | solution.py:106
  189.2 5.8 %collective-permute-start.34 = (bf16[32,3072]{1,0:T(8,128)(2,1)S(1)}, bf16[32,3072]{1,0:T(8,128)(2,1)S(1)}, u32[]{:S(2)}, u32[]{:S(2)}) collective-permute-start(bf16[32,3072]{1,0:T(8,128)(2,1)S(1)} %get-tuple-element.96), channel_id=1, source_target_pairs={{0,1},{2,0},{4,2},{6,4},{7,6},{5,7},{3,5},{1,3},{8,9},{10,8},{12,1... | collective-permute-start | bytes 589832 | tf_op jit(solution)/shard_map/ppermute | solution.py:59
  190.8 5.8 %collective-permute-start.37 = (bf16[32,3072]{1,0:T(8,128)(2,1)S(1)}, bf16[32,3072]{1,0:T(8,128)(2,1)S(1)}, u32[]{:S(2)}, u32[]{:S(2)}) collective-permute-start(bf16[32,3072]{1,0:T(8,128)(2,1)S(1)} %get-tuple-element.96), channel_id=1, source_target_pairs={{0,2},{2,4},{4,6},{6,7},{7,5},{5,3},{3,1},{1,0},{8,10},{10,12},{12... | collective-permute-start | bytes 589832 | tf_op jit(solution)/shard_map/ppermute | solution.py:58
  195.0 6.0 %collective-permute-start.35 = (bf16[32,3072]{1,0:T(8,128)(2,1)S(1)}, bf16[32,3072]{1,0:T(8,128)(2,1)S(1)}, u32[]{:S(2)}, u32[]{:S(2)}) collective-permute-start(bf16[32,3072]{1,0:T(8,128)(2,1)S(1)} %collective-permute-done.34), channel_id=1, source_target_pairs={{0,1},{2,0},{4,2},{6,4},{7,6},{5,7},{3,5},{1,3},{8,9},{10,8},{12,1... | collective-permute-start | bytes 589832 | tf_op jit(solution)/shard_map/ppermute | solution.py:71
  196.6 6.0 %collective-permute-start.38 = (bf16[32,3072]{1,0:T(8,128)(2,1)S(1)}, bf16[32,3072]{1,0:T(8,128)(2,1)S(1)}, u32[]{:S(2)}, u32[]{:S(2)}) collective-permute-start(bf16[32,3072]{1,0:T(8,128)(2,1)S(1)} %collective-permute-done.37), channel_id=1, source_target_pairs={{0,2},{2,4},{4,6},{6,7},{7,5},{5,3},{3,1},{1,0},{8,10},{10,12},{12... | collective-permute-start | bytes 589832 | tf_op jit(solution)/shard_map/ppermute | solution.py:68
  201.0 5.7 %collective-permute-start.36 = (bf16[32,3072]{1,0:T(8,128)(2,1)S(1)}, bf16[32,3072]{1,0:T(8,128)(2,1)S(1)}, u32[]{:S(2)}, u32[]{:S(2)}) collective-permute-start(bf16[32,3072]{1,0:T(8,128)(2,1)S(1)} %collective-permute-done.35), channel_id=1, source_target_pairs={{0,1},{2,0},{4,2},{6,4},{7,6},{5,7},{3,5},{1,3},{8,9},{10,8},{12,1... | collective-permute-start | bytes 589832 | tf_op jit(solution)/shard_map/ppermute | solution.py:71
  202.6 5.7 %collective-permute-start.39 = (bf16[32,3072]{1,0:T(8,128)(2,1)S(1)}, bf16[32,3072]{1,0:T(8,128)(2,1)S(1)}, u32[]{:S(2)}, u32[]{:S(2)}) collective-permute-start(bf16[32,3072]{1,0:T(8,128)(2,1)S(1)} %collective-permute-done.38), channel_id=1, source_target_pairs={{0,2},{2,4},{4,6},{6,7},{7,5},{5,3},{3,1},{1,0},{8,10},{10,12},{12... | collective-permute-start | bytes 589832 | tf_op jit(solution)/shard_map/ppermute | solution.py:68
  206.7 4.7 %collective-permute-start.41 = (bf16[16,3072]{1,0:T(8,128)(2,1)S(1)}, bf16[16,3072]{1,0:T(8,128)(2,1)S(1)}, u32[]{:S(2)}, u32[]{:S(2)}) collective-permute-start(bf16[16,3072]{1,0:T(8,128)(2,1)S(1)} %slice.401), channel_id=1, source_target_pairs={{0,1},{2,0},{4,2},{6,4},{7,6},{5,7},{3,5},{1,3},{8,9},{10,8},{12,1... | collective-permute-start | bytes 294920 | tf_op jit(solution)/shard_map/ppermute | solution.py:65
  208.3 4.7 %collective-permute-start.40 = (bf16[16,3072]{1,0:T(8,128)(2,1)S(1)}, bf16[16,3072]{1,0:T(8,128)(2,1)S(1)}, u32[]{:S(2)}, u32[]{:S(2)}) collective-permute-start(bf16[16,3072]{1,0:T(8,128)(2,1)S(1)} %slice.400), channel_id=1, source_target_pairs={{0,2},{2,4},{4,6},{6,7},{7,5},{5,3},{3,1},{1,0},{8,10},{10,12},{12... | collective-permute-start | bytes 294920 | tf_op jit(solution)/shard_map/ppermute | solution.py:64
  218.2 1.7 copy-start.3
  221.6 2.9 %collective-permute-start.42 = (bf16[256,128]{1,0:T(8,128)(2,1)S(1)}, bf16[256,128]{1,0:T(8,128)(2,1)S(1)}, u32[]{:S(2)}, u32[]{:S(2)}) collective-permute-start(bf16[256,128]{1,0:T(8,128)(2,1)S(1)} %convolution_convert_fusion.4), channel_id=1, source_target_pairs={{0,8},{1,9},{2,10},{3,11},{4,12},{5,13},{6,14},{7,15},{16,24},{17,... | collective-permute-start | bytes 196616 | tf_op jit(solution)/shard_map/ppermute | solution.py:14
  222.9 2.2 collective-permute-start.43
  227.9 4.7 %collective-permute-start.44 = (bf16[16,3072]{1,0:T(8,128)(2,1)S(1)}, bf16[16,3072]{1,0:T(8,128)(2,1)S(1)}, u32[]{:S(2)}, u32[]{:S(2)}) collective-permute-start(bf16[16,3072]{1,0:T(8,128)(2,1)S(1)} %get-tuple-element.107), channel_id=1, source_target_pairs={{0,2},{2,4},{4,6},{6,7},{7,5},{5,3},{3,1},{1,0},{8,10},{10,12},{12... | collective-permute-start | bytes 294920 | tf_op jit(solution)/shard_map/ppermute | solution.py:106
  228.5 4.8 %collective-permute-start.48 = (bf16[16,3072]{1,0:T(8,128)(2,1)S(1)}, bf16[16,3072]{1,0:T(8,128)(2,1)S(1)}, u32[]{:S(2)}, u32[]{:S(2)}) collective-permute-start(bf16[16,3072]{1,0:T(8,128)(2,1)S(1)} %get-tuple-element.108), channel_id=1, source_target_pairs={{0,1},{2,0},{4,2},{6,4},{7,6},{5,7},{3,5},{1,3},{8,9},{10,8},{12,1... | collective-permute-start | bytes 294920 | tf_op jit(solution)/shard_map/ppermute | solution.py:106
  232.6 7.7 %collective-permute-start.45 = (bf16[32,3072]{1,0:T(8,128)(2,1)S(1)}, bf16[32,3072]{1,0:T(8,128)(2,1)S(1)}, u32[]{:S(2)}, u32[]{:S(2)}) collective-permute-start(bf16[32,3072]{1,0:T(8,128)(2,1)S(1)} %convert_element_type.358), channel_id=1, source_target_pairs={{0,2},{2,4},{4,6},{6,7},{7,5},{5,3},{3,1},{1,0},{8,10},{10,12},{12... | collective-permute-start | bytes 589832 | tf_op jit(solution)/shard_map/ppermute | solution.py:106
  233.3 7.6 %collective-permute-start.49 = (bf16[32,3072]{1,0:T(8,128)(2,1)S(1)}, bf16[32,3072]{1,0:T(8,128)(2,1)S(1)}, u32[]{:S(2)}, u32[]{:S(2)}) collective-permute-start(bf16[32,3072]{1,0:T(8,128)(2,1)S(1)} %convert_element_type.368), channel_id=1, source_target_pairs={{0,1},{2,0},{4,2},{6,4},{7,6},{5,7},{3,5},{1,3},{8,9},{10,8},{12,1... | collective-permute-start | bytes 589832 | tf_op jit(solution)/shard_map/ppermute | solution.py:106
  240.4 7.1 %collective-permute-start.46 = (bf16[32,3072]{1,0:T(8,128)(2,1)S(1)}, bf16[32,3072]{1,0:T(8,128)(2,1)S(1)}, u32[]{:S(2)}, u32[]{:S(2)}) collective-permute-start(bf16[32,3072]{1,0:T(8,128)(2,1)S(1)} %add_convert_fusion.4), channel_id=1, source_target_pairs={{0,2},{2,4},{4,6},{6,7},{7,5},{5,3},{3,1},{1,0},{8,10},{10,12},{12... | collective-permute-start | bytes 589832 | tf_op jit(solution)/shard_map/ppermute | solution.py:106
  247.6 6.3 %collective-permute-start.50 = (bf16[32,3072]{1,0:T(8,128)(2,1)S(1)}, bf16[32,3072]{1,0:T(8,128)(2,1)S(1)}, u32[]{:S(2)}, u32[]{:S(2)}) collective-permute-start(bf16[32,3072]{1,0:T(8,128)(2,1)S(1)} %get-tuple-element.106), channel_id=1, source_target_pairs={{0,1},{2,0},{4,2},{6,4},{7,6},{5,7},{3,5},{1,3},{8,9},{10,8},{12,1... | collective-permute-start | bytes 589832 | tf_op jit(solution)/shard_map/ppermute | solution.py:106
  249.3 6.3 %collective-permute-start.47 = (bf16[32,3072]{1,0:T(8,128)(2,1)S(1)}, bf16[32,3072]{1,0:T(8,128)(2,1)S(1)}, u32[]{:S(2)}, u32[]{:S(2)}) collective-permute-start(bf16[32,3072]{1,0:T(8,128)(2,1)S(1)} %get-tuple-element.105), channel_id=1, source_target_pairs={{0,2},{2,4},{4,6},{6,7},{7,5},{5,3},{3,1},{1,0},{8,10},{10,12},{12... | collective-permute-start | bytes 589832 | tf_op jit(solution)/shard_map/ppermute | solution.py:106
  253.9 5.7 %collective-permute-start.51 = (bf16[32,3072]{1,0:T(8,128)(2,1)S(1)}, bf16[32,3072]{1,0:T(8,128)(2,1)S(1)}, u32[]{:S(2)}, u32[]{:S(2)}) collective-permute-start(bf16[32,3072]{1,0:T(8,128)(2,1)S(1)} %add_convert_fusion.1), channel_id=1, source_target_pairs={{0,1},{2,0},{4,2},{6,4},{7,6},{5,7},{3,5},{1,3},{8,9},{10,8},{12,1... | collective-permute-start | bytes 589832 | tf_op jit(solution)/shard_map/ppermute | solution.py:106

commit v10 on v9

--- a/solution.py
+++ b/solution.py
@@ -132,60 +132,93 @@
     return lax.optimization_barrier(term.astype(jnp.bfloat16)).astype(jnp.float32)
 
 
-def conv_gate_kernel(slab_ref, gain_ref, weight_ref, out_ref, filt_acc, gate_acc):
-    tap = pl.program_id(0)
-    chunk = pl.program_id(1)
-
-    @pl.when((tap == 0) & (chunk == 0))
-    def _():
-        filt_acc[...] = jnp.zeros_like(filt_acc)
-        gate_acc[...] = jnp.zeros_like(gate_acc)
-
+def normed_rows(slab_ref, gain_ref):
     wide = slab_ref[...].astype(jnp.float32)
     scale = lax.rsqrt(jnp.mean(wide * wide, axis=-1, keepdims=True) + 1e-06)
-    rows = (wide * scale * gain_ref[...]).astype(jnp.bfloat16)
-    filt_acc[...] += jnp.dot(rows, weight_ref[0], preferred_element_type=jnp.float32)
-    gate_acc[...] += jnp.dot(rows, weight_ref[1], preferred_element_type=jnp.float32)
-
-    @pl.when((tap == pl.num_programs(0) - 1) & (chunk == pl.num_programs(1) - 1))
+    return (wide * scale * gain_ref[...]).astype(jnp.bfloat16)
+
+
+def first_tap_kernel(slab_ref, gain_ref, weight_ref, filt_ref, gate_ref):
+    rows = normed_rows(slab_ref, gain_ref)
+    weight = weight_ref[...]
+    filt_ref[...] = jnp.dot(rows, weight[0], preferred_element_type=jnp.float32)
+    gate_ref[...] = jnp.dot(rows, weight[1], preferred_element_type=jnp.float32)
+
+
+def later_taps_kernel(slab_ref, gain_ref, weight_ref, filt_in, gate_in, out_ref, filt_acc, gate_acc):
+    tap = pl.program_id(0)
+
+    @pl.when(tap == 0)
+    def _():
+        filt_acc[...] = filt_in[...]
+        gate_acc[...] = gate_in[...]
+
+    rows = normed_rows(slab_ref, gain_ref)
+    weight = weight_ref[...]
+    filt_acc[...] += jnp.dot(rows, weight[0], preferred_element_type=jnp.float32)
+    gate_acc[...] += jnp.dot(rows, weight[1], preferred_element_type=jnp.float32)
+
+    @pl.when(tap == pl.num_programs(0) - 1)
     def _():
         out_ref[...] = (jnp.tanh(filt_acc[...]) * jax.nn.sigmoid(gate_acc[...])).astype(out_ref.dtype)
 
 
 def convolution_gate(state, gain, conv_by_half, layer_idx, dilation_factor):
-    hidden = state
-    all_rows = hidden.shape[0]
-    width = hidden.shape[1]
+    all_rows = state.shape[0]
+    width = state.shape[1]
     taps = conv_by_half.shape[1]
     own_width = conv_by_half.shape[-1]
     border_rows = 2 * LARGEST_DILATION
-    before = shifted(hidden[all_rows - border_rows :], "blk", 1)
-    padded = jnp.concatenate([before, hidden], axis=0)
+    gain_row = gain.reshape(1, width)
+    acc_shape = jax.ShapeDtypeStruct((all_rows, own_width), jnp.float32)
+    weight_bytes = 2 * 2 * width * own_width
+    filt, gate = pl.pallas_call(
+        first_tap_kernel,
+        out_shape=(acc_shape, acc_shape),
+        grid=(1,),
+        in_specs=[
+            pl.BlockSpec((all_rows, width), lambda t: (0, 0)),
+            pl.BlockSpec((1, width), lambda t: (0, 0)),
+            pl.BlockSpec((None, None, 2, width, own_width), lambda t: (layer_idx, 0, 0, 0, 0)),
+        ],
+        out_specs=(
+            pl.BlockSpec((all_rows, own_width), lambda t: (0, 0)),
+            pl.BlockSpec((all_rows, own_width), lambda t: (0, 0)),
+        ),
+        cost_estimate=pl.CostEstimate(
+            flops=4 * all_rows * width * own_width,
+            transcendentals=0,
+            bytes_accessed=2 * all_rows * width + weight_bytes + 8 * all_rows * own_width,
+        ),
+    )(state, gain_row, conv_by_half)
+    before = shifted(state[all_rows - border_rows :], "blk", 1)
+    padded = jnp.concatenate([before, state], axis=0)
     slabs = jnp.stack(
         [
             lax.dynamic_slice_in_dim(padded, border_rows - tap_idx * dilation_factor, all_rows, 0)
-            for tap_idx in range(taps)
+            for tap_idx in range(1, taps)
         ]
     )
-    chunk = width
     return pl.pallas_call(
-        conv_gate_kernel,
+        later_taps_kernel,
         out_shape=jax.ShapeDtypeStruct((all_rows, own_width), jnp.bfloat16),
-        grid=(taps, width // chunk),
+        grid=(taps - 1,),
         in_specs=[
-            pl.BlockSpec((None, all_rows, chunk), lambda t, k: (t, 0, k)),
-            pl.BlockSpec((1, width), lambda t, k: (0, 0)),
-            pl.BlockSpec((None, None, 2, chunk, own_width), lambda t, k: (layer_idx, t, 0, k, 0)),
+            pl.BlockSpec((None, all_rows, width), lambda t: (t, 0, 0)),
+            pl.BlockSpec((1, width), lambda t: (0, 0)),
+            pl.BlockSpec((None, None, 2, width, own_width), lambda t: (layer_idx, t + 1, 0, 0, 0)),
+            pl.BlockSpec((all_rows, own_width), lambda t: (0, 0)),
+            pl.BlockSpec((all_rows, own_width), lambda t: (0, 0)),
         ],
-        out_specs=pl.BlockSpec((all_rows, own_width), lambda t, k: (0, 0)),
+        out_specs=pl.BlockSpec((all_rows, own_width), lambda t: (0, 0)),
         scratch_shapes=[pltpu.VMEM((all_rows, own_width), jnp.float32)] * 2,
-        compiler_params=pltpu.CompilerParams(dimension_semantics=("arbitrary", "arbitrary")),
+        compiler_params=pltpu.CompilerParams(dimension_semantics=("arbitrary",)),
         cost_estimate=pl.CostEstimate(
-            flops=4 * taps * all_rows * width * own_width,
+            flops=4 * (taps - 1) * all_rows * width * own_width,
             transcendentals=2 * all_rows * own_width,
-            bytes_accessed=2 * taps * (all_rows * width + 2 * width * own_width + all_rows * own_width // taps),
+            bytes_accessed=(taps - 1) * (2 * all_rows * width + weight_bytes) + 10 * all_rows * own_width,
         ),
-    )(slabs, gain.reshape(1, width), conv_by_half)
+    )(slabs, gain_row, conv_by_half, filt, gate)
 
 
 def conv_share(gated, weight, tok_rows, tables):

time: 261 us -> 269 us (1.031)
  Pallas kernels: 21.7 us -> 27.9 us
    pallas_call x2 -> x4, Pallas kernels: 21.7 us -> 27.9 us  [the longest x2 16.4 us: convolution_gate(): pl.pallas_call(later_taps_kernel, out_shape=jax.ShapeDtypeStruct((all_row...]
    unnamed x25 -> x29, local copies, waits for them, and re-layouts: 32.8 us -> 32.9 us
  transfers between devices with their start and end apart: 52 -> 52, of which waited for: 31 -> 33; matrix products, arithmetic and copies ran while one was open for 13% -> 12% of each run, Pallas kernels for 0% -> 4%
where the time goes in v10:
time: 269 us
  waiting for transfers between devices  102 us (38%)
  starting transfers between devices  58.9 us (22%)
  local copies, waits for them, and re-layouts  48.2 us (18%)
  Pallas kernels  27.9 us (10%)
  other arithmetic  19.2 us (7%)
  matrix products  7.99 us (3%)
  between operations  4.44 us (2%)
    ppermute x24, waiting for transfers between devices, chain(): passed = lax.ppermute(part.astype(value.dtype), axis, pairs)  69.5 us
    unnamed x29, local copies, waits for them, and re-layouts  32.9 us
    ppermute x24, starting transfers between devices, chain(): passed = lax.ppermute(part.astype(value.dtype), axis, pairs)  25 us
    pallas_call x2, Pallas kernels, convolution_gate(): pl.pallas_call(later_taps_kernel, out_shape=jax.ShapeDtypeStruct((all_row...  16.4 us
    ppermute x5, waiting for transfers between devices, ring_gather(): bwd = lax.ppermute(bwd, axis, backward)  14.1 us
    another operation x4, other arithmetic, convolution_gate(): jnp.stack([lax.dynamic_slice_in_dim(padded, border_rows - tap_idx * dilat...  11.8 us
    pallas_call x2, Pallas kernels, convolution_gate(): pl.pallas_call(first_tap_kernel, out_shape=(acc_shape, acc_shape), grid=(...  11.5 us
    ppermute x4, starting transfers between devices, ring_gather(): lax.ppermute(value, axis, [(order[p], order[(p - k) % length]) for p in r...  8.49 us
  transfers between devices with their start and end apart: 52, of which 33 were waited for; matrix products, arithmetic and copies ran while one was open for 12% of the time, Pallas kernels for 4%

profile of v10, /device:TPU:0, one launch (start us, length us, event | category | flops | bytes accessed | tf_op | source)
XLA Modules:
  0.0 268.7 jit_solution(730997832732924610)
XLA Ops:
  0.0 4.0 %collective-permute-start.1 = (bf16[32,3072]{1,0:T(8,128)(2,1)}, bf16[32,3072]{1,0:T(8,128)(2,1)S(1)}, u32[]{:S(2)}, u32[]{:S(2)}) collective-permute-start(bf16[32,3072]{1,0:T(8,128)(2,1)} %param.22), channel_id=1, source_target_pairs={{0,3},{2,1},{4,0},{6,2},{7,4},{5,6},{3,7},{1,5},{8,11},{10,9},{12,... | collective-permute-start | bytes 589832 | tf_op jit(solution)/shard_map/ppermute | solution.py:59
  4.0 1.6 collective-permute-start
  9.4 1.6 bitcast_dynamic-update-slice_fusion.20
  11.1 19.6 %copy.11 = bf16[2,3,3072,2,384]{4,2,3,1,0:T(8,128)(2,1)} copy(bf16[2,3,3072,2,384]{4,3,2,1,0:T(2,128)(2,1)} %param.25) | data formatting | bytes 56623104 | tf_op args[3]
  31.4 1.8 collective-permute-start.2
  34.9 2.3 collective-permute-done.2
  37.2 1.7 collective-permute-start.6
  40.1 1.8 collective-permute-done.6
  41.9 1.7 collective-permute-done.5
  46.4 2.1 gather_fusion
  48.6 2.2 collective-permute-start.8
  51.4 5.8 %shard_map.82 = (f32[256,384]{1,0:T(8,128)}, f32[256,384]{1,0:T(8,128)}) custom-call(bf16[256,3072]{1,0:T(8,128)(2,1)} %bitcast.128, f32[1,3072]{1,0:T(1,128)} %get-tuple-element.132.gain_ref, bf16[2,3,2,3072,384]{4,3,2,1,0:T(8,128)(2,1)} %bitcast.122), custom_call_target="tpu_custom_call" | custom-call | flops 1207959552 | bytes 7077888 | tf_op jit(solution)/shard_map/pallas_call | solution.py:175
  57.2 3.9 %fusion.19 = (bf16[1,256,3072]{2,1,0:T(8,128)(2,1)S(1)}, bf16[1,256,3072]{2,1,0:T(8,128)(2,1)S(1)}) fusion(s32[]{:T(128)S(6)} %select_n.21, bf16[256,3072]{1,0:T(8,128)(2,1)} %bitcast.129, bf16[128,3072]{1,0:T(8,128)(2,1)} %collective-permute-done.8, s32[]{:T(128)S(6)} %select_n.22), kind=kLoop, calls=%fused_computation.42 | loop fusion | flops 6291456 | bytes 5505032 | tf_op jit(solution)/shard_map/stack | solution.py:196
  61.1 1.9 pad_maximum_fusion.slab_ref
  63.0 8.2 %shard_map.83 = bf16[256,384]{1,0:T(8,128)(2,1)} custom-call(bf16[2,256,3072]{2,1,0:T(8,128)(2,1)} %pad_maximum_fusion.slab_ref, f32[1,3072]{1,0:T(1,128)} %get-tuple-element.132.gain_ref, bf16[2,3,2,3072,384]{4,3,2,1,0:T(8,128)(2,1)} %bitcast.123, f32[256,384]{1,0:T(8,128)} %get-tuple-element.93.filt_in, f32[256,384]{1,0:T(8,128)} %get-tuple-element.94.gate_in), custom_call_target="tpu_custom_call" | custom-call | flops 2415919104 | bytes 13565952 | tf_op jit(solution)/shard_map/pallas_call | solution.py:202
  71.2 1.5 gather_fusion.1
  72.7 2.7 convolution_convert_fusion.2
  75.9 1.7 collective-permute-start.13
  77.6 2.7 %collective-permute-done.9 = bf16[16,3072]{1,0:T(8,128)(2,1)S(1)} collective-permute-done((bf16[16,3072]{1,0:T(8,128)(2,1)S(1)}, bf16[16,3072]{1,0:T(8,128)(2,1)S(1)}, u32[]{:S(2)}, u32[]{:S(2)}) %collective-permute-start.9) | collective-permute-done | bytes 98336 | tf_op jit(solution)/shard_map/ppermute | solution.py:106
  81.2 1.4 collective-permute-start.14
  82.6 3.8 %collective-permute-done.10 = bf16[32,3072]{1,0:T(8,128)(2,1)S(1)} collective-permute-done((bf16[32,3072]{1,0:T(8,128)(2,1)S(1)}, bf16[32,3072]{1,0:T(8,128)(2,1)S(1)}, u32[]{:S(2)}, u32[]{:S(2)}) %collective-permute-start.10) | collective-permute-done | bytes 196640 | tf_op jit(solution)/shard_map/ppermute | solution.py:106
  87.5 5.5 %collective-permute-done.11 = bf16[32,3072]{1,0:T(8,128)(2,1)S(1)} collective-permute-done((bf16[32,3072]{1,0:T(8,128)(2,1)S(1)}, bf16[32,3072]{1,0:T(8,128)(2,1)S(1)}, u32[]{:S(2)}, u32[]{:S(2)}) %collective-permute-start.11) | collective-permute-done | bytes 196640 | tf_op jit(solution)/shard_map/ppermute | solution.py:106
  93.1 1.6 collective-permute-start.15
  95.2 5.1 %collective-permute-done.15 = bf16[32,3072]{1,0:T(8,128)(2,1)S(1)} collective-permute-done((bf16[32,3072]{1,0:T(8,128)(2,1)S(1)}, bf16[32,3072]{1,0:T(8,128)(2,1)S(1)}, u32[]{:S(2)}, u32[]{:S(2)}) %collective-permute-start.15) | collective-permute-done | bytes 196640 | tf_op jit(solution)/shard_map/ppermute | solution.py:106
  100.3 1.6 collective-permute-start.16
  102.1 5.7 %collective-permute-done.16 = bf16[32,3072]{1,0:T(8,128)(2,1)S(1)} collective-permute-done((bf16[32,3072]{1,0:T(8,128)(2,1)S(1)}, bf16[32,3072]{1,0:T(8,128)(2,1)S(1)}, u32[]{:S(2)}, u32[]{:S(2)}) %collective-permute-start.16) | collective-permute-done | bytes 196640 | tf_op jit(solution)/shard_map/ppermute | solution.py:106
  108.6 1.6 collective-permute-start.17
  110.7 3.8 %collective-permute-done.17 = bf16[32,3072]{1,0:T(8,128)(2,1)S(1)} collective-permute-done((bf16[32,3072]{1,0:T(8,128)(2,1)S(1)}, bf16[32,3072]{1,0:T(8,128)(2,1)S(1)}, u32[]{:S(2)}, u32[]{:S(2)}) %collective-permute-start.17) | collective-permute-done | bytes 196640 | tf_op jit(solution)/shard_map/ppermute | solution.py:59
  114.5 1.6 collective-permute-start.18
  117.2 2.9 %collective-permute-done.18 = bf16[32,3072]{1,0:T(8,128)(2,1)S(1)} collective-permute-done((bf16[32,3072]{1,0:T(8,128)(2,1)S(1)}, bf16[32,3072]{1,0:T(8,128)(2,1)S(1)}, u32[]{:S(2)}, u32[]{:S(2)}) %collective-permute-start.18) | collective-permute-done | bytes 196640 | tf_op jit(solution)/shard_map/ppermute | solution.py:71
  120.1 1.6 collective-permute-start.19
  122.9 2.9 %collective-permute-done.19 = bf16[32,3072]{1,0:T(8,128)(2,1)S(1)} collective-permute-done((bf16[32,3072]{1,0:T(8,128)(2,1)S(1)}, bf16[32,3072]{1,0:T(8,128)(2,1)S(1)}, u32[]{:S(2)}, u32[]{:S(2)}) %collective-permute-start.19) | collective-permute-done | bytes 196640 | tf_op jit(solution)/shard_map/ppermute | solution.py:71
  125.8 1.6 collective-permute-start.24
  128.7 1.8 collective-permute-done.24
  130.5 1.7 collective-permute-done.23
  134.9 2.1 gather_fusion.2
  137.0 2.2 collective-permute-start.25
  141.3 5.8 %shard_map.84 = (f32[256,384]{1,0:T(8,128)}, f32[256,384]{1,0:T(8,128)}) custom-call(bf16[256,3072]{1,0:T(8,128)(2,1)} %bitcast.126, f32[1,3072]{1,0:T(1,128)} %get-tuple-element.133.gain_ref, bf16[2,3,2,3072,384]{4,3,2,1,0:T(8,128)(2,1)} %bitcast.124), custom_call_target="tpu_custom_call" | custom-call | flops 1207959552 | bytes 7077888 | tf_op jit(solution)/shard_map/pallas_call | solution.py:175
  147.1 4.0 %fusion.15 = (bf16[1,256,3072]{2,1,0:T(8,128)(2,1)S(1)}, bf16[1,256,3072]{2,1,0:T(8,128)(2,1)S(1)}) fusion(s32[]{:T(128)S(6)} %select_n.23, bf16[256,3072]{1,0:T(8,128)(2,1)} %bitcast.127, bf16[128,3072]{1,0:T(8,128)(2,1)} %collective-permute-done.25, s32[]{:T(128)S(6)} %select_n.24), kind=kLoop, calls=%fused_computation.38 | loop fusion | flops 6291456 | bytes 5505032 | tf_op jit(solution)/shard_map/stack | solution.py:196
  151.0 1.9 pad_maximum_fusion.1.slab_ref
  153.0 8.2 %shard_map.85 = bf16[256,384]{1,0:T(8,128)(2,1)} custom-call(bf16[2,256,3072]{2,1,0:T(8,128)(2,1)} %pad_maximum_fusion.1.slab_ref, f32[1,3072]{1,0:T(1,128)} %get-tuple-element.133.gain_ref, bf16[2,3,2,3072,384]{4,3,2,1,0:T(8,128)(2,1)} %bitcast.125, f32[256,384]{1,0:T(8,128)} %get-tuple-element.95.filt_in, f32[256,384]{1,0:T(8,128)} %get-tuple-element.96.gate_in), custom_call_target="tpu_custom_call" | custom-call | flops 2415919104 | bytes 13565952 | tf_op jit(solution)/shard_map/pallas_call | solution.py:202
  161.1 1.5 gather_fusion.3
  162.7 2.6 convolution_convert_fusion.1
  165.9 1.6 collective-permute-start.30
  167.5 2.6 collective-permute-done.26
  170.8 1.6 collective-permute-start.31
  172.4 3.9 %collective-permute-done.27 = bf16[32,3072]{1,0:T(8,128)(2,1)S(1)} collective-permute-done((bf16[32,3072]{1,0:T(8,128)(2,1)S(1)}, bf16[32,3072]{1,0:T(8,128)(2,1)S(1)}, u32[]{:S(2)}, u32[]{:S(2)}) %collective-permute-start.27) | collective-permute-done | bytes 196640 | tf_op jit(solution)/shard_map/ppermute | solution.py:106
  176.5 1.8 collective-permute-done.31
  178.3 3.8 %collective-permute-done.28 = bf16[32,3072]{1,0:T(8,128)(2,1)S(1)} collective-permute-done((bf16[32,3072]{1,0:T(8,128)(2,1)S(1)}, bf16[32,3072]{1,0:T(8,128)(2,1)S(1)}, u32[]{:S(2)}, u32[]{:S(2)}) %collective-permute-start.28) | collective-permute-done | bytes 196640 | tf_op jit(solution)/shard_map/ppermute | solution.py:106
  184.3 5.2 %collective-permute-done.32 = bf16[32,3072]{1,0:T(8,128)(2,1)S(1)} collective-permute-done((bf16[32,3072]{1,0:T(8,128)(2,1)S(1)}, bf16[32,3072]{1,0:T(8,128)(2,1)S(1)}, u32[]{:S(2)}, u32[]{:S(2)}) %collective-permute-start.32) | collective-permute-done | bytes 196640 | tf_op jit(solution)/shard_map/ppermute | solution.py:106
  191.0 5.9 %collective-permute-done.33 = bf16[32,3072]{1,0:T(8,128)(2,1)S(1)} collective-permute-done((bf16[32,3072]{1,0:T(8,128)(2,1)S(1)}, bf16[32,3072]{1,0:T(8,128)(2,1)S(1)}, u32[]{:S(2)}, u32[]{:S(2)}) %collective-permute-start.33) | collective-permute-done | bytes 196640 | tf_op jit(solution)/shard_map/ppermute | solution.py:106
  199.8 3.8 %collective-permute-done.34 = bf16[32,3072]{1,0:T(8,128)(2,1)S(1)} collective-permute-done((bf16[32,3072]{1,0:T(8,128)(2,1)S(1)}, bf16[32,3072]{1,0:T(8,128)(2,1)S(1)}, u32[]{:S(2)}, u32[]{:S(2)}) %collective-permute-start.34) | collective-permute-done | bytes 196640 | tf_op jit(solution)/shard_map/ppermute | solution.py:59
  206.3 2.9 %collective-permute-done.35 = bf16[32,3072]{1,0:T(8,128)(2,1)S(1)} collective-permute-done((bf16[32,3072]{1,0:T(8,128)(2,1)S(1)}, bf16[32,3072]{1,0:T(8,128)(2,1)S(1)}, u32[]{:S(2)}, u32[]{:S(2)}) %collective-permute-start.35) | collective-permute-done | bytes 196640 | tf_op jit(solution)/shard_map/ppermute | solution.py:71
  211.9 3.0 %collective-permute-done.36 = bf16[32,3072]{1,0:T(8,128)(2,1)S(1)} collective-permute-done((bf16[32,3072]{1,0:T(8,128)(2,1)S(1)}, bf16[32,3072]{1,0:T(8,128)(2,1)S(1)}, u32[]{:S(2)}, u32[]{:S(2)}) %collective-permute-start.36) | collective-permute-done | bytes 196640 | tf_op jit(solution)/shard_map/ppermute | solution.py:71
  214.9 1.4 collective-permute-start.41
  218.0 1.6 collective-permute-done.41
  219.6 1.7 collective-permute-done.40
  224.1 2.1 gather_fusion.4
  236.9 1.4 collective-permute-start.48
  238.4 2.5 collective-permute-done.44
  243.2 5.5 %collective-permute-done.45 = bf16[32,3072]{1,0:T(8,128)(2,1)S(1)} collective-permute-done((bf16[32,3072]{1,0:T(8,128)(2,1)S(1)}, bf16[32,3072]{1,0:T(8,128)(2,1)S(1)}, u32[]{:S(2)}, u32[]{:S(2)}) %collective-permute-start.45) | collective-permute-done | bytes 196640 | tf_op jit(solution)/shard_map/ppermute | solution.py:106
  249.4 6.4 %collective-permute-done.46 = bf16[32,3072]{1,0:T(8,128)(2,1)S(1)} collective-permute-done((bf16[32,3072]{1,0:T(8,128)(2,1)S(1)}, bf16[32,3072]{1,0:T(8,128)(2,1)S(1)}, u32[]{:S(2)}, u32[]{:S(2)}) %collective-permute-start.46) | collective-permute-done | bytes 196640 | tf_op jit(solution)/shard_map/ppermute | solution.py:106
  258.0 4.2 %collective-permute-done.50 = bf16[32,3072]{1,0:T(8,128)(2,1)S(1)} collective-permute-done((bf16[32,3072]{1,0:T(8,128)(2,1)S(1)}, bf16[32,3072]{1,0:T(8,128)(2,1)S(1)}, u32[]{:S(2)}, u32[]{:S(2)}) %collective-permute-start.50) | collective-permute-done | bytes 196640 | tf_op jit(solution)/shard_map/ppermute | solution.py:106
  263.5 4.4 %collective-permute-done.51 = bf16[32,3072]{1,0:T(8,128)(2,1)S(1)} collective-permute-done((bf16[32,3072]{1,0:T(8,128)(2,1)S(1)}, bf16[32,3072]{1,0:T(8,128)(2,1)S(1)}, u32[]{:S(2)}, u32[]{:S(2)}) %collective-permute-start.51) | collective-permute-done | bytes 196640 | tf_op jit(solution)/shard_map/ppermute | solution.py:106
  (150 shorter events, 56.1 us)
Async XLA Ops:
  0.0 235.6 %copy-start = (bf16[1,128,3072]{2,1,0:T(8,128)(2,1)S(1)}, bf16[1,128,3072]{2,1,0:T(8,128)(2,1)}, u32[]{:S(2)}) copy-start(bf16[1,128,3072]{2,1,0:T(8,128)(2,1)} %param.28) | copy-start | bytes 2359300
  0.0 31.4 %collective-permute-start.1 = (bf16[32,3072]{1,0:T(8,128)(2,1)}, bf16[32,3072]{1,0:T(8,128)(2,1)S(1)}, u32[]{:S(2)}, u32[]{:S(2)}) collective-permute-start(bf16[32,3072]{1,0:T(8,128)(2,1)} %param.22), channel_id=1, source_target_pairs={{0,3},{2,1},{4,0},{6,2},{7,4},{5,6},{3,7},{1,5},{8,11},{10,9},{12,... | collective-permute-start | bytes 589832 | tf_op jit(solution)/shard_map/ppermute | solution.py:59
  4.0 29.5 %collective-permute-start = (bf16[32,3072]{1,0:T(8,128)(2,1)}, bf16[32,3072]{1,0:T(8,128)(2,1)S(1)}, u32[]{:S(2)}, u32[]{:S(2)}) collective-permute-start(bf16[32,3072]{1,0:T(8,128)(2,1)} %param.22), channel_id=1, source_target_pairs={{0,1},{2,0},{4,2},{6,4},{7,6},{5,7},{3,5},{1,3},{8,9},{10,8},{12,1... | collective-permute-start | bytes 589832 | tf_op jit(solution)/shard_map/ppermute | solution.py:59
  5.6 40.2 %collective-permute-start.7 = (bf16[32,3072]{1,0:T(8,128)(2,1)}, bf16[32,3072]{1,0:T(8,128)(2,1)S(1)}, u32[]{:S(2)}, u32[]{:S(2)}) collective-permute-start(bf16[32,3072]{1,0:T(8,128)(2,1)} %param.22), channel_id=1, source_target_pairs={{0,2},{2,4},{4,6},{6,7},{7,5},{5,3},{3,1},{1,0},{8,10},{10,12},{12... | collective-permute-start | bytes 589832 | tf_op jit(solution)/shard_map/ppermute | solution.py:58
  6.0 27.2 %collective-permute-start.3 = (bf16[32,3072]{1,0:T(8,128)(2,1)}, bf16[32,3072]{1,0:T(8,128)(2,1)S(1)}, u32[]{:S(2)}, u32[]{:S(2)}) collective-permute-start(bf16[32,3072]{1,0:T(8,128)(2,1)} %param.22), channel_id=1, source_target_pairs={{0,4},{2,6},{4,7},{6,5},{7,3},{5,1},{3,0},{1,2},{8,12},{10,14},{12... | collective-permute-start | bytes 589832 | tf_op jit(solution)/shard_map/ppermute | solution.py:58
  31.4 5.9 %collective-permute-start.2 = (bf16[32,3072]{1,0:T(8,128)(2,1)S(1)}, bf16[32,3072]{1,0:T(8,128)(2,1)S(1)}, u32[]{:S(2)}, u32[]{:S(2)}) collective-permute-start(bf16[32,3072]{1,0:T(8,128)(2,1)S(1)} %collective-permute-done.1), channel_id=1, source_target_pairs={{0,1},{2,0},{4,2},{6,4},{7,6},{5,7},{3,5},{1,3},{8,9},{10,8},{12,1... | collective-permute-start | bytes 589832 | tf_op jit(solution)/shard_map/ppermute | solution.py:71
  33.2 5.7 %collective-permute-start.4 = (bf16[32,3072]{1,0:T(8,128)(2,1)S(1)}, bf16[32,3072]{1,0:T(8,128)(2,1)S(1)}, u32[]{:S(2)}, u32[]{:S(2)}) collective-permute-start(bf16[32,3072]{1,0:T(8,128)(2,1)S(1)} %collective-permute-done.3), channel_id=1, source_target_pairs={{0,2},{2,4},{4,6},{6,7},{7,5},{5,3},{3,1},{1,0},{8,10},{10,12},{12... | collective-permute-start | bytes 589832 | tf_op jit(solution)/shard_map/ppermute | solution.py:68
  37.2 4.7 %collective-permute-start.6 = (bf16[16,3072]{1,0:T(8,128)(2,1)S(1)}, bf16[16,3072]{1,0:T(8,128)(2,1)S(1)}, u32[]{:S(2)}, u32[]{:S(2)}) collective-permute-start(bf16[16,3072]{1,0:T(8,128)(2,1)S(1)} %slice.373), channel_id=1, source_target_pairs={{0,1},{2,0},{4,2},{6,4},{7,6},{5,7},{3,5},{1,3},{8,9},{10,8},{12,1... | collective-permute-start | bytes 294920 | tf_op jit(solution)/shard_map/ppermute | solution.py:65
  39.0 4.7 %collective-permute-start.5 = (bf16[16,3072]{1,0:T(8,128)(2,1)S(1)}, bf16[16,3072]{1,0:T(8,128)(2,1)S(1)}, u32[]{:S(2)}, u32[]{:S(2)}) collective-permute-start(bf16[16,3072]{1,0:T(8,128)(2,1)S(1)} %slice.372), channel_id=1, source_target_pairs={{0,2},{2,4},{4,6},{6,7},{7,5},{5,3},{3,1},{1,0},{8,10},{10,12},{12... | collective-permute-start | bytes 294920 | tf_op jit(solution)/shard_map/ppermute | solution.py:64
  48.5 2.9 %copy-start.2 = (bf16[8,32,3072]{2,1,0:T(8,128)(2,1)}, bf16[8,32,3072]{2,1,0:T(8,128)(2,1)S(1)}, u32[]{:S(2)}) copy-start(bf16[8,32,3072]{2,1,0:T(8,128)(2,1)S(1)} %gather_fusion) | copy-start | bytes 4718596
  48.5 2.3 copy-start.4
  48.6 8.6 %collective-permute-start.8 = (bf16[128,3072]{1,0:T(8,128)(2,1)S(1)}, bf16[128,3072]{1,0:T(8,128)(2,1)}, u32[]{:S(2)}, u32[]{:S(2)}) collective-permute-start(bf16[128,3072]{1,0:T(8,128)(2,1)S(1)} %bitcast.136), channel_id=1, source_target_pairs={{0,8},{1,9},{2,10},{3,11},{4,12},{5,13},{6,14},{7,15},{16,24},{17,... | collective-permute-start | bytes 2359304 | tf_op jit(solution)/shard_map/ppermute | solution.py:14
  75.4 4.9 %collective-permute-start.9 = (bf16[16,3072]{1,0:T(8,128)(2,1)S(1)}, bf16[16,3072]{1,0:T(8,128)(2,1)S(1)}, u32[]{:S(2)}, u32[]{:S(2)}) collective-permute-start(bf16[16,3072]{1,0:T(8,128)(2,1)S(1)} %get-tuple-element.127), channel_id=1, source_target_pairs={{0,2},{2,4},{4,6},{6,7},{7,5},{5,3},{3,1},{1,0},{8,10},{10,12},{12... | collective-permute-start | bytes 294920 | tf_op jit(solution)/shard_map/ppermute | solution.py:106
  75.9 5.2 %collective-permute-start.13 = (bf16[16,3072]{1,0:T(8,128)(2,1)S(1)}, bf16[16,3072]{1,0:T(8,128)(2,1)S(1)}, u32[]{:S(2)}, u32[]{:S(2)}) collective-permute-start(bf16[16,3072]{1,0:T(8,128)(2,1)S(1)} %get-tuple-element.128), channel_id=1, source_target_pairs={{0,1},{2,0},{4,2},{6,4},{7,6},{5,7},{3,5},{1,3},{8,9},{10,8},{12,1... | collective-permute-start | bytes 294920 | tf_op jit(solution)/shard_map/ppermute | solution.py:106
  80.4 6.1 %collective-permute-start.10 = (bf16[32,3072]{1,0:T(8,128)(2,1)S(1)}, bf16[32,3072]{1,0:T(8,128)(2,1)S(1)}, u32[]{:S(2)}, u32[]{:S(2)}) collective-permute-start(bf16[32,3072]{1,0:T(8,128)(2,1)S(1)} %convert_element_type.301), channel_id=1, source_target_pairs={{0,2},{2,4},{4,6},{6,7},{7,5},{5,3},{3,1},{1,0},{8,10},{10,12},{12... | collective-permute-start | bytes 589832 | tf_op jit(solution)/shard_map/ppermute | solution.py:106
  81.1 26.7 %copy-start.3 = (bf16[32,3072]{1,0:T(8,128)(2,1)S(1)}, bf16[32,3072]{1,0:T(8,128)(2,1)}, u32[]{:S(2)}) copy-start(bf16[32,3072]{1,0:T(8,128)(2,1)} %param.22) | copy-start | bytes 589828
  81.2 6.3 %collective-permute-start.14 = (bf16[32,3072]{1,0:T(8,128)(2,1)S(1)}, bf16[32,3072]{1,0:T(8,128)(2,1)S(1)}, u32[]{:S(2)}, u32[]{:S(2)}) collective-permute-start(bf16[32,3072]{1,0:T(8,128)(2,1)S(1)} %convert_element_type.311), channel_id=1, source_target_pairs={{0,1},{2,0},{4,2},{6,4},{7,6},{5,7},{3,5},{1,3},{8,9},{10,8},{12,1... | collective-permute-start | bytes 589832 | tf_op jit(solution)/shard_map/ppermute | solution.py:106
  86.5 6.5 %collective-permute-start.11 = (bf16[32,3072]{1,0:T(8,128)(2,1)S(1)}, bf16[32,3072]{1,0:T(8,128)(2,1)S(1)}, u32[]{:S(2)}, u32[]{:S(2)}) collective-permute-start(bf16[32,3072]{1,0:T(8,128)(2,1)S(1)} %add_convert_fusion.14), channel_id=1, source_target_pairs={{0,2},{2,4},{4,6},{6,7},{7,5},{5,3},{3,1},{1,0},{8,10},{10,12},{12... | collective-permute-start | bytes 589832 | tf_op jit(solution)/shard_map/ppermute | solution.py:106
  93.1 7.2 %collective-permute-start.15 = (bf16[32,3072]{1,0:T(8,128)(2,1)S(1)}, bf16[32,3072]{1,0:T(8,128)(2,1)S(1)}, u32[]{:S(2)}, u32[]{:S(2)}) collective-permute-start(bf16[32,3072]{1,0:T(8,128)(2,1)S(1)} %get-tuple-element.126), channel_id=1, source_target_pairs={{0,1},{2,0},{4,2},{6,4},{7,6},{5,7},{3,5},{1,3},{8,9},{10,8},{12,1... | collective-permute-start | bytes 589832 | tf_op jit(solution)/shard_map/ppermute | solution.py:106
  94.7 7.4 %collective-permute-start.12 = (bf16[32,3072]{1,0:T(8,128)(2,1)S(1)}, bf16[32,3072]{1,0:T(8,128)(2,1)S(1)}, u32[]{:S(2)}, u32[]{:S(2)}) collective-permute-start(bf16[32,3072]{1,0:T(8,128)(2,1)S(1)} %get-tuple-element.125), channel_id=1, source_target_pairs={{0,2},{2,4},{4,6},{6,7},{7,5},{5,3},{3,1},{1,0},{8,10},{10,12},{12... | collective-permute-start | bytes 589832 | tf_op jit(solution)/shard_map/ppermute | solution.py:106
  100.3 7.5 %collective-permute-start.16 = (bf16[32,3072]{1,0:T(8,128)(2,1)S(1)}, bf16[32,3072]{1,0:T(8,128)(2,1)S(1)}, u32[]{:S(2)}, u32[]{:S(2)}) collective-permute-start(bf16[32,3072]{1,0:T(8,128)(2,1)S(1)} %add_convert_fusion.11), channel_id=1, source_target_pairs={{0,1},{2,0},{4,2},{6,4},{7,6},{5,7},{3,5},{1,3},{8,9},{10,8},{12,1... | collective-permute-start | bytes 589832 | tf_op jit(solution)/shard_map/ppermute | solution.py:106
  108.6 5.8 %collective-permute-start.17 = (bf16[32,3072]{1,0:T(8,128)(2,1)S(1)}, bf16[32,3072]{1,0:T(8,128)(2,1)S(1)}, u32[]{:S(2)}, u32[]{:S(2)}) collective-permute-start(bf16[32,3072]{1,0:T(8,128)(2,1)S(1)} %get-tuple-element.106), channel_id=1, source_target_pairs={{0,1},{2,0},{4,2},{6,4},{7,6},{5,7},{3,5},{1,3},{8,9},{10,8},{12,1... | collective-permute-start | bytes 589832 | tf_op jit(solution)/shard_map/ppermute | solution.py:59
  110.2 5.9 %collective-permute-start.20 = (bf16[32,3072]{1,0:T(8,128)(2,1)S(1)}, bf16[32,3072]{1,0:T(8,128)(2,1)S(1)}, u32[]{:S(2)}, u32[]{:S(2)}) collective-permute-start(bf16[32,3072]{1,0:T(8,128)(2,1)S(1)} %get-tuple-element.106), channel_id=1, source_target_pairs={{0,2},{2,4},{4,6},{6,7},{7,5},{5,3},{3,1},{1,0},{8,10},{10,12},{12... | collective-permute-start | bytes 589832 | tf_op jit(solution)/shard_map/ppermute | solution.py:58
  114.5 5.7 %collective-permute-start.18 = (bf16[32,3072]{1,0:T(8,128)(2,1)S(1)}, bf16[32,3072]{1,0:T(8,128)(2,1)S(1)}, u32[]{:S(2)}, u32[]{:S(2)}) collective-permute-start(bf16[32,3072]{1,0:T(8,128)(2,1)S(1)} %collective-permute-done.17), channel_id=1, source_target_pairs={{0,1},{2,0},{4,2},{6,4},{7,6},{5,7},{3,5},{1,3},{8,9},{10,8},{12,1... | collective-permute-start | bytes 589832 | tf_op jit(solution)/shard_map/ppermute | solution.py:71
  116.1 5.7 %collective-permute-start.21 = (bf16[32,3072]{1,0:T(8,128)(2,1)S(1)}, bf16[32,3072]{1,0:T(8,128)(2,1)S(1)}, u32[]{:S(2)}, u32[]{:S(2)}) collective-permute-start(bf16[32,3072]{1,0:T(8,128)(2,1)S(1)} %collective-permute-done.20), channel_id=1, source_target_pairs={{0,2},{2,4},{4,6},{6,7},{7,5},{5,3},{3,1},{1,0},{8,10},{10,12},{12... | collective-permute-start | bytes 589832 | tf_op jit(solution)/shard_map/ppermute | solution.py:68
  120.1 5.7 %collective-permute-start.19 = (bf16[32,3072]{1,0:T(8,128)(2,1)S(1)}, bf16[32,3072]{1,0:T(8,128)(2,1)S(1)}, u32[]{:S(2)}, u32[]{:S(2)}) collective-permute-start(bf16[32,3072]{1,0:T(8,128)(2,1)S(1)} %collective-permute-done.18), channel_id=1, source_target_pairs={{0,1},{2,0},{4,2},{6,4},{7,6},{5,7},{3,5},{1,3},{8,9},{10,8},{12,1... | collective-permute-start | bytes 589832 | tf_op jit(solution)/shard_map/ppermute | solution.py:71
  121.7 5.7 %collective-permute-start.22 = (bf16[32,3072]{1,0:T(8,128)(2,1)S(1)}, bf16[32,3072]{1,0:T(8,128)(2,1)S(1)}, u32[]{:S(2)}, u32[]{:S(2)}) collective-permute-start(bf16[32,3072]{1,0:T(8,128)(2,1)S(1)} %collective-permute-done.21), channel_id=1, source_target_pairs={{0,2},{2,4},{4,6},{6,7},{7,5},{5,3},{3,1},{1,0},{8,10},{10,12},{12... | collective-permute-start | bytes 589832 | tf_op jit(solution)/shard_map/ppermute | solution.py:68
  125.8 4.7 %collective-permute-start.24 = (bf16[16,3072]{1,0:T(8,128)(2,1)S(1)}, bf16[16,3072]{1,0:T(8,128)(2,1)S(1)}, u32[]{:S(2)}, u32[]{:S(2)}) collective-permute-start(bf16[16,3072]{1,0:T(8,128)(2,1)S(1)} %slice.387), channel_id=1, source_target_pairs={{0,1},{2,0},{4,2},{6,4},{7,6},{5,7},{3,5},{1,3},{8,9},{10,8},{12,1... | collective-permute-start | bytes 294920 | tf_op jit(solution)/shard_map/ppermute | solution.py:65
  127.5 4.7 %collective-permute-start.23 = (bf16[16,3072]{1,0:T(8,128)(2,1)S(1)}, bf16[16,3072]{1,0:T(8,128)(2,1)S(1)}, u32[]{:S(2)}, u32[]{:S(2)}) collective-permute-start(bf16[16,3072]{1,0:T(8,128)(2,1)S(1)} %slice.386), channel_id=1, source_target_pairs={{0,2},{2,4},{4,6},{6,7},{7,5},{5,3},{3,1},{1,0},{8,10},{10,12},{12... | collective-permute-start | bytes 294920 | tf_op jit(solution)/shard_map/ppermute | solution.py:64
  137.0 4.3 %copy-start.1 = (bf16[8,32,3072]{2,1,0:T(8,128)(2,1)}, bf16[8,32,3072]{2,1,0:T(8,128)(2,1)S(1)}, u32[]{:S(2)}) copy-start(bf16[8,32,3072]{2,1,0:T(8,128)(2,1)S(1)} %gather_fusion.2) | copy-start | bytes 4718596
  137.0 10.0 %collective-permute-start.25 = (bf16[128,3072]{1,0:T(8,128)(2,1)S(1)}, bf16[128,3072]{1,0:T(8,128)(2,1)}, u32[]{:S(2)}, u32[]{:S(2)}) collective-permute-start(bf16[128,3072]{1,0:T(8,128)(2,1)S(1)} %bitcast.135), channel_id=1, source_target_pairs={{0,8},{1,9},{2,10},{3,11},{4,12},{5,13},{6,14},{7,15},{16,24},{17,... | collective-permute-start | bytes 2359304 | tf_op jit(solution)/shard_map/ppermute | solution.py:14
  165.3 4.8 %collective-permute-start.26 = (bf16[16,3072]{1,0:T(8,128)(2,1)S(1)}, bf16[16,3072]{1,0:T(8,128)(2,1)S(1)}, u32[]{:S(2)}, u32[]{:S(2)}) collective-permute-start(bf16[16,3072]{1,0:T(8,128)(2,1)S(1)} %get-tuple-element.121), channel_id=1, source_target_pairs={{0,2},{2,4},{4,6},{6,7},{7,5},{5,3},{3,1},{1,0},{8,10},{10,12},{12... | collective-permute-start | bytes 294920 | tf_op jit(solution)/shard_map/ppermute | solution.py:106
  165.9 4.8 %collective-permute-start.30 = (bf16[16,3072]{1,0:T(8,128)(2,1)S(1)}, bf16[16,3072]{1,0:T(8,128)(2,1)S(1)}, u32[]{:S(2)}, u32[]{:S(2)}) collective-permute-start(bf16[16,3072]{1,0:T(8,128)(2,1)S(1)} %get-tuple-element.122), channel_id=1, source_target_pairs={{0,1},{2,0},{4,2},{6,4},{7,6},{5,7},{3,5},{1,3},{8,9},{10,8},{12,1... | collective-permute-start | bytes 294920 | tf_op jit(solution)/shard_map/ppermute | solution.py:106
  170.2 6.1 %collective-permute-start.27 = (bf16[32,3072]{1,0:T(8,128)(2,1)S(1)}, bf16[32,3072]{1,0:T(8,128)(2,1)S(1)}, u32[]{:S(2)}, u32[]{:S(2)}) collective-permute-start(bf16[32,3072]{1,0:T(8,128)(2,1)S(1)} %convert_element_type.325), channel_id=1, source_target_pairs={{0,2},{2,4},{4,6},{6,7},{7,5},{5,3},{3,1},{1,0},{8,10},{10,12},{12... | collective-permute-start | bytes 589832 | tf_op jit(solution)/shard_map/ppermute | solution.py:106
  170.8 7.5 %collective-permute-start.31 = (bf16[32,3072]{1,0:T(8,128)(2,1)S(1)}, bf16[32,3072]{1,0:T(8,128)(2,1)S(1)}, u32[]{:S(2)}, u32[]{:S(2)}) collective-permute-start(bf16[32,3072]{1,0:T(8,128)(2,1)S(1)} %convert_element_type.335), channel_id=1, source_target_pairs={{0,1},{2,0},{4,2},{6,4},{7,6},{5,7},{3,5},{1,3},{8,9},{10,8},{12,1... | collective-permute-start | bytes 589832 | tf_op jit(solution)/shard_map/ppermute | solution.py:106
  176.4 5.7 %collective-permute-start.28 = (bf16[32,3072]{1,0:T(8,128)(2,1)S(1)}, bf16[32,3072]{1,0:T(8,128)(2,1)S(1)}, u32[]{:S(2)}, u32[]{:S(2)}) collective-permute-start(bf16[32,3072]{1,0:T(8,128)(2,1)S(1)} %add_convert_fusion.9), channel_id=1, source_target_pairs={{0,2},{2,4},{4,6},{6,7},{7,5},{5,3},{3,1},{1,0},{8,10},{10,12},{12... | collective-permute-start | bytes 589832 | tf_op jit(solution)/shard_map/ppermute | solution.py:106
  182.2 7.2 %collective-permute-start.32 = (bf16[32,3072]{1,0:T(8,128)(2,1)S(1)}, bf16[32,3072]{1,0:T(8,128)(2,1)S(1)}, u32[]{:S(2)}, u32[]{:S(2)}) collective-permute-start(bf16[32,3072]{1,0:T(8,128)(2,1)S(1)} %get-tuple-element.120), channel_id=1, source_target_pairs={{0,1},{2,0},{4,2},{6,4},{7,6},{5,7},{3,5},{1,3},{8,9},{10,8},{12,1... | collective-permute-start | bytes 589832 | tf_op jit(solution)/shard_map/ppermute | solution.py:106
  183.6 7.4 %collective-permute-start.29 = (bf16[32,3072]{1,0:T(8,128)(2,1)S(1)}, bf16[32,3072]{1,0:T(8,128)(2,1)S(1)}, u32[]{:S(2)}, u32[]{:S(2)}) collective-permute-start(bf16[32,3072]{1,0:T(8,128)(2,1)S(1)} %get-tuple-element.119), channel_id=1, source_target_pairs={{0,2},{2,4},{4,6},{6,7},{7,5},{5,3},{3,1},{1,0},{8,10},{10,12},{12... | collective-permute-start | bytes 589832 | tf_op jit(solution)/shard_map/ppermute | solution.py:106
  189.5 7.4 %collective-permute-start.33 = (bf16[32,3072]{1,0:T(8,128)(2,1)S(1)}, bf16[32,3072]{1,0:T(8,128)(2,1)S(1)}, u32[]{:S(2)}, u32[]{:S(2)}) collective-permute-start(bf16[32,3072]{1,0:T(8,128)(2,1)S(1)} %add_convert_fusion.6), channel_id=1, source_target_pairs={{0,1},{2,0},{4,2},{6,4},{7,6},{5,7},{3,5},{1,3},{8,9},{10,8},{12,1... | collective-permute-start | bytes 589832 | tf_op jit(solution)/shard_map/ppermute | solution.py:106
  197.7 5.8 %collective-permute-start.34 = (bf16[32,3072]{1,0:T(8,128)(2,1)S(1)}, bf16[32,3072]{1,0:T(8,128)(2,1)S(1)}, u32[]{:S(2)}, u32[]{:S(2)}) collective-permute-start(bf16[32,3072]{1,0:T(8,128)(2,1)S(1)} %get-tuple-element.104), channel_id=1, source_target_pairs={{0,1},{2,0},{4,2},{6,4},{7,6},{5,7},{3,5},{1,3},{8,9},{10,8},{12,1... | collective-permute-start | bytes 589832 | tf_op jit(solution)/shard_map/ppermute | solution.py:59
  199.1 5.8 %collective-permute-start.37 = (bf16[32,3072]{1,0:T(8,128)(2,1)S(1)}, bf16[32,3072]{1,0:T(8,128)(2,1)S(1)}, u32[]{:S(2)}, u32[]{:S(2)}) collective-permute-start(bf16[32,3072]{1,0:T(8,128)(2,1)S(1)} %get-tuple-element.104), channel_id=1, source_target_pairs={{0,2},{2,4},{4,6},{6,7},{7,5},{5,3},{3,1},{1,0},{8,10},{10,12},{12... | collective-permute-start | bytes 589832 | tf_op jit(solution)/shard_map/ppermute | solution.py:58
  203.6 5.7 %collective-permute-start.35 = (bf16[32,3072]{1,0:T(8,128)(2,1)S(1)}, bf16[32,3072]{1,0:T(8,128)(2,1)S(1)}, u32[]{:S(2)}, u32[]{:S(2)}) collective-permute-start(bf16[32,3072]{1,0:T(8,128)(2,1)S(1)} %collective-permute-done.34), channel_id=1, source_target_pairs={{0,1},{2,0},{4,2},{6,4},{7,6},{5,7},{3,5},{1,3},{8,9},{10,8},{12,1... | collective-permute-start | bytes 589832 | tf_op jit(solution)/shard_map/ppermute | solution.py:71
  204.9 5.7 %collective-permute-start.38 = (bf16[32,3072]{1,0:T(8,128)(2,1)S(1)}, bf16[32,3072]{1,0:T(8,128)(2,1)S(1)}, u32[]{:S(2)}, u32[]{:S(2)}) collective-permute-start(bf16[32,3072]{1,0:T(8,128)(2,1)S(1)} %collective-permute-done.37), channel_id=1, source_target_pairs={{0,2},{2,4},{4,6},{6,7},{7,5},{5,3},{3,1},{1,0},{8,10},{10,12},{12... | collective-permute-start | bytes 589832 | tf_op jit(solution)/shard_map/ppermute | solution.py:68
  209.2 5.7 %collective-permute-start.36 = (bf16[32,3072]{1,0:T(8,128)(2,1)S(1)}, bf16[32,3072]{1,0:T(8,128)(2,1)S(1)}, u32[]{:S(2)}, u32[]{:S(2)}) collective-permute-start(bf16[32,3072]{1,0:T(8,128)(2,1)S(1)} %collective-permute-done.35), channel_id=1, source_target_pairs={{0,1},{2,0},{4,2},{6,4},{7,6},{5,7},{3,5},{1,3},{8,9},{10,8},{12,1... | collective-permute-start | bytes 589832 | tf_op jit(solution)/shard_map/ppermute | solution.py:71
  210.6 5.7 %collective-permute-start.39 = (bf16[32,3072]{1,0:T(8,128)(2,1)S(1)}, bf16[32,3072]{1,0:T(8,128)(2,1)S(1)}, u32[]{:S(2)}, u32[]{:S(2)}) collective-permute-start(bf16[32,3072]{1,0:T(8,128)(2,1)S(1)} %collective-permute-done.38), channel_id=1, source_target_pairs={{0,2},{2,4},{4,6},{6,7},{7,5},{5,3},{3,1},{1,0},{8,10},{10,12},{12... | collective-permute-start | bytes 589832 | tf_op jit(solution)/shard_map/ppermute | solution.py:68
  214.9 4.7 %collective-permute-start.41 = (bf16[16,3072]{1,0:T(8,128)(2,1)S(1)}, bf16[16,3072]{1,0:T(8,128)(2,1)S(1)}, u32[]{:S(2)}, u32[]{:S(2)}) collective-permute-start(bf16[16,3072]{1,0:T(8,128)(2,1)S(1)} %slice.401), channel_id=1, source_target_pairs={{0,1},{2,0},{4,2},{6,4},{7,6},{5,7},{3,5},{1,3},{8,9},{10,8},{12,1... | collective-permute-start | bytes 294920 | tf_op jit(solution)/shard_map/ppermute | solution.py:65
  216.4 4.9 %collective-permute-start.40 = (bf16[16,3072]{1,0:T(8,128)(2,1)S(1)}, bf16[16,3072]{1,0:T(8,128)(2,1)S(1)}, u32[]{:S(2)}, u32[]{:S(2)}) collective-permute-start(bf16[16,3072]{1,0:T(8,128)(2,1)S(1)} %slice.400), channel_id=1, source_target_pairs={{0,2},{2,4},{4,6},{6,7},{7,5},{5,3},{3,1},{1,0},{8,10},{10,12},{12... | collective-permute-start | bytes 294920 | tf_op jit(solution)/shard_map/ppermute | solution.py:64
  226.5 1.7 copy-start.5
  229.9 2.9 %collective-permute-start.42 = (bf16[256,128]{1,0:T(8,128)(2,1)S(1)}, bf16[256,128]{1,0:T(8,128)(2,1)S(1)}, u32[]{:S(2)}, u32[]{:S(2)}) collective-permute-start(bf16[256,128]{1,0:T(8,128)(2,1)S(1)} %convolution_convert_fusion.4), channel_id=1, source_target_pairs={{0,8},{1,9},{2,10},{3,11},{4,12},{5,13},{6,14},{7,15},{16,24},{17,... | collective-permute-start | bytes 196616 | tf_op jit(solution)/shard_map/ppermute | solution.py:14
  231.2 2.2 collective-permute-start.43
  236.2 4.7 %collective-permute-start.44 = (bf16[16,3072]{1,0:T(8,128)(2,1)S(1)}, bf16[16,3072]{1,0:T(8,128)(2,1)S(1)}, u32[]{:S(2)}, u32[]{:S(2)}) collective-permute-start(bf16[16,3072]{1,0:T(8,128)(2,1)S(1)} %get-tuple-element.115), channel_id=1, source_target_pairs={{0,2},{2,4},{4,6},{6,7},{7,5},{5,3},{3,1},{1,0},{8,10},{10,12},{12... | collective-permute-start | bytes 294920 | tf_op jit(solution)/shard_map/ppermute | solution.py:106
  236.9 4.8 %collective-permute-start.48 = (bf16[16,3072]{1,0:T(8,128)(2,1)S(1)}, bf16[16,3072]{1,0:T(8,128)(2,1)S(1)}, u32[]{:S(2)}, u32[]{:S(2)}) collective-permute-start(bf16[16,3072]{1,0:T(8,128)(2,1)S(1)} %get-tuple-element.116), channel_id=1, source_target_pairs={{0,1},{2,0},{4,2},{6,4},{7,6},{5,7},{3,5},{1,3},{8,9},{10,8},{12,1... | collective-permute-start | bytes 294920 | tf_op jit(solution)/shard_map/ppermute | solution.py:106
  240.9 7.7 %collective-permute-start.45 = (bf16[32,3072]{1,0:T(8,128)(2,1)S(1)}, bf16[32,3072]{1,0:T(8,128)(2,1)S(1)}, u32[]{:S(2)}, u32[]{:S(2)}) collective-permute-start(bf16[32,3072]{1,0:T(8,128)(2,1)S(1)} %convert_element_type.358), channel_id=1, source_target_pairs={{0,2},{2,4},{4,6},{6,7},{7,5},{5,3},{3,1},{1,0},{8,10},{10,12},{12... | collective-permute-start | bytes 589832 | tf_op jit(solution)/shard_map/ppermute | solution.py:106
  241.8 7.6 %collective-permute-start.49 = (bf16[32,3072]{1,0:T(8,128)(2,1)S(1)}, bf16[32,3072]{1,0:T(8,128)(2,1)S(1)}, u32[]{:S(2)}, u32[]{:S(2)}) collective-permute-start(bf16[32,3072]{1,0:T(8,128)(2,1)S(1)} %convert_element_type.368), channel_id=1, source_target_pairs={{0,1},{2,0},{4,2},{6,4},{7,6},{5,7},{3,5},{1,3},{8,9},{10,8},{12,1... | collective-permute-start | bytes 589832 | tf_op jit(solution)/shard_map/ppermute | solution.py:106
  248.7 7.1 %collective-permute-start.46 = (bf16[32,3072]{1,0:T(8,128)(2,1)S(1)}, bf16[32,3072]{1,0:T(8,128)(2,1)S(1)}, u32[]{:S(2)}, u32[]{:S(2)}) collective-permute-start(bf16[32,3072]{1,0:T(8,128)(2,1)S(1)} %add_convert_fusion.4), channel_id=1, source_target_pairs={{0,2},{2,4},{4,6},{6,7},{7,5},{5,3},{3,1},{1,0},{8,10},{10,12},{12... | collective-permute-start | bytes 589832 | tf_op jit(solution)/shard_map/ppermute | solution.py:106
  255.9 6.3 %collective-permute-start.50 = (bf16[32,3072]{1,0:T(8,128)(2,1)S(1)}, bf16[32,3072]{1,0:T(8,128)(2,1)S(1)}, u32[]{:S(2)}, u32[]{:S(2)}) collective-permute-start(bf16[32,3072]{1,0:T(8,128)(2,1)S(1)} %get-tuple-element.114), channel_id=1, source_target_pairs={{0,1},{2,0},{4,2},{6,4},{7,6},{5,7},{3,5},{1,3},{8,9},{10,8},{12,1... | collective-permute-start | bytes 589832 | tf_op jit(solution)/shard_map/ppermute | solution.py:106
  257.1 6.4 %collective-permute-start.47 = (bf16[32,3072]{1,0:T(8,128)(2,1)S(1)}, bf16[32,3072]{1,0:T(8,128)(2,1)S(1)}, u32[]{:S(2)}, u32[]{:S(2)}) collective-permute-start(bf16[32,3072]{1,0:T(8,128)(2,1)S(1)} %get-tuple-element.113), channel_id=1, source_target_pairs={{0,2},{2,4},{4,6},{6,7},{7,5},{5,3},{3,1},{1,0},{8,10},{10,12},{12... | collective-permute-start | bytes 589832 | tf_op jit(solution)/shard_map/ppermute | solution.py:106
  262.2 5.7 %collective-permute-start.51 = (bf16[32,3072]{1,0:T(8,128)(2,1)S(1)}, bf16[32,3072]{1,0:T(8,128)(2,1)S(1)}, u32[]{:S(2)}, u32[]{:S(2)}) collective-permute-start(bf16[32,3072]{1,0:T(8,128)(2,1)S(1)} %add_convert_fusion.1), channel_id=1, source_target_pairs={{0,1},{2,0},{4,2},{6,4},{7,6},{5,7},{3,5},{1,3},{8,9},{10,8},{12,1... | collective-permute-start | bytes 589832 | tf_op jit(solution)/shard_map/ppermute | solution.py:106

commit v11 on v9

--- a/solution.py
+++ b/solution.py
@@ -80,7 +80,7 @@
     return jnp.take(blocks, tables[0], axis=0, mode="clip").reshape(rows_in.shape)
 
 
-def ring_scatter_sum(value, axis, tables):
+def ring_scatter_sum(value, axis, tables, far=None):
     length = lax.axis_size(axis)
     forward, backward = ring_pairs(length)
     ahead = length // 2
@@ -91,6 +91,8 @@
     by_offset = value.reshape((length, rows) + value.shape[1:])
 
     def own(offset):
+        if far is not None and offset % length == ahead:
+            return far.astype(jnp.float32)
         return by_offset[offset % length].astype(jnp.float32)
 
     def chain(offsets, pairs, first_rows):
@@ -188,6 +190,10 @@
     )(slabs, gain.reshape(1, width), conv_by_half)
 
 
+def far_rows(ordered, tok_rows):
+    return ordered[(lax.axis_size("head") // 2) * tok_rows :][:tok_rows]
+
+
 def conv_share(gated, weight, tok_rows, tables):
     gated = ring_ordered(gated, "head", tables)
 
@@ -195,7 +201,10 @@
         return rounded_term(gated, weight)
 
     return ring_scatter_sum(
-        term(jnp.int32(0), tok_rows * lax.axis_size("head")).astype(jnp.bfloat16), "head", tables
+        term(jnp.int32(0), tok_rows * lax.axis_size("head")).astype(jnp.bfloat16),
+        "head",
+        tables,
+        far=rounded_term(far_rows(gated, tok_rows), weight).astype(jnp.bfloat16),
     )
 
 
@@ -206,7 +215,10 @@
         return rounded_term(heads_out, out_block)
 
     return ring_scatter_sum(
-        term(jnp.int32(0), tok_rows * lax.axis_size("head")).astype(jnp.bfloat16), "head", tables
+        term(jnp.int32(0), tok_rows * lax.axis_size("head")).astype(jnp.bfloat16),
+        "head",
+        tables,
+        far=rounded_term(far_rows(heads_out, tok_rows), out_block).astype(jnp.bfloat16),
     )
 
 

time: 261 us -> 260 us (level)
  waiting for transfers between devices: 103 us -> 97.5 us
  matrix products: 7.99 us -> 12.6 us
    ppermute x24, waiting for transfers between devices: 67.9 us -> 62.4 us  [chain(): passed = lax.ppermute(part.astype(value.dtype), axis, pairs)]
    dot_general x3 -> x6, matrix products: 5.85 us -> 10.4 us  [rounded_term(): term = jnp.dot(left, right, preferred_element_type=jnp.float32)]
  transfers between devices with their start and end apart: 52 -> 52, of which waited for: 31 -> 29; matrix products, arithmetic and copies ran while one was open for 13% -> 15% of each run, Pallas kernels for 0% -> 0%
where the time goes in v11:
time: 260 us; the launch traced here: 259 us
  waiting for transfers between devices  97.5 us (38%)
  starting transfers between devices  58.1 us (22%)
  local copies, waits for them, and re-layouts  48.1 us (18%)
  Pallas kernels  21.7 us (8%)
  other arithmetic  17.2 us (7%)
  matrix products  12.6 us (5%)
  between operations  4.29 us (2%)
    ppermute x24, waiting for transfers between devices, chain(): passed = lax.ppermute(part.astype(value.dtype), axis, pairs)  62.4 us
    unnamed x25, local copies, waits for them, and re-layouts  32.8 us
    ppermute x24, starting transfers between devices, chain(): passed = lax.ppermute(part.astype(value.dtype), axis, pairs)  25.2 us
    pallas_call x2, Pallas kernels, convolution_gate(): pl.pallas_call(conv_gate_kernel, out_shape=jax.ShapeDtypeStruct((all_rows...  21.7 us
    ppermute x5, waiting for transfers between devices, ring_gather(): bwd = lax.ppermute(bwd, axis, backward)  14.2 us
    dot_general x6, matrix products, rounded_term(): term = jnp.dot(left, right, preferred_element_type=jnp.float32)  10.4 us
    another operation x4, other arithmetic, convolution_gate(): jnp.stack([lax.dynamic_slice_in_dim(padded, border_rows - tap_idx * dilat...  9.77 us
    ppermute x4, starting transfers between devices, ring_gather(): lax.ppermute(value, axis, [(order[p], order[(p - k) % length]) for p in r...  8.71 us
  transfers between devices with their start and end apart: 52, of which 29 were waited for; matrix products, arithmetic and copies ran while one was open for 15% of the time, Pallas kernels for 0%

profile of v11, /device:TPU:0, one launch (start us, length us, event | category | flops | bytes accessed | tf_op | source)
XLA Modules:
  0.0 259.4 jit_solution(5898473041095432345)
XLA Ops:
  0.0 4.0 %collective-permute-start.1 = (bf16[32,3072]{1,0:T(8,128)(2,1)}, bf16[32,3072]{1,0:T(8,128)(2,1)S(1)}, u32[]{:S(2)}, u32[]{:S(2)}) collective-permute-start(bf16[32,3072]{1,0:T(8,128)(2,1)} %param.22), channel_id=1, source_target_pairs={{0,3},{2,1},{4,0},{6,2},{7,4},{5,6},{3,7},{1,5},{8,11},{10,9},{12,... | collective-permute-start | bytes 589832 | tf_op jit(solution)/shard_map/ppermute | solution.py:59
  9.4 1.6 bitcast_dynamic-update-slice_fusion.20
  11.0 19.6 %copy.11 = bf16[2,3,3072,2,384]{4,2,3,1,0:T(8,128)(2,1)} copy(bf16[2,3,3072,2,384]{4,3,2,1,0:T(2,128)(2,1)} %param.25) | data formatting | bytes 56623104 | tf_op args[3]
  31.3 1.8 collective-permute-start.2
  34.8 2.4 collective-permute-done.2
  37.2 1.7 collective-permute-start.6
  40.0 1.8 collective-permute-done.6
  41.9 1.7 collective-permute-done.5
  46.4 2.1 gather_fusion
  51.7 2.2 fusion.23
  53.9 2.4 pad_maximum_fusion.slab_ref
  56.3 10.8 %shard_map.82 = bf16[256,384]{1,0:T(8,128)(2,1)} custom-call(bf16[3,256,3072]{2,1,0:T(8,128)(2,1)} %pad_maximum_fusion.slab_ref, f32[1,3072]{1,0:T(1,128)} %get-tuple-element.124.gain_ref, bf16[2,3,2,3072,384]{4,3,2,1,0:T(8,128)(2,1)} %bitcast.139), custom_call_target="tpu_custom_call" | custom-call | flops 3623878656 | bytes 19070976 | tf_op jit(solution)/shard_map/pallas_call | solution.py:173
  68.7 2.2 convolution_convert_fusion.4
  71.3 1.7 collective-permute-start.13
  73.0 2.6 %convolution_convert_fusion.2 = bf16[256,3072]{1,0:T(8,128)(2,1)S(1)} fusion(bf16[256,384]{1,0:T(8,128)(2,1)S(1)} %bitcast.154, bf16[2,384,3072]{2,1,0:T(8,128)(2,1)} %param.26), kind=kOutput, calls=%fused_computation.19 | convolution fusion | flops 604766208 | bytes 4128768 | tf_op jit(solution)/shard_map/dot_general | solution.py:133
  76.6 1.7 collective-permute-start.14
  78.3 4.2 %collective-permute-done.10 = bf16[32,3072]{1,0:T(8,128)(2,1)S(1)} collective-permute-done((bf16[32,3072]{1,0:T(8,128)(2,1)S(1)}, bf16[32,3072]{1,0:T(8,128)(2,1)S(1)}, u32[]{:S(2)}, u32[]{:S(2)}) %collective-permute-start.10) | collective-permute-done | bytes 196640 | tf_op jit(solution)/shard_map/ppermute | solution.py:108
  83.0 5.3 %collective-permute-done.11 = bf16[32,3072]{1,0:T(8,128)(2,1)S(1)} collective-permute-done((bf16[32,3072]{1,0:T(8,128)(2,1)S(1)}, bf16[32,3072]{1,0:T(8,128)(2,1)S(1)}, u32[]{:S(2)}, u32[]{:S(2)}) %collective-permute-start.11) | collective-permute-done | bytes 196640 | tf_op jit(solution)/shard_map/ppermute | solution.py:108
  88.4 1.6 collective-permute-start.15
  90.4 4.6 %collective-permute-done.15 = bf16[32,3072]{1,0:T(8,128)(2,1)S(1)} collective-permute-done((bf16[32,3072]{1,0:T(8,128)(2,1)S(1)}, bf16[32,3072]{1,0:T(8,128)(2,1)S(1)}, u32[]{:S(2)}, u32[]{:S(2)}) %collective-permute-start.15) | collective-permute-done | bytes 196640 | tf_op jit(solution)/shard_map/ppermute | solution.py:108
  95.1 1.6 collective-permute-start.16
  96.7 5.5 %collective-permute-done.16 = bf16[32,3072]{1,0:T(8,128)(2,1)S(1)} collective-permute-done((bf16[32,3072]{1,0:T(8,128)(2,1)S(1)}, bf16[32,3072]{1,0:T(8,128)(2,1)S(1)}, u32[]{:S(2)}, u32[]{:S(2)}) %collective-permute-start.16) | collective-permute-done | bytes 196640 | tf_op jit(solution)/shard_map/ppermute | solution.py:108
  103.0 1.6 collective-permute-start.17
  105.0 4.5 %collective-permute-done.17 = bf16[32,3072]{1,0:T(8,128)(2,1)S(1)} collective-permute-done((bf16[32,3072]{1,0:T(8,128)(2,1)S(1)}, bf16[32,3072]{1,0:T(8,128)(2,1)S(1)}, u32[]{:S(2)}, u32[]{:S(2)}) %collective-permute-start.17) | collective-permute-done | bytes 196640 | tf_op jit(solution)/shard_map/ppermute | solution.py:59
  109.5 1.6 collective-permute-start.18
  112.2 2.9 %collective-permute-done.18 = bf16[32,3072]{1,0:T(8,128)(2,1)S(1)} collective-permute-done((bf16[32,3072]{1,0:T(8,128)(2,1)S(1)}, bf16[32,3072]{1,0:T(8,128)(2,1)S(1)}, u32[]{:S(2)}, u32[]{:S(2)}) %collective-permute-start.18) | collective-permute-done | bytes 196640 | tf_op jit(solution)/shard_map/ppermute | solution.py:71
  117.9 2.9 %collective-permute-done.19 = bf16[32,3072]{1,0:T(8,128)(2,1)S(1)} collective-permute-done((bf16[32,3072]{1,0:T(8,128)(2,1)S(1)}, bf16[32,3072]{1,0:T(8,128)(2,1)S(1)}, u32[]{:S(2)}, u32[]{:S(2)}) %collective-permute-start.19) | collective-permute-done | bytes 196640 | tf_op jit(solution)/shard_map/ppermute | solution.py:71
  120.9 1.6 collective-permute-start.24
  123.7 1.8 collective-permute-done.24
  125.5 1.6 collective-permute-done.23
  130.0 2.1 gather_fusion.2
  132.1 2.2 collective-permute-start.25
  136.2 2.8 %fusion.19 = (bf16[1,256,3072]{2,1,0:T(8,128)(2,1)S(1)}, bf16[1,256,3072]{2,1,0:T(8,128)(2,1)S(1)}) fusion(s32[]{:T(128)S(6)} %select_n.23, bf16[256,3072]{1,0:T(8,128)(2,1)S(1)} %bitcast.141, bf16[128,3072]{1,0:T(8,128)(2,1)} %collective-permute-done.25, s32[]{:T(128)S(6)} %select_n.24), kind=kLoop, calls=%fused_computation.45 | loop fusion | flops 6291456 | bytes 5505032 | tf_op jit(solution)/shard_map/stack | solution.py:166
  139.0 2.4 pad_maximum_fusion.1.slab_ref
  141.4 10.8 %shard_map.83 = bf16[256,384]{1,0:T(8,128)(2,1)} custom-call(bf16[3,256,3072]{2,1,0:T(8,128)(2,1)} %pad_maximum_fusion.1.slab_ref, f32[1,3072]{1,0:T(1,128)} %get-tuple-element.125.gain_ref, bf16[2,3,2,3072,384]{4,3,2,1,0:T(8,128)(2,1)} %bitcast.140), custom_call_target="tpu_custom_call" | custom-call | flops 3623878656 | bytes 19070976 | tf_op jit(solution)/shard_map/pallas_call | solution.py:173
  153.7 2.2 convolution_convert_fusion.3
  156.4 1.6 collective-permute-start.30
  158.0 2.6 %convolution_convert_fusion.1 = bf16[256,3072]{1,0:T(8,128)(2,1)S(1)} fusion(bf16[256,384]{1,0:T(8,128)(2,1)S(1)} %bitcast.155, bf16[2,384,3072]{2,1,0:T(8,128)(2,1)} %param.26), kind=kOutput, calls=%fused_computation.18 | convolution fusion | flops 604766208 | bytes 4128768 | tf_op jit(solution)/shard_map/dot_general | solution.py:133
  161.4 1.6 collective-permute-start.31
  163.0 3.7 %collective-permute-done.27 = bf16[32,3072]{1,0:T(8,128)(2,1)S(1)} collective-permute-done((bf16[32,3072]{1,0:T(8,128)(2,1)S(1)}, bf16[32,3072]{1,0:T(8,128)(2,1)S(1)}, u32[]{:S(2)}, u32[]{:S(2)}) %collective-permute-start.27) | collective-permute-done | bytes 196640 | tf_op jit(solution)/shard_map/ppermute | solution.py:108
  167.3 5.2 %collective-permute-done.28 = bf16[32,3072]{1,0:T(8,128)(2,1)S(1)} collective-permute-done((bf16[32,3072]{1,0:T(8,128)(2,1)S(1)}, bf16[32,3072]{1,0:T(8,128)(2,1)S(1)}, u32[]{:S(2)}, u32[]{:S(2)}) %collective-permute-start.28) | collective-permute-done | bytes 196640 | tf_op jit(solution)/shard_map/ppermute | solution.py:108
  172.6 1.6 collective-permute-start.32
  174.7 5.2 %collective-permute-done.32 = bf16[32,3072]{1,0:T(8,128)(2,1)S(1)} collective-permute-done((bf16[32,3072]{1,0:T(8,128)(2,1)S(1)}, bf16[32,3072]{1,0:T(8,128)(2,1)S(1)}, u32[]{:S(2)}, u32[]{:S(2)}) %collective-permute-start.32) | collective-permute-done | bytes 196640 | tf_op jit(solution)/shard_map/ppermute | solution.py:108
  179.9 1.6 collective-permute-start.33
  181.5 6.1 %collective-permute-done.33 = bf16[32,3072]{1,0:T(8,128)(2,1)S(1)} collective-permute-done((bf16[32,3072]{1,0:T(8,128)(2,1)S(1)}, bf16[32,3072]{1,0:T(8,128)(2,1)S(1)}, u32[]{:S(2)}, u32[]{:S(2)}) %collective-permute-start.33) | collective-permute-done | bytes 196640 | tf_op jit(solution)/shard_map/ppermute | solution.py:108
  188.4 1.6 collective-permute-start.34
  190.5 4.1 %collective-permute-done.34 = bf16[32,3072]{1,0:T(8,128)(2,1)S(1)} collective-permute-done((bf16[32,3072]{1,0:T(8,128)(2,1)S(1)}, bf16[32,3072]{1,0:T(8,128)(2,1)S(1)}, u32[]{:S(2)}, u32[]{:S(2)}) %collective-permute-start.34) | collective-permute-done | bytes 196640 | tf_op jit(solution)/shard_map/ppermute | solution.py:59
  194.6 1.6 collective-permute-start.35
  197.3 3.0 %collective-permute-done.35 = bf16[32,3072]{1,0:T(8,128)(2,1)S(1)} collective-permute-done((bf16[32,3072]{1,0:T(8,128)(2,1)S(1)}, bf16[32,3072]{1,0:T(8,128)(2,1)S(1)}, u32[]{:S(2)}, u32[]{:S(2)}) %collective-permute-start.35) | collective-permute-done | bytes 196640 | tf_op jit(solution)/shard_map/ppermute | solution.py:71
  200.3 1.6 collective-permute-start.36
  203.0 2.9 %collective-permute-done.36 = bf16[32,3072]{1,0:T(8,128)(2,1)S(1)} collective-permute-done((bf16[32,3072]{1,0:T(8,128)(2,1)S(1)}, bf16[32,3072]{1,0:T(8,128)(2,1)S(1)}, u32[]{:S(2)}, u32[]{:S(2)}) %collective-permute-start.36) | collective-permute-done | bytes 196640 | tf_op jit(solution)/shard_map/ppermute | solution.py:71
  205.9 1.6 collective-permute-start.41
  208.8 1.8 collective-permute-done.41
  210.6 1.6 collective-permute-done.40
  215.0 2.1 gather_fusion.4
  227.3 1.6 collective-permute-start.48
  229.5 2.0 collective-permute-done.44
  232.2 1.6 collective-permute-start.49
  233.8 5.5 %collective-permute-done.45 = bf16[32,3072]{1,0:T(8,128)(2,1)S(1)} collective-permute-done((bf16[32,3072]{1,0:T(8,128)(2,1)S(1)}, bf16[32,3072]{1,0:T(8,128)(2,1)S(1)}, u32[]{:S(2)}, u32[]{:S(2)}) %collective-permute-start.45) | collective-permute-done | bytes 196640 | tf_op jit(solution)/shard_map/ppermute | solution.py:108
  239.9 6.6 %collective-permute-done.46 = bf16[32,3072]{1,0:T(8,128)(2,1)S(1)} collective-permute-done((bf16[32,3072]{1,0:T(8,128)(2,1)S(1)}, bf16[32,3072]{1,0:T(8,128)(2,1)S(1)}, u32[]{:S(2)}, u32[]{:S(2)}) %collective-permute-start.46) | collective-permute-done | bytes 196640 | tf_op jit(solution)/shard_map/ppermute | solution.py:108
  246.5 1.6 collective-permute-start.50
  248.6 4.2 %collective-permute-done.50 = bf16[32,3072]{1,0:T(8,128)(2,1)S(1)} collective-permute-done((bf16[32,3072]{1,0:T(8,128)(2,1)S(1)}, bf16[32,3072]{1,0:T(8,128)(2,1)S(1)}, u32[]{:S(2)}, u32[]{:S(2)}) %collective-permute-start.50) | collective-permute-done | bytes 196640 | tf_op jit(solution)/shard_map/ppermute | solution.py:108
  252.8 1.6 collective-permute-start.51
  254.5 4.1 %collective-permute-done.51 = bf16[32,3072]{1,0:T(8,128)(2,1)S(1)} collective-permute-done((bf16[32,3072]{1,0:T(8,128)(2,1)S(1)}, bf16[32,3072]{1,0:T(8,128)(2,1)S(1)}, u32[]{:S(2)}, u32[]{:S(2)}) %collective-permute-start.51) | collective-permute-done | bytes 196640 | tf_op jit(solution)/shard_map/ppermute | solution.py:108
  (147 shorter events, 51.4 us)
Async XLA Ops:
  0.0 226.6 %copy-start = (bf16[1,128,3072]{2,1,0:T(8,128)(2,1)S(1)}, bf16[1,128,3072]{2,1,0:T(8,128)(2,1)}, u32[]{:S(2)}) copy-start(bf16[1,128,3072]{2,1,0:T(8,128)(2,1)} %param.28) | copy-start | bytes 2359300
  0.0 31.3 %collective-permute-start.1 = (bf16[32,3072]{1,0:T(8,128)(2,1)}, bf16[32,3072]{1,0:T(8,128)(2,1)S(1)}, u32[]{:S(2)}, u32[]{:S(2)}) collective-permute-start(bf16[32,3072]{1,0:T(8,128)(2,1)} %param.22), channel_id=1, source_target_pairs={{0,3},{2,1},{4,0},{6,2},{7,4},{5,6},{3,7},{1,5},{8,11},{10,9},{12,... | collective-permute-start | bytes 589832 | tf_op jit(solution)/shard_map/ppermute | solution.py:59
  4.0 29.4 %collective-permute-start = (bf16[32,3072]{1,0:T(8,128)(2,1)}, bf16[32,3072]{1,0:T(8,128)(2,1)S(1)}, u32[]{:S(2)}, u32[]{:S(2)}) collective-permute-start(bf16[32,3072]{1,0:T(8,128)(2,1)} %param.22), channel_id=1, source_target_pairs={{0,1},{2,0},{4,2},{6,4},{7,6},{5,7},{3,5},{1,3},{8,9},{10,8},{12,1... | collective-permute-start | bytes 589832 | tf_op jit(solution)/shard_map/ppermute | solution.py:59
  5.6 40.1 %collective-permute-start.7 = (bf16[32,3072]{1,0:T(8,128)(2,1)}, bf16[32,3072]{1,0:T(8,128)(2,1)S(1)}, u32[]{:S(2)}, u32[]{:S(2)}) collective-permute-start(bf16[32,3072]{1,0:T(8,128)(2,1)} %param.22), channel_id=1, source_target_pairs={{0,2},{2,4},{4,6},{6,7},{7,5},{5,3},{3,1},{1,0},{8,10},{10,12},{12... | collective-permute-start | bytes 589832 | tf_op jit(solution)/shard_map/ppermute | solution.py:58
  6.0 27.2 %collective-permute-start.3 = (bf16[32,3072]{1,0:T(8,128)(2,1)}, bf16[32,3072]{1,0:T(8,128)(2,1)S(1)}, u32[]{:S(2)}, u32[]{:S(2)}) collective-permute-start(bf16[32,3072]{1,0:T(8,128)(2,1)} %param.22), channel_id=1, source_target_pairs={{0,4},{2,6},{4,7},{6,5},{7,3},{5,1},{3,0},{1,2},{8,12},{10,14},{12... | collective-permute-start | bytes 589832 | tf_op jit(solution)/shard_map/ppermute | solution.py:58
  31.3 5.9 %collective-permute-start.2 = (bf16[32,3072]{1,0:T(8,128)(2,1)S(1)}, bf16[32,3072]{1,0:T(8,128)(2,1)S(1)}, u32[]{:S(2)}, u32[]{:S(2)}) collective-permute-start(bf16[32,3072]{1,0:T(8,128)(2,1)S(1)} %collective-permute-done.1), channel_id=1, source_target_pairs={{0,1},{2,0},{4,2},{6,4},{7,6},{5,7},{3,5},{1,3},{8,9},{10,8},{12,1... | collective-permute-start | bytes 589832 | tf_op jit(solution)/shard_map/ppermute | solution.py:71
  33.2 5.7 %collective-permute-start.4 = (bf16[32,3072]{1,0:T(8,128)(2,1)S(1)}, bf16[32,3072]{1,0:T(8,128)(2,1)S(1)}, u32[]{:S(2)}, u32[]{:S(2)}) collective-permute-start(bf16[32,3072]{1,0:T(8,128)(2,1)S(1)} %collective-permute-done.3), channel_id=1, source_target_pairs={{0,2},{2,4},{4,6},{6,7},{7,5},{5,3},{3,1},{1,0},{8,10},{10,12},{12... | collective-permute-start | bytes 589832 | tf_op jit(solution)/shard_map/ppermute | solution.py:68
  37.2 4.7 %collective-permute-start.6 = (bf16[16,3072]{1,0:T(8,128)(2,1)S(1)}, bf16[16,3072]{1,0:T(8,128)(2,1)S(1)}, u32[]{:S(2)}, u32[]{:S(2)}) collective-permute-start(bf16[16,3072]{1,0:T(8,128)(2,1)S(1)} %slice.391), channel_id=1, source_target_pairs={{0,1},{2,0},{4,2},{6,4},{7,6},{5,7},{3,5},{1,3},{8,9},{10,8},{12,1... | collective-permute-start | bytes 294920 | tf_op jit(solution)/shard_map/ppermute | solution.py:65
  38.9 4.7 %collective-permute-start.5 = (bf16[16,3072]{1,0:T(8,128)(2,1)S(1)}, bf16[16,3072]{1,0:T(8,128)(2,1)S(1)}, u32[]{:S(2)}, u32[]{:S(2)}) collective-permute-start(bf16[16,3072]{1,0:T(8,128)(2,1)S(1)} %slice.390), channel_id=1, source_target_pairs={{0,2},{2,4},{4,6},{6,7},{7,5},{5,3},{3,1},{1,0},{8,10},{10,12},{12... | collective-permute-start | bytes 294920 | tf_op jit(solution)/shard_map/ppermute | solution.py:64
  48.4 1.4 copy-start.2
  48.5 3.2 %collective-permute-start.8 = (bf16[128,3072]{1,0:T(8,128)(2,1)S(1)}, bf16[128,3072]{1,0:T(8,128)(2,1)S(1)}, u32[]{:S(2)}, u32[]{:S(2)}) collective-permute-start(bf16[128,3072]{1,0:T(8,128)(2,1)S(1)} %bitcast.151), channel_id=1, source_target_pairs={{0,8},{1,9},{2,10},{3,11},{4,12},{5,13},{6,14},{7,15},{16,24},{17,... | collective-permute-start | bytes 2359304 | tf_op jit(solution)/shard_map/ppermute | solution.py:14
  70.9 5.1 %collective-permute-start.9 = (bf16[16,3072]{1,0:T(8,128)(2,1)S(1)}, bf16[16,3072]{1,0:T(8,128)(2,1)S(1)}, u32[]{:S(2)}, u32[]{:S(2)}) collective-permute-start(bf16[16,3072]{1,0:T(8,128)(2,1)S(1)} %get-tuple-element.121), channel_id=1, source_target_pairs={{0,2},{2,4},{4,6},{6,7},{7,5},{5,3},{3,1},{1,0},{8,10},{10,12},{12... | collective-permute-start | bytes 294920 | tf_op jit(solution)/shard_map/ppermute | solution.py:108
  71.3 5.2 %collective-permute-start.13 = (bf16[16,3072]{1,0:T(8,128)(2,1)S(1)}, bf16[16,3072]{1,0:T(8,128)(2,1)S(1)}, u32[]{:S(2)}, u32[]{:S(2)}) collective-permute-start(bf16[16,3072]{1,0:T(8,128)(2,1)S(1)} %get-tuple-element.122), channel_id=1, source_target_pairs={{0,1},{2,0},{4,2},{6,4},{7,6},{5,7},{3,5},{1,3},{8,9},{10,8},{12,1... | collective-permute-start | bytes 294920 | tf_op jit(solution)/shard_map/ppermute | solution.py:108
  76.1 6.4 %collective-permute-start.10 = (bf16[32,3072]{1,0:T(8,128)(2,1)S(1)}, bf16[32,3072]{1,0:T(8,128)(2,1)S(1)}, u32[]{:S(2)}, u32[]{:S(2)}) collective-permute-start(bf16[32,3072]{1,0:T(8,128)(2,1)S(1)} %convert_element_type.317), channel_id=1, source_target_pairs={{0,2},{2,4},{4,6},{6,7},{7,5},{5,3},{3,1},{1,0},{8,10},{10,12},{12... | collective-permute-start | bytes 589832 | tf_op jit(solution)/shard_map/ppermute | solution.py:108
  76.5 25.7 %copy-start.1 = (bf16[32,3072]{1,0:T(8,128)(2,1)S(1)}, bf16[32,3072]{1,0:T(8,128)(2,1)}, u32[]{:S(2)}) copy-start(bf16[32,3072]{1,0:T(8,128)(2,1)} %param.22) | copy-start | bytes 589828
  76.6 6.4 %collective-permute-start.14 = (bf16[32,3072]{1,0:T(8,128)(2,1)S(1)}, bf16[32,3072]{1,0:T(8,128)(2,1)S(1)}, u32[]{:S(2)}, u32[]{:S(2)}) collective-permute-start(bf16[32,3072]{1,0:T(8,128)(2,1)S(1)} %convert_element_type.327), channel_id=1, source_target_pairs={{0,1},{2,0},{4,2},{6,4},{7,6},{5,7},{3,5},{1,3},{8,9},{10,8},{12,1... | collective-permute-start | bytes 589832 | tf_op jit(solution)/shard_map/ppermute | solution.py:108
  82.5 5.7 %collective-permute-start.11 = (bf16[32,3072]{1,0:T(8,128)(2,1)S(1)}, bf16[32,3072]{1,0:T(8,128)(2,1)S(1)}, u32[]{:S(2)}, u32[]{:S(2)}) collective-permute-start(bf16[32,3072]{1,0:T(8,128)(2,1)S(1)} %add_convert_fusion.14), channel_id=1, source_target_pairs={{0,2},{2,4},{4,6},{6,7},{7,5},{5,3},{3,1},{1,0},{8,10},{10,12},{12... | collective-permute-start | bytes 589832 | tf_op jit(solution)/shard_map/ppermute | solution.py:108
  88.4 6.6 %collective-permute-start.15 = (bf16[32,3072]{1,0:T(8,128)(2,1)S(1)}, bf16[32,3072]{1,0:T(8,128)(2,1)S(1)}, u32[]{:S(2)}, u32[]{:S(2)}) collective-permute-start(bf16[32,3072]{1,0:T(8,128)(2,1)S(1)} %get-tuple-element.114), channel_id=1, source_target_pairs={{0,1},{2,0},{4,2},{6,4},{7,6},{5,7},{3,5},{1,3},{8,9},{10,8},{12,1... | collective-permute-start | bytes 589832 | tf_op jit(solution)/shard_map/ppermute | solution.py:108
  90.0 6.7 %collective-permute-start.12 = (bf16[32,3072]{1,0:T(8,128)(2,1)S(1)}, bf16[32,3072]{1,0:T(8,128)(2,1)S(1)}, u32[]{:S(2)}, u32[]{:S(2)}) collective-permute-start(bf16[32,3072]{1,0:T(8,128)(2,1)S(1)} %get-tuple-element.113), channel_id=1, source_target_pairs={{0,2},{2,4},{4,6},{6,7},{7,5},{5,3},{3,1},{1,0},{8,10},{10,12},{12... | collective-permute-start | bytes 589832 | tf_op jit(solution)/shard_map/ppermute | solution.py:108
  95.1 7.1 %collective-permute-start.16 = (bf16[32,3072]{1,0:T(8,128)(2,1)S(1)}, bf16[32,3072]{1,0:T(8,128)(2,1)S(1)}, u32[]{:S(2)}, u32[]{:S(2)}) collective-permute-start(bf16[32,3072]{1,0:T(8,128)(2,1)S(1)} %add_convert_fusion.11), channel_id=1, source_target_pairs={{0,1},{2,0},{4,2},{6,4},{7,6},{5,7},{3,5},{1,3},{8,9},{10,8},{12,1... | collective-permute-start | bytes 589832 | tf_op jit(solution)/shard_map/ppermute | solution.py:108
  103.0 6.5 %collective-permute-start.17 = (bf16[32,3072]{1,0:T(8,128)(2,1)S(1)}, bf16[32,3072]{1,0:T(8,128)(2,1)S(1)}, u32[]{:S(2)}, u32[]{:S(2)}) collective-permute-start(bf16[32,3072]{1,0:T(8,128)(2,1)S(1)} %get-tuple-element.98), channel_id=1, source_target_pairs={{0,1},{2,0},{4,2},{6,4},{7,6},{5,7},{3,5},{1,3},{8,9},{10,8},{12,1... | collective-permute-start | bytes 589832 | tf_op jit(solution)/shard_map/ppermute | solution.py:59
  104.6 6.5 %collective-permute-start.20 = (bf16[32,3072]{1,0:T(8,128)(2,1)S(1)}, bf16[32,3072]{1,0:T(8,128)(2,1)S(1)}, u32[]{:S(2)}, u32[]{:S(2)}) collective-permute-start(bf16[32,3072]{1,0:T(8,128)(2,1)S(1)} %get-tuple-element.98), channel_id=1, source_target_pairs={{0,2},{2,4},{4,6},{6,7},{7,5},{5,3},{3,1},{1,0},{8,10},{10,12},{12... | collective-permute-start | bytes 589832 | tf_op jit(solution)/shard_map/ppermute | solution.py:58
  109.5 5.7 %collective-permute-start.18 = (bf16[32,3072]{1,0:T(8,128)(2,1)S(1)}, bf16[32,3072]{1,0:T(8,128)(2,1)S(1)}, u32[]{:S(2)}, u32[]{:S(2)}) collective-permute-start(bf16[32,3072]{1,0:T(8,128)(2,1)S(1)} %collective-permute-done.17), channel_id=1, source_target_pairs={{0,1},{2,0},{4,2},{6,4},{7,6},{5,7},{3,5},{1,3},{8,9},{10,8},{12,1... | collective-permute-start | bytes 589832 | tf_op jit(solution)/shard_map/ppermute | solution.py:71
  111.1 5.7 %collective-permute-start.21 = (bf16[32,3072]{1,0:T(8,128)(2,1)S(1)}, bf16[32,3072]{1,0:T(8,128)(2,1)S(1)}, u32[]{:S(2)}, u32[]{:S(2)}) collective-permute-start(bf16[32,3072]{1,0:T(8,128)(2,1)S(1)} %collective-permute-done.20), channel_id=1, source_target_pairs={{0,2},{2,4},{4,6},{6,7},{7,5},{5,3},{3,1},{1,0},{8,10},{10,12},{12... | collective-permute-start | bytes 589832 | tf_op jit(solution)/shard_map/ppermute | solution.py:68
  115.2 5.7 %collective-permute-start.19 = (bf16[32,3072]{1,0:T(8,128)(2,1)S(1)}, bf16[32,3072]{1,0:T(8,128)(2,1)S(1)}, u32[]{:S(2)}, u32[]{:S(2)}) collective-permute-start(bf16[32,3072]{1,0:T(8,128)(2,1)S(1)} %collective-permute-done.18), channel_id=1, source_target_pairs={{0,1},{2,0},{4,2},{6,4},{7,6},{5,7},{3,5},{1,3},{8,9},{10,8},{12,1... | collective-permute-start | bytes 589832 | tf_op jit(solution)/shard_map/ppermute | solution.py:71
  116.8 5.7 %collective-permute-start.22 = (bf16[32,3072]{1,0:T(8,128)(2,1)S(1)}, bf16[32,3072]{1,0:T(8,128)(2,1)S(1)}, u32[]{:S(2)}, u32[]{:S(2)}) collective-permute-start(bf16[32,3072]{1,0:T(8,128)(2,1)S(1)} %collective-permute-done.21), channel_id=1, source_target_pairs={{0,2},{2,4},{4,6},{6,7},{7,5},{5,3},{3,1},{1,0},{8,10},{10,12},{12... | collective-permute-start | bytes 589832 | tf_op jit(solution)/shard_map/ppermute | solution.py:68
  120.9 4.7 %collective-permute-start.24 = (bf16[16,3072]{1,0:T(8,128)(2,1)S(1)}, bf16[16,3072]{1,0:T(8,128)(2,1)S(1)}, u32[]{:S(2)}, u32[]{:S(2)}) collective-permute-start(bf16[16,3072]{1,0:T(8,128)(2,1)S(1)} %slice.406), channel_id=1, source_target_pairs={{0,1},{2,0},{4,2},{6,4},{7,6},{5,7},{3,5},{1,3},{8,9},{10,8},{12,1... | collective-permute-start | bytes 294920 | tf_op jit(solution)/shard_map/ppermute | solution.py:65
  122.5 4.7 %collective-permute-start.23 = (bf16[16,3072]{1,0:T(8,128)(2,1)S(1)}, bf16[16,3072]{1,0:T(8,128)(2,1)S(1)}, u32[]{:S(2)}, u32[]{:S(2)}) collective-permute-start(bf16[16,3072]{1,0:T(8,128)(2,1)S(1)} %slice.405), channel_id=1, source_target_pairs={{0,2},{2,4},{4,6},{6,7},{7,5},{5,3},{3,1},{1,0},{8,10},{10,12},{12... | collective-permute-start | bytes 294920 | tf_op jit(solution)/shard_map/ppermute | solution.py:64
  132.1 4.1 %collective-permute-start.25 = (bf16[128,3072]{1,0:T(8,128)(2,1)S(1)}, bf16[128,3072]{1,0:T(8,128)(2,1)}, u32[]{:S(2)}, u32[]{:S(2)}) collective-permute-start(bf16[128,3072]{1,0:T(8,128)(2,1)S(1)} %bitcast.150), channel_id=1, source_target_pairs={{0,8},{1,9},{2,10},{3,11},{4,12},{5,13},{6,14},{7,15},{16,24},{17,... | collective-permute-start | bytes 2359304 | tf_op jit(solution)/shard_map/ppermute | solution.py:14
  155.9 4.8 %collective-permute-start.26 = (bf16[16,3072]{1,0:T(8,128)(2,1)S(1)}, bf16[16,3072]{1,0:T(8,128)(2,1)S(1)}, u32[]{:S(2)}, u32[]{:S(2)}) collective-permute-start(bf16[16,3072]{1,0:T(8,128)(2,1)S(1)} %get-tuple-element.119), channel_id=1, source_target_pairs={{0,2},{2,4},{4,6},{6,7},{7,5},{5,3},{3,1},{1,0},{8,10},{10,12},{12... | collective-permute-start | bytes 294920 | tf_op jit(solution)/shard_map/ppermute | solution.py:108
  156.4 4.9 %collective-permute-start.30 = (bf16[16,3072]{1,0:T(8,128)(2,1)S(1)}, bf16[16,3072]{1,0:T(8,128)(2,1)S(1)}, u32[]{:S(2)}, u32[]{:S(2)}) collective-permute-start(bf16[16,3072]{1,0:T(8,128)(2,1)S(1)} %get-tuple-element.120), channel_id=1, source_target_pairs={{0,1},{2,0},{4,2},{6,4},{7,6},{5,7},{3,5},{1,3},{8,9},{10,8},{12,1... | collective-permute-start | bytes 294920 | tf_op jit(solution)/shard_map/ppermute | solution.py:108
  160.8 5.9 %collective-permute-start.27 = (bf16[32,3072]{1,0:T(8,128)(2,1)S(1)}, bf16[32,3072]{1,0:T(8,128)(2,1)S(1)}, u32[]{:S(2)}, u32[]{:S(2)}) collective-permute-start(bf16[32,3072]{1,0:T(8,128)(2,1)S(1)} %convert_element_type.342), channel_id=1, source_target_pairs={{0,2},{2,4},{4,6},{6,7},{7,5},{5,3},{3,1},{1,0},{8,10},{10,12},{12... | collective-permute-start | bytes 589832 | tf_op jit(solution)/shard_map/ppermute | solution.py:108
  161.4 5.9 %collective-permute-start.31 = (bf16[32,3072]{1,0:T(8,128)(2,1)S(1)}, bf16[32,3072]{1,0:T(8,128)(2,1)S(1)}, u32[]{:S(2)}, u32[]{:S(2)}) collective-permute-start(bf16[32,3072]{1,0:T(8,128)(2,1)S(1)} %convert_element_type.352), channel_id=1, source_target_pairs={{0,1},{2,0},{4,2},{6,4},{7,6},{5,7},{3,5},{1,3},{8,9},{10,8},{12,1... | collective-permute-start | bytes 589832 | tf_op jit(solution)/shard_map/ppermute | solution.py:108
  166.8 5.7 %collective-permute-start.28 = (bf16[32,3072]{1,0:T(8,128)(2,1)S(1)}, bf16[32,3072]{1,0:T(8,128)(2,1)S(1)}, u32[]{:S(2)}, u32[]{:S(2)}) collective-permute-start(bf16[32,3072]{1,0:T(8,128)(2,1)S(1)} %add_convert_fusion.9), channel_id=1, source_target_pairs={{0,2},{2,4},{4,6},{6,7},{7,5},{5,3},{3,1},{1,0},{8,10},{10,12},{12... | collective-permute-start | bytes 589832 | tf_op jit(solution)/shard_map/ppermute | solution.py:108
  172.6 7.3 %collective-permute-start.32 = (bf16[32,3072]{1,0:T(8,128)(2,1)S(1)}, bf16[32,3072]{1,0:T(8,128)(2,1)S(1)}, u32[]{:S(2)}, u32[]{:S(2)}) collective-permute-start(bf16[32,3072]{1,0:T(8,128)(2,1)S(1)} %get-tuple-element.110), channel_id=1, source_target_pairs={{0,1},{2,0},{4,2},{6,4},{7,6},{5,7},{3,5},{1,3},{8,9},{10,8},{12,1... | collective-permute-start | bytes 589832 | tf_op jit(solution)/shard_map/ppermute | solution.py:108
  174.2 7.3 %collective-permute-start.29 = (bf16[32,3072]{1,0:T(8,128)(2,1)S(1)}, bf16[32,3072]{1,0:T(8,128)(2,1)S(1)}, u32[]{:S(2)}, u32[]{:S(2)}) collective-permute-start(bf16[32,3072]{1,0:T(8,128)(2,1)S(1)} %get-tuple-element.109), channel_id=1, source_target_pairs={{0,2},{2,4},{4,6},{6,7},{7,5},{5,3},{3,1},{1,0},{8,10},{10,12},{12... | collective-permute-start | bytes 589832 | tf_op jit(solution)/shard_map/ppermute | solution.py:108
  179.9 7.7 %collective-permute-start.33 = (bf16[32,3072]{1,0:T(8,128)(2,1)S(1)}, bf16[32,3072]{1,0:T(8,128)(2,1)S(1)}, u32[]{:S(2)}, u32[]{:S(2)}) collective-permute-start(bf16[32,3072]{1,0:T(8,128)(2,1)S(1)} %add_convert_fusion.6), channel_id=1, source_target_pairs={{0,1},{2,0},{4,2},{6,4},{7,6},{5,7},{3,5},{1,3},{8,9},{10,8},{12,1... | collective-permute-start | bytes 589832 | tf_op jit(solution)/shard_map/ppermute | solution.py:108
  188.4 6.1 %collective-permute-start.34 = (bf16[32,3072]{1,0:T(8,128)(2,1)S(1)}, bf16[32,3072]{1,0:T(8,128)(2,1)S(1)}, u32[]{:S(2)}, u32[]{:S(2)}) collective-permute-start(bf16[32,3072]{1,0:T(8,128)(2,1)S(1)} %get-tuple-element.96), channel_id=1, source_target_pairs={{0,1},{2,0},{4,2},{6,4},{7,6},{5,7},{3,5},{1,3},{8,9},{10,8},{12,1... | collective-permute-start | bytes 589832 | tf_op jit(solution)/shard_map/ppermute | solution.py:59
  190.0 6.1 %collective-permute-start.37 = (bf16[32,3072]{1,0:T(8,128)(2,1)S(1)}, bf16[32,3072]{1,0:T(8,128)(2,1)S(1)}, u32[]{:S(2)}, u32[]{:S(2)}) collective-permute-start(bf16[32,3072]{1,0:T(8,128)(2,1)S(1)} %get-tuple-element.96), channel_id=1, source_target_pairs={{0,2},{2,4},{4,6},{6,7},{7,5},{5,3},{3,1},{1,0},{8,10},{10,12},{12... | collective-permute-start | bytes 589832 | tf_op jit(solution)/shard_map/ppermute | solution.py:58
  194.6 5.7 %collective-permute-start.35 = (bf16[32,3072]{1,0:T(8,128)(2,1)S(1)}, bf16[32,3072]{1,0:T(8,128)(2,1)S(1)}, u32[]{:S(2)}, u32[]{:S(2)}) collective-permute-start(bf16[32,3072]{1,0:T(8,128)(2,1)S(1)} %collective-permute-done.34), channel_id=1, source_target_pairs={{0,1},{2,0},{4,2},{6,4},{7,6},{5,7},{3,5},{1,3},{8,9},{10,8},{12,1... | collective-permute-start | bytes 589832 | tf_op jit(solution)/shard_map/ppermute | solution.py:71
  196.2 5.7 %collective-permute-start.38 = (bf16[32,3072]{1,0:T(8,128)(2,1)S(1)}, bf16[32,3072]{1,0:T(8,128)(2,1)S(1)}, u32[]{:S(2)}, u32[]{:S(2)}) collective-permute-start(bf16[32,3072]{1,0:T(8,128)(2,1)S(1)} %collective-permute-done.37), channel_id=1, source_target_pairs={{0,2},{2,4},{4,6},{6,7},{7,5},{5,3},{3,1},{1,0},{8,10},{10,12},{12... | collective-permute-start | bytes 589832 | tf_op jit(solution)/shard_map/ppermute | solution.py:68
  200.3 5.7 %collective-permute-start.36 = (bf16[32,3072]{1,0:T(8,128)(2,1)S(1)}, bf16[32,3072]{1,0:T(8,128)(2,1)S(1)}, u32[]{:S(2)}, u32[]{:S(2)}) collective-permute-start(bf16[32,3072]{1,0:T(8,128)(2,1)S(1)} %collective-permute-done.35), channel_id=1, source_target_pairs={{0,1},{2,0},{4,2},{6,4},{7,6},{5,7},{3,5},{1,3},{8,9},{10,8},{12,1... | collective-permute-start | bytes 589832 | tf_op jit(solution)/shard_map/ppermute | solution.py:71
  201.8 5.7 %collective-permute-start.39 = (bf16[32,3072]{1,0:T(8,128)(2,1)S(1)}, bf16[32,3072]{1,0:T(8,128)(2,1)S(1)}, u32[]{:S(2)}, u32[]{:S(2)}) collective-permute-start(bf16[32,3072]{1,0:T(8,128)(2,1)S(1)} %collective-permute-done.38), channel_id=1, source_target_pairs={{0,2},{2,4},{4,6},{6,7},{7,5},{5,3},{3,1},{1,0},{8,10},{10,12},{12... | collective-permute-start | bytes 589832 | tf_op jit(solution)/shard_map/ppermute | solution.py:68
  205.9 4.7 %collective-permute-start.41 = (bf16[16,3072]{1,0:T(8,128)(2,1)S(1)}, bf16[16,3072]{1,0:T(8,128)(2,1)S(1)}, u32[]{:S(2)}, u32[]{:S(2)}) collective-permute-start(bf16[16,3072]{1,0:T(8,128)(2,1)S(1)} %slice.421), channel_id=1, source_target_pairs={{0,1},{2,0},{4,2},{6,4},{7,6},{5,7},{3,5},{1,3},{8,9},{10,8},{12,1... | collective-permute-start | bytes 294920 | tf_op jit(solution)/shard_map/ppermute | solution.py:65
  207.6 4.7 %collective-permute-start.40 = (bf16[16,3072]{1,0:T(8,128)(2,1)S(1)}, bf16[16,3072]{1,0:T(8,128)(2,1)S(1)}, u32[]{:S(2)}, u32[]{:S(2)}) collective-permute-start(bf16[16,3072]{1,0:T(8,128)(2,1)S(1)} %slice.420), channel_id=1, source_target_pairs={{0,2},{2,4},{4,6},{6,7},{7,5},{5,3},{3,1},{1,0},{8,10},{10,12},{12... | collective-permute-start | bytes 294920 | tf_op jit(solution)/shard_map/ppermute | solution.py:64
  217.5 1.7 copy-start.3
  220.8 2.9 %collective-permute-start.42 = (bf16[256,128]{1,0:T(8,128)(2,1)S(1)}, bf16[256,128]{1,0:T(8,128)(2,1)S(1)}, u32[]{:S(2)}, u32[]{:S(2)}) collective-permute-start(bf16[256,128]{1,0:T(8,128)(2,1)S(1)} %convolution_convert_fusion.7), channel_id=1, source_target_pairs={{0,8},{1,9},{2,10},{3,11},{4,12},{5,13},{6,14},{7,15},{16,24},{17,... | collective-permute-start | bytes 196616 | tf_op jit(solution)/shard_map/ppermute | solution.py:14
  222.1 2.2 collective-permute-start.43
  226.8 4.7 %collective-permute-start.44 = (bf16[16,3072]{1,0:T(8,128)(2,1)S(1)}, bf16[16,3072]{1,0:T(8,128)(2,1)S(1)}, u32[]{:S(2)}, u32[]{:S(2)}) collective-permute-start(bf16[16,3072]{1,0:T(8,128)(2,1)S(1)} %get-tuple-element.117), channel_id=1, source_target_pairs={{0,2},{2,4},{4,6},{6,7},{7,5},{5,3},{3,1},{1,0},{8,10},{10,12},{12... | collective-permute-start | bytes 294920 | tf_op jit(solution)/shard_map/ppermute | solution.py:108
  227.3 4.7 %collective-permute-start.48 = (bf16[16,3072]{1,0:T(8,128)(2,1)S(1)}, bf16[16,3072]{1,0:T(8,128)(2,1)S(1)}, u32[]{:S(2)}, u32[]{:S(2)}) collective-permute-start(bf16[16,3072]{1,0:T(8,128)(2,1)S(1)} %get-tuple-element.118), channel_id=1, source_target_pairs={{0,1},{2,0},{4,2},{6,4},{7,6},{5,7},{3,5},{1,3},{8,9},{10,8},{12,1... | collective-permute-start | bytes 294920 | tf_op jit(solution)/shard_map/ppermute | solution.py:108
  231.6 7.7 %collective-permute-start.45 = (bf16[32,3072]{1,0:T(8,128)(2,1)S(1)}, bf16[32,3072]{1,0:T(8,128)(2,1)S(1)}, u32[]{:S(2)}, u32[]{:S(2)}) collective-permute-start(bf16[32,3072]{1,0:T(8,128)(2,1)S(1)} %convert_element_type.376), channel_id=1, source_target_pairs={{0,2},{2,4},{4,6},{6,7},{7,5},{5,3},{3,1},{1,0},{8,10},{10,12},{12... | collective-permute-start | bytes 589832 | tf_op jit(solution)/shard_map/ppermute | solution.py:108
  232.2 7.7 %collective-permute-start.49 = (bf16[32,3072]{1,0:T(8,128)(2,1)S(1)}, bf16[32,3072]{1,0:T(8,128)(2,1)S(1)}, u32[]{:S(2)}, u32[]{:S(2)}) collective-permute-start(bf16[32,3072]{1,0:T(8,128)(2,1)S(1)} %convert_element_type.386), channel_id=1, source_target_pairs={{0,1},{2,0},{4,2},{6,4},{7,6},{5,7},{3,5},{1,3},{8,9},{10,8},{12,1... | collective-permute-start | bytes 589832 | tf_op jit(solution)/shard_map/ppermute | solution.py:108
  239.4 7.1 %collective-permute-start.46 = (bf16[32,3072]{1,0:T(8,128)(2,1)S(1)}, bf16[32,3072]{1,0:T(8,128)(2,1)S(1)}, u32[]{:S(2)}, u32[]{:S(2)}) collective-permute-start(bf16[32,3072]{1,0:T(8,128)(2,1)S(1)} %add_convert_fusion.4), channel_id=1, source_target_pairs={{0,2},{2,4},{4,6},{6,7},{7,5},{5,3},{3,1},{1,0},{8,10},{10,12},{12... | collective-permute-start | bytes 589832 | tf_op jit(solution)/shard_map/ppermute | solution.py:108
  246.5 6.3 %collective-permute-start.50 = (bf16[32,3072]{1,0:T(8,128)(2,1)S(1)}, bf16[32,3072]{1,0:T(8,128)(2,1)S(1)}, u32[]{:S(2)}, u32[]{:S(2)}) collective-permute-start(bf16[32,3072]{1,0:T(8,128)(2,1)S(1)} %get-tuple-element.106), channel_id=1, source_target_pairs={{0,1},{2,0},{4,2},{6,4},{7,6},{5,7},{3,5},{1,3},{8,9},{10,8},{12,1... | collective-permute-start | bytes 589832 | tf_op jit(solution)/shard_map/ppermute | solution.py:108
  248.2 6.3 %collective-permute-start.47 = (bf16[32,3072]{1,0:T(8,128)(2,1)S(1)}, bf16[32,3072]{1,0:T(8,128)(2,1)S(1)}, u32[]{:S(2)}, u32[]{:S(2)}) collective-permute-start(bf16[32,3072]{1,0:T(8,128)(2,1)S(1)} %get-tuple-element.105), channel_id=1, source_target_pairs={{0,2},{2,4},{4,6},{6,7},{7,5},{5,3},{3,1},{1,0},{8,10},{10,12},{12... | collective-permute-start | bytes 589832 | tf_op jit(solution)/shard_map/ppermute | solution.py:108
  252.8 5.7 %collective-permute-start.51 = (bf16[32,3072]{1,0:T(8,128)(2,1)S(1)}, bf16[32,3072]{1,0:T(8,128)(2,1)S(1)}, u32[]{:S(2)}, u32[]{:S(2)}) collective-permute-start(bf16[32,3072]{1,0:T(8,128)(2,1)S(1)} %add_convert_fusion.1), channel_id=1, source_target_pairs={{0,1},{2,0},{4,2},{6,4},{7,6},{5,7},{3,5},{1,3},{8,9},{10,8},{12,1... | collective-permute-start | bytes 589832 | tf_op jit(solution)/shard_map/ppermute | solution.py:108

commit v12 on v11

--- a/solution.py
+++ b/solution.py
@@ -134,7 +134,7 @@
     return lax.optimization_barrier(term.astype(jnp.bfloat16)).astype(jnp.float32)
 
 
-def conv_gate_kernel(slab_ref, gain_ref, weight_ref, out_ref, filt_acc, gate_acc):
+def conv_gate_kernel(slab_ref, scale_ref, gain_ref, weight_ref, out_ref, filt_acc, gate_acc):
     tap = pl.program_id(0)
     chunk = pl.program_id(1)
 
@@ -143,9 +143,7 @@
         filt_acc[...] = jnp.zeros_like(filt_acc)
         gate_acc[...] = jnp.zeros_like(gate_acc)
 
-    wide = slab_ref[...].astype(jnp.float32)
-    scale = lax.rsqrt(jnp.mean(wide * wide, axis=-1, keepdims=True) + 1e-06)
-    rows = (wide * scale * gain_ref[...]).astype(jnp.bfloat16)
+    rows = (slab_ref[...].astype(jnp.float32) * scale_ref[...] * gain_ref[...]).astype(jnp.bfloat16)
     filt_acc[...] += jnp.dot(rows, weight_ref[0], preferred_element_type=jnp.float32)
     gate_acc[...] += jnp.dot(rows, weight_ref[1], preferred_element_type=jnp.float32)
 
@@ -163,20 +161,20 @@
     border_rows = 2 * LARGEST_DILATION
     before = shifted(hidden[all_rows - border_rows :], "blk", 1)
     padded = jnp.concatenate([before, hidden], axis=0)
-    slabs = jnp.stack(
-        [
-            lax.dynamic_slice_in_dim(padded, border_rows - tap_idx * dilation_factor, all_rows, 0)
-            for tap_idx in range(taps)
-        ]
-    )
-    chunk = width
+    wide = padded.astype(jnp.float32)
+    row_scale = lax.rsqrt(jnp.mean(wide * wide, axis=-1, keepdims=True) + 1e-06)
+    starts = [border_rows - tap_idx * dilation_factor for tap_idx in range(taps)]
+    slabs = jnp.stack([lax.dynamic_slice_in_dim(padded, s, all_rows, 0) for s in starts])
+    scales = jnp.stack([lax.dynamic_slice_in_dim(row_scale, s, all_rows, 0) for s in starts])
+    chunk = width // 2 if width % 256 == 0 else width
     return pl.pallas_call(
         conv_gate_kernel,
         out_shape=jax.ShapeDtypeStruct((all_rows, own_width), jnp.bfloat16),
         grid=(taps, width // chunk),
         in_specs=[
             pl.BlockSpec((None, all_rows, chunk), lambda t, k: (t, 0, k)),
-            pl.BlockSpec((1, width), lambda t, k: (0, 0)),
+            pl.BlockSpec((None, all_rows, 1), lambda t, k: (t, 0, 0)),
+            pl.BlockSpec((1, chunk), lambda t, k: (0, k)),
             pl.BlockSpec((None, None, 2, chunk, own_width), lambda t, k: (layer_idx, t, 0, k, 0)),
         ],
         out_specs=pl.BlockSpec((all_rows, own_width), lambda t, k: (0, 0)),
@@ -187,7 +185,7 @@
             transcendentals=2 * all_rows * own_width,
             bytes_accessed=2 * taps * (all_rows * width + 2 * width * own_width + all_rows * own_width // taps),
         ),
-    )(slabs, gain.reshape(1, width), conv_by_half)
+    )(slabs, scales, gain.reshape(1, width), conv_by_half)
 
 
 def far_rows(ordered, tok_rows):

time: 260 us -> 264 us (1.015)
  local copies, waits for them, and re-layouts: 48.1 us -> 51 us
    another operation x4 -> x6, other arithmetic: 9.77 us -> 9.09 us  [the longest x4 9.07 us: convolution_gate(): jnp.stack([lax.dynamic_slice_in_dim(padded, s, all_rows, 0) for s in star...]
  transfers between devices with their start and end apart: 52 -> 52, of which waited for: 29 -> 30; matrix products, arithmetic and copies ran while one was open for 15% -> 15% of each run, Pallas kernels for 0% -> 0%
where the time goes in v12:
time: 264 us; the launch traced here: 263 us
  waiting for transfers between devices  97.8 us (37%)
  starting transfers between devices  57.2 us (22%)
  local copies, waits for them, and re-layouts  51 us (19%)
  Pallas kernels  22.7 us (9%)
  other arithmetic  17.6 us (7%)
  matrix products  12.6 us (5%)
  between operations  4.27 us (2%)
    ppermute x24, waiting for transfers between devices, chain(): passed = lax.ppermute(part.astype(value.dtype), axis, pairs)  62.1 us
    unnamed x25, local copies, waits for them, and re-layouts  32.8 us
    ppermute x24, starting transfers between devices, chain(): passed = lax.ppermute(part.astype(value.dtype), axis, pairs)  25 us
    pallas_call x2, Pallas kernels, convolution_gate(): pl.pallas_call(conv_gate_kernel, out_shape=jax.ShapeDtypeStruct((all_rows...  22.7 us
    ppermute x5, waiting for transfers between devices, ring_gather(): bwd = lax.ppermute(bwd, axis, backward)  14.3 us
    dot_general x6, matrix products, rounded_term(): term = jnp.dot(left, right, preferred_element_type=jnp.float32)  10.4 us
    ppermute x4, waiting for transfers between devices, ring_gather(): lax.ppermute(value, axis, [(order[p], order[(p - k) % length]) for p in r...  9.2 us
    another operation x4, other arithmetic, convolution_gate(): jnp.stack([lax.dynamic_slice_in_dim(padded, s, all_rows, 0) for s in star...  9.07 us
  transfers between devices with their start and end apart: 52, of which 30 were waited for; matrix products, arithmetic and copies ran while one was open for 15% of the time, Pallas kernels for 0%

profile of v12, /device:TPU:0, one launch (start us, length us, event | category | flops | bytes accessed | tf_op | source)
XLA Modules:
  0.0 263.2 jit_solution(11085873611451478681)
XLA Ops:
  0.0 4.0 %collective-permute-start.1 = (bf16[32,3072]{1,0:T(8,128)(2,1)}, bf16[32,3072]{1,0:T(8,128)(2,1)S(1)}, u32[]{:S(2)}, u32[]{:S(2)}) collective-permute-start(bf16[32,3072]{1,0:T(8,128)(2,1)} %param.22), channel_id=1, source_target_pairs={{0,3},{2,1},{4,0},{6,2},{7,4},{5,6},{3,7},{1,5},{8,11},{10,9},{12,... | collective-permute-start | bytes 589832 | tf_op jit(solution)/shard_map/ppermute | solution.py:59
  4.0 1.6 collective-permute-start
  9.4 1.6 bitcast_dynamic-update-slice_fusion.20
  11.1 19.6 %copy.21 = bf16[2,3,3072,2,384]{4,2,3,1,0:T(8,128)(2,1)} copy(bf16[2,3,3072,2,384]{4,3,2,1,0:T(2,128)(2,1)} %param.25) | data formatting | bytes 56623104 | tf_op args[3]
  31.4 1.8 collective-permute-start.2
  34.8 2.4 collective-permute-done.2
  37.2 1.7 collective-permute-start.6
  40.1 1.8 collective-permute-done.6
  41.9 1.7 collective-permute-done.5
  46.4 2.1 gather_fusion
  53.3 2.1 fusion.21
  55.5 2.4 pad_maximum_fusion.slab_ref
  57.9 11.4 %shard_map.82 = bf16[256,384]{1,0:T(8,128)(2,1)} custom-call(bf16[3,256,3072]{2,1,0:T(8,128)(2,1)} %pad_maximum_fusion.slab_ref, f32[3,256,1]{2,1,0:T(8,128)} %copy.18.scale_ref, f32[1,3072]{1,0:T(1,128)} %get-tuple-element.124.gain_ref, bf16[2,3,2,3072,384]{4,3,2,1,0:T(8,128)(2,1)} %bitcast.145), custom_call_target="tpu_custom_call" | custom-call | flops 3623878656 | bytes 19070976 | tf_op jit(solution)/shard_map/pallas_call | solution.py:170
  69.2 1.5 gather_fusion.1
  70.7 2.2 convolution_convert_fusion.4
  73.4 1.6 collective-permute-start.13
  75.0 2.6 %convolution_convert_fusion.2 = bf16[256,3072]{1,0:T(8,128)(2,1)S(1)} fusion(bf16[256,384]{1,0:T(8,128)(2,1)S(1)} %bitcast.161, bf16[2,384,3072]{2,1,0:T(8,128)(2,1)} %param.26), kind=kOutput, calls=%fused_computation.21 | convolution fusion | flops 604766208 | bytes 4128768 | tf_op jit(solution)/shard_map/dot_general | solution.py:133
  78.7 1.8 collective-permute-start.14
  80.4 4.3 %collective-permute-done.10 = bf16[32,3072]{1,0:T(8,128)(2,1)S(1)} collective-permute-done((bf16[32,3072]{1,0:T(8,128)(2,1)S(1)}, bf16[32,3072]{1,0:T(8,128)(2,1)S(1)}, u32[]{:S(2)}, u32[]{:S(2)}) %collective-permute-start.10) | collective-permute-done | bytes 196640 | tf_op jit(solution)/shard_map/ppermute | solution.py:108
  85.1 5.4 %collective-permute-done.11 = bf16[32,3072]{1,0:T(8,128)(2,1)S(1)} collective-permute-done((bf16[32,3072]{1,0:T(8,128)(2,1)S(1)}, bf16[32,3072]{1,0:T(8,128)(2,1)S(1)}, u32[]{:S(2)}, u32[]{:S(2)}) %collective-permute-start.11) | collective-permute-done | bytes 196640 | tf_op jit(solution)/shard_map/ppermute | solution.py:108
  92.7 4.5 %collective-permute-done.15 = bf16[32,3072]{1,0:T(8,128)(2,1)S(1)} collective-permute-done((bf16[32,3072]{1,0:T(8,128)(2,1)S(1)}, bf16[32,3072]{1,0:T(8,128)(2,1)S(1)}, u32[]{:S(2)}, u32[]{:S(2)}) %collective-permute-start.15) | collective-permute-done | bytes 196640 | tf_op jit(solution)/shard_map/ppermute | solution.py:108
  97.2 1.6 collective-permute-start.16
  98.8 5.4 %collective-permute-done.16 = bf16[32,3072]{1,0:T(8,128)(2,1)S(1)} collective-permute-done((bf16[32,3072]{1,0:T(8,128)(2,1)S(1)}, bf16[32,3072]{1,0:T(8,128)(2,1)S(1)}, u32[]{:S(2)}, u32[]{:S(2)}) %collective-permute-start.16) | collective-permute-done | bytes 196640 | tf_op jit(solution)/shard_map/ppermute | solution.py:108
  105.0 1.7 collective-permute-start.17
  107.0 4.6 %collective-permute-done.17 = bf16[32,3072]{1,0:T(8,128)(2,1)S(1)} collective-permute-done((bf16[32,3072]{1,0:T(8,128)(2,1)S(1)}, bf16[32,3072]{1,0:T(8,128)(2,1)S(1)}, u32[]{:S(2)}, u32[]{:S(2)}) %collective-permute-start.17) | collective-permute-done | bytes 196640 | tf_op jit(solution)/shard_map/ppermute | solution.py:59
  111.6 1.6 collective-permute-start.18
  114.4 3.0 %collective-permute-done.18 = bf16[32,3072]{1,0:T(8,128)(2,1)S(1)} collective-permute-done((bf16[32,3072]{1,0:T(8,128)(2,1)S(1)}, bf16[32,3072]{1,0:T(8,128)(2,1)S(1)}, u32[]{:S(2)}, u32[]{:S(2)}) %collective-permute-start.18) | collective-permute-done | bytes 196640 | tf_op jit(solution)/shard_map/ppermute | solution.py:71
  120.1 2.9 %collective-permute-done.19 = bf16[32,3072]{1,0:T(8,128)(2,1)S(1)} collective-permute-done((bf16[32,3072]{1,0:T(8,128)(2,1)S(1)}, bf16[32,3072]{1,0:T(8,128)(2,1)S(1)}, u32[]{:S(2)}, u32[]{:S(2)}) %collective-permute-start.19) | collective-permute-done | bytes 196640 | tf_op jit(solution)/shard_map/ppermute | solution.py:71
  123.1 1.5 collective-permute-start.24
  125.9 1.8 collective-permute-done.24
  127.7 1.5 collective-permute-done.23
  132.1 2.1 gather_fusion.2
  135.1 1.5 collective-permute-start.25
  140.1 2.1 fusion.17
  142.2 2.4 pad_maximum_fusion.1.slab_ref
  144.6 11.4 %shard_map.83 = bf16[256,384]{1,0:T(8,128)(2,1)} custom-call(bf16[3,256,3072]{2,1,0:T(8,128)(2,1)} %pad_maximum_fusion.1.slab_ref, f32[3,256,1]{2,1,0:T(8,128)} %copy.19.scale_ref, f32[1,3072]{1,0:T(1,128)} %get-tuple-element.125.gain_ref, bf16[2,3,2,3072,384]{4,3,2,1,0:T(8,128)(2,1)} %bitcast.146), custom_call_target="tpu_custom_call" | custom-call | flops 3623878656 | bytes 19070976 | tf_op jit(solution)/shard_map/pallas_call | solution.py:170
  156.0 1.5 gather_fusion.3
  157.5 2.2 convolution_convert_fusion.3
  161.8 2.6 %convolution_convert_fusion.1 = bf16[256,3072]{1,0:T(8,128)(2,1)S(1)} fusion(bf16[256,384]{1,0:T(8,128)(2,1)S(1)} %bitcast.162, bf16[2,384,3072]{2,1,0:T(8,128)(2,1)} %param.26), kind=kOutput, calls=%fused_computation.20 | convolution fusion | flops 604766208 | bytes 4128768 | tf_op jit(solution)/shard_map/dot_general | solution.py:133
  165.7 1.5 collective-permute-start.31
  167.2 4.3 %collective-permute-done.27 = bf16[32,3072]{1,0:T(8,128)(2,1)S(1)} collective-permute-done((bf16[32,3072]{1,0:T(8,128)(2,1)S(1)}, bf16[32,3072]{1,0:T(8,128)(2,1)S(1)}, u32[]{:S(2)}, u32[]{:S(2)}) %collective-permute-start.27) | collective-permute-done | bytes 196640 | tf_op jit(solution)/shard_map/ppermute | solution.py:108
  172.1 5.1 %collective-permute-done.28 = bf16[32,3072]{1,0:T(8,128)(2,1)S(1)} collective-permute-done((bf16[32,3072]{1,0:T(8,128)(2,1)S(1)}, bf16[32,3072]{1,0:T(8,128)(2,1)S(1)}, u32[]{:S(2)}, u32[]{:S(2)}) %collective-permute-start.28) | collective-permute-done | bytes 196640 | tf_op jit(solution)/shard_map/ppermute | solution.py:108
  177.3 1.6 collective-permute-start.32
  179.4 4.5 %collective-permute-done.32 = bf16[32,3072]{1,0:T(8,128)(2,1)S(1)} collective-permute-done((bf16[32,3072]{1,0:T(8,128)(2,1)S(1)}, bf16[32,3072]{1,0:T(8,128)(2,1)S(1)}, u32[]{:S(2)}, u32[]{:S(2)}) %collective-permute-start.32) | collective-permute-done | bytes 196640 | tf_op jit(solution)/shard_map/ppermute | solution.py:108
  184.0 1.6 collective-permute-start.33
  185.6 5.4 %collective-permute-done.33 = bf16[32,3072]{1,0:T(8,128)(2,1)S(1)} collective-permute-done((bf16[32,3072]{1,0:T(8,128)(2,1)S(1)}, bf16[32,3072]{1,0:T(8,128)(2,1)S(1)}, u32[]{:S(2)}, u32[]{:S(2)}) %collective-permute-start.33) | collective-permute-done | bytes 196640 | tf_op jit(solution)/shard_map/ppermute | solution.py:108
  191.8 1.6 collective-permute-start.34
  193.8 4.6 %collective-permute-done.34 = bf16[32,3072]{1,0:T(8,128)(2,1)S(1)} collective-permute-done((bf16[32,3072]{1,0:T(8,128)(2,1)S(1)}, bf16[32,3072]{1,0:T(8,128)(2,1)S(1)}, u32[]{:S(2)}, u32[]{:S(2)}) %collective-permute-start.34) | collective-permute-done | bytes 196640 | tf_op jit(solution)/shard_map/ppermute | solution.py:59
  198.4 1.6 collective-permute-start.35
  201.1 3.0 %collective-permute-done.35 = bf16[32,3072]{1,0:T(8,128)(2,1)S(1)} collective-permute-done((bf16[32,3072]{1,0:T(8,128)(2,1)S(1)}, bf16[32,3072]{1,0:T(8,128)(2,1)S(1)}, u32[]{:S(2)}, u32[]{:S(2)}) %collective-permute-start.35) | collective-permute-done | bytes 196640 | tf_op jit(solution)/shard_map/ppermute | solution.py:71
  204.2 1.6 collective-permute-start.36
  206.9 2.9 %collective-permute-done.36 = bf16[32,3072]{1,0:T(8,128)(2,1)S(1)} collective-permute-done((bf16[32,3072]{1,0:T(8,128)(2,1)S(1)}, bf16[32,3072]{1,0:T(8,128)(2,1)S(1)}, u32[]{:S(2)}, u32[]{:S(2)}) %collective-permute-start.36) | collective-permute-done | bytes 196640 | tf_op jit(solution)/shard_map/ppermute | solution.py:71
  209.8 1.6 collective-permute-start.41
  212.7 1.8 collective-permute-done.41
  214.5 1.6 collective-permute-done.40
  218.9 2.1 gather_fusion.4
  231.2 1.6 collective-permute-start.48
  233.4 2.0 collective-permute-done.44
  236.0 1.6 collective-permute-start.49
  237.7 5.5 %collective-permute-done.45 = bf16[32,3072]{1,0:T(8,128)(2,1)S(1)} collective-permute-done((bf16[32,3072]{1,0:T(8,128)(2,1)S(1)}, bf16[32,3072]{1,0:T(8,128)(2,1)S(1)}, u32[]{:S(2)}, u32[]{:S(2)}) %collective-permute-start.45) | collective-permute-done | bytes 196640 | tf_op jit(solution)/shard_map/ppermute | solution.py:108
  243.7 6.6 %collective-permute-done.46 = bf16[32,3072]{1,0:T(8,128)(2,1)S(1)} collective-permute-done((bf16[32,3072]{1,0:T(8,128)(2,1)S(1)}, bf16[32,3072]{1,0:T(8,128)(2,1)S(1)}, u32[]{:S(2)}, u32[]{:S(2)}) %collective-permute-start.46) | collective-permute-done | bytes 196640 | tf_op jit(solution)/shard_map/ppermute | solution.py:108
  250.4 1.5 collective-permute-start.50
  252.5 4.2 %collective-permute-done.50 = bf16[32,3072]{1,0:T(8,128)(2,1)S(1)} collective-permute-done((bf16[32,3072]{1,0:T(8,128)(2,1)S(1)}, bf16[32,3072]{1,0:T(8,128)(2,1)S(1)}, u32[]{:S(2)}, u32[]{:S(2)}) %collective-permute-start.50) | collective-permute-done | bytes 196640 | tf_op jit(solution)/shard_map/ppermute | solution.py:108
  258.2 4.2 %collective-permute-done.51 = bf16[32,3072]{1,0:T(8,128)(2,1)S(1)} collective-permute-done((bf16[32,3072]{1,0:T(8,128)(2,1)S(1)}, bf16[32,3072]{1,0:T(8,128)(2,1)S(1)}, u32[]{:S(2)}, u32[]{:S(2)}) %collective-permute-start.51) | collective-permute-done | bytes 196640 | tf_op jit(solution)/shard_map/ppermute | solution.py:108
  (157 shorter events, 56.2 us)
Async XLA Ops:
  0.0 230.5 %copy-start = (bf16[1,128,3072]{2,1,0:T(8,128)(2,1)S(1)}, bf16[1,128,3072]{2,1,0:T(8,128)(2,1)}, u32[]{:S(2)}) copy-start(bf16[1,128,3072]{2,1,0:T(8,128)(2,1)} %param.28) | copy-start | bytes 2359300
  0.0 31.4 %collective-permute-start.1 = (bf16[32,3072]{1,0:T(8,128)(2,1)}, bf16[32,3072]{1,0:T(8,128)(2,1)S(1)}, u32[]{:S(2)}, u32[]{:S(2)}) collective-permute-start(bf16[32,3072]{1,0:T(8,128)(2,1)} %param.22), channel_id=1, source_target_pairs={{0,3},{2,1},{4,0},{6,2},{7,4},{5,6},{3,7},{1,5},{8,11},{10,9},{12,... | collective-permute-start | bytes 589832 | tf_op jit(solution)/shard_map/ppermute | solution.py:59
  4.0 29.5 %collective-permute-start = (bf16[32,3072]{1,0:T(8,128)(2,1)}, bf16[32,3072]{1,0:T(8,128)(2,1)S(1)}, u32[]{:S(2)}, u32[]{:S(2)}) collective-permute-start(bf16[32,3072]{1,0:T(8,128)(2,1)} %param.22), channel_id=1, source_target_pairs={{0,1},{2,0},{4,2},{6,4},{7,6},{5,7},{3,5},{1,3},{8,9},{10,8},{12,1... | collective-permute-start | bytes 589832 | tf_op jit(solution)/shard_map/ppermute | solution.py:59
  5.6 40.2 %collective-permute-start.7 = (bf16[32,3072]{1,0:T(8,128)(2,1)}, bf16[32,3072]{1,0:T(8,128)(2,1)S(1)}, u32[]{:S(2)}, u32[]{:S(2)}) collective-permute-start(bf16[32,3072]{1,0:T(8,128)(2,1)} %param.22), channel_id=1, source_target_pairs={{0,2},{2,4},{4,6},{6,7},{7,5},{5,3},{3,1},{1,0},{8,10},{10,12},{12... | collective-permute-start | bytes 589832 | tf_op jit(solution)/shard_map/ppermute | solution.py:58
  6.0 27.2 %collective-permute-start.3 = (bf16[32,3072]{1,0:T(8,128)(2,1)}, bf16[32,3072]{1,0:T(8,128)(2,1)S(1)}, u32[]{:S(2)}, u32[]{:S(2)}) collective-permute-start(bf16[32,3072]{1,0:T(8,128)(2,1)} %param.22), channel_id=1, source_target_pairs={{0,4},{2,6},{4,7},{6,5},{7,3},{5,1},{3,0},{1,2},{8,12},{10,14},{12... | collective-permute-start | bytes 589832 | tf_op jit(solution)/shard_map/ppermute | solution.py:58
  31.4 5.9 %collective-permute-start.2 = (bf16[32,3072]{1,0:T(8,128)(2,1)S(1)}, bf16[32,3072]{1,0:T(8,128)(2,1)S(1)}, u32[]{:S(2)}, u32[]{:S(2)}) collective-permute-start(bf16[32,3072]{1,0:T(8,128)(2,1)S(1)} %collective-permute-done.1), channel_id=1, source_target_pairs={{0,1},{2,0},{4,2},{6,4},{7,6},{5,7},{3,5},{1,3},{8,9},{10,8},{12,1... | collective-permute-start | bytes 589832 | tf_op jit(solution)/shard_map/ppermute | solution.py:71
  33.2 5.7 %collective-permute-start.4 = (bf16[32,3072]{1,0:T(8,128)(2,1)S(1)}, bf16[32,3072]{1,0:T(8,128)(2,1)S(1)}, u32[]{:S(2)}, u32[]{:S(2)}) collective-permute-start(bf16[32,3072]{1,0:T(8,128)(2,1)S(1)} %collective-permute-done.3), channel_id=1, source_target_pairs={{0,2},{2,4},{4,6},{6,7},{7,5},{5,3},{3,1},{1,0},{8,10},{10,12},{12... | collective-permute-start | bytes 589832 | tf_op jit(solution)/shard_map/ppermute | solution.py:68
  37.2 4.7 %collective-permute-start.6 = (bf16[16,3072]{1,0:T(8,128)(2,1)S(1)}, bf16[16,3072]{1,0:T(8,128)(2,1)S(1)}, u32[]{:S(2)}, u32[]{:S(2)}) collective-permute-start(bf16[16,3072]{1,0:T(8,128)(2,1)S(1)} %slice.393), channel_id=1, source_target_pairs={{0,1},{2,0},{4,2},{6,4},{7,6},{5,7},{3,5},{1,3},{8,9},{10,8},{12,1... | collective-permute-start | bytes 294920 | tf_op jit(solution)/shard_map/ppermute | solution.py:65
  39.0 4.7 %collective-permute-start.5 = (bf16[16,3072]{1,0:T(8,128)(2,1)S(1)}, bf16[16,3072]{1,0:T(8,128)(2,1)S(1)}, u32[]{:S(2)}, u32[]{:S(2)}) collective-permute-start(bf16[16,3072]{1,0:T(8,128)(2,1)S(1)} %slice.392), channel_id=1, source_target_pairs={{0,2},{2,4},{4,6},{6,7},{7,5},{5,3},{3,1},{1,0},{8,10},{10,12},{12... | collective-permute-start | bytes 294920 | tf_op jit(solution)/shard_map/ppermute | solution.py:64
  48.5 1.4 copy-start.2
  48.5 3.2 %collective-permute-start.8 = (bf16[128,3072]{1,0:T(8,128)(2,1)S(1)}, bf16[128,3072]{1,0:T(8,128)(2,1)S(1)}, u32[]{:S(2)}, u32[]{:S(2)}) collective-permute-start(bf16[128,3072]{1,0:T(8,128)(2,1)S(1)} %bitcast.158), channel_id=1, source_target_pairs={{0,8},{1,9},{2,10},{3,11},{4,12},{5,13},{6,14},{7,15},{16,24},{17,... | collective-permute-start | bytes 2359304 | tf_op jit(solution)/shard_map/ppermute | solution.py:14
  73.0 5.2 %collective-permute-start.9 = (bf16[16,3072]{1,0:T(8,128)(2,1)S(1)}, bf16[16,3072]{1,0:T(8,128)(2,1)S(1)}, u32[]{:S(2)}, u32[]{:S(2)}) collective-permute-start(bf16[16,3072]{1,0:T(8,128)(2,1)S(1)} %get-tuple-element.121), channel_id=1, source_target_pairs={{0,2},{2,4},{4,6},{6,7},{7,5},{5,3},{3,1},{1,0},{8,10},{10,12},{12... | collective-permute-start | bytes 294920 | tf_op jit(solution)/shard_map/ppermute | solution.py:108
  73.4 5.2 %collective-permute-start.13 = (bf16[16,3072]{1,0:T(8,128)(2,1)S(1)}, bf16[16,3072]{1,0:T(8,128)(2,1)S(1)}, u32[]{:S(2)}, u32[]{:S(2)}) collective-permute-start(bf16[16,3072]{1,0:T(8,128)(2,1)S(1)} %get-tuple-element.122), channel_id=1, source_target_pairs={{0,1},{2,0},{4,2},{6,4},{7,6},{5,7},{3,5},{1,3},{8,9},{10,8},{12,1... | collective-permute-start | bytes 294920 | tf_op jit(solution)/shard_map/ppermute | solution.py:108
  78.2 6.5 %collective-permute-start.10 = (bf16[32,3072]{1,0:T(8,128)(2,1)S(1)}, bf16[32,3072]{1,0:T(8,128)(2,1)S(1)}, u32[]{:S(2)}, u32[]{:S(2)}) collective-permute-start(bf16[32,3072]{1,0:T(8,128)(2,1)S(1)} %convert_element_type.324), channel_id=1, source_target_pairs={{0,2},{2,4},{4,6},{6,7},{7,5},{5,3},{3,1},{1,0},{8,10},{10,12},{12... | collective-permute-start | bytes 589832 | tf_op jit(solution)/shard_map/ppermute | solution.py:108
  78.6 25.6 %copy-start.1 = (bf16[32,3072]{1,0:T(8,128)(2,1)S(1)}, bf16[32,3072]{1,0:T(8,128)(2,1)}, u32[]{:S(2)}) copy-start(bf16[32,3072]{1,0:T(8,128)(2,1)} %param.22) | copy-start | bytes 589828
  78.7 6.4 %collective-permute-start.14 = (bf16[32,3072]{1,0:T(8,128)(2,1)S(1)}, bf16[32,3072]{1,0:T(8,128)(2,1)S(1)}, u32[]{:S(2)}, u32[]{:S(2)}) collective-permute-start(bf16[32,3072]{1,0:T(8,128)(2,1)S(1)} %convert_element_type.334), channel_id=1, source_target_pairs={{0,1},{2,0},{4,2},{6,4},{7,6},{5,7},{3,5},{1,3},{8,9},{10,8},{12,1... | collective-permute-start | bytes 589832 | tf_op jit(solution)/shard_map/ppermute | solution.py:108
  84.8 5.7 %collective-permute-start.11 = (bf16[32,3072]{1,0:T(8,128)(2,1)S(1)}, bf16[32,3072]{1,0:T(8,128)(2,1)S(1)}, u32[]{:S(2)}, u32[]{:S(2)}) collective-permute-start(bf16[32,3072]{1,0:T(8,128)(2,1)S(1)} %add_convert_fusion.14), channel_id=1, source_target_pairs={{0,2},{2,4},{4,6},{6,7},{7,5},{5,3},{3,1},{1,0},{8,10},{10,12},{12... | collective-permute-start | bytes 589832 | tf_op jit(solution)/shard_map/ppermute | solution.py:108
  90.6 6.5 %collective-permute-start.15 = (bf16[32,3072]{1,0:T(8,128)(2,1)S(1)}, bf16[32,3072]{1,0:T(8,128)(2,1)S(1)}, u32[]{:S(2)}, u32[]{:S(2)}) collective-permute-start(bf16[32,3072]{1,0:T(8,128)(2,1)S(1)} %get-tuple-element.114), channel_id=1, source_target_pairs={{0,1},{2,0},{4,2},{6,4},{7,6},{5,7},{3,5},{1,3},{8,9},{10,8},{12,1... | collective-permute-start | bytes 589832 | tf_op jit(solution)/shard_map/ppermute | solution.py:108
  92.1 6.7 %collective-permute-start.12 = (bf16[32,3072]{1,0:T(8,128)(2,1)S(1)}, bf16[32,3072]{1,0:T(8,128)(2,1)S(1)}, u32[]{:S(2)}, u32[]{:S(2)}) collective-permute-start(bf16[32,3072]{1,0:T(8,128)(2,1)S(1)} %get-tuple-element.113), channel_id=1, source_target_pairs={{0,2},{2,4},{4,6},{6,7},{7,5},{5,3},{3,1},{1,0},{8,10},{10,12},{12... | collective-permute-start | bytes 589832 | tf_op jit(solution)/shard_map/ppermute | solution.py:108
  97.2 7.0 %collective-permute-start.16 = (bf16[32,3072]{1,0:T(8,128)(2,1)S(1)}, bf16[32,3072]{1,0:T(8,128)(2,1)S(1)}, u32[]{:S(2)}, u32[]{:S(2)}) collective-permute-start(bf16[32,3072]{1,0:T(8,128)(2,1)S(1)} %add_convert_fusion.11), channel_id=1, source_target_pairs={{0,1},{2,0},{4,2},{6,4},{7,6},{5,7},{3,5},{1,3},{8,9},{10,8},{12,1... | collective-permute-start | bytes 589832 | tf_op jit(solution)/shard_map/ppermute | solution.py:108
  105.0 6.6 %collective-permute-start.17 = (bf16[32,3072]{1,0:T(8,128)(2,1)S(1)}, bf16[32,3072]{1,0:T(8,128)(2,1)S(1)}, u32[]{:S(2)}, u32[]{:S(2)}) collective-permute-start(bf16[32,3072]{1,0:T(8,128)(2,1)S(1)} %get-tuple-element.98), channel_id=1, source_target_pairs={{0,1},{2,0},{4,2},{6,4},{7,6},{5,7},{3,5},{1,3},{8,9},{10,8},{12,1... | collective-permute-start | bytes 589832 | tf_op jit(solution)/shard_map/ppermute | solution.py:59
  106.7 6.5 %collective-permute-start.20 = (bf16[32,3072]{1,0:T(8,128)(2,1)S(1)}, bf16[32,3072]{1,0:T(8,128)(2,1)S(1)}, u32[]{:S(2)}, u32[]{:S(2)}) collective-permute-start(bf16[32,3072]{1,0:T(8,128)(2,1)S(1)} %get-tuple-element.98), channel_id=1, source_target_pairs={{0,2},{2,4},{4,6},{6,7},{7,5},{5,3},{3,1},{1,0},{8,10},{10,12},{12... | collective-permute-start | bytes 589832 | tf_op jit(solution)/shard_map/ppermute | solution.py:58
  111.6 5.8 %collective-permute-start.18 = (bf16[32,3072]{1,0:T(8,128)(2,1)S(1)}, bf16[32,3072]{1,0:T(8,128)(2,1)S(1)}, u32[]{:S(2)}, u32[]{:S(2)}) collective-permute-start(bf16[32,3072]{1,0:T(8,128)(2,1)S(1)} %collective-permute-done.17), channel_id=1, source_target_pairs={{0,1},{2,0},{4,2},{6,4},{7,6},{5,7},{3,5},{1,3},{8,9},{10,8},{12,1... | collective-permute-start | bytes 589832 | tf_op jit(solution)/shard_map/ppermute | solution.py:71
  113.2 5.7 %collective-permute-start.21 = (bf16[32,3072]{1,0:T(8,128)(2,1)S(1)}, bf16[32,3072]{1,0:T(8,128)(2,1)S(1)}, u32[]{:S(2)}, u32[]{:S(2)}) collective-permute-start(bf16[32,3072]{1,0:T(8,128)(2,1)S(1)} %collective-permute-done.20), channel_id=1, source_target_pairs={{0,2},{2,4},{4,6},{6,7},{7,5},{5,3},{3,1},{1,0},{8,10},{10,12},{12... | collective-permute-start | bytes 589832 | tf_op jit(solution)/shard_map/ppermute | solution.py:68
  117.4 5.7 %collective-permute-start.19 = (bf16[32,3072]{1,0:T(8,128)(2,1)S(1)}, bf16[32,3072]{1,0:T(8,128)(2,1)S(1)}, u32[]{:S(2)}, u32[]{:S(2)}) collective-permute-start(bf16[32,3072]{1,0:T(8,128)(2,1)S(1)} %collective-permute-done.18), channel_id=1, source_target_pairs={{0,1},{2,0},{4,2},{6,4},{7,6},{5,7},{3,5},{1,3},{8,9},{10,8},{12,1... | collective-permute-start | bytes 589832 | tf_op jit(solution)/shard_map/ppermute | solution.py:71
  118.9 5.7 %collective-permute-start.22 = (bf16[32,3072]{1,0:T(8,128)(2,1)S(1)}, bf16[32,3072]{1,0:T(8,128)(2,1)S(1)}, u32[]{:S(2)}, u32[]{:S(2)}) collective-permute-start(bf16[32,3072]{1,0:T(8,128)(2,1)S(1)} %collective-permute-done.21), channel_id=1, source_target_pairs={{0,2},{2,4},{4,6},{6,7},{7,5},{5,3},{3,1},{1,0},{8,10},{10,12},{12... | collective-permute-start | bytes 589832 | tf_op jit(solution)/shard_map/ppermute | solution.py:68
  123.1 4.7 %collective-permute-start.24 = (bf16[16,3072]{1,0:T(8,128)(2,1)S(1)}, bf16[16,3072]{1,0:T(8,128)(2,1)S(1)}, u32[]{:S(2)}, u32[]{:S(2)}) collective-permute-start(bf16[16,3072]{1,0:T(8,128)(2,1)S(1)} %slice.408), channel_id=1, source_target_pairs={{0,1},{2,0},{4,2},{6,4},{7,6},{5,7},{3,5},{1,3},{8,9},{10,8},{12,1... | collective-permute-start | bytes 294920 | tf_op jit(solution)/shard_map/ppermute | solution.py:65
  124.6 4.7 %collective-permute-start.23 = (bf16[16,3072]{1,0:T(8,128)(2,1)S(1)}, bf16[16,3072]{1,0:T(8,128)(2,1)S(1)}, u32[]{:S(2)}, u32[]{:S(2)}) collective-permute-start(bf16[16,3072]{1,0:T(8,128)(2,1)S(1)} %slice.407), channel_id=1, source_target_pairs={{0,2},{2,4},{4,6},{6,7},{7,5},{5,3},{3,1},{1,0},{8,10},{10,12},{12... | collective-permute-start | bytes 294920 | tf_op jit(solution)/shard_map/ppermute | solution.py:64
  135.1 3.4 %collective-permute-start.25 = (bf16[128,3072]{1,0:T(8,128)(2,1)}, bf16[128,3072]{1,0:T(8,128)(2,1)S(1)}, u32[]{:S(2)}, u32[]{:S(2)}) collective-permute-start(bf16[128,3072]{1,0:T(8,128)(2,1)} %bitcast.36), channel_id=1, source_target_pairs={{0,8},{1,9},{2,10},{3,11},{4,12},{5,13},{6,14},{7,15},{16,24},{17,... | collective-permute-start | bytes 2359304 | tf_op jit(solution)/shard_map/ppermute | solution.py:14
  159.7 5.2 %collective-permute-start.26 = (bf16[16,3072]{1,0:T(8,128)(2,1)S(1)}, bf16[16,3072]{1,0:T(8,128)(2,1)S(1)}, u32[]{:S(2)}, u32[]{:S(2)}) collective-permute-start(bf16[16,3072]{1,0:T(8,128)(2,1)S(1)} %get-tuple-element.119), channel_id=1, source_target_pairs={{0,2},{2,4},{4,6},{6,7},{7,5},{5,3},{3,1},{1,0},{8,10},{10,12},{12... | collective-permute-start | bytes 294920 | tf_op jit(solution)/shard_map/ppermute | solution.py:108
  160.3 5.3 %collective-permute-start.30 = (bf16[16,3072]{1,0:T(8,128)(2,1)S(1)}, bf16[16,3072]{1,0:T(8,128)(2,1)S(1)}, u32[]{:S(2)}, u32[]{:S(2)}) collective-permute-start(bf16[16,3072]{1,0:T(8,128)(2,1)S(1)} %get-tuple-element.120), channel_id=1, source_target_pairs={{0,1},{2,0},{4,2},{6,4},{7,6},{5,7},{3,5},{1,3},{8,9},{10,8},{12,1... | collective-permute-start | bytes 294920 | tf_op jit(solution)/shard_map/ppermute | solution.py:108
  165.0 6.5 %collective-permute-start.27 = (bf16[32,3072]{1,0:T(8,128)(2,1)S(1)}, bf16[32,3072]{1,0:T(8,128)(2,1)S(1)}, u32[]{:S(2)}, u32[]{:S(2)}) collective-permute-start(bf16[32,3072]{1,0:T(8,128)(2,1)S(1)} %convert_element_type.350), channel_id=1, source_target_pairs={{0,2},{2,4},{4,6},{6,7},{7,5},{5,3},{3,1},{1,0},{8,10},{10,12},{12... | collective-permute-start | bytes 589832 | tf_op jit(solution)/shard_map/ppermute | solution.py:108
  165.7 6.5 %collective-permute-start.31 = (bf16[32,3072]{1,0:T(8,128)(2,1)S(1)}, bf16[32,3072]{1,0:T(8,128)(2,1)S(1)}, u32[]{:S(2)}, u32[]{:S(2)}) collective-permute-start(bf16[32,3072]{1,0:T(8,128)(2,1)S(1)} %convert_element_type.360), channel_id=1, source_target_pairs={{0,1},{2,0},{4,2},{6,4},{7,6},{5,7},{3,5},{1,3},{8,9},{10,8},{12,1... | collective-permute-start | bytes 589832 | tf_op jit(solution)/shard_map/ppermute | solution.py:108
  171.5 5.7 %collective-permute-start.28 = (bf16[32,3072]{1,0:T(8,128)(2,1)S(1)}, bf16[32,3072]{1,0:T(8,128)(2,1)S(1)}, u32[]{:S(2)}, u32[]{:S(2)}) collective-permute-start(bf16[32,3072]{1,0:T(8,128)(2,1)S(1)} %add_convert_fusion.9), channel_id=1, source_target_pairs={{0,2},{2,4},{4,6},{6,7},{7,5},{5,3},{3,1},{1,0},{8,10},{10,12},{12... | collective-permute-start | bytes 589832 | tf_op jit(solution)/shard_map/ppermute | solution.py:108
  177.3 6.6 %collective-permute-start.32 = (bf16[32,3072]{1,0:T(8,128)(2,1)S(1)}, bf16[32,3072]{1,0:T(8,128)(2,1)S(1)}, u32[]{:S(2)}, u32[]{:S(2)}) collective-permute-start(bf16[32,3072]{1,0:T(8,128)(2,1)S(1)} %get-tuple-element.110), channel_id=1, source_target_pairs={{0,1},{2,0},{4,2},{6,4},{7,6},{5,7},{3,5},{1,3},{8,9},{10,8},{12,1... | collective-permute-start | bytes 589832 | tf_op jit(solution)/shard_map/ppermute | solution.py:108
  179.0 6.6 %collective-permute-start.29 = (bf16[32,3072]{1,0:T(8,128)(2,1)S(1)}, bf16[32,3072]{1,0:T(8,128)(2,1)S(1)}, u32[]{:S(2)}, u32[]{:S(2)}) collective-permute-start(bf16[32,3072]{1,0:T(8,128)(2,1)S(1)} %get-tuple-element.109), channel_id=1, source_target_pairs={{0,2},{2,4},{4,6},{6,7},{7,5},{5,3},{3,1},{1,0},{8,10},{10,12},{12... | collective-permute-start | bytes 589832 | tf_op jit(solution)/shard_map/ppermute | solution.py:108
  184.0 7.0 %collective-permute-start.33 = (bf16[32,3072]{1,0:T(8,128)(2,1)S(1)}, bf16[32,3072]{1,0:T(8,128)(2,1)S(1)}, u32[]{:S(2)}, u32[]{:S(2)}) collective-permute-start(bf16[32,3072]{1,0:T(8,128)(2,1)S(1)} %add_convert_fusion.6), channel_id=1, source_target_pairs={{0,1},{2,0},{4,2},{6,4},{7,6},{5,7},{3,5},{1,3},{8,9},{10,8},{12,1... | collective-permute-start | bytes 589832 | tf_op jit(solution)/shard_map/ppermute | solution.py:108
  191.8 6.6 %collective-permute-start.34 = (bf16[32,3072]{1,0:T(8,128)(2,1)S(1)}, bf16[32,3072]{1,0:T(8,128)(2,1)S(1)}, u32[]{:S(2)}, u32[]{:S(2)}) collective-permute-start(bf16[32,3072]{1,0:T(8,128)(2,1)S(1)} %get-tuple-element.96), channel_id=1, source_target_pairs={{0,1},{2,0},{4,2},{6,4},{7,6},{5,7},{3,5},{1,3},{8,9},{10,8},{12,1... | collective-permute-start | bytes 589832 | tf_op jit(solution)/shard_map/ppermute | solution.py:59
  193.4 6.6 %collective-permute-start.37 = (bf16[32,3072]{1,0:T(8,128)(2,1)S(1)}, bf16[32,3072]{1,0:T(8,128)(2,1)S(1)}, u32[]{:S(2)}, u32[]{:S(2)}) collective-permute-start(bf16[32,3072]{1,0:T(8,128)(2,1)S(1)} %get-tuple-element.96), channel_id=1, source_target_pairs={{0,2},{2,4},{4,6},{6,7},{7,5},{5,3},{3,1},{1,0},{8,10},{10,12},{12... | collective-permute-start | bytes 589832 | tf_op jit(solution)/shard_map/ppermute | solution.py:58
  198.4 5.8 %collective-permute-start.35 = (bf16[32,3072]{1,0:T(8,128)(2,1)S(1)}, bf16[32,3072]{1,0:T(8,128)(2,1)S(1)}, u32[]{:S(2)}, u32[]{:S(2)}) collective-permute-start(bf16[32,3072]{1,0:T(8,128)(2,1)S(1)} %collective-permute-done.34), channel_id=1, source_target_pairs={{0,1},{2,0},{4,2},{6,4},{7,6},{5,7},{3,5},{1,3},{8,9},{10,8},{12,1... | collective-permute-start | bytes 589832 | tf_op jit(solution)/shard_map/ppermute | solution.py:71
  200.0 5.8 %collective-permute-start.38 = (bf16[32,3072]{1,0:T(8,128)(2,1)S(1)}, bf16[32,3072]{1,0:T(8,128)(2,1)S(1)}, u32[]{:S(2)}, u32[]{:S(2)}) collective-permute-start(bf16[32,3072]{1,0:T(8,128)(2,1)S(1)} %collective-permute-done.37), channel_id=1, source_target_pairs={{0,2},{2,4},{4,6},{6,7},{7,5},{5,3},{3,1},{1,0},{8,10},{10,12},{12... | collective-permute-start | bytes 589832 | tf_op jit(solution)/shard_map/ppermute | solution.py:68
  204.2 5.7 %collective-permute-start.36 = (bf16[32,3072]{1,0:T(8,128)(2,1)S(1)}, bf16[32,3072]{1,0:T(8,128)(2,1)S(1)}, u32[]{:S(2)}, u32[]{:S(2)}) collective-permute-start(bf16[32,3072]{1,0:T(8,128)(2,1)S(1)} %collective-permute-done.35), channel_id=1, source_target_pairs={{0,1},{2,0},{4,2},{6,4},{7,6},{5,7},{3,5},{1,3},{8,9},{10,8},{12,1... | collective-permute-start | bytes 589832 | tf_op jit(solution)/shard_map/ppermute | solution.py:71
  205.7 5.7 %collective-permute-start.39 = (bf16[32,3072]{1,0:T(8,128)(2,1)S(1)}, bf16[32,3072]{1,0:T(8,128)(2,1)S(1)}, u32[]{:S(2)}, u32[]{:S(2)}) collective-permute-start(bf16[32,3072]{1,0:T(8,128)(2,1)S(1)} %collective-permute-done.38), channel_id=1, source_target_pairs={{0,2},{2,4},{4,6},{6,7},{7,5},{5,3},{3,1},{1,0},{8,10},{10,12},{12... | collective-permute-start | bytes 589832 | tf_op jit(solution)/shard_map/ppermute | solution.py:68
  209.8 4.7 %collective-permute-start.41 = (bf16[16,3072]{1,0:T(8,128)(2,1)S(1)}, bf16[16,3072]{1,0:T(8,128)(2,1)S(1)}, u32[]{:S(2)}, u32[]{:S(2)}) collective-permute-start(bf16[16,3072]{1,0:T(8,128)(2,1)S(1)} %slice.423), channel_id=1, source_target_pairs={{0,1},{2,0},{4,2},{6,4},{7,6},{5,7},{3,5},{1,3},{8,9},{10,8},{12,1... | collective-permute-start | bytes 294920 | tf_op jit(solution)/shard_map/ppermute | solution.py:65
  211.5 4.7 %collective-permute-start.40 = (bf16[16,3072]{1,0:T(8,128)(2,1)S(1)}, bf16[16,3072]{1,0:T(8,128)(2,1)S(1)}, u32[]{:S(2)}, u32[]{:S(2)}) collective-permute-start(bf16[16,3072]{1,0:T(8,128)(2,1)S(1)} %slice.422), channel_id=1, source_target_pairs={{0,2},{2,4},{4,6},{6,7},{7,5},{5,3},{3,1},{1,0},{8,10},{10,12},{12... | collective-permute-start | bytes 294920 | tf_op jit(solution)/shard_map/ppermute | solution.py:64
  221.4 1.7 copy-start.3
  224.7 2.9 %collective-permute-start.42 = (bf16[256,128]{1,0:T(8,128)(2,1)S(1)}, bf16[256,128]{1,0:T(8,128)(2,1)S(1)}, u32[]{:S(2)}, u32[]{:S(2)}) collective-permute-start(bf16[256,128]{1,0:T(8,128)(2,1)S(1)} %convolution_convert_fusion.7), channel_id=1, source_target_pairs={{0,8},{1,9},{2,10},{3,11},{4,12},{5,13},{6,14},{7,15},{16,24},{17,... | collective-permute-start | bytes 196616 | tf_op jit(solution)/shard_map/ppermute | solution.py:14
  226.0 2.2 collective-permute-start.43
  230.7 4.7 %collective-permute-start.44 = (bf16[16,3072]{1,0:T(8,128)(2,1)S(1)}, bf16[16,3072]{1,0:T(8,128)(2,1)S(1)}, u32[]{:S(2)}, u32[]{:S(2)}) collective-permute-start(bf16[16,3072]{1,0:T(8,128)(2,1)S(1)} %get-tuple-element.117), channel_id=1, source_target_pairs={{0,2},{2,4},{4,6},{6,7},{7,5},{5,3},{3,1},{1,0},{8,10},{10,12},{12... | collective-permute-start | bytes 294920 | tf_op jit(solution)/shard_map/ppermute | solution.py:108
  231.2 4.7 %collective-permute-start.48 = (bf16[16,3072]{1,0:T(8,128)(2,1)S(1)}, bf16[16,3072]{1,0:T(8,128)(2,1)S(1)}, u32[]{:S(2)}, u32[]{:S(2)}) collective-permute-start(bf16[16,3072]{1,0:T(8,128)(2,1)S(1)} %get-tuple-element.118), channel_id=1, source_target_pairs={{0,1},{2,0},{4,2},{6,4},{7,6},{5,7},{3,5},{1,3},{8,9},{10,8},{12,1... | collective-permute-start | bytes 294920 | tf_op jit(solution)/shard_map/ppermute | solution.py:108
  235.5 7.7 %collective-permute-start.45 = (bf16[32,3072]{1,0:T(8,128)(2,1)S(1)}, bf16[32,3072]{1,0:T(8,128)(2,1)S(1)}, u32[]{:S(2)}, u32[]{:S(2)}) collective-permute-start(bf16[32,3072]{1,0:T(8,128)(2,1)S(1)} %convert_element_type.384), channel_id=1, source_target_pairs={{0,2},{2,4},{4,6},{6,7},{7,5},{5,3},{3,1},{1,0},{8,10},{10,12},{12... | collective-permute-start | bytes 589832 | tf_op jit(solution)/shard_map/ppermute | solution.py:108
  236.0 7.7 %collective-permute-start.49 = (bf16[32,3072]{1,0:T(8,128)(2,1)S(1)}, bf16[32,3072]{1,0:T(8,128)(2,1)S(1)}, u32[]{:S(2)}, u32[]{:S(2)}) collective-permute-start(bf16[32,3072]{1,0:T(8,128)(2,1)S(1)} %convert_element_type.394), channel_id=1, source_target_pairs={{0,1},{2,0},{4,2},{6,4},{7,6},{5,7},{3,5},{1,3},{8,9},{10,8},{12,1... | collective-permute-start | bytes 589832 | tf_op jit(solution)/shard_map/ppermute | solution.py:108
  243.2 7.1 %collective-permute-start.46 = (bf16[32,3072]{1,0:T(8,128)(2,1)S(1)}, bf16[32,3072]{1,0:T(8,128)(2,1)S(1)}, u32[]{:S(2)}, u32[]{:S(2)}) collective-permute-start(bf16[32,3072]{1,0:T(8,128)(2,1)S(1)} %add_convert_fusion.4), channel_id=1, source_target_pairs={{0,2},{2,4},{4,6},{6,7},{7,5},{5,3},{3,1},{1,0},{8,10},{10,12},{12... | collective-permute-start | bytes 589832 | tf_op jit(solution)/shard_map/ppermute | solution.py:108
  250.4 6.3 %collective-permute-start.50 = (bf16[32,3072]{1,0:T(8,128)(2,1)S(1)}, bf16[32,3072]{1,0:T(8,128)(2,1)S(1)}, u32[]{:S(2)}, u32[]{:S(2)}) collective-permute-start(bf16[32,3072]{1,0:T(8,128)(2,1)S(1)} %get-tuple-element.106), channel_id=1, source_target_pairs={{0,1},{2,0},{4,2},{6,4},{7,6},{5,7},{3,5},{1,3},{8,9},{10,8},{12,1... | collective-permute-start | bytes 589832 | tf_op jit(solution)/shard_map/ppermute | solution.py:108
  251.9 6.3 %collective-permute-start.47 = (bf16[32,3072]{1,0:T(8,128)(2,1)S(1)}, bf16[32,3072]{1,0:T(8,128)(2,1)S(1)}, u32[]{:S(2)}, u32[]{:S(2)}) collective-permute-start(bf16[32,3072]{1,0:T(8,128)(2,1)S(1)} %get-tuple-element.105), channel_id=1, source_target_pairs={{0,2},{2,4},{4,6},{6,7},{7,5},{5,3},{3,1},{1,0},{8,10},{10,12},{12... | collective-permute-start | bytes 589832 | tf_op jit(solution)/shard_map/ppermute | solution.py:108
  256.7 5.7 %collective-permute-start.51 = (bf16[32,3072]{1,0:T(8,128)(2,1)S(1)}, bf16[32,3072]{1,0:T(8,128)(2,1)S(1)}, u32[]{:S(2)}, u32[]{:S(2)}) collective-permute-start(bf16[32,3072]{1,0:T(8,128)(2,1)S(1)} %add_convert_fusion.1), channel_id=1, source_target_pairs={{0,1},{2,0},{4,2},{6,4},{7,6},{5,7},{3,5},{1,3},{8,9},{10,8},{12,1... | collective-permute-start | bytes 589832 | tf_op jit(solution)/shard_map/ppermute | solution.py:108

commit v13 on v11

--- a/solution.py
+++ b/solution.py
@@ -134,7 +134,7 @@
     return lax.optimization_barrier(term.astype(jnp.bfloat16)).astype(jnp.float32)
 
 
-def conv_gate_kernel(slab_ref, gain_ref, weight_ref, out_ref, filt_acc, gate_acc):
+def conv_gate_kernel(head_at_ref, slab_ref, gain_ref, weight_ref, mix_ref, out_ref, filt_acc, gate_acc, gated, ordered):
     tap = pl.program_id(0)
     chunk = pl.program_id(1)
 
@@ -151,10 +151,18 @@
 
     @pl.when((tap == pl.num_programs(0) - 1) & (chunk == pl.num_programs(1) - 1))
     def _():
-        out_ref[...] = (jnp.tanh(filt_acc[...]) * jax.nn.sigmoid(gate_acc[...])).astype(out_ref.dtype)
-
-
-def convolution_gate(state, gain, conv_by_half, layer_idx, dilation_factor):
+        gated[...] = (jnp.tanh(filt_acc[...]) * jax.nn.sigmoid(gate_acc[...])).astype(jnp.bfloat16).astype(jnp.float32)
+        blocks = head_at_ref.shape[0]
+        block_rows = gated.shape[0] // blocks
+        for m in range(blocks):
+            start = pl.multiple_of(head_at_ref[m] * block_rows, block_rows)
+            ordered[m * block_rows : (m + 1) * block_rows, :] = gated[pl.ds(start, block_rows), :]
+        out_ref[...] = jnp.dot(
+            ordered[...].astype(jnp.bfloat16), mix_ref[...], preferred_element_type=jnp.float32
+        ).astype(out_ref.dtype)
+
+
+def convolution_gate(state, gain, conv_by_half, layer_idx, dilation_factor, w_mix, head_at):
     hidden = state
     all_rows = hidden.shape[0]
     width = hidden.shape[1]
@@ -172,22 +180,26 @@
     chunk = width
     return pl.pallas_call(
         conv_gate_kernel,
-        out_shape=jax.ShapeDtypeStruct((all_rows, own_width), jnp.bfloat16),
-        grid=(taps, width // chunk),
-        in_specs=[
-            pl.BlockSpec((None, all_rows, chunk), lambda t, k: (t, 0, k)),
-            pl.BlockSpec((1, width), lambda t, k: (0, 0)),
-            pl.BlockSpec((None, None, 2, chunk, own_width), lambda t, k: (layer_idx, t, 0, k, 0)),
-        ],
-        out_specs=pl.BlockSpec((all_rows, own_width), lambda t, k: (0, 0)),
-        scratch_shapes=[pltpu.VMEM((all_rows, own_width), jnp.float32)] * 2,
+        out_shape=jax.ShapeDtypeStruct((all_rows, width), jnp.bfloat16),
+        grid_spec=pltpu.PrefetchScalarGridSpec(
+            num_scalar_prefetch=1,
+            grid=(taps, width // chunk),
+            in_specs=[
+                pl.BlockSpec((None, all_rows, chunk), lambda t, k, h: (t, 0, k)),
+                pl.BlockSpec((1, width), lambda t, k, h: (0, 0)),
+                pl.BlockSpec((None, None, 2, chunk, own_width), lambda t, k, h: (layer_idx, t, 0, k, 0)),
+                pl.BlockSpec((None, own_width, width), lambda t, k, h: (layer_idx, 0, 0)),
+            ],
+            out_specs=pl.BlockSpec((all_rows, width), lambda t, k, h: (0, 0)),
+            scratch_shapes=[pltpu.VMEM((all_rows, own_width), jnp.float32)] * 4,
+        ),
         compiler_params=pltpu.CompilerParams(dimension_semantics=("arbitrary", "arbitrary")),
         cost_estimate=pl.CostEstimate(
             flops=4 * taps * all_rows * width * own_width,
             transcendentals=2 * all_rows * own_width,
             bytes_accessed=2 * taps * (all_rows * width + 2 * width * own_width + all_rows * own_width // taps),
         ),
-    )(slabs, gain.reshape(1, width), conv_by_half)
+    )(head_at, slabs, gain.reshape(1, width), conv_by_half, w_mix)
 
 
 def far_rows(ordered, tok_rows):
@@ -264,10 +276,10 @@
     state = ring_gather(stream, "head", tables, direct=2)
     conv_by_half = jnp.transpose(w_conv, (0, 1, 3, 2, 4))
     for layer_idx in range(layers):
-        gated = convolution_gate(
-            state, gains[layer_idx], conv_by_half, layer_idx, dilations[layer_idx]
+        mixed_rows = convolution_gate(
+            state, gains[layer_idx], conv_by_half, layer_idx, dilations[layer_idx], w_mix, tables[0]
         )
-        summed = conv_share(gated, w_mix[layer_idx], tok_rows, tables)
+        summed = ring_scatter_sum(mixed_rows, "head", tables)
         share = (share.astype(jnp.float32) + summed).astype(jnp.bfloat16)
         state = ring_gather(share, "head", tables)
     all_rows = state.shape[0]

time: 260 us -> 274 us (1.054)
  waiting for transfers between devices: 97.5 us -> 113 us
  matrix products: 12.6 us -> 2.93 us
  Pallas kernels: 21.7 us -> 27.3 us
  other arithmetic: 17.2 us -> 20.3 us
    ppermute x5, waiting for transfers between devices: 0.01 us -> 11.3 us  [ring_gather(): fwd = lax.ppermute(fwd, axis, forward)]
    dot_general x6 -> x2, matrix products: 10.4 us -> 0.8 us  [rounded_term(): term = jnp.dot(left, right, preferred_element_type=jnp.float32)]
    ppermute x24, waiting for transfers between devices: 62.4 us -> 71 us  [chain(): passed = lax.ppermute(part.astype(value.dtype), axis, pairs)]
    ppermute x5, waiting for transfers between devices: 14.2 us -> 5.71 us  [ring_gather(): bwd = lax.ppermute(bwd, axis, backward)]
    pallas_call x2, Pallas kernels: 21.7 us -> 27.3 us  [convolution_gate(): pl.pallas_call(conv_gate_kernel, out_shape=jax.ShapeDtypeStruct((all_rows...]
    ppermute x5, starting transfers between devices: 2.03 us -> 6.81 us  [ring_gather(): fwd = lax.ppermute(fwd, axis, forward)]
    ppermute x4, waiting for transfers between devices: 8.6 us -> 12.5 us  [ring_gather(): lax.ppermute(value, axis, [(order[p], order[(p - k) % length]) for p in r...]
    ppermute x24, starting transfers between devices: 25.2 us -> 21.5 us  [chain(): passed = lax.ppermute(part.astype(value.dtype), axis, pairs)]
  transfers between devices with their start and end apart: 52 -> 52, of which waited for: 29 -> 37; matrix products, arithmetic and copies ran while one was open for 15% -> 13% of each run, Pallas kernels for 0% -> 0%
where the time goes in v13:
time: 274 us; the launch traced here: 273 us
  waiting for transfers between devices  113 us (41%)
  starting transfers between devices  58.4 us (21%)
  local copies, waits for them, and re-layouts  47 us (17%)
  Pallas kernels  27.3 us (10%)
  other arithmetic  20.3 us (7%)
  between operations  4.52 us (2%)
  matrix products  2.93 us (1%)
    ppermute x24, waiting for transfers between devices, chain(): passed = lax.ppermute(part.astype(value.dtype), axis, pairs)  71 us
    unnamed x33, local copies, waits for them, and re-layouts  33 us
    pallas_call x2, Pallas kernels, convolution_gate(): pl.pallas_call(conv_gate_kernel, out_shape=jax.ShapeDtypeStruct((all_rows...  27.3 us
    ppermute x24, starting transfers between devices, chain(): passed = lax.ppermute(part.astype(value.dtype), axis, pairs)  21.5 us
    ppermute x4, waiting for transfers between devices, ring_gather(): lax.ppermute(value, axis, [(order[p], order[(p - k) % length]) for p in r...  12.5 us
    ppermute x5, waiting for transfers between devices, ring_gather(): fwd = lax.ppermute(fwd, axis, forward)  11.3 us
    another operation x4, other arithmetic, convolution_gate(): jnp.stack([lax.dynamic_slice_in_dim(padded, border_rows - tap_idx * dilat...  10.7 us
    ppermute x4, starting transfers between devices, ring_gather(): lax.ppermute(value, axis, [(order[p], order[(p - k) % length]) for p in r...  8.05 us
  transfers between devices with their start and end apart: 52, of which 37 were waited for; matrix products, arithmetic and copies ran while one was open for 13% of the time, Pallas kernels for 0%

profile of v13, /device:TPU:0, one launch (start us, length us, event | category | flops | bytes accessed | tf_op | source)
XLA Modules:
  0.0 273.4 jit_solution(11671109335838217155)
XLA Ops:
  0.0 4.0 %collective-permute-start.1 = (bf16[32,3072]{1,0:T(8,128)(2,1)}, bf16[32,3072]{1,0:T(8,128)(2,1)S(1)}, u32[]{:S(2)}, u32[]{:S(2)}) collective-permute-start(bf16[32,3072]{1,0:T(8,128)(2,1)} %param.22), channel_id=1, source_target_pairs={{0,3},{2,1},{4,0},{6,2},{7,4},{5,6},{3,7},{1,5},{8,11},{10,9},{12,... | collective-permute-start | bytes 589832 | tf_op jit(solution)/shard_map/ppermute | solution.py:59
  4.0 1.6 collective-permute-start
  6.1 1.7 bitcast_dynamic-update-slice_fusion.20
  7.8 1.3 fusion.34
  9.1 5.2 %collective-permute-done.1 = bf16[32,3072]{1,0:T(8,128)(2,1)S(1)} collective-permute-done((bf16[32,3072]{1,0:T(8,128)(2,1)}, bf16[32,3072]{1,0:T(8,128)(2,1)S(1)}, u32[]{:S(2)}, u32[]{:S(2)}) %collective-permute-start.1) | collective-permute-done | bytes 196640 | tf_op jit(solution)/shard_map/ppermute | solution.py:59
  14.2 2.9 %collective-permute-done.3 = bf16[32,3072]{1,0:T(8,128)(2,1)S(1)} collective-permute-done((bf16[32,3072]{1,0:T(8,128)(2,1)}, bf16[32,3072]{1,0:T(8,128)(2,1)S(1)}, u32[]{:S(2)}, u32[]{:S(2)}) %collective-permute-start.3) | collective-permute-done | bytes 196640 | tf_op jit(solution)/shard_map/ppermute | solution.py:58
  17.1 4.3 %collective-permute-start.4 = (bf16[32,3072]{1,0:T(8,128)(2,1)S(1)}, bf16[32,3072]{1,0:T(8,128)(2,1)S(1)}, u32[]{:S(2)}, u32[]{:S(2)}) collective-permute-start(bf16[32,3072]{1,0:T(8,128)(2,1)S(1)} %collective-permute-done.3), channel_id=1, source_target_pairs={{0,2},{2,4},{4,6},{6,7},{7,5},{5,3},{3,1},{1,0},{8,10},{10,12},{12... | collective-permute-start | bytes 589832 | tf_op jit(solution)/shard_map/ppermute | solution.py:68
  22.8 2.4 collective-permute-done.4
  25.3 2.5 collective-permute-start.5
  28.6 1.4 collective-permute-done.5
  30.0 2.5 collective-permute-done.6
  35.3 2.1 gather_fusion
  37.4 2.2 collective-permute-start.8
  42.3 19.6 %copy.11 = bf16[2,3,3072,2,384]{4,2,3,1,0:T(8,128)(2,1)} copy(bf16[2,3,3072,2,384]{4,3,2,1,0:T(2,128)(2,1)} %param.25) | data formatting | bytes 56623104 | tf_op args[3]
  62.6 2.8 %fusion.15 = (bf16[1,256,3072]{2,1,0:T(8,128)(2,1)S(1)}, bf16[1,256,3072]{2,1,0:T(8,128)(2,1)S(1)}) fusion(s32[]{:T(128)S(6)} %select_n.21, bf16[256,3072]{1,0:T(8,128)(2,1)S(1)} %bitcast.119, bf16[128,3072]{1,0:T(8,128)(2,1)} %collective-permute-done.8, s32[]{:T(128)S(6)} %select_n.22), kind=kLoop, calls=%fused_computation.35 | loop fusion | flops 6291456 | bytes 5505032 | tf_op jit(solution)/shard_map/stack | solution.py:174
  65.4 2.4 pad_maximum_fusion.slab_ref
  67.8 13.7 %shard_map.82 = bf16[256,3072]{1,0:T(8,128)(2,1)} custom-call(s32[8]{0:T(128)} %get-tuple-element.127.head_at_ref, bf16[3,256,3072]{2,1,0:T(8,128)(2,1)} %pad_maximum_fusion.slab_ref, f32[1,3072]{1,0:T(1,128)} %get-tuple-element.124.gain_ref, bf16[2,3,2,3072,384]{4,3,2,1,0:T(8,128)(2,1)} %bitcast.117, bf16[2,384,3072]{2,1,0:T(8,128)(2,1)} %mix_ref.3), custom_call_target="tpu_custom_call" | custom-call | flops 3623878656 | bytes 19070976 | tf_op jit(solution)/shard_map/pallas_call | solution.py:181
  83.7 1.9 collective-permute-start.13
  85.6 1.6 collective-permute-done.9
  88.4 1.9 collective-permute-start.14
  90.4 2.6 collective-permute-done.10
  93.1 2.9 %collective-permute-done.14 = bf16[32,3072]{1,0:T(8,128)(2,1)S(1)} collective-permute-done((bf16[32,3072]{1,0:T(8,128)(2,1)S(1)}, bf16[32,3072]{1,0:T(8,128)(2,1)S(1)}, u32[]{:S(2)}, u32[]{:S(2)}) %collective-permute-start.14) | collective-permute-done | bytes 196640 | tf_op jit(solution)/shard_map/ppermute | solution.py:108
  96.0 4.5 %collective-permute-done.11 = bf16[32,3072]{1,0:T(8,128)(2,1)S(1)} collective-permute-done((bf16[32,3072]{1,0:T(8,128)(2,1)S(1)}, bf16[32,3072]{1,0:T(8,128)(2,1)S(1)}, u32[]{:S(2)}, u32[]{:S(2)}) %collective-permute-start.11) | collective-permute-done | bytes 196640 | tf_op jit(solution)/shard_map/ppermute | solution.py:108
  101.2 1.4 collective-permute-start.12
  102.6 5.7 %collective-permute-done.15 = bf16[32,3072]{1,0:T(8,128)(2,1)S(1)} collective-permute-done((bf16[32,3072]{1,0:T(8,128)(2,1)S(1)}, bf16[32,3072]{1,0:T(8,128)(2,1)S(1)}, u32[]{:S(2)}, u32[]{:S(2)}) %collective-permute-start.15) | collective-permute-done | bytes 196640 | tf_op jit(solution)/shard_map/ppermute | solution.py:108
  108.4 6.7 %collective-permute-done.16 = bf16[32,3072]{1,0:T(8,128)(2,1)S(1)} collective-permute-done((bf16[32,3072]{1,0:T(8,128)(2,1)S(1)}, bf16[32,3072]{1,0:T(8,128)(2,1)S(1)}, u32[]{:S(2)}, u32[]{:S(2)}) %collective-permute-start.16) | collective-permute-done | bytes 196640 | tf_op jit(solution)/shard_map/ppermute | solution.py:108
  116.7 1.3 collective-permute-start.20
  118.0 3.6 %collective-permute-done.17 = bf16[32,3072]{1,0:T(8,128)(2,1)S(1)} collective-permute-done((bf16[32,3072]{1,0:T(8,128)(2,1)S(1)}, bf16[32,3072]{1,0:T(8,128)(2,1)S(1)}, u32[]{:S(2)}, u32[]{:S(2)}) %collective-permute-start.17) | collective-permute-done | bytes 196640 | tf_op jit(solution)/shard_map/ppermute | solution.py:59
  124.4 2.9 %collective-permute-done.18 = bf16[32,3072]{1,0:T(8,128)(2,1)S(1)} collective-permute-done((bf16[32,3072]{1,0:T(8,128)(2,1)S(1)}, bf16[32,3072]{1,0:T(8,128)(2,1)S(1)}, u32[]{:S(2)}, u32[]{:S(2)}) %collective-permute-start.18) | collective-permute-done | bytes 196640 | tf_op jit(solution)/shard_map/ppermute | solution.py:71
  130.1 3.7 %collective-permute-done.22 = bf16[32,3072]{1,0:T(8,128)(2,1)S(1)} collective-permute-done((bf16[32,3072]{1,0:T(8,128)(2,1)S(1)}, bf16[32,3072]{1,0:T(8,128)(2,1)S(1)}, u32[]{:S(2)}, u32[]{:S(2)}) %collective-permute-start.22) | collective-permute-done | bytes 196640 | tf_op jit(solution)/shard_map/ppermute | solution.py:68
  136.7 1.8 collective-permute-done.23
  142.6 2.1 gather_fusion.1
  144.7 2.2 collective-permute-start.25
  149.1 3.1 %fusion.11 = (bf16[1,256,3072]{2,1,0:T(8,128)(2,1)S(1)}, bf16[1,256,3072]{2,1,0:T(8,128)(2,1)S(1)}) fusion(s32[]{:T(128)S(6)} %select_n.23, bf16[256,3072]{1,0:T(8,128)(2,1)S(1)} %bitcast.121, bf16[128,3072]{1,0:T(8,128)(2,1)} %collective-permute-done.25, s32[]{:T(128)S(6)} %select_n.24), kind=kLoop, calls=%fused_computation.31 | loop fusion | flops 6291456 | bytes 5505032 | tf_op jit(solution)/shard_map/stack | solution.py:174
  152.1 2.4 pad_maximum_fusion.1.slab_ref
  154.5 13.7 %shard_map.83 = bf16[256,3072]{1,0:T(8,128)(2,1)} custom-call(s32[8]{0:T(128)} %get-tuple-element.127.head_at_ref, bf16[3,256,3072]{2,1,0:T(8,128)(2,1)} %pad_maximum_fusion.1.slab_ref, f32[1,3072]{1,0:T(1,128)} %get-tuple-element.125.gain_ref, bf16[2,3,2,3072,384]{4,3,2,1,0:T(8,128)(2,1)} %bitcast.118, bf16[2,384,3072]{2,1,0:T(8,128)(2,1)} %mix_ref.3), custom_call_target="tpu_custom_call" | custom-call | flops 3623878656 | bytes 19070976 | tf_op jit(solution)/shard_map/pallas_call | solution.py:181
  170.4 1.9 collective-permute-start.30
  172.4 1.5 collective-permute-done.26
  175.2 1.9 collective-permute-start.31
  177.1 2.7 collective-permute-done.27
  180.9 5.1 %collective-permute-done.28 = bf16[32,3072]{1,0:T(8,128)(2,1)S(1)} collective-permute-done((bf16[32,3072]{1,0:T(8,128)(2,1)S(1)}, bf16[32,3072]{1,0:T(8,128)(2,1)S(1)}, u32[]{:S(2)}, u32[]{:S(2)}) %collective-permute-start.28) | collective-permute-done | bytes 196640 | tf_op jit(solution)/shard_map/ppermute | solution.py:108
  186.4 1.7 collective-permute-start.29
  188.1 5.0 %collective-permute-done.32 = bf16[32,3072]{1,0:T(8,128)(2,1)S(1)} collective-permute-done((bf16[32,3072]{1,0:T(8,128)(2,1)S(1)}, bf16[32,3072]{1,0:T(8,128)(2,1)S(1)}, u32[]{:S(2)}, u32[]{:S(2)}) %collective-permute-start.32) | collective-permute-done | bytes 196640 | tf_op jit(solution)/shard_map/ppermute | solution.py:108
  194.3 5.9 %collective-permute-done.33 = bf16[32,3072]{1,0:T(8,128)(2,1)S(1)} collective-permute-done((bf16[32,3072]{1,0:T(8,128)(2,1)S(1)}, bf16[32,3072]{1,0:T(8,128)(2,1)S(1)}, u32[]{:S(2)}, u32[]{:S(2)}) %collective-permute-start.33) | collective-permute-done | bytes 196640 | tf_op jit(solution)/shard_map/ppermute | solution.py:108
  200.9 1.8 collective-permute-start.34
  202.9 3.6 %collective-permute-done.34 = bf16[32,3072]{1,0:T(8,128)(2,1)S(1)} collective-permute-done((bf16[32,3072]{1,0:T(8,128)(2,1)S(1)}, bf16[32,3072]{1,0:T(8,128)(2,1)S(1)}, u32[]{:S(2)}, u32[]{:S(2)}) %collective-permute-start.34) | collective-permute-done | bytes 196640 | tf_op jit(solution)/shard_map/ppermute | solution.py:59
  206.6 2.1 collective-permute-start.35
  209.4 2.8 %collective-permute-done.35 = bf16[32,3072]{1,0:T(8,128)(2,1)S(1)} collective-permute-done((bf16[32,3072]{1,0:T(8,128)(2,1)S(1)}, bf16[32,3072]{1,0:T(8,128)(2,1)S(1)}, u32[]{:S(2)}, u32[]{:S(2)}) %collective-permute-start.35) | collective-permute-done | bytes 196640 | tf_op jit(solution)/shard_map/ppermute | solution.py:71
  212.2 2.1 collective-permute-start.36
  215.2 5.0 %collective-permute-done.39 = bf16[32,3072]{1,0:T(8,128)(2,1)S(1)} collective-permute-done((bf16[32,3072]{1,0:T(8,128)(2,1)S(1)}, bf16[32,3072]{1,0:T(8,128)(2,1)S(1)}, u32[]{:S(2)}, u32[]{:S(2)}) %collective-permute-start.39) | collective-permute-done | bytes 196640 | tf_op jit(solution)/shard_map/ppermute | solution.py:68
  220.3 2.1 collective-permute-start.41
  223.0 1.8 collective-permute-done.40
  227.8 2.1 gather_fusion.2
  233.6 1.3 collective-permute-start.42
  235.1 1.3 collective-permute-start.43
  240.7 1.9 collective-permute-start.48
  242.5 2.5 collective-permute-done.44
  245.4 1.9 collective-permute-start.49
  247.3 5.3 %collective-permute-done.45 = bf16[32,3072]{1,0:T(8,128)(2,1)S(1)} collective-permute-done((bf16[32,3072]{1,0:T(8,128)(2,1)S(1)}, bf16[32,3072]{1,0:T(8,128)(2,1)S(1)}, u32[]{:S(2)}, u32[]{:S(2)}) %collective-permute-start.45) | collective-permute-done | bytes 196640 | tf_op jit(solution)/shard_map/ppermute | solution.py:108
  253.1 7.1 %collective-permute-done.46 = bf16[32,3072]{1,0:T(8,128)(2,1)S(1)} collective-permute-done((bf16[32,3072]{1,0:T(8,128)(2,1)S(1)}, bf16[32,3072]{1,0:T(8,128)(2,1)S(1)}, u32[]{:S(2)}, u32[]{:S(2)}) %collective-permute-start.46) | collective-permute-done | bytes 196640 | tf_op jit(solution)/shard_map/ppermute | solution.py:108
  260.3 1.8 collective-permute-start.50
  262.4 4.5 %collective-permute-done.50 = bf16[32,3072]{1,0:T(8,128)(2,1)S(1)} collective-permute-done((bf16[32,3072]{1,0:T(8,128)(2,1)S(1)}, bf16[32,3072]{1,0:T(8,128)(2,1)S(1)}, u32[]{:S(2)}, u32[]{:S(2)}) %collective-permute-start.50) | collective-permute-done | bytes 196640 | tf_op jit(solution)/shard_map/ppermute | solution.py:108
  266.9 1.5 collective-permute-start.51
  268.4 4.2 %collective-permute-done.51 = bf16[32,3072]{1,0:T(8,128)(2,1)S(1)} collective-permute-done((bf16[32,3072]{1,0:T(8,128)(2,1)S(1)}, bf16[32,3072]{1,0:T(8,128)(2,1)S(1)}, u32[]{:S(2)}, u32[]{:S(2)}) %collective-permute-start.51) | collective-permute-done | bytes 196640 | tf_op jit(solution)/shard_map/ppermute | solution.py:108
  (149 shorter events, 48.6 us)
Async XLA Ops:
  0.0 239.5 %copy-start = (bf16[1,128,3072]{2,1,0:T(8,128)(2,1)S(1)}, bf16[1,128,3072]{2,1,0:T(8,128)(2,1)}, u32[]{:S(2)}) copy-start(bf16[1,128,3072]{2,1,0:T(8,128)(2,1)} %param.28) | copy-start | bytes 2359300
  0.0 14.2 %collective-permute-start.1 = (bf16[32,3072]{1,0:T(8,128)(2,1)}, bf16[32,3072]{1,0:T(8,128)(2,1)S(1)}, u32[]{:S(2)}, u32[]{:S(2)}) collective-permute-start(bf16[32,3072]{1,0:T(8,128)(2,1)} %param.22), channel_id=1, source_target_pairs={{0,3},{2,1},{4,0},{6,2},{7,4},{5,6},{3,7},{1,5},{8,11},{10,9},{12,... | collective-permute-start | bytes 589832 | tf_op jit(solution)/shard_map/ppermute | solution.py:59
  4.0 17.5 %collective-permute-start = (bf16[32,3072]{1,0:T(8,128)(2,1)}, bf16[32,3072]{1,0:T(8,128)(2,1)S(1)}, u32[]{:S(2)}, u32[]{:S(2)}) collective-permute-start(bf16[32,3072]{1,0:T(8,128)(2,1)} %param.22), channel_id=1, source_target_pairs={{0,1},{2,0},{4,2},{6,4},{7,6},{5,7},{3,5},{1,3},{8,9},{10,8},{12,1... | collective-permute-start | bytes 589832 | tf_op jit(solution)/shard_map/ppermute | solution.py:59
  5.6 11.6 %collective-permute-start.3 = (bf16[32,3072]{1,0:T(8,128)(2,1)}, bf16[32,3072]{1,0:T(8,128)(2,1)S(1)}, u32[]{:S(2)}, u32[]{:S(2)}) collective-permute-start(bf16[32,3072]{1,0:T(8,128)(2,1)} %param.22), channel_id=1, source_target_pairs={{0,4},{2,6},{4,7},{6,5},{7,3},{5,1},{3,0},{1,2},{8,12},{10,14},{12... | collective-permute-start | bytes 589832 | tf_op jit(solution)/shard_map/ppermute | solution.py:58
  5.9 28.7 %collective-permute-start.7 = (bf16[32,3072]{1,0:T(8,128)(2,1)}, bf16[32,3072]{1,0:T(8,128)(2,1)S(1)}, u32[]{:S(2)}, u32[]{:S(2)}) collective-permute-start(bf16[32,3072]{1,0:T(8,128)(2,1)} %param.22), channel_id=1, source_target_pairs={{0,2},{2,4},{4,6},{6,7},{7,5},{5,3},{3,1},{1,0},{8,10},{10,12},{12... | collective-permute-start | bytes 589832 | tf_op jit(solution)/shard_map/ppermute | solution.py:58
  14.2 13.6 %collective-permute-start.2 = (bf16[32,3072]{1,0:T(8,128)(2,1)S(1)}, bf16[32,3072]{1,0:T(8,128)(2,1)S(1)}, u32[]{:S(2)}, u32[]{:S(2)}) collective-permute-start(bf16[32,3072]{1,0:T(8,128)(2,1)S(1)} %collective-permute-done.1), channel_id=1, source_target_pairs={{0,1},{2,0},{4,2},{6,4},{7,6},{5,7},{3,5},{1,3},{8,9},{10,8},{12,1... | collective-permute-start | bytes 589832 | tf_op jit(solution)/shard_map/ppermute | solution.py:71
  17.1 8.1 %collective-permute-start.4 = (bf16[32,3072]{1,0:T(8,128)(2,1)S(1)}, bf16[32,3072]{1,0:T(8,128)(2,1)S(1)}, u32[]{:S(2)}, u32[]{:S(2)}) collective-permute-start(bf16[32,3072]{1,0:T(8,128)(2,1)S(1)} %collective-permute-done.3), channel_id=1, source_target_pairs={{0,2},{2,4},{4,6},{6,7},{7,5},{5,3},{3,1},{1,0},{8,10},{10,12},{12... | collective-permute-start | bytes 589832 | tf_op jit(solution)/shard_map/ppermute | solution.py:68
  25.3 4.8 %collective-permute-start.5 = (bf16[16,3072]{1,0:T(8,128)(2,1)S(1)}, bf16[16,3072]{1,0:T(8,128)(2,1)S(1)}, u32[]{:S(2)}, u32[]{:S(2)}) collective-permute-start(bf16[16,3072]{1,0:T(8,128)(2,1)S(1)} %slice.366), channel_id=1, source_target_pairs={{0,2},{2,4},{4,6},{6,7},{7,5},{5,3},{3,1},{1,0},{8,10},{10,12},{12... | collective-permute-start | bytes 294920 | tf_op jit(solution)/shard_map/ppermute | solution.py:64
  27.8 4.7 %collective-permute-start.6 = (bf16[16,3072]{1,0:T(8,128)(2,1)S(1)}, bf16[16,3072]{1,0:T(8,128)(2,1)S(1)}, u32[]{:S(2)}, u32[]{:S(2)}) collective-permute-start(bf16[16,3072]{1,0:T(8,128)(2,1)S(1)} %slice.367), channel_id=1, source_target_pairs={{0,1},{2,0},{4,2},{6,4},{7,6},{5,7},{3,5},{1,3},{8,9},{10,8},{12,1... | collective-permute-start | bytes 294920 | tf_op jit(solution)/shard_map/ppermute | solution.py:65
  37.4 2.3 copy-start.6
  37.4 25.1 %collective-permute-start.8 = (bf16[128,3072]{1,0:T(8,128)(2,1)S(1)}, bf16[128,3072]{1,0:T(8,128)(2,1)}, u32[]{:S(2)}, u32[]{:S(2)}) collective-permute-start(bf16[128,3072]{1,0:T(8,128)(2,1)S(1)} %bitcast.126), channel_id=1, source_target_pairs={{0,8},{1,9},{2,10},{3,11},{4,12},{5,13},{6,14},{7,15},{16,24},{17,... | collective-permute-start | bytes 2359304 | tf_op jit(solution)/shard_map/ppermute | solution.py:14
  42.3 19.7 %copy-start.4 = (f32[3,3072]{1,0:T(4,128)S(1)}, f32[3,3072]{1,0:T(4,128)}, u32[]{:S(2)}) copy-start(f32[3,3072]{1,0:T(4,128)} %param.23) | copy-start | bytes 110596
  82.4 10.6 %copy-start.2 = (bf16[256,3072]{1,0:T(8,128)(2,1)S(1)}, bf16[256,3072]{1,0:T(8,128)(2,1)}, u32[]{:S(2)}) copy-start(bf16[256,3072]{1,0:T(8,128)(2,1)} %shard_map.82) | copy-start | bytes 4718596
  82.4 4.8 %collective-permute-start.9 = (bf16[16,3072]{1,0:T(8,128)(2,1)S(1)}, bf16[16,3072]{1,0:T(8,128)(2,1)S(1)}, u32[]{:S(2)}, u32[]{:S(2)}) collective-permute-start(bf16[16,3072]{1,0:T(8,128)(2,1)S(1)} %get-tuple-element.117), channel_id=1, source_target_pairs={{0,2},{2,4},{4,6},{6,7},{7,5},{5,3},{3,1},{1,0},{8,10},{10,12},{12... | collective-permute-start | bytes 294920 | tf_op jit(solution)/shard_map/ppermute | solution.py:108
  83.7 4.7 %collective-permute-start.13 = (bf16[16,3072]{1,0:T(8,128)(2,1)S(1)}, bf16[16,3072]{1,0:T(8,128)(2,1)S(1)}, u32[]{:S(2)}, u32[]{:S(2)}) collective-permute-start(bf16[16,3072]{1,0:T(8,128)(2,1)S(1)} %get-tuple-element.118), channel_id=1, source_target_pairs={{0,1},{2,0},{4,2},{6,4},{7,6},{5,7},{3,5},{1,3},{8,9},{10,8},{12,1... | collective-permute-start | bytes 294920 | tf_op jit(solution)/shard_map/ppermute | solution.py:108
  87.3 5.7 %collective-permute-start.10 = (bf16[32,3072]{1,0:T(8,128)(2,1)S(1)}, bf16[32,3072]{1,0:T(8,128)(2,1)S(1)}, u32[]{:S(2)}, u32[]{:S(2)}) collective-permute-start(bf16[32,3072]{1,0:T(8,128)(2,1)S(1)} %convert_element_type.295), channel_id=1, source_target_pairs={{0,2},{2,4},{4,6},{6,7},{7,5},{5,3},{3,1},{1,0},{8,10},{10,12},{12... | collective-permute-start | bytes 589832 | tf_op jit(solution)/shard_map/ppermute | solution.py:108
  88.4 26.8 %copy-start.3 = (bf16[32,3072]{1,0:T(8,128)(2,1)S(1)}, bf16[32,3072]{1,0:T(8,128)(2,1)}, u32[]{:S(2)}) copy-start(bf16[32,3072]{1,0:T(8,128)(2,1)} %param.22) | copy-start | bytes 589828
  88.4 7.5 %collective-permute-start.14 = (bf16[32,3072]{1,0:T(8,128)(2,1)S(1)}, bf16[32,3072]{1,0:T(8,128)(2,1)S(1)}, u32[]{:S(2)}, u32[]{:S(2)}) collective-permute-start(bf16[32,3072]{1,0:T(8,128)(2,1)S(1)} %convert_element_type.305), channel_id=1, source_target_pairs={{0,1},{2,0},{4,2},{6,4},{7,6},{5,7},{3,5},{1,3},{8,9},{10,8},{12,1... | collective-permute-start | bytes 589832 | tf_op jit(solution)/shard_map/ppermute | solution.py:108
  93.0 7.4 %collective-permute-start.11 = (bf16[32,3072]{1,0:T(8,128)(2,1)S(1)}, bf16[32,3072]{1,0:T(8,128)(2,1)S(1)}, u32[]{:S(2)}, u32[]{:S(2)}) collective-permute-start(bf16[32,3072]{1,0:T(8,128)(2,1)S(1)} %add_convert_fusion.14), channel_id=1, source_target_pairs={{0,2},{2,4},{4,6},{6,7},{7,5},{5,3},{3,1},{1,0},{8,10},{10,12},{12... | collective-permute-start | bytes 589832 | tf_op jit(solution)/shard_map/ppermute | solution.py:108
  100.5 7.8 %collective-permute-start.15 = (bf16[32,3072]{1,0:T(8,128)(2,1)S(1)}, bf16[32,3072]{1,0:T(8,128)(2,1)S(1)}, u32[]{:S(2)}, u32[]{:S(2)}) collective-permute-start(bf16[32,3072]{1,0:T(8,128)(2,1)S(1)} %get-tuple-element.116), channel_id=1, source_target_pairs={{0,1},{2,0},{4,2},{6,4},{7,6},{5,7},{3,5},{1,3},{8,9},{10,8},{12,1... | collective-permute-start | bytes 589832 | tf_op jit(solution)/shard_map/ppermute | solution.py:108
  101.2 7.2 %collective-permute-start.12 = (bf16[32,3072]{1,0:T(8,128)(2,1)S(1)}, bf16[32,3072]{1,0:T(8,128)(2,1)S(1)}, u32[]{:S(2)}, u32[]{:S(2)}) collective-permute-start(bf16[32,3072]{1,0:T(8,128)(2,1)S(1)} %get-tuple-element.115), channel_id=1, source_target_pairs={{0,2},{2,4},{4,6},{6,7},{7,5},{5,3},{3,1},{1,0},{8,10},{10,12},{12... | collective-permute-start | bytes 589832 | tf_op jit(solution)/shard_map/ppermute | solution.py:108
  108.4 6.8 %collective-permute-start.16 = (bf16[32,3072]{1,0:T(8,128)(2,1)S(1)}, bf16[32,3072]{1,0:T(8,128)(2,1)S(1)}, u32[]{:S(2)}, u32[]{:S(2)}) collective-permute-start(bf16[32,3072]{1,0:T(8,128)(2,1)S(1)} %add_convert_fusion.11), channel_id=1, source_target_pairs={{0,1},{2,0},{4,2},{6,4},{7,6},{5,7},{3,5},{1,3},{8,9},{10,8},{12,1... | collective-permute-start | bytes 589832 | tf_op jit(solution)/shard_map/ppermute | solution.py:108
  116.0 5.7 %collective-permute-start.17 = (bf16[32,3072]{1,0:T(8,128)(2,1)S(1)}, bf16[32,3072]{1,0:T(8,128)(2,1)S(1)}, u32[]{:S(2)}, u32[]{:S(2)}) collective-permute-start(bf16[32,3072]{1,0:T(8,128)(2,1)S(1)} %get-tuple-element.98), channel_id=1, source_target_pairs={{0,1},{2,0},{4,2},{6,4},{7,6},{5,7},{3,5},{1,3},{8,9},{10,8},{12,1... | collective-permute-start | bytes 589832 | tf_op jit(solution)/shard_map/ppermute | solution.py:59
  116.7 5.8 %collective-permute-start.20 = (bf16[32,3072]{1,0:T(8,128)(2,1)S(1)}, bf16[32,3072]{1,0:T(8,128)(2,1)S(1)}, u32[]{:S(2)}, u32[]{:S(2)}) collective-permute-start(bf16[32,3072]{1,0:T(8,128)(2,1)S(1)} %get-tuple-element.98), channel_id=1, source_target_pairs={{0,2},{2,4},{4,6},{6,7},{7,5},{5,3},{3,1},{1,0},{8,10},{10,12},{12... | collective-permute-start | bytes 589832 | tf_op jit(solution)/shard_map/ppermute | solution.py:58
  121.6 5.7 %collective-permute-start.18 = (bf16[32,3072]{1,0:T(8,128)(2,1)S(1)}, bf16[32,3072]{1,0:T(8,128)(2,1)S(1)}, u32[]{:S(2)}, u32[]{:S(2)}) collective-permute-start(bf16[32,3072]{1,0:T(8,128)(2,1)S(1)} %collective-permute-done.17), channel_id=1, source_target_pairs={{0,1},{2,0},{4,2},{6,4},{7,6},{5,7},{3,5},{1,3},{8,9},{10,8},{12,1... | collective-permute-start | bytes 589832 | tf_op jit(solution)/shard_map/ppermute | solution.py:71
  122.5 5.7 %collective-permute-start.21 = (bf16[32,3072]{1,0:T(8,128)(2,1)S(1)}, bf16[32,3072]{1,0:T(8,128)(2,1)S(1)}, u32[]{:S(2)}, u32[]{:S(2)}) collective-permute-start(bf16[32,3072]{1,0:T(8,128)(2,1)S(1)} %collective-permute-done.20), channel_id=1, source_target_pairs={{0,2},{2,4},{4,6},{6,7},{7,5},{5,3},{3,1},{1,0},{8,10},{10,12},{12... | collective-permute-start | bytes 589832 | tf_op jit(solution)/shard_map/ppermute | solution.py:68
  127.3 7.9 %collective-permute-start.19 = (bf16[32,3072]{1,0:T(8,128)(2,1)S(1)}, bf16[32,3072]{1,0:T(8,128)(2,1)S(1)}, u32[]{:S(2)}, u32[]{:S(2)}) collective-permute-start(bf16[32,3072]{1,0:T(8,128)(2,1)S(1)} %collective-permute-done.18), channel_id=1, source_target_pairs={{0,1},{2,0},{4,2},{6,4},{7,6},{5,7},{3,5},{1,3},{8,9},{10,8},{12,1... | collective-permute-start | bytes 589832 | tf_op jit(solution)/shard_map/ppermute | solution.py:71
  128.2 5.7 %collective-permute-start.22 = (bf16[32,3072]{1,0:T(8,128)(2,1)S(1)}, bf16[32,3072]{1,0:T(8,128)(2,1)S(1)}, u32[]{:S(2)}, u32[]{:S(2)}) collective-permute-start(bf16[32,3072]{1,0:T(8,128)(2,1)S(1)} %collective-permute-done.21), channel_id=1, source_target_pairs={{0,2},{2,4},{4,6},{6,7},{7,5},{5,3},{3,1},{1,0},{8,10},{10,12},{12... | collective-permute-start | bytes 589832 | tf_op jit(solution)/shard_map/ppermute | solution.py:68
  133.9 4.7 %collective-permute-start.23 = (bf16[16,3072]{1,0:T(8,128)(2,1)S(1)}, bf16[16,3072]{1,0:T(8,128)(2,1)S(1)}, u32[]{:S(2)}, u32[]{:S(2)}) collective-permute-start(bf16[16,3072]{1,0:T(8,128)(2,1)S(1)} %slice.380), channel_id=1, source_target_pairs={{0,2},{2,4},{4,6},{6,7},{7,5},{5,3},{3,1},{1,0},{8,10},{10,12},{12... | collective-permute-start | bytes 294920 | tf_op jit(solution)/shard_map/ppermute | solution.py:64
  135.2 4.7 %collective-permute-start.24 = (bf16[16,3072]{1,0:T(8,128)(2,1)S(1)}, bf16[16,3072]{1,0:T(8,128)(2,1)S(1)}, u32[]{:S(2)}, u32[]{:S(2)}) collective-permute-start(bf16[16,3072]{1,0:T(8,128)(2,1)S(1)} %slice.381), channel_id=1, source_target_pairs={{0,1},{2,0},{4,2},{6,4},{7,6},{5,7},{3,5},{1,3},{8,9},{10,8},{12,1... | collective-permute-start | bytes 294920 | tf_op jit(solution)/shard_map/ppermute | solution.py:65
  144.7 4.3 %collective-permute-start.25 = (bf16[128,3072]{1,0:T(8,128)(2,1)S(1)}, bf16[128,3072]{1,0:T(8,128)(2,1)}, u32[]{:S(2)}, u32[]{:S(2)}) collective-permute-start(bf16[128,3072]{1,0:T(8,128)(2,1)S(1)} %bitcast.127), channel_id=1, source_target_pairs={{0,8},{1,9},{2,10},{3,11},{4,12},{5,13},{6,14},{7,15},{16,24},{17,... | collective-permute-start | bytes 2359304 | tf_op jit(solution)/shard_map/ppermute | solution.py:14
  169.1 10.6 %copy-start.1 = (bf16[256,3072]{1,0:T(8,128)(2,1)S(1)}, bf16[256,3072]{1,0:T(8,128)(2,1)}, u32[]{:S(2)}) copy-start(bf16[256,3072]{1,0:T(8,128)(2,1)} %shard_map.83) | copy-start | bytes 4718596
  169.2 4.7 %collective-permute-start.26 = (bf16[16,3072]{1,0:T(8,128)(2,1)S(1)}, bf16[16,3072]{1,0:T(8,128)(2,1)S(1)}, u32[]{:S(2)}, u32[]{:S(2)}) collective-permute-start(bf16[16,3072]{1,0:T(8,128)(2,1)S(1)} %get-tuple-element.111), channel_id=1, source_target_pairs={{0,2},{2,4},{4,6},{6,7},{7,5},{5,3},{3,1},{1,0},{8,10},{10,12},{12... | collective-permute-start | bytes 294920 | tf_op jit(solution)/shard_map/ppermute | solution.py:108
  170.4 4.7 %collective-permute-start.30 = (bf16[16,3072]{1,0:T(8,128)(2,1)S(1)}, bf16[16,3072]{1,0:T(8,128)(2,1)S(1)}, u32[]{:S(2)}, u32[]{:S(2)}) collective-permute-start(bf16[16,3072]{1,0:T(8,128)(2,1)S(1)} %get-tuple-element.112), channel_id=1, source_target_pairs={{0,1},{2,0},{4,2},{6,4},{7,6},{5,7},{3,5},{1,3},{8,9},{10,8},{12,1... | collective-permute-start | bytes 294920 | tf_op jit(solution)/shard_map/ppermute | solution.py:108
  173.9 5.9 %collective-permute-start.27 = (bf16[32,3072]{1,0:T(8,128)(2,1)S(1)}, bf16[32,3072]{1,0:T(8,128)(2,1)S(1)}, u32[]{:S(2)}, u32[]{:S(2)}) collective-permute-start(bf16[32,3072]{1,0:T(8,128)(2,1)S(1)} %convert_element_type.318), channel_id=1, source_target_pairs={{0,2},{2,4},{4,6},{6,7},{7,5},{5,3},{3,1},{1,0},{8,10},{10,12},{12... | collective-permute-start | bytes 589832 | tf_op jit(solution)/shard_map/ppermute | solution.py:108
  175.2 5.7 %collective-permute-start.31 = (bf16[32,3072]{1,0:T(8,128)(2,1)S(1)}, bf16[32,3072]{1,0:T(8,128)(2,1)S(1)}, u32[]{:S(2)}, u32[]{:S(2)}) collective-permute-start(bf16[32,3072]{1,0:T(8,128)(2,1)S(1)} %convert_element_type.328), channel_id=1, source_target_pairs={{0,1},{2,0},{4,2},{6,4},{7,6},{5,7},{3,5},{1,3},{8,9},{10,8},{12,1... | collective-permute-start | bytes 589832 | tf_op jit(solution)/shard_map/ppermute | solution.py:108
  179.8 23.1 %copy-start.5 = (s32[8]{0:T(128)S(1)}, s32[8]{0:T(128)}, u32[]{:S(2)}) copy-start(s32[8]{0:T(128)} %get-tuple-element.127.head_at_ref) | copy-start | bytes 100
  179.8 6.1 %collective-permute-start.28 = (bf16[32,3072]{1,0:T(8,128)(2,1)S(1)}, bf16[32,3072]{1,0:T(8,128)(2,1)S(1)}, u32[]{:S(2)}, u32[]{:S(2)}) collective-permute-start(bf16[32,3072]{1,0:T(8,128)(2,1)S(1)} %add_convert_fusion.9), channel_id=1, source_target_pairs={{0,2},{2,4},{4,6},{6,7},{7,5},{5,3},{3,1},{1,0},{8,10},{10,12},{12... | collective-permute-start | bytes 589832 | tf_op jit(solution)/shard_map/ppermute | solution.py:108
  186.0 7.1 %collective-permute-start.32 = (bf16[32,3072]{1,0:T(8,128)(2,1)S(1)}, bf16[32,3072]{1,0:T(8,128)(2,1)S(1)}, u32[]{:S(2)}, u32[]{:S(2)}) collective-permute-start(bf16[32,3072]{1,0:T(8,128)(2,1)S(1)} %get-tuple-element.110), channel_id=1, source_target_pairs={{0,1},{2,0},{4,2},{6,4},{7,6},{5,7},{3,5},{1,3},{8,9},{10,8},{12,1... | collective-permute-start | bytes 589832 | tf_op jit(solution)/shard_map/ppermute | solution.py:108
  186.4 7.8 %collective-permute-start.29 = (bf16[32,3072]{1,0:T(8,128)(2,1)S(1)}, bf16[32,3072]{1,0:T(8,128)(2,1)S(1)}, u32[]{:S(2)}, u32[]{:S(2)}) collective-permute-start(bf16[32,3072]{1,0:T(8,128)(2,1)S(1)} %get-tuple-element.109), channel_id=1, source_target_pairs={{0,2},{2,4},{4,6},{6,7},{7,5},{5,3},{3,1},{1,0},{8,10},{10,12},{12... | collective-permute-start | bytes 589832 | tf_op jit(solution)/shard_map/ppermute | solution.py:108
  193.2 6.9 %collective-permute-start.33 = (bf16[32,3072]{1,0:T(8,128)(2,1)S(1)}, bf16[32,3072]{1,0:T(8,128)(2,1)S(1)}, u32[]{:S(2)}, u32[]{:S(2)}) collective-permute-start(bf16[32,3072]{1,0:T(8,128)(2,1)S(1)} %add_convert_fusion.6), channel_id=1, source_target_pairs={{0,1},{2,0},{4,2},{6,4},{7,6},{5,7},{3,5},{1,3},{8,9},{10,8},{12,1... | collective-permute-start | bytes 589832 | tf_op jit(solution)/shard_map/ppermute | solution.py:108
  200.9 5.7 %collective-permute-start.34 = (bf16[32,3072]{1,0:T(8,128)(2,1)S(1)}, bf16[32,3072]{1,0:T(8,128)(2,1)S(1)}, u32[]{:S(2)}, u32[]{:S(2)}) collective-permute-start(bf16[32,3072]{1,0:T(8,128)(2,1)S(1)} %get-tuple-element.96), channel_id=1, source_target_pairs={{0,1},{2,0},{4,2},{6,4},{7,6},{5,7},{3,5},{1,3},{8,9},{10,8},{12,1... | collective-permute-start | bytes 589832 | tf_op jit(solution)/shard_map/ppermute | solution.py:59
  202.7 6.0 %collective-permute-start.37 = (bf16[32,3072]{1,0:T(8,128)(2,1)S(1)}, bf16[32,3072]{1,0:T(8,128)(2,1)S(1)}, u32[]{:S(2)}, u32[]{:S(2)}) collective-permute-start(bf16[32,3072]{1,0:T(8,128)(2,1)S(1)} %get-tuple-element.96), channel_id=1, source_target_pairs={{0,2},{2,4},{4,6},{6,7},{7,5},{5,3},{3,1},{1,0},{8,10},{10,12},{12... | collective-permute-start | bytes 589832 | tf_op jit(solution)/shard_map/ppermute | solution.py:58
  206.6 5.7 %collective-permute-start.35 = (bf16[32,3072]{1,0:T(8,128)(2,1)S(1)}, bf16[32,3072]{1,0:T(8,128)(2,1)S(1)}, u32[]{:S(2)}, u32[]{:S(2)}) collective-permute-start(bf16[32,3072]{1,0:T(8,128)(2,1)S(1)} %collective-permute-done.34), channel_id=1, source_target_pairs={{0,1},{2,0},{4,2},{6,4},{7,6},{5,7},{3,5},{1,3},{8,9},{10,8},{12,1... | collective-permute-start | bytes 589832 | tf_op jit(solution)/shard_map/ppermute | solution.py:71
  208.7 5.8 %collective-permute-start.38 = (bf16[32,3072]{1,0:T(8,128)(2,1)S(1)}, bf16[32,3072]{1,0:T(8,128)(2,1)S(1)}, u32[]{:S(2)}, u32[]{:S(2)}) collective-permute-start(bf16[32,3072]{1,0:T(8,128)(2,1)S(1)} %collective-permute-done.37), channel_id=1, source_target_pairs={{0,2},{2,4},{4,6},{6,7},{7,5},{5,3},{3,1},{1,0},{8,10},{10,12},{12... | collective-permute-start | bytes 589832 | tf_op jit(solution)/shard_map/ppermute | solution.py:68
  212.2 8.0 %collective-permute-start.36 = (bf16[32,3072]{1,0:T(8,128)(2,1)S(1)}, bf16[32,3072]{1,0:T(8,128)(2,1)S(1)}, u32[]{:S(2)}, u32[]{:S(2)}) collective-permute-start(bf16[32,3072]{1,0:T(8,128)(2,1)S(1)} %collective-permute-done.35), channel_id=1, source_target_pairs={{0,1},{2,0},{4,2},{6,4},{7,6},{5,7},{3,5},{1,3},{8,9},{10,8},{12,1... | collective-permute-start | bytes 589832 | tf_op jit(solution)/shard_map/ppermute | solution.py:71
  214.5 5.7 %collective-permute-start.39 = (bf16[32,3072]{1,0:T(8,128)(2,1)S(1)}, bf16[32,3072]{1,0:T(8,128)(2,1)S(1)}, u32[]{:S(2)}, u32[]{:S(2)}) collective-permute-start(bf16[32,3072]{1,0:T(8,128)(2,1)S(1)} %collective-permute-done.38), channel_id=1, source_target_pairs={{0,2},{2,4},{4,6},{6,7},{7,5},{5,3},{3,1},{1,0},{8,10},{10,12},{12... | collective-permute-start | bytes 589832 | tf_op jit(solution)/shard_map/ppermute | solution.py:68
  220.2 4.7 %collective-permute-start.40 = (bf16[16,3072]{1,0:T(8,128)(2,1)S(1)}, bf16[16,3072]{1,0:T(8,128)(2,1)S(1)}, u32[]{:S(2)}, u32[]{:S(2)}) collective-permute-start(bf16[16,3072]{1,0:T(8,128)(2,1)S(1)} %slice.394), channel_id=1, source_target_pairs={{0,2},{2,4},{4,6},{6,7},{7,5},{5,3},{3,1},{1,0},{8,10},{10,12},{12... | collective-permute-start | bytes 294920 | tf_op jit(solution)/shard_map/ppermute | solution.py:64
  220.3 4.7 %collective-permute-start.41 = (bf16[16,3072]{1,0:T(8,128)(2,1)S(1)}, bf16[16,3072]{1,0:T(8,128)(2,1)S(1)}, u32[]{:S(2)}, u32[]{:S(2)}) collective-permute-start(bf16[16,3072]{1,0:T(8,128)(2,1)S(1)} %slice.395), channel_id=1, source_target_pairs={{0,1},{2,0},{4,2},{6,4},{7,6},{5,7},{3,5},{1,3},{8,9},{10,8},{12,1... | collective-permute-start | bytes 294920 | tf_op jit(solution)/shard_map/ppermute | solution.py:65
  230.2 1.7 copy-start.7
  233.6 2.9 %collective-permute-start.42 = (bf16[256,128]{1,0:T(8,128)(2,1)S(1)}, bf16[256,128]{1,0:T(8,128)(2,1)S(1)}, u32[]{:S(2)}, u32[]{:S(2)}) collective-permute-start(bf16[256,128]{1,0:T(8,128)(2,1)S(1)} %convolution_convert_fusion.3), channel_id=1, source_target_pairs={{0,8},{1,9},{2,10},{3,11},{4,12},{5,13},{6,14},{7,15},{16,24},{17,... | collective-permute-start | bytes 196616 | tf_op jit(solution)/shard_map/ppermute | solution.py:14
  235.1 2.2 collective-permute-start.43
  240.3 4.7 %collective-permute-start.44 = (bf16[16,3072]{1,0:T(8,128)(2,1)S(1)}, bf16[16,3072]{1,0:T(8,128)(2,1)S(1)}, u32[]{:S(2)}, u32[]{:S(2)}) collective-permute-start(bf16[16,3072]{1,0:T(8,128)(2,1)S(1)} %get-tuple-element.121), channel_id=1, source_target_pairs={{0,2},{2,4},{4,6},{6,7},{7,5},{5,3},{3,1},{1,0},{8,10},{10,12},{12... | collective-permute-start | bytes 294920 | tf_op jit(solution)/shard_map/ppermute | solution.py:108
  240.7 4.7 %collective-permute-start.48 = (bf16[16,3072]{1,0:T(8,128)(2,1)S(1)}, bf16[16,3072]{1,0:T(8,128)(2,1)S(1)}, u32[]{:S(2)}, u32[]{:S(2)}) collective-permute-start(bf16[16,3072]{1,0:T(8,128)(2,1)S(1)} %get-tuple-element.122), channel_id=1, source_target_pairs={{0,1},{2,0},{4,2},{6,4},{7,6},{5,7},{3,5},{1,3},{8,9},{10,8},{12,1... | collective-permute-start | bytes 294920 | tf_op jit(solution)/shard_map/ppermute | solution.py:108
  245.1 7.6 %collective-permute-start.45 = (bf16[32,3072]{1,0:T(8,128)(2,1)S(1)}, bf16[32,3072]{1,0:T(8,128)(2,1)S(1)}, u32[]{:S(2)}, u32[]{:S(2)}) collective-permute-start(bf16[32,3072]{1,0:T(8,128)(2,1)S(1)} %convert_element_type.352), channel_id=1, source_target_pairs={{0,2},{2,4},{4,6},{6,7},{7,5},{5,3},{3,1},{1,0},{8,10},{10,12},{12... | collective-permute-start | bytes 589832 | tf_op jit(solution)/shard_map/ppermute | solution.py:108
  245.4 7.6 %collective-permute-start.49 = (bf16[32,3072]{1,0:T(8,128)(2,1)S(1)}, bf16[32,3072]{1,0:T(8,128)(2,1)S(1)}, u32[]{:S(2)}, u32[]{:S(2)}) collective-permute-start(bf16[32,3072]{1,0:T(8,128)(2,1)S(1)} %convert_element_type.362), channel_id=1, source_target_pairs={{0,1},{2,0},{4,2},{6,4},{7,6},{5,7},{3,5},{1,3},{8,9},{10,8},{12,1... | collective-permute-start | bytes 589832 | tf_op jit(solution)/shard_map/ppermute | solution.py:108
  252.7 7.5 %collective-permute-start.46 = (bf16[32,3072]{1,0:T(8,128)(2,1)S(1)}, bf16[32,3072]{1,0:T(8,128)(2,1)S(1)}, u32[]{:S(2)}, u32[]{:S(2)}) collective-permute-start(bf16[32,3072]{1,0:T(8,128)(2,1)S(1)} %add_convert_fusion.4), channel_id=1, source_target_pairs={{0,2},{2,4},{4,6},{6,7},{7,5},{5,3},{3,1},{1,0},{8,10},{10,12},{12... | collective-permute-start | bytes 589832 | tf_op jit(solution)/shard_map/ppermute | solution.py:108
  260.3 6.6 %collective-permute-start.50 = (bf16[32,3072]{1,0:T(8,128)(2,1)S(1)}, bf16[32,3072]{1,0:T(8,128)(2,1)S(1)}, u32[]{:S(2)}, u32[]{:S(2)}) collective-permute-start(bf16[32,3072]{1,0:T(8,128)(2,1)S(1)} %get-tuple-element.106), channel_id=1, source_target_pairs={{0,1},{2,0},{4,2},{6,4},{7,6},{5,7},{3,5},{1,3},{8,9},{10,8},{12,1... | collective-permute-start | bytes 589832 | tf_op jit(solution)/shard_map/ppermute | solution.py:108
  262.1 6.3 %collective-permute-start.47 = (bf16[32,3072]{1,0:T(8,128)(2,1)S(1)}, bf16[32,3072]{1,0:T(8,128)(2,1)S(1)}, u32[]{:S(2)}, u32[]{:S(2)}) collective-permute-start(bf16[32,3072]{1,0:T(8,128)(2,1)S(1)} %get-tuple-element.105), channel_id=1, source_target_pairs={{0,2},{2,4},{4,6},{6,7},{7,5},{5,3},{3,1},{1,0},{8,10},{10,12},{12... | collective-permute-start | bytes 589832 | tf_op jit(solution)/shard_map/ppermute | solution.py:108
  266.9 5.7 %collective-permute-start.51 = (bf16[32,3072]{1,0:T(8,128)(2,1)S(1)}, bf16[32,3072]{1,0:T(8,128)(2,1)S(1)}, u32[]{:S(2)}, u32[]{:S(2)}) collective-permute-start(bf16[32,3072]{1,0:T(8,128)(2,1)S(1)} %add_convert_fusion.1), channel_id=1, source_target_pairs={{0,1},{2,0},{4,2},{6,4},{7,6},{5,7},{3,5},{1,3},{8,9},{10,8},{12,1... | collective-permute-start | bytes 589832 | tf_op jit(solution)/shard_map/ppermute | solution.py:108

commit v14 on v11

--- a/solution.py
+++ b/solution.py
@@ -134,22 +134,27 @@
     return lax.optimization_barrier(term.astype(jnp.bfloat16)).astype(jnp.float32)
 
 
-def conv_gate_kernel(slab_ref, gain_ref, weight_ref, out_ref, filt_acc, gate_acc):
+def conv_gate_kernel(slab_ref, gain_ref, weight_ref, out_ref, filt_acc, gate_acc, normed_rows):
     tap = pl.program_id(0)
-    chunk = pl.program_id(1)
-
-    @pl.when((tap == 0) & (chunk == 0))
+    half = pl.program_id(1)
+
+    @pl.when((tap == 0) & (half == 0))
     def _():
         filt_acc[...] = jnp.zeros_like(filt_acc)
         gate_acc[...] = jnp.zeros_like(gate_acc)
 
-    wide = slab_ref[...].astype(jnp.float32)
-    scale = lax.rsqrt(jnp.mean(wide * wide, axis=-1, keepdims=True) + 1e-06)
-    rows = (wide * scale * gain_ref[...]).astype(jnp.bfloat16)
-    filt_acc[...] += jnp.dot(rows, weight_ref[0], preferred_element_type=jnp.float32)
-    gate_acc[...] += jnp.dot(rows, weight_ref[1], preferred_element_type=jnp.float32)
-
-    @pl.when((tap == pl.num_programs(0) - 1) & (chunk == pl.num_programs(1) - 1))
+    @pl.when(half == 0)
+    def _():
+        wide = slab_ref[...].astype(jnp.float32)
+        scale = lax.rsqrt(jnp.mean(wide * wide, axis=-1, keepdims=True) + 1e-06)
+        normed_rows[...] = (wide * scale * gain_ref[...]).astype(jnp.bfloat16)
+        filt_acc[...] += jnp.dot(normed_rows[...], weight_ref[...], preferred_element_type=jnp.float32)
+
+    @pl.when(half == 1)
+    def _():
+        gate_acc[...] += jnp.dot(normed_rows[...], weight_ref[...], preferred_element_type=jnp.float32)
+
+    @pl.when((tap == pl.num_programs(0) - 1) & (half == 1))
     def _():
         out_ref[...] = (jnp.tanh(filt_acc[...]) * jax.nn.sigmoid(gate_acc[...])).astype(out_ref.dtype)
 
@@ -169,18 +174,18 @@
             for tap_idx in range(taps)
         ]
     )
-    chunk = width
     return pl.pallas_call(
         conv_gate_kernel,
         out_shape=jax.ShapeDtypeStruct((all_rows, own_width), jnp.bfloat16),
-        grid=(taps, width // chunk),
+        grid=(taps, 2),
         in_specs=[
-            pl.BlockSpec((None, all_rows, chunk), lambda t, k: (t, 0, k)),
-            pl.BlockSpec((1, width), lambda t, k: (0, 0)),
-            pl.BlockSpec((None, None, 2, chunk, own_width), lambda t, k: (layer_idx, t, 0, k, 0)),
+            pl.BlockSpec((None, all_rows, width), lambda t, g: (t, 0, 0)),
+            pl.BlockSpec((1, width), lambda t, g: (0, 0)),
+            pl.BlockSpec((None, None, None, width, own_width), lambda t, g: (layer_idx, t, g, 0, 0)),
         ],
-        out_specs=pl.BlockSpec((all_rows, own_width), lambda t, k: (0, 0)),
-        scratch_shapes=[pltpu.VMEM((all_rows, own_width), jnp.float32)] * 2,
+        out_specs=pl.BlockSpec((all_rows, own_width), lambda t, g: (0, 0)),
+        scratch_shapes=[pltpu.VMEM((all_rows, own_width), jnp.float32)] * 2
+        + [pltpu.VMEM((all_rows, width), jnp.bfloat16)],
         compiler_params=pltpu.CompilerParams(dimension_semantics=("arbitrary", "arbitrary")),
         cost_estimate=pl.CostEstimate(
             flops=4 * taps * all_rows * width * own_width,

time: 260 us -> 264 us (1.015)
  Pallas kernels: 21.7 us -> 25 us
    pallas_call x2, Pallas kernels: 21.7 us -> 25 us  [convolution_gate(): pl.pallas_call(conv_gate_kernel, out_shape=jax.ShapeDtypeStruct((all_rows...]
where the time goes in v14:
time: 264 us; the launch traced here: 263 us
  waiting for transfers between devices  97.5 us (37%)
  starting transfers between devices  58.1 us (22%)
  local copies, waits for them, and re-layouts  48.1 us (18%)
  Pallas kernels  25 us (9%)
  other arithmetic  17.4 us (7%)
  matrix products  12.6 us (5%)
  between operations  4.29 us (2%)
    ppermute x24, waiting for transfers between devices, chain(): passed = lax.ppermute(part.astype(value.dtype), axis, pairs)  62.4 us
    unnamed x25, local copies, waits for them, and re-layouts  32.8 us
    ppermute x24, starting transfers between devices, chain(): passed = lax.ppermute(part.astype(value.dtype), axis, pairs)  25.2 us
    pallas_call x2, Pallas kernels, convolution_gate(): pl.pallas_call(conv_gate_kernel, out_shape=jax.ShapeDtypeStruct((all_rows...  25 us
    ppermute x5, waiting for transfers between devices, ring_gather(): bwd = lax.ppermute(bwd, axis, backward)  14.2 us
    dot_general x6, matrix products, rounded_term(): term = jnp.dot(left, right, preferred_element_type=jnp.float32)  10.4 us
    another operation x4, other arithmetic, convolution_gate(): jnp.stack([lax.dynamic_slice_in_dim(padded, border_rows - tap_idx * dilat...  10 us
    ppermute x4, starting transfers between devices, ring_gather(): lax.ppermute(value, axis, [(order[p], order[(p - k) % length]) for p in r...  8.7 us
  transfers between devices with their start and end apart: 52, of which 29 were waited for; matrix products, arithmetic and copies ran while one was open for 15% of the time, Pallas kernels for 0%

profile of v14, /device:TPU:0, one launch (start us, length us, event | category | flops | bytes accessed | tf_op | source)
XLA Modules:
  0.0 263.0 jit_solution(13339639118731719079)
XLA Ops:
  0.0 4.0 %collective-permute-start.1 = (bf16[32,3072]{1,0:T(8,128)(2,1)}, bf16[32,3072]{1,0:T(8,128)(2,1)S(1)}, u32[]{:S(2)}, u32[]{:S(2)}) collective-permute-start(bf16[32,3072]{1,0:T(8,128)(2,1)} %param.22), channel_id=1, source_target_pairs={{0,3},{2,1},{4,0},{6,2},{7,4},{5,6},{3,7},{1,5},{8,11},{10,9},{12,... | collective-permute-start | bytes 589832 | tf_op jit(solution)/shard_map/ppermute | solution.py:59
  9.4 1.6 bitcast_dynamic-update-slice_fusion.20
  11.0 19.6 %copy.11 = bf16[2,3,3072,2,384]{4,2,3,1,0:T(8,128)(2,1)} copy(bf16[2,3,3072,2,384]{4,3,2,1,0:T(2,128)(2,1)} %param.25) | data formatting | bytes 56623104 | tf_op args[3]
  31.3 1.8 collective-permute-start.2
  34.8 2.4 collective-permute-done.2
  37.2 1.7 collective-permute-start.6
  40.0 1.8 collective-permute-done.6
  41.9 1.7 collective-permute-done.5
  46.4 2.1 gather_fusion
  51.7 2.2 fusion.23
  53.9 2.4 pad_maximum_fusion.slab_ref
  56.3 12.5 %shard_map.82 = bf16[256,384]{1,0:T(8,128)(2,1)} custom-call(bf16[3,256,3072]{2,1,0:T(8,128)(2,1)} %pad_maximum_fusion.slab_ref, f32[1,3072]{1,0:T(1,128)} %get-tuple-element.124.gain_ref, bf16[2,3,2,3072,384]{4,3,2,1,0:T(8,128)(2,1)} %bitcast.139), custom_call_target="tpu_custom_call" | custom-call | flops 3623878656 | bytes 19070976 | tf_op jit(solution)/shard_map/pallas_call | solution.py:177
  70.3 2.2 convolution_convert_fusion.4
  73.0 1.7 collective-permute-start.13
  74.6 2.6 %convolution_convert_fusion.2 = bf16[256,3072]{1,0:T(8,128)(2,1)S(1)} fusion(bf16[256,384]{1,0:T(8,128)(2,1)S(1)} %bitcast.154, bf16[2,384,3072]{2,1,0:T(8,128)(2,1)} %param.26), kind=kOutput, calls=%fused_computation.19 | convolution fusion | flops 604766208 | bytes 4128768 | tf_op jit(solution)/shard_map/dot_general | solution.py:133
  78.2 1.7 collective-permute-start.14
  80.0 4.2 %collective-permute-done.10 = bf16[32,3072]{1,0:T(8,128)(2,1)S(1)} collective-permute-done((bf16[32,3072]{1,0:T(8,128)(2,1)S(1)}, bf16[32,3072]{1,0:T(8,128)(2,1)S(1)}, u32[]{:S(2)}, u32[]{:S(2)}) %collective-permute-start.10) | collective-permute-done | bytes 196640 | tf_op jit(solution)/shard_map/ppermute | solution.py:108
  84.6 5.3 %collective-permute-done.11 = bf16[32,3072]{1,0:T(8,128)(2,1)S(1)} collective-permute-done((bf16[32,3072]{1,0:T(8,128)(2,1)S(1)}, bf16[32,3072]{1,0:T(8,128)(2,1)S(1)}, u32[]{:S(2)}, u32[]{:S(2)}) %collective-permute-start.11) | collective-permute-done | bytes 196640 | tf_op jit(solution)/shard_map/ppermute | solution.py:108
  90.0 1.6 collective-permute-start.15
  92.1 4.6 %collective-permute-done.15 = bf16[32,3072]{1,0:T(8,128)(2,1)S(1)} collective-permute-done((bf16[32,3072]{1,0:T(8,128)(2,1)S(1)}, bf16[32,3072]{1,0:T(8,128)(2,1)S(1)}, u32[]{:S(2)}, u32[]{:S(2)}) %collective-permute-start.15) | collective-permute-done | bytes 196640 | tf_op jit(solution)/shard_map/ppermute | solution.py:108
  96.7 1.6 collective-permute-start.16
  98.4 5.5 %collective-permute-done.16 = bf16[32,3072]{1,0:T(8,128)(2,1)S(1)} collective-permute-done((bf16[32,3072]{1,0:T(8,128)(2,1)S(1)}, bf16[32,3072]{1,0:T(8,128)(2,1)S(1)}, u32[]{:S(2)}, u32[]{:S(2)}) %collective-permute-start.16) | collective-permute-done | bytes 196640 | tf_op jit(solution)/shard_map/ppermute | solution.py:108
  106.7 4.5 %collective-permute-done.17 = bf16[32,3072]{1,0:T(8,128)(2,1)S(1)} collective-permute-done((bf16[32,3072]{1,0:T(8,128)(2,1)S(1)}, bf16[32,3072]{1,0:T(8,128)(2,1)S(1)}, u32[]{:S(2)}, u32[]{:S(2)}) %collective-permute-start.17) | collective-permute-done | bytes 196640 | tf_op jit(solution)/shard_map/ppermute | solution.py:59
  111.2 1.6 collective-permute-start.18
  113.9 2.9 %collective-permute-done.18 = bf16[32,3072]{1,0:T(8,128)(2,1)S(1)} collective-permute-done((bf16[32,3072]{1,0:T(8,128)(2,1)S(1)}, bf16[32,3072]{1,0:T(8,128)(2,1)S(1)}, u32[]{:S(2)}, u32[]{:S(2)}) %collective-permute-start.18) | collective-permute-done | bytes 196640 | tf_op jit(solution)/shard_map/ppermute | solution.py:71
  116.9 1.6 collective-permute-start.19
  119.6 2.9 %collective-permute-done.19 = bf16[32,3072]{1,0:T(8,128)(2,1)S(1)} collective-permute-done((bf16[32,3072]{1,0:T(8,128)(2,1)S(1)}, bf16[32,3072]{1,0:T(8,128)(2,1)S(1)}, u32[]{:S(2)}, u32[]{:S(2)}) %collective-permute-start.19) | collective-permute-done | bytes 196640 | tf_op jit(solution)/shard_map/ppermute | solution.py:71
  122.6 1.6 collective-permute-start.24
  125.4 1.8 collective-permute-done.24
  127.2 1.6 collective-permute-done.23
  131.7 2.1 gather_fusion.2
  133.8 2.2 collective-permute-start.25
  137.9 3.0 %fusion.19 = (bf16[1,256,3072]{2,1,0:T(8,128)(2,1)S(1)}, bf16[1,256,3072]{2,1,0:T(8,128)(2,1)S(1)}) fusion(s32[]{:T(128)S(6)} %select_n.23, bf16[256,3072]{1,0:T(8,128)(2,1)S(1)} %bitcast.141, bf16[128,3072]{1,0:T(8,128)(2,1)} %collective-permute-done.25, s32[]{:T(128)S(6)} %select_n.24), kind=kLoop, calls=%fused_computation.45 | loop fusion | flops 6291456 | bytes 5505032 | tf_op jit(solution)/shard_map/stack | solution.py:171
  140.9 2.4 pad_maximum_fusion.1.slab_ref
  143.3 12.5 %shard_map.83 = bf16[256,384]{1,0:T(8,128)(2,1)} custom-call(bf16[3,256,3072]{2,1,0:T(8,128)(2,1)} %pad_maximum_fusion.1.slab_ref, f32[1,3072]{1,0:T(1,128)} %get-tuple-element.125.gain_ref, bf16[2,3,2,3072,384]{4,3,2,1,0:T(8,128)(2,1)} %bitcast.140), custom_call_target="tpu_custom_call" | custom-call | flops 3623878656 | bytes 19070976 | tf_op jit(solution)/shard_map/pallas_call | solution.py:177
  157.4 2.2 convolution_convert_fusion.3
  160.1 1.6 collective-permute-start.30
  161.7 2.6 %convolution_convert_fusion.1 = bf16[256,3072]{1,0:T(8,128)(2,1)S(1)} fusion(bf16[256,384]{1,0:T(8,128)(2,1)S(1)} %bitcast.155, bf16[2,384,3072]{2,1,0:T(8,128)(2,1)} %param.26), kind=kOutput, calls=%fused_computation.18 | convolution fusion | flops 604766208 | bytes 4128768 | tf_op jit(solution)/shard_map/dot_general | solution.py:133
  165.0 1.6 collective-permute-start.31
  166.7 3.7 %collective-permute-done.27 = bf16[32,3072]{1,0:T(8,128)(2,1)S(1)} collective-permute-done((bf16[32,3072]{1,0:T(8,128)(2,1)S(1)}, bf16[32,3072]{1,0:T(8,128)(2,1)S(1)}, u32[]{:S(2)}, u32[]{:S(2)}) %collective-permute-start.27) | collective-permute-done | bytes 196640 | tf_op jit(solution)/shard_map/ppermute | solution.py:108
  170.9 5.2 %collective-permute-done.28 = bf16[32,3072]{1,0:T(8,128)(2,1)S(1)} collective-permute-done((bf16[32,3072]{1,0:T(8,128)(2,1)S(1)}, bf16[32,3072]{1,0:T(8,128)(2,1)S(1)}, u32[]{:S(2)}, u32[]{:S(2)}) %collective-permute-start.28) | collective-permute-done | bytes 196640 | tf_op jit(solution)/shard_map/ppermute | solution.py:108
  176.2 1.6 collective-permute-start.32
  178.3 5.2 %collective-permute-done.32 = bf16[32,3072]{1,0:T(8,128)(2,1)S(1)} collective-permute-done((bf16[32,3072]{1,0:T(8,128)(2,1)S(1)}, bf16[32,3072]{1,0:T(8,128)(2,1)S(1)}, u32[]{:S(2)}, u32[]{:S(2)}) %collective-permute-start.32) | collective-permute-done | bytes 196640 | tf_op jit(solution)/shard_map/ppermute | solution.py:108
  183.6 1.6 collective-permute-start.33
  185.2 6.1 %collective-permute-done.33 = bf16[32,3072]{1,0:T(8,128)(2,1)S(1)} collective-permute-done((bf16[32,3072]{1,0:T(8,128)(2,1)S(1)}, bf16[32,3072]{1,0:T(8,128)(2,1)S(1)}, u32[]{:S(2)}, u32[]{:S(2)}) %collective-permute-start.33) | collective-permute-done | bytes 196640 | tf_op jit(solution)/shard_map/ppermute | solution.py:108
  192.1 1.6 collective-permute-start.34
  194.1 4.1 %collective-permute-done.34 = bf16[32,3072]{1,0:T(8,128)(2,1)S(1)} collective-permute-done((bf16[32,3072]{1,0:T(8,128)(2,1)S(1)}, bf16[32,3072]{1,0:T(8,128)(2,1)S(1)}, u32[]{:S(2)}, u32[]{:S(2)}) %collective-permute-start.34) | collective-permute-done | bytes 196640 | tf_op jit(solution)/shard_map/ppermute | solution.py:59
  198.2 1.6 collective-permute-start.35
  200.9 3.0 %collective-permute-done.35 = bf16[32,3072]{1,0:T(8,128)(2,1)S(1)} collective-permute-done((bf16[32,3072]{1,0:T(8,128)(2,1)S(1)}, bf16[32,3072]{1,0:T(8,128)(2,1)S(1)}, u32[]{:S(2)}, u32[]{:S(2)}) %collective-permute-start.35) | collective-permute-done | bytes 196640 | tf_op jit(solution)/shard_map/ppermute | solution.py:71
  203.9 1.6 collective-permute-start.36
  206.6 2.9 %collective-permute-done.36 = bf16[32,3072]{1,0:T(8,128)(2,1)S(1)} collective-permute-done((bf16[32,3072]{1,0:T(8,128)(2,1)S(1)}, bf16[32,3072]{1,0:T(8,128)(2,1)S(1)}, u32[]{:S(2)}, u32[]{:S(2)}) %collective-permute-start.36) | collective-permute-done | bytes 196640 | tf_op jit(solution)/shard_map/ppermute | solution.py:71
  209.6 1.6 collective-permute-start.41
  212.4 1.8 collective-permute-done.41
  214.2 1.6 collective-permute-done.40
  218.7 2.1 gather_fusion.4
  231.0 1.6 collective-permute-start.48
  233.2 2.0 collective-permute-done.44
  235.8 1.6 collective-permute-start.49
  237.4 5.5 %collective-permute-done.45 = bf16[32,3072]{1,0:T(8,128)(2,1)S(1)} collective-permute-done((bf16[32,3072]{1,0:T(8,128)(2,1)S(1)}, bf16[32,3072]{1,0:T(8,128)(2,1)S(1)}, u32[]{:S(2)}, u32[]{:S(2)}) %collective-permute-start.45) | collective-permute-done | bytes 196640 | tf_op jit(solution)/shard_map/ppermute | solution.py:108
  243.5 6.6 %collective-permute-done.46 = bf16[32,3072]{1,0:T(8,128)(2,1)S(1)} collective-permute-done((bf16[32,3072]{1,0:T(8,128)(2,1)S(1)}, bf16[32,3072]{1,0:T(8,128)(2,1)S(1)}, u32[]{:S(2)}, u32[]{:S(2)}) %collective-permute-start.46) | collective-permute-done | bytes 196640 | tf_op jit(solution)/shard_map/ppermute | solution.py:108
  250.2 1.6 collective-permute-start.50
  252.3 4.2 %collective-permute-done.50 = bf16[32,3072]{1,0:T(8,128)(2,1)S(1)} collective-permute-done((bf16[32,3072]{1,0:T(8,128)(2,1)S(1)}, bf16[32,3072]{1,0:T(8,128)(2,1)S(1)}, u32[]{:S(2)}, u32[]{:S(2)}) %collective-permute-start.50) | collective-permute-done | bytes 196640 | tf_op jit(solution)/shard_map/ppermute | solution.py:108
  256.5 1.6 collective-permute-start.51
  258.1 4.1 %collective-permute-done.51 = bf16[32,3072]{1,0:T(8,128)(2,1)S(1)} collective-permute-done((bf16[32,3072]{1,0:T(8,128)(2,1)S(1)}, bf16[32,3072]{1,0:T(8,128)(2,1)S(1)}, u32[]{:S(2)}, u32[]{:S(2)}) %collective-permute-start.51) | collective-permute-done | bytes 196640 | tf_op jit(solution)/shard_map/ppermute | solution.py:108
  (147 shorter events, 51.3 us)
Async XLA Ops:
  0.0 230.2 %copy-start = (bf16[1,128,3072]{2,1,0:T(8,128)(2,1)S(1)}, bf16[1,128,3072]{2,1,0:T(8,128)(2,1)}, u32[]{:S(2)}) copy-start(bf16[1,128,3072]{2,1,0:T(8,128)(2,1)} %param.28) | copy-start | bytes 2359300
  0.0 31.3 %collective-permute-start.1 = (bf16[32,3072]{1,0:T(8,128)(2,1)}, bf16[32,3072]{1,0:T(8,128)(2,1)S(1)}, u32[]{:S(2)}, u32[]{:S(2)}) collective-permute-start(bf16[32,3072]{1,0:T(8,128)(2,1)} %param.22), channel_id=1, source_target_pairs={{0,3},{2,1},{4,0},{6,2},{7,4},{5,6},{3,7},{1,5},{8,11},{10,9},{12,... | collective-permute-start | bytes 589832 | tf_op jit(solution)/shard_map/ppermute | solution.py:59
  4.0 29.4 %collective-permute-start = (bf16[32,3072]{1,0:T(8,128)(2,1)}, bf16[32,3072]{1,0:T(8,128)(2,1)S(1)}, u32[]{:S(2)}, u32[]{:S(2)}) collective-permute-start(bf16[32,3072]{1,0:T(8,128)(2,1)} %param.22), channel_id=1, source_target_pairs={{0,1},{2,0},{4,2},{6,4},{7,6},{5,7},{3,5},{1,3},{8,9},{10,8},{12,1... | collective-permute-start | bytes 589832 | tf_op jit(solution)/shard_map/ppermute | solution.py:59
  5.6 40.1 %collective-permute-start.7 = (bf16[32,3072]{1,0:T(8,128)(2,1)}, bf16[32,3072]{1,0:T(8,128)(2,1)S(1)}, u32[]{:S(2)}, u32[]{:S(2)}) collective-permute-start(bf16[32,3072]{1,0:T(8,128)(2,1)} %param.22), channel_id=1, source_target_pairs={{0,2},{2,4},{4,6},{6,7},{7,5},{5,3},{3,1},{1,0},{8,10},{10,12},{12... | collective-permute-start | bytes 589832 | tf_op jit(solution)/shard_map/ppermute | solution.py:58
  6.0 27.2 %collective-permute-start.3 = (bf16[32,3072]{1,0:T(8,128)(2,1)}, bf16[32,3072]{1,0:T(8,128)(2,1)S(1)}, u32[]{:S(2)}, u32[]{:S(2)}) collective-permute-start(bf16[32,3072]{1,0:T(8,128)(2,1)} %param.22), channel_id=1, source_target_pairs={{0,4},{2,6},{4,7},{6,5},{7,3},{5,1},{3,0},{1,2},{8,12},{10,14},{12... | collective-permute-start | bytes 589832 | tf_op jit(solution)/shard_map/ppermute | solution.py:58
  31.3 5.9 %collective-permute-start.2 = (bf16[32,3072]{1,0:T(8,128)(2,1)S(1)}, bf16[32,3072]{1,0:T(8,128)(2,1)S(1)}, u32[]{:S(2)}, u32[]{:S(2)}) collective-permute-start(bf16[32,3072]{1,0:T(8,128)(2,1)S(1)} %collective-permute-done.1), channel_id=1, source_target_pairs={{0,1},{2,0},{4,2},{6,4},{7,6},{5,7},{3,5},{1,3},{8,9},{10,8},{12,1... | collective-permute-start | bytes 589832 | tf_op jit(solution)/shard_map/ppermute | solution.py:71
  33.2 5.7 %collective-permute-start.4 = (bf16[32,3072]{1,0:T(8,128)(2,1)S(1)}, bf16[32,3072]{1,0:T(8,128)(2,1)S(1)}, u32[]{:S(2)}, u32[]{:S(2)}) collective-permute-start(bf16[32,3072]{1,0:T(8,128)(2,1)S(1)} %collective-permute-done.3), channel_id=1, source_target_pairs={{0,2},{2,4},{4,6},{6,7},{7,5},{5,3},{3,1},{1,0},{8,10},{10,12},{12... | collective-permute-start | bytes 589832 | tf_op jit(solution)/shard_map/ppermute | solution.py:68
  37.2 4.7 %collective-permute-start.6 = (bf16[16,3072]{1,0:T(8,128)(2,1)S(1)}, bf16[16,3072]{1,0:T(8,128)(2,1)S(1)}, u32[]{:S(2)}, u32[]{:S(2)}) collective-permute-start(bf16[16,3072]{1,0:T(8,128)(2,1)S(1)} %slice.391), channel_id=1, source_target_pairs={{0,1},{2,0},{4,2},{6,4},{7,6},{5,7},{3,5},{1,3},{8,9},{10,8},{12,1... | collective-permute-start | bytes 294920 | tf_op jit(solution)/shard_map/ppermute | solution.py:65
  38.9 4.7 %collective-permute-start.5 = (bf16[16,3072]{1,0:T(8,128)(2,1)S(1)}, bf16[16,3072]{1,0:T(8,128)(2,1)S(1)}, u32[]{:S(2)}, u32[]{:S(2)}) collective-permute-start(bf16[16,3072]{1,0:T(8,128)(2,1)S(1)} %slice.390), channel_id=1, source_target_pairs={{0,2},{2,4},{4,6},{6,7},{7,5},{5,3},{3,1},{1,0},{8,10},{10,12},{12... | collective-permute-start | bytes 294920 | tf_op jit(solution)/shard_map/ppermute | solution.py:64
  48.4 1.4 copy-start.2
  48.5 3.2 %collective-permute-start.8 = (bf16[128,3072]{1,0:T(8,128)(2,1)S(1)}, bf16[128,3072]{1,0:T(8,128)(2,1)S(1)}, u32[]{:S(2)}, u32[]{:S(2)}) collective-permute-start(bf16[128,3072]{1,0:T(8,128)(2,1)S(1)} %bitcast.151), channel_id=1, source_target_pairs={{0,8},{1,9},{2,10},{3,11},{4,12},{5,13},{6,14},{7,15},{16,24},{17,... | collective-permute-start | bytes 2359304 | tf_op jit(solution)/shard_map/ppermute | solution.py:14
  72.5 5.1 %collective-permute-start.9 = (bf16[16,3072]{1,0:T(8,128)(2,1)S(1)}, bf16[16,3072]{1,0:T(8,128)(2,1)S(1)}, u32[]{:S(2)}, u32[]{:S(2)}) collective-permute-start(bf16[16,3072]{1,0:T(8,128)(2,1)S(1)} %get-tuple-element.121), channel_id=1, source_target_pairs={{0,2},{2,4},{4,6},{6,7},{7,5},{5,3},{3,1},{1,0},{8,10},{10,12},{12... | collective-permute-start | bytes 294920 | tf_op jit(solution)/shard_map/ppermute | solution.py:108
  73.0 5.2 %collective-permute-start.13 = (bf16[16,3072]{1,0:T(8,128)(2,1)S(1)}, bf16[16,3072]{1,0:T(8,128)(2,1)S(1)}, u32[]{:S(2)}, u32[]{:S(2)}) collective-permute-start(bf16[16,3072]{1,0:T(8,128)(2,1)S(1)} %get-tuple-element.122), channel_id=1, source_target_pairs={{0,1},{2,0},{4,2},{6,4},{7,6},{5,7},{3,5},{1,3},{8,9},{10,8},{12,1... | collective-permute-start | bytes 294920 | tf_op jit(solution)/shard_map/ppermute | solution.py:108
  77.7 6.4 %collective-permute-start.10 = (bf16[32,3072]{1,0:T(8,128)(2,1)S(1)}, bf16[32,3072]{1,0:T(8,128)(2,1)S(1)}, u32[]{:S(2)}, u32[]{:S(2)}) collective-permute-start(bf16[32,3072]{1,0:T(8,128)(2,1)S(1)} %convert_element_type.317), channel_id=1, source_target_pairs={{0,2},{2,4},{4,6},{6,7},{7,5},{5,3},{3,1},{1,0},{8,10},{10,12},{12... | collective-permute-start | bytes 589832 | tf_op jit(solution)/shard_map/ppermute | solution.py:108
  78.2 25.7 %copy-start.1 = (bf16[32,3072]{1,0:T(8,128)(2,1)S(1)}, bf16[32,3072]{1,0:T(8,128)(2,1)}, u32[]{:S(2)}) copy-start(bf16[32,3072]{1,0:T(8,128)(2,1)} %param.22) | copy-start | bytes 589828
  78.2 6.4 %collective-permute-start.14 = (bf16[32,3072]{1,0:T(8,128)(2,1)S(1)}, bf16[32,3072]{1,0:T(8,128)(2,1)S(1)}, u32[]{:S(2)}, u32[]{:S(2)}) collective-permute-start(bf16[32,3072]{1,0:T(8,128)(2,1)S(1)} %convert_element_type.327), channel_id=1, source_target_pairs={{0,1},{2,0},{4,2},{6,4},{7,6},{5,7},{3,5},{1,3},{8,9},{10,8},{12,1... | collective-permute-start | bytes 589832 | tf_op jit(solution)/shard_map/ppermute | solution.py:108
  84.2 5.7 %collective-permute-start.11 = (bf16[32,3072]{1,0:T(8,128)(2,1)S(1)}, bf16[32,3072]{1,0:T(8,128)(2,1)S(1)}, u32[]{:S(2)}, u32[]{:S(2)}) collective-permute-start(bf16[32,3072]{1,0:T(8,128)(2,1)S(1)} %add_convert_fusion.14), channel_id=1, source_target_pairs={{0,2},{2,4},{4,6},{6,7},{7,5},{5,3},{3,1},{1,0},{8,10},{10,12},{12... | collective-permute-start | bytes 589832 | tf_op jit(solution)/shard_map/ppermute | solution.py:108
  90.0 6.6 %collective-permute-start.15 = (bf16[32,3072]{1,0:T(8,128)(2,1)S(1)}, bf16[32,3072]{1,0:T(8,128)(2,1)S(1)}, u32[]{:S(2)}, u32[]{:S(2)}) collective-permute-start(bf16[32,3072]{1,0:T(8,128)(2,1)S(1)} %get-tuple-element.114), channel_id=1, source_target_pairs={{0,1},{2,0},{4,2},{6,4},{7,6},{5,7},{3,5},{1,3},{8,9},{10,8},{12,1... | collective-permute-start | bytes 589832 | tf_op jit(solution)/shard_map/ppermute | solution.py:108
  91.7 6.7 %collective-permute-start.12 = (bf16[32,3072]{1,0:T(8,128)(2,1)S(1)}, bf16[32,3072]{1,0:T(8,128)(2,1)S(1)}, u32[]{:S(2)}, u32[]{:S(2)}) collective-permute-start(bf16[32,3072]{1,0:T(8,128)(2,1)S(1)} %get-tuple-element.113), channel_id=1, source_target_pairs={{0,2},{2,4},{4,6},{6,7},{7,5},{5,3},{3,1},{1,0},{8,10},{10,12},{12... | collective-permute-start | bytes 589832 | tf_op jit(solution)/shard_map/ppermute | solution.py:108
  96.7 7.1 %collective-permute-start.16 = (bf16[32,3072]{1,0:T(8,128)(2,1)S(1)}, bf16[32,3072]{1,0:T(8,128)(2,1)S(1)}, u32[]{:S(2)}, u32[]{:S(2)}) collective-permute-start(bf16[32,3072]{1,0:T(8,128)(2,1)S(1)} %add_convert_fusion.11), channel_id=1, source_target_pairs={{0,1},{2,0},{4,2},{6,4},{7,6},{5,7},{3,5},{1,3},{8,9},{10,8},{12,1... | collective-permute-start | bytes 589832 | tf_op jit(solution)/shard_map/ppermute | solution.py:108
  104.7 6.5 %collective-permute-start.17 = (bf16[32,3072]{1,0:T(8,128)(2,1)S(1)}, bf16[32,3072]{1,0:T(8,128)(2,1)S(1)}, u32[]{:S(2)}, u32[]{:S(2)}) collective-permute-start(bf16[32,3072]{1,0:T(8,128)(2,1)S(1)} %get-tuple-element.98), channel_id=1, source_target_pairs={{0,1},{2,0},{4,2},{6,4},{7,6},{5,7},{3,5},{1,3},{8,9},{10,8},{12,1... | collective-permute-start | bytes 589832 | tf_op jit(solution)/shard_map/ppermute | solution.py:59
  106.3 6.5 %collective-permute-start.20 = (bf16[32,3072]{1,0:T(8,128)(2,1)S(1)}, bf16[32,3072]{1,0:T(8,128)(2,1)S(1)}, u32[]{:S(2)}, u32[]{:S(2)}) collective-permute-start(bf16[32,3072]{1,0:T(8,128)(2,1)S(1)} %get-tuple-element.98), channel_id=1, source_target_pairs={{0,2},{2,4},{4,6},{6,7},{7,5},{5,3},{3,1},{1,0},{8,10},{10,12},{12... | collective-permute-start | bytes 589832 | tf_op jit(solution)/shard_map/ppermute | solution.py:58
  111.2 5.7 %collective-permute-start.18 = (bf16[32,3072]{1,0:T(8,128)(2,1)S(1)}, bf16[32,3072]{1,0:T(8,128)(2,1)S(1)}, u32[]{:S(2)}, u32[]{:S(2)}) collective-permute-start(bf16[32,3072]{1,0:T(8,128)(2,1)S(1)} %collective-permute-done.17), channel_id=1, source_target_pairs={{0,1},{2,0},{4,2},{6,4},{7,6},{5,7},{3,5},{1,3},{8,9},{10,8},{12,1... | collective-permute-start | bytes 589832 | tf_op jit(solution)/shard_map/ppermute | solution.py:71
  112.8 5.7 %collective-permute-start.21 = (bf16[32,3072]{1,0:T(8,128)(2,1)S(1)}, bf16[32,3072]{1,0:T(8,128)(2,1)S(1)}, u32[]{:S(2)}, u32[]{:S(2)}) collective-permute-start(bf16[32,3072]{1,0:T(8,128)(2,1)S(1)} %collective-permute-done.20), channel_id=1, source_target_pairs={{0,2},{2,4},{4,6},{6,7},{7,5},{5,3},{3,1},{1,0},{8,10},{10,12},{12... | collective-permute-start | bytes 589832 | tf_op jit(solution)/shard_map/ppermute | solution.py:68
  116.9 5.7 %collective-permute-start.19 = (bf16[32,3072]{1,0:T(8,128)(2,1)S(1)}, bf16[32,3072]{1,0:T(8,128)(2,1)S(1)}, u32[]{:S(2)}, u32[]{:S(2)}) collective-permute-start(bf16[32,3072]{1,0:T(8,128)(2,1)S(1)} %collective-permute-done.18), channel_id=1, source_target_pairs={{0,1},{2,0},{4,2},{6,4},{7,6},{5,7},{3,5},{1,3},{8,9},{10,8},{12,1... | collective-permute-start | bytes 589832 | tf_op jit(solution)/shard_map/ppermute | solution.py:71
  118.5 5.7 %collective-permute-start.22 = (bf16[32,3072]{1,0:T(8,128)(2,1)S(1)}, bf16[32,3072]{1,0:T(8,128)(2,1)S(1)}, u32[]{:S(2)}, u32[]{:S(2)}) collective-permute-start(bf16[32,3072]{1,0:T(8,128)(2,1)S(1)} %collective-permute-done.21), channel_id=1, source_target_pairs={{0,2},{2,4},{4,6},{6,7},{7,5},{5,3},{3,1},{1,0},{8,10},{10,12},{12... | collective-permute-start | bytes 589832 | tf_op jit(solution)/shard_map/ppermute | solution.py:68
  122.6 4.7 %collective-permute-start.24 = (bf16[16,3072]{1,0:T(8,128)(2,1)S(1)}, bf16[16,3072]{1,0:T(8,128)(2,1)S(1)}, u32[]{:S(2)}, u32[]{:S(2)}) collective-permute-start(bf16[16,3072]{1,0:T(8,128)(2,1)S(1)} %slice.406), channel_id=1, source_target_pairs={{0,1},{2,0},{4,2},{6,4},{7,6},{5,7},{3,5},{1,3},{8,9},{10,8},{12,1... | collective-permute-start | bytes 294920 | tf_op jit(solution)/shard_map/ppermute | solution.py:65
  124.2 4.7 %collective-permute-start.23 = (bf16[16,3072]{1,0:T(8,128)(2,1)S(1)}, bf16[16,3072]{1,0:T(8,128)(2,1)S(1)}, u32[]{:S(2)}, u32[]{:S(2)}) collective-permute-start(bf16[16,3072]{1,0:T(8,128)(2,1)S(1)} %slice.405), channel_id=1, source_target_pairs={{0,2},{2,4},{4,6},{6,7},{7,5},{5,3},{3,1},{1,0},{8,10},{10,12},{12... | collective-permute-start | bytes 294920 | tf_op jit(solution)/shard_map/ppermute | solution.py:64
  133.8 4.1 %collective-permute-start.25 = (bf16[128,3072]{1,0:T(8,128)(2,1)S(1)}, bf16[128,3072]{1,0:T(8,128)(2,1)}, u32[]{:S(2)}, u32[]{:S(2)}) collective-permute-start(bf16[128,3072]{1,0:T(8,128)(2,1)S(1)} %bitcast.150), channel_id=1, source_target_pairs={{0,8},{1,9},{2,10},{3,11},{4,12},{5,13},{6,14},{7,15},{16,24},{17,... | collective-permute-start | bytes 2359304 | tf_op jit(solution)/shard_map/ppermute | solution.py:14
  159.6 4.8 %collective-permute-start.26 = (bf16[16,3072]{1,0:T(8,128)(2,1)S(1)}, bf16[16,3072]{1,0:T(8,128)(2,1)S(1)}, u32[]{:S(2)}, u32[]{:S(2)}) collective-permute-start(bf16[16,3072]{1,0:T(8,128)(2,1)S(1)} %get-tuple-element.119), channel_id=1, source_target_pairs={{0,2},{2,4},{4,6},{6,7},{7,5},{5,3},{3,1},{1,0},{8,10},{10,12},{12... | collective-permute-start | bytes 294920 | tf_op jit(solution)/shard_map/ppermute | solution.py:108
  160.1 4.9 %collective-permute-start.30 = (bf16[16,3072]{1,0:T(8,128)(2,1)S(1)}, bf16[16,3072]{1,0:T(8,128)(2,1)S(1)}, u32[]{:S(2)}, u32[]{:S(2)}) collective-permute-start(bf16[16,3072]{1,0:T(8,128)(2,1)S(1)} %get-tuple-element.120), channel_id=1, source_target_pairs={{0,1},{2,0},{4,2},{6,4},{7,6},{5,7},{3,5},{1,3},{8,9},{10,8},{12,1... | collective-permute-start | bytes 294920 | tf_op jit(solution)/shard_map/ppermute | solution.py:108
  164.5 5.9 %collective-permute-start.27 = (bf16[32,3072]{1,0:T(8,128)(2,1)S(1)}, bf16[32,3072]{1,0:T(8,128)(2,1)S(1)}, u32[]{:S(2)}, u32[]{:S(2)}) collective-permute-start(bf16[32,3072]{1,0:T(8,128)(2,1)S(1)} %convert_element_type.342), channel_id=1, source_target_pairs={{0,2},{2,4},{4,6},{6,7},{7,5},{5,3},{3,1},{1,0},{8,10},{10,12},{12... | collective-permute-start | bytes 589832 | tf_op jit(solution)/shard_map/ppermute | solution.py:108
  165.0 5.9 %collective-permute-start.31 = (bf16[32,3072]{1,0:T(8,128)(2,1)S(1)}, bf16[32,3072]{1,0:T(8,128)(2,1)S(1)}, u32[]{:S(2)}, u32[]{:S(2)}) collective-permute-start(bf16[32,3072]{1,0:T(8,128)(2,1)S(1)} %convert_element_type.352), channel_id=1, source_target_pairs={{0,1},{2,0},{4,2},{6,4},{7,6},{5,7},{3,5},{1,3},{8,9},{10,8},{12,1... | collective-permute-start | bytes 589832 | tf_op jit(solution)/shard_map/ppermute | solution.py:108
  170.4 5.7 %collective-permute-start.28 = (bf16[32,3072]{1,0:T(8,128)(2,1)S(1)}, bf16[32,3072]{1,0:T(8,128)(2,1)S(1)}, u32[]{:S(2)}, u32[]{:S(2)}) collective-permute-start(bf16[32,3072]{1,0:T(8,128)(2,1)S(1)} %add_convert_fusion.9), channel_id=1, source_target_pairs={{0,2},{2,4},{4,6},{6,7},{7,5},{5,3},{3,1},{1,0},{8,10},{10,12},{12... | collective-permute-start | bytes 589832 | tf_op jit(solution)/shard_map/ppermute | solution.py:108
  176.2 7.3 %collective-permute-start.32 = (bf16[32,3072]{1,0:T(8,128)(2,1)S(1)}, bf16[32,3072]{1,0:T(8,128)(2,1)S(1)}, u32[]{:S(2)}, u32[]{:S(2)}) collective-permute-start(bf16[32,3072]{1,0:T(8,128)(2,1)S(1)} %get-tuple-element.110), channel_id=1, source_target_pairs={{0,1},{2,0},{4,2},{6,4},{7,6},{5,7},{3,5},{1,3},{8,9},{10,8},{12,1... | collective-permute-start | bytes 589832 | tf_op jit(solution)/shard_map/ppermute | solution.py:108
  177.9 7.3 %collective-permute-start.29 = (bf16[32,3072]{1,0:T(8,128)(2,1)S(1)}, bf16[32,3072]{1,0:T(8,128)(2,1)S(1)}, u32[]{:S(2)}, u32[]{:S(2)}) collective-permute-start(bf16[32,3072]{1,0:T(8,128)(2,1)S(1)} %get-tuple-element.109), channel_id=1, source_target_pairs={{0,2},{2,4},{4,6},{6,7},{7,5},{5,3},{3,1},{1,0},{8,10},{10,12},{12... | collective-permute-start | bytes 589832 | tf_op jit(solution)/shard_map/ppermute | solution.py:108
  183.6 7.7 %collective-permute-start.33 = (bf16[32,3072]{1,0:T(8,128)(2,1)S(1)}, bf16[32,3072]{1,0:T(8,128)(2,1)S(1)}, u32[]{:S(2)}, u32[]{:S(2)}) collective-permute-start(bf16[32,3072]{1,0:T(8,128)(2,1)S(1)} %add_convert_fusion.6), channel_id=1, source_target_pairs={{0,1},{2,0},{4,2},{6,4},{7,6},{5,7},{3,5},{1,3},{8,9},{10,8},{12,1... | collective-permute-start | bytes 589832 | tf_op jit(solution)/shard_map/ppermute | solution.py:108
  192.1 6.1 %collective-permute-start.34 = (bf16[32,3072]{1,0:T(8,128)(2,1)S(1)}, bf16[32,3072]{1,0:T(8,128)(2,1)S(1)}, u32[]{:S(2)}, u32[]{:S(2)}) collective-permute-start(bf16[32,3072]{1,0:T(8,128)(2,1)S(1)} %get-tuple-element.96), channel_id=1, source_target_pairs={{0,1},{2,0},{4,2},{6,4},{7,6},{5,7},{3,5},{1,3},{8,9},{10,8},{12,1... | collective-permute-start | bytes 589832 | tf_op jit(solution)/shard_map/ppermute | solution.py:59
  193.6 6.1 %collective-permute-start.37 = (bf16[32,3072]{1,0:T(8,128)(2,1)S(1)}, bf16[32,3072]{1,0:T(8,128)(2,1)S(1)}, u32[]{:S(2)}, u32[]{:S(2)}) collective-permute-start(bf16[32,3072]{1,0:T(8,128)(2,1)S(1)} %get-tuple-element.96), channel_id=1, source_target_pairs={{0,2},{2,4},{4,6},{6,7},{7,5},{5,3},{3,1},{1,0},{8,10},{10,12},{12... | collective-permute-start | bytes 589832 | tf_op jit(solution)/shard_map/ppermute | solution.py:58
  198.2 5.7 %collective-permute-start.35 = (bf16[32,3072]{1,0:T(8,128)(2,1)S(1)}, bf16[32,3072]{1,0:T(8,128)(2,1)S(1)}, u32[]{:S(2)}, u32[]{:S(2)}) collective-permute-start(bf16[32,3072]{1,0:T(8,128)(2,1)S(1)} %collective-permute-done.34), channel_id=1, source_target_pairs={{0,1},{2,0},{4,2},{6,4},{7,6},{5,7},{3,5},{1,3},{8,9},{10,8},{12,1... | collective-permute-start | bytes 589832 | tf_op jit(solution)/shard_map/ppermute | solution.py:71
  199.8 5.7 %collective-permute-start.38 = (bf16[32,3072]{1,0:T(8,128)(2,1)S(1)}, bf16[32,3072]{1,0:T(8,128)(2,1)S(1)}, u32[]{:S(2)}, u32[]{:S(2)}) collective-permute-start(bf16[32,3072]{1,0:T(8,128)(2,1)S(1)} %collective-permute-done.37), channel_id=1, source_target_pairs={{0,2},{2,4},{4,6},{6,7},{7,5},{5,3},{3,1},{1,0},{8,10},{10,12},{12... | collective-permute-start | bytes 589832 | tf_op jit(solution)/shard_map/ppermute | solution.py:68
  203.9 5.7 %collective-permute-start.36 = (bf16[32,3072]{1,0:T(8,128)(2,1)S(1)}, bf16[32,3072]{1,0:T(8,128)(2,1)S(1)}, u32[]{:S(2)}, u32[]{:S(2)}) collective-permute-start(bf16[32,3072]{1,0:T(8,128)(2,1)S(1)} %collective-permute-done.35), channel_id=1, source_target_pairs={{0,1},{2,0},{4,2},{6,4},{7,6},{5,7},{3,5},{1,3},{8,9},{10,8},{12,1... | collective-permute-start | bytes 589832 | tf_op jit(solution)/shard_map/ppermute | solution.py:71
  205.5 5.7 %collective-permute-start.39 = (bf16[32,3072]{1,0:T(8,128)(2,1)S(1)}, bf16[32,3072]{1,0:T(8,128)(2,1)S(1)}, u32[]{:S(2)}, u32[]{:S(2)}) collective-permute-start(bf16[32,3072]{1,0:T(8,128)(2,1)S(1)} %collective-permute-done.38), channel_id=1, source_target_pairs={{0,2},{2,4},{4,6},{6,7},{7,5},{5,3},{3,1},{1,0},{8,10},{10,12},{12... | collective-permute-start | bytes 589832 | tf_op jit(solution)/shard_map/ppermute | solution.py:68
  209.6 4.7 %collective-permute-start.41 = (bf16[16,3072]{1,0:T(8,128)(2,1)S(1)}, bf16[16,3072]{1,0:T(8,128)(2,1)S(1)}, u32[]{:S(2)}, u32[]{:S(2)}) collective-permute-start(bf16[16,3072]{1,0:T(8,128)(2,1)S(1)} %slice.421), channel_id=1, source_target_pairs={{0,1},{2,0},{4,2},{6,4},{7,6},{5,7},{3,5},{1,3},{8,9},{10,8},{12,1... | collective-permute-start | bytes 294920 | tf_op jit(solution)/shard_map/ppermute | solution.py:65
  211.2 4.7 %collective-permute-start.40 = (bf16[16,3072]{1,0:T(8,128)(2,1)S(1)}, bf16[16,3072]{1,0:T(8,128)(2,1)S(1)}, u32[]{:S(2)}, u32[]{:S(2)}) collective-permute-start(bf16[16,3072]{1,0:T(8,128)(2,1)S(1)} %slice.420), channel_id=1, source_target_pairs={{0,2},{2,4},{4,6},{6,7},{7,5},{5,3},{3,1},{1,0},{8,10},{10,12},{12... | collective-permute-start | bytes 294920 | tf_op jit(solution)/shard_map/ppermute | solution.py:64
  221.1 1.7 copy-start.3
  224.5 2.9 %collective-permute-start.42 = (bf16[256,128]{1,0:T(8,128)(2,1)S(1)}, bf16[256,128]{1,0:T(8,128)(2,1)S(1)}, u32[]{:S(2)}, u32[]{:S(2)}) collective-permute-start(bf16[256,128]{1,0:T(8,128)(2,1)S(1)} %convolution_convert_fusion.7), channel_id=1, source_target_pairs={{0,8},{1,9},{2,10},{3,11},{4,12},{5,13},{6,14},{7,15},{16,24},{17,... | collective-permute-start | bytes 196616 | tf_op jit(solution)/shard_map/ppermute | solution.py:14
  225.8 2.2 collective-permute-start.43
  230.5 4.7 %collective-permute-start.44 = (bf16[16,3072]{1,0:T(8,128)(2,1)S(1)}, bf16[16,3072]{1,0:T(8,128)(2,1)S(1)}, u32[]{:S(2)}, u32[]{:S(2)}) collective-permute-start(bf16[16,3072]{1,0:T(8,128)(2,1)S(1)} %get-tuple-element.117), channel_id=1, source_target_pairs={{0,2},{2,4},{4,6},{6,7},{7,5},{5,3},{3,1},{1,0},{8,10},{10,12},{12... | collective-permute-start | bytes 294920 | tf_op jit(solution)/shard_map/ppermute | solution.py:108
  231.0 4.7 %collective-permute-start.48 = (bf16[16,3072]{1,0:T(8,128)(2,1)S(1)}, bf16[16,3072]{1,0:T(8,128)(2,1)S(1)}, u32[]{:S(2)}, u32[]{:S(2)}) collective-permute-start(bf16[16,3072]{1,0:T(8,128)(2,1)S(1)} %get-tuple-element.118), channel_id=1, source_target_pairs={{0,1},{2,0},{4,2},{6,4},{7,6},{5,7},{3,5},{1,3},{8,9},{10,8},{12,1... | collective-permute-start | bytes 294920 | tf_op jit(solution)/shard_map/ppermute | solution.py:108
  235.2 7.7 %collective-permute-start.45 = (bf16[32,3072]{1,0:T(8,128)(2,1)S(1)}, bf16[32,3072]{1,0:T(8,128)(2,1)S(1)}, u32[]{:S(2)}, u32[]{:S(2)}) collective-permute-start(bf16[32,3072]{1,0:T(8,128)(2,1)S(1)} %convert_element_type.376), channel_id=1, source_target_pairs={{0,2},{2,4},{4,6},{6,7},{7,5},{5,3},{3,1},{1,0},{8,10},{10,12},{12... | collective-permute-start | bytes 589832 | tf_op jit(solution)/shard_map/ppermute | solution.py:108
  235.8 7.7 %collective-permute-start.49 = (bf16[32,3072]{1,0:T(8,128)(2,1)S(1)}, bf16[32,3072]{1,0:T(8,128)(2,1)S(1)}, u32[]{:S(2)}, u32[]{:S(2)}) collective-permute-start(bf16[32,3072]{1,0:T(8,128)(2,1)S(1)} %convert_element_type.386), channel_id=1, source_target_pairs={{0,1},{2,0},{4,2},{6,4},{7,6},{5,7},{3,5},{1,3},{8,9},{10,8},{12,1... | collective-permute-start | bytes 589832 | tf_op jit(solution)/shard_map/ppermute | solution.py:108
  243.0 7.1 %collective-permute-start.46 = (bf16[32,3072]{1,0:T(8,128)(2,1)S(1)}, bf16[32,3072]{1,0:T(8,128)(2,1)S(1)}, u32[]{:S(2)}, u32[]{:S(2)}) collective-permute-start(bf16[32,3072]{1,0:T(8,128)(2,1)S(1)} %add_convert_fusion.4), channel_id=1, source_target_pairs={{0,2},{2,4},{4,6},{6,7},{7,5},{5,3},{3,1},{1,0},{8,10},{10,12},{12... | collective-permute-start | bytes 589832 | tf_op jit(solution)/shard_map/ppermute | solution.py:108
  250.2 6.2 %collective-permute-start.50 = (bf16[32,3072]{1,0:T(8,128)(2,1)S(1)}, bf16[32,3072]{1,0:T(8,128)(2,1)S(1)}, u32[]{:S(2)}, u32[]{:S(2)}) collective-permute-start(bf16[32,3072]{1,0:T(8,128)(2,1)S(1)} %get-tuple-element.106), channel_id=1, source_target_pairs={{0,1},{2,0},{4,2},{6,4},{7,6},{5,7},{3,5},{1,3},{8,9},{10,8},{12,1... | collective-permute-start | bytes 589832 | tf_op jit(solution)/shard_map/ppermute | solution.py:108
  251.8 6.3 %collective-permute-start.47 = (bf16[32,3072]{1,0:T(8,128)(2,1)S(1)}, bf16[32,3072]{1,0:T(8,128)(2,1)S(1)}, u32[]{:S(2)}, u32[]{:S(2)}) collective-permute-start(bf16[32,3072]{1,0:T(8,128)(2,1)S(1)} %get-tuple-element.105), channel_id=1, source_target_pairs={{0,2},{2,4},{4,6},{6,7},{7,5},{5,3},{3,1},{1,0},{8,10},{10,12},{12... | collective-permute-start | bytes 589832 | tf_op jit(solution)/shard_map/ppermute | solution.py:108
  256.5 5.7 %collective-permute-start.51 = (bf16[32,3072]{1,0:T(8,128)(2,1)S(1)}, bf16[32,3072]{1,0:T(8,128)(2,1)S(1)}, u32[]{:S(2)}, u32[]{:S(2)}) collective-permute-start(bf16[32,3072]{1,0:T(8,128)(2,1)S(1)} %add_convert_fusion.1), channel_id=1, source_target_pairs={{0,1},{2,0},{4,2},{6,4},{7,6},{5,7},{3,5},{1,3},{8,9},{10,8},{12,1... | collective-permute-start | bytes 589832 | tf_op jit(solution)/shard_map/ppermute | solution.py:108

commit v15 on v11

--- a/solution.py
+++ b/solution.py
@@ -261,7 +261,7 @@
     layers = w_conv.shape[0]
     share = stream
     tables = ring_tables("head")
-    state = ring_gather(stream, "head", tables, direct=2)
+    state = ring_gather(stream, "head", tables, direct=3)
     conv_by_half = jnp.transpose(w_conv, (0, 1, 3, 2, 4))
     for layer_idx in range(layers):
         gated = convolution_gate(

time: 260 us -> 263 us (1.012)
  starting transfers between devices: 58.1 us -> 61.9 us
    ppermute x4 -> x5, starting transfers between devices: 1.46 us -> 7.97 us  [ring_gather(): lax.ppermute(value, axis, [(order[p], order[(p + k) % length]) for p in r...]
    ppermute x4 -> x5, starting transfers between devices: 8.71 us -> 6.14 us  [ring_gather(): lax.ppermute(value, axis, [(order[p], order[(p - k) % length]) for p in r...]
    ppermute x5 -> x4, starting transfers between devices: 8.16 us -> 5.93 us  [ring_gather(): bwd = lax.ppermute(bwd, axis, backward)]
    ppermute x5 -> x4, waiting for transfers between devices: 14.2 us -> 12.1 us  [ring_gather(): bwd = lax.ppermute(bwd, axis, backward)]
    ppermute x4 -> x5, waiting for transfers between devices: 8.6 us -> 8.89 us  [ring_gather(): lax.ppermute(value, axis, [(order[p], order[(p - k) % length]) for p in r...]
where the time goes in v15:
time: 263 us; the launch traced here: 262 us
  waiting for transfers between devices  96.6 us (37%)
  starting transfers between devices  61.9 us (24%)
  local copies, waits for them, and re-layouts  48.2 us (18%)
  Pallas kernels  21.7 us (8%)
  other arithmetic  17.2 us (7%)
  matrix products  12.6 us (5%)
  between operations  4.29 us (2%)
    ppermute x24, waiting for transfers between devices, chain(): passed = lax.ppermute(part.astype(value.dtype), axis, pairs)  62.7 us
    unnamed x25, local copies, waits for them, and re-layouts  32.9 us
    ppermute x24, starting transfers between devices, chain(): passed = lax.ppermute(part.astype(value.dtype), axis, pairs)  27.1 us
    pallas_call x2, Pallas kernels, convolution_gate(): pl.pallas_call(conv_gate_kernel, out_shape=jax.ShapeDtypeStruct((all_rows...  21.7 us
    ppermute x4, waiting for transfers between devices, ring_gather(): bwd = lax.ppermute(bwd, axis, backward)  12.1 us
    dot_general x6, matrix products, rounded_term(): term = jnp.dot(left, right, preferred_element_type=jnp.float32)  10.4 us
    another operation x4, other arithmetic, convolution_gate(): jnp.stack([lax.dynamic_slice_in_dim(padded, border_rows - tap_idx * dilat...  9.81 us
    ppermute x5, waiting for transfers between devices, ring_gather(): lax.ppermute(value, axis, [(order[p], order[(p - k) % length]) for p in r...  8.89 us
  transfers between devices with their start and end apart: 52, of which 29 were waited for; matrix products, arithmetic and copies ran while one was open for 15% of the time, Pallas kernels for 0%

profile of v15, /device:TPU:0, one launch (start us, length us, event | category | flops | bytes accessed | tf_op | source)
XLA Modules:
  0.0 262.4 jit_solution(18025204165733744077)
XLA Ops:
  0.0 5.0 %collective-permute-start.3 = (bf16[32,3072]{1,0:T(8,128)(2,1)}, bf16[32,3072]{1,0:T(8,128)(2,1)S(1)}, u32[]{:S(2)}, u32[]{:S(2)}) collective-permute-start(bf16[32,3072]{1,0:T(8,128)(2,1)} %param.22), channel_id=1, source_target_pairs={{0,6},{2,7},{4,5},{6,3},{7,1},{5,0},{3,2},{1,4},{8,14},{10,15},{12... | collective-permute-start | bytes 589832 | tf_op jit(solution)/shard_map/ppermute | solution.py:58
  5.1 2.8 %collective-permute-start.1 = (bf16[32,3072]{1,0:T(8,128)(2,1)}, bf16[32,3072]{1,0:T(8,128)(2,1)S(1)}, u32[]{:S(2)}, u32[]{:S(2)}) collective-permute-start(bf16[32,3072]{1,0:T(8,128)(2,1)} %param.22), channel_id=1, source_target_pairs={{0,3},{2,1},{4,0},{6,2},{7,4},{5,6},{3,7},{1,5},{8,11},{10,9},{12,... | collective-permute-start | bytes 589832 | tf_op jit(solution)/shard_map/ppermute | solution.py:59
  7.8 2.0 collective-permute-start.7
  13.1 1.6 bitcast_dynamic-update-slice_fusion.20
  14.7 19.7 %copy.11 = bf16[2,3,3072,2,384]{4,2,3,1,0:T(8,128)(2,1)} copy(bf16[2,3,3072,2,384]{4,3,2,1,0:T(2,128)(2,1)} %param.25) | data formatting | bytes 56623104 | tf_op args[3]
  35.4 1.6 collective-permute-start.4
  39.6 2.5 collective-permute-done.4
  43.5 2.1 collective-permute-done.6
  47.0 2.1 gather_fusion
  52.3 2.2 fusion.23
  54.5 2.4 pad_maximum_fusion.slab_ref
  56.9 10.8 %shard_map.82 = bf16[256,384]{1,0:T(8,128)(2,1)} custom-call(bf16[3,256,3072]{2,1,0:T(8,128)(2,1)} %pad_maximum_fusion.slab_ref, f32[1,3072]{1,0:T(1,128)} %get-tuple-element.124.gain_ref, bf16[2,3,2,3072,384]{4,3,2,1,0:T(8,128)(2,1)} %bitcast.139), custom_call_target="tpu_custom_call" | custom-call | flops 3623878656 | bytes 19070976 | tf_op jit(solution)/shard_map/pallas_call | solution.py:173
  67.7 1.5 gather_fusion.1
  69.2 2.2 convolution_convert_fusion.4
  71.5 2.7 %collective-permute-start.9 = (bf16[16,3072]{1,0:T(8,128)(2,1)S(1)}, bf16[16,3072]{1,0:T(8,128)(2,1)S(1)}, u32[]{:S(2)}, u32[]{:S(2)}) collective-permute-start(bf16[16,3072]{1,0:T(8,128)(2,1)S(1)} %get-tuple-element.121), channel_id=1, source_target_pairs={{0,2},{2,4},{4,6},{6,7},{7,5},{5,3},{3,1},{1,0},{8,10},{10,12},{12... | collective-permute-start | bytes 294920 | tf_op jit(solution)/shard_map/ppermute | solution.py:108
  74.1 1.6 collective-permute-start.13
  75.7 2.6 %convolution_convert_fusion.2 = bf16[256,3072]{1,0:T(8,128)(2,1)S(1)} fusion(bf16[256,384]{1,0:T(8,128)(2,1)S(1)} %bitcast.154, bf16[2,384,3072]{2,1,0:T(8,128)(2,1)} %param.26), kind=kOutput, calls=%fused_computation.19 | convolution fusion | flops 604766208 | bytes 4128768 | tf_op jit(solution)/shard_map/dot_general | solution.py:133
  79.7 1.5 collective-permute-start.14
  81.2 4.4 %collective-permute-done.10 = bf16[32,3072]{1,0:T(8,128)(2,1)S(1)} collective-permute-done((bf16[32,3072]{1,0:T(8,128)(2,1)S(1)}, bf16[32,3072]{1,0:T(8,128)(2,1)S(1)}, u32[]{:S(2)}, u32[]{:S(2)}) %collective-permute-start.10) | collective-permute-done | bytes 196640 | tf_op jit(solution)/shard_map/ppermute | solution.py:108
  86.5 5.1 %collective-permute-done.11 = bf16[32,3072]{1,0:T(8,128)(2,1)S(1)} collective-permute-done((bf16[32,3072]{1,0:T(8,128)(2,1)S(1)}, bf16[32,3072]{1,0:T(8,128)(2,1)S(1)}, u32[]{:S(2)}, u32[]{:S(2)}) %collective-permute-start.11) | collective-permute-done | bytes 196640 | tf_op jit(solution)/shard_map/ppermute | solution.py:108
  91.6 1.5 collective-permute-start.15
  93.7 4.3 %collective-permute-done.15 = bf16[32,3072]{1,0:T(8,128)(2,1)S(1)} collective-permute-done((bf16[32,3072]{1,0:T(8,128)(2,1)S(1)}, bf16[32,3072]{1,0:T(8,128)(2,1)S(1)}, u32[]{:S(2)}, u32[]{:S(2)}) %collective-permute-start.15) | collective-permute-done | bytes 196640 | tf_op jit(solution)/shard_map/ppermute | solution.py:108
  98.1 1.7 collective-permute-start.16
  99.8 5.1 %collective-permute-done.16 = bf16[32,3072]{1,0:T(8,128)(2,1)S(1)} collective-permute-done((bf16[32,3072]{1,0:T(8,128)(2,1)S(1)}, bf16[32,3072]{1,0:T(8,128)(2,1)S(1)}, u32[]{:S(2)}, u32[]{:S(2)}) %collective-permute-start.16) | collective-permute-done | bytes 196640 | tf_op jit(solution)/shard_map/ppermute | solution.py:108
  105.7 2.0 collective-permute-start.17
  107.8 4.8 %collective-permute-done.17 = bf16[32,3072]{1,0:T(8,128)(2,1)S(1)} collective-permute-done((bf16[32,3072]{1,0:T(8,128)(2,1)S(1)}, bf16[32,3072]{1,0:T(8,128)(2,1)S(1)}, u32[]{:S(2)}, u32[]{:S(2)}) %collective-permute-start.17) | collective-permute-done | bytes 196640 | tf_op jit(solution)/shard_map/ppermute | solution.py:59
  112.5 1.7 collective-permute-start.18
  115.3 3.2 %collective-permute-done.18 = bf16[32,3072]{1,0:T(8,128)(2,1)S(1)} collective-permute-done((bf16[32,3072]{1,0:T(8,128)(2,1)S(1)}, bf16[32,3072]{1,0:T(8,128)(2,1)S(1)}, u32[]{:S(2)}, u32[]{:S(2)}) %collective-permute-start.18) | collective-permute-done | bytes 196640 | tf_op jit(solution)/shard_map/ppermute | solution.py:71
  118.5 1.4 collective-permute-start.19
  121.2 2.9 %collective-permute-done.19 = bf16[32,3072]{1,0:T(8,128)(2,1)S(1)} collective-permute-done((bf16[32,3072]{1,0:T(8,128)(2,1)S(1)}, bf16[32,3072]{1,0:T(8,128)(2,1)S(1)}, u32[]{:S(2)}, u32[]{:S(2)}) %collective-permute-start.19) | collective-permute-done | bytes 196640 | tf_op jit(solution)/shard_map/ppermute | solution.py:71
  124.2 1.5 collective-permute-start.24
  127.0 1.8 collective-permute-done.24
  128.8 1.5 collective-permute-done.23
  133.1 2.1 gather_fusion.2
  135.2 2.2 collective-permute-start.25
  139.3 2.8 %fusion.19 = (bf16[1,256,3072]{2,1,0:T(8,128)(2,1)S(1)}, bf16[1,256,3072]{2,1,0:T(8,128)(2,1)S(1)}) fusion(s32[]{:T(128)S(6)} %select_n.23, bf16[256,3072]{1,0:T(8,128)(2,1)S(1)} %bitcast.141, bf16[128,3072]{1,0:T(8,128)(2,1)} %collective-permute-done.25, s32[]{:T(128)S(6)} %select_n.24), kind=kLoop, calls=%fused_computation.45 | loop fusion | flops 6291456 | bytes 5505032 | tf_op jit(solution)/shard_map/stack | solution.py:166
  142.1 2.4 pad_maximum_fusion.1.slab_ref
  144.6 10.8 %shard_map.83 = bf16[256,384]{1,0:T(8,128)(2,1)} custom-call(bf16[3,256,3072]{2,1,0:T(8,128)(2,1)} %pad_maximum_fusion.1.slab_ref, f32[1,3072]{1,0:T(1,128)} %get-tuple-element.125.gain_ref, bf16[2,3,2,3072,384]{4,3,2,1,0:T(8,128)(2,1)} %bitcast.140), custom_call_target="tpu_custom_call" | custom-call | flops 3623878656 | bytes 19070976 | tf_op jit(solution)/shard_map/pallas_call | solution.py:173
  155.4 1.5 gather_fusion.3
  156.9 2.2 convolution_convert_fusion.3
  159.8 1.4 collective-permute-start.30
  161.2 2.6 %convolution_convert_fusion.1 = bf16[256,3072]{1,0:T(8,128)(2,1)S(1)} fusion(bf16[256,384]{1,0:T(8,128)(2,1)S(1)} %bitcast.155, bf16[2,384,3072]{2,1,0:T(8,128)(2,1)} %param.26), kind=kOutput, calls=%fused_computation.18 | convolution fusion | flops 604766208 | bytes 4128768 | tf_op jit(solution)/shard_map/dot_general | solution.py:133
  164.7 1.5 collective-permute-start.31
  166.2 3.7 %collective-permute-done.27 = bf16[32,3072]{1,0:T(8,128)(2,1)S(1)} collective-permute-done((bf16[32,3072]{1,0:T(8,128)(2,1)S(1)}, bf16[32,3072]{1,0:T(8,128)(2,1)S(1)}, u32[]{:S(2)}, u32[]{:S(2)}) %collective-permute-start.27) | collective-permute-done | bytes 196640 | tf_op jit(solution)/shard_map/ppermute | solution.py:108
  170.6 5.1 %collective-permute-done.28 = bf16[32,3072]{1,0:T(8,128)(2,1)S(1)} collective-permute-done((bf16[32,3072]{1,0:T(8,128)(2,1)S(1)}, bf16[32,3072]{1,0:T(8,128)(2,1)S(1)}, u32[]{:S(2)}, u32[]{:S(2)}) %collective-permute-start.28) | collective-permute-done | bytes 196640 | tf_op jit(solution)/shard_map/ppermute | solution.py:108
  175.8 1.5 collective-permute-start.32
  177.9 5.2 %collective-permute-done.32 = bf16[32,3072]{1,0:T(8,128)(2,1)S(1)} collective-permute-done((bf16[32,3072]{1,0:T(8,128)(2,1)S(1)}, bf16[32,3072]{1,0:T(8,128)(2,1)S(1)}, u32[]{:S(2)}, u32[]{:S(2)}) %collective-permute-start.32) | collective-permute-done | bytes 196640 | tf_op jit(solution)/shard_map/ppermute | solution.py:108
  183.1 1.5 collective-permute-start.33
  184.6 6.3 %collective-permute-done.33 = bf16[32,3072]{1,0:T(8,128)(2,1)S(1)} collective-permute-done((bf16[32,3072]{1,0:T(8,128)(2,1)S(1)}, bf16[32,3072]{1,0:T(8,128)(2,1)S(1)}, u32[]{:S(2)}, u32[]{:S(2)}) %collective-permute-start.33) | collective-permute-done | bytes 196640 | tf_op jit(solution)/shard_map/ppermute | solution.py:108
  191.6 1.4 collective-permute-start.34
  193.6 4.1 %collective-permute-done.34 = bf16[32,3072]{1,0:T(8,128)(2,1)S(1)} collective-permute-done((bf16[32,3072]{1,0:T(8,128)(2,1)S(1)}, bf16[32,3072]{1,0:T(8,128)(2,1)S(1)}, u32[]{:S(2)}, u32[]{:S(2)}) %collective-permute-start.34) | collective-permute-done | bytes 196640 | tf_op jit(solution)/shard_map/ppermute | solution.py:59
  200.5 3.0 %collective-permute-done.35 = bf16[32,3072]{1,0:T(8,128)(2,1)S(1)} collective-permute-done((bf16[32,3072]{1,0:T(8,128)(2,1)S(1)}, bf16[32,3072]{1,0:T(8,128)(2,1)S(1)}, u32[]{:S(2)}, u32[]{:S(2)}) %collective-permute-start.35) | collective-permute-done | bytes 196640 | tf_op jit(solution)/shard_map/ppermute | solution.py:71
  206.2 2.9 %collective-permute-done.36 = bf16[32,3072]{1,0:T(8,128)(2,1)S(1)} collective-permute-done((bf16[32,3072]{1,0:T(8,128)(2,1)S(1)}, bf16[32,3072]{1,0:T(8,128)(2,1)S(1)}, u32[]{:S(2)}, u32[]{:S(2)}) %collective-permute-start.36) | collective-permute-done | bytes 196640 | tf_op jit(solution)/shard_map/ppermute | solution.py:71
  209.1 1.5 collective-permute-start.41
  212.0 1.8 collective-permute-done.41
  213.8 1.5 collective-permute-done.40
  218.0 2.1 gather_fusion.4
  230.5 1.4 collective-permute-start.48
  232.5 2.0 collective-permute-done.44
  235.3 1.5 collective-permute-start.49
  236.8 5.5 %collective-permute-done.45 = bf16[32,3072]{1,0:T(8,128)(2,1)S(1)} collective-permute-done((bf16[32,3072]{1,0:T(8,128)(2,1)S(1)}, bf16[32,3072]{1,0:T(8,128)(2,1)S(1)}, u32[]{:S(2)}, u32[]{:S(2)}) %collective-permute-start.45) | collective-permute-done | bytes 196640 | tf_op jit(solution)/shard_map/ppermute | solution.py:108
  243.0 6.4 %collective-permute-done.46 = bf16[32,3072]{1,0:T(8,128)(2,1)S(1)} collective-permute-done((bf16[32,3072]{1,0:T(8,128)(2,1)S(1)}, bf16[32,3072]{1,0:T(8,128)(2,1)S(1)}, u32[]{:S(2)}, u32[]{:S(2)}) %collective-permute-start.46) | collective-permute-done | bytes 196640 | tf_op jit(solution)/shard_map/ppermute | solution.py:108
  251.6 4.2 %collective-permute-done.50 = bf16[32,3072]{1,0:T(8,128)(2,1)S(1)} collective-permute-done((bf16[32,3072]{1,0:T(8,128)(2,1)S(1)}, bf16[32,3072]{1,0:T(8,128)(2,1)S(1)}, u32[]{:S(2)}, u32[]{:S(2)}) %collective-permute-start.50) | collective-permute-done | bytes 196640 | tf_op jit(solution)/shard_map/ppermute | solution.py:108
  256.9 4.7 %collective-permute-done.51 = bf16[32,3072]{1,0:T(8,128)(2,1)S(1)} collective-permute-done((bf16[32,3072]{1,0:T(8,128)(2,1)S(1)}, bf16[32,3072]{1,0:T(8,128)(2,1)S(1)}, u32[]{:S(2)}, u32[]{:S(2)}) %collective-permute-start.51) | collective-permute-done | bytes 196640 | tf_op jit(solution)/shard_map/ppermute | solution.py:108
  (147 shorter events, 52.3 us)
Async XLA Ops:
  0.0 229.6 %copy-start = (bf16[1,128,3072]{2,1,0:T(8,128)(2,1)S(1)}, bf16[1,128,3072]{2,1,0:T(8,128)(2,1)}, u32[]{:S(2)}) copy-start(bf16[1,128,3072]{2,1,0:T(8,128)(2,1)} %param.28) | copy-start | bytes 2359300
  0.0 35.1 %collective-permute-start.3 = (bf16[32,3072]{1,0:T(8,128)(2,1)}, bf16[32,3072]{1,0:T(8,128)(2,1)S(1)}, u32[]{:S(2)}, u32[]{:S(2)}) collective-permute-start(bf16[32,3072]{1,0:T(8,128)(2,1)} %param.22), channel_id=1, source_target_pairs={{0,6},{2,7},{4,5},{6,3},{7,1},{5,0},{3,2},{1,4},{8,14},{10,15},{12... | collective-permute-start | bytes 589832 | tf_op jit(solution)/shard_map/ppermute | solution.py:58
  5.1 30.4 %collective-permute-start.2 = (bf16[32,3072]{1,0:T(8,128)(2,1)}, bf16[32,3072]{1,0:T(8,128)(2,1)S(1)}, u32[]{:S(2)}, u32[]{:S(2)}) collective-permute-start(bf16[32,3072]{1,0:T(8,128)(2,1)} %param.22), channel_id=1, source_target_pairs={{0,5},{2,3},{4,1},{6,0},{7,2},{5,4},{3,6},{1,7},{8,13},{10,11},{12... | collective-permute-start | bytes 589832 | tf_op jit(solution)/shard_map/ppermute | solution.py:59
  5.1 33.2 %collective-permute-start.1 = (bf16[32,3072]{1,0:T(8,128)(2,1)}, bf16[32,3072]{1,0:T(8,128)(2,1)S(1)}, u32[]{:S(2)}, u32[]{:S(2)}) collective-permute-start(bf16[32,3072]{1,0:T(8,128)(2,1)} %param.22), channel_id=1, source_target_pairs={{0,3},{2,1},{4,0},{6,2},{7,4},{5,6},{3,7},{1,5},{8,11},{10,9},{12,... | collective-permute-start | bytes 589832 | tf_op jit(solution)/shard_map/ppermute | solution.py:59
  7.8 29.2 %collective-permute-start = (bf16[32,3072]{1,0:T(8,128)(2,1)}, bf16[32,3072]{1,0:T(8,128)(2,1)S(1)}, u32[]{:S(2)}, u32[]{:S(2)}) collective-permute-start(bf16[32,3072]{1,0:T(8,128)(2,1)} %param.22), channel_id=1, source_target_pairs={{0,1},{2,0},{4,2},{6,4},{7,6},{5,7},{3,5},{1,3},{8,9},{10,8},{12,1... | collective-permute-start | bytes 589832 | tf_op jit(solution)/shard_map/ppermute | solution.py:59
  7.8 38.5 %collective-permute-start.7 = (bf16[32,3072]{1,0:T(8,128)(2,1)}, bf16[32,3072]{1,0:T(8,128)(2,1)S(1)}, u32[]{:S(2)}, u32[]{:S(2)}) collective-permute-start(bf16[32,3072]{1,0:T(8,128)(2,1)} %param.22), channel_id=1, source_target_pairs={{0,2},{2,4},{4,6},{6,7},{7,5},{5,3},{3,1},{1,0},{8,10},{10,12},{12... | collective-permute-start | bytes 589832 | tf_op jit(solution)/shard_map/ppermute | solution.py:58
  14.7 20.4 %copy-start.1 = (bf16[32,3072]{1,0:T(8,128)(2,1)S(1)}, bf16[32,3072]{1,0:T(8,128)(2,1)}, u32[]{:S(2)}) copy-start(bf16[32,3072]{1,0:T(8,128)(2,1)} %param.22) | copy-start | bytes 589828
  35.2 10.4 %collective-permute-start.6 = (bf16[32,3072]{1,0:T(8,128)(2,1)S(1)}, bf16[32,3072]{1,0:T(8,128)(2,1)S(1)}, u32[]{:S(2)}, u32[]{:S(2)}) collective-permute-start(bf16[32,3072]{1,0:T(8,128)(2,1)S(1)} %copy-done.1), channel_id=1, source_target_pairs={{0,4},{2,6},{4,7},{6,5},{7,3},{5,1},{3,0},{1,2},{8,12},{10,14},{12... | collective-permute-start | bytes 589832 | tf_op jit(solution)/shard_map/ppermute | solution.py:58
  35.4 6.7 %collective-permute-start.4 = (bf16[16,3072]{1,0:T(8,128)(2,1)S(1)}, bf16[16,3072]{1,0:T(8,128)(2,1)S(1)}, u32[]{:S(2)}, u32[]{:S(2)}) collective-permute-start(bf16[16,3072]{1,0:T(8,128)(2,1)S(1)} %slice.390), channel_id=1, source_target_pairs={{0,2},{2,4},{4,6},{6,7},{7,5},{5,3},{3,1},{1,0},{8,10},{10,12},{12... | collective-permute-start | bytes 294920 | tf_op jit(solution)/shard_map/ppermute | solution.py:64
  37.0 5.1 %collective-permute-start.5 = (bf16[16,3072]{1,0:T(8,128)(2,1)S(1)}, bf16[16,3072]{1,0:T(8,128)(2,1)S(1)}, u32[]{:S(2)}, u32[]{:S(2)}) collective-permute-start(bf16[16,3072]{1,0:T(8,128)(2,1)S(1)} %slice.391), channel_id=1, source_target_pairs={{0,1},{2,0},{4,2},{6,4},{7,6},{5,7},{3,5},{1,3},{8,9},{10,8},{12,1... | collective-permute-start | bytes 294920 | tf_op jit(solution)/shard_map/ppermute | solution.py:65
  49.0 1.4 copy-start.2
  49.1 3.2 %collective-permute-start.8 = (bf16[128,3072]{1,0:T(8,128)(2,1)S(1)}, bf16[128,3072]{1,0:T(8,128)(2,1)S(1)}, u32[]{:S(2)}, u32[]{:S(2)}) collective-permute-start(bf16[128,3072]{1,0:T(8,128)(2,1)S(1)} %bitcast.151), channel_id=1, source_target_pairs={{0,8},{1,9},{2,10},{3,11},{4,12},{5,13},{6,14},{7,15},{16,24},{17,... | collective-permute-start | bytes 2359304 | tf_op jit(solution)/shard_map/ppermute | solution.py:14
  71.5 7.5 %collective-permute-start.9 = (bf16[16,3072]{1,0:T(8,128)(2,1)S(1)}, bf16[16,3072]{1,0:T(8,128)(2,1)S(1)}, u32[]{:S(2)}, u32[]{:S(2)}) collective-permute-start(bf16[16,3072]{1,0:T(8,128)(2,1)S(1)} %get-tuple-element.121), channel_id=1, source_target_pairs={{0,2},{2,4},{4,6},{6,7},{7,5},{5,3},{3,1},{1,0},{8,10},{10,12},{12... | collective-permute-start | bytes 294920 | tf_op jit(solution)/shard_map/ppermute | solution.py:108
  74.1 5.5 %collective-permute-start.13 = (bf16[16,3072]{1,0:T(8,128)(2,1)S(1)}, bf16[16,3072]{1,0:T(8,128)(2,1)S(1)}, u32[]{:S(2)}, u32[]{:S(2)}) collective-permute-start(bf16[16,3072]{1,0:T(8,128)(2,1)S(1)} %get-tuple-element.122), channel_id=1, source_target_pairs={{0,1},{2,0},{4,2},{6,4},{7,6},{5,7},{3,5},{1,3},{8,9},{10,8},{12,1... | collective-permute-start | bytes 294920 | tf_op jit(solution)/shard_map/ppermute | solution.py:108
  79.0 6.7 %collective-permute-start.10 = (bf16[32,3072]{1,0:T(8,128)(2,1)S(1)}, bf16[32,3072]{1,0:T(8,128)(2,1)S(1)}, u32[]{:S(2)}, u32[]{:S(2)}) collective-permute-start(bf16[32,3072]{1,0:T(8,128)(2,1)S(1)} %convert_element_type.317), channel_id=1, source_target_pairs={{0,2},{2,4},{4,6},{6,7},{7,5},{5,3},{3,1},{1,0},{8,10},{10,12},{12... | collective-permute-start | bytes 589832 | tf_op jit(solution)/shard_map/ppermute | solution.py:108
  79.7 6.7 %collective-permute-start.14 = (bf16[32,3072]{1,0:T(8,128)(2,1)S(1)}, bf16[32,3072]{1,0:T(8,128)(2,1)S(1)}, u32[]{:S(2)}, u32[]{:S(2)}) collective-permute-start(bf16[32,3072]{1,0:T(8,128)(2,1)S(1)} %convert_element_type.327), channel_id=1, source_target_pairs={{0,1},{2,0},{4,2},{6,4},{7,6},{5,7},{3,5},{1,3},{8,9},{10,8},{12,1... | collective-permute-start | bytes 589832 | tf_op jit(solution)/shard_map/ppermute | solution.py:108
  85.7 5.8 %collective-permute-start.11 = (bf16[32,3072]{1,0:T(8,128)(2,1)S(1)}, bf16[32,3072]{1,0:T(8,128)(2,1)S(1)}, u32[]{:S(2)}, u32[]{:S(2)}) collective-permute-start(bf16[32,3072]{1,0:T(8,128)(2,1)S(1)} %add_convert_fusion.14), channel_id=1, source_target_pairs={{0,2},{2,4},{4,6},{6,7},{7,5},{5,3},{3,1},{1,0},{8,10},{10,12},{12... | collective-permute-start | bytes 589832 | tf_op jit(solution)/shard_map/ppermute | solution.py:108
  91.6 6.4 %collective-permute-start.15 = (bf16[32,3072]{1,0:T(8,128)(2,1)S(1)}, bf16[32,3072]{1,0:T(8,128)(2,1)S(1)}, u32[]{:S(2)}, u32[]{:S(2)}) collective-permute-start(bf16[32,3072]{1,0:T(8,128)(2,1)S(1)} %get-tuple-element.114), channel_id=1, source_target_pairs={{0,1},{2,0},{4,2},{6,4},{7,6},{5,7},{3,5},{1,3},{8,9},{10,8},{12,1... | collective-permute-start | bytes 589832 | tf_op jit(solution)/shard_map/ppermute | solution.py:108
  93.1 6.7 %collective-permute-start.12 = (bf16[32,3072]{1,0:T(8,128)(2,1)S(1)}, bf16[32,3072]{1,0:T(8,128)(2,1)S(1)}, u32[]{:S(2)}, u32[]{:S(2)}) collective-permute-start(bf16[32,3072]{1,0:T(8,128)(2,1)S(1)} %get-tuple-element.113), channel_id=1, source_target_pairs={{0,2},{2,4},{4,6},{6,7},{7,5},{5,3},{3,1},{1,0},{8,10},{10,12},{12... | collective-permute-start | bytes 589832 | tf_op jit(solution)/shard_map/ppermute | solution.py:108
  98.1 6.9 %collective-permute-start.16 = (bf16[32,3072]{1,0:T(8,128)(2,1)S(1)}, bf16[32,3072]{1,0:T(8,128)(2,1)S(1)}, u32[]{:S(2)}, u32[]{:S(2)}) collective-permute-start(bf16[32,3072]{1,0:T(8,128)(2,1)S(1)} %add_convert_fusion.11), channel_id=1, source_target_pairs={{0,1},{2,0},{4,2},{6,4},{7,6},{5,7},{3,5},{1,3},{8,9},{10,8},{12,1... | collective-permute-start | bytes 589832 | tf_op jit(solution)/shard_map/ppermute | solution.py:108
  105.7 6.8 %collective-permute-start.17 = (bf16[32,3072]{1,0:T(8,128)(2,1)S(1)}, bf16[32,3072]{1,0:T(8,128)(2,1)S(1)}, u32[]{:S(2)}, u32[]{:S(2)}) collective-permute-start(bf16[32,3072]{1,0:T(8,128)(2,1)S(1)} %get-tuple-element.98), channel_id=1, source_target_pairs={{0,1},{2,0},{4,2},{6,4},{7,6},{5,7},{3,5},{1,3},{8,9},{10,8},{12,1... | collective-permute-start | bytes 589832 | tf_op jit(solution)/shard_map/ppermute | solution.py:59
  107.7 6.5 %collective-permute-start.20 = (bf16[32,3072]{1,0:T(8,128)(2,1)S(1)}, bf16[32,3072]{1,0:T(8,128)(2,1)S(1)}, u32[]{:S(2)}, u32[]{:S(2)}) collective-permute-start(bf16[32,3072]{1,0:T(8,128)(2,1)S(1)} %get-tuple-element.98), channel_id=1, source_target_pairs={{0,2},{2,4},{4,6},{6,7},{7,5},{5,3},{3,1},{1,0},{8,10},{10,12},{12... | collective-permute-start | bytes 589832 | tf_op jit(solution)/shard_map/ppermute | solution.py:58
  112.5 5.9 %collective-permute-start.18 = (bf16[32,3072]{1,0:T(8,128)(2,1)S(1)}, bf16[32,3072]{1,0:T(8,128)(2,1)S(1)}, u32[]{:S(2)}, u32[]{:S(2)}) collective-permute-start(bf16[32,3072]{1,0:T(8,128)(2,1)S(1)} %collective-permute-done.17), channel_id=1, source_target_pairs={{0,1},{2,0},{4,2},{6,4},{7,6},{5,7},{3,5},{1,3},{8,9},{10,8},{12,1... | collective-permute-start | bytes 589832 | tf_op jit(solution)/shard_map/ppermute | solution.py:71
  114.2 5.7 %collective-permute-start.21 = (bf16[32,3072]{1,0:T(8,128)(2,1)S(1)}, bf16[32,3072]{1,0:T(8,128)(2,1)S(1)}, u32[]{:S(2)}, u32[]{:S(2)}) collective-permute-start(bf16[32,3072]{1,0:T(8,128)(2,1)S(1)} %collective-permute-done.20), channel_id=1, source_target_pairs={{0,2},{2,4},{4,6},{6,7},{7,5},{5,3},{3,1},{1,0},{8,10},{10,12},{12... | collective-permute-start | bytes 589832 | tf_op jit(solution)/shard_map/ppermute | solution.py:68
  118.5 5.7 %collective-permute-start.19 = (bf16[32,3072]{1,0:T(8,128)(2,1)S(1)}, bf16[32,3072]{1,0:T(8,128)(2,1)S(1)}, u32[]{:S(2)}, u32[]{:S(2)}) collective-permute-start(bf16[32,3072]{1,0:T(8,128)(2,1)S(1)} %collective-permute-done.18), channel_id=1, source_target_pairs={{0,1},{2,0},{4,2},{6,4},{7,6},{5,7},{3,5},{1,3},{8,9},{10,8},{12,1... | collective-permute-start | bytes 589832 | tf_op jit(solution)/shard_map/ppermute | solution.py:71
  119.9 5.7 %collective-permute-start.22 = (bf16[32,3072]{1,0:T(8,128)(2,1)S(1)}, bf16[32,3072]{1,0:T(8,128)(2,1)S(1)}, u32[]{:S(2)}, u32[]{:S(2)}) collective-permute-start(bf16[32,3072]{1,0:T(8,128)(2,1)S(1)} %collective-permute-done.21), channel_id=1, source_target_pairs={{0,2},{2,4},{4,6},{6,7},{7,5},{5,3},{3,1},{1,0},{8,10},{10,12},{12... | collective-permute-start | bytes 589832 | tf_op jit(solution)/shard_map/ppermute | solution.py:68
  124.2 4.7 %collective-permute-start.24 = (bf16[16,3072]{1,0:T(8,128)(2,1)S(1)}, bf16[16,3072]{1,0:T(8,128)(2,1)S(1)}, u32[]{:S(2)}, u32[]{:S(2)}) collective-permute-start(bf16[16,3072]{1,0:T(8,128)(2,1)S(1)} %slice.406), channel_id=1, source_target_pairs={{0,1},{2,0},{4,2},{6,4},{7,6},{5,7},{3,5},{1,3},{8,9},{10,8},{12,1... | collective-permute-start | bytes 294920 | tf_op jit(solution)/shard_map/ppermute | solution.py:65
  125.6 4.7 %collective-permute-start.23 = (bf16[16,3072]{1,0:T(8,128)(2,1)S(1)}, bf16[16,3072]{1,0:T(8,128)(2,1)S(1)}, u32[]{:S(2)}, u32[]{:S(2)}) collective-permute-start(bf16[16,3072]{1,0:T(8,128)(2,1)S(1)} %slice.405), channel_id=1, source_target_pairs={{0,2},{2,4},{4,6},{6,7},{7,5},{5,3},{3,1},{1,0},{8,10},{10,12},{12... | collective-permute-start | bytes 294920 | tf_op jit(solution)/shard_map/ppermute | solution.py:64
  135.2 4.1 %collective-permute-start.25 = (bf16[128,3072]{1,0:T(8,128)(2,1)S(1)}, bf16[128,3072]{1,0:T(8,128)(2,1)}, u32[]{:S(2)}, u32[]{:S(2)}) collective-permute-start(bf16[128,3072]{1,0:T(8,128)(2,1)S(1)} %bitcast.150), channel_id=1, source_target_pairs={{0,8},{1,9},{2,10},{3,11},{4,12},{5,13},{6,14},{7,15},{16,24},{17,... | collective-permute-start | bytes 2359304 | tf_op jit(solution)/shard_map/ppermute | solution.py:14
  159.1 4.8 %collective-permute-start.26 = (bf16[16,3072]{1,0:T(8,128)(2,1)S(1)}, bf16[16,3072]{1,0:T(8,128)(2,1)S(1)}, u32[]{:S(2)}, u32[]{:S(2)}) collective-permute-start(bf16[16,3072]{1,0:T(8,128)(2,1)S(1)} %get-tuple-element.119), channel_id=1, source_target_pairs={{0,2},{2,4},{4,6},{6,7},{7,5},{5,3},{3,1},{1,0},{8,10},{10,12},{12... | collective-permute-start | bytes 294920 | tf_op jit(solution)/shard_map/ppermute | solution.py:108
  159.8 4.9 %collective-permute-start.30 = (bf16[16,3072]{1,0:T(8,128)(2,1)S(1)}, bf16[16,3072]{1,0:T(8,128)(2,1)S(1)}, u32[]{:S(2)}, u32[]{:S(2)}) collective-permute-start(bf16[16,3072]{1,0:T(8,128)(2,1)S(1)} %get-tuple-element.120), channel_id=1, source_target_pairs={{0,1},{2,0},{4,2},{6,4},{7,6},{5,7},{3,5},{1,3},{8,9},{10,8},{12,1... | collective-permute-start | bytes 294920 | tf_op jit(solution)/shard_map/ppermute | solution.py:108
  164.0 5.9 %collective-permute-start.27 = (bf16[32,3072]{1,0:T(8,128)(2,1)S(1)}, bf16[32,3072]{1,0:T(8,128)(2,1)S(1)}, u32[]{:S(2)}, u32[]{:S(2)}) collective-permute-start(bf16[32,3072]{1,0:T(8,128)(2,1)S(1)} %convert_element_type.342), channel_id=1, source_target_pairs={{0,2},{2,4},{4,6},{6,7},{7,5},{5,3},{3,1},{1,0},{8,10},{10,12},{12... | collective-permute-start | bytes 589832 | tf_op jit(solution)/shard_map/ppermute | solution.py:108
  164.7 5.9 %collective-permute-start.31 = (bf16[32,3072]{1,0:T(8,128)(2,1)S(1)}, bf16[32,3072]{1,0:T(8,128)(2,1)S(1)}, u32[]{:S(2)}, u32[]{:S(2)}) collective-permute-start(bf16[32,3072]{1,0:T(8,128)(2,1)S(1)} %convert_element_type.352), channel_id=1, source_target_pairs={{0,1},{2,0},{4,2},{6,4},{7,6},{5,7},{3,5},{1,3},{8,9},{10,8},{12,1... | collective-permute-start | bytes 589832 | tf_op jit(solution)/shard_map/ppermute | solution.py:108
  170.0 5.7 %collective-permute-start.28 = (bf16[32,3072]{1,0:T(8,128)(2,1)S(1)}, bf16[32,3072]{1,0:T(8,128)(2,1)S(1)}, u32[]{:S(2)}, u32[]{:S(2)}) collective-permute-start(bf16[32,3072]{1,0:T(8,128)(2,1)S(1)} %add_convert_fusion.9), channel_id=1, source_target_pairs={{0,2},{2,4},{4,6},{6,7},{7,5},{5,3},{3,1},{1,0},{8,10},{10,12},{12... | collective-permute-start | bytes 589832 | tf_op jit(solution)/shard_map/ppermute | solution.py:108
  175.8 7.3 %collective-permute-start.32 = (bf16[32,3072]{1,0:T(8,128)(2,1)S(1)}, bf16[32,3072]{1,0:T(8,128)(2,1)S(1)}, u32[]{:S(2)}, u32[]{:S(2)}) collective-permute-start(bf16[32,3072]{1,0:T(8,128)(2,1)S(1)} %get-tuple-element.110), channel_id=1, source_target_pairs={{0,1},{2,0},{4,2},{6,4},{7,6},{5,7},{3,5},{1,3},{8,9},{10,8},{12,1... | collective-permute-start | bytes 589832 | tf_op jit(solution)/shard_map/ppermute | solution.py:108
  177.2 7.3 %collective-permute-start.29 = (bf16[32,3072]{1,0:T(8,128)(2,1)S(1)}, bf16[32,3072]{1,0:T(8,128)(2,1)S(1)}, u32[]{:S(2)}, u32[]{:S(2)}) collective-permute-start(bf16[32,3072]{1,0:T(8,128)(2,1)S(1)} %get-tuple-element.109), channel_id=1, source_target_pairs={{0,2},{2,4},{4,6},{6,7},{7,5},{5,3},{3,1},{1,0},{8,10},{10,12},{12... | collective-permute-start | bytes 589832 | tf_op jit(solution)/shard_map/ppermute | solution.py:108
  183.1 7.7 %collective-permute-start.33 = (bf16[32,3072]{1,0:T(8,128)(2,1)S(1)}, bf16[32,3072]{1,0:T(8,128)(2,1)S(1)}, u32[]{:S(2)}, u32[]{:S(2)}) collective-permute-start(bf16[32,3072]{1,0:T(8,128)(2,1)S(1)} %add_convert_fusion.6), channel_id=1, source_target_pairs={{0,1},{2,0},{4,2},{6,4},{7,6},{5,7},{3,5},{1,3},{8,9},{10,8},{12,1... | collective-permute-start | bytes 589832 | tf_op jit(solution)/shard_map/ppermute | solution.py:108
  191.6 6.1 %collective-permute-start.34 = (bf16[32,3072]{1,0:T(8,128)(2,1)S(1)}, bf16[32,3072]{1,0:T(8,128)(2,1)S(1)}, u32[]{:S(2)}, u32[]{:S(2)}) collective-permute-start(bf16[32,3072]{1,0:T(8,128)(2,1)S(1)} %get-tuple-element.96), channel_id=1, source_target_pairs={{0,1},{2,0},{4,2},{6,4},{7,6},{5,7},{3,5},{1,3},{8,9},{10,8},{12,1... | collective-permute-start | bytes 589832 | tf_op jit(solution)/shard_map/ppermute | solution.py:59
  193.0 6.1 %collective-permute-start.37 = (bf16[32,3072]{1,0:T(8,128)(2,1)S(1)}, bf16[32,3072]{1,0:T(8,128)(2,1)S(1)}, u32[]{:S(2)}, u32[]{:S(2)}) collective-permute-start(bf16[32,3072]{1,0:T(8,128)(2,1)S(1)} %get-tuple-element.96), channel_id=1, source_target_pairs={{0,2},{2,4},{4,6},{6,7},{7,5},{5,3},{3,1},{1,0},{8,10},{10,12},{12... | collective-permute-start | bytes 589832 | tf_op jit(solution)/shard_map/ppermute | solution.py:58
  197.7 5.7 %collective-permute-start.35 = (bf16[32,3072]{1,0:T(8,128)(2,1)S(1)}, bf16[32,3072]{1,0:T(8,128)(2,1)S(1)}, u32[]{:S(2)}, u32[]{:S(2)}) collective-permute-start(bf16[32,3072]{1,0:T(8,128)(2,1)S(1)} %collective-permute-done.34), channel_id=1, source_target_pairs={{0,1},{2,0},{4,2},{6,4},{7,6},{5,7},{3,5},{1,3},{8,9},{10,8},{12,1... | collective-permute-start | bytes 589832 | tf_op jit(solution)/shard_map/ppermute | solution.py:71
  199.2 5.7 %collective-permute-start.38 = (bf16[32,3072]{1,0:T(8,128)(2,1)S(1)}, bf16[32,3072]{1,0:T(8,128)(2,1)S(1)}, u32[]{:S(2)}, u32[]{:S(2)}) collective-permute-start(bf16[32,3072]{1,0:T(8,128)(2,1)S(1)} %collective-permute-done.37), channel_id=1, source_target_pairs={{0,2},{2,4},{4,6},{6,7},{7,5},{5,3},{3,1},{1,0},{8,10},{10,12},{12... | collective-permute-start | bytes 589832 | tf_op jit(solution)/shard_map/ppermute | solution.py:68
  203.4 5.7 %collective-permute-start.36 = (bf16[32,3072]{1,0:T(8,128)(2,1)S(1)}, bf16[32,3072]{1,0:T(8,128)(2,1)S(1)}, u32[]{:S(2)}, u32[]{:S(2)}) collective-permute-start(bf16[32,3072]{1,0:T(8,128)(2,1)S(1)} %collective-permute-done.35), channel_id=1, source_target_pairs={{0,1},{2,0},{4,2},{6,4},{7,6},{5,7},{3,5},{1,3},{8,9},{10,8},{12,1... | collective-permute-start | bytes 589832 | tf_op jit(solution)/shard_map/ppermute | solution.py:71
  204.8 5.7 %collective-permute-start.39 = (bf16[32,3072]{1,0:T(8,128)(2,1)S(1)}, bf16[32,3072]{1,0:T(8,128)(2,1)S(1)}, u32[]{:S(2)}, u32[]{:S(2)}) collective-permute-start(bf16[32,3072]{1,0:T(8,128)(2,1)S(1)} %collective-permute-done.38), channel_id=1, source_target_pairs={{0,2},{2,4},{4,6},{6,7},{7,5},{5,3},{3,1},{1,0},{8,10},{10,12},{12... | collective-permute-start | bytes 589832 | tf_op jit(solution)/shard_map/ppermute | solution.py:68
  209.1 4.7 %collective-permute-start.41 = (bf16[16,3072]{1,0:T(8,128)(2,1)S(1)}, bf16[16,3072]{1,0:T(8,128)(2,1)S(1)}, u32[]{:S(2)}, u32[]{:S(2)}) collective-permute-start(bf16[16,3072]{1,0:T(8,128)(2,1)S(1)} %slice.421), channel_id=1, source_target_pairs={{0,1},{2,0},{4,2},{6,4},{7,6},{5,7},{3,5},{1,3},{8,9},{10,8},{12,1... | collective-permute-start | bytes 294920 | tf_op jit(solution)/shard_map/ppermute | solution.py:65
  210.6 4.7 %collective-permute-start.40 = (bf16[16,3072]{1,0:T(8,128)(2,1)S(1)}, bf16[16,3072]{1,0:T(8,128)(2,1)S(1)}, u32[]{:S(2)}, u32[]{:S(2)}) collective-permute-start(bf16[16,3072]{1,0:T(8,128)(2,1)S(1)} %slice.420), channel_id=1, source_target_pairs={{0,2},{2,4},{4,6},{6,7},{7,5},{5,3},{3,1},{1,0},{8,10},{10,12},{12... | collective-permute-start | bytes 294920 | tf_op jit(solution)/shard_map/ppermute | solution.py:64
  220.5 1.7 copy-start.3
  223.8 2.9 %collective-permute-start.42 = (bf16[256,128]{1,0:T(8,128)(2,1)S(1)}, bf16[256,128]{1,0:T(8,128)(2,1)S(1)}, u32[]{:S(2)}, u32[]{:S(2)}) collective-permute-start(bf16[256,128]{1,0:T(8,128)(2,1)S(1)} %convolution_convert_fusion.7), channel_id=1, source_target_pairs={{0,8},{1,9},{2,10},{3,11},{4,12},{5,13},{6,14},{7,15},{16,24},{17,... | collective-permute-start | bytes 196616 | tf_op jit(solution)/shard_map/ppermute | solution.py:14
  225.1 2.2 collective-permute-start.43
  229.8 4.7 %collective-permute-start.44 = (bf16[16,3072]{1,0:T(8,128)(2,1)S(1)}, bf16[16,3072]{1,0:T(8,128)(2,1)S(1)}, u32[]{:S(2)}, u32[]{:S(2)}) collective-permute-start(bf16[16,3072]{1,0:T(8,128)(2,1)S(1)} %get-tuple-element.117), channel_id=1, source_target_pairs={{0,2},{2,4},{4,6},{6,7},{7,5},{5,3},{3,1},{1,0},{8,10},{10,12},{12... | collective-permute-start | bytes 294920 | tf_op jit(solution)/shard_map/ppermute | solution.py:108
  230.5 4.7 %collective-permute-start.48 = (bf16[16,3072]{1,0:T(8,128)(2,1)S(1)}, bf16[16,3072]{1,0:T(8,128)(2,1)S(1)}, u32[]{:S(2)}, u32[]{:S(2)}) collective-permute-start(bf16[16,3072]{1,0:T(8,128)(2,1)S(1)} %get-tuple-element.118), channel_id=1, source_target_pairs={{0,1},{2,0},{4,2},{6,4},{7,6},{5,7},{3,5},{1,3},{8,9},{10,8},{12,1... | collective-permute-start | bytes 294920 | tf_op jit(solution)/shard_map/ppermute | solution.py:108
  234.6 7.7 %collective-permute-start.45 = (bf16[32,3072]{1,0:T(8,128)(2,1)S(1)}, bf16[32,3072]{1,0:T(8,128)(2,1)S(1)}, u32[]{:S(2)}, u32[]{:S(2)}) collective-permute-start(bf16[32,3072]{1,0:T(8,128)(2,1)S(1)} %convert_element_type.376), channel_id=1, source_target_pairs={{0,2},{2,4},{4,6},{6,7},{7,5},{5,3},{3,1},{1,0},{8,10},{10,12},{12... | collective-permute-start | bytes 589832 | tf_op jit(solution)/shard_map/ppermute | solution.py:108
  235.3 7.7 %collective-permute-start.49 = (bf16[32,3072]{1,0:T(8,128)(2,1)S(1)}, bf16[32,3072]{1,0:T(8,128)(2,1)S(1)}, u32[]{:S(2)}, u32[]{:S(2)}) collective-permute-start(bf16[32,3072]{1,0:T(8,128)(2,1)S(1)} %convert_element_type.386), channel_id=1, source_target_pairs={{0,1},{2,0},{4,2},{6,4},{7,6},{5,7},{3,5},{1,3},{8,9},{10,8},{12,1... | collective-permute-start | bytes 589832 | tf_op jit(solution)/shard_map/ppermute | solution.py:108
  242.4 7.1 %collective-permute-start.46 = (bf16[32,3072]{1,0:T(8,128)(2,1)S(1)}, bf16[32,3072]{1,0:T(8,128)(2,1)S(1)}, u32[]{:S(2)}, u32[]{:S(2)}) collective-permute-start(bf16[32,3072]{1,0:T(8,128)(2,1)S(1)} %add_convert_fusion.4), channel_id=1, source_target_pairs={{0,2},{2,4},{4,6},{6,7},{7,5},{5,3},{3,1},{1,0},{8,10},{10,12},{12... | collective-permute-start | bytes 589832 | tf_op jit(solution)/shard_map/ppermute | solution.py:108
  249.5 6.3 %collective-permute-start.50 = (bf16[32,3072]{1,0:T(8,128)(2,1)S(1)}, bf16[32,3072]{1,0:T(8,128)(2,1)S(1)}, u32[]{:S(2)}, u32[]{:S(2)}) collective-permute-start(bf16[32,3072]{1,0:T(8,128)(2,1)S(1)} %get-tuple-element.106), channel_id=1, source_target_pairs={{0,1},{2,0},{4,2},{6,4},{7,6},{5,7},{3,5},{1,3},{8,9},{10,8},{12,1... | collective-permute-start | bytes 589832 | tf_op jit(solution)/shard_map/ppermute | solution.py:108
  250.3 6.6 %collective-permute-start.47 = (bf16[32,3072]{1,0:T(8,128)(2,1)S(1)}, bf16[32,3072]{1,0:T(8,128)(2,1)S(1)}, u32[]{:S(2)}, u32[]{:S(2)}) collective-permute-start(bf16[32,3072]{1,0:T(8,128)(2,1)S(1)} %get-tuple-element.105), channel_id=1, source_target_pairs={{0,2},{2,4},{4,6},{6,7},{7,5},{5,3},{3,1},{1,0},{8,10},{10,12},{12... | collective-permute-start | bytes 589832 | tf_op jit(solution)/shard_map/ppermute | solution.py:108
  255.9 5.7 %collective-permute-start.51 = (bf16[32,3072]{1,0:T(8,128)(2,1)S(1)}, bf16[32,3072]{1,0:T(8,128)(2,1)S(1)}, u32[]{:S(2)}, u32[]{:S(2)}) collective-permute-start(bf16[32,3072]{1,0:T(8,128)(2,1)S(1)} %add_convert_fusion.1), channel_id=1, source_target_pairs={{0,1},{2,0},{4,2},{6,4},{7,6},{5,7},{3,5},{1,3},{8,9},{10,8},{12,1... | collective-permute-start | bytes 589832 | tf_op jit(solution)/shard_map/ppermute | solution.py:108

commit v16 on v15

--- a/solution.py
+++ b/solution.py
@@ -40,7 +40,7 @@
     return forward, backward
 
 
-def ring_gather(value, axis, tables, direct=1):
+def ring_gather(value, axis, tables, direct=1, tail_rows=0):
     length = lax.axis_size(axis)
     forward, backward = ring_pairs(length)
     order = ring_order(length)
@@ -71,7 +71,12 @@
             bwd = lax.ppermute(bwd, axis, backward)
             pieces[k] = bwd
     stacked = jnp.stack(pieces)
-    return jnp.take(stacked, tables[1], axis=0, mode="clip").reshape((length * rows,) + value.shape[1:])
+    whole = jnp.take(stacked, tables[1], axis=0, mode="clip").reshape((length * rows,) + value.shape[1:])
+    if not tail_rows:
+        return whole
+    tail_blocks = tail_rows // rows
+    tail = jnp.take(stacked, tables[1][length - tail_blocks :], axis=0, mode="clip")
+    return whole, tail.reshape((tail_rows,) + value.shape[1:])
 
 
 def ring_ordered(rows_in, axis, tables):
@@ -154,14 +159,14 @@
         out_ref[...] = (jnp.tanh(filt_acc[...]) * jax.nn.sigmoid(gate_acc[...])).astype(out_ref.dtype)
 
 
-def convolution_gate(state, gain, conv_by_half, layer_idx, dilation_factor):
+def convolution_gate(state, tail, gain, conv_by_half, layer_idx, dilation_factor):
     hidden = state
     all_rows = hidden.shape[0]
     width = hidden.shape[1]
     taps = conv_by_half.shape[1]
     own_width = conv_by_half.shape[-1]
     border_rows = 2 * LARGEST_DILATION
-    before = shifted(hidden[all_rows - border_rows :], "blk", 1)
+    before = shifted(tail, "blk", 1)
     padded = jnp.concatenate([before, hidden], axis=0)
     slabs = jnp.stack(
         [
@@ -261,15 +266,19 @@
     layers = w_conv.shape[0]
     share = stream
     tables = ring_tables("head")
-    state = ring_gather(stream, "head", tables, direct=3)
+    border_rows = 2 * LARGEST_DILATION
+    state, tail = ring_gather(stream, "head", tables, direct=2, tail_rows=border_rows)
     conv_by_half = jnp.transpose(w_conv, (0, 1, 3, 2, 4))
     for layer_idx in range(layers):
         gated = convolution_gate(
-            state, gains[layer_idx], conv_by_half, layer_idx, dilations[layer_idx]
+            state, tail, gains[layer_idx], conv_by_half, layer_idx, dilations[layer_idx]
         )
         summed = conv_share(gated, w_mix[layer_idx], tok_rows, tables)
         share = (share.astype(jnp.float32) + summed).astype(jnp.bfloat16)
-        state = ring_gather(share, "head", tables)
+        if layer_idx + 1 < layers:
+            state, tail = ring_gather(share, "head", tables, tail_rows=border_rows)
+        else:
+            state = ring_gather(share, "head", tables)
     all_rows = state.shape[0]
     attn_in = normed(state, gains[layers])
     qkv_parts = jnp.transpose(w_qkv[:, :, 0, :], (1, 0, 2))

time: 263 us -> 257 us (0.977)
  local copies, waits for them, and re-layouts: 48.2 us -> 41.2 us
  waiting for transfers between devices: 96.6 us -> 101 us
    unnamed x25 -> x29, local copies, waits for them, and re-layouts: 32.9 us -> 25.4 us
    ppermute x5 -> x4, starting transfers between devices: 7.97 us -> 1.02 us  [ring_gather(): lax.ppermute(value, axis, [(order[p], order[(p + k) % length]) for p in r...]
    ppermute x4 -> x5, waiting for transfers between devices: 12.1 us -> 17.3 us  [ring_gather(): bwd = lax.ppermute(bwd, axis, backward)]
    ppermute x5 -> x4, starting transfers between devices: 6.14 us -> 10.2 us  [ring_gather(): lax.ppermute(value, axis, [(order[p], order[(p - k) % length]) for p in r...]
    ppermute x4 -> x5, starting transfers between devices: 5.93 us -> 9.32 us  [ring_gather(): bwd = lax.ppermute(bwd, axis, backward)]
    ppermute x3, waiting for transfers between devices: 3.65 us -> 6.68 us  [ring_gather(): bwd = lax.ppermute(bwd[half:], axis, backward)]
    ppermute x5 -> x4, waiting for transfers between devices: 8.89 us -> 8.35 us  [ring_gather(): lax.ppermute(value, axis, [(order[p], order[(p - k) % length]) for p in r...]
  transfers between devices with their start and end apart: 52 -> 52, of which waited for: 29 -> 31; matrix products, arithmetic and copies ran while one was open for 15% -> 15% of each run, Pallas kernels for 0% -> 0%
where the time goes in v16:
time: 257 us
  waiting for transfers between devices  101 us (39%)
  starting transfers between devices  60.1 us (23%)
  local copies, waits for them, and re-layouts  41.2 us (16%)
  Pallas kernels  21.7 us (8%)
  other arithmetic  16 us (6%)
  matrix products  12.6 us (5%)
  between operations  4.44 us (2%)
    ppermute x24, waiting for transfers between devices, chain(): passed = lax.ppermute(part.astype(value.dtype), axis, pairs)  61.5 us
    unnamed x29, local copies, waits for them, and re-layouts  25.4 us
    ppermute x24, starting transfers between devices, chain(): passed = lax.ppermute(part.astype(value.dtype), axis, pairs)  25 us
    pallas_call x2, Pallas kernels, convolution_gate(): pl.pallas_call(conv_gate_kernel, out_shape=jax.ShapeDtypeStruct((all_rows...  21.7 us
    ppermute x5, waiting for transfers between devices, ring_gather(): bwd = lax.ppermute(bwd, axis, backward)  17.3 us
    another operation x4, other arithmetic, convolution_gate(): jnp.stack([lax.dynamic_slice_in_dim(padded, border_rows - tap_idx * dilat...  10.7 us
    dot_general x6, matrix products, rounded_term(): term = jnp.dot(left, right, preferred_element_type=jnp.float32)  10.4 us
    ppermute x4, starting transfers between devices, ring_gather(): lax.ppermute(value, axis, [(order[p], order[(p - k) % length]) for p in r...  10.2 us
  transfers between devices with their start and end apart: 52, of which 31 were waited for; matrix products, arithmetic and copies ran while one was open for 15% of the time, Pallas kernels for 0%

profile of v16, /device:TPU:0, one launch (start us, length us, event | category | flops | bytes accessed | tf_op | source)
XLA Modules:
  0.0 256.6 jit_solution(13792404228714959545)
XLA Ops:
  0.0 4.0 %collective-permute-start.1 = (bf16[32,3072]{1,0:T(8,128)(2,1)}, bf16[32,3072]{1,0:T(8,128)(2,1)S(1)}, u32[]{:S(2)}, u32[]{:S(2)}) collective-permute-start(bf16[32,3072]{1,0:T(8,128)(2,1)} %param.22), channel_id=1, source_target_pairs={{0,3},{2,1},{4,0},{6,2},{7,4},{5,6},{3,7},{1,5},{8,11},{10,9},{12,... | collective-permute-start | bytes 589832 | tf_op jit(solution)/shard_map/ppermute | solution.py:59
  4.0 1.6 collective-permute-start
  10.4 19.7 %copy.11 = bf16[2,3,3072,2,384]{4,2,3,1,0:T(8,128)(2,1)} copy(bf16[2,3,3072,2,384]{4,3,2,1,0:T(2,128)(2,1)} %param.25) | data formatting | bytes 56623104 | tf_op args[3]
  31.5 1.8 collective-permute-start.2
  33.7 3.7 %collective-permute-done.2 = bf16[32,3072]{1,0:T(8,128)(2,1)S(1)} collective-permute-done((bf16[32,3072]{1,0:T(8,128)(2,1)S(1)}, bf16[32,3072]{1,0:T(8,128)(2,1)S(1)}, u32[]{:S(2)}, u32[]{:S(2)}) %collective-permute-start.2) | collective-permute-done | bytes 196640 | tf_op jit(solution)/shard_map/ppermute | solution.py:71
  37.4 1.7 collective-permute-start.6
  39.6 2.5 collective-permute-done.6
  42.1 1.7 collective-permute-done.5
  44.5 2.2 collective-permute-start.8
  47.3 2.1 gather_fusion
  49.4 3.0 %fusion.23 = (bf16[1,256,3072]{2,1,0:T(8,128)(2,1)S(1)}, bf16[1,256,3072]{2,1,0:T(8,128)(2,1)S(1)}) fusion(s32[]{:T(128)S(6)} %select_n.21, bf16[256,3072]{1,0:T(8,128)(2,1)S(1)} %bitcast.143, bf16[128,3072]{1,0:T(8,128)(2,1)} %collective-permute-done.8, s32[]{:T(128)S(6)} %select_n.22), kind=kLoop, calls=%fused_computation.51 | loop fusion | flops 6291456 | bytes 5505032 | tf_op jit(solution)/shard_map/stack | solution.py:171
  52.5 2.4 pad_maximum_fusion.slab_ref
  54.9 10.8 %shard_map.82 = bf16[256,384]{1,0:T(8,128)(2,1)} custom-call(bf16[3,256,3072]{2,1,0:T(8,128)(2,1)} %pad_maximum_fusion.slab_ref, f32[1,3072]{1,0:T(1,128)} %get-tuple-element.124.gain_ref, bf16[2,3,2,3072,384]{4,3,2,1,0:T(8,128)(2,1)} %bitcast.141), custom_call_target="tpu_custom_call" | custom-call | flops 3623878656 | bytes 19070976 | tf_op jit(solution)/shard_map/pallas_call | solution.py:178
  67.2 2.2 convolution_convert_fusion.4
  69.8 1.7 collective-permute-start.13
  71.5 2.6 %convolution_convert_fusion.2 = bf16[256,3072]{1,0:T(8,128)(2,1)S(1)} fusion(bf16[256,384]{1,0:T(8,128)(2,1)S(1)} %bitcast.156, bf16[2,384,3072]{2,1,0:T(8,128)(2,1)} %param.26), kind=kOutput, calls=%fused_computation.21 | convolution fusion | flops 604766208 | bytes 4128768 | tf_op jit(solution)/shard_map/dot_general | solution.py:138
  74.8 1.7 collective-permute-start.14
  76.5 3.6 %collective-permute-done.10 = bf16[32,3072]{1,0:T(8,128)(2,1)S(1)} collective-permute-done((bf16[32,3072]{1,0:T(8,128)(2,1)S(1)}, bf16[32,3072]{1,0:T(8,128)(2,1)S(1)}, u32[]{:S(2)}, u32[]{:S(2)}) %collective-permute-start.10) | collective-permute-done | bytes 196640 | tf_op jit(solution)/shard_map/ppermute | solution.py:113
  80.6 5.3 %collective-permute-done.11 = bf16[32,3072]{1,0:T(8,128)(2,1)S(1)} collective-permute-done((bf16[32,3072]{1,0:T(8,128)(2,1)S(1)}, bf16[32,3072]{1,0:T(8,128)(2,1)S(1)}, u32[]{:S(2)}, u32[]{:S(2)}) %collective-permute-start.11) | collective-permute-done | bytes 196640 | tf_op jit(solution)/shard_map/ppermute | solution.py:113
  86.0 1.6 collective-permute-start.15
  88.1 5.4 %collective-permute-done.15 = bf16[32,3072]{1,0:T(8,128)(2,1)S(1)} collective-permute-done((bf16[32,3072]{1,0:T(8,128)(2,1)S(1)}, bf16[32,3072]{1,0:T(8,128)(2,1)S(1)}, u32[]{:S(2)}, u32[]{:S(2)}) %collective-permute-start.15) | collective-permute-done | bytes 196640 | tf_op jit(solution)/shard_map/ppermute | solution.py:113
  93.6 1.6 collective-permute-start.16
  95.2 5.1 %collective-permute-done.16 = bf16[32,3072]{1,0:T(8,128)(2,1)S(1)} collective-permute-done((bf16[32,3072]{1,0:T(8,128)(2,1)S(1)}, bf16[32,3072]{1,0:T(8,128)(2,1)S(1)}, u32[]{:S(2)}, u32[]{:S(2)}) %collective-permute-start.16) | collective-permute-done | bytes 196640 | tf_op jit(solution)/shard_map/ppermute | solution.py:113
  100.4 1.6 collective-permute-start.17
  102.5 3.6 %collective-permute-done.17 = bf16[32,3072]{1,0:T(8,128)(2,1)S(1)} collective-permute-done((bf16[32,3072]{1,0:T(8,128)(2,1)S(1)}, bf16[32,3072]{1,0:T(8,128)(2,1)S(1)}, u32[]{:S(2)}, u32[]{:S(2)}) %collective-permute-start.17) | collective-permute-done | bytes 196640 | tf_op jit(solution)/shard_map/ppermute | solution.py:59
  106.1 1.6 collective-permute-start.18
  108.2 4.4 %collective-permute-done.18 = bf16[32,3072]{1,0:T(8,128)(2,1)S(1)} collective-permute-done((bf16[32,3072]{1,0:T(8,128)(2,1)S(1)}, bf16[32,3072]{1,0:T(8,128)(2,1)S(1)}, u32[]{:S(2)}, u32[]{:S(2)}) %collective-permute-start.18) | collective-permute-done | bytes 196640 | tf_op jit(solution)/shard_map/ppermute | solution.py:71
  112.6 1.6 collective-permute-start.19
  114.6 3.6 %collective-permute-done.19 = bf16[32,3072]{1,0:T(8,128)(2,1)S(1)} collective-permute-done((bf16[32,3072]{1,0:T(8,128)(2,1)S(1)}, bf16[32,3072]{1,0:T(8,128)(2,1)S(1)}, u32[]{:S(2)}, u32[]{:S(2)}) %collective-permute-start.19) | collective-permute-done | bytes 196640 | tf_op jit(solution)/shard_map/ppermute | solution.py:71
  118.3 1.6 collective-permute-start.24
  120.4 2.5 collective-permute-done.24
  123.0 1.6 collective-permute-done.23
  125.3 2.2 collective-permute-start.25
  129.4 2.1 gather_fusion.3
  131.4 2.8 %fusion.19 = (bf16[1,256,3072]{2,1,0:T(8,128)(2,1)S(1)}, bf16[1,256,3072]{2,1,0:T(8,128)(2,1)S(1)}) fusion(s32[]{:T(128)S(6)} %select_n.23, bf16[256,3072]{1,0:T(8,128)(2,1)S(1)} %bitcast.145, bf16[128,3072]{1,0:T(8,128)(2,1)} %collective-permute-done.25, s32[]{:T(128)S(6)} %select_n.24), kind=kLoop, calls=%fused_computation.47 | loop fusion | flops 6291456 | bytes 5505032 | tf_op jit(solution)/shard_map/stack | solution.py:171
  134.3 2.4 pad_maximum_fusion.1.slab_ref
  136.7 10.8 %shard_map.83 = bf16[256,384]{1,0:T(8,128)(2,1)} custom-call(bf16[3,256,3072]{2,1,0:T(8,128)(2,1)} %pad_maximum_fusion.1.slab_ref, f32[1,3072]{1,0:T(1,128)} %get-tuple-element.125.gain_ref, bf16[2,3,2,3072,384]{4,3,2,1,0:T(8,128)(2,1)} %bitcast.142), custom_call_target="tpu_custom_call" | custom-call | flops 3623878656 | bytes 19070976 | tf_op jit(solution)/shard_map/pallas_call | solution.py:178
  149.0 2.2 convolution_convert_fusion.3
  151.7 1.6 collective-permute-start.30
  153.3 2.6 %convolution_convert_fusion.1 = bf16[256,3072]{1,0:T(8,128)(2,1)S(1)} fusion(bf16[256,384]{1,0:T(8,128)(2,1)S(1)} %bitcast.157, bf16[2,384,3072]{2,1,0:T(8,128)(2,1)} %param.26), kind=kOutput, calls=%fused_computation.20 | convolution fusion | flops 604766208 | bytes 4128768 | tf_op jit(solution)/shard_map/dot_general | solution.py:138
  156.8 1.6 collective-permute-start.31
  158.4 4.8 %collective-permute-done.27 = bf16[32,3072]{1,0:T(8,128)(2,1)S(1)} collective-permute-done((bf16[32,3072]{1,0:T(8,128)(2,1)S(1)}, bf16[32,3072]{1,0:T(8,128)(2,1)S(1)}, u32[]{:S(2)}, u32[]{:S(2)}) %collective-permute-start.27) | collective-permute-done | bytes 196640 | tf_op jit(solution)/shard_map/ppermute | solution.py:113
  163.8 6.2 %collective-permute-done.28 = bf16[32,3072]{1,0:T(8,128)(2,1)S(1)} collective-permute-done((bf16[32,3072]{1,0:T(8,128)(2,1)S(1)}, bf16[32,3072]{1,0:T(8,128)(2,1)S(1)}, u32[]{:S(2)}, u32[]{:S(2)}) %collective-permute-start.28) | collective-permute-done | bytes 196640 | tf_op jit(solution)/shard_map/ppermute | solution.py:113
  172.2 3.6 %collective-permute-done.32 = bf16[32,3072]{1,0:T(8,128)(2,1)S(1)} collective-permute-done((bf16[32,3072]{1,0:T(8,128)(2,1)S(1)}, bf16[32,3072]{1,0:T(8,128)(2,1)S(1)}, u32[]{:S(2)}, u32[]{:S(2)}) %collective-permute-start.32) | collective-permute-done | bytes 196640 | tf_op jit(solution)/shard_map/ppermute | solution.py:113
  175.9 2.0 collective-permute-start.33
  178.2 3.6 %collective-permute-done.33 = bf16[32,3072]{1,0:T(8,128)(2,1)S(1)} collective-permute-done((bf16[32,3072]{1,0:T(8,128)(2,1)S(1)}, bf16[32,3072]{1,0:T(8,128)(2,1)S(1)}, u32[]{:S(2)}, u32[]{:S(2)}) %collective-permute-start.33) | collective-permute-done | bytes 196640 | tf_op jit(solution)/shard_map/ppermute | solution.py:113
  182.6 3.0 %collective-permute-start.34 = (bf16[32,3072]{1,0:T(8,128)(2,1)S(1)}, bf16[32,3072]{1,0:T(8,128)(2,1)S(1)}, u32[]{:S(2)}, u32[]{:S(2)}) collective-permute-start(bf16[32,3072]{1,0:T(8,128)(2,1)S(1)} %get-tuple-element.96), channel_id=1, source_target_pairs={{0,1},{2,0},{4,2},{6,4},{7,6},{5,7},{3,5},{1,3},{8,9},{10,8},{12,1... | collective-permute-start | bytes 589832 | tf_op jit(solution)/shard_map/ppermute | solution.py:59
  185.6 4.7 %collective-permute-done.34 = bf16[32,3072]{1,0:T(8,128)(2,1)S(1)} collective-permute-done((bf16[32,3072]{1,0:T(8,128)(2,1)S(1)}, bf16[32,3072]{1,0:T(8,128)(2,1)S(1)}, u32[]{:S(2)}, u32[]{:S(2)}) %collective-permute-start.34) | collective-permute-done | bytes 196640 | tf_op jit(solution)/shard_map/ppermute | solution.py:59
  190.3 2.3 collective-permute-start.35
  193.5 2.7 %collective-permute-done.35 = bf16[32,3072]{1,0:T(8,128)(2,1)S(1)} collective-permute-done((bf16[32,3072]{1,0:T(8,128)(2,1)S(1)}, bf16[32,3072]{1,0:T(8,128)(2,1)S(1)}, u32[]{:S(2)}, u32[]{:S(2)}) %collective-permute-start.35) | collective-permute-done | bytes 196640 | tf_op jit(solution)/shard_map/ppermute | solution.py:71
  196.2 2.1 collective-permute-start.36
  199.1 2.8 %collective-permute-done.36 = bf16[32,3072]{1,0:T(8,128)(2,1)S(1)} collective-permute-done((bf16[32,3072]{1,0:T(8,128)(2,1)S(1)}, bf16[32,3072]{1,0:T(8,128)(2,1)S(1)}, u32[]{:S(2)}, u32[]{:S(2)}) %collective-permute-start.36) | collective-permute-done | bytes 196640 | tf_op jit(solution)/shard_map/ppermute | solution.py:71
  201.9 2.1 collective-permute-start.41
  204.9 1.7 collective-permute-done.41
  206.5 2.3 collective-permute-done.40
  211.6 2.1 gather_fusion.6
  223.5 2.1 collective-permute-start.48
  226.2 1.9 collective-permute-done.44
  228.3 2.1 collective-permute-start.49
  230.4 5.3 %collective-permute-done.45 = bf16[32,3072]{1,0:T(8,128)(2,1)S(1)} collective-permute-done((bf16[32,3072]{1,0:T(8,128)(2,1)S(1)}, bf16[32,3072]{1,0:T(8,128)(2,1)S(1)}, u32[]{:S(2)}, u32[]{:S(2)}) %collective-permute-start.45) | collective-permute-done | bytes 196640 | tf_op jit(solution)/shard_map/ppermute | solution.py:113
  235.9 7.4 %collective-permute-done.46 = bf16[32,3072]{1,0:T(8,128)(2,1)S(1)} collective-permute-done((bf16[32,3072]{1,0:T(8,128)(2,1)S(1)}, bf16[32,3072]{1,0:T(8,128)(2,1)S(1)}, u32[]{:S(2)}, u32[]{:S(2)}) %collective-permute-start.46) | collective-permute-done | bytes 196640 | tf_op jit(solution)/shard_map/ppermute | solution.py:113
  243.4 1.8 collective-permute-start.50
  245.5 4.5 %collective-permute-done.50 = bf16[32,3072]{1,0:T(8,128)(2,1)S(1)} collective-permute-done((bf16[32,3072]{1,0:T(8,128)(2,1)S(1)}, bf16[32,3072]{1,0:T(8,128)(2,1)S(1)}, u32[]{:S(2)}, u32[]{:S(2)}) %collective-permute-start.50) | collective-permute-done | bytes 196640 | tf_op jit(solution)/shard_map/ppermute | solution.py:113
  251.5 4.2 %collective-permute-done.51 = bf16[32,3072]{1,0:T(8,128)(2,1)S(1)} collective-permute-done((bf16[32,3072]{1,0:T(8,128)(2,1)S(1)}, bf16[32,3072]{1,0:T(8,128)(2,1)S(1)}, u32[]{:S(2)}, u32[]{:S(2)}) %collective-permute-start.51) | collective-permute-done | bytes 196640 | tf_op jit(solution)/shard_map/ppermute | solution.py:113
  (152 shorter events, 38.7 us)
Async XLA Ops:
  0.0 223.2 %copy-start = (bf16[1,128,3072]{2,1,0:T(8,128)(2,1)S(1)}, bf16[1,128,3072]{2,1,0:T(8,128)(2,1)}, u32[]{:S(2)}) copy-start(bf16[1,128,3072]{2,1,0:T(8,128)(2,1)} %param.28) | copy-start | bytes 2359300
  0.0 31.5 %collective-permute-start.1 = (bf16[32,3072]{1,0:T(8,128)(2,1)}, bf16[32,3072]{1,0:T(8,128)(2,1)S(1)}, u32[]{:S(2)}, u32[]{:S(2)}) collective-permute-start(bf16[32,3072]{1,0:T(8,128)(2,1)} %param.22), channel_id=1, source_target_pairs={{0,3},{2,1},{4,0},{6,2},{7,4},{5,6},{3,7},{1,5},{8,11},{10,9},{12,... | collective-permute-start | bytes 589832 | tf_op jit(solution)/shard_map/ppermute | solution.py:59
  4.0 29.6 %collective-permute-start = (bf16[32,3072]{1,0:T(8,128)(2,1)}, bf16[32,3072]{1,0:T(8,128)(2,1)S(1)}, u32[]{:S(2)}, u32[]{:S(2)}) collective-permute-start(bf16[32,3072]{1,0:T(8,128)(2,1)} %param.22), channel_id=1, source_target_pairs={{0,1},{2,0},{4,2},{6,4},{7,6},{5,7},{3,5},{1,3},{8,9},{10,8},{12,1... | collective-permute-start | bytes 589832 | tf_op jit(solution)/shard_map/ppermute | solution.py:59
  5.6 38.3 %collective-permute-start.7 = (bf16[32,3072]{1,0:T(8,128)(2,1)}, bf16[32,3072]{1,0:T(8,128)(2,1)S(1)}, u32[]{:S(2)}, u32[]{:S(2)}) collective-permute-start(bf16[32,3072]{1,0:T(8,128)(2,1)} %param.22), channel_id=1, source_target_pairs={{0,2},{2,4},{4,6},{6,7},{7,5},{5,3},{3,1},{1,0},{8,10},{10,12},{12... | collective-permute-start | bytes 589832 | tf_op jit(solution)/shard_map/ppermute | solution.py:58
  6.0 27.4 %collective-permute-start.3 = (bf16[32,3072]{1,0:T(8,128)(2,1)}, bf16[32,3072]{1,0:T(8,128)(2,1)S(1)}, u32[]{:S(2)}, u32[]{:S(2)}) collective-permute-start(bf16[32,3072]{1,0:T(8,128)(2,1)} %param.22), channel_id=1, source_target_pairs={{0,4},{2,6},{4,7},{6,5},{7,3},{5,1},{3,0},{1,2},{8,12},{10,14},{12... | collective-permute-start | bytes 589832 | tf_op jit(solution)/shard_map/ppermute | solution.py:58
  31.5 5.9 %collective-permute-start.2 = (bf16[32,3072]{1,0:T(8,128)(2,1)S(1)}, bf16[32,3072]{1,0:T(8,128)(2,1)S(1)}, u32[]{:S(2)}, u32[]{:S(2)}) collective-permute-start(bf16[32,3072]{1,0:T(8,128)(2,1)S(1)} %collective-permute-done.1), channel_id=1, source_target_pairs={{0,1},{2,0},{4,2},{6,4},{7,6},{5,7},{3,5},{1,3},{8,9},{10,8},{12,1... | collective-permute-start | bytes 589832 | tf_op jit(solution)/shard_map/ppermute | solution.py:71
  33.4 5.7 %collective-permute-start.4 = (bf16[32,3072]{1,0:T(8,128)(2,1)S(1)}, bf16[32,3072]{1,0:T(8,128)(2,1)S(1)}, u32[]{:S(2)}, u32[]{:S(2)}) collective-permute-start(bf16[32,3072]{1,0:T(8,128)(2,1)S(1)} %collective-permute-done.3), channel_id=1, source_target_pairs={{0,2},{2,4},{4,6},{6,7},{7,5},{5,3},{3,1},{1,0},{8,10},{10,12},{12... | collective-permute-start | bytes 589832 | tf_op jit(solution)/shard_map/ppermute | solution.py:68
  37.4 4.7 %collective-permute-start.6 = (bf16[16,3072]{1,0:T(8,128)(2,1)S(1)}, bf16[16,3072]{1,0:T(8,128)(2,1)S(1)}, u32[]{:S(2)}, u32[]{:S(2)}) collective-permute-start(bf16[16,3072]{1,0:T(8,128)(2,1)S(1)} %slice.386), channel_id=1, source_target_pairs={{0,1},{2,0},{4,2},{6,4},{7,6},{5,7},{3,5},{1,3},{8,9},{10,8},{12,1... | collective-permute-start | bytes 294920 | tf_op jit(solution)/shard_map/ppermute | solution.py:65
  39.1 4.7 %collective-permute-start.5 = (bf16[16,3072]{1,0:T(8,128)(2,1)S(1)}, bf16[16,3072]{1,0:T(8,128)(2,1)S(1)}, u32[]{:S(2)}, u32[]{:S(2)}) collective-permute-start(bf16[16,3072]{1,0:T(8,128)(2,1)S(1)} %slice.385), channel_id=1, source_target_pairs={{0,2},{2,4},{4,6},{6,7},{7,5},{5,3},{3,1},{1,0},{8,10},{10,12},{12... | collective-permute-start | bytes 294920 | tf_op jit(solution)/shard_map/ppermute | solution.py:64
  39.6 7.1 %copy-start.4 = (f32[3,3072]{1,0:T(4,128)S(1)}, f32[3,3072]{1,0:T(4,128)}, u32[]{:S(2)}) copy-start(f32[3,3072]{1,0:T(4,128)} %param.23) | copy-start | bytes 110596
  43.9 3.4 %copy-start.1 = (bf16[8,32,3072]{2,1,0:T(8,128)(2,1)}, bf16[8,32,3072]{2,1,0:T(8,128)(2,1)S(1)}, u32[]{:S(2)}) copy-start(bf16[8,32,3072]{2,1,0:T(8,128)(2,1)S(1)} %bitcast_dynamic-update-slice_fusion.14) | copy-start | bytes 4718596
  44.5 4.9 %collective-permute-start.8 = (bf16[128,3072]{1,0:T(8,128)(2,1)S(1)}, bf16[128,3072]{1,0:T(8,128)(2,1)}, u32[]{:S(2)}, u32[]{:S(2)}) collective-permute-start(bf16[128,3072]{1,0:T(8,128)(2,1)S(1)} %bitcast.153), channel_id=1, source_target_pairs={{0,8},{1,9},{2,10},{3,11},{4,12},{5,13},{6,14},{7,15},{16,24},{17,... | collective-permute-start | bytes 2359304 | tf_op jit(solution)/shard_map/ppermute | solution.py:14
  69.4 4.8 %collective-permute-start.9 = (bf16[16,3072]{1,0:T(8,128)(2,1)S(1)}, bf16[16,3072]{1,0:T(8,128)(2,1)S(1)}, u32[]{:S(2)}, u32[]{:S(2)}) collective-permute-start(bf16[16,3072]{1,0:T(8,128)(2,1)S(1)} %get-tuple-element.121), channel_id=1, source_target_pairs={{0,2},{2,4},{4,6},{6,7},{7,5},{5,3},{3,1},{1,0},{8,10},{10,12},{12... | collective-permute-start | bytes 294920 | tf_op jit(solution)/shard_map/ppermute | solution.py:113
  69.8 4.9 %collective-permute-start.13 = (bf16[16,3072]{1,0:T(8,128)(2,1)S(1)}, bf16[16,3072]{1,0:T(8,128)(2,1)S(1)}, u32[]{:S(2)}, u32[]{:S(2)}) collective-permute-start(bf16[16,3072]{1,0:T(8,128)(2,1)S(1)} %get-tuple-element.122), channel_id=1, source_target_pairs={{0,1},{2,0},{4,2},{6,4},{7,6},{5,7},{3,5},{1,3},{8,9},{10,8},{12,1... | collective-permute-start | bytes 294920 | tf_op jit(solution)/shard_map/ppermute | solution.py:113
  74.3 5.9 %collective-permute-start.10 = (bf16[32,3072]{1,0:T(8,128)(2,1)S(1)}, bf16[32,3072]{1,0:T(8,128)(2,1)S(1)}, u32[]{:S(2)}, u32[]{:S(2)}) collective-permute-start(bf16[32,3072]{1,0:T(8,128)(2,1)S(1)} %convert_element_type.317), channel_id=1, source_target_pairs={{0,2},{2,4},{4,6},{6,7},{7,5},{5,3},{3,1},{1,0},{8,10},{10,12},{12... | collective-permute-start | bytes 589832 | tf_op jit(solution)/shard_map/ppermute | solution.py:113
  74.8 25.5 %copy-start.3 = (bf16[32,3072]{1,0:T(8,128)(2,1)S(1)}, bf16[32,3072]{1,0:T(8,128)(2,1)}, u32[]{:S(2)}) copy-start(bf16[32,3072]{1,0:T(8,128)(2,1)} %param.22) | copy-start | bytes 589828
  74.8 5.8 %collective-permute-start.14 = (bf16[32,3072]{1,0:T(8,128)(2,1)S(1)}, bf16[32,3072]{1,0:T(8,128)(2,1)S(1)}, u32[]{:S(2)}, u32[]{:S(2)}) collective-permute-start(bf16[32,3072]{1,0:T(8,128)(2,1)S(1)} %convert_element_type.327), channel_id=1, source_target_pairs={{0,1},{2,0},{4,2},{6,4},{7,6},{5,7},{3,5},{1,3},{8,9},{10,8},{12,1... | collective-permute-start | bytes 589832 | tf_op jit(solution)/shard_map/ppermute | solution.py:113
  80.2 5.7 %collective-permute-start.11 = (bf16[32,3072]{1,0:T(8,128)(2,1)S(1)}, bf16[32,3072]{1,0:T(8,128)(2,1)S(1)}, u32[]{:S(2)}, u32[]{:S(2)}) collective-permute-start(bf16[32,3072]{1,0:T(8,128)(2,1)S(1)} %add_convert_fusion.14), channel_id=1, source_target_pairs={{0,2},{2,4},{4,6},{6,7},{7,5},{5,3},{3,1},{1,0},{8,10},{10,12},{12... | collective-permute-start | bytes 589832 | tf_op jit(solution)/shard_map/ppermute | solution.py:113
  86.0 7.5 %collective-permute-start.15 = (bf16[32,3072]{1,0:T(8,128)(2,1)S(1)}, bf16[32,3072]{1,0:T(8,128)(2,1)S(1)}, u32[]{:S(2)}, u32[]{:S(2)}) collective-permute-start(bf16[32,3072]{1,0:T(8,128)(2,1)S(1)} %get-tuple-element.114), channel_id=1, source_target_pairs={{0,1},{2,0},{4,2},{6,4},{7,6},{5,7},{3,5},{1,3},{8,9},{10,8},{12,1... | collective-permute-start | bytes 589832 | tf_op jit(solution)/shard_map/ppermute | solution.py:113
  87.7 7.6 %collective-permute-start.12 = (bf16[32,3072]{1,0:T(8,128)(2,1)S(1)}, bf16[32,3072]{1,0:T(8,128)(2,1)S(1)}, u32[]{:S(2)}, u32[]{:S(2)}) collective-permute-start(bf16[32,3072]{1,0:T(8,128)(2,1)S(1)} %get-tuple-element.113), channel_id=1, source_target_pairs={{0,2},{2,4},{4,6},{6,7},{7,5},{5,3},{3,1},{1,0},{8,10},{10,12},{12... | collective-permute-start | bytes 589832 | tf_op jit(solution)/shard_map/ppermute | solution.py:113
  93.6 6.7 %collective-permute-start.16 = (bf16[32,3072]{1,0:T(8,128)(2,1)S(1)}, bf16[32,3072]{1,0:T(8,128)(2,1)S(1)}, u32[]{:S(2)}, u32[]{:S(2)}) collective-permute-start(bf16[32,3072]{1,0:T(8,128)(2,1)S(1)} %add_convert_fusion.11), channel_id=1, source_target_pairs={{0,1},{2,0},{4,2},{6,4},{7,6},{5,7},{3,5},{1,3},{8,9},{10,8},{12,1... | collective-permute-start | bytes 589832 | tf_op jit(solution)/shard_map/ppermute | solution.py:113
  100.4 5.7 %collective-permute-start.17 = (bf16[32,3072]{1,0:T(8,128)(2,1)S(1)}, bf16[32,3072]{1,0:T(8,128)(2,1)S(1)}, u32[]{:S(2)}, u32[]{:S(2)}) collective-permute-start(bf16[32,3072]{1,0:T(8,128)(2,1)S(1)} %get-tuple-element.98), channel_id=1, source_target_pairs={{0,1},{2,0},{4,2},{6,4},{7,6},{5,7},{3,5},{1,3},{8,9},{10,8},{12,1... | collective-permute-start | bytes 589832 | tf_op jit(solution)/shard_map/ppermute | solution.py:59
  102.0 5.7 %collective-permute-start.20 = (bf16[32,3072]{1,0:T(8,128)(2,1)S(1)}, bf16[32,3072]{1,0:T(8,128)(2,1)S(1)}, u32[]{:S(2)}, u32[]{:S(2)}) collective-permute-start(bf16[32,3072]{1,0:T(8,128)(2,1)S(1)} %get-tuple-element.98), channel_id=1, source_target_pairs={{0,2},{2,4},{4,6},{6,7},{7,5},{5,3},{3,1},{1,0},{8,10},{10,12},{12... | collective-permute-start | bytes 589832 | tf_op jit(solution)/shard_map/ppermute | solution.py:58
  106.1 6.5 %collective-permute-start.18 = (bf16[32,3072]{1,0:T(8,128)(2,1)S(1)}, bf16[32,3072]{1,0:T(8,128)(2,1)S(1)}, u32[]{:S(2)}, u32[]{:S(2)}) collective-permute-start(bf16[32,3072]{1,0:T(8,128)(2,1)S(1)} %collective-permute-done.17), channel_id=1, source_target_pairs={{0,1},{2,0},{4,2},{6,4},{7,6},{5,7},{3,5},{1,3},{8,9},{10,8},{12,1... | collective-permute-start | bytes 589832 | tf_op jit(solution)/shard_map/ppermute | solution.py:71
  107.7 6.5 %collective-permute-start.21 = (bf16[32,3072]{1,0:T(8,128)(2,1)S(1)}, bf16[32,3072]{1,0:T(8,128)(2,1)S(1)}, u32[]{:S(2)}, u32[]{:S(2)}) collective-permute-start(bf16[32,3072]{1,0:T(8,128)(2,1)S(1)} %collective-permute-done.20), channel_id=1, source_target_pairs={{0,2},{2,4},{4,6},{6,7},{7,5},{5,3},{3,1},{1,0},{8,10},{10,12},{12... | collective-permute-start | bytes 589832 | tf_op jit(solution)/shard_map/ppermute | solution.py:68
  112.6 5.7 %collective-permute-start.19 = (bf16[32,3072]{1,0:T(8,128)(2,1)S(1)}, bf16[32,3072]{1,0:T(8,128)(2,1)S(1)}, u32[]{:S(2)}, u32[]{:S(2)}) collective-permute-start(bf16[32,3072]{1,0:T(8,128)(2,1)S(1)} %collective-permute-done.18), channel_id=1, source_target_pairs={{0,1},{2,0},{4,2},{6,4},{7,6},{5,7},{3,5},{1,3},{8,9},{10,8},{12,1... | collective-permute-start | bytes 589832 | tf_op jit(solution)/shard_map/ppermute | solution.py:71
  114.2 5.7 %collective-permute-start.22 = (bf16[32,3072]{1,0:T(8,128)(2,1)S(1)}, bf16[32,3072]{1,0:T(8,128)(2,1)S(1)}, u32[]{:S(2)}, u32[]{:S(2)}) collective-permute-start(bf16[32,3072]{1,0:T(8,128)(2,1)S(1)} %collective-permute-done.21), channel_id=1, source_target_pairs={{0,2},{2,4},{4,6},{6,7},{7,5},{5,3},{3,1},{1,0},{8,10},{10,12},{12... | collective-permute-start | bytes 589832 | tf_op jit(solution)/shard_map/ppermute | solution.py:68
  118.3 4.7 %collective-permute-start.24 = (bf16[16,3072]{1,0:T(8,128)(2,1)S(1)}, bf16[16,3072]{1,0:T(8,128)(2,1)S(1)}, u32[]{:S(2)}, u32[]{:S(2)}) collective-permute-start(bf16[16,3072]{1,0:T(8,128)(2,1)S(1)} %slice.400), channel_id=1, source_target_pairs={{0,1},{2,0},{4,2},{6,4},{7,6},{5,7},{3,5},{1,3},{8,9},{10,8},{12,1... | collective-permute-start | bytes 294920 | tf_op jit(solution)/shard_map/ppermute | solution.py:65
  119.9 4.7 %collective-permute-start.23 = (bf16[16,3072]{1,0:T(8,128)(2,1)S(1)}, bf16[16,3072]{1,0:T(8,128)(2,1)S(1)}, u32[]{:S(2)}, u32[]{:S(2)}) collective-permute-start(bf16[16,3072]{1,0:T(8,128)(2,1)S(1)} %slice.399), channel_id=1, source_target_pairs={{0,2},{2,4},{4,6},{6,7},{7,5},{5,3},{3,1},{1,0},{8,10},{10,12},{12... | collective-permute-start | bytes 294920 | tf_op jit(solution)/shard_map/ppermute | solution.py:64
  124.7 4.7 %copy-start.2 = (bf16[8,32,3072]{2,1,0:T(8,128)(2,1)}, bf16[8,32,3072]{2,1,0:T(8,128)(2,1)S(1)}, u32[]{:S(2)}) copy-start(bf16[8,32,3072]{2,1,0:T(8,128)(2,1)S(1)} %bitcast_dynamic-update-slice_fusion.7) | copy-start | bytes 4718596
  125.3 6.1 %collective-permute-start.25 = (bf16[128,3072]{1,0:T(8,128)(2,1)S(1)}, bf16[128,3072]{1,0:T(8,128)(2,1)}, u32[]{:S(2)}, u32[]{:S(2)}) collective-permute-start(bf16[128,3072]{1,0:T(8,128)(2,1)S(1)} %bitcast.152), channel_id=1, source_target_pairs={{0,8},{1,9},{2,10},{3,11},{4,12},{5,13},{6,14},{7,15},{16,24},{17,... | collective-permute-start | bytes 2359304 | tf_op jit(solution)/shard_map/ppermute | solution.py:14
  151.2 4.8 %collective-permute-start.26 = (bf16[16,3072]{1,0:T(8,128)(2,1)S(1)}, bf16[16,3072]{1,0:T(8,128)(2,1)S(1)}, u32[]{:S(2)}, u32[]{:S(2)}) collective-permute-start(bf16[16,3072]{1,0:T(8,128)(2,1)S(1)} %get-tuple-element.119), channel_id=1, source_target_pairs={{0,2},{2,4},{4,6},{6,7},{7,5},{5,3},{3,1},{1,0},{8,10},{10,12},{12... | collective-permute-start | bytes 294920 | tf_op jit(solution)/shard_map/ppermute | solution.py:113
  151.7 5.0 %collective-permute-start.30 = (bf16[16,3072]{1,0:T(8,128)(2,1)S(1)}, bf16[16,3072]{1,0:T(8,128)(2,1)S(1)}, u32[]{:S(2)}, u32[]{:S(2)}) collective-permute-start(bf16[16,3072]{1,0:T(8,128)(2,1)S(1)} %get-tuple-element.120), channel_id=1, source_target_pairs={{0,1},{2,0},{4,2},{6,4},{7,6},{5,7},{3,5},{1,3},{8,9},{10,8},{12,1... | collective-permute-start | bytes 294920 | tf_op jit(solution)/shard_map/ppermute | solution.py:113
  156.1 7.1 %collective-permute-start.27 = (bf16[32,3072]{1,0:T(8,128)(2,1)S(1)}, bf16[32,3072]{1,0:T(8,128)(2,1)S(1)}, u32[]{:S(2)}, u32[]{:S(2)}) collective-permute-start(bf16[32,3072]{1,0:T(8,128)(2,1)S(1)} %convert_element_type.342), channel_id=1, source_target_pairs={{0,2},{2,4},{4,6},{6,7},{7,5},{5,3},{3,1},{1,0},{8,10},{10,12},{12... | collective-permute-start | bytes 589832 | tf_op jit(solution)/shard_map/ppermute | solution.py:113
  156.8 7.0 %collective-permute-start.31 = (bf16[32,3072]{1,0:T(8,128)(2,1)S(1)}, bf16[32,3072]{1,0:T(8,128)(2,1)S(1)}, u32[]{:S(2)}, u32[]{:S(2)}) collective-permute-start(bf16[32,3072]{1,0:T(8,128)(2,1)S(1)} %convert_element_type.352), channel_id=1, source_target_pairs={{0,1},{2,0},{4,2},{6,4},{7,6},{5,7},{3,5},{1,3},{8,9},{10,8},{12,1... | collective-permute-start | bytes 589832 | tf_op jit(solution)/shard_map/ppermute | solution.py:113
  163.3 6.7 %collective-permute-start.28 = (bf16[32,3072]{1,0:T(8,128)(2,1)S(1)}, bf16[32,3072]{1,0:T(8,128)(2,1)S(1)}, u32[]{:S(2)}, u32[]{:S(2)}) collective-permute-start(bf16[32,3072]{1,0:T(8,128)(2,1)S(1)} %add_convert_fusion.9), channel_id=1, source_target_pairs={{0,2},{2,4},{4,6},{6,7},{7,5},{5,3},{3,1},{1,0},{8,10},{10,12},{12... | collective-permute-start | bytes 589832 | tf_op jit(solution)/shard_map/ppermute | solution.py:113
  170.1 5.7 %collective-permute-start.32 = (bf16[32,3072]{1,0:T(8,128)(2,1)S(1)}, bf16[32,3072]{1,0:T(8,128)(2,1)S(1)}, u32[]{:S(2)}, u32[]{:S(2)}) collective-permute-start(bf16[32,3072]{1,0:T(8,128)(2,1)S(1)} %get-tuple-element.110), channel_id=1, source_target_pairs={{0,1},{2,0},{4,2},{6,4},{7,6},{5,7},{3,5},{1,3},{8,9},{10,8},{12,1... | collective-permute-start | bytes 589832 | tf_op jit(solution)/shard_map/ppermute | solution.py:113
  171.3 7.0 %collective-permute-start.29 = (bf16[32,3072]{1,0:T(8,128)(2,1)S(1)}, bf16[32,3072]{1,0:T(8,128)(2,1)S(1)}, u32[]{:S(2)}, u32[]{:S(2)}) collective-permute-start(bf16[32,3072]{1,0:T(8,128)(2,1)S(1)} %get-tuple-element.109), channel_id=1, source_target_pairs={{0,2},{2,4},{4,6},{6,7},{7,5},{5,3},{3,1},{1,0},{8,10},{10,12},{12... | collective-permute-start | bytes 589832 | tf_op jit(solution)/shard_map/ppermute | solution.py:113
  175.9 6.0 %collective-permute-start.33 = (bf16[32,3072]{1,0:T(8,128)(2,1)S(1)}, bf16[32,3072]{1,0:T(8,128)(2,1)S(1)}, u32[]{:S(2)}, u32[]{:S(2)}) collective-permute-start(bf16[32,3072]{1,0:T(8,128)(2,1)S(1)} %add_convert_fusion.6), channel_id=1, source_target_pairs={{0,1},{2,0},{4,2},{6,4},{7,6},{5,7},{3,5},{1,3},{8,9},{10,8},{12,1... | collective-permute-start | bytes 589832 | tf_op jit(solution)/shard_map/ppermute | solution.py:113
  182.6 7.7 %collective-permute-start.34 = (bf16[32,3072]{1,0:T(8,128)(2,1)S(1)}, bf16[32,3072]{1,0:T(8,128)(2,1)S(1)}, u32[]{:S(2)}, u32[]{:S(2)}) collective-permute-start(bf16[32,3072]{1,0:T(8,128)(2,1)S(1)} %get-tuple-element.96), channel_id=1, source_target_pairs={{0,1},{2,0},{4,2},{6,4},{7,6},{5,7},{3,5},{1,3},{8,9},{10,8},{12,1... | collective-permute-start | bytes 589832 | tf_op jit(solution)/shard_map/ppermute | solution.py:59
  185.6 7.1 %collective-permute-start.37 = (bf16[32,3072]{1,0:T(8,128)(2,1)S(1)}, bf16[32,3072]{1,0:T(8,128)(2,1)S(1)}, u32[]{:S(2)}, u32[]{:S(2)}) collective-permute-start(bf16[32,3072]{1,0:T(8,128)(2,1)S(1)} %get-tuple-element.96), channel_id=1, source_target_pairs={{0,2},{2,4},{4,6},{6,7},{7,5},{5,3},{3,1},{1,0},{8,10},{10,12},{12... | collective-permute-start | bytes 589832 | tf_op jit(solution)/shard_map/ppermute | solution.py:58
  190.3 5.9 %collective-permute-start.35 = (bf16[32,3072]{1,0:T(8,128)(2,1)S(1)}, bf16[32,3072]{1,0:T(8,128)(2,1)S(1)}, u32[]{:S(2)}, u32[]{:S(2)}) collective-permute-start(bf16[32,3072]{1,0:T(8,128)(2,1)S(1)} %collective-permute-done.34), channel_id=1, source_target_pairs={{0,1},{2,0},{4,2},{6,4},{7,6},{5,7},{3,5},{1,3},{8,9},{10,8},{12,1... | collective-permute-start | bytes 589832 | tf_op jit(solution)/shard_map/ppermute | solution.py:71
  192.8 5.7 %collective-permute-start.38 = (bf16[32,3072]{1,0:T(8,128)(2,1)S(1)}, bf16[32,3072]{1,0:T(8,128)(2,1)S(1)}, u32[]{:S(2)}, u32[]{:S(2)}) collective-permute-start(bf16[32,3072]{1,0:T(8,128)(2,1)S(1)} %collective-permute-done.37), channel_id=1, source_target_pairs={{0,2},{2,4},{4,6},{6,7},{7,5},{5,3},{3,1},{1,0},{8,10},{10,12},{12... | collective-permute-start | bytes 589832 | tf_op jit(solution)/shard_map/ppermute | solution.py:68
  196.2 5.7 %collective-permute-start.36 = (bf16[32,3072]{1,0:T(8,128)(2,1)S(1)}, bf16[32,3072]{1,0:T(8,128)(2,1)S(1)}, u32[]{:S(2)}, u32[]{:S(2)}) collective-permute-start(bf16[32,3072]{1,0:T(8,128)(2,1)S(1)} %collective-permute-done.35), channel_id=1, source_target_pairs={{0,1},{2,0},{4,2},{6,4},{7,6},{5,7},{3,5},{1,3},{8,9},{10,8},{12,1... | collective-permute-start | bytes 589832 | tf_op jit(solution)/shard_map/ppermute | solution.py:71
  198.4 5.7 %collective-permute-start.39 = (bf16[32,3072]{1,0:T(8,128)(2,1)S(1)}, bf16[32,3072]{1,0:T(8,128)(2,1)S(1)}, u32[]{:S(2)}, u32[]{:S(2)}) collective-permute-start(bf16[32,3072]{1,0:T(8,128)(2,1)S(1)} %collective-permute-done.38), channel_id=1, source_target_pairs={{0,2},{2,4},{4,6},{6,7},{7,5},{5,3},{3,1},{1,0},{8,10},{10,12},{12... | collective-permute-start | bytes 589832 | tf_op jit(solution)/shard_map/ppermute | solution.py:68
  201.9 4.7 %collective-permute-start.41 = (bf16[16,3072]{1,0:T(8,128)(2,1)S(1)}, bf16[16,3072]{1,0:T(8,128)(2,1)S(1)}, u32[]{:S(2)}, u32[]{:S(2)}) collective-permute-start(bf16[16,3072]{1,0:T(8,128)(2,1)S(1)} %slice.414), channel_id=1, source_target_pairs={{0,1},{2,0},{4,2},{6,4},{7,6},{5,7},{3,5},{1,3},{8,9},{10,8},{12,1... | collective-permute-start | bytes 294920 | tf_op jit(solution)/shard_map/ppermute | solution.py:65
  204.1 4.7 %collective-permute-start.40 = (bf16[16,3072]{1,0:T(8,128)(2,1)S(1)}, bf16[16,3072]{1,0:T(8,128)(2,1)S(1)}, u32[]{:S(2)}, u32[]{:S(2)}) collective-permute-start(bf16[16,3072]{1,0:T(8,128)(2,1)S(1)} %slice.413), channel_id=1, source_target_pairs={{0,2},{2,4},{4,6},{6,7},{7,5},{5,3},{3,1},{1,0},{8,10},{10,12},{12... | collective-permute-start | bytes 294920 | tf_op jit(solution)/shard_map/ppermute | solution.py:64
  214.1 1.7 copy-start.5
  217.4 2.9 %collective-permute-start.42 = (bf16[256,128]{1,0:T(8,128)(2,1)S(1)}, bf16[256,128]{1,0:T(8,128)(2,1)S(1)}, u32[]{:S(2)}, u32[]{:S(2)}) collective-permute-start(bf16[256,128]{1,0:T(8,128)(2,1)S(1)} %convolution_convert_fusion.7), channel_id=1, source_target_pairs={{0,8},{1,9},{2,10},{3,11},{4,12},{5,13},{6,14},{7,15},{16,24},{17,... | collective-permute-start | bytes 196616 | tf_op jit(solution)/shard_map/ppermute | solution.py:14
  218.7 2.2 collective-permute-start.43
  223.4 4.7 %collective-permute-start.44 = (bf16[16,3072]{1,0:T(8,128)(2,1)S(1)}, bf16[16,3072]{1,0:T(8,128)(2,1)S(1)}, u32[]{:S(2)}, u32[]{:S(2)}) collective-permute-start(bf16[16,3072]{1,0:T(8,128)(2,1)S(1)} %get-tuple-element.117), channel_id=1, source_target_pairs={{0,2},{2,4},{4,6},{6,7},{7,5},{5,3},{3,1},{1,0},{8,10},{10,12},{12... | collective-permute-start | bytes 294920 | tf_op jit(solution)/shard_map/ppermute | solution.py:113
  223.5 4.7 %collective-permute-start.48 = (bf16[16,3072]{1,0:T(8,128)(2,1)S(1)}, bf16[16,3072]{1,0:T(8,128)(2,1)S(1)}, u32[]{:S(2)}, u32[]{:S(2)}) collective-permute-start(bf16[16,3072]{1,0:T(8,128)(2,1)S(1)} %get-tuple-element.118), channel_id=1, source_target_pairs={{0,1},{2,0},{4,2},{6,4},{7,6},{5,7},{3,5},{1,3},{8,9},{10,8},{12,1... | collective-permute-start | bytes 294920 | tf_op jit(solution)/shard_map/ppermute | solution.py:113
  228.2 7.5 %collective-permute-start.45 = (bf16[32,3072]{1,0:T(8,128)(2,1)S(1)}, bf16[32,3072]{1,0:T(8,128)(2,1)S(1)}, u32[]{:S(2)}, u32[]{:S(2)}) collective-permute-start(bf16[32,3072]{1,0:T(8,128)(2,1)S(1)} %convert_element_type.376), channel_id=1, source_target_pairs={{0,2},{2,4},{4,6},{6,7},{7,5},{5,3},{3,1},{1,0},{8,10},{10,12},{12... | collective-permute-start | bytes 589832 | tf_op jit(solution)/shard_map/ppermute | solution.py:113
  228.3 7.5 %collective-permute-start.49 = (bf16[32,3072]{1,0:T(8,128)(2,1)S(1)}, bf16[32,3072]{1,0:T(8,128)(2,1)S(1)}, u32[]{:S(2)}, u32[]{:S(2)}) collective-permute-start(bf16[32,3072]{1,0:T(8,128)(2,1)S(1)} %convert_element_type.386), channel_id=1, source_target_pairs={{0,1},{2,0},{4,2},{6,4},{7,6},{5,7},{3,5},{1,3},{8,9},{10,8},{12,1... | collective-permute-start | bytes 589832 | tf_op jit(solution)/shard_map/ppermute | solution.py:113
  235.8 7.6 %collective-permute-start.46 = (bf16[32,3072]{1,0:T(8,128)(2,1)S(1)}, bf16[32,3072]{1,0:T(8,128)(2,1)S(1)}, u32[]{:S(2)}, u32[]{:S(2)}) collective-permute-start(bf16[32,3072]{1,0:T(8,128)(2,1)S(1)} %add_convert_fusion.4), channel_id=1, source_target_pairs={{0,2},{2,4},{4,6},{6,7},{7,5},{5,3},{3,1},{1,0},{8,10},{10,12},{12... | collective-permute-start | bytes 589832 | tf_op jit(solution)/shard_map/ppermute | solution.py:113
  243.4 6.6 %collective-permute-start.50 = (bf16[32,3072]{1,0:T(8,128)(2,1)S(1)}, bf16[32,3072]{1,0:T(8,128)(2,1)S(1)}, u32[]{:S(2)}, u32[]{:S(2)}) collective-permute-start(bf16[32,3072]{1,0:T(8,128)(2,1)S(1)} %get-tuple-element.106), channel_id=1, source_target_pairs={{0,1},{2,0},{4,2},{6,4},{7,6},{5,7},{3,5},{1,3},{8,9},{10,8},{12,1... | collective-permute-start | bytes 589832 | tf_op jit(solution)/shard_map/ppermute | solution.py:113
  245.2 6.3 %collective-permute-start.47 = (bf16[32,3072]{1,0:T(8,128)(2,1)S(1)}, bf16[32,3072]{1,0:T(8,128)(2,1)S(1)}, u32[]{:S(2)}, u32[]{:S(2)}) collective-permute-start(bf16[32,3072]{1,0:T(8,128)(2,1)S(1)} %get-tuple-element.105), channel_id=1, source_target_pairs={{0,2},{2,4},{4,6},{6,7},{7,5},{5,3},{3,1},{1,0},{8,10},{10,12},{12... | collective-permute-start | bytes 589832 | tf_op jit(solution)/shard_map/ppermute | solution.py:113
  250.0 5.7 %collective-permute-start.51 = (bf16[32,3072]{1,0:T(8,128)(2,1)S(1)}, bf16[32,3072]{1,0:T(8,128)(2,1)S(1)}, u32[]{:S(2)}, u32[]{:S(2)}) collective-permute-start(bf16[32,3072]{1,0:T(8,128)(2,1)S(1)} %add_convert_fusion.1), channel_id=1, source_target_pairs={{0,1},{2,0},{4,2},{6,4},{7,6},{5,7},{3,5},{1,3},{8,9},{10,8},{12,1... | collective-permute-start | bytes 589832 | tf_op jit(solution)/shard_map/ppermute | solution.py:113

commit v17 on v16

--- a/solution.py
+++ b/solution.py
@@ -286,7 +286,9 @@
         jnp.dot(attn_in, qkv_parts[i], preferred_element_type=jnp.float32).astype(jnp.bfloat16)
         for i in range(3)
     )
-    keys_prev, values_prev = shifted((keys_own, values_own), "blk", 1)
+    keys_values_prev = shifted(jnp.concatenate([keys_own, values_own], axis=1), "blk", 1)
+    keys_prev = keys_values_prev[:, :head_size]
+    values_prev = keys_values_prev[:, head_size:]
     own_part = attend(queries, keys_own, values_own, True)
     crossing_portion = lax.cond(
         blk_pos > 0,

time: 257 us -> 256 us (level)
    ppermute x4 -> x3, starting transfers between devices: 6.92 us -> 5.65 us  [shifted(): return lax.ppermute(value, axis, pairs)]
  transfers between devices with their start and end apart: 52 -> 51, of which waited for: 31 -> 31; matrix products, arithmetic and copies ran while one was open for 15% -> 15% of each run, Pallas kernels for 0% -> 0%
where the time goes in v17:
time: 256 us; the launch traced here: 255 us
  waiting for transfers between devices  101 us (39%)
  starting transfers between devices  58.2 us (23%)
  local copies, waits for them, and re-layouts  41.2 us (16%)
  Pallas kernels  21.7 us (8%)
  other arithmetic  16.1 us (6%)
  matrix products  12.8 us (5%)
  between operations  4.41 us (2%)
    ppermute x24, waiting for transfers between devices, chain(): passed = lax.ppermute(part.astype(value.dtype), axis, pairs)  61.7 us
    unnamed x29, local copies, waits for them, and re-layouts  25.4 us
    ppermute x24, starting transfers between devices, chain(): passed = lax.ppermute(part.astype(value.dtype), axis, pairs)  24.9 us
    pallas_call x2, Pallas kernels, convolution_gate(): pl.pallas_call(conv_gate_kernel, out_shape=jax.ShapeDtypeStruct((all_rows...  21.7 us
    ppermute x5, waiting for transfers between devices, ring_gather(): bwd = lax.ppermute(bwd, axis, backward)  17.4 us
    another operation x4, other arithmetic, convolution_gate(): jnp.stack([lax.dynamic_slice_in_dim(padded, border_rows - tap_idx * dilat...  10.8 us
    dot_general x6, matrix products, rounded_term(): term = jnp.dot(left, right, preferred_element_type=jnp.float32)  10.5 us
    ppermute x4, starting transfers between devices, ring_gather(): lax.ppermute(value, axis, [(order[p], order[(p - k) % length]) for p in r...  10 us
  transfers between devices with their start and end apart: 51, of which 31 were waited for; matrix products, arithmetic and copies ran while one was open for 15% of the time, Pallas kernels for 0%

profile of v17, /device:TPU:0, one launch (start us, length us, event | category | flops | bytes accessed | tf_op | source)
XLA Modules:
  0.0 255.5 jit_solution(8184407430934197671)
XLA Ops:
  0.0 4.0 %collective-permute-start.1 = (bf16[32,3072]{1,0:T(8,128)(2,1)}, bf16[32,3072]{1,0:T(8,128)(2,1)S(1)}, u32[]{:S(2)}, u32[]{:S(2)}) collective-permute-start(bf16[32,3072]{1,0:T(8,128)(2,1)} %param.22), channel_id=1, source_target_pairs={{0,3},{2,1},{4,0},{6,2},{7,4},{5,6},{3,7},{1,5},{8,11},{10,9},{12,... | collective-permute-start | bytes 589832 | tf_op jit(solution)/shard_map/ppermute | solution.py:59
  4.0 1.6 collective-permute-start
  10.4 19.7 %copy.12 = bf16[2,3,3072,2,384]{4,2,3,1,0:T(8,128)(2,1)} copy(bf16[2,3,3072,2,384]{4,3,2,1,0:T(2,128)(2,1)} %param.25) | data formatting | bytes 56623104 | tf_op args[3]
  31.5 1.8 collective-permute-start.2
  33.6 3.7 %collective-permute-done.2 = bf16[32,3072]{1,0:T(8,128)(2,1)S(1)} collective-permute-done((bf16[32,3072]{1,0:T(8,128)(2,1)S(1)}, bf16[32,3072]{1,0:T(8,128)(2,1)S(1)}, u32[]{:S(2)}, u32[]{:S(2)}) %collective-permute-start.2) | collective-permute-done | bytes 196640 | tf_op jit(solution)/shard_map/ppermute | solution.py:71
  37.4 1.7 collective-permute-start.6
  39.5 2.5 collective-permute-done.6
  42.0 1.7 collective-permute-done.5
  44.5 2.2 collective-permute-start.8
  47.3 2.1 gather_fusion
  49.4 2.9 %fusion.25 = (bf16[1,256,3072]{2,1,0:T(8,128)(2,1)S(1)}, bf16[1,256,3072]{2,1,0:T(8,128)(2,1)S(1)}) fusion(s32[]{:T(128)S(6)} %select_n.21, bf16[256,3072]{1,0:T(8,128)(2,1)S(1)} %bitcast.141, bf16[128,3072]{1,0:T(8,128)(2,1)} %collective-permute-done.8, s32[]{:T(128)S(6)} %select_n.22), kind=kLoop, calls=%fused_computation.53 | loop fusion | flops 6291456 | bytes 5505032 | tf_op jit(solution)/shard_map/stack | solution.py:171
  52.2 2.4 pad_maximum_fusion.slab_ref
  54.7 10.8 %shard_map.82 = bf16[256,384]{1,0:T(8,128)(2,1)} custom-call(bf16[3,256,3072]{2,1,0:T(8,128)(2,1)} %pad_maximum_fusion.slab_ref, f32[1,3072]{1,0:T(1,128)} %get-tuple-element.126.gain_ref, bf16[2,3,2,3072,384]{4,3,2,1,0:T(8,128)(2,1)} %bitcast.139), custom_call_target="tpu_custom_call" | custom-call | flops 3623878656 | bytes 19070976 | tf_op jit(solution)/shard_map/pallas_call | solution.py:178
  67.0 2.2 convolution_convert_fusion.4
  69.6 1.7 collective-permute-start.13
  71.3 2.6 %convolution_convert_fusion.2 = bf16[256,3072]{1,0:T(8,128)(2,1)S(1)} fusion(bf16[256,384]{1,0:T(8,128)(2,1)S(1)} %bitcast.157, bf16[2,384,3072]{2,1,0:T(8,128)(2,1)} %param.26), kind=kOutput, calls=%fused_computation.23 | convolution fusion | flops 604766208 | bytes 4128768 | tf_op jit(solution)/shard_map/dot_general | solution.py:138
  74.6 1.7 collective-permute-start.14
  76.3 3.6 %collective-permute-done.10 = bf16[32,3072]{1,0:T(8,128)(2,1)S(1)} collective-permute-done((bf16[32,3072]{1,0:T(8,128)(2,1)S(1)}, bf16[32,3072]{1,0:T(8,128)(2,1)S(1)}, u32[]{:S(2)}, u32[]{:S(2)}) %collective-permute-start.10) | collective-permute-done | bytes 196640 | tf_op jit(solution)/shard_map/ppermute | solution.py:113
  80.5 5.3 %collective-permute-done.11 = bf16[32,3072]{1,0:T(8,128)(2,1)S(1)} collective-permute-done((bf16[32,3072]{1,0:T(8,128)(2,1)S(1)}, bf16[32,3072]{1,0:T(8,128)(2,1)S(1)}, u32[]{:S(2)}, u32[]{:S(2)}) %collective-permute-start.11) | collective-permute-done | bytes 196640 | tf_op jit(solution)/shard_map/ppermute | solution.py:113
  85.9 1.6 collective-permute-start.15
  88.0 5.4 %collective-permute-done.15 = bf16[32,3072]{1,0:T(8,128)(2,1)S(1)} collective-permute-done((bf16[32,3072]{1,0:T(8,128)(2,1)S(1)}, bf16[32,3072]{1,0:T(8,128)(2,1)S(1)}, u32[]{:S(2)}, u32[]{:S(2)}) %collective-permute-start.15) | collective-permute-done | bytes 196640 | tf_op jit(solution)/shard_map/ppermute | solution.py:113
  93.4 1.6 collective-permute-start.16
  95.0 5.1 %collective-permute-done.16 = bf16[32,3072]{1,0:T(8,128)(2,1)S(1)} collective-permute-done((bf16[32,3072]{1,0:T(8,128)(2,1)S(1)}, bf16[32,3072]{1,0:T(8,128)(2,1)S(1)}, u32[]{:S(2)}, u32[]{:S(2)}) %collective-permute-start.16) | collective-permute-done | bytes 196640 | tf_op jit(solution)/shard_map/ppermute | solution.py:113
  100.2 1.6 collective-permute-start.17
  102.3 3.6 %collective-permute-done.17 = bf16[32,3072]{1,0:T(8,128)(2,1)S(1)} collective-permute-done((bf16[32,3072]{1,0:T(8,128)(2,1)S(1)}, bf16[32,3072]{1,0:T(8,128)(2,1)S(1)}, u32[]{:S(2)}, u32[]{:S(2)}) %collective-permute-start.17) | collective-permute-done | bytes 196640 | tf_op jit(solution)/shard_map/ppermute | solution.py:59
  105.9 1.6 collective-permute-start.18
  108.0 4.4 %collective-permute-done.18 = bf16[32,3072]{1,0:T(8,128)(2,1)S(1)} collective-permute-done((bf16[32,3072]{1,0:T(8,128)(2,1)S(1)}, bf16[32,3072]{1,0:T(8,128)(2,1)S(1)}, u32[]{:S(2)}, u32[]{:S(2)}) %collective-permute-start.18) | collective-permute-done | bytes 196640 | tf_op jit(solution)/shard_map/ppermute | solution.py:71
  112.4 1.6 collective-permute-start.19
  114.5 3.6 %collective-permute-done.19 = bf16[32,3072]{1,0:T(8,128)(2,1)S(1)} collective-permute-done((bf16[32,3072]{1,0:T(8,128)(2,1)S(1)}, bf16[32,3072]{1,0:T(8,128)(2,1)S(1)}, u32[]{:S(2)}, u32[]{:S(2)}) %collective-permute-start.19) | collective-permute-done | bytes 196640 | tf_op jit(solution)/shard_map/ppermute | solution.py:71
  118.1 1.6 collective-permute-start.24
  120.3 2.5 collective-permute-done.24
  122.8 1.6 collective-permute-done.23
  125.1 2.2 collective-permute-start.25
  129.1 2.1 gather_fusion.3
  131.2 3.0 %fusion.21 = (bf16[1,256,3072]{2,1,0:T(8,128)(2,1)S(1)}, bf16[1,256,3072]{2,1,0:T(8,128)(2,1)S(1)}) fusion(s32[]{:T(128)S(6)} %select_n.23, bf16[256,3072]{1,0:T(8,128)(2,1)S(1)} %bitcast.143, bf16[128,3072]{1,0:T(8,128)(2,1)} %collective-permute-done.25, s32[]{:T(128)S(6)} %select_n.24), kind=kLoop, calls=%fused_computation.49 | loop fusion | flops 6291456 | bytes 5505032 | tf_op jit(solution)/shard_map/stack | solution.py:171
  134.3 2.4 pad_maximum_fusion.1.slab_ref
  136.7 10.8 %shard_map.83 = bf16[256,384]{1,0:T(8,128)(2,1)} custom-call(bf16[3,256,3072]{2,1,0:T(8,128)(2,1)} %pad_maximum_fusion.1.slab_ref, f32[1,3072]{1,0:T(1,128)} %get-tuple-element.127.gain_ref, bf16[2,3,2,3072,384]{4,3,2,1,0:T(8,128)(2,1)} %bitcast.140), custom_call_target="tpu_custom_call" | custom-call | flops 3623878656 | bytes 19070976 | tf_op jit(solution)/shard_map/pallas_call | solution.py:178
  149.0 2.2 convolution_convert_fusion.3
  151.8 1.6 collective-permute-start.30
  153.3 2.6 %convolution_convert_fusion.1 = bf16[256,3072]{1,0:T(8,128)(2,1)S(1)} fusion(bf16[256,384]{1,0:T(8,128)(2,1)S(1)} %bitcast.158, bf16[2,384,3072]{2,1,0:T(8,128)(2,1)} %param.26), kind=kOutput, calls=%fused_computation.22 | convolution fusion | flops 604766208 | bytes 4128768 | tf_op jit(solution)/shard_map/dot_general | solution.py:138
  156.8 1.6 collective-permute-start.31
  158.3 4.9 %collective-permute-done.27 = bf16[32,3072]{1,0:T(8,128)(2,1)S(1)} collective-permute-done((bf16[32,3072]{1,0:T(8,128)(2,1)S(1)}, bf16[32,3072]{1,0:T(8,128)(2,1)S(1)}, u32[]{:S(2)}, u32[]{:S(2)}) %collective-permute-start.27) | collective-permute-done | bytes 196640 | tf_op jit(solution)/shard_map/ppermute | solution.py:113
  163.8 6.2 %collective-permute-done.28 = bf16[32,3072]{1,0:T(8,128)(2,1)S(1)} collective-permute-done((bf16[32,3072]{1,0:T(8,128)(2,1)S(1)}, bf16[32,3072]{1,0:T(8,128)(2,1)S(1)}, u32[]{:S(2)}, u32[]{:S(2)}) %collective-permute-start.28) | collective-permute-done | bytes 196640 | tf_op jit(solution)/shard_map/ppermute | solution.py:113
  172.2 3.6 %collective-permute-done.32 = bf16[32,3072]{1,0:T(8,128)(2,1)S(1)} collective-permute-done((bf16[32,3072]{1,0:T(8,128)(2,1)S(1)}, bf16[32,3072]{1,0:T(8,128)(2,1)S(1)}, u32[]{:S(2)}, u32[]{:S(2)}) %collective-permute-start.32) | collective-permute-done | bytes 196640 | tf_op jit(solution)/shard_map/ppermute | solution.py:113
  175.9 1.9 collective-permute-start.33
  178.1 3.7 %collective-permute-done.33 = bf16[32,3072]{1,0:T(8,128)(2,1)S(1)} collective-permute-done((bf16[32,3072]{1,0:T(8,128)(2,1)S(1)}, bf16[32,3072]{1,0:T(8,128)(2,1)S(1)}, u32[]{:S(2)}, u32[]{:S(2)}) %collective-permute-start.33) | collective-permute-done | bytes 196640 | tf_op jit(solution)/shard_map/ppermute | solution.py:113
  182.6 2.9 %collective-permute-start.34 = (bf16[32,3072]{1,0:T(8,128)(2,1)S(1)}, bf16[32,3072]{1,0:T(8,128)(2,1)S(1)}, u32[]{:S(2)}, u32[]{:S(2)}) collective-permute-start(bf16[32,3072]{1,0:T(8,128)(2,1)S(1)} %get-tuple-element.98), channel_id=1, source_target_pairs={{0,1},{2,0},{4,2},{6,4},{7,6},{5,7},{3,5},{1,3},{8,9},{10,8},{12,1... | collective-permute-start | bytes 589832 | tf_op jit(solution)/shard_map/ppermute | solution.py:59
  185.5 4.8 %collective-permute-done.34 = bf16[32,3072]{1,0:T(8,128)(2,1)S(1)} collective-permute-done((bf16[32,3072]{1,0:T(8,128)(2,1)S(1)}, bf16[32,3072]{1,0:T(8,128)(2,1)S(1)}, u32[]{:S(2)}, u32[]{:S(2)}) %collective-permute-start.34) | collective-permute-done | bytes 196640 | tf_op jit(solution)/shard_map/ppermute | solution.py:59
  190.3 2.2 collective-permute-start.35
  193.4 2.8 %collective-permute-done.35 = bf16[32,3072]{1,0:T(8,128)(2,1)S(1)} collective-permute-done((bf16[32,3072]{1,0:T(8,128)(2,1)S(1)}, bf16[32,3072]{1,0:T(8,128)(2,1)S(1)}, u32[]{:S(2)}, u32[]{:S(2)}) %collective-permute-start.35) | collective-permute-done | bytes 196640 | tf_op jit(solution)/shard_map/ppermute | solution.py:71
  196.2 2.0 collective-permute-start.36
  199.0 2.8 %collective-permute-done.36 = bf16[32,3072]{1,0:T(8,128)(2,1)S(1)} collective-permute-done((bf16[32,3072]{1,0:T(8,128)(2,1)S(1)}, bf16[32,3072]{1,0:T(8,128)(2,1)S(1)}, u32[]{:S(2)}, u32[]{:S(2)}) %collective-permute-start.36) | collective-permute-done | bytes 196640 | tf_op jit(solution)/shard_map/ppermute | solution.py:71
  201.9 2.0 collective-permute-start.41
  204.8 1.8 collective-permute-done.41
  206.5 2.2 collective-permute-done.40
  211.5 2.1 gather_fusion.6
  222.4 2.1 collective-permute-start.47
  225.1 1.9 collective-permute-done.43
  227.3 2.1 collective-permute-start.48
  229.3 5.2 %collective-permute-done.44 = bf16[32,3072]{1,0:T(8,128)(2,1)S(1)} collective-permute-done((bf16[32,3072]{1,0:T(8,128)(2,1)S(1)}, bf16[32,3072]{1,0:T(8,128)(2,1)S(1)}, u32[]{:S(2)}, u32[]{:S(2)}) %collective-permute-start.44) | collective-permute-done | bytes 196640 | tf_op jit(solution)/shard_map/ppermute | solution.py:113
  234.7 7.5 %collective-permute-done.45 = bf16[32,3072]{1,0:T(8,128)(2,1)S(1)} collective-permute-done((bf16[32,3072]{1,0:T(8,128)(2,1)S(1)}, bf16[32,3072]{1,0:T(8,128)(2,1)S(1)}, u32[]{:S(2)}, u32[]{:S(2)}) %collective-permute-start.45) | collective-permute-done | bytes 196640 | tf_op jit(solution)/shard_map/ppermute | solution.py:113
  242.3 1.8 collective-permute-start.49
  244.4 4.6 %collective-permute-done.49 = bf16[32,3072]{1,0:T(8,128)(2,1)S(1)} collective-permute-done((bf16[32,3072]{1,0:T(8,128)(2,1)S(1)}, bf16[32,3072]{1,0:T(8,128)(2,1)S(1)}, u32[]{:S(2)}, u32[]{:S(2)}) %collective-permute-start.49) | collective-permute-done | bytes 196640 | tf_op jit(solution)/shard_map/ppermute | solution.py:113
  250.4 4.3 %collective-permute-done.50 = bf16[32,3072]{1,0:T(8,128)(2,1)S(1)} collective-permute-done((bf16[32,3072]{1,0:T(8,128)(2,1)S(1)}, bf16[32,3072]{1,0:T(8,128)(2,1)S(1)}, u32[]{:S(2)}, u32[]{:S(2)}) %collective-permute-start.50) | collective-permute-done | bytes 196640 | tf_op jit(solution)/shard_map/ppermute | solution.py:113
  (151 shorter events, 37.7 us)
Async XLA Ops:
  0.0 222.1 %copy-start = (bf16[1,128,3072]{2,1,0:T(8,128)(2,1)S(1)}, bf16[1,128,3072]{2,1,0:T(8,128)(2,1)}, u32[]{:S(2)}) copy-start(bf16[1,128,3072]{2,1,0:T(8,128)(2,1)} %param.28) | copy-start | bytes 2359300
  0.0 31.5 %collective-permute-start.1 = (bf16[32,3072]{1,0:T(8,128)(2,1)}, bf16[32,3072]{1,0:T(8,128)(2,1)S(1)}, u32[]{:S(2)}, u32[]{:S(2)}) collective-permute-start(bf16[32,3072]{1,0:T(8,128)(2,1)} %param.22), channel_id=1, source_target_pairs={{0,3},{2,1},{4,0},{6,2},{7,4},{5,6},{3,7},{1,5},{8,11},{10,9},{12,... | collective-permute-start | bytes 589832 | tf_op jit(solution)/shard_map/ppermute | solution.py:59
  4.0 29.6 %collective-permute-start = (bf16[32,3072]{1,0:T(8,128)(2,1)}, bf16[32,3072]{1,0:T(8,128)(2,1)S(1)}, u32[]{:S(2)}, u32[]{:S(2)}) collective-permute-start(bf16[32,3072]{1,0:T(8,128)(2,1)} %param.22), channel_id=1, source_target_pairs={{0,1},{2,0},{4,2},{6,4},{7,6},{5,7},{3,5},{1,3},{8,9},{10,8},{12,1... | collective-permute-start | bytes 589832 | tf_op jit(solution)/shard_map/ppermute | solution.py:59
  5.6 38.3 %collective-permute-start.7 = (bf16[32,3072]{1,0:T(8,128)(2,1)}, bf16[32,3072]{1,0:T(8,128)(2,1)S(1)}, u32[]{:S(2)}, u32[]{:S(2)}) collective-permute-start(bf16[32,3072]{1,0:T(8,128)(2,1)} %param.22), channel_id=1, source_target_pairs={{0,2},{2,4},{4,6},{6,7},{7,5},{5,3},{3,1},{1,0},{8,10},{10,12},{12... | collective-permute-start | bytes 589832 | tf_op jit(solution)/shard_map/ppermute | solution.py:58
  6.0 27.3 %collective-permute-start.3 = (bf16[32,3072]{1,0:T(8,128)(2,1)}, bf16[32,3072]{1,0:T(8,128)(2,1)S(1)}, u32[]{:S(2)}, u32[]{:S(2)}) collective-permute-start(bf16[32,3072]{1,0:T(8,128)(2,1)} %param.22), channel_id=1, source_target_pairs={{0,4},{2,6},{4,7},{6,5},{7,3},{5,1},{3,0},{1,2},{8,12},{10,14},{12... | collective-permute-start | bytes 589832 | tf_op jit(solution)/shard_map/ppermute | solution.py:58
  31.5 5.9 %collective-permute-start.2 = (bf16[32,3072]{1,0:T(8,128)(2,1)S(1)}, bf16[32,3072]{1,0:T(8,128)(2,1)S(1)}, u32[]{:S(2)}, u32[]{:S(2)}) collective-permute-start(bf16[32,3072]{1,0:T(8,128)(2,1)S(1)} %collective-permute-done.1), channel_id=1, source_target_pairs={{0,1},{2,0},{4,2},{6,4},{7,6},{5,7},{3,5},{1,3},{8,9},{10,8},{12,1... | collective-permute-start | bytes 589832 | tf_op jit(solution)/shard_map/ppermute | solution.py:71
  33.4 5.7 %collective-permute-start.4 = (bf16[32,3072]{1,0:T(8,128)(2,1)S(1)}, bf16[32,3072]{1,0:T(8,128)(2,1)S(1)}, u32[]{:S(2)}, u32[]{:S(2)}) collective-permute-start(bf16[32,3072]{1,0:T(8,128)(2,1)S(1)} %collective-permute-done.3), channel_id=1, source_target_pairs={{0,2},{2,4},{4,6},{6,7},{7,5},{5,3},{3,1},{1,0},{8,10},{10,12},{12... | collective-permute-start | bytes 589832 | tf_op jit(solution)/shard_map/ppermute | solution.py:68
  37.4 4.7 %collective-permute-start.6 = (bf16[16,3072]{1,0:T(8,128)(2,1)S(1)}, bf16[16,3072]{1,0:T(8,128)(2,1)S(1)}, u32[]{:S(2)}, u32[]{:S(2)}) collective-permute-start(bf16[16,3072]{1,0:T(8,128)(2,1)S(1)} %slice.396), channel_id=1, source_target_pairs={{0,1},{2,0},{4,2},{6,4},{7,6},{5,7},{3,5},{1,3},{8,9},{10,8},{12,1... | collective-permute-start | bytes 294920 | tf_op jit(solution)/shard_map/ppermute | solution.py:65
  39.1 4.7 %collective-permute-start.5 = (bf16[16,3072]{1,0:T(8,128)(2,1)S(1)}, bf16[16,3072]{1,0:T(8,128)(2,1)S(1)}, u32[]{:S(2)}, u32[]{:S(2)}) collective-permute-start(bf16[16,3072]{1,0:T(8,128)(2,1)S(1)} %slice.395), channel_id=1, source_target_pairs={{0,2},{2,4},{4,6},{6,7},{7,5},{5,3},{3,1},{1,0},{8,10},{10,12},{12... | collective-permute-start | bytes 294920 | tf_op jit(solution)/shard_map/ppermute | solution.py:64
  39.5 7.1 %copy-start.5 = (f32[3,3072]{1,0:T(4,128)S(1)}, f32[3,3072]{1,0:T(4,128)}, u32[]{:S(2)}) copy-start(f32[3,3072]{1,0:T(4,128)} %param.23) | copy-start | bytes 110596
  43.9 3.4 %copy-start.1 = (bf16[8,32,3072]{2,1,0:T(8,128)(2,1)}, bf16[8,32,3072]{2,1,0:T(8,128)(2,1)S(1)}, u32[]{:S(2)}) copy-start(bf16[8,32,3072]{2,1,0:T(8,128)(2,1)S(1)} %bitcast_dynamic-update-slice_fusion.14) | copy-start | bytes 4718596
  44.5 4.9 %collective-permute-start.8 = (bf16[128,3072]{1,0:T(8,128)(2,1)S(1)}, bf16[128,3072]{1,0:T(8,128)(2,1)}, u32[]{:S(2)}, u32[]{:S(2)}) collective-permute-start(bf16[128,3072]{1,0:T(8,128)(2,1)S(1)} %bitcast.154), channel_id=1, source_target_pairs={{0,8},{1,9},{2,10},{3,11},{4,12},{5,13},{6,14},{7,15},{16,24},{17,... | collective-permute-start | bytes 2359304 | tf_op jit(solution)/shard_map/ppermute | solution.py:14
  69.2 4.8 %collective-permute-start.9 = (bf16[16,3072]{1,0:T(8,128)(2,1)S(1)}, bf16[16,3072]{1,0:T(8,128)(2,1)S(1)}, u32[]{:S(2)}, u32[]{:S(2)}) collective-permute-start(bf16[16,3072]{1,0:T(8,128)(2,1)S(1)} %get-tuple-element.123), channel_id=1, source_target_pairs={{0,2},{2,4},{4,6},{6,7},{7,5},{5,3},{3,1},{1,0},{8,10},{10,12},{12... | collective-permute-start | bytes 294920 | tf_op jit(solution)/shard_map/ppermute | solution.py:113
  69.6 4.9 %collective-permute-start.13 = (bf16[16,3072]{1,0:T(8,128)(2,1)S(1)}, bf16[16,3072]{1,0:T(8,128)(2,1)S(1)}, u32[]{:S(2)}, u32[]{:S(2)}) collective-permute-start(bf16[16,3072]{1,0:T(8,128)(2,1)S(1)} %get-tuple-element.124), channel_id=1, source_target_pairs={{0,1},{2,0},{4,2},{6,4},{7,6},{5,7},{3,5},{1,3},{8,9},{10,8},{12,1... | collective-permute-start | bytes 294920 | tf_op jit(solution)/shard_map/ppermute | solution.py:113
  74.1 5.9 %collective-permute-start.10 = (bf16[32,3072]{1,0:T(8,128)(2,1)S(1)}, bf16[32,3072]{1,0:T(8,128)(2,1)S(1)}, u32[]{:S(2)}, u32[]{:S(2)}) collective-permute-start(bf16[32,3072]{1,0:T(8,128)(2,1)S(1)} %convert_element_type.317), channel_id=1, source_target_pairs={{0,2},{2,4},{4,6},{6,7},{7,5},{5,3},{3,1},{1,0},{8,10},{10,12},{12... | collective-permute-start | bytes 589832 | tf_op jit(solution)/shard_map/ppermute | solution.py:113
  74.6 25.5 %copy-start.4 = (bf16[32,3072]{1,0:T(8,128)(2,1)S(1)}, bf16[32,3072]{1,0:T(8,128)(2,1)}, u32[]{:S(2)}) copy-start(bf16[32,3072]{1,0:T(8,128)(2,1)} %param.22) | copy-start | bytes 589828
  74.6 5.8 %collective-permute-start.14 = (bf16[32,3072]{1,0:T(8,128)(2,1)S(1)}, bf16[32,3072]{1,0:T(8,128)(2,1)S(1)}, u32[]{:S(2)}, u32[]{:S(2)}) collective-permute-start(bf16[32,3072]{1,0:T(8,128)(2,1)S(1)} %convert_element_type.327), channel_id=1, source_target_pairs={{0,1},{2,0},{4,2},{6,4},{7,6},{5,7},{3,5},{1,3},{8,9},{10,8},{12,1... | collective-permute-start | bytes 589832 | tf_op jit(solution)/shard_map/ppermute | solution.py:113
  80.0 5.7 %collective-permute-start.11 = (bf16[32,3072]{1,0:T(8,128)(2,1)S(1)}, bf16[32,3072]{1,0:T(8,128)(2,1)S(1)}, u32[]{:S(2)}, u32[]{:S(2)}) collective-permute-start(bf16[32,3072]{1,0:T(8,128)(2,1)S(1)} %add_convert_fusion.14), channel_id=1, source_target_pairs={{0,2},{2,4},{4,6},{6,7},{7,5},{5,3},{3,1},{1,0},{8,10},{10,12},{12... | collective-permute-start | bytes 589832 | tf_op jit(solution)/shard_map/ppermute | solution.py:113
  85.9 7.5 %collective-permute-start.15 = (bf16[32,3072]{1,0:T(8,128)(2,1)S(1)}, bf16[32,3072]{1,0:T(8,128)(2,1)S(1)}, u32[]{:S(2)}, u32[]{:S(2)}) collective-permute-start(bf16[32,3072]{1,0:T(8,128)(2,1)S(1)} %get-tuple-element.116), channel_id=1, source_target_pairs={{0,1},{2,0},{4,2},{6,4},{7,6},{5,7},{3,5},{1,3},{8,9},{10,8},{12,1... | collective-permute-start | bytes 589832 | tf_op jit(solution)/shard_map/ppermute | solution.py:113
  87.5 7.6 %collective-permute-start.12 = (bf16[32,3072]{1,0:T(8,128)(2,1)S(1)}, bf16[32,3072]{1,0:T(8,128)(2,1)S(1)}, u32[]{:S(2)}, u32[]{:S(2)}) collective-permute-start(bf16[32,3072]{1,0:T(8,128)(2,1)S(1)} %get-tuple-element.115), channel_id=1, source_target_pairs={{0,2},{2,4},{4,6},{6,7},{7,5},{5,3},{3,1},{1,0},{8,10},{10,12},{12... | collective-permute-start | bytes 589832 | tf_op jit(solution)/shard_map/ppermute | solution.py:113
  93.4 6.7 %collective-permute-start.16 = (bf16[32,3072]{1,0:T(8,128)(2,1)S(1)}, bf16[32,3072]{1,0:T(8,128)(2,1)S(1)}, u32[]{:S(2)}, u32[]{:S(2)}) collective-permute-start(bf16[32,3072]{1,0:T(8,128)(2,1)S(1)} %add_convert_fusion.11), channel_id=1, source_target_pairs={{0,1},{2,0},{4,2},{6,4},{7,6},{5,7},{3,5},{1,3},{8,9},{10,8},{12,1... | collective-permute-start | bytes 589832 | tf_op jit(solution)/shard_map/ppermute | solution.py:113
  100.2 5.7 %collective-permute-start.17 = (bf16[32,3072]{1,0:T(8,128)(2,1)S(1)}, bf16[32,3072]{1,0:T(8,128)(2,1)S(1)}, u32[]{:S(2)}, u32[]{:S(2)}) collective-permute-start(bf16[32,3072]{1,0:T(8,128)(2,1)S(1)} %get-tuple-element.100), channel_id=1, source_target_pairs={{0,1},{2,0},{4,2},{6,4},{7,6},{5,7},{3,5},{1,3},{8,9},{10,8},{12,1... | collective-permute-start | bytes 589832 | tf_op jit(solution)/shard_map/ppermute | solution.py:59
  101.8 5.7 %collective-permute-start.20 = (bf16[32,3072]{1,0:T(8,128)(2,1)S(1)}, bf16[32,3072]{1,0:T(8,128)(2,1)S(1)}, u32[]{:S(2)}, u32[]{:S(2)}) collective-permute-start(bf16[32,3072]{1,0:T(8,128)(2,1)S(1)} %get-tuple-element.100), channel_id=1, source_target_pairs={{0,2},{2,4},{4,6},{6,7},{7,5},{5,3},{3,1},{1,0},{8,10},{10,12},{12... | collective-permute-start | bytes 589832 | tf_op jit(solution)/shard_map/ppermute | solution.py:58
  105.9 6.5 %collective-permute-start.18 = (bf16[32,3072]{1,0:T(8,128)(2,1)S(1)}, bf16[32,3072]{1,0:T(8,128)(2,1)S(1)}, u32[]{:S(2)}, u32[]{:S(2)}) collective-permute-start(bf16[32,3072]{1,0:T(8,128)(2,1)S(1)} %collective-permute-done.17), channel_id=1, source_target_pairs={{0,1},{2,0},{4,2},{6,4},{7,6},{5,7},{3,5},{1,3},{8,9},{10,8},{12,1... | collective-permute-start | bytes 589832 | tf_op jit(solution)/shard_map/ppermute | solution.py:71
  107.5 6.5 %collective-permute-start.21 = (bf16[32,3072]{1,0:T(8,128)(2,1)S(1)}, bf16[32,3072]{1,0:T(8,128)(2,1)S(1)}, u32[]{:S(2)}, u32[]{:S(2)}) collective-permute-start(bf16[32,3072]{1,0:T(8,128)(2,1)S(1)} %collective-permute-done.20), channel_id=1, source_target_pairs={{0,2},{2,4},{4,6},{6,7},{7,5},{5,3},{3,1},{1,0},{8,10},{10,12},{12... | collective-permute-start | bytes 589832 | tf_op jit(solution)/shard_map/ppermute | solution.py:68
  112.4 5.7 %collective-permute-start.19 = (bf16[32,3072]{1,0:T(8,128)(2,1)S(1)}, bf16[32,3072]{1,0:T(8,128)(2,1)S(1)}, u32[]{:S(2)}, u32[]{:S(2)}) collective-permute-start(bf16[32,3072]{1,0:T(8,128)(2,1)S(1)} %collective-permute-done.18), channel_id=1, source_target_pairs={{0,1},{2,0},{4,2},{6,4},{7,6},{5,7},{3,5},{1,3},{8,9},{10,8},{12,1... | collective-permute-start | bytes 589832 | tf_op jit(solution)/shard_map/ppermute | solution.py:71
  114.0 5.7 %collective-permute-start.22 = (bf16[32,3072]{1,0:T(8,128)(2,1)S(1)}, bf16[32,3072]{1,0:T(8,128)(2,1)S(1)}, u32[]{:S(2)}, u32[]{:S(2)}) collective-permute-start(bf16[32,3072]{1,0:T(8,128)(2,1)S(1)} %collective-permute-done.21), channel_id=1, source_target_pairs={{0,2},{2,4},{4,6},{6,7},{7,5},{5,3},{3,1},{1,0},{8,10},{10,12},{12... | collective-permute-start | bytes 589832 | tf_op jit(solution)/shard_map/ppermute | solution.py:68
  118.1 4.7 %collective-permute-start.24 = (bf16[16,3072]{1,0:T(8,128)(2,1)S(1)}, bf16[16,3072]{1,0:T(8,128)(2,1)S(1)}, u32[]{:S(2)}, u32[]{:S(2)}) collective-permute-start(bf16[16,3072]{1,0:T(8,128)(2,1)S(1)} %slice.410), channel_id=1, source_target_pairs={{0,1},{2,0},{4,2},{6,4},{7,6},{5,7},{3,5},{1,3},{8,9},{10,8},{12,1... | collective-permute-start | bytes 294920 | tf_op jit(solution)/shard_map/ppermute | solution.py:65
  119.7 4.7 %collective-permute-start.23 = (bf16[16,3072]{1,0:T(8,128)(2,1)S(1)}, bf16[16,3072]{1,0:T(8,128)(2,1)S(1)}, u32[]{:S(2)}, u32[]{:S(2)}) collective-permute-start(bf16[16,3072]{1,0:T(8,128)(2,1)S(1)} %slice.409), channel_id=1, source_target_pairs={{0,2},{2,4},{4,6},{6,7},{7,5},{5,3},{3,1},{1,0},{8,10},{10,12},{12... | collective-permute-start | bytes 294920 | tf_op jit(solution)/shard_map/ppermute | solution.py:64
  124.5 4.6 %copy-start.2 = (bf16[8,32,3072]{2,1,0:T(8,128)(2,1)}, bf16[8,32,3072]{2,1,0:T(8,128)(2,1)S(1)}, u32[]{:S(2)}) copy-start(bf16[8,32,3072]{2,1,0:T(8,128)(2,1)S(1)} %bitcast_dynamic-update-slice_fusion.7) | copy-start | bytes 4718596
  125.1 6.1 %collective-permute-start.25 = (bf16[128,3072]{1,0:T(8,128)(2,1)S(1)}, bf16[128,3072]{1,0:T(8,128)(2,1)}, u32[]{:S(2)}, u32[]{:S(2)}) collective-permute-start(bf16[128,3072]{1,0:T(8,128)(2,1)S(1)} %bitcast.153), channel_id=1, source_target_pairs={{0,8},{1,9},{2,10},{3,11},{4,12},{5,13},{6,14},{7,15},{16,24},{17,... | collective-permute-start | bytes 2359304 | tf_op jit(solution)/shard_map/ppermute | solution.py:14
  151.3 4.8 %collective-permute-start.26 = (bf16[16,3072]{1,0:T(8,128)(2,1)S(1)}, bf16[16,3072]{1,0:T(8,128)(2,1)S(1)}, u32[]{:S(2)}, u32[]{:S(2)}) collective-permute-start(bf16[16,3072]{1,0:T(8,128)(2,1)S(1)} %get-tuple-element.121), channel_id=1, source_target_pairs={{0,2},{2,4},{4,6},{6,7},{7,5},{5,3},{3,1},{1,0},{8,10},{10,12},{12... | collective-permute-start | bytes 294920 | tf_op jit(solution)/shard_map/ppermute | solution.py:113
  151.8 4.9 %collective-permute-start.30 = (bf16[16,3072]{1,0:T(8,128)(2,1)S(1)}, bf16[16,3072]{1,0:T(8,128)(2,1)S(1)}, u32[]{:S(2)}, u32[]{:S(2)}) collective-permute-start(bf16[16,3072]{1,0:T(8,128)(2,1)S(1)} %get-tuple-element.122), channel_id=1, source_target_pairs={{0,1},{2,0},{4,2},{6,4},{7,6},{5,7},{3,5},{1,3},{8,9},{10,8},{12,1... | collective-permute-start | bytes 294920 | tf_op jit(solution)/shard_map/ppermute | solution.py:113
  156.1 7.1 %collective-permute-start.27 = (bf16[32,3072]{1,0:T(8,128)(2,1)S(1)}, bf16[32,3072]{1,0:T(8,128)(2,1)S(1)}, u32[]{:S(2)}, u32[]{:S(2)}) collective-permute-start(bf16[32,3072]{1,0:T(8,128)(2,1)S(1)} %convert_element_type.342), channel_id=1, source_target_pairs={{0,2},{2,4},{4,6},{6,7},{7,5},{5,3},{3,1},{1,0},{8,10},{10,12},{12... | collective-permute-start | bytes 589832 | tf_op jit(solution)/shard_map/ppermute | solution.py:113
  156.8 7.0 %collective-permute-start.31 = (bf16[32,3072]{1,0:T(8,128)(2,1)S(1)}, bf16[32,3072]{1,0:T(8,128)(2,1)S(1)}, u32[]{:S(2)}, u32[]{:S(2)}) collective-permute-start(bf16[32,3072]{1,0:T(8,128)(2,1)S(1)} %convert_element_type.352), channel_id=1, source_target_pairs={{0,1},{2,0},{4,2},{6,4},{7,6},{5,7},{3,5},{1,3},{8,9},{10,8},{12,1... | collective-permute-start | bytes 589832 | tf_op jit(solution)/shard_map/ppermute | solution.py:113
  163.3 6.7 %collective-permute-start.28 = (bf16[32,3072]{1,0:T(8,128)(2,1)S(1)}, bf16[32,3072]{1,0:T(8,128)(2,1)S(1)}, u32[]{:S(2)}, u32[]{:S(2)}) collective-permute-start(bf16[32,3072]{1,0:T(8,128)(2,1)S(1)} %add_convert_fusion.9), channel_id=1, source_target_pairs={{0,2},{2,4},{4,6},{6,7},{7,5},{5,3},{3,1},{1,0},{8,10},{10,12},{12... | collective-permute-start | bytes 589832 | tf_op jit(solution)/shard_map/ppermute | solution.py:113
  170.1 5.7 %collective-permute-start.32 = (bf16[32,3072]{1,0:T(8,128)(2,1)S(1)}, bf16[32,3072]{1,0:T(8,128)(2,1)S(1)}, u32[]{:S(2)}, u32[]{:S(2)}) collective-permute-start(bf16[32,3072]{1,0:T(8,128)(2,1)S(1)} %get-tuple-element.112), channel_id=1, source_target_pairs={{0,1},{2,0},{4,2},{6,4},{7,6},{5,7},{3,5},{1,3},{8,9},{10,8},{12,1... | collective-permute-start | bytes 589832 | tf_op jit(solution)/shard_map/ppermute | solution.py:113
  171.2 6.9 %collective-permute-start.29 = (bf16[32,3072]{1,0:T(8,128)(2,1)S(1)}, bf16[32,3072]{1,0:T(8,128)(2,1)S(1)}, u32[]{:S(2)}, u32[]{:S(2)}) collective-permute-start(bf16[32,3072]{1,0:T(8,128)(2,1)S(1)} %get-tuple-element.111), channel_id=1, source_target_pairs={{0,2},{2,4},{4,6},{6,7},{7,5},{5,3},{3,1},{1,0},{8,10},{10,12},{12... | collective-permute-start | bytes 589832 | tf_op jit(solution)/shard_map/ppermute | solution.py:113
  175.9 6.0 %collective-permute-start.33 = (bf16[32,3072]{1,0:T(8,128)(2,1)S(1)}, bf16[32,3072]{1,0:T(8,128)(2,1)S(1)}, u32[]{:S(2)}, u32[]{:S(2)}) collective-permute-start(bf16[32,3072]{1,0:T(8,128)(2,1)S(1)} %add_convert_fusion.6), channel_id=1, source_target_pairs={{0,1},{2,0},{4,2},{6,4},{7,6},{5,7},{3,5},{1,3},{8,9},{10,8},{12,1... | collective-permute-start | bytes 589832 | tf_op jit(solution)/shard_map/ppermute | solution.py:113
  182.6 7.7 %collective-permute-start.34 = (bf16[32,3072]{1,0:T(8,128)(2,1)S(1)}, bf16[32,3072]{1,0:T(8,128)(2,1)S(1)}, u32[]{:S(2)}, u32[]{:S(2)}) collective-permute-start(bf16[32,3072]{1,0:T(8,128)(2,1)S(1)} %get-tuple-element.98), channel_id=1, source_target_pairs={{0,1},{2,0},{4,2},{6,4},{7,6},{5,7},{3,5},{1,3},{8,9},{10,8},{12,1... | collective-permute-start | bytes 589832 | tf_op jit(solution)/shard_map/ppermute | solution.py:59
  185.5 7.2 %collective-permute-start.37 = (bf16[32,3072]{1,0:T(8,128)(2,1)S(1)}, bf16[32,3072]{1,0:T(8,128)(2,1)S(1)}, u32[]{:S(2)}, u32[]{:S(2)}) collective-permute-start(bf16[32,3072]{1,0:T(8,128)(2,1)S(1)} %get-tuple-element.98), channel_id=1, source_target_pairs={{0,2},{2,4},{4,6},{6,7},{7,5},{5,3},{3,1},{1,0},{8,10},{10,12},{12... | collective-permute-start | bytes 589832 | tf_op jit(solution)/shard_map/ppermute | solution.py:58
  190.3 5.8 %collective-permute-start.35 = (bf16[32,3072]{1,0:T(8,128)(2,1)S(1)}, bf16[32,3072]{1,0:T(8,128)(2,1)S(1)}, u32[]{:S(2)}, u32[]{:S(2)}) collective-permute-start(bf16[32,3072]{1,0:T(8,128)(2,1)S(1)} %collective-permute-done.34), channel_id=1, source_target_pairs={{0,1},{2,0},{4,2},{6,4},{7,6},{5,7},{3,5},{1,3},{8,9},{10,8},{12,1... | collective-permute-start | bytes 589832 | tf_op jit(solution)/shard_map/ppermute | solution.py:71
  192.7 5.7 %collective-permute-start.38 = (bf16[32,3072]{1,0:T(8,128)(2,1)S(1)}, bf16[32,3072]{1,0:T(8,128)(2,1)S(1)}, u32[]{:S(2)}, u32[]{:S(2)}) collective-permute-start(bf16[32,3072]{1,0:T(8,128)(2,1)S(1)} %collective-permute-done.37), channel_id=1, source_target_pairs={{0,2},{2,4},{4,6},{6,7},{7,5},{5,3},{3,1},{1,0},{8,10},{10,12},{12... | collective-permute-start | bytes 589832 | tf_op jit(solution)/shard_map/ppermute | solution.py:68
  196.2 5.7 %collective-permute-start.36 = (bf16[32,3072]{1,0:T(8,128)(2,1)S(1)}, bf16[32,3072]{1,0:T(8,128)(2,1)S(1)}, u32[]{:S(2)}, u32[]{:S(2)}) collective-permute-start(bf16[32,3072]{1,0:T(8,128)(2,1)S(1)} %collective-permute-done.35), channel_id=1, source_target_pairs={{0,1},{2,0},{4,2},{6,4},{7,6},{5,7},{3,5},{1,3},{8,9},{10,8},{12,1... | collective-permute-start | bytes 589832 | tf_op jit(solution)/shard_map/ppermute | solution.py:71
  198.3 5.7 %collective-permute-start.39 = (bf16[32,3072]{1,0:T(8,128)(2,1)S(1)}, bf16[32,3072]{1,0:T(8,128)(2,1)S(1)}, u32[]{:S(2)}, u32[]{:S(2)}) collective-permute-start(bf16[32,3072]{1,0:T(8,128)(2,1)S(1)} %collective-permute-done.38), channel_id=1, source_target_pairs={{0,2},{2,4},{4,6},{6,7},{7,5},{5,3},{3,1},{1,0},{8,10},{10,12},{12... | collective-permute-start | bytes 589832 | tf_op jit(solution)/shard_map/ppermute | solution.py:68
  201.9 4.7 %collective-permute-start.41 = (bf16[16,3072]{1,0:T(8,128)(2,1)S(1)}, bf16[16,3072]{1,0:T(8,128)(2,1)S(1)}, u32[]{:S(2)}, u32[]{:S(2)}) collective-permute-start(bf16[16,3072]{1,0:T(8,128)(2,1)S(1)} %slice.424), channel_id=1, source_target_pairs={{0,1},{2,0},{4,2},{6,4},{7,6},{5,7},{3,5},{1,3},{8,9},{10,8},{12,1... | collective-permute-start | bytes 294920 | tf_op jit(solution)/shard_map/ppermute | solution.py:65
  204.0 4.7 %collective-permute-start.40 = (bf16[16,3072]{1,0:T(8,128)(2,1)S(1)}, bf16[16,3072]{1,0:T(8,128)(2,1)S(1)}, u32[]{:S(2)}, u32[]{:S(2)}) collective-permute-start(bf16[16,3072]{1,0:T(8,128)(2,1)S(1)} %slice.423), channel_id=1, source_target_pairs={{0,2},{2,4},{4,6},{6,7},{7,5},{5,3},{3,1},{1,0},{8,10},{10,12},{12... | collective-permute-start | bytes 294920 | tf_op jit(solution)/shard_map/ppermute | solution.py:64
  214.0 1.7 copy-start.3
  217.6 2.3 collective-permute-start.42
  222.4 4.7 %collective-permute-start.43 = (bf16[16,3072]{1,0:T(8,128)(2,1)S(1)}, bf16[16,3072]{1,0:T(8,128)(2,1)S(1)}, u32[]{:S(2)}, u32[]{:S(2)}) collective-permute-start(bf16[16,3072]{1,0:T(8,128)(2,1)S(1)} %get-tuple-element.119), channel_id=1, source_target_pairs={{0,2},{2,4},{4,6},{6,7},{7,5},{5,3},{3,1},{1,0},{8,10},{10,12},{12... | collective-permute-start | bytes 294920 | tf_op jit(solution)/shard_map/ppermute | solution.py:113
  222.4 4.7 %collective-permute-start.47 = (bf16[16,3072]{1,0:T(8,128)(2,1)S(1)}, bf16[16,3072]{1,0:T(8,128)(2,1)S(1)}, u32[]{:S(2)}, u32[]{:S(2)}) collective-permute-start(bf16[16,3072]{1,0:T(8,128)(2,1)S(1)} %get-tuple-element.120), channel_id=1, source_target_pairs={{0,1},{2,0},{4,2},{6,4},{7,6},{5,7},{3,5},{1,3},{8,9},{10,8},{12,1... | collective-permute-start | bytes 294920 | tf_op jit(solution)/shard_map/ppermute | solution.py:113
  227.1 7.4 %collective-permute-start.44 = (bf16[32,3072]{1,0:T(8,128)(2,1)S(1)}, bf16[32,3072]{1,0:T(8,128)(2,1)S(1)}, u32[]{:S(2)}, u32[]{:S(2)}) collective-permute-start(bf16[32,3072]{1,0:T(8,128)(2,1)S(1)} %convert_element_type.376), channel_id=1, source_target_pairs={{0,2},{2,4},{4,6},{6,7},{7,5},{5,3},{3,1},{1,0},{8,10},{10,12},{12... | collective-permute-start | bytes 589832 | tf_op jit(solution)/shard_map/ppermute | solution.py:113
  227.3 7.4 %collective-permute-start.48 = (bf16[32,3072]{1,0:T(8,128)(2,1)S(1)}, bf16[32,3072]{1,0:T(8,128)(2,1)S(1)}, u32[]{:S(2)}, u32[]{:S(2)}) collective-permute-start(bf16[32,3072]{1,0:T(8,128)(2,1)S(1)} %convert_element_type.386), channel_id=1, source_target_pairs={{0,1},{2,0},{4,2},{6,4},{7,6},{5,7},{3,5},{1,3},{8,9},{10,8},{12,1... | collective-permute-start | bytes 589832 | tf_op jit(solution)/shard_map/ppermute | solution.py:113
  234.6 7.6 %collective-permute-start.45 = (bf16[32,3072]{1,0:T(8,128)(2,1)S(1)}, bf16[32,3072]{1,0:T(8,128)(2,1)S(1)}, u32[]{:S(2)}, u32[]{:S(2)}) collective-permute-start(bf16[32,3072]{1,0:T(8,128)(2,1)S(1)} %add_convert_fusion.4), channel_id=1, source_target_pairs={{0,2},{2,4},{4,6},{6,7},{7,5},{5,3},{3,1},{1,0},{8,10},{10,12},{12... | collective-permute-start | bytes 589832 | tf_op jit(solution)/shard_map/ppermute | solution.py:113
  242.3 6.6 %collective-permute-start.49 = (bf16[32,3072]{1,0:T(8,128)(2,1)S(1)}, bf16[32,3072]{1,0:T(8,128)(2,1)S(1)}, u32[]{:S(2)}, u32[]{:S(2)}) collective-permute-start(bf16[32,3072]{1,0:T(8,128)(2,1)S(1)} %get-tuple-element.108), channel_id=1, source_target_pairs={{0,1},{2,0},{4,2},{6,4},{7,6},{5,7},{3,5},{1,3},{8,9},{10,8},{12,1... | collective-permute-start | bytes 589832 | tf_op jit(solution)/shard_map/ppermute | solution.py:113
  244.1 6.4 %collective-permute-start.46 = (bf16[32,3072]{1,0:T(8,128)(2,1)S(1)}, bf16[32,3072]{1,0:T(8,128)(2,1)S(1)}, u32[]{:S(2)}, u32[]{:S(2)}) collective-permute-start(bf16[32,3072]{1,0:T(8,128)(2,1)S(1)} %get-tuple-element.107), channel_id=1, source_target_pairs={{0,2},{2,4},{4,6},{6,7},{7,5},{5,3},{3,1},{1,0},{8,10},{10,12},{12... | collective-permute-start | bytes 589832 | tf_op jit(solution)/shard_map/ppermute | solution.py:113
  249.0 5.8 %collective-permute-start.50 = (bf16[32,3072]{1,0:T(8,128)(2,1)S(1)}, bf16[32,3072]{1,0:T(8,128)(2,1)S(1)}, u32[]{:S(2)}, u32[]{:S(2)}) collective-permute-start(bf16[32,3072]{1,0:T(8,128)(2,1)S(1)} %add_convert_fusion.1), channel_id=1, source_target_pairs={{0,1},{2,0},{4,2},{6,4},{7,6},{5,7},{3,5},{1,3},{8,9},{10,8},{12,1... | collective-permute-start | bytes 589832 | tf_op jit(solution)/shard_map/ppermute | solution.py:113
